TPU v7x, 32 devices: a whole 2x2x4 slice. The times are simulated.
32 devices in a mesh: dom: 2 (over x), shot: 8 (over z, y), space: 2 (over core).
Axes of the slice: x: 2, y: 2, z: 4, core: 2. Of those that a mesh axis runs over, the one named last changes fastest.
Arguments:
- wave_prev: float32 [16, 64, 64, 128], P(('dom', 'shot'), 'space'), parts along dimension 0, may hold values from -13 to 13
- wave_now: float32 [16, 64, 64, 128], P(('dom', 'shot'), 'space'), parts along dimension 0, may hold values from -13 to 13
- velocity_code: int32 [128, 64, 128], P(('dom', 'space')), parts along dimension 0, may hold values from 0 to 255
- perturb: float32 [128, 64, 128], P(('dom', 'space'), None, 'shot'), parts along dimension 0, may hold values from -3 to 3
- gains: float32 [256, 64], P(('dom', 'shot')), parts along dimension 0, may hold values from 0.25 to 4
- wavelet: float32 [16, 4], P(('dom', 'shot')), parts along dimension 0, may hold values from -12 to 12
- source_index: int32 [16], P(('dom', 'shot')), parts along dimension 0, may hold values from 0 to 524287
- receiver_index: int32 [16, 256], P(('dom', 'shot')), parts along dimension 0, may hold values from 0 to 524287
- absorb_width: int32 [12], P('dom'), parts along dimension 0, may hold values from 4 to 20
Outputs:
- filtered: float32 [128, 64, 128], P(('dom', 'space'), None, 'shot'), parts along dimension 0
- born_field: float32 [16, 64, 64, 128], P(('dom', 'shot'), 'space'), parts along dimension 0
- traces: float32 [16, 2, 256], P(('dom', 'shot')), parts along dimension 0
There are 2 independent parts, one for each index of `dom`. A program takes and returns all parts, laid end to end along the dimension named above; each array names one. Nothing has to cross between parts.
Inputs may be any that keep to these rules, and one draw needn't show every extreme that they name: `absorb_width`: entries are the widths at the low and high end of the first, second and third dimension, in that order. `source_index`: flat row-major cell indices of the whole window. `receiver_index`: flat row-major cell indices of the whole window.
All inputs are finite; a program needn't handle non-finite values.
Results may differ from a plain program's by a relative error of at most 0.0003.
Values sent between devices are 32-bit elements; how exact they have to be, the bound alone decides.
No kernel may reach another device: no remote copies, remote signals or barrier semaphores. Data moves between devices by JAX's collectives and lax.ppermute only.
A program may use at most 64 MiB of HBM per device.

v0:
```python
import math

import jax
import jax.numpy as jnp
from jax import lax
from jax.sharding import PartitionSpec as P

STEPS_A = 2
STEPS_B = 2


STENCIL = (-205.0 / 72.0, 8.0 / 5.0, -1.0 / 5.0, 8.0 / 315.0, -1.0 / 560.0)
damp_peak = 0.5
eps = 1e-05


def with_halo(x, sides, width):
    for axis, dim in sides:
        size, length = (lax.axis_size(axis), x.shape[dim])
        up = [(i, (i + 1) % size) for i in range(size - 1)]
        down = [(j, i) for i, j in up]
        last = lax.slice_in_dim(x, length - width, length, axis=dim)
        first = lax.slice_in_dim(x, 0, width, axis=dim)
        before = lax.ppermute(last, axis, up)
        after = lax.ppermute(first, axis, down)
        x = jnp.concatenate([before, x, after], axis=dim)
    return x


def coefficient(levels):
    speed = 1500.0 + 15.0 * levels.astype(jnp.float32)
    ratio = 0.45 * speed / 5325.0
    return ratio * ratio


def ramp(position, count, lower, upper):
    low_part = jnp.maximum(lower - position, 0.0) / lower
    high_part = jnp.maximum(upper - (count - 1.0 - position), 0.0) / upper
    return low_part * low_part + high_part * high_part


def damping(widths, positions, count_x, count_y, count_z):
    edges = widths.astype(jnp.float32)
    along_x = ramp(positions, count_x, edges[0], edges[1])
    along_y = ramp(jnp.arange(count_y, dtype=jnp.float32), count_y, edges[2], edges[3])
    along_z = ramp(jnp.arange(count_z, dtype=jnp.float32), count_z, edges[4], edges[5])
    return damp_peak * (along_x[:, None, None] + along_y[None, :, None] + along_z[None, None, :])


def widen(field):
    lead = [(0, 0)] * (field.ndim - 2)
    return jnp.pad(field, lead + [(4, 4), (4, 4)])


def laplace(padded):
    width_x = padded.shape[-3] - 8
    width_y = padded.shape[-2] - 8
    width_z = padded.shape[-1] - 8

    def part(move_x, move_y, move_z):
        return padded[
            ...,
            4 + move_x : 4 + move_x + width_x,
            4 + move_y : 4 + move_y + width_y,
            4 + move_z : 4 + move_z + width_z,
        ]

    total = 3.0 * STENCIL[0] * part(0, 0, 0)
    for reach in range(1, 5):
        beside_all = (
            part(reach, 0, 0)
            + part(-reach, 0, 0)
            + part(0, reach, 0)
            + part(0, -reach, 0)
            + part(0, 0, reach)
            + part(0, 0, -reach)
        )
        total = total + STENCIL[reach] * beside_all
    return total


def lateral_filter(field, table):
    count = field.shape[1]
    index = jnp.arange(count)
    phase = index[:, None] * index[None, :] % count
    angle = 2.0 * math.pi / count * phase.astype(jnp.float32)
    cosine = jnp.cos(angle)
    sine = jnp.sin(angle)
    real_part = jnp.einsum("xyz,yk->xzk", field, cosine, precision=lax.Precision.HIGHEST)
    imag_part = jnp.einsum("xyz,yk->xzk", field, sine, precision=lax.Precision.HIGHEST)
    weight = table[None, :, :]
    back = jnp.einsum("xzk,yk->xyz", real_part * weight, cosine, precision=lax.Precision.HIGHEST)
    back = back + jnp.einsum(
        "xzk,yk->xyz", imag_part * weight, sine, precision=lax.Precision.HIGHEST
    )
    return back / count


def body(
    wave_prev,
    wave_now,
    velocity_code,
    perturb,
    gains,
    wavelet,
    source_index,
    receiver_index,
    absorb_width,
):
    shots, span_x, span_y, span_z = wave_now.shape
    start_x = lax.axis_index("space") * span_x
    total_x = span_x * lax.axis_size("space")
    speed_term = coefficient(velocity_code)
    positions = start_x.astype(jnp.float32) + jnp.arange(span_x, dtype=jnp.float32)
    absorber = damping(absorb_width, positions, total_x, span_y, span_z)
    term_flat = speed_term.reshape(-1)
    cells = span_x * span_y * span_z
    offset = start_x * span_y * span_z
    rows = jnp.arange(shots)
    source_local = source_index - offset
    source_owned = (source_local >= 0) & (source_local < cells)
    source_safe = jnp.clip(source_local, 0, cells - 1)
    source_gain = jnp.where(source_owned, term_flat[source_safe], 0.0)
    model = lax.all_gather(perturb, "shot", axis=2, tiled=True)

    def inject(field, moment):
        flat = field.reshape(shots, -1)
        flat = flat.at[rows, source_safe].add(source_gain * wavelet[:, moment])
        return flat.reshape(field.shape)

    def advance(current, prior, born, field_model, moment, first):
        if first:
            padded = widen(with_halo(current, (("space", 1),), 4))
        else:
            both = widen(with_halo(jnp.stack([current, born]), (("space", 2),), 4))
            padded = both[0]
            born_padded = both[1]
        drive = speed_term * laplace(padded)
        later = inject(2.0 * current - prior + drive - absorber * (current - prior), moment)
        if first:
            born_later = field_model * drive
        else:
            born_later = (
                2.0 * born
                + speed_term * laplace(born_padded)
                - absorber * born
                + field_model * drive
            )
        return (later, born_later, drive)

    current, prior = (wave_now, wave_prev)
    born = None
    image = jnp.zeros((span_x, span_y, span_z), jnp.float32)
    light = jnp.zeros((span_x, span_y, span_z), jnp.float32)
    for moment in range(STEPS_A):
        later, born_later, drive = advance(current, prior, born, model, moment, moment == 0)
        image = image + jnp.sum(drive * born_later, axis=0)
        light = light + jnp.sum(drive * drive, axis=0)
        prior, current = (current, later)
        born = born_later
    planes = gains.shape[0]
    image_all, light_all = lax.psum((image, light), "shot")
    table_all = lax.all_gather(gains, "shot", axis=0, tiled=True)
    new_model = lateral_filter(image_all / (light_all + eps), table_all)
    filtered = lax.dynamic_slice_in_dim(new_model, lax.axis_index("shot") * planes, planes, 2)
    receiver_local = receiver_index - offset
    receiver_owned = (receiver_local >= 0) & (receiver_local < cells)
    receiver_safe = jnp.clip(receiver_local, 0, cells - 1)
    born = None
    records = []
    for moment in range(STEPS_B):
        later, born_later, drive = advance(
            current, prior, born, new_model, STEPS_A + moment, moment == 0
        )
        sample = jnp.take_along_axis(born_later.reshape(shots, -1), receiver_safe, axis=1)
        records.append(jnp.where(receiver_owned, sample, 0.0))
        prior, current = (current, later)
        born = born_later
    traces = lax.psum(jnp.stack(records, axis=1), "space")
    return (filtered, born, traces)


def solution(mesh):
    in_specs = (
        P(("dom", "shot"), "space", None, None),
        P(("dom", "shot"), "space", None, None),
        P(("dom", "space"), None, None),
        P(("dom", "space"), None, "shot"),
        P(("dom", "shot"), None),
        P(("dom", "shot"), None),
        P(("dom", "shot")),
        P(("dom", "shot"), None),
        P("dom"),
    )
    out_specs = (
        P(("dom", "space"), None, "shot"),
        P(("dom", "shot"), "space", None, None),
        P(("dom", "shot"), None, None),
    )
    return jax.shard_map(body, mesh=mesh, in_specs=in_specs, out_specs=out_specs, check_vma=False)
```

profile of v0, /device:TPU:0, one launch (start us, length us, event | category | flops | bytes accessed | tf_op | source)
XLA Modules:
  0.0 278.1 jit_solution(2789940103628602469)
XLA Ops:
  7.2 1.7 fusion.136
  9.0 2.4 collective-permute-start.1
  12.6 1.7 copy.18
  15.7 1.4 multiply_multiply_fusion
  27.0 7.3 %multiply_subtract_fusion.2 = (f32[1,32,64,128]{3,2,1,0:T(8,128)S(1)}, f32[1,32,64,128]{3,2,1,0:T(8,128)}) fusion(f32[1,32,64,128]{3,2,1,0:T(8,128)} %param.18, f32[1,32,64,128]{3,2,1,0:T(8,128)} %param.17, f32[128]{0:T(128)S(1)} %fusion.117, f32[32,64]{1,0:T(8,128)S(1)} %broadcast_add_fusion, f32[1,40,72,136]{3,2,1,0:T(8,128)S(1)} %select_maximum_fusion.8, ...), kind=kLoop, calls=%fused_computation.250 | loop fusion | flops 11272192 | bytes 30417408 | tf_op jit(solution)/shard_map/sub | solution.py:139
  36.9 29.7 %all-gather.2.cloned.1.call-done = f32[32,64,128]{1,0,2:T(8,128)} async-done(((f32[32,64,16]{1,0,2:T(8,128)}), f32[32,64,128]{1,0,2:T(8,128)}) %all-gather.2.cloned.1.call-update) | async-done | bytes 1048592 | tf_op jit(solution)/shard_map/all_gather | solution.py:124
  66.7 3.7 %copy.19 = f32[32,64,128]{2,1,0:T(8,128)} copy(f32[32,64,128]{1,0,2:T(8,128)} %all-gather.2.cloned.1.call-done) | data formatting | bytes 2097152 | tf_op jit(solution)/shard_map/all_gather | solution.py:124
  70.3 1.4 fusion.93
  71.8 1.3 collective-permute-start.2
  73.1 1.5 collective-permute-start.3
  74.6 1.9 collective-permute-done.3
  76.5 4.7 %select_maximum_fusion.3 = f32[2,1,40,72,136]{4,3,2,1,0:T(8,128)S(1)} fusion(f32[2,1,4,64,128]{4,3,2,1,0:T(8,128)S(1)} %collective-permute-done.3, f32[2,1,4,64,128]{4,3,2,1,0:T(8,128)S(1)} %collective-permute-done.2, f32[1,1,32,64,128]{4,3,2,1,0:T(8,128)S(1)} %fusion.93, f32[1,1,32,64,128]{4,3,2,1,0:T(8,128)S(1)} %bitcast.94), kind=kLoop, calls=%fused_computation.9 | loop fusion | flops 14100480 | bytes 5754880 | tf_op jit(solution)/shard_map/concatenate | solution.py:26
  82.5 8.2 %multiply_subtract_fusion.1 = (f32[1,32,64,128]{3,2,1,0:T(8,128)}, f32[1,32,64,128]{3,2,1,0:T(8,128)S(1)}) fusion(f32[1,32,64,128]{3,2,1,0:T(8,128)S(1)} %bitcast.95, f32[1,32,64,128]{3,2,1,0:T(8,128)S(1)} %copy-done.4, f32[128]{0:T(128)S(1)} %copy-done.12, f32[32,64]{1,0:T(8,128)S(1)} %broadcast_add_fusion, f32[1,40,72,136]{3,2,1,0:T(8,128)S(1)} %get-tuple-element.71, ...), kind=kLoop, calls=%fused_computation.246 | loop fusion | flops 11272192 | bytes 31465984 | tf_op jit(solution)/shard_map/sub | solution.py:139
  92.2 8.2 %fusion.68 = f32[32,64,128]{2,1,0:T(8,128)} fusion(f32[1,32,64,128]{3,2,1,0:T(8,128)S(1)} %get-tuple-element.65, f32[1,40,72,136]{3,2,1,0:T(8,128)S(1)} %get-tuple-element.70, f32[32,64,128]{2,1,0:T(8,128)S(1)} %copy-done.9, f32[1,32,64,128]{3,2,1,0:T(8,128)S(1)} %copy-done.6, f32[128]{0:T(128)S(1)} %copy-done.12, f32[32,64]{1,0:T(8,128)S(1)} %broadcast_add_fusion, ...), kind=kLoop, calls=%fused_computation.156 | loop fusion | flops 12320768 | bytes 31465984 | tf_op jit(solution)/shard_map/add | solution.py:157
  101.1 1.3 fusion.140
  108.1 3.0 %collective-permute-start.5 = (f32[1,4,64,128]{3,2,1,0:T(8,128)S(1)}, f32[1,4,64,128]{3,2,1,0:T(8,128)S(1)}, u32[]{:S(2)}, u32[]{:S(2)}) collective-permute-start(f32[1,4,64,128]{3,2,1,0:T(8,128)S(1)} %get-tuple-element.76), channel_id=1, source_target_pairs={{0,1},{2,3},{4,5},{6,7},{8,9},{10,11},{12,13},{14,15},{16,17},{18,... | collective-permute-start | bytes 393224 | tf_op jit(solution)/shard_map/ppermute | solution.py:24
  111.8 31.3 %all_gather.7 = f32[128,64]{1,0:T(8,128)S(1)} all-gather(f32[16,64]{1,0:T(8,128)S(1)} %copy-done.14), channel_id=1, replica_groups=mesh['dom'=2,'shot'=8,'space'=2] {'shot'}, dimensions={0}, use_global_device_ids=true | all-gather | bytes 36864 | tf_op jit(solution)/shard_map/all_gather | solution.py:163
  143.1 2.1 select_maximum_fusion.6
  145.2 10.9 %multiply_subtract_fusion = (f32[1,32,64,128]{3,2,1,0:T(8,128)}, f32[1,32,64,128]{3,2,1,0:T(8,128)}) fusion(f32[1,32,64,128]{3,2,1,0:T(8,128)} %bitcast.104, f32[1,32,64,128]{3,2,1,0:T(8,128)} %bitcast.96, f32[128]{0:T(128)S(1)} %copy-done.12, f32[32,64]{1,0:T(8,128)S(1)} %broadcast_add_fusion, f32[1,40,72,136]{3,2,1,0:T(8,128)S(1)} %select_maximum_fusion.6, ...), kind=kLoop, calls=%fused_computation.245 | loop fusion | flops 13369344 | bytes 22290944 | tf_op jit(solution)/shard_map/sub | solution.py:139
  159.4 1.4 scatter-add.14
  160.7 41.4 %all-reduce.7.cloned.1.call-done = (f32[32,64,128]{2,1,0:T(8,128)}, f32[32,64,128]{2,1,0:T(8,128)}) async-done(((f32[32,64,128]{2,1,0:T(8,128)}, f32[32,64,128]{2,1,0:T(8,128)}), (f32[32,64,128]{2,1,0:T(8,128)}, f32[32,64,128]{2,1,0:T(8,128)})) %all-reduce.7.cloned.1.call-update) | async-done | bytes 2097168 | tf_op jit(solution)/shard_map/psum | solution.py:162
  202.1 3.0 %convolution_multiply_fusion = f32[32,128,64]{1,2,0:T(8,128)S(1)} fusion(f32[128,64]{0,1:T(8,128)S(1)} %copy.21, f32[32,64,128]{2,1,0:T(8,128)} %get-tuple-element.60, f32[32,64,128]{2,1,0:T(8,128)} %get-tuple-element.61), kind=kOutput, calls=%fused_computation.38 | convolution fusion | flops 202170368 | bytes 3178496 | tf_op jit(solution)/shard_map/xyz,yk->xzk/dot_general | solution.py:90
  205.2 1.3 convolution_multiply_fusion.1
  210.2 1.5 collective-permute-start.6
  213.0 1.3 dynamic-slice_bitcast_fusion
  214.4 2.2 copy.23
  216.6 1.7 gather_fusion
  218.4 4.5 %select_maximum_fusion = f32[2,1,40,72,136]{4,3,2,1,0:T(8,128)S(1)} fusion(f32[2,1,4,64,128]{4,3,2,1,0:T(8,128)} %collective-permute-done.7, f32[2,1,4,64,128]{4,3,2,1,0:T(8,128)S(1)} %collective-permute-done.6, f32[1,1,32,64,128]{4,3,2,1,0:T(8,128)S(1)} %bitcast.99, f32[1,1,32,64,128]{4,3,2,1,0:T(8,128)S(1)} %bitcast.108), kind=kLoop, calls=%fused_computation.6 | loop fusion | flops 14100480 | bytes 5754880 | tf_op jit(solution)/shard_map/concatenate | solution.py:26
  222.9 2.1 slice_bitcast_fusion.1
  225.0 35.2 %fusion.40 = f32[1,32,64,128]{3,2,1,0:T(8,128)} fusion(f32[1,40,72,136]{3,2,1,0:T(8,128)} %get-tuple-element.69, f32[1,40,72,136]{3,2,1,0:T(8,128)S(1)} %get-tuple-element.68, f32[64,32,128]{2,0,1:T(8,128)} %copy-done.5, f32[1,32,64,128]{3,2,1,0:T(8,128)} %copy-done.2, f32[128]{0:T(128)S(1)} %copy-done.13, f32[32,64]{1,0:T(8,128)S(1)} %broadcast_add_fusion, ...), kind=kLoop, calls=%fused_computation.80 | loop fusion | flops 19136512 | bytes 56631808 | tf_op jit(solution)/shard_map/add | solution.py:144
  260.2 6.2 %gather_fusion.1 = f32[256]{0:T(256)S(1)} fusion(f32[262144]{0:T(1024)} %bitcast.109, s32[1024]{0:T(1024)S(1)} %pad_clamp_fusion), kind=kCustom, calls=%fused_computation.1.clone | custom fusion | bytes 3072 | tf_op jit(solution)/shard_map/jit(take_along_axis)/gather | solution.py:175
  266.5 4.7 %psum.23 = f32[1,2,256]{2,1,0:T(2,128)} all-reduce(f32[1,2,256]{2,1,0:T(2,128)S(1)} %pad_maximum_fusion.6), channel_id=1, replica_groups=mesh['dom'=2,'shot'=8,'space'=2] {'space'}, use_global_device_ids=true, to_apply=%region_3.5 | all-reduce | flops 512 | bytes 4096 | tf_op jit(solution)/shard_map/psum | solution.py:179
  (82 shorter events, 23.9 us)
Async XLA Ops:
  7.2 17.7 %copy-start.3 = (f32[1,32,64,128]{3,2,1,0:T(8,128)S(1)}, f32[1,32,64,128]{3,2,1,0:T(8,128)}, u32[]{:S(2)}) copy-start(f32[1,32,64,128]{3,2,1,0:T(8,128)} %param.18) | copy-start | bytes 3145732
  7.2 12.5 %copy-start.15 = (f32[1,4]{1,0:T(1,128)S(1)}, f32[1,4]{1,0:T(1,128)}, u32[]{:S(2)}) copy-start(f32[1,4]{1,0:T(1,128)} %param.22) | copy-start | bytes 52
  7.2 59.5 %all-gather.2.cloned.1.call-start = ((), (), s32[]{:S(2)}) async-start(), calls=%async_computation | async-start | bytes 2359296 | tf_op jit(solution)/shard_map/all_gather | solution.py:124
  9.0 15.8 %collective-permute-start.1 = (f32[1,4,64,128]{3,2,1,0:T(8,128)S(1)}, f32[1,4,64,128]{3,2,1,0:T(8,128)S(1)}, u32[]{:S(2)}, u32[]{:S(2)}) collective-permute-start(f32[1,4,64,128]{3,2,1,0:T(8,128)S(1)} %get-tuple-element.80), channel_id=1, source_target_pairs={{0,1},{2,3},{4,5},{6,7},{8,9},{10,11},{12,13},{14,15},{16,17},{18,... | collective-permute-start | bytes 393224 | tf_op jit(solution)/shard_map/ppermute | solution.py:24
  11.3 13.8 %collective-permute-start = (f32[1,4,64,128]{3,2,1,0:T(8,128)}, f32[1,4,64,128]{3,2,1,0:T(8,128)S(1)}, u32[]{:S(2)}, u32[]{:S(2)}) collective-permute-start(f32[1,4,64,128]{3,2,1,0:T(8,128)} %get-tuple-element.81), channel_id=1, source_target_pairs={{1,0},{3,2},{5,4},{7,6},{9,8},{11,10},{13,12},{15,14},{17,16},{19,... | collective-permute-start | bytes 393224 | tf_op jit(solution)/shard_map/ppermute | solution.py:25
  14.4 187.8 %all-reduce.7.cloned.1.call-start = ((), (), s32[]{:S(2)}) async-start(), calls=%async_computation.1 | async-start | bytes 4194304 | tf_op jit(solution)/shard_map/psum | solution.py:162
  24.8 2.2 copy-start.11
  25.1 1.0 copy-start.7
  25.1 1.9 copy-start
  34.3 36.0 %copy-start.6 = (f32[1,32,64,128]{3,2,1,0:T(8,128)S(1)}, f32[1,32,64,128]{3,2,1,0:T(8,128)}, u32[]{:S(2)}) copy-start(f32[1,32,64,128]{3,2,1,0:T(8,128)} %get-tuple-element.67) | copy-start | bytes 3145732
  36.9 44.7 %copy-start.1 = (f32[1,262144]{1,0:T(1,128)}, f32[1,262144]{1,0:T(1,128)S(1)}, u32[]{:S(2)}) copy-start(f32[1,262144]{1,0:T(1,128)S(1)} %scatter-add.10) | copy-start | bytes 3145732
  71.8 2.8 %collective-permute-start.2 = (f32[2,1,4,64,128]{4,3,2,1,0:T(8,128)S(1)}, f32[2,1,4,64,128]{4,3,2,1,0:T(8,128)S(1)}, u32[]{:S(2)}, u32[]{:S(2)}) collective-permute-start(f32[2,1,4,64,128]{4,3,2,1,0:T(8,128)S(1)} %get-tuple-element.74), channel_id=1, source_target_pairs={{0,1},{2,3},{4,5},{6,7},{8,9},{10,11},{12,13},{14,15},{16,17},{18,... | collective-permute-start | bytes 786440 | tf_op jit(solution)/shard_map/ppermute | solution.py:24
  73.1 3.4 %collective-permute-start.3 = (f32[2,1,4,64,128]{4,3,2,1,0:T(8,128)S(1)}, f32[2,1,4,64,128]{4,3,2,1,0:T(8,128)S(1)}, u32[]{:S(2)}, u32[]{:S(2)}) collective-permute-start(f32[2,1,4,64,128]{4,3,2,1,0:T(8,128)S(1)} %get-tuple-element.75), channel_id=1, source_target_pairs={{1,0},{3,2},{5,4},{7,6},{9,8},{11,10},{13,12},{15,14},{17,16},{19,... | collective-permute-start | bytes 786440 | tf_op jit(solution)/shard_map/ppermute | solution.py:25
  81.2 1.2 copy-start.4
  81.2 1.2 copy-start.12
  90.7 1.5 copy-start.9
  92.2 19.5 %copy-start.14 = (f32[16,64]{1,0:T(8,128)S(1)}, f32[16,64]{1,0:T(8,128)}, u32[]{:S(2)}) copy-start(f32[16,64]{1,0:T(8,128)} %param.21) | copy-start | bytes 12292
  106.8 36.3 %collective-permute-start.4 = (f32[1,4,64,128]{3,2,1,0:T(8,128)S(1)}, f32[1,4,64,128]{3,2,1,0:T(8,128)S(1)}, u32[]{:S(2)}, u32[]{:S(2)}) collective-permute-start(f32[1,4,64,128]{3,2,1,0:T(8,128)S(1)} %get-tuple-element.77), channel_id=1, source_target_pairs={{1,0},{3,2},{5,4},{7,6},{9,8},{11,10},{13,12},{15,14},{17,16},{19,... | collective-permute-start | bytes 393224 | tf_op jit(solution)/shard_map/ppermute | solution.py:25
  108.1 35.0 %collective-permute-start.5 = (f32[1,4,64,128]{3,2,1,0:T(8,128)S(1)}, f32[1,4,64,128]{3,2,1,0:T(8,128)S(1)}, u32[]{:S(2)}, u32[]{:S(2)}) collective-permute-start(f32[1,4,64,128]{3,2,1,0:T(8,128)S(1)} %get-tuple-element.76), channel_id=1, source_target_pairs={{0,1},{2,3},{4,5},{6,7},{8,9},{10,11},{12,13},{14,15},{16,17},{18,... | collective-permute-start | bytes 393224 | tf_op jit(solution)/shard_map/ppermute | solution.py:24
  202.1 3.0 %copy-start.17 = (f32[32,64,128]{2,1,0:T(8,128)S(1)}, f32[32,64,128]{2,1,0:T(8,128)}, u32[]{:S(2)}) copy-start(f32[32,64,128]{2,1,0:T(8,128)} %get-tuple-element.60) | copy-start | bytes 3145732
  202.1 3.0 %copy-start.18 = (f32[32,64,128]{2,1,0:T(8,128)S(1)}, f32[32,64,128]{2,1,0:T(8,128)}, u32[]{:S(2)}) copy-start(f32[32,64,128]{2,1,0:T(8,128)} %get-tuple-element.61) | copy-start | bytes 3145732
  206.5 2.4 copy-start.10
  207.7 1.4 copy-start.8
  208.9 5.4 %copy-start.5 = (f32[64,32,128]{2,0,1:T(8,128)}, f32[64,32,128]{2,0,1:T(8,128)S(1)}, u32[]{:S(2)}) copy-start(f32[64,32,128]{2,0,1:T(8,128)S(1)} %fusion.6) | copy-start | bytes 3145732
  208.9 4.1 %copy-start.16 = (s32[1,256]{1,0:T(1,128)S(1)}, s32[1,256]{1,0:T(1,128)}, u32[]{:S(2)}) copy-start(s32[1,256]{1,0:T(1,128)} %param.24) | copy-start | bytes 3076
  209.1 9.2 %copy-start.2 = (f32[1,32,64,128]{3,2,1,0:T(8,128)}, f32[1,32,64,128]{3,2,1,0:T(8,128)S(1)}, u32[]{:S(2)}) copy-start(f32[1,32,64,128]{3,2,1,0:T(8,128)S(1)} %bitcast_multiply_fusion) | copy-start | bytes 3145732
  210.2 8.2 %collective-permute-start.6 = (f32[2,1,4,64,128]{4,3,2,1,0:T(8,128)}, f32[2,1,4,64,128]{4,3,2,1,0:T(8,128)S(1)}, u32[]{:S(2)}, u32[]{:S(2)}) collective-permute-start(f32[2,1,4,64,128]{4,3,2,1,0:T(8,128)} %get-tuple-element.72), channel_id=1, source_target_pairs={{0,1},{2,3},{4,5},{6,7},{8,9},{10,11},{12,13},{14,15},{16,17},{18,... | collective-permute-start | bytes 786440 | tf_op jit(solution)/shard_map/ppermute | solution.py:24
  211.7 6.7 %collective-permute-start.7 = (f32[2,1,4,64,128]{4,3,2,1,0:T(8,128)}, f32[2,1,4,64,128]{4,3,2,1,0:T(8,128)}, u32[]{:S(2)}, u32[]{:S(2)}) collective-permute-start(f32[2,1,4,64,128]{4,3,2,1,0:T(8,128)} %get-tuple-element.73), channel_id=1, source_target_pairs={{1,0},{3,2},{5,4},{7,6},{9,8},{11,10},{13,12},{15,14},{17,16},{19,... | collective-permute-start | bytes 786440 | tf_op jit(solution)/shard_map/ppermute | solution.py:25
  222.9 2.1 copy-start.13
Sparse Core Ops, SparseCore 0:
  14.5 52.1 all-gather.1
  100.6 101.5 all-reduce.6
where the time goes:
time: 279 us; the launch traced here: 278 us
  other arithmetic  95.6 us (34%)
  waiting for transfers between devices  73.2 us (26%)
  blocking collectives  36 us (13%)
  local copies, waits for them, and re-layouts  29.3 us (11%)
  between operations  23.6 us (8%)
  starting transfers between devices  13.6 us (5%)
  matrix products  6.7 us (2%)
    psum x1, waiting for transfers between devices, body(): image_all, light_all = lax.psum((image, light), 'shot')  41.4 us
    add x1, other arithmetic, advance(): 2.0 * born + speed_term * laplace(born_padded) - absorber * born  35.2 us
    all_gather x1, blocking collectives, body(): table_all = lax.all_gather(gains, 'shot', axis=0, tiled=True)  31.3 us
    all_gather x1, waiting for transfers between devices, body(): model = lax.all_gather(perturb, 'shot', axis=2, tiled=True)  29.7 us
    sub x3, other arithmetic, advance(): 2.0 * current - prior + drive - absorber * (current - prior)  26.4 us
    concatenate x4, other arithmetic, with_halo(): x = jnp.concatenate([before, x, after], axis=dim)  12.2 us
    ppermute x4, starting transfers between devices, with_halo(): before = lax.ppermute(last, axis, up)  8.22 us
    add x1, other arithmetic, body(): image = image + jnp.sum(drive * born_later, axis=0)  8.2 us
  transfers between devices with their start and end apart: 10, of which 3 were waited for; matrix products, arithmetic and copies ran while one was open for 16% of the time, Pallas kernels for 0%

commit v1 on v0

v1 whole, which is shorter than its diff:
```python
import math

import jax
import jax.numpy as jnp
from jax import lax
from jax.sharding import PartitionSpec as P

STEPS_A = 2
STEPS_B = 2


STENCIL = (-205.0 / 72.0, 8.0 / 5.0, -1.0 / 5.0, 8.0 / 315.0, -1.0 / 560.0)
damp_peak = 0.5
eps = 1e-05
HALO = 4


def coefficient(levels):
    speed = 1500.0 + 15.0 * levels.astype(jnp.float32)
    ratio = 0.45 * speed / 5325.0
    return ratio * ratio


def ramp(position, count, lower, upper):
    low_part = jnp.maximum(lower - position, 0.0) / lower
    high_part = jnp.maximum(upper - (count - 1.0 - position), 0.0) / upper
    return low_part * low_part + high_part * high_part


def damping(widths, positions, count_x, count_y, count_z):
    edges = widths.astype(jnp.float32)
    along_x = ramp(positions, count_x, edges[0], edges[1])
    along_y = ramp(jnp.arange(count_y, dtype=jnp.float32), count_y, edges[2], edges[3])
    along_z = ramp(jnp.arange(count_z, dtype=jnp.float32), count_z, edges[4], edges[5])
    return damp_peak * (along_x[:, None, None] + along_y[None, :, None] + along_z[None, None, :])


def with_halo(x):
    size = lax.axis_size("space")
    length = x.shape[0]
    if size == 2:
        me = lax.axis_index("space")
        piece = lax.dynamic_slice_in_dim(x, (1 - me) * (length - HALO), HALO, 0)
        got = lax.ppermute(piece, "space", [(0, 1), (1, 0)])
        zeros = jnp.zeros((HALO,) + x.shape[1:], x.dtype)
        padded = jnp.concatenate([zeros, x, zeros], axis=0)
        return lax.dynamic_update_slice_in_dim(padded, got, (1 - me) * (length + HALO), 0)
    up = [(i, (i + 1) % size) for i in range(size - 1)]
    down = [(j, i) for i, j in up]
    before = lax.ppermute(x[length - HALO :], "space", up)
    after = lax.ppermute(x[:HALO], "space", down)
    return jnp.concatenate([before, x, after], axis=0)


def laplace_x(padded):
    width_x = padded.shape[0] - 8
    width_y = padded.shape[1]
    width_z = padded.shape[2]
    full = jnp.pad(padded, [(0, 0), (4, 4), (4, 4)])

    def part(move_x, move_y, move_z):
        return full[
            4 + move_x : 4 + move_x + width_x,
            4 + move_y : 4 + move_y + width_y,
            4 + move_z : 4 + move_z + width_z,
        ]

    total = 3.0 * STENCIL[0] * part(0, 0, 0)
    for reach in range(1, 5):
        beside_all = (
            part(reach, 0, 0)
            + part(-reach, 0, 0)
            + part(0, reach, 0)
            + part(0, -reach, 0)
            + part(0, 0, reach)
            + part(0, 0, -reach)
        )
        total = total + STENCIL[reach] * beside_all
    return total


def lateral_filter(field, table):
    count = field.shape[1]
    index = jnp.arange(count)
    phase = index[:, None] * index[None, :] % count
    angle = 2.0 * math.pi / count * phase.astype(jnp.float32)
    cosine = jnp.cos(angle)
    sine = jnp.sin(angle)
    real_part = jnp.einsum("xyz,yk->xzk", field, cosine, precision=lax.Precision.HIGHEST)
    imag_part = jnp.einsum("xyz,yk->xzk", field, sine, precision=lax.Precision.HIGHEST)
    weight = table[None, :, :]
    back = jnp.einsum("xzk,yk->xyz", real_part * weight, cosine, precision=lax.Precision.HIGHEST)
    back = back + jnp.einsum(
        "xzk,yk->xyz", imag_part * weight, sine, precision=lax.Precision.HIGHEST
    )
    return back / count


def shot_bits(n):
    bits = []
    k = 1
    while k < n:
        bits.append(k)
        k *= 2
    assert k == n
    return bits


def gather_shot(block):
    n = lax.axis_size("shot")
    me = lax.axis_index("shot")
    held = block[None]
    for k in reversed(shot_bits(n)):
        theirs = lax.ppermute(held, "shot", [(i, i ^ k) for i in range(n)])
        low = (me // k) % 2 == 0
        pair = jnp.where(low, jnp.stack([held, theirs], axis=1), jnp.stack([theirs, held], axis=1))
        held = pair.reshape((-1,) + block.shape)
    return held


def scatter_shot(parts):
    n = lax.axis_size("shot")
    me = lax.axis_index("shot")
    held = parts
    for k in shot_bits(n):
        m = held.shape[0] // 2
        split = held.reshape((m, 2) + held.shape[1:])
        mine = (me // k) % 2
        keep = lax.dynamic_index_in_dim(split, mine, axis=1, keepdims=False)
        send = lax.dynamic_index_in_dim(split, 1 - mine, axis=1, keepdims=False)
        held = keep + lax.ppermute(send, "shot", [(i, i ^ k) for i in range(n)])
    return held[0]


def body(
    wave_prev,
    wave_now,
    velocity_code,
    perturb,
    gains,
    wavelet,
    source_index,
    receiver_index,
    absorb_width,
):
    shots, span_x, span_y, span_z = wave_now.shape
    n_shot = lax.axis_size("shot")
    me_shot = lax.axis_index("shot")
    start_x = lax.axis_index("space") * span_x
    total_x = span_x * lax.axis_size("space")
    speed_term = coefficient(velocity_code)
    positions = start_x.astype(jnp.float32) + jnp.arange(span_x, dtype=jnp.float32)
    absorber = damping(absorb_width, positions, total_x, span_y, span_z)
    term_flat = speed_term.reshape(-1)
    cells = span_x * span_y * span_z
    offset = start_x * span_y * span_z
    source_local = source_index - offset
    source_owned = (source_local >= 0) & (source_local < cells)
    source_safe = jnp.clip(source_local, 0, cells - 1)
    source_gain = jnp.where(source_owned, term_flat[source_safe], 0.0)

    depth = perturb.shape[2]
    dense = perturb.reshape(span_x, span_y * depth // span_z, span_z)
    blocks = gather_shot(dense)
    model = (
        blocks.reshape(n_shot, span_x, span_y, depth)
        .transpose(1, 2, 0, 3)
        .reshape(span_x, span_y, span_z)
    )
    table_all = gather_shot(gains).reshape(n_shot * gains.shape[0], gains.shape[1])

    def inject(field, moment):
        flat = field.reshape(1, -1)
        flat = flat.at[jnp.arange(1), source_safe].add(source_gain * wavelet[:, moment])
        return flat.reshape(field.shape)

    def wave_step(current, prior, moment, last):
        drive = speed_term * laplace_x(with_halo(current))
        if last:
            return None, drive
        later = inject(2.0 * current - prior + drive - absorber * (current - prior), moment)
        return later, drive

    def born_second(born, field_model, drive):
        return (
            2.0 * born
            + speed_term * laplace_x(with_halo(born))
            - absorber * born
            + field_model * drive
        )

    w0, wp = wave_now[0], wave_prev[0]
    w1, drive0 = wave_step(w0, wp, 0, False)
    w2, drive1 = wave_step(w1, w0, 1, False)
    w3, drive2 = wave_step(w2, w1, 2, False)
    _, drive3 = wave_step(w3, w2, 3, True)

    slab = span_x // n_shot
    light = drive0 * drive0 + drive1 * drive1
    light_part = scatter_shot(light.reshape(n_shot, slab, span_y, span_z))

    born1 = model * drive0
    born2 = born_second(born1, model, drive1)
    image = drive0 * born1 + drive1 * born2
    image_part = scatter_shot(image.reshape(n_shot, slab, span_y, span_z))

    table_x = table_all
    filt_part = lateral_filter(image_part / (light_part + eps), table_x)
    new_model = gather_shot(filt_part).reshape(span_x, span_y, span_z)
    filtered = lax.dynamic_slice_in_dim(new_model, me_shot * depth, depth, 2)

    b1 = new_model * drive2
    b2 = born_second(b1, new_model, drive3)

    receiver_local = receiver_index[0] - offset
    receiver_owned = (receiver_local >= 0) & (receiver_local < cells)
    receiver_safe = jnp.clip(receiver_local, 0, cells - 1)
    rx = receiver_safe // (span_y * span_z)
    ry = (receiver_safe // span_z) % span_y
    rz = receiver_safe % span_z
    lane = jnp.arange(span_z)[None, :] == rz[:, None]

    def sample(field):
        rows = field[rx, ry]
        picked = jnp.sum(jnp.where(lane, rows, 0.0), axis=1)
        return jnp.where(receiver_owned, picked, 0.0)

    records = jnp.stack([sample(b1), sample(b2)], axis=0)[None]
    traces = records + lax.ppermute(records, "space", [(0, 1), (1, 0)])
    return (filtered, b2[None], traces)


def solution(mesh):
    in_specs = (
        P(("dom", "shot"), "space", None, None),
        P(("dom", "shot"), "space", None, None),
        P(("dom", "space"), None, None),
        P(("dom", "space"), None, "shot"),
        P(("dom", "shot"), None),
        P(("dom", "shot"), None),
        P(("dom", "shot")),
        P(("dom", "shot"), None),
        P("dom"),
    )
    out_specs = (
        P(("dom", "space"), None, "shot"),
        P(("dom", "shot"), "space", None, None),
        P(("dom", "shot"), None, None),
    )
    return jax.shard_map(body, mesh=mesh, in_specs=in_specs, out_specs=out_specs, check_vma=False)
```

time: 279 us -> 206 us (0.74)
  other arithmetic: 95.6 us -> 42.4 us
  blocking collectives: 36 us -> 0 us
  starting transfers between devices: 13.6 us -> 27.6 us
  local copies, waits for them, and re-layouts: 29.3 us -> 43.2 us
  between operations: 23.6 us -> 10.2 us
  waiting for transfers between devices: 73.2 us -> 79.1 us
  matrix products: 6.7 us -> 1.7 us
    ppermute x8 -> x22, waiting for transfers between devices: 1.97 us -> 79.1 us  [the longest x9 57.5 us: gather_shot(): theirs = lax.ppermute(held, 'shot', [(i, i ^ k) for i in range(n)])]
    psum x1 -> x0, waiting for transfers between devices: 41.4 us -> none  [body(): image_all, light_all = lax.psum((image, light), 'shot')]
    add x6 -> x10, other arithmetic: 47.8 us -> 14.5 us  [the longest x1 7.06 us: born_second(): 2.0 * born + speed_term * laplace_x(with_halo(born)) - absorber * born]
    all_gather x1 -> x0, blocking collectives: 31.3 us -> none  [body(): table_all = lax.all_gather(gains, 'shot', axis=0, tiled=True)]
    all_gather x1 -> x0, waiting for transfers between devices: 29.7 us -> none  [body(): model = lax.all_gather(perturb, 'shot', axis=2, tiled=True)]
    sub x3, other arithmetic: 26.4 us -> 7.85 us  [wave_step(): 2.0 * current - prior + drive - absorber * (current - prior)]
    ppermute x8 -> x22, starting transfers between devices: 13.6 us -> 27.6 us  [the longest x9 13.9 us: gather_shot(): theirs = lax.ppermute(held, 'shot', [(i, i ^ k) for i in range(n)])]
    concatenate x4 -> x6, other arithmetic: 12.2 us -> 3.64 us  [the longest x5 3.61 us: with_halo(): padded = jnp.concatenate([zeros, x, zeros], axis=0)]
  transfers between devices with their start and end apart: 10 -> 22, of which waited for: 3 -> 14; matrix products, arithmetic and copies ran while one was open for 16% -> 18% of each run, Pallas kernels for 0% -> 0%
where the time goes in v1:
time: 206 us; the launch traced here: 204 us
  waiting for transfers between devices  79.1 us (38%)
  local copies, waits for them, and re-layouts  43.2 us (21%)
  other arithmetic  42.4 us (21%)
  starting transfers between devices  27.6 us (13%)
  between operations  10.2 us (5%)
    ppermute x9, waiting for transfers between devices, gather_shot(): theirs = lax.ppermute(held, 'shot', [(i, i ^ k) for i in range(n)])  57.5 us
    ppermute x6, waiting for transfers between devices, scatter_shot(): held = keep + lax.ppermute(send, 'shot', [(i, i ^ k) for i in range(n)])  19.3 us
    ppermute x9, starting transfers between devices, gather_shot(): theirs = lax.ppermute(held, 'shot', [(i, i ^ k) for i in range(n)])  13.9 us
    gather x2, local copies, waits for them, and re-layouts, sample(): rows = field[rx, ry]  11.8 us
    ppermute x6, starting transfers between devices, scatter_shot(): held = keep + lax.ppermute(send, 'shot', [(i, i ^ k) for i in range(n)])  11.8 us
    unnamed x54, local copies, waits for them, and re-layouts  7.94 us
    sub x3, other arithmetic, wave_step(): 2.0 * current - prior + drive - absorber * (current - prior)  7.85 us
    add x1, other arithmetic, born_second(): 2.0 * born + speed_term * laplace_x(with_halo(born)) - absorber * born  7.06 us
  transfers between devices with their start and end apart: 22, of which 14 were waited for; matrix products, arithmetic and copies ran while one was open for 18% of the time, Pallas kernels for 0%

profile of v1, /device:TPU:0, one launch (start us, length us, event | category | flops | bytes accessed | tf_op | source)
XLA Modules:
  0.0 204.2 jit_solution(6748828869746407363)
XLA Ops:
  1.9 4.1 %collective-permute-start.1 = (f32[1,32,8,128]{1,3,2,0:T(8,128)S(1)}, f32[1,32,8,128]{1,3,2,0:T(8,128)S(1)}, u32[]{:S(2)}, u32[]{:S(2)}) collective-permute-start(f32[1,32,8,128]{1,3,2,0:T(8,128)S(1)} %bitcast.165), channel_id=1, source_target_pairs={{0,8},{2,10},{4,12},{6,14},{8,0},{10,2},{12,4},{14,6},{1,9},{3,11}... | collective-permute-start | bytes 393224 | tf_op jit(solution)/shard_map/ppermute | solution.py:114
  6.0 1.6 dynamic-slice_bitcast_fusion.4
  10.3 18.8 %collective-permute-done.1 = f32[1,32,8,128]{1,3,2,0:T(8,128)S(1)} collective-permute-done((f32[1,32,8,128]{1,3,2,0:T(8,128)S(1)}, f32[1,32,8,128]{1,3,2,0:T(8,128)S(1)}, u32[]{:S(2)}, u32[]{:S(2)}) %collective-permute-start.1) | collective-permute-done | bytes 131104 | tf_op jit(solution)/shard_map/ppermute | solution.py:114
  30.2 1.9 fusion.193
  33.1 3.8 %collective-permute-done.2 = f32[2,32,8,128]{3,2,1,0:T(8,128)S(1)} collective-permute-done((f32[2,32,8,128]{3,2,1,0:T(8,128)S(1)}, f32[2,32,8,128]{3,2,1,0:T(8,128)S(1)}, u32[]{:S(2)}, u32[]{:S(2)}) %collective-permute-start.2) | collective-permute-done | bytes 262176 | tf_op jit(solution)/shard_map/ppermute | solution.py:114
  42.2 7.0 %collective-permute-done.3 = f32[4,32,8,128]{3,2,1,0:T(8,128)S(1)} collective-permute-done((f32[4,32,8,128]{3,2,1,0:T(8,128)S(1)}, f32[4,32,8,128]{3,2,1,0:T(8,128)S(1)}, u32[]{:S(2)}, u32[]{:S(2)}) %collective-permute-start.3) | collective-permute-done | bytes 524320 | tf_op jit(solution)/shard_map/ppermute | solution.py:114
  50.0 1.6 maximum_select_fusion
  51.7 2.7 %copy.70 = f32[4,2,32,8,128]{2,4,3,1,0:T(8,128)} copy(f32[4,2,32,8,128]{4,3,2,1,0:T(8,128)S(1)} %maximum_select_fusion) | data formatting | bytes 2097152 | tf_op jit(solution)/shard_map/jit(_where)/select_n | solution.py:116
  54.3 4.9 %copy.71 = f32[32,64,8,16]{1,3,2,0:T(8,128)} copy(f32[32,64,8,16]{0,3,1,2:T(8,128)} %bitcast.152) | data formatting | bytes 2097152 | tf_op jit(solution)/shard_map/transpose | solution.py:167
  59.2 3.2 %copy.72 = f32[32,64,128]{2,1,0:T(8,128)} copy(f32[32,64,128]{1,2,0:T(8,128)} %bitcast.160) | data formatting | bytes 2097152 | tf_op jit(solution)/shard_map/reshape | solution.py:168
  62.5 4.4 %fusion.211 = (f32[32,64,128]{2,1,0:T(8,128)}, f32[32,64,128]{2,1,0:T(8,128)S(1)}, f32[32,64,128]{2,1,0:T(8,128)S(1)}) fusion(f32[32,64,128]{2,1,0:T(8,128)} %copy.72, f32[40,64,128]{2,1,0:T(8,128)S(1)} %constant_dynamic-update-slice_fusion.5, s32[32,64,128]{2,1,0:T(8,128)S(1)} %copy-done), kind=kLoop, calls=%fused_computation.430 | loop fusion | flops 9437184 | bytes 15990784 | tf_op jit(solution)/shard_map/mul | solution.py:202
  73.5 1.6 constant_dynamic-slice_fusion.8
  76.3 3.6 %multiply_subtract_fusion.1 = (f32[32,64,128]{2,1,0:T(8,128)S(1)}, f32[32,64,128]{2,1,0:T(8,128)}) fusion(f32[32,64,128]{2,1,0:T(8,128)S(1)} %bitcast.150, f32[128]{0:T(128)S(1)} %copy-done.20, f32[32,64]{1,0:T(8,128)S(1)} %broadcast_add_fusion, f32[1,32,64,128]{3,2,1,0:T(8,128)S(1)} %copy-done.4, ...), kind=kLoop, calls=%fused_computation.311 | loop fusion | flops 11272192 | bytes 16007680 | tf_op jit(solution)/shard_map/sub | solution.py:181
  84.1 3.6 %multiply_subtract_fusion = (f32[32,64,128]{2,1,0:T(8,128)S(1)}, f32[32,64,128]{2,1,0:T(8,128)}) fusion(f32[32,64,128]{2,1,0:T(8,128)S(1)} %bitcast.158, f32[32,64,128]{2,1,0:T(8,128)S(1)} %bitcast.151, f32[128]{0:T(128)S(1)} %copy-done.21, f32[32,64]{1,0:T(8,128)S(1)} %broadcast_add_fusion, f32[40,64,128]{2,1,0:T(8,128)S(1)} %constant_dynamic-update-slice_fusion.2, ...), kind=kLoop, calls=%fused_computation.310 | loop fusion | flops 11272192 | bytes 16007680 | tf_op jit(solution)/shard_map/sub | solution.py:181
  92.7 1.9 pad_maximum_fusion
  95.5 3.7 %fusion.65 = (f32[32,64,128]{2,1,0:T(8,128)S(1)}, f32[32,64,128]{2,1,0:T(8,128)}) fusion(f32[32,64,128]{2,1,0:T(8,128)S(1)} %copy-done.11, f32[40,64,128]{2,1,0:T(8,128)S(1)} %constant_dynamic-update-slice_fusion.3, f32[32,64,128]{2,1,0:T(8,128)S(1)} %copy-done.7, f32[32,64,128]{2,1,0:T(8,128)S(1)} %copy-done.5, f32[32,64,128]{2,1,0:T(8,128)S(1)} %copy-done.9, ...), kind=kLoop, calls=%fused_computation.178 | loop fusion | flops 12845056 | bytes 18104832 | tf_op jit(solution)/shard_map/add | solution.py:204
  102.0 4.8 %collective-permute-start.12 = (f32[1,16,64]{2,1,0:T(8,128)}, f32[1,16,64]{2,1,0:T(8,128)}, u32[]{:S(2)}, u32[]{:S(2)}) collective-permute-start(f32[1,16,64]{2,1,0:T(8,128)} %bitcast.49), channel_id=1, source_target_pairs={{0,8},{2,10},{4,12},{6,14},{8,0},{10,2},{12,4},{14,6},{1,9},{3,11}... | collective-permute-start | bytes 12296 | tf_op jit(solution)/shard_map/ppermute | solution.py:114
  111.8 4.4 %collective-permute-done.6 = f32[4,4,64,128]{3,2,1,0:T(8,128)} collective-permute-done((f32[4,4,64,128]{3,2,1,0:T(8,128)}, f32[4,4,64,128]{3,2,1,0:T(8,128)}, u32[]{:S(2)}, u32[]{:S(2)}) %collective-permute-start.6) | collective-permute-done | bytes 524320 | tf_op jit(solution)/shard_map/ppermute | solution.py:131
  117.3 2.3 %collective-permute-start.7 = (f32[2,4,64,128]{3,2,1,0:T(8,128)S(1)}, f32[2,4,64,128]{3,2,1,0:T(8,128)S(1)}, u32[]{:S(2)}, u32[]{:S(2)}) collective-permute-start(f32[2,4,64,128]{3,2,1,0:T(8,128)S(1)} %dynamic-slice_bitcast_fusion.3), channel_id=1, source_target_pairs={{0,4},{2,6},{4,0},{6,2},{8,12},{10,14},{12,8},{14,10},{1,5},{3,7},... | collective-permute-start | bytes 786440 | tf_op jit(solution)/shard_map/ppermute | solution.py:131
  119.6 7.1 %collective-permute-done.9 = f32[4,4,64,128]{3,2,1,0:T(8,128)S(1)} collective-permute-done((f32[4,4,64,128]{3,2,1,0:T(8,128)S(1)}, f32[4,4,64,128]{3,2,1,0:T(8,128)S(1)}, u32[]{:S(2)}, u32[]{:S(2)}) %collective-permute-start.9) | collective-permute-done | bytes 524320 | tf_op jit(solution)/shard_map/ppermute | solution.py:131
  126.8 2.3 %collective-permute-start.10 = (f32[2,4,64,128]{3,2,1,0:T(8,128)S(1)}, f32[2,4,64,128]{3,2,1,0:T(8,128)S(1)}, u32[]{:S(2)}, u32[]{:S(2)}) collective-permute-start(f32[2,4,64,128]{3,2,1,0:T(8,128)S(1)} %dynamic-slice_bitcast_fusion.2), channel_id=1, source_target_pairs={{0,4},{2,6},{4,0},{6,2},{8,12},{10,14},{12,8},{14,10},{1,5},{3,7},... | collective-permute-start | bytes 786440 | tf_op jit(solution)/shard_map/ppermute | solution.py:131
  129.2 3.1 %collective-permute-start.8 = (f32[1,4,64,128]{3,2,1,0:T(8,128)S(1)}, f32[1,4,64,128]{3,2,1,0:T(8,128)S(1)}, u32[]{:S(2)}, u32[]{:S(2)}) collective-permute-start(f32[1,4,64,128]{3,2,1,0:T(8,128)S(1)} %constant_dynamic-slice_fusion.7), channel_id=1, source_target_pairs={{0,8},{2,10},{4,12},{6,14},{8,0},{10,2},{12,4},{14,6},{1,9},{3,11}... | collective-permute-start | bytes 393224 | tf_op jit(solution)/shard_map/ppermute | solution.py:131
  132.4 5.6 %collective-permute-done.10 = f32[2,4,64,128]{3,2,1,0:T(8,128)S(1)} collective-permute-done((f32[2,4,64,128]{3,2,1,0:T(8,128)S(1)}, f32[2,4,64,128]{3,2,1,0:T(8,128)S(1)}, u32[]{:S(2)}, u32[]{:S(2)}) %collective-permute-start.10) | collective-permute-done | bytes 262176 | tf_op jit(solution)/shard_map/ppermute | solution.py:131
  138.0 2.4 %collective-permute-start.11 = (f32[1,4,64,128]{3,2,1,0:T(8,128)S(1)}, f32[1,4,64,128]{3,2,1,0:T(8,128)S(1)}, u32[]{:S(2)}, u32[]{:S(2)}) collective-permute-start(f32[1,4,64,128]{3,2,1,0:T(8,128)S(1)} %constant_dynamic-slice_fusion.6), channel_id=1, source_target_pairs={{0,8},{2,10},{4,12},{6,14},{8,0},{10,2},{12,4},{14,6},{1,9},{3,11}... | collective-permute-start | bytes 393224 | tf_op jit(solution)/shard_map/ppermute | solution.py:131
  141.8 2.7 %collective-permute-done.14 = f32[4,16,64]{2,1,0:T(8,128)S(1)} collective-permute-done((f32[4,16,64]{2,1,0:T(8,128)S(1)}, f32[4,16,64]{2,1,0:T(8,128)S(1)}, u32[]{:S(2)}, u32[]{:S(2)}) %collective-permute-start.14) | collective-permute-done | bytes 16416 | tf_op jit(solution)/shard_map/ppermute | solution.py:114
  144.6 2.2 %collective-permute-done.11 = f32[1,4,64,128]{3,2,1,0:T(8,128)S(1)} collective-permute-done((f32[1,4,64,128]{3,2,1,0:T(8,128)S(1)}, f32[1,4,64,128]{3,2,1,0:T(8,128)S(1)}, u32[]{:S(2)}, u32[]{:S(2)}) %collective-permute-start.11) | collective-permute-done | bytes 131104 | tf_op jit(solution)/shard_map/ppermute | solution.py:131
  148.6 7.3 %collective-permute-done.15 = f32[1,4,64,128]{3,2,1,0:T(8,128)S(1)} collective-permute-done((f32[1,4,64,128]{3,2,1,0:T(8,128)S(1)}, f32[1,4,64,128]{3,2,1,0:T(8,128)S(1)}, u32[]{:S(2)}, u32[]{:S(2)}) %collective-permute-start.15) | collective-permute-done | bytes 131104 | tf_op jit(solution)/shard_map/ppermute | solution.py:114
  156.1 7.2 %collective-permute-done.16 = f32[2,4,64,128]{3,2,1,0:T(8,128)S(1)} collective-permute-done((f32[2,4,64,128]{3,2,1,0:T(8,128)S(1)}, f32[2,4,64,128]{3,2,1,0:T(8,128)S(1)}, u32[]{:S(2)}, u32[]{:S(2)}) %collective-permute-start.16) | collective-permute-done | bytes 262176 | tf_op jit(solution)/shard_map/ppermute | solution.py:114
  165.8 9.5 %collective-permute-done.17 = f32[4,4,64,128]{3,2,1,0:T(8,128)S(1)} collective-permute-done((f32[4,4,64,128]{3,2,1,0:T(8,128)S(1)}, f32[4,4,64,128]{3,2,1,0:T(8,128)S(1)}, u32[]{:S(2)}, u32[]{:S(2)}) %collective-permute-start.17) | collective-permute-done | bytes 524320 | tf_op jit(solution)/shard_map/ppermute | solution.py:114
  181.1 5.9 %gather_fusion = f32[256,128]{1,0:T(8,128)S(1)} fusion(f32[32,64,128]{2,1,0:T(8,128)} %bitcast_multiply_fusion, s32[256]{0:T(256)S(1)} %bitcast.144), kind=kCustom, calls=%fused_computation | custom fusion | bytes 264192 | tf_op jit(solution)/shard_map/gather | solution.py:224
  188.4 7.1 %fusion.118 = f32[32,64,128]{2,1,0:T(8,128)} fusion(f32[40,64,128]{2,1,0:T(8,128)S(1)} %constant_dynamic-update-slice_fusion.1, f32[40,64,128]{2,1,0:T(8,128)S(1)} %constant_dynamic-update-slice_fusion, f32[128]{0:T(128)S(1)} %copy-done.23, f32[32,64]{1,0:T(8,128)S(1)} %broadcast_add_fusion, f32[4,2,4,64,128]{4,3,2,1,0:T(8,128)} %copy-done.1, ...), kind=kLoop, calls=%fused_computation.231 | loop fusion | flops 19398656 | bytes 25707008 | tf_op jit(solution)/shard_map/add | solution.py:186
  195.5 5.9 %gather_fusion.1 = f32[256,128]{1,0:T(8,128)S(1)} fusion(f32[32,64,128]{2,1,0:T(8,128)} %fusion.118, s32[256]{0:T(256)S(1)} %bitcast.145), kind=kCustom, calls=%fused_computation.1 | custom fusion | bytes 264192 | tf_op jit(solution)/shard_map/gather | solution.py:224
  (153 shorter events, 45.8 us)
Async XLA Ops:
  1.9 27.3 %collective-permute-start.1 = (f32[1,32,8,128]{1,3,2,0:T(8,128)S(1)}, f32[1,32,8,128]{1,3,2,0:T(8,128)S(1)}, u32[]{:S(2)}, u32[]{:S(2)}) collective-permute-start(f32[1,32,8,128]{1,3,2,0:T(8,128)S(1)} %bitcast.165), channel_id=1, source_target_pairs={{0,8},{2,10},{4,12},{6,14},{8,0},{10,2},{12,4},{14,6},{1,9},{3,11}... | collective-permute-start | bytes 393224 | tf_op jit(solution)/shard_map/ppermute | solution.py:114
  7.6 33.8 %collective-permute-start = (f32[4,64,128]{2,1,0:T(8,128)}, f32[4,64,128]{2,1,0:T(8,128)}, u32[]{:S(2)}, u32[]{:S(2)}) collective-permute-start(f32[4,64,128]{2,1,0:T(8,128)} %dynamic-slice_bitcast_fusion.4), channel_id=1, source_target_pairs={{0,1},{1,0},{2,3},{3,2},{4,5},{5,4},{6,7},{7,6},{8,9},{9,8},{10,11... | collective-permute-start | bytes 393224 | tf_op jit(solution)/shard_map/ppermute | solution.py:44
  8.9 23.4 %copy-start.24 = (f32[1,4]{1,0:T(1,128)S(1)}, f32[1,4]{1,0:T(1,128)}, u32[]{:S(2)}) copy-start(f32[1,4]{1,0:T(1,128)} %param.20) | copy-start | bytes 52
  29.4 7.6 %collective-permute-start.2 = (f32[2,32,8,128]{3,2,1,0:T(8,128)S(1)}, f32[2,32,8,128]{3,2,1,0:T(8,128)S(1)}, u32[]{:S(2)}, u32[]{:S(2)}) collective-permute-start(f32[2,32,8,128]{3,2,1,0:T(8,128)S(1)} %maximum_select_fusion.5), channel_id=1, source_target_pairs={{0,4},{2,6},{4,0},{6,2},{8,12},{10,14},{12,8},{14,10},{1,5},{3,7},... | collective-permute-start | bytes 786440 | tf_op jit(solution)/shard_map/ppermute | solution.py:114
  32.2 8.9 %copy-start.3 = (f32[1,32,64,128]{3,2,1,0:T(8,128)S(1)}, f32[1,32,64,128]{3,2,1,0:T(8,128)}, u32[]{:S(2)}) copy-start(f32[1,32,64,128]{3,2,1,0:T(8,128)} %param.16) | copy-start | bytes 3145732
  37.0 4.3 %copy-start.15 = (f32[2,2,32,8,128]{4,3,2,1,0:T(8,128)}, f32[2,2,32,8,128]{4,3,2,1,0:T(8,128)S(1)}, u32[]{:S(2)}) copy-start(f32[2,2,32,8,128]{4,3,2,1,0:T(8,128)S(1)} %maximum_select_fusion.2) | copy-start | bytes 1572868
  37.0 12.3 %collective-permute-start.3 = (f32[4,32,8,128]{3,2,1,0:T(8,128)S(1)}, f32[4,32,8,128]{3,2,1,0:T(8,128)S(1)}, u32[]{:S(2)}, u32[]{:S(2)}) collective-permute-start(f32[4,32,8,128]{3,2,1,0:T(8,128)S(1)} %bitcast.176), channel_id=1, source_target_pairs={{0,2},{2,0},{4,6},{6,4},{8,10},{10,8},{12,14},{14,12},{1,3},{3,1},... | collective-permute-start | bytes 1572872 | tf_op jit(solution)/shard_map/ppermute | solution.py:114
  59.2 3.2 %copy-start = (s32[32,64,128]{2,1,0:T(8,128)S(1)}, s32[32,64,128]{2,1,0:T(8,128)}, u32[]{:S(2)}) copy-start(s32[32,64,128]{2,1,0:T(8,128)} %param.17) | copy-start | bytes 3145732
  62.5 6.3 %copy-start.16 = (f32[1,32,64,128]{3,2,1,0:T(8,128)S(1)}, f32[1,32,64,128]{3,2,1,0:T(8,128)}, u32[]{:S(2)}) copy-start(f32[1,32,64,128]{3,2,1,0:T(8,128)} %param.15) | copy-start | bytes 3145732
  62.5 6.3 %copy-start.19 = (f32[128]{0:T(128)S(1)}, f32[128]{0:T(128)}, u32[]{:S(2)}) copy-start(f32[128]{0:T(128)} %fusion.193) | copy-start | bytes 1540
  72.2 3.5 %collective-permute-start.4 = (f32[4,64,128]{2,1,0:T(8,128)S(1)}, f32[4,64,128]{2,1,0:T(8,128)S(1)}, u32[]{:S(2)}, u32[]{:S(2)}) collective-permute-start(f32[4,64,128]{2,1,0:T(8,128)S(1)} %constant_dynamic-slice_fusion.9), channel_id=1, source_target_pairs={{0,1},{1,0},{2,3},{3,2},{4,5},{5,4},{6,7},{7,6},{8,9},{9,8},{10,11... | collective-permute-start | bytes 393224 | tf_op jit(solution)/shard_map/ppermute | solution.py:44
  75.0 19.5 %collective-permute-start.5 = (f32[4,64,128]{2,1,0:T(8,128)}, f32[4,64,128]{2,1,0:T(8,128)}, u32[]{:S(2)}, u32[]{:S(2)}) collective-permute-start(f32[4,64,128]{2,1,0:T(8,128)} %constant_dynamic-slice_fusion.8), channel_id=1, source_target_pairs={{0,1},{1,0},{2,3},{3,2},{4,5},{5,4},{6,7},{7,6},{8,9},{9,8},{10,11... | collective-permute-start | bytes 393224 | tf_op jit(solution)/shard_map/ppermute | solution.py:44
  82.5 1.6 collective-permute-start.18
  99.2 7.6 %copy-start.12 = (f32[32,64,128]{2,1,0:T(8,128)S(1)}, f32[32,64,128]{2,1,0:T(8,128)}, u32[]{:S(2)}) copy-start(f32[32,64,128]{2,1,0:T(8,128)} %get-tuple-element.73) | copy-start | bytes 3145732
  101.1 15.1 %copy-start.14 = (f32[32,64,128]{2,1,0:T(8,128)S(1)}, f32[32,64,128]{2,1,0:T(8,128)}, u32[]{:S(2)}) copy-start(f32[32,64,128]{2,1,0:T(8,128)} %copy-done.13) | copy-start | bytes 3145732
  101.1 15.1 %collective-permute-start.6 = (f32[4,4,64,128]{3,2,1,0:T(8,128)}, f32[4,4,64,128]{3,2,1,0:T(8,128)}, u32[]{:S(2)}, u32[]{:S(2)}) collective-permute-start(f32[4,4,64,128]{3,2,1,0:T(8,128)} %dynamic-slice_bitcast_fusion.1), channel_id=1, source_target_pairs={{0,2},{2,0},{4,6},{6,4},{8,10},{10,8},{12,14},{14,12},{1,3},{3,1},... | collective-permute-start | bytes 1572872 | tf_op jit(solution)/shard_map/ppermute | solution.py:131
  102.0 6.8 %collective-permute-start.12 = (f32[1,16,64]{2,1,0:T(8,128)}, f32[1,16,64]{2,1,0:T(8,128)}, u32[]{:S(2)}, u32[]{:S(2)}) collective-permute-start(f32[1,16,64]{2,1,0:T(8,128)} %bitcast.49), channel_id=1, source_target_pairs={{0,8},{2,10},{4,12},{6,14},{8,0},{10,2},{12,4},{14,6},{1,9},{3,11}... | collective-permute-start | bytes 12296 | tf_op jit(solution)/shard_map/ppermute | solution.py:114
  106.9 19.8 %collective-permute-start.9 = (f32[4,4,64,128]{3,2,1,0:T(8,128)S(1)}, f32[4,4,64,128]{3,2,1,0:T(8,128)S(1)}, u32[]{:S(2)}, u32[]{:S(2)}) collective-permute-start(f32[4,4,64,128]{3,2,1,0:T(8,128)S(1)} %dynamic-slice_bitcast_fusion), channel_id=1, source_target_pairs={{0,2},{2,0},{4,6},{6,4},{8,10},{10,8},{12,14},{14,12},{1,3},{3,1},... | collective-permute-start | bytes 1572872 | tf_op jit(solution)/shard_map/ppermute | solution.py:131
  109.6 30.9 %collective-permute-start.13 = (f32[2,16,64]{2,1,0:T(8,128)S(1)}, f32[2,16,64]{2,1,0:T(8,128)S(1)}, u32[]{:S(2)}, u32[]{:S(2)}) collective-permute-start(f32[2,16,64]{2,1,0:T(8,128)S(1)} %maximum_select_fusion.11), channel_id=1, source_target_pairs={{0,4},{2,6},{4,0},{6,2},{8,12},{10,14},{12,8},{14,10},{1,5},{3,7},... | collective-permute-start | bytes 24584 | tf_op jit(solution)/shard_map/ppermute | solution.py:114
  117.3 11.9 %collective-permute-start.7 = (f32[2,4,64,128]{3,2,1,0:T(8,128)S(1)}, f32[2,4,64,128]{3,2,1,0:T(8,128)S(1)}, u32[]{:S(2)}, u32[]{:S(2)}) collective-permute-start(f32[2,4,64,128]{3,2,1,0:T(8,128)S(1)} %dynamic-slice_bitcast_fusion.3), channel_id=1, source_target_pairs={{0,4},{2,6},{4,0},{6,2},{8,12},{10,14},{12,8},{14,10},{1,5},{3,7},... | collective-permute-start | bytes 786440 | tf_op jit(solution)/shard_map/ppermute | solution.py:131
  126.8 11.2 %collective-permute-start.10 = (f32[2,4,64,128]{3,2,1,0:T(8,128)S(1)}, f32[2,4,64,128]{3,2,1,0:T(8,128)S(1)}, u32[]{:S(2)}, u32[]{:S(2)}) collective-permute-start(f32[2,4,64,128]{3,2,1,0:T(8,128)S(1)} %dynamic-slice_bitcast_fusion.2), channel_id=1, source_target_pairs={{0,4},{2,6},{4,0},{6,2},{8,12},{10,14},{12,8},{14,10},{1,5},{3,7},... | collective-permute-start | bytes 786440 | tf_op jit(solution)/shard_map/ppermute | solution.py:131
  129.2 15.3 %collective-permute-start.8 = (f32[1,4,64,128]{3,2,1,0:T(8,128)S(1)}, f32[1,4,64,128]{3,2,1,0:T(8,128)S(1)}, u32[]{:S(2)}, u32[]{:S(2)}) collective-permute-start(f32[1,4,64,128]{3,2,1,0:T(8,128)S(1)} %constant_dynamic-slice_fusion.7), channel_id=1, source_target_pairs={{0,8},{2,10},{4,12},{6,14},{8,0},{10,2},{12,4},{14,6},{1,9},{3,11}... | collective-permute-start | bytes 393224 | tf_op jit(solution)/shard_map/ppermute | solution.py:131
  138.0 8.7 %collective-permute-start.11 = (f32[1,4,64,128]{3,2,1,0:T(8,128)S(1)}, f32[1,4,64,128]{3,2,1,0:T(8,128)S(1)}, u32[]{:S(2)}, u32[]{:S(2)}) collective-permute-start(f32[1,4,64,128]{3,2,1,0:T(8,128)S(1)} %constant_dynamic-slice_fusion.6), channel_id=1, source_target_pairs={{0,8},{2,10},{4,12},{6,14},{8,0},{10,2},{12,4},{14,6},{1,9},{3,11}... | collective-permute-start | bytes 393224 | tf_op jit(solution)/shard_map/ppermute | solution.py:131
  140.5 4.0 %collective-permute-start.14 = (f32[4,16,64]{2,1,0:T(8,128)S(1)}, f32[4,16,64]{2,1,0:T(8,128)S(1)}, u32[]{:S(2)}, u32[]{:S(2)}) collective-permute-start(f32[4,16,64]{2,1,0:T(8,128)S(1)} %bitcast.192), channel_id=1, source_target_pairs={{0,2},{2,0},{4,6},{6,4},{8,10},{10,8},{12,14},{14,12},{1,3},{3,1},... | collective-permute-start | bytes 49160 | tf_op jit(solution)/shard_map/ppermute | solution.py:114
  148.6 7.4 %collective-permute-start.15 = (f32[1,4,64,128]{3,2,1,0:T(8,128)S(1)}, f32[1,4,64,128]{3,2,1,0:T(8,128)S(1)}, u32[]{:S(2)}, u32[]{:S(2)}) collective-permute-start(f32[1,4,64,128]{3,2,1,0:T(8,128)S(1)} %bitcast.182), channel_id=1, source_target_pairs={{0,8},{2,10},{4,12},{6,14},{8,0},{10,2},{12,4},{14,6},{1,9},{3,11}... | collective-permute-start | bytes 393224 | tf_op jit(solution)/shard_map/ppermute | solution.py:114
  156.0 7.3 %collective-permute-start.16 = (f32[2,4,64,128]{3,2,1,0:T(8,128)S(1)}, f32[2,4,64,128]{3,2,1,0:T(8,128)S(1)}, u32[]{:S(2)}, u32[]{:S(2)}) collective-permute-start(f32[2,4,64,128]{3,2,1,0:T(8,128)S(1)} %maximum_select_fusion.7), channel_id=1, source_target_pairs={{0,4},{2,6},{4,0},{6,2},{8,12},{10,14},{12,8},{14,10},{1,5},{3,7},... | collective-permute-start | bytes 786440 | tf_op jit(solution)/shard_map/ppermute | solution.py:114
  156.0 7.4 %copy-start.25 = (s32[1,256]{1,0:T(1,128)S(1)}, s32[1,256]{1,0:T(1,128)}, u32[]{:S(2)}) copy-start(s32[1,256]{1,0:T(1,128)} %param.22) | copy-start | bytes 3076
  163.3 12.0 %collective-permute-start.17 = (f32[4,4,64,128]{3,2,1,0:T(8,128)S(1)}, f32[4,4,64,128]{3,2,1,0:T(8,128)S(1)}, u32[]{:S(2)}, u32[]{:S(2)}) collective-permute-start(f32[4,4,64,128]{3,2,1,0:T(8,128)S(1)} %bitcast.174), channel_id=1, source_target_pairs={{0,2},{2,0},{4,6},{6,4},{8,10},{10,8},{12,14},{14,12},{1,3},{3,1},... | collective-permute-start | bytes 1572872 | tf_op jit(solution)/shard_map/ppermute | solution.py:114
  164.4 1.4 collective-permute-start.20
  181.0 7.3 %collective-permute-start.19 = (f32[4,64,128]{2,1,0:T(8,128)S(1)}, f32[4,64,128]{2,1,0:T(8,128)S(1)}, u32[]{:S(2)}, u32[]{:S(2)}) collective-permute-start(f32[4,64,128]{2,1,0:T(8,128)S(1)} %constant_dynamic-slice_fusion.2), channel_id=1, source_target_pairs={{0,1},{1,0},{2,3},{3,2},{4,5},{5,4},{6,7},{7,6},{8,9},{9,8},{10,11... | collective-permute-start | bytes 393224 | tf_op jit(solution)/shard_map/ppermute | solution.py:44
  195.5 6.7 %copy-start.2 = (f32[4,2,4,64,128]{4,3,2,1,0:T(8,128)S(1)}, f32[4,2,4,64,128]{4,3,2,1,0:T(8,128)}, u32[]{:S(2)}) copy-start(f32[4,2,4,64,128]{4,3,2,1,0:T(8,128)} %copy-done.1) | copy-start | bytes 3145732
  201.7 1.9 collective-permute-start.21
  (16 other events, 30.0 us)

commit v2 on v1

--- a/solution.py
+++ b/solution.py
@@ -106,30 +106,24 @@
     return bits
 
 
-def gather_shot(block):
+def ag_step(held, k):
     n = lax.axis_size("shot")
     me = lax.axis_index("shot")
-    held = block[None]
-    for k in reversed(shot_bits(n)):
-        theirs = lax.ppermute(held, "shot", [(i, i ^ k) for i in range(n)])
-        low = (me // k) % 2 == 0
-        pair = jnp.where(low, jnp.stack([held, theirs], axis=1), jnp.stack([theirs, held], axis=1))
-        held = pair.reshape((-1,) + block.shape)
-    return held
-
-
-def scatter_shot(parts):
+    theirs = lax.ppermute(held, "shot", [(i, i ^ k) for i in range(n)])
+    low = (me // k) % 2 == 0
+    pair = jnp.where(low, jnp.stack([held, theirs], axis=1), jnp.stack([theirs, held], axis=1))
+    return pair.reshape((-1,) + held.shape[1:])
+
+
+def rs_step(held, k):
     n = lax.axis_size("shot")
     me = lax.axis_index("shot")
-    held = parts
-    for k in shot_bits(n):
-        m = held.shape[0] // 2
-        split = held.reshape((m, 2) + held.shape[1:])
-        mine = (me // k) % 2
-        keep = lax.dynamic_index_in_dim(split, mine, axis=1, keepdims=False)
-        send = lax.dynamic_index_in_dim(split, 1 - mine, axis=1, keepdims=False)
-        held = keep + lax.ppermute(send, "shot", [(i, i ^ k) for i in range(n)])
-    return held[0]
+    m = held.shape[0] // 2
+    split = held.reshape((m, 2) + held.shape[1:])
+    mine = (me // k) % 2
+    keep = lax.dynamic_index_in_dim(split, mine, axis=1, keepdims=False)
+    send = lax.dynamic_index_in_dim(split, 1 - mine, axis=1, keepdims=False)
+    return keep + lax.ppermute(send, "shot", [(i, i ^ k) for i in range(n)])
 
 
 def body(
@@ -146,6 +140,7 @@
     shots, span_x, span_y, span_z = wave_now.shape
     n_shot = lax.axis_size("shot")
     me_shot = lax.axis_index("shot")
+    bits = shot_bits(n_shot)
     start_x = lax.axis_index("space") * span_x
     total_x = span_x * lax.axis_size("space")
     speed_term = coefficient(velocity_code)
@@ -158,16 +153,7 @@
     source_owned = (source_local >= 0) & (source_local < cells)
     source_safe = jnp.clip(source_local, 0, cells - 1)
     source_gain = jnp.where(source_owned, term_flat[source_safe], 0.0)
-
-    depth = perturb.shape[2]
-    dense = perturb.reshape(span_x, span_y * depth // span_z, span_z)
-    blocks = gather_shot(dense)
-    model = (
-        blocks.reshape(n_shot, span_x, span_y, depth)
-        .transpose(1, 2, 0, 3)
-        .reshape(span_x, span_y, span_z)
-    )
-    table_all = gather_shot(gains).reshape(n_shot * gains.shape[0], gains.shape[1])
+    barrier = lax.optimization_barrier
 
     def inject(field, moment):
         flat = field.reshape(1, -1)
@@ -189,39 +175,93 @@
             + field_model * drive
         )
 
-    w0, wp = wave_now[0], wave_prev[0]
-    w1, drive0 = wave_step(w0, wp, 0, False)
-    w2, drive1 = wave_step(w1, w0, 1, False)
-    w3, drive2 = wave_step(w2, w1, 2, False)
-    _, drive3 = wave_step(w3, w2, 3, True)
-
     slab = span_x // n_shot
-    light = drive0 * drive0 + drive1 * drive1
-    light_part = scatter_shot(light.reshape(n_shot, slab, span_y, span_z))
-
-    born1 = model * drive0
-    born2 = born_second(born1, model, drive1)
-    image = drive0 * born1 + drive1 * born2
-    image_part = scatter_shot(image.reshape(n_shot, slab, span_y, span_z))
-
-    table_x = table_all
-    filt_part = lateral_filter(image_part / (light_part + eps), table_x)
-    new_model = gather_shot(filt_part).reshape(span_x, span_y, span_z)
+    depth = perturb.shape[2]
+    model_held = perturb.transpose(2, 0, 1).reshape(1, depth, span_x * span_y)
+    gains_held = gains[None]
+    st = {"w0": wave_now[0], "wp": wave_prev[0]}
+
+    def task_wave(i):
+        def run():
+            last = i == 3
+            cur, pri = (st["w0"], st["wp"]) if i == 0 else (st["w%d" % i], st["w%d" % (i - 1)])
+            later, drive = wave_step(cur, pri, i, last)
+            st["drive%d" % i] = drive
+            if not last:
+                st["w%d" % (i + 1)] = later
+        return run
+
+    tasks = [task_wave(0), task_wave(1), task_wave(2)]
+    keys = []
+    for i, k in enumerate(reversed(bits)):
+        model_held = ag_step(model_held, k)
+        gains_held = ag_step(gains_held, k)
+        if i < len(tasks):
+            tasks[i]()
+        keys = sorted(st.keys())
+        out = barrier((model_held, gains_held, [st[n] for n in keys]))
+        model_held, gains_held = out[0], out[1]
+        st.update(zip(keys, out[2]))
+    for i in range(len(bits), len(tasks)):
+        tasks[i]()
+
+    light = st["drive0"] * st["drive0"] + st["drive1"] * st["drive1"]
+    light_held = light.reshape(n_shot, slab, span_y, span_z)
+
+    def born_one():
+        model = model_held.reshape(span_z, span_x * span_y).T.reshape(span_x, span_y, span_z)
+        st["model"] = model
+        st["born1"] = model * st["drive0"]
+
+    def born_two():
+        st["born2"] = born_second(st["born1"], st["model"], st["drive1"])
+
+    tasks = [born_one, born_two]
+    for i, k in enumerate(bits):
+        light_held = rs_step(light_held, k)
+        if i < len(tasks):
+            tasks[i]()
+        keys = sorted(st.keys())
+        out = barrier((light_held, [st[n] for n in keys]))
+        light_held = out[0]
+        st.update(zip(keys, out[1]))
+    for i in range(len(bits), len(tasks)):
+        tasks[i]()
+
+    image = st["drive0"] * st["born1"] + st["drive1"] * st["born2"]
+    image_held = image.reshape(n_shot, slab, span_y, span_z)
+    tasks = [task_wave(3)]
+    for i, k in enumerate(bits):
+        image_held = rs_step(image_held, k)
+        if i < len(tasks):
+            tasks[i]()
+        keys = sorted(st.keys())
+        out = barrier((image_held, [st[n] for n in keys]))
+        image_held = out[0]
+        st.update(zip(keys, out[1]))
+    for i in range(len(bits), len(tasks)):
+        tasks[i]()
+
+    table_all = gains_held.reshape(n_shot * gains.shape[0], gains.shape[1])
+    filt_part = lateral_filter(image_held[0] / (light_held[0] + eps), table_all)
+    filt_held = filt_part[None]
+    for k in reversed(bits):
+        filt_held = ag_step(filt_held, k)
+    new_model = filt_held.reshape(span_x, span_y, span_z)
     filtered = lax.dynamic_slice_in_dim(new_model, me_shot * depth, depth, 2)
 
-    b1 = new_model * drive2
-    b2 = born_second(b1, new_model, drive3)
+    b1 = new_model * st["drive2"]
+    b2 = born_second(b1, new_model, st["drive3"])
 
     receiver_local = receiver_index[0] - offset
     receiver_owned = (receiver_local >= 0) & (receiver_local < cells)
     receiver_safe = jnp.clip(receiver_local, 0, cells - 1)
-    rx = receiver_safe // (span_y * span_z)
-    ry = (receiver_safe // span_z) % span_y
+    row = receiver_safe // span_z
     rz = receiver_safe % span_z
     lane = jnp.arange(span_z)[None, :] == rz[:, None]
 
     def sample(field):
-        rows = field[rx, ry]
+        rows = jnp.take(field.reshape(span_x * span_y, span_z), row, axis=0)
         picked = jnp.sum(jnp.where(lane, rows, 0.0), axis=1)
         return jnp.where(receiver_owned, picked, 0.0)
 

time: 206 us -> 175 us (0.85)
  local copies, waits for them, and re-layouts: 43.2 us -> 22.2 us
  starting transfers between devices: 27.6 us -> 20.3 us
  waiting for transfers between devices: 79.1 us -> 74.6 us
  other arithmetic: 42.4 us -> 45.8 us
    gather x2, local copies, waits for them, and re-layouts: 11.8 us -> 1.87 us  [sample(): rows = jnp.take(field.reshape(span_x * span_y, span_z), row, axis=0)]
    ppermute x15, starting transfers between devices: 25.7 us -> 18.8 us  [the longest x9 9.8 us: ag_step(): theirs = lax.ppermute(held, 'shot', [(i, i ^ k) for i in range(n)])]
    sub x3, other arithmetic: 7.85 us -> 12 us  [wave_step(): 2.0 * current - prior + drive - absorber * (current - prior)]
    reshape x1 -> x0, local copies, waits for them, and re-layouts: 3.24 us -> none  [body(): model = blocks.reshape(n_shot, span_x, span_y, depth).transpose(1, 2, 0,...]
    unnamed x54 -> x49, local copies, waits for them, and re-layouts: 7.94 us -> 5.07 us
    concatenate x5 -> x6, other arithmetic: 3.61 us -> 0.78 us  [with_halo(): padded = jnp.concatenate([zeros, x, zeros], axis=0)]
    ppermute x15, waiting for transfers between devices: 76.9 us -> 74.1 us  [the longest x6 45.5 us: rs_step(): return keep + lax.ppermute(send, 'shot', [(i, i ^ k) for i in range(n)])]
    transpose x1 -> x2, local copies, waits for them, and re-layouts: 4.89 us -> 2.34 us  [the longest x1 1.31 us: born_one(): model_held.reshape(span_z, span_x * span_y)]
  transfers between devices with their start and end apart: 22 -> 22, of which waited for: 14 -> 14; matrix products, arithmetic and copies ran while one was open for 18% -> 25% of each run, Pallas kernels for 0% -> 0%
where the time goes in v2:
time: 175 us
  waiting for transfers between devices  74.6 us (43%)
  other arithmetic  45.8 us (26%)
  local copies, waits for them, and re-layouts  22.2 us (13%)
  starting transfers between devices  20.3 us (12%)
  between operations  9.87 us (6%)
    ppermute x6, waiting for transfers between devices, rs_step(): return keep + lax.ppermute(send, 'shot', [(i, i ^ k) for i in range(n)])  45.5 us
    ppermute x9, waiting for transfers between devices, ag_step(): theirs = lax.ppermute(held, 'shot', [(i, i ^ k) for i in range(n)])  28.6 us
    sub x3, other arithmetic, wave_step(): 2.0 * current - prior + drive - absorber * (current - prior)  12 us
    ppermute x9, starting transfers between devices, ag_step(): theirs = lax.ppermute(held, 'shot', [(i, i ^ k) for i in range(n)])  9.8 us
    ppermute x6, starting transfers between devices, rs_step(): return keep + lax.ppermute(send, 'shot', [(i, i ^ k) for i in range(n)])  8.97 us
    add x2, other arithmetic, born_second(): 2.0 * born + speed_term * laplace_x(with_halo(born)) - absorber * born  6.51 us
    select_n x10, other arithmetic, ag_step(): jnp.where(low, jnp.stack([held, theirs], axis=1), jnp.stack([theirs, held...  6.04 us
    unnamed x49, local copies, waits for them, and re-layouts  5.07 us
  transfers between devices with their start and end apart: 22, of which 14 were waited for; matrix products, arithmetic and copies ran while one was open for 25% of the time, Pallas kernels for 0%

profile of v2, /device:TPU:0, one launch (start us, length us, event | category | flops | bytes accessed | tf_op | source)
XLA Modules:
  0.0 174.5 jit_solution(7343775463715152729)
XLA Ops:
  0.6 1.7 dynamic-slice_bitcast_fusion.4
  4.6 3.6 %collective-permute-start = (f32[1,16,2048]{2,1,0:T(8,128)}, f32[1,16,2048]{2,1,0:T(8,128)}, u32[]{:S(2)}, u32[]{:S(2)}) collective-permute-start(f32[1,16,2048]{2,1,0:T(8,128)} %stack.117), channel_id=1, source_target_pairs={{0,8},{2,10},{4,12},{6,14},{8,0},{10,2},{12,4},{14,6},{1,9},{3,11}... | collective-permute-start | bytes 393224 | tf_op jit(solution)/shard_map/ppermute | solution.py:112
  9.5 1.4 fusion.202
  13.8 1.8 %fusion.182 = f32[128]{0:T(128)} fusion(f32[]{:T(128)} %bitcast.11, f32[]{:T(128)} %bitcast.10), kind=kLoop, calls=%fused_computation.387 | loop fusion | flops 1280 | bytes 520 | tf_op jit(solution)/shard_map/add | solution.py:27
  17.0 1.4 maximum_select_fusion.9
  19.4 4.7 %multiply_subtract_fusion.2 = (f32[32,64,128]{2,1,0:T(8,128)S(1)}, f32[32,64,128]{2,1,0:T(8,128)}, f32[32,64,128]{2,1,0:T(8,128)S(1)}) fusion(f32[128]{0:T(128)} %fusion.182, f32[32,64]{1,0:T(8,128)S(1)} %broadcast_add_fusion, f32[1,32,64,128]{3,2,1,0:T(8,128)} %param.17, f32[1,32,64,128]{3,2,1,0:T(8,128)} %param.18, ...), kind=kLoop, calls=%fused_computation.306 | loop fusion | flops 11272192 | bytes 17056256 | tf_op jit(solution)/shard_map/sub | solution.py:167
  29.9 1.7 collective-permute-start.4
  34.5 3.6 %multiply_subtract_fusion.1 = (f32[32,64,128]{2,1,0:T(8,128)S(1)}, f32[32,64,128]{2,1,0:T(8,128)}) fusion(f32[32,64,128]{2,1,0:T(8,128)S(1)} %bitcast.115, f32[32,64,128]{2,1,0:T(8,128)S(1)} %bitcast.124, f32[128]{0:T(128)S(1)} %copy-done.16, f32[32,64]{1,0:T(8,128)S(1)} %broadcast_add_fusion, f32[40,64,128]{2,1,0:T(8,128)S(1)} %constant_dynamic-update-slice_fusion.4, ...), kind=kLoop, calls=%fused_computation.305 | loop fusion | flops 11272192 | bytes 16007680 | tf_op jit(solution)/shard_map/sub | solution.py:167
  43.0 1.6 collective-permute-start.7
  45.3 1.7 collective-permute-done.7
  47.7 3.6 %multiply_subtract_fusion = (f32[32,64,128]{2,1,0:T(8,128)S(1)}, f32[32,64,128]{2,1,0:T(8,128)}) fusion(f32[32,64,128]{2,1,0:T(8,128)S(1)} %bitcast.122, f32[32,64,128]{2,1,0:T(8,128)S(1)} %bitcast.116, f32[128]{0:T(128)S(1)} %copy-done.17, f32[32,64]{1,0:T(8,128)S(1)} %broadcast_add_fusion, f32[40,64,128]{2,1,0:T(8,128)S(1)} %constant_dynamic-update-slice_fusion.3, ...), kind=kLoop, calls=%fused_computation.304 | loop fusion | flops 11272192 | bytes 16007680 | tf_op jit(solution)/shard_map/sub | solution.py:167
  55.9 3.3 %collective-permute-done.6 = f32[4,16,2048]{2,1,0:T(8,128)} collective-permute-done((f32[4,16,2048]{2,1,0:T(8,128)}, f32[4,16,2048]{2,1,0:T(8,128)}, u32[]{:S(2)}, u32[]{:S(2)}) %collective-permute-start.6) | collective-permute-done | bytes 524320 | tf_op jit(solution)/shard_map/ppermute | solution.py:112
  59.2 1.6 maximum_select_fusion
  62.2 1.9 %fusion.201 = (f32[32,64,128]{2,1,0:T(8,128)S(1)}, f32[32,64,128]{2,1,0:T(8,128)S(1)}) fusion(f32[32,64,128]{2,1,0:T(8,128)} %bitcast.126, f32[32,64,128]{2,1,0:T(8,128)} %get-tuple-element.117, f32[32,64,128]{2,1,0:T(8,128)S(1)} %copy-done.1), kind=kLoop, calls=%fused_computation.413 | loop fusion | flops 1048576 | bytes 5242880 | tf_op jit(solution)/shard_map/mul | solution.py:214
  66.7 12.7 %collective-permute-done.9 = f32[4,4,64,128]{3,2,1,0:T(8,128)} collective-permute-done((f32[4,4,64,128]{3,2,1,0:T(8,128)}, f32[4,4,64,128]{3,2,1,0:T(8,128)}, u32[]{:S(2)}, u32[]{:S(2)}) %collective-permute-start.9) | collective-permute-done | bytes 524320 | tf_op jit(solution)/shard_map/ppermute | solution.py:126
  80.8 1.5 collective-permute-start.10
  82.5 3.6 %fusion.88 = f32[32,64,128]{2,1,0:T(8,128)} fusion(f32[40,64,128]{2,1,0:T(8,128)S(1)} %constant_dynamic-update-slice_fusion.2, f32[32,64,128]{2,1,0:T(8,128)S(1)} %bitcast.127, f32[32,64,128]{2,1,0:T(8,128)S(1)} %copy-done.1, f32[32,64,128]{2,1,0:T(8,128)S(1)} %get-tuple-element.118, f32[128]{0:T(128)S(1)} %copy-done.18, ...), kind=kLoop, calls=%fused_computation.201 | loop fusion | flops 11272192 | bytes 16007680 | tf_op jit(solution)/shard_map/add | solution.py:172
  86.1 3.5 %collective-permute-done.10 = f32[2,4,64,128]{3,2,1,0:T(8,128)S(1)} collective-permute-done((f32[2,4,64,128]{3,2,1,0:T(8,128)S(1)}, f32[2,4,64,128]{3,2,1,0:T(8,128)S(1)}, u32[]{:S(2)}, u32[]{:S(2)}) %collective-permute-start.10) | collective-permute-done | bytes 262176 | tf_op jit(solution)/shard_map/ppermute | solution.py:126
  90.3 2.6 %collective-permute-start.12 = (f32[1,4,64,128]{3,2,1,0:T(8,128)}, f32[1,4,64,128]{3,2,1,0:T(8,128)}, u32[]{:S(2)}, u32[]{:S(2)}) collective-permute-start(f32[1,4,64,128]{3,2,1,0:T(8,128)} %constant_dynamic-slice_fusion.4), channel_id=1, source_target_pairs={{0,8},{2,10},{4,12},{6,14},{8,0},{10,2},{12,4},{14,6},{1,9},{3,11}... | collective-permute-start | bytes 393224 | tf_op jit(solution)/shard_map/ppermute | solution.py:126
  92.9 6.5 %collective-permute-done.12 = f32[1,4,64,128]{3,2,1,0:T(8,128)} collective-permute-done((f32[1,4,64,128]{3,2,1,0:T(8,128)}, f32[1,4,64,128]{3,2,1,0:T(8,128)}, u32[]{:S(2)}, u32[]{:S(2)}) %collective-permute-start.12) | collective-permute-done | bytes 131104 | tf_op jit(solution)/shard_map/ppermute | solution.py:126
  99.4 1.6 dynamic-slice_add_fusion.1
  102.0 2.0 %multiply_add_fusion = f32[32,64,128]{2,1,0:T(8,128)S(1)} fusion(f32[32,64,128]{2,1,0:T(8,128)S(1)} %copy-done.1, f32[32,64,128]{2,1,0:T(8,128)} %fusion.88, f32[32,64,128]{2,1,0:T(8,128)} %get-tuple-element.117, f32[32,64,128]{2,1,0:T(8,128)S(1)} %get-tuple-element.118), kind=kLoop, calls=%fused_computation.302 | loop fusion | flops 786432 | bytes 5242880 | tf_op jit(solution)/shard_map/add | solution.py:231
  105.3 3.2 %fusion.113 = f32[32,64,128]{2,1,0:T(8,128)} fusion(f32[40,64,128]{2,1,0:T(8,128)S(1)} %constant_dynamic-update-slice_fusion.1, s32[32,64,128]{2,1,0:T(8,128)S(1)} %copy-done), kind=kLoop, calls=%fused_computation.226 | loop fusion | flops 9175040 | bytes 12845056 | tf_op jit(solution)/shard_map/mul | solution.py:164
  108.6 9.8 %collective-permute-done.13 = f32[4,4,64,128]{3,2,1,0:T(8,128)S(1)} collective-permute-done((f32[4,4,64,128]{3,2,1,0:T(8,128)S(1)}, f32[4,4,64,128]{3,2,1,0:T(8,128)S(1)}, u32[]{:S(2)}, u32[]{:S(2)}) %collective-permute-start.13) | collective-permute-done | bytes 524320 | tf_op jit(solution)/shard_map/ppermute | solution.py:126
  119.2 7.3 %collective-permute-done.15 = f32[2,4,64,128]{3,2,1,0:T(8,128)S(1)} collective-permute-done((f32[2,4,64,128]{3,2,1,0:T(8,128)S(1)}, f32[2,4,64,128]{3,2,1,0:T(8,128)S(1)}, u32[]{:S(2)}, u32[]{:S(2)}) %collective-permute-start.15) | collective-permute-done | bytes 262176 | tf_op jit(solution)/shard_map/ppermute | solution.py:126
  126.6 2.3 %collective-permute-start.16 = (f32[1,4,64,128]{3,2,1,0:T(8,128)S(1)}, f32[1,4,64,128]{3,2,1,0:T(8,128)S(1)}, u32[]{:S(2)}, u32[]{:S(2)}) collective-permute-start(f32[1,4,64,128]{3,2,1,0:T(8,128)S(1)} %constant_dynamic-slice_fusion.2), channel_id=1, source_target_pairs={{0,8},{2,10},{4,12},{6,14},{8,0},{10,2},{12,4},{14,6},{1,9},{3,11}... | collective-permute-start | bytes 393224 | tf_op jit(solution)/shard_map/ppermute | solution.py:126
  129.0 5.6 %collective-permute-done.16 = f32[1,4,64,128]{3,2,1,0:T(8,128)S(1)} collective-permute-done((f32[1,4,64,128]{3,2,1,0:T(8,128)S(1)}, f32[1,4,64,128]{3,2,1,0:T(8,128)S(1)}, u32[]{:S(2)}, u32[]{:S(2)}) %collective-permute-start.16) | collective-permute-done | bytes 131104 | tf_op jit(solution)/shard_map/ppermute | solution.py:126
  136.6 8.1 %collective-permute-done.17 = f32[1,4,64,128]{3,2,1,0:T(8,128)S(1)} collective-permute-done((f32[1,4,64,128]{3,2,1,0:T(8,128)S(1)}, f32[1,4,64,128]{3,2,1,0:T(8,128)S(1)}, u32[]{:S(2)}, u32[]{:S(2)}) %collective-permute-start.17) | collective-permute-done | bytes 131104 | tf_op jit(solution)/shard_map/ppermute | solution.py:112
  144.8 6.6 %collective-permute-done.18 = f32[2,4,64,128]{3,2,1,0:T(8,128)S(1)} collective-permute-done((f32[2,4,64,128]{3,2,1,0:T(8,128)S(1)}, f32[2,4,64,128]{3,2,1,0:T(8,128)S(1)}, u32[]{:S(2)}, u32[]{:S(2)}) %collective-permute-start.18) | collective-permute-done | bytes 262176 | tf_op jit(solution)/shard_map/ppermute | solution.py:112
  151.5 1.6 collective-permute-start.19
  154.8 8.3 %collective-permute-done.19 = f32[4,4,64,128]{3,2,1,0:T(8,128)S(1)} collective-permute-done((f32[4,4,64,128]{3,2,1,0:T(8,128)S(1)}, f32[4,4,64,128]{3,2,1,0:T(8,128)S(1)}, u32[]{:S(2)}, u32[]{:S(2)}) %collective-permute-start.19) | collective-permute-done | bytes 524320 | tf_op jit(solution)/shard_map/ppermute | solution.py:112
  167.7 2.9 %fusion.141 = f32[32,64,128]{2,1,0:T(8,128)S(1)} fusion(f32[40,64,128]{2,1,0:T(8,128)S(1)} %constant_dynamic-update-slice_fusion, f32[32,64,128]{2,1,0:T(8,128)S(1)} %copy-done.9, f32[128]{0:T(128)S(1)} %copy-done.19, f32[32,64]{1,0:T(8,128)S(1)} %broadcast_add_fusion, f32[4,2,4,64,128]{4,3,2,1,0:T(8,128)S(1)} %copy.41, f32[32,64,128]{2,1,0:T(8,128)S(1)} %copy-done.5, ...), kind=kLoop, calls=%fused_computation.254 | loop fusion | flops 11534336 | bytes 16007680 | tf_op jit(solution)/shard_map/add | solution.py:172
  (150 shorter events, 41.4 us)
Async XLA Ops:
  0.6 10.3 %copy-start.2 = (f32[1,32,64,128]{3,2,1,0:T(8,128)S(1)}, f32[1,32,64,128]{3,2,1,0:T(8,128)}, u32[]{:S(2)}) copy-start(f32[1,32,64,128]{3,2,1,0:T(8,128)} %param.18) | copy-start | bytes 3145732
  2.3 16.1 %collective-permute-start.2 = (f32[4,64,128]{2,1,0:T(8,128)}, f32[4,64,128]{2,1,0:T(8,128)}, u32[]{:S(2)}, u32[]{:S(2)}) collective-permute-start(f32[4,64,128]{2,1,0:T(8,128)} %dynamic-slice_bitcast_fusion.4), channel_id=1, source_target_pairs={{0,1},{1,0},{2,3},{3,2},{4,5},{5,4},{6,7},{7,6},{8,9},{9,8},{10,11... | collective-permute-start | bytes 393224 | tf_op jit(solution)/shard_map/ppermute | solution.py:44
  4.6 23.9 %collective-permute-start = (f32[1,16,2048]{2,1,0:T(8,128)}, f32[1,16,2048]{2,1,0:T(8,128)}, u32[]{:S(2)}, u32[]{:S(2)}) collective-permute-start(f32[1,16,2048]{2,1,0:T(8,128)} %stack.117), channel_id=1, source_target_pairs={{0,8},{2,10},{4,12},{6,14},{8,0},{10,2},{12,4},{14,6},{1,9},{3,11}... | collective-permute-start | bytes 393224 | tf_op jit(solution)/shard_map/ppermute | solution.py:112
  8.2 8.9 %collective-permute-start.1 = (f32[1,16,64]{2,1,0:T(8,128)}, f32[1,16,64]{2,1,0:T(8,128)}, u32[]{:S(2)}, u32[]{:S(2)}) collective-permute-start(f32[1,16,64]{2,1,0:T(8,128)} %bitcast.162), channel_id=1, source_target_pairs={{0,8},{2,10},{4,12},{6,14},{8,0},{10,2},{12,4},{14,6},{1,9},{3,11}... | collective-permute-start | bytes 12296 | tf_op jit(solution)/shard_map/ppermute | solution.py:112
  11.0 8.4 %copy-start = (s32[32,64,128]{2,1,0:T(8,128)S(1)}, s32[32,64,128]{2,1,0:T(8,128)}, u32[]{:S(2)}) copy-start(s32[32,64,128]{2,1,0:T(8,128)} %param.19) | copy-start | bytes 3145732
  29.6 4.3 %copy-start.15 = (f32[2,16,64]{2,1,0:T(8,128)S(1)}, f32[2,16,64]{2,1,0:T(8,128)}, u32[]{:S(2)}) copy-start(f32[2,16,64]{2,1,0:T(8,128)} %maximum_select_fusion.9) | copy-start | bytes 24580
  29.6 4.9 %copy-start.3 = (f32[1,32,64,128]{3,2,1,0:T(8,128)S(1)}, f32[1,32,64,128]{3,2,1,0:T(8,128)}, u32[]{:S(2)}) copy-start(f32[1,32,64,128]{3,2,1,0:T(8,128)} %param.18) | copy-start | bytes 3145732
  29.6 4.9 %copy-start.16 = (f32[128]{0:T(128)S(1)}, f32[128]{0:T(128)}, u32[]{:S(2)}) copy-start(f32[128]{0:T(128)} %fusion.182) | copy-start | bytes 1540
  29.6 4.9 %collective-permute-start.5 = (f32[4,64,128]{2,1,0:T(8,128)S(1)}, f32[4,64,128]{2,1,0:T(8,128)S(1)}, u32[]{:S(2)}, u32[]{:S(2)}) collective-permute-start(f32[4,64,128]{2,1,0:T(8,128)S(1)} %constant_dynamic-slice_fusion.9), channel_id=1, source_target_pairs={{0,1},{1,0},{2,3},{3,2},{4,5},{5,4},{6,7},{7,6},{8,9},{9,8},{10,11... | collective-permute-start | bytes 393224 | tf_op jit(solution)/shard_map/ppermute | solution.py:44
  29.9 3.9 %collective-permute-start.4 = (f32[2,16,64]{2,1,0:T(8,128)}, f32[2,16,64]{2,1,0:T(8,128)S(1)}, u32[]{:S(2)}, u32[]{:S(2)}) collective-permute-start(f32[2,16,64]{2,1,0:T(8,128)} %maximum_select_fusion.9), channel_id=1, source_target_pairs={{0,4},{2,6},{4,0},{6,2},{8,12},{10,14},{12,8},{14,10},{1,5},{3,7},... | collective-permute-start | bytes 24584 | tf_op jit(solution)/shard_map/ppermute | solution.py:112
  32.4 8.5 %collective-permute-start.3 = (f32[2,16,2048]{2,1,0:T(8,128)S(1)}, f32[2,16,2048]{2,1,0:T(8,128)}, u32[]{:S(2)}, u32[]{:S(2)}) collective-permute-start(f32[2,16,2048]{2,1,0:T(8,128)S(1)} %maximum_select_fusion.4), channel_id=1, source_target_pairs={{0,4},{2,6},{4,0},{6,2},{8,12},{10,14},{12,8},{14,10},{1,5},{3,7},... | collective-permute-start | bytes 786440 | tf_op jit(solution)/shard_map/ppermute | solution.py:112
  42.9 4.7 %copy-start.17 = (f32[128]{0:T(128)S(1)}, f32[128]{0:T(128)}, u32[]{:S(2)}) copy-start(f32[128]{0:T(128)} %fusion.182) | copy-start | bytes 1540
  42.9 4.7 %collective-permute-start.8 = (f32[4,64,128]{2,1,0:T(8,128)S(1)}, f32[4,64,128]{2,1,0:T(8,128)S(1)}, u32[]{:S(2)}, u32[]{:S(2)}) collective-permute-start(f32[4,64,128]{2,1,0:T(8,128)S(1)} %constant_dynamic-slice_fusion.7), channel_id=1, source_target_pairs={{0,1},{1,0},{2,3},{3,2},{4,5},{5,4},{6,7},{7,6},{8,9},{9,8},{10,11... | collective-permute-start | bytes 393224 | tf_op jit(solution)/shard_map/ppermute | solution.py:44
  43.0 4.0 %collective-permute-start.7 = (f32[4,16,64]{2,1,0:T(8,128)S(1)}, f32[4,16,64]{2,1,0:T(8,128)S(1)}, u32[]{:S(2)}, u32[]{:S(2)}) collective-permute-start(f32[4,16,64]{2,1,0:T(8,128)S(1)} %bitcast.155), channel_id=1, source_target_pairs={{0,2},{2,0},{4,6},{6,4},{8,10},{10,8},{12,14},{14,12},{1,3},{3,1},... | collective-permute-start | bytes 49160 | tf_op jit(solution)/shard_map/ppermute | solution.py:112
  44.8 14.4 %collective-permute-start.6 = (f32[4,16,2048]{2,1,0:T(8,128)}, f32[4,16,2048]{2,1,0:T(8,128)}, u32[]{:S(2)}, u32[]{:S(2)}) collective-permute-start(f32[4,16,2048]{2,1,0:T(8,128)} %bitcast.22), channel_id=1, source_target_pairs={{0,2},{2,0},{4,6},{6,4},{8,10},{10,8},{12,14},{14,12},{1,3},{3,1},... | collective-permute-start | bytes 1572872 | tf_op jit(solution)/shard_map/ppermute | solution.py:112
  65.9 13.5 %collective-permute-start.9 = (f32[4,4,64,128]{3,2,1,0:T(8,128)}, f32[4,4,64,128]{3,2,1,0:T(8,128)}, u32[]{:S(2)}, u32[]{:S(2)}) collective-permute-start(f32[4,4,64,128]{3,2,1,0:T(8,128)} %dynamic-slice_bitcast_fusion.1), channel_id=1, source_target_pairs={{0,2},{2,0},{4,6},{6,4},{8,10},{10,8},{12,14},{14,12},{1,3},{3,1},... | collective-permute-start | bytes 1572872 | tf_op jit(solution)/shard_map/ppermute | solution.py:126
  80.7 1.8 %collective-permute-start.11 = (f32[4,64,128]{2,1,0:T(8,128)S(1)}, f32[4,64,128]{2,1,0:T(8,128)S(1)}, u32[]{:S(2)}, u32[]{:S(2)}) collective-permute-start(f32[4,64,128]{2,1,0:T(8,128)S(1)} %constant_dynamic-slice_fusion.5), channel_id=1, source_target_pairs={{0,1},{1,0},{2,3},{3,2},{4,5},{5,4},{6,7},{7,6},{8,9},{9,8},{10,11... | collective-permute-start | bytes 393224 | tf_op jit(solution)/shard_map/ppermute | solution.py:44
  80.8 8.8 %collective-permute-start.10 = (f32[2,4,64,128]{3,2,1,0:T(8,128)S(1)}, f32[2,4,64,128]{3,2,1,0:T(8,128)S(1)}, u32[]{:S(2)}, u32[]{:S(2)}) collective-permute-start(f32[2,4,64,128]{3,2,1,0:T(8,128)S(1)} %dynamic-slice_bitcast_fusion.3), channel_id=1, source_target_pairs={{0,4},{2,6},{4,0},{6,2},{8,12},{10,14},{12,8},{14,10},{1,5},{3,7},... | collective-permute-start | bytes 786440 | tf_op jit(solution)/shard_map/ppermute | solution.py:126
  90.3 9.1 %collective-permute-start.12 = (f32[1,4,64,128]{3,2,1,0:T(8,128)}, f32[1,4,64,128]{3,2,1,0:T(8,128)}, u32[]{:S(2)}, u32[]{:S(2)}) collective-permute-start(f32[1,4,64,128]{3,2,1,0:T(8,128)} %constant_dynamic-slice_fusion.4), channel_id=1, source_target_pairs={{0,8},{2,10},{4,12},{6,14},{8,0},{10,2},{12,4},{14,6},{1,9},{3,11}... | collective-permute-start | bytes 393224 | tf_op jit(solution)/shard_map/ppermute | solution.py:126
  101.9 3.4 %collective-permute-start.14 = (f32[4,64,128]{2,1,0:T(8,128)S(1)}, f32[4,64,128]{2,1,0:T(8,128)S(1)}, u32[]{:S(2)}, u32[]{:S(2)}) collective-permute-start(f32[4,64,128]{2,1,0:T(8,128)S(1)} %constant_dynamic-slice_fusion.3), channel_id=1, source_target_pairs={{0,1},{1,0},{2,3},{3,2},{4,5},{5,4},{6,7},{7,6},{8,9},{9,8},{10,11... | collective-permute-start | bytes 393224 | tf_op jit(solution)/shard_map/ppermute | solution.py:44
  104.0 14.4 %collective-permute-start.13 = (f32[4,4,64,128]{3,2,1,0:T(8,128)S(1)}, f32[4,4,64,128]{3,2,1,0:T(8,128)S(1)}, u32[]{:S(2)}, u32[]{:S(2)}) collective-permute-start(f32[4,4,64,128]{3,2,1,0:T(8,128)S(1)} %dynamic-slice_bitcast_fusion), channel_id=1, source_target_pairs={{0,2},{2,0},{4,6},{6,4},{8,10},{10,8},{12,14},{14,12},{1,3},{3,1},... | collective-permute-start | bytes 1572872 | tf_op jit(solution)/shard_map/ppermute | solution.py:126
  108.6 20.3 %copy-start.12 = (f32[4,2,16,64]{3,2,1,0:T(8,128)S(1)}, f32[4,2,16,64]{3,2,1,0:T(8,128)}, u32[]{:S(2)}) copy-start(f32[4,2,16,64]{3,2,1,0:T(8,128)} %copy.34) | copy-start | bytes 98308
  118.5 16.1 %copy-start.13 = (f32[1,4,64,128]{3,2,1,0:T(8,128)S(1)}, f32[1,4,64,128]{3,2,1,0:T(8,128)}, u32[]{:S(2)}) copy-start(f32[1,4,64,128]{3,2,1,0:T(8,128)} %dynamic-slice_add_fusion.1) | copy-start | bytes 393220
  118.5 8.0 %collective-permute-start.15 = (f32[2,4,64,128]{3,2,1,0:T(8,128)S(1)}, f32[2,4,64,128]{3,2,1,0:T(8,128)S(1)}, u32[]{:S(2)}, u32[]{:S(2)}) collective-permute-start(f32[2,4,64,128]{3,2,1,0:T(8,128)S(1)} %dynamic-slice_bitcast_fusion.2), channel_id=1, source_target_pairs={{0,4},{2,6},{4,0},{6,2},{8,12},{10,14},{12,8},{14,10},{1,5},{3,7},... | collective-permute-start | bytes 786440 | tf_op jit(solution)/shard_map/ppermute | solution.py:126
  126.6 8.0 %collective-permute-start.16 = (f32[1,4,64,128]{3,2,1,0:T(8,128)S(1)}, f32[1,4,64,128]{3,2,1,0:T(8,128)S(1)}, u32[]{:S(2)}, u32[]{:S(2)}) collective-permute-start(f32[1,4,64,128]{3,2,1,0:T(8,128)S(1)} %constant_dynamic-slice_fusion.2), channel_id=1, source_target_pairs={{0,8},{2,10},{4,12},{6,14},{8,0},{10,2},{12,4},{14,6},{1,9},{3,11}... | collective-permute-start | bytes 393224 | tf_op jit(solution)/shard_map/ppermute | solution.py:126
  134.6 10.2 %copy-start.21 = (s32[1,256]{1,0:T(1,128)S(1)}, s32[1,256]{1,0:T(1,128)}, u32[]{:S(2)}) copy-start(s32[1,256]{1,0:T(1,128)} %param.24) | copy-start | bytes 3076
  136.4 8.3 %collective-permute-start.17 = (f32[1,4,64,128]{3,2,1,0:T(8,128)S(1)}, f32[1,4,64,128]{3,2,1,0:T(8,128)S(1)}, u32[]{:S(2)}, u32[]{:S(2)}) collective-permute-start(f32[1,4,64,128]{3,2,1,0:T(8,128)S(1)} %bitcast.145), channel_id=1, source_target_pairs={{0,8},{2,10},{4,12},{6,14},{8,0},{10,2},{12,4},{14,6},{1,9},{3,11}... | collective-permute-start | bytes 393224 | tf_op jit(solution)/shard_map/ppermute | solution.py:112
  144.7 6.7 %collective-permute-start.18 = (f32[2,4,64,128]{3,2,1,0:T(8,128)S(1)}, f32[2,4,64,128]{3,2,1,0:T(8,128)S(1)}, u32[]{:S(2)}, u32[]{:S(2)}) collective-permute-start(f32[2,4,64,128]{3,2,1,0:T(8,128)S(1)} %maximum_select_fusion.6), channel_id=1, source_target_pairs={{0,4},{2,6},{4,0},{6,2},{8,12},{10,14},{12,8},{14,10},{1,5},{3,7},... | collective-permute-start | bytes 786440 | tf_op jit(solution)/shard_map/ppermute | solution.py:112
  151.5 11.6 %collective-permute-start.19 = (f32[4,4,64,128]{3,2,1,0:T(8,128)S(1)}, f32[4,4,64,128]{3,2,1,0:T(8,128)S(1)}, u32[]{:S(2)}, u32[]{:S(2)}) collective-permute-start(f32[4,4,64,128]{3,2,1,0:T(8,128)S(1)} %bitcast.139), channel_id=1, source_target_pairs={{0,2},{2,0},{4,6},{6,4},{8,10},{10,8},{12,14},{14,12},{1,3},{3,1},... | collective-permute-start | bytes 1572872 | tf_op jit(solution)/shard_map/ppermute | solution.py:112
  165.3 1.6 collective-permute-start.20
  167.7 4.0 %copy-start.23 = (pred[256]{0:T(512)(128)(4,1)S(1)}, pred[256]{0:T(512)(128)(4,1)}, u32[]{:S(2)}) copy-start(pred[256]{0:T(512)(128)(4,1)} %get-tuple-element.159) | copy-start | bytes 772
  172.0 1.9 %collective-permute-start.21 = (f32[1,2,256]{2,1,0:T(2,128)S(1)}, f32[1,2,256]{2,1,0:T(2,128)S(1)}, u32[]{:S(2)}, u32[]{:S(2)}) collective-permute-start(f32[1,2,256]{2,1,0:T(2,128)S(1)} %maximum_bitcast_fusion), channel_id=1, source_target_pairs={{0,1},{1,0},{2,3},{3,2},{4,5},{5,4},{6,7},{7,6},{8,9},{9,8},{10,11... | collective-permute-start | bytes 6152 | tf_op jit(solution)/shard_map/ppermute | solution.py:269
  (14 other events, 23.1 us)

commit v3 on v2

--- a/solution.py
+++ b/solution.py
@@ -191,54 +191,51 @@
                 st["w%d" % (i + 1)] = later
         return run
 
-    tasks = [task_wave(0), task_wave(1), task_wave(2)]
-    keys = []
-    for i, k in enumerate(reversed(bits)):
-        model_held = ag_step(model_held, k)
-        gains_held = ag_step(gains_held, k)
-        if i < len(tasks):
-            tasks[i]()
+    def run_group(comm, compute):
+        moved = [step(held, k) for held, step, k in comm]
+        compute()
         keys = sorted(st.keys())
-        out = barrier((model_held, gains_held, [st[n] for n in keys]))
-        model_held, gains_held = out[0], out[1]
-        st.update(zip(keys, out[2]))
+        out = barrier((moved, [st[n] for n in keys]))
+        st.update(zip(keys, out[1]))
+        return out[0]
+
+    def nothing():
+        return None
+
+    def light_prep():
+        task_wave(2)()
+        st["light"] = st["drive0"] * st["drive0"] + st["drive1"] * st["drive1"]
+
+    ag_bits = list(reversed(bits))
+    tasks = [task_wave(0), task_wave(1), light_prep]
+    for i, k in enumerate(ag_bits):
+        model_held, gains_held = run_group(
+            [(model_held, ag_step, k), (gains_held, ag_step, k)],
+            tasks[i] if i < len(tasks) else nothing,
+        )
     for i in range(len(bits), len(tasks)):
         tasks[i]()
-
-    light = st["drive0"] * st["drive0"] + st["drive1"] * st["drive1"]
-    light_held = light.reshape(n_shot, slab, span_y, span_z)
-
-    def born_one():
+    light_held = st["light"].reshape(n_shot, slab, span_y, span_z)
+
+    def born_pass():
         model = model_held.reshape(span_z, span_x * span_y).T.reshape(span_x, span_y, span_z)
-        st["model"] = model
         st["born1"] = model * st["drive0"]
-
-    def born_two():
-        st["born2"] = born_second(st["born1"], st["model"], st["drive1"])
-
-    tasks = [born_one, born_two]
-    for i, k in enumerate(bits):
-        light_held = rs_step(light_held, k)
-        if i < len(tasks):
-            tasks[i]()
-        keys = sorted(st.keys())
-        out = barrier((light_held, [st[n] for n in keys]))
-        light_held = out[0]
-        st.update(zip(keys, out[1]))
-    for i in range(len(bits), len(tasks)):
-        tasks[i]()
-
-    image = st["drive0"] * st["born1"] + st["drive1"] * st["born2"]
+        st["born2"] = born_second(st["born1"], model, st["drive1"])
+
+    (light_held,) = run_group([(light_held, rs_step, bits[0])], born_pass)
+    born1, born2 = st["born1"], st["born2"]
+
+    image = st["drive0"] * born1 + st["drive1"] * born2
     image_held = image.reshape(n_shot, slab, span_y, span_z)
     tasks = [task_wave(3)]
     for i, k in enumerate(bits):
-        image_held = rs_step(image_held, k)
-        if i < len(tasks):
-            tasks[i]()
-        keys = sorted(st.keys())
-        out = barrier((image_held, [st[n] for n in keys]))
-        image_held = out[0]
-        st.update(zip(keys, out[1]))
+        comm = [(image_held, rs_step, k)]
+        if i + 1 < len(bits):
+            comm.append((light_held, rs_step, bits[i + 1]))
+        moved = run_group(comm, tasks[i] if i < len(tasks) else nothing)
+        image_held = moved[0]
+        if i + 1 < len(bits):
+            light_held = moved[1]
     for i in range(len(bits), len(tasks)):
         tasks[i]()
 

time: 175 us -> 160 us (0.914)
  waiting for transfers between devices: 74.6 us -> 66.1 us
  other arithmetic: 45.8 us -> 40.6 us
  starting transfers between devices: 20.3 us -> 16.9 us
  local copies, waits for them, and re-layouts: 22.2 us -> 24.1 us
    ppermute x6, waiting for transfers between devices: 45.5 us -> 35.6 us  [rs_step(): return keep + lax.ppermute(send, 'shot', [(i, i ^ k) for i in range(n)])]
    add x6, other arithmetic: 2.98 us -> 0.23 us  [rs_step(): return keep + lax.ppermute(send, 'shot', [(i, i ^ k) for i in range(n)])]
    ppermute x6, starting transfers between devices: 8.97 us -> 6.95 us  [rs_step(): return keep + lax.ppermute(send, 'shot', [(i, i ^ k) for i in range(n)])]
    unnamed x49 -> x53, local copies, waits for them, and re-layouts: 5.07 us -> 6.14 us
  transfers between devices with their start and end apart: 22 -> 22, of which waited for: 14 -> 13; matrix products, arithmetic and copies ran while one was open for 25% -> 27% of each run, Pallas kernels for 0% -> 0%
where the time goes in v3:
time: 160 us
  waiting for transfers between devices  66.1 us (41%)
  other arithmetic  40.6 us (25%)
  local copies, waits for them, and re-layouts  24.1 us (15%)
  starting transfers between devices  16.9 us (11%)
  between operations  10.2 us (6%)
  matrix products  1.7 us (1%)
    ppermute x6, waiting for transfers between devices, rs_step(): return keep + lax.ppermute(send, 'shot', [(i, i ^ k) for i in range(n)])  35.6 us
    ppermute x9, waiting for transfers between devices, ag_step(): theirs = lax.ppermute(held, 'shot', [(i, i ^ k) for i in range(n)])  30 us
    sub x3, other arithmetic, wave_step(): 2.0 * current - prior + drive - absorber * (current - prior)  11.9 us
    ppermute x9, starting transfers between devices, ag_step(): theirs = lax.ppermute(held, 'shot', [(i, i ^ k) for i in range(n)])  8.45 us
    ppermute x6, starting transfers between devices, rs_step(): return keep + lax.ppermute(send, 'shot', [(i, i ^ k) for i in range(n)])  6.95 us
    select_n x10, other arithmetic, ag_step(): jnp.where(low, jnp.stack([held, theirs], axis=1), jnp.stack([theirs, held...  6.15 us
    unnamed x53, local copies, waits for them, and re-layouts  6.14 us
    add x2, other arithmetic, born_second(): 2.0 * born + speed_term * laplace_x(with_halo(born)) - absorber * born  5.8 us
  transfers between devices with their start and end apart: 22, of which 13 were waited for; matrix products, arithmetic and copies ran while one was open for 27% of the time, Pallas kernels for 0%

profile of v3, /device:TPU:0, one launch (start us, length us, event | category | flops | bytes accessed | tf_op | source)
XLA Modules:
  0.0 159.7 jit_solution(149094179054590227)
XLA Ops:
  0.6 1.7 %dynamic-slice_bitcast_fusion.4 = f32[4,64,128]{2,1,0:T(8,128)} fusion(f32[1,32,64,128]{3,2,1,0:T(8,128)} %param.18, s32[]{:T(128)S(6)} %select_n.303), kind=kLoop, calls=%fused_computation.332 | loop fusion | bytes 262148 | tf_op jit(solution)/shard_map/dynamic_slice | solution.py:43
  4.6 3.6 %collective-permute-start = (f32[1,16,2048]{2,1,0:T(8,128)}, f32[1,16,2048]{2,1,0:T(8,128)}, u32[]{:S(2)}, u32[]{:S(2)}) collective-permute-start(f32[1,16,2048]{2,1,0:T(8,128)} %stack.117), channel_id=1, source_target_pairs={{0,8},{2,10},{4,12},{6,14},{8,0},{10,2},{12,4},{14,6},{1,9},{3,11}... | collective-permute-start | bytes 393224 | tf_op jit(solution)/shard_map/ppermute | solution.py:112
  9.5 1.4 fusion.201
  11.1 1.4 fusion.183
  12.5 1.3 fusion.184
  13.9 1.8 %fusion.182 = f32[128]{0:T(128)} fusion(f32[]{:T(128)} %bitcast.11, f32[]{:T(128)} %bitcast.10), kind=kLoop, calls=%fused_computation.387 | loop fusion | flops 1280 | bytes 520 | tf_op jit(solution)/shard_map/add | solution.py:27
  17.2 1.4 maximum_select_fusion.9
  19.5 4.7 %multiply_subtract_fusion.2 = (f32[32,64,128]{2,1,0:T(8,128)S(1)}, f32[32,64,128]{2,1,0:T(8,128)}, f32[32,64,128]{2,1,0:T(8,128)S(1)}) fusion(f32[128]{0:T(128)} %fusion.182, f32[32,64]{1,0:T(8,128)S(1)} %broadcast_add_fusion, f32[1,32,64,128]{3,2,1,0:T(8,128)} %param.17, f32[1,32,64,128]{3,2,1,0:T(8,128)} %param.18, ...), kind=kLoop, calls=%fused_computation.306 | loop fusion | flops 11272192 | bytes 17056256 | tf_op jit(solution)/shard_map/sub | solution.py:167
  30.2 1.7 %collective-permute-start.4 = (f32[2,16,64]{2,1,0:T(8,128)}, f32[2,16,64]{2,1,0:T(8,128)S(1)}, u32[]{:S(2)}, u32[]{:S(2)}) collective-permute-start(f32[2,16,64]{2,1,0:T(8,128)} %maximum_select_fusion.9), channel_id=1, source_target_pairs={{0,4},{2,6},{4,0},{6,2},{8,12},{10,14},{12,8},{14,10},{1,5},{3,7},... | collective-permute-start | bytes 24584 | tf_op jit(solution)/shard_map/ppermute | solution.py:112
  34.9 3.7 %multiply_subtract_fusion.1 = (f32[32,64,128]{2,1,0:T(8,128)S(1)}, f32[32,64,128]{2,1,0:T(8,128)}) fusion(f32[32,64,128]{2,1,0:T(8,128)S(1)} %bitcast.115, f32[32,64,128]{2,1,0:T(8,128)S(1)} %bitcast.124, f32[128]{0:T(128)S(1)} %copy-done.18, f32[32,64]{1,0:T(8,128)S(1)} %broadcast_add_fusion, f32[40,64,128]{2,1,0:T(8,128)S(1)} %constant_dynamic-update-slice_fusion.4, ...), kind=kLoop, calls=%fused_computation.305 | loop fusion | flops 11272192 | bytes 16007680 | tf_op jit(solution)/shard_map/sub | solution.py:167
  42.0 1.3 scatter-add.11
  43.3 1.2 maximum_select_fusion.2
  46.3 1.6 %collective-permute-start.7 = (f32[4,16,64]{2,1,0:T(8,128)S(1)}, f32[4,16,64]{2,1,0:T(8,128)S(1)}, u32[]{:S(2)}, u32[]{:S(2)}) collective-permute-start(f32[4,16,64]{2,1,0:T(8,128)S(1)} %bitcast.155), channel_id=1, source_target_pairs={{0,2},{2,0},{4,6},{6,4},{8,10},{10,8},{12,14},{14,12},{1,3},{3,1},... | collective-permute-start | bytes 49160 | tf_op jit(solution)/shard_map/ppermute | solution.py:112
  51.0 3.6 %multiply_subtract_fusion = (f32[32,64,128]{2,1,0:T(8,128)S(1)}, f32[32,64,128]{2,1,0:T(8,128)}) fusion(f32[32,64,128]{2,1,0:T(8,128)S(1)} %bitcast.122, f32[32,64,128]{2,1,0:T(8,128)S(1)} %bitcast.116, f32[128]{0:T(128)S(1)} %copy-done.19, f32[32,64]{1,0:T(8,128)S(1)} %broadcast_add_fusion, f32[40,64,128]{2,1,0:T(8,128)S(1)} %constant_dynamic-update-slice_fusion.3, ...), kind=kLoop, calls=%fused_computation.303 | loop fusion | flops 11272192 | bytes 16007680 | tf_op jit(solution)/shard_map/sub | solution.py:167
  57.9 1.2 scatter-add.14
  59.1 3.1 %collective-permute-done.6 = f32[4,16,2048]{2,1,0:T(8,128)} collective-permute-done((f32[4,16,2048]{2,1,0:T(8,128)}, f32[4,16,2048]{2,1,0:T(8,128)}, u32[]{:S(2)}, u32[]{:S(2)}) %collective-permute-start.6) | collective-permute-done | bytes 524320 | tf_op jit(solution)/shard_map/ppermute | solution.py:112
  62.2 1.6 %maximum_select_fusion = f32[4,2,16,2048]{3,2,0,1:T(8,128)S(1)} fusion(f32[4,1,16,2048]{3,2,0,1:T(8,128)} %bitcast.31, f32[4,1,16,2048]{3,2,0,1:T(8,128)} %bitcast.30, pred[]{:T(512)S(6)} %eq.48), kind=kLoop, calls=%fused_computation.300 | loop fusion | flops 786432 | bytes 2097153 | tf_op jit(solution)/shard_map/jit(_where)/select_n | solution.py:114
  64.9 1.5 copy.35
  69.0 2.9 %fusion.88 = f32[32,64,128]{2,1,0:T(8,128)S(1)} fusion(f32[40,64,128]{2,1,0:T(8,128)S(1)} %constant_dynamic-update-slice_fusion.2, f32[32,64,128]{2,1,0:T(8,128)S(1)} %bitcast.127, f32[32,64,128]{2,1,0:T(8,128)S(1)} %copy-done.3, f32[32,64,128]{2,1,0:T(8,128)S(1)} %mul.364, f32[128]{0:T(128)S(1)} %copy-done.20, f32[32,64]{1,0:T(8,128)S(1)} %broadcast_add_fusion, ...), kind=kLoop, calls=%fused_computation.201 | loop fusion | flops 11272192 | bytes 16007680 | tf_op jit(solution)/shard_map/add | solution.py:172
  71.9 9.3 %collective-permute-done.9 = f32[4,4,64,128]{3,2,1,0:T(8,128)S(1)} collective-permute-done((f32[4,4,64,128]{3,2,1,0:T(8,128)S(1)}, f32[4,4,64,128]{3,2,1,0:T(8,128)S(1)}, u32[]{:S(2)}, u32[]{:S(2)}) %collective-permute-start.9) | collective-permute-done | bytes 524320 | tf_op jit(solution)/shard_map/ppermute | solution.py:126
  81.5 1.7 %collective-permute-start.12 = (f32[2,4,64,128]{3,2,1,0:T(8,128)S(1)}, f32[2,4,64,128]{3,2,1,0:T(8,128)S(1)}, u32[]{:S(2)}, u32[]{:S(2)}) collective-permute-start(f32[2,4,64,128]{3,2,1,0:T(8,128)S(1)} %dynamic-slice_bitcast_fusion.3), channel_id=1, source_target_pairs={{0,4},{2,6},{4,0},{6,2},{8,12},{10,14},{12,8},{14,10},{1,5},{3,7},... | collective-permute-start | bytes 786440 | tf_op jit(solution)/shard_map/ppermute | solution.py:126
  84.9 3.2 %fusion.113 = f32[32,64,128]{2,1,0:T(8,128)} fusion(f32[40,64,128]{2,1,0:T(8,128)S(1)} %constant_dynamic-update-slice_fusion.1, s32[32,64,128]{2,1,0:T(8,128)S(1)} %copy-done), kind=kLoop, calls=%fused_computation.226 | loop fusion | flops 9175040 | bytes 12845056 | tf_op jit(solution)/shard_map/mul | solution.py:164
  88.2 2.1 %collective-permute-done.12 = f32[2,4,64,128]{3,2,1,0:T(8,128)S(1)} collective-permute-done((f32[2,4,64,128]{3,2,1,0:T(8,128)S(1)}, f32[2,4,64,128]{3,2,1,0:T(8,128)S(1)}, u32[]{:S(2)}, u32[]{:S(2)}) %collective-permute-start.12) | collective-permute-done | bytes 262176 | tf_op jit(solution)/shard_map/ppermute | solution.py:126
  90.2 7.5 %collective-permute-done.11 = f32[4,4,64,128]{3,2,1,0:T(8,128)S(1)} collective-permute-done((f32[4,4,64,128]{3,2,1,0:T(8,128)S(1)}, f32[4,4,64,128]{3,2,1,0:T(8,128)S(1)}, u32[]{:S(2)}, u32[]{:S(2)}) %collective-permute-start.11) | collective-permute-done | bytes 524320 | tf_op jit(solution)/shard_map/ppermute | solution.py:126
  97.9 2.6 %collective-permute-start.15 = (f32[1,4,64,128]{3,2,1,0:T(8,128)S(1)}, f32[1,4,64,128]{3,2,1,0:T(8,128)S(1)}, u32[]{:S(2)}, u32[]{:S(2)}) collective-permute-start(f32[1,4,64,128]{3,2,1,0:T(8,128)S(1)} %constant_dynamic-slice_fusion.3), channel_id=1, source_target_pairs={{0,8},{2,10},{4,12},{6,14},{8,0},{10,2},{12,4},{14,6},{1,9},{3,11}... | collective-permute-start | bytes 393224 | tf_op jit(solution)/shard_map/ppermute | solution.py:126
  101.2 5.3 %collective-permute-done.15 = f32[1,4,64,128]{3,2,1,0:T(8,128)S(1)} collective-permute-done((f32[1,4,64,128]{3,2,1,0:T(8,128)S(1)}, f32[1,4,64,128]{3,2,1,0:T(8,128)S(1)}, u32[]{:S(2)}, u32[]{:S(2)}) %collective-permute-start.15) | collective-permute-done | bytes 131104 | tf_op jit(solution)/shard_map/ppermute | solution.py:126
  106.5 4.1 %collective-permute-done.14 = f32[2,4,64,128]{3,2,1,0:T(8,128)S(1)} collective-permute-done((f32[2,4,64,128]{3,2,1,0:T(8,128)S(1)}, f32[2,4,64,128]{3,2,1,0:T(8,128)S(1)}, u32[]{:S(2)}, u32[]{:S(2)}) %collective-permute-start.14) | collective-permute-done | bytes 262176 | tf_op jit(solution)/shard_map/ppermute | solution.py:126
  110.8 7.3 %collective-permute-done.16 = f32[1,4,64,128]{3,2,1,0:T(8,128)S(1)} collective-permute-done((f32[1,4,64,128]{3,2,1,0:T(8,128)S(1)}, f32[1,4,64,128]{3,2,1,0:T(8,128)S(1)}, u32[]{:S(2)}, u32[]{:S(2)}) %collective-permute-start.16) | collective-permute-done | bytes 131104 | tf_op jit(solution)/shard_map/ppermute | solution.py:126
  120.0 7.1 %collective-permute-done.17 = f32[1,4,64,128]{3,2,1,0:T(8,128)S(1)} collective-permute-done((f32[1,4,64,128]{3,2,1,0:T(8,128)S(1)}, f32[1,4,64,128]{3,2,1,0:T(8,128)S(1)}, u32[]{:S(2)}, u32[]{:S(2)}) %collective-permute-start.17) | collective-permute-done | bytes 131104 | tf_op jit(solution)/shard_map/ppermute | solution.py:112
  127.2 8.1 %collective-permute-done.18 = f32[2,4,64,128]{3,2,1,0:T(8,128)S(1)} collective-permute-done((f32[2,4,64,128]{3,2,1,0:T(8,128)S(1)}, f32[2,4,64,128]{3,2,1,0:T(8,128)S(1)}, u32[]{:S(2)}, u32[]{:S(2)}) %collective-permute-start.18) | collective-permute-done | bytes 262176 | tf_op jit(solution)/shard_map/ppermute | solution.py:112
  137.5 10.7 %collective-permute-done.19 = f32[4,4,64,128]{3,2,1,0:T(8,128)S(1)} collective-permute-done((f32[4,4,64,128]{3,2,1,0:T(8,128)S(1)}, f32[4,4,64,128]{3,2,1,0:T(8,128)S(1)}, u32[]{:S(2)}, u32[]{:S(2)}) %collective-permute-start.19) | collective-permute-done | bytes 524320 | tf_op jit(solution)/shard_map/ppermute | solution.py:112
  152.9 2.9 %fusion.141 = f32[32,64,128]{2,1,0:T(8,128)S(1)} fusion(f32[40,64,128]{2,1,0:T(8,128)S(1)} %constant_dynamic-update-slice_fusion, f32[32,64,128]{2,1,0:T(8,128)S(1)} %copy-done.12, f32[128]{0:T(128)S(1)} %copy-done.21, f32[32,64]{1,0:T(8,128)S(1)} %broadcast_add_fusion, f32[4,2,4,64,128]{4,3,2,1,0:T(8,128)S(1)} %copy.41, f32[32,64,128]{2,1,0:T(8,128)S(1)} %copy-done.9, ...), kind=kLoop, calls=%fused_computation.254 | loop fusion | flops 11534336 | bytes 16007680 | tf_op jit(solution)/shard_map/add | solution.py:172
  (155 shorter events, 36.8 us)
Async XLA Ops:
  0.6 10.3 %copy-start.6 = (f32[1,32,64,128]{3,2,1,0:T(8,128)S(1)}, f32[1,32,64,128]{3,2,1,0:T(8,128)}, u32[]{:S(2)}) copy-start(f32[1,32,64,128]{3,2,1,0:T(8,128)} %param.18) | copy-start | bytes 3145732
  2.3 16.3 %collective-permute-start.2 = (f32[4,64,128]{2,1,0:T(8,128)}, f32[4,64,128]{2,1,0:T(8,128)}, u32[]{:S(2)}, u32[]{:S(2)}) collective-permute-start(f32[4,64,128]{2,1,0:T(8,128)} %dynamic-slice_bitcast_fusion.4), channel_id=1, source_target_pairs={{0,1},{1,0},{2,3},{3,2},{4,5},{5,4},{6,7},{7,6},{8,9},{9,8},{10,11... | collective-permute-start | bytes 393224 | tf_op jit(solution)/shard_map/ppermute | solution.py:44
  4.6 24.2 %collective-permute-start = (f32[1,16,2048]{2,1,0:T(8,128)}, f32[1,16,2048]{2,1,0:T(8,128)}, u32[]{:S(2)}, u32[]{:S(2)}) collective-permute-start(f32[1,16,2048]{2,1,0:T(8,128)} %stack.117), channel_id=1, source_target_pairs={{0,8},{2,10},{4,12},{6,14},{8,0},{10,2},{12,4},{14,6},{1,9},{3,11}... | collective-permute-start | bytes 393224 | tf_op jit(solution)/shard_map/ppermute | solution.py:112
  8.1 9.1 %collective-permute-start.1 = (f32[1,16,64]{2,1,0:T(8,128)}, f32[1,16,64]{2,1,0:T(8,128)}, u32[]{:S(2)}, u32[]{:S(2)}) collective-permute-start(f32[1,16,64]{2,1,0:T(8,128)} %bitcast.162), channel_id=1, source_target_pairs={{0,8},{2,10},{4,12},{6,14},{8,0},{10,2},{12,4},{14,6},{1,9},{3,11}... | collective-permute-start | bytes 12296 | tf_op jit(solution)/shard_map/ppermute | solution.py:112
  11.0 8.6 %copy-start = (s32[32,64,128]{2,1,0:T(8,128)S(1)}, s32[32,64,128]{2,1,0:T(8,128)}, u32[]{:S(2)}) copy-start(s32[32,64,128]{2,1,0:T(8,128)} %param.19) | copy-start | bytes 3145732
  29.9 4.3 %copy-start.17 = (f32[2,16,64]{2,1,0:T(8,128)S(1)}, f32[2,16,64]{2,1,0:T(8,128)}, u32[]{:S(2)}) copy-start(f32[2,16,64]{2,1,0:T(8,128)} %maximum_select_fusion.9) | copy-start | bytes 24580
  29.9 4.9 %copy-start.7 = (f32[1,32,64,128]{3,2,1,0:T(8,128)S(1)}, f32[1,32,64,128]{3,2,1,0:T(8,128)}, u32[]{:S(2)}) copy-start(f32[1,32,64,128]{3,2,1,0:T(8,128)} %param.18) | copy-start | bytes 3145732
  29.9 4.9 %copy-start.18 = (f32[128]{0:T(128)S(1)}, f32[128]{0:T(128)}, u32[]{:S(2)}) copy-start(f32[128]{0:T(128)} %fusion.182) | copy-start | bytes 1540
  30.0 4.9 %collective-permute-start.5 = (f32[4,64,128]{2,1,0:T(8,128)S(1)}, f32[4,64,128]{2,1,0:T(8,128)S(1)}, u32[]{:S(2)}, u32[]{:S(2)}) collective-permute-start(f32[4,64,128]{2,1,0:T(8,128)S(1)} %constant_dynamic-slice_fusion.9), channel_id=1, source_target_pairs={{0,1},{1,0},{2,3},{3,2},{4,5},{5,4},{6,7},{7,6},{8,9},{9,8},{10,11... | collective-permute-start | bytes 393224 | tf_op jit(solution)/shard_map/ppermute | solution.py:44
  30.2 3.9 %collective-permute-start.4 = (f32[2,16,64]{2,1,0:T(8,128)}, f32[2,16,64]{2,1,0:T(8,128)S(1)}, u32[]{:S(2)}, u32[]{:S(2)}) collective-permute-start(f32[2,16,64]{2,1,0:T(8,128)} %maximum_select_fusion.9), channel_id=1, source_target_pairs={{0,4},{2,6},{4,0},{6,2},{8,12},{10,14},{12,8},{14,10},{1,5},{3,7},... | collective-permute-start | bytes 24584 | tf_op jit(solution)/shard_map/ppermute | solution.py:112
  32.7 10.6 %collective-permute-start.3 = (f32[2,16,2048]{2,1,0:T(8,128)S(1)}, f32[2,16,2048]{2,1,0:T(8,128)}, u32[]{:S(2)}, u32[]{:S(2)}) collective-permute-start(f32[2,16,2048]{2,1,0:T(8,128)S(1)} %maximum_select_fusion.4), channel_id=1, source_target_pairs={{0,4},{2,6},{4,0},{6,2},{8,12},{10,14},{12,8},{14,10},{1,5},{3,7},... | collective-permute-start | bytes 786440 | tf_op jit(solution)/shard_map/ppermute | solution.py:112
  38.5 9.9 %copy-start.1 = (f32[32,64,128]{2,1,0:T(8,128)S(1)}, f32[32,64,128]{2,1,0:T(8,128)}, u32[]{:S(2)}) copy-start(f32[32,64,128]{2,1,0:T(8,128)} %get-tuple-element.93) | copy-start | bytes 3145732
  43.3 5.1 %copy-start.2 = (f32[32,64,128]{2,1,0:T(8,128)S(1)}, f32[32,64,128]{2,1,0:T(8,128)}, u32[]{:S(2)}) copy-start(f32[32,64,128]{2,1,0:T(8,128)} %get-tuple-element.95) | copy-start | bytes 3145732
  46.2 4.7 %collective-permute-start.8 = (f32[4,64,128]{2,1,0:T(8,128)S(1)}, f32[4,64,128]{2,1,0:T(8,128)S(1)}, u32[]{:S(2)}, u32[]{:S(2)}) collective-permute-start(f32[4,64,128]{2,1,0:T(8,128)S(1)} %constant_dynamic-slice_fusion.7), channel_id=1, source_target_pairs={{0,1},{1,0},{2,3},{3,2},{4,5},{5,4},{6,7},{7,6},{8,9},{9,8},{10,11... | collective-permute-start | bytes 393224 | tf_op jit(solution)/shard_map/ppermute | solution.py:44
  46.3 4.0 %collective-permute-start.7 = (f32[4,16,64]{2,1,0:T(8,128)S(1)}, f32[4,16,64]{2,1,0:T(8,128)S(1)}, u32[]{:S(2)}, u32[]{:S(2)}) collective-permute-start(f32[4,16,64]{2,1,0:T(8,128)S(1)} %bitcast.155), channel_id=1, source_target_pairs={{0,2},{2,0},{4,6},{6,4},{8,10},{10,8},{12,14},{14,12},{1,3},{3,1},... | collective-permute-start | bytes 49160 | tf_op jit(solution)/shard_map/ppermute | solution.py:112
  47.9 14.3 %collective-permute-start.6 = (f32[4,16,2048]{2,1,0:T(8,128)}, f32[4,16,2048]{2,1,0:T(8,128)}, u32[]{:S(2)}, u32[]{:S(2)}) collective-permute-start(f32[4,16,2048]{2,1,0:T(8,128)} %bitcast.22), channel_id=1, source_target_pairs={{0,2},{2,0},{4,6},{6,4},{8,10},{10,8},{12,14},{14,12},{1,3},{3,1},... | collective-permute-start | bytes 1572872 | tf_op jit(solution)/shard_map/ppermute | solution.py:112
  66.7 2.1 %collective-permute-start.10 = (f32[4,64,128]{2,1,0:T(8,128)S(1)}, f32[4,64,128]{2,1,0:T(8,128)S(1)}, u32[]{:S(2)}, u32[]{:S(2)}) collective-permute-start(f32[4,64,128]{2,1,0:T(8,128)S(1)} %constant_dynamic-slice_fusion.5), channel_id=1, source_target_pairs={{0,1},{1,0},{2,3},{3,2},{4,5},{5,4},{6,7},{7,6},{8,9},{9,8},{10,11... | collective-permute-start | bytes 393224 | tf_op jit(solution)/shard_map/ppermute | solution.py:44
  67.8 13.4 %collective-permute-start.9 = (f32[4,4,64,128]{3,2,1,0:T(8,128)S(1)}, f32[4,4,64,128]{3,2,1,0:T(8,128)S(1)}, u32[]{:S(2)}, u32[]{:S(2)}) collective-permute-start(f32[4,4,64,128]{3,2,1,0:T(8,128)S(1)} %dynamic-slice_bitcast_fusion.1), channel_id=1, source_target_pairs={{0,2},{2,0},{4,6},{6,4},{8,10},{10,8},{12,14},{14,12},{1,3},{3,1},... | collective-permute-start | bytes 1572872 | tf_op jit(solution)/shard_map/ppermute | solution.py:126
  71.9 9.4 %copy-start.11 = (f32[1,262144]{1,0:T(1,128)S(1)}, f32[1,262144]{1,0:T(1,128)}, u32[]{:S(2)}) copy-start(f32[1,262144]{1,0:T(1,128)} %scatter-add.14) | copy-start | bytes 3145732
  81.3 3.5 %collective-permute-start.13 = (f32[4,64,128]{2,1,0:T(8,128)S(1)}, f32[4,64,128]{2,1,0:T(8,128)S(1)}, u32[]{:S(2)}, u32[]{:S(2)}) collective-permute-start(f32[4,64,128]{2,1,0:T(8,128)S(1)} %constant_dynamic-slice_fusion.4), channel_id=1, source_target_pairs={{0,1},{1,0},{2,3},{3,2},{4,5},{5,4},{6,7},{7,6},{8,9},{9,8},{10,11... | collective-permute-start | bytes 393224 | tf_op jit(solution)/shard_map/ppermute | solution.py:44
  81.5 8.8 %collective-permute-start.12 = (f32[2,4,64,128]{3,2,1,0:T(8,128)S(1)}, f32[2,4,64,128]{3,2,1,0:T(8,128)S(1)}, u32[]{:S(2)}, u32[]{:S(2)}) collective-permute-start(f32[2,4,64,128]{3,2,1,0:T(8,128)S(1)} %dynamic-slice_bitcast_fusion.3), channel_id=1, source_target_pairs={{0,4},{2,6},{4,0},{6,2},{8,12},{10,14},{12,8},{14,10},{1,5},{3,7},... | collective-permute-start | bytes 786440 | tf_op jit(solution)/shard_map/ppermute | solution.py:126
  83.7 14.1 %collective-permute-start.11 = (f32[4,4,64,128]{3,2,1,0:T(8,128)S(1)}, f32[4,4,64,128]{3,2,1,0:T(8,128)S(1)}, u32[]{:S(2)}, u32[]{:S(2)}) collective-permute-start(f32[4,4,64,128]{3,2,1,0:T(8,128)S(1)} %dynamic-slice_bitcast_fusion), channel_id=1, source_target_pairs={{0,2},{2,0},{4,6},{6,4},{8,10},{10,8},{12,14},{14,12},{1,3},{3,1},... | collective-permute-start | bytes 1572872 | tf_op jit(solution)/shard_map/ppermute | solution.py:126
  97.9 12.9 %copy-start.15 = (f32[4,2,16,64]{3,2,1,0:T(8,128)S(1)}, f32[4,2,16,64]{3,2,1,0:T(8,128)}, u32[]{:S(2)}) copy-start(f32[4,2,16,64]{3,2,1,0:T(8,128)} %copy.34) | copy-start | bytes 98308
  97.9 8.5 %collective-permute-start.15 = (f32[1,4,64,128]{3,2,1,0:T(8,128)S(1)}, f32[1,4,64,128]{3,2,1,0:T(8,128)S(1)}, u32[]{:S(2)}, u32[]{:S(2)}) collective-permute-start(f32[1,4,64,128]{3,2,1,0:T(8,128)S(1)} %constant_dynamic-slice_fusion.3), channel_id=1, source_target_pairs={{0,8},{2,10},{4,12},{6,14},{8,0},{10,2},{12,4},{14,6},{1,9},{3,11}... | collective-permute-start | bytes 393224 | tf_op jit(solution)/shard_map/ppermute | solution.py:126
  100.5 10.1 %collective-permute-start.14 = (f32[2,4,64,128]{3,2,1,0:T(8,128)S(1)}, f32[2,4,64,128]{3,2,1,0:T(8,128)S(1)}, u32[]{:S(2)}, u32[]{:S(2)}) collective-permute-start(f32[2,4,64,128]{3,2,1,0:T(8,128)S(1)} %dynamic-slice_bitcast_fusion.2), channel_id=1, source_target_pairs={{0,4},{2,6},{4,0},{6,2},{8,12},{10,14},{12,8},{14,10},{1,5},{3,7},... | collective-permute-start | bytes 786440 | tf_op jit(solution)/shard_map/ppermute | solution.py:126
  110.7 7.5 %collective-permute-start.16 = (f32[1,4,64,128]{3,2,1,0:T(8,128)S(1)}, f32[1,4,64,128]{3,2,1,0:T(8,128)S(1)}, u32[]{:S(2)}, u32[]{:S(2)}) collective-permute-start(f32[1,4,64,128]{3,2,1,0:T(8,128)S(1)} %constant_dynamic-slice_fusion.2), channel_id=1, source_target_pairs={{0,8},{2,10},{4,12},{6,14},{8,0},{10,2},{12,4},{14,6},{1,9},{3,11}... | collective-permute-start | bytes 393224 | tf_op jit(solution)/shard_map/ppermute | solution.py:126
  118.1 9.0 %copy-start.23 = (s32[1,256]{1,0:T(1,128)S(1)}, s32[1,256]{1,0:T(1,128)}, u32[]{:S(2)}) copy-start(s32[1,256]{1,0:T(1,128)} %param.24) | copy-start | bytes 3076
  119.9 7.1 %collective-permute-start.17 = (f32[1,4,64,128]{3,2,1,0:T(8,128)S(1)}, f32[1,4,64,128]{3,2,1,0:T(8,128)S(1)}, u32[]{:S(2)}, u32[]{:S(2)}) collective-permute-start(f32[1,4,64,128]{3,2,1,0:T(8,128)S(1)} %bitcast.145), channel_id=1, source_target_pairs={{0,8},{2,10},{4,12},{6,14},{8,0},{10,2},{12,4},{14,6},{1,9},{3,11}... | collective-permute-start | bytes 393224 | tf_op jit(solution)/shard_map/ppermute | solution.py:112
  127.0 8.2 %collective-permute-start.18 = (f32[2,4,64,128]{3,2,1,0:T(8,128)S(1)}, f32[2,4,64,128]{3,2,1,0:T(8,128)S(1)}, u32[]{:S(2)}, u32[]{:S(2)}) collective-permute-start(f32[2,4,64,128]{3,2,1,0:T(8,128)S(1)} %maximum_select_fusion.6), channel_id=1, source_target_pairs={{0,4},{2,6},{4,0},{6,2},{8,12},{10,14},{12,8},{14,10},{1,5},{3,7},... | collective-permute-start | bytes 786440 | tf_op jit(solution)/shard_map/ppermute | solution.py:112
  135.3 12.9 %collective-permute-start.19 = (f32[4,4,64,128]{3,2,1,0:T(8,128)S(1)}, f32[4,4,64,128]{3,2,1,0:T(8,128)S(1)}, u32[]{:S(2)}, u32[]{:S(2)}) collective-permute-start(f32[4,4,64,128]{3,2,1,0:T(8,128)S(1)} %bitcast.139), channel_id=1, source_target_pairs={{0,2},{2,0},{4,6},{6,4},{8,10},{10,8},{12,14},{14,12},{1,3},{3,1},... | collective-permute-start | bytes 1572872 | tf_op jit(solution)/shard_map/ppermute | solution.py:112
  150.5 1.6 collective-permute-start.20
  157.1 1.9 %collective-permute-start.21 = (f32[1,2,256]{2,1,0:T(2,128)S(1)}, f32[1,2,256]{2,1,0:T(2,128)S(1)}, u32[]{:S(2)}, u32[]{:S(2)}) collective-permute-start(f32[1,2,256]{2,1,0:T(2,128)S(1)} %maximum_bitcast_fusion), channel_id=1, source_target_pairs={{0,1},{1,0},{2,3},{3,2},{4,5},{5,4},{6,7},{7,6},{8,9},{9,8},{10,11... | collective-permute-start | bytes 6152 | tf_op jit(solution)/shard_map/ppermute | solution.py:266
  (16 other events, 30.4 us)

commit v4 on v3

--- a/solution.py
+++ b/solution.py
@@ -42,9 +42,10 @@
         me = lax.axis_index("space")
         piece = lax.dynamic_slice_in_dim(x, (1 - me) * (length - HALO), HALO, 0)
         got = lax.ppermute(piece, "space", [(0, 1), (1, 0)])
-        zeros = jnp.zeros((HALO,) + x.shape[1:], x.dtype)
-        padded = jnp.concatenate([zeros, x, zeros], axis=0)
-        return lax.dynamic_update_slice_in_dim(padded, got, (1 - me) * (length + HALO), 0)
+        zero = jnp.zeros_like(got)
+        before = jnp.where(me == 1, got, zero)
+        after = jnp.where(me == 0, got, zero)
+        return jnp.concatenate([before, x, after], axis=0)
     up = [(i, (i + 1) % size) for i in range(size - 1)]
     down = [(j, i) for i, j in up]
     before = lax.ppermute(x[length - HALO :], "space", up)
@@ -155,10 +156,15 @@
     source_gain = jnp.where(source_owned, term_flat[source_safe], 0.0)
     barrier = lax.optimization_barrier
 
+    plane = span_y * span_z
+    hit = (
+        (jnp.arange(span_x)[:, None, None] == source_safe[0] // plane)
+        & (jnp.arange(span_y)[None, :, None] == (source_safe[0] // span_z) % span_y)
+        & (jnp.arange(span_z)[None, None, :] == source_safe[0] % span_z)
+    )
+
     def inject(field, moment):
-        flat = field.reshape(1, -1)
-        flat = flat.at[jnp.arange(1), source_safe].add(source_gain * wavelet[:, moment])
-        return flat.reshape(field.shape)
+        return field + jnp.where(hit, source_gain[0] * wavelet[0, moment], 0.0)
 
     def wave_step(current, prior, moment, last):
         drive = speed_term * laplace_x(with_halo(current))
@@ -202,40 +208,42 @@
     def nothing():
         return None
 
-    def light_prep():
-        task_wave(2)()
+    def early_waves():
+        task_wave(0)()
+        task_wave(1)()
         st["light"] = st["drive0"] * st["drive0"] + st["drive1"] * st["drive1"]
 
     ag_bits = list(reversed(bits))
-    tasks = [task_wave(0), task_wave(1), light_prep]
-    for i, k in enumerate(ag_bits):
-        model_held, gains_held = run_group(
-            [(model_held, ag_step, k), (gains_held, ag_step, k)],
-            tasks[i] if i < len(tasks) else nothing,
+    model_held, gains_held = run_group(
+        [(model_held, ag_step, ag_bits[0]), (gains_held, ag_step, ag_bits[0])], early_waves
+    )
+    light_held = st["light"].reshape(n_shot, slab, span_y, span_z)
+    tasks = [task_wave(2)]
+    for i in range(1, len(bits)):
+        model_held, gains_held, light_held = run_group(
+            [
+                (model_held, ag_step, ag_bits[i]),
+                (gains_held, ag_step, ag_bits[i]),
+                (light_held, rs_step, bits[i - 1]),
+            ],
+            tasks[i - 1] if i - 1 < len(tasks) else nothing,
         )
-    for i in range(len(bits), len(tasks)):
+    for i in range(len(bits) - 1, len(tasks)):
         tasks[i]()
-    light_held = st["light"].reshape(n_shot, slab, span_y, span_z)
 
     def born_pass():
         model = model_held.reshape(span_z, span_x * span_y).T.reshape(span_x, span_y, span_z)
         st["born1"] = model * st["drive0"]
         st["born2"] = born_second(st["born1"], model, st["drive1"])
 
-    (light_held,) = run_group([(light_held, rs_step, bits[0])], born_pass)
+    (light_held,) = run_group([(light_held, rs_step, bits[-1])], born_pass)
     born1, born2 = st["born1"], st["born2"]
 
     image = st["drive0"] * born1 + st["drive1"] * born2
     image_held = image.reshape(n_shot, slab, span_y, span_z)
     tasks = [task_wave(3)]
     for i, k in enumerate(bits):
-        comm = [(image_held, rs_step, k)]
-        if i + 1 < len(bits):
-            comm.append((light_held, rs_step, bits[i + 1]))
-        moved = run_group(comm, tasks[i] if i < len(tasks) else nothing)
-        image_held = moved[0]
-        if i + 1 < len(bits):
-            light_held = moved[1]
+        (image_held,) = run_group([(image_held, rs_step, k)], tasks[i] if i < len(tasks) else nothing)
     for i in range(len(bits), len(tasks)):
         tasks[i]()
 

time: 160 us -> 186 us (1.16)
  other arithmetic: 40.6 us -> 94 us
  waiting for transfers between devices: 66.1 us -> 48.7 us
  local copies, waits for them, and re-layouts: 24.1 us -> 17 us
  between operations: 10.2 us -> 4.68 us
  starting transfers between devices: 16.9 us -> 19.3 us
    add x4, other arithmetic: 2.96 us -> 35.3 us  [the longest x3 33.5 us: inject(): return field + jnp.where(hit, source_gain[0] * wavelet[0, moment], 0.0)]
    ppermute x6, waiting for transfers between devices: 35.6 us -> 15.5 us  [rs_step(): return keep + lax.ppermute(send, 'shot', [(i, i ^ k) for i in range(n)])]
    add x2, other arithmetic: 5.8 us -> 22.4 us  [born_second(): 2.0 * born + speed_term * laplace_x(with_halo(born)) - absorber * born]
    sub x3 -> x0, other arithmetic: 11.9 us -> none  [wave_step(): 2.0 * current - prior + drive - absorber * (current - prior)]
    concatenate x6, other arithmetic: 0.89 us -> 9.9 us  [with_halo(): return jnp.concatenate([before, x, after], axis=0)]
    mul x1, other arithmetic: 3.24 us -> 10.5 us  [wave_step(): drive = speed_term * laplace_x(with_halo(current))]
    add x6, other arithmetic: 0.23 us -> 4.18 us  [rs_step(): return keep + lax.ppermute(send, 'shot', [(i, i ^ k) for i in range(n)])]
    select_n x10, other arithmetic: 6.15 us -> 2.51 us  [ag_step(): jnp.where(low, jnp.stack([held, theirs], axis=1), jnp.stack([theirs, held...]
  transfers between devices with their start and end apart: 22 -> 22, of which waited for: 13 -> 8; matrix products, arithmetic and copies ran while one was open for 27% -> 38% of each run, Pallas kernels for 0% -> 0%
where the time goes in v4:
time: 186 us; the launch traced here: 185 us
  other arithmetic  94 us (51%)
  waiting for transfers between devices  48.7 us (26%)
  starting transfers between devices  19.3 us (10%)
  local copies, waits for them, and re-layouts  17 us (9%)
  between operations  4.68 us (3%)
    add x3, other arithmetic, inject(): return field + jnp.where(hit, source_gain[0] * wavelet[0, moment], 0.0)  33.5 us
    ppermute x9, waiting for transfers between devices, ag_step(): theirs = lax.ppermute(held, 'shot', [(i, i ^ k) for i in range(n)])  32.6 us
    add x2, other arithmetic, born_second(): 2.0 * born + speed_term * laplace_x(with_halo(born)) - absorber * born  22.4 us
    ppermute x6, waiting for transfers between devices, rs_step(): return keep + lax.ppermute(send, 'shot', [(i, i ^ k) for i in range(n)])  15.5 us
    mul x1, other arithmetic, wave_step(): drive = speed_term * laplace_x(with_halo(current))  10.5 us
    concatenate x6, other arithmetic, with_halo(): return jnp.concatenate([before, x, after], axis=0)  9.9 us
    ppermute x9, starting transfers between devices, ag_step(): theirs = lax.ppermute(held, 'shot', [(i, i ^ k) for i in range(n)])  8.9 us
    ppermute x6, starting transfers between devices, rs_step(): return keep + lax.ppermute(send, 'shot', [(i, i ^ k) for i in range(n)])  8.67 us
  transfers between devices with their start and end apart: 22, of which 8 were waited for; matrix products, arithmetic and copies ran while one was open for 38% of the time, Pallas kernels for 0%

profile of v4, /device:TPU:0, one launch (start us, length us, event | category | flops | bytes accessed | tf_op | source)
XLA Modules:
  0.0 185.4 jit_solution(15965349791890545376)
XLA Ops:
  3.3 3.7 %collective-permute-start = (f32[1,16,2048]{2,1,0:T(8,128)S(1)}, f32[1,16,2048]{2,1,0:T(8,128)}, u32[]{:S(2)}, u32[]{:S(2)}) collective-permute-start(f32[1,16,2048]{2,1,0:T(8,128)S(1)} %stack.117), channel_id=1, source_target_pairs={{0,8},{2,10},{4,12},{6,14},{8,0},{10,2},{12,4},{14,6},{1,9},{3,11}... | collective-permute-start | bytes 393224 | tf_op jit(solution)/shard_map/ppermute | solution.py:113
  7.8 1.4 multiply_multiply_fusion
  10.6 1.3 fusion.225
  13.1 1.3 fusion.224
  17.6 2.1 %select_maximum_fusion.10 = f32[40,72,136]{2,1,0:T(8,128)S(1)} fusion(f32[4,64,128]{2,1,0:T(8,128)S(1)} %get-tuple-element.122, f32[32,64,128]{2,1,0:T(8,128)} %bitcast.106, f32[4,64,128]{2,1,0:T(8,128)S(1)} %get-tuple-element.121), kind=kLoop, calls=%fused_computation.16 | loop fusion | flops 5875200 | bytes 2877440 | tf_op jit(solution)/shard_map/concatenate | solution.py:48
  19.7 11.1 %fusion.184 = (f32[32,64,128]{2,1,0:T(8,128)}, f32[32,64,128]{2,1,0:T(8,128)}) fusion(f32[]{:T(128)S(6)} %mul.334, f32[128]{0:T(128)S(1)} %fusion.224, f32[32,64]{1,0:T(8,128)S(1)} %broadcast_add_fusion, pred[128]{0:T(512)(128)(4,1)S(1)} %iota_compare_fusion.5, pred[32,64]{1,0:T(8,128)(4,1)S(1)} %broadcast_and_fusion, f32[1,32,64,128]{3,2,1,0:T(8,128)} %param.11, ...), kind=kLoop, calls=%fused_computation.280 | loop fusion | flops 14155776 | bytes 23341700 | tf_op jit(solution)/shard_map/add | solution.py:167
  33.1 2.1 %select_maximum_fusion.8 = f32[40,72,136]{2,1,0:T(8,128)S(1)} fusion(f32[4,64,128]{2,1,0:T(8,128)S(1)} %get-tuple-element.120, f32[32,64,128]{2,1,0:T(8,128)} %get-tuple-element.47, f32[4,64,128]{2,1,0:T(8,128)S(1)} %get-tuple-element.119), kind=kLoop, calls=%fused_computation.14 | loop fusion | flops 5875200 | bytes 2877440 | tf_op jit(solution)/shard_map/concatenate | solution.py:48
  35.2 11.5 %fusion.185 = (f32[32,64,128]{2,1,0:T(8,128)}, f32[32,64,128]{2,1,0:T(8,128)}) fusion(f32[]{:T(128)S(6)} %mul.345, f32[]{:T(128)S(6)} %mul.334, f32[128]{0:T(128)S(1)} %fusion.224, f32[32,64]{1,0:T(8,128)S(1)} %broadcast_add_fusion, f32[32,64,128]{2,1,0:T(8,128)} %get-tuple-element.61, pred[128]{0:T(512)(128)(4,1)S(1)} %iota_compare_fusion.5, ...), kind=kLoop, calls=%fused_computation.281 | loop fusion | flops 16252928 | bytes 24390280 | tf_op jit(solution)/shard_map/add | solution.py:167
  46.7 1.8 multiply_add_fusion.1
  49.0 1.8 collective-permute-start.5
  51.6 1.5 collective-permute-start.6
  54.5 10.9 %fusion.186 = (f32[32,64,128]{2,1,0:T(8,128)}, f32[32,64,128]{2,1,0:T(8,128)}) fusion(f32[32,64,128]{2,1,0:T(8,128)} %get-tuple-element.46, f32[32,64,128]{2,1,0:T(8,128)} %get-tuple-element.47, f32[]{:T(128)S(6)} %mul.354, f32[128]{0:T(128)S(1)} %fusion.224, f32[32,64]{1,0:T(8,128)S(1)} %broadcast_add_fusion, pred[128]{0:T(512)(128)(4,1)S(1)} %iota_compare_fusion.5, ...), kind=kLoop, calls=%fused_computation.282 | loop fusion | flops 14155776 | bytes 22293124 | tf_op jit(solution)/shard_map/add | solution.py:167
  66.6 1.3 bitcast_add_fusion
  68.8 1.6 collective-permute-start.10
  71.6 10.2 %collective-permute-done.9 = f32[4,16,64]{2,1,0:T(8,128)S(1)} collective-permute-done((f32[4,16,64]{2,1,0:T(8,128)S(1)}, f32[4,16,64]{2,1,0:T(8,128)S(1)}, u32[]{:S(2)}, u32[]{:S(2)}) %collective-permute-start.9) | collective-permute-done | bytes 16416 | tf_op jit(solution)/shard_map/ppermute | solution.py:113
  85.1 2.6 %collective-permute-start.11 = (f32[1,4,64,128]{3,2,1,0:T(8,128)}, f32[1,4,64,128]{3,2,1,0:T(8,128)}, u32[]{:S(2)}, u32[]{:S(2)}) collective-permute-start(f32[1,4,64,128]{3,2,1,0:T(8,128)} %constant_dynamic-slice_fusion.5), channel_id=1, source_target_pairs={{0,8},{2,10},{4,12},{6,14},{8,0},{10,2},{12,4},{14,6},{1,9},{3,11}... | collective-permute-start | bytes 393224 | tf_op jit(solution)/shard_map/ppermute | solution.py:127
  87.7 2.1 %select_maximum_fusion.4 = f32[40,72,136]{2,1,0:T(8,128)S(1)} fusion(f32[4,64,128]{2,1,0:T(8,128)S(1)} %get-tuple-element.115, f32[32,64,128]{2,1,0:T(8,128)} %copy-done.1, f32[4,64,128]{2,1,0:T(8,128)S(1)} %get-tuple-element.116), kind=kLoop, calls=%fused_computation.10 | loop fusion | flops 5875200 | bytes 2877440 | tf_op jit(solution)/shard_map/concatenate | solution.py:48
  89.7 11.4 %fusion.77 = f32[32,64,128]{2,1,0:T(8,128)} fusion(f32[32,64,128]{2,1,0:T(8,128)} %copy-done.1, f32[4,64,128]{2,1,0:T(8,128)S(1)} %get-tuple-element.116, f32[4,64,128]{2,1,0:T(8,128)S(1)} %get-tuple-element.115, f32[40,72,136]{2,1,0:T(8,128)S(1)} %select_maximum_fusion.4, f32[32,64,128]{2,1,0:T(8,128)} %bitcast.111, f32[32,64,128]{2,1,0:T(8,128)} %get-tuple-element.63, ...), kind=kLoop, calls=%fused_computation.173 | loop fusion | flops 13369344 | bytes 22290944 | tf_op jit(solution)/shard_map/add | solution.py:178
  101.1 1.6 dynamic-slice_add_fusion.1
  103.9 2.6 %multiply_add_fusion = f32[32,64,128]{2,1,0:T(8,128)S(1)} fusion(f32[32,64,128]{2,1,0:T(8,128)} %get-tuple-element.63, f32[32,64,128]{2,1,0:T(8,128)} %fusion.77, f32[32,64,128]{2,1,0:T(8,128)} %get-tuple-element.61, f32[32,64,128]{2,1,0:T(8,128)} %copy-done.1), kind=kLoop, calls=%fused_computation.333 | loop fusion | flops 786432 | bytes 5242880 | tf_op jit(solution)/shard_map/add | solution.py:242
  108.9 10.5 %fusion.45 = f32[32,64,128]{2,1,0:T(8,128)} fusion(f32[32,64,128]{2,1,0:T(8,128)} %get-tuple-element.66, f32[4,64,128]{2,1,0:T(8,128)S(1)} %get-tuple-element.114, f32[4,64,128]{2,1,0:T(8,128)S(1)} %get-tuple-element.113, f32[40,72,136]{2,1,0:T(8,128)S(1)} %select_maximum_fusion.2, s32[32,64,128]{2,1,0:T(8,128)} %param.13), kind=kLoop, calls=%fused_computation.141 | loop fusion | flops 11272192 | bytes 20185088 | tf_op jit(solution)/shard_map/mul | solution.py:170
  119.4 2.5 %collective-permute-done.13 = f32[4,4,64,128]{3,2,1,0:T(8,128)} collective-permute-done((f32[4,4,64,128]{3,2,1,0:T(8,128)}, f32[4,4,64,128]{3,2,1,0:T(8,128)}, u32[]{:S(2)}, u32[]{:S(2)}) %collective-permute-start.13) | collective-permute-done | bytes 524320 | tf_op jit(solution)/shard_map/ppermute | solution.py:127
  123.2 1.6 collective-permute-start.15
  124.8 6.1 %collective-permute-done.15 = f32[2,4,64,128]{3,2,1,0:T(8,128)S(1)} collective-permute-done((f32[2,4,64,128]{3,2,1,0:T(8,128)S(1)}, f32[2,4,64,128]{3,2,1,0:T(8,128)S(1)}, u32[]{:S(2)}, u32[]{:S(2)}) %collective-permute-start.15) | collective-permute-done | bytes 262176 | tf_op jit(solution)/shard_map/ppermute | solution.py:127
  131.8 6.9 %collective-permute-done.16 = f32[1,4,64,128]{3,2,1,0:T(8,128)S(1)} collective-permute-done((f32[1,4,64,128]{3,2,1,0:T(8,128)S(1)}, f32[1,4,64,128]{3,2,1,0:T(8,128)S(1)}, u32[]{:S(2)}, u32[]{:S(2)}) %collective-permute-start.16) | collective-permute-done | bytes 131104 | tf_op jit(solution)/shard_map/ppermute | solution.py:127
  140.5 6.6 %collective-permute-done.17 = f32[1,4,64,128]{3,2,1,0:T(8,128)S(1)} collective-permute-done((f32[1,4,64,128]{3,2,1,0:T(8,128)S(1)}, f32[1,4,64,128]{3,2,1,0:T(8,128)S(1)}, u32[]{:S(2)}, u32[]{:S(2)}) %collective-permute-start.17) | collective-permute-done | bytes 131104 | tf_op jit(solution)/shard_map/ppermute | solution.py:113
  147.3 6.3 %collective-permute-done.18 = f32[2,4,64,128]{3,2,1,0:T(8,128)S(1)} collective-permute-done((f32[2,4,64,128]{3,2,1,0:T(8,128)S(1)}, f32[2,4,64,128]{3,2,1,0:T(8,128)S(1)}, u32[]{:S(2)}, u32[]{:S(2)}) %collective-permute-start.18) | collective-permute-done | bytes 262176 | tf_op jit(solution)/shard_map/ppermute | solution.py:113
  154.4 9.4 %collective-permute-done.19 = f32[4,4,64,128]{3,2,1,0:T(8,128)S(1)} collective-permute-done((f32[4,4,64,128]{3,2,1,0:T(8,128)S(1)}, f32[4,4,64,128]{3,2,1,0:T(8,128)S(1)}, u32[]{:S(2)}, u32[]{:S(2)}) %collective-permute-start.19) | collective-permute-done | bytes 524320 | tf_op jit(solution)/shard_map/ppermute | solution.py:113
  166.7 2.1 %select_maximum_fusion = f32[40,72,136]{2,1,0:T(8,128)S(1)} fusion(f32[4,64,128]{2,1,0:T(8,128)S(1)} %get-tuple-element.111, f32[32,64,128]{2,1,0:T(8,128)} %copy-done.2, f32[4,64,128]{2,1,0:T(8,128)S(1)} %get-tuple-element.112), kind=kLoop, calls=%fused_computation.6 | loop fusion | flops 5875200 | bytes 2877440 | tf_op jit(solution)/shard_map/concatenate | solution.py:48
  168.8 11.0 %fusion.16 = f32[32,64,128]{2,1,0:T(8,128)} fusion(f32[32,64,128]{2,1,0:T(8,128)} %copy-done.2, f32[4,64,128]{2,1,0:T(8,128)S(1)} %get-tuple-element.112, f32[4,64,128]{2,1,0:T(8,128)S(1)} %get-tuple-element.111, f32[40,72,136]{2,1,0:T(8,128)S(1)} %select_maximum_fusion, f32[32,64,128]{2,1,0:T(8,128)} %fusion.45, f32[128]{0:T(128)S(1)} %copy-done.13, ...), kind=kLoop, calls=%fused_computation.112 | loop fusion | flops 13369344 | bytes 22290944 | tf_op jit(solution)/shard_map/add | solution.py:178
  179.8 1.9 %gather_fusion.1 = f32[256,128]{1,0:T(8,128)S(1)} fusion(f32[2048,128]{1,0:T(8,128)} %bitcast.112, s32[1024]{0:T(1024)S(1)} %pad_clamp_fusion), kind=kCustom, calls=%fused_computation.1.clone | custom fusion | bytes 263168 | tf_op jit(solution)/shard_map/jit(_take)/gather | solution.py:269
  182.2 1.6 constant_dynamic-slice_fusion.1
  (138 shorter events, 30.5 us)
Async XLA Ops:
  0.6 16.9 %copy-start.14 = (f32[16,64]{1,0:T(8,128)S(1)}, f32[16,64]{1,0:T(8,128)}, u32[]{:S(2)}) copy-start(f32[16,64]{1,0:T(8,128)} %param.15) | copy-start | bytes 12292
  0.6 8.5 %copy-start.15 = (f32[1,4]{1,0:T(1,128)S(1)}, f32[1,4]{1,0:T(1,128)}, u32[]{:S(2)}) copy-start(f32[1,4]{1,0:T(1,128)} %param.16) | copy-start | bytes 52
  0.7 9.2 %copy-start.18 = (s32[6]{0:T(128)S(1)}, s32[6]{0:T(128)}, u32[]{:S(2)}) copy-start(s32[6]{0:T(128)} %param.19) | copy-start | bytes 76
  1.6 16.0 %collective-permute-start.2 = (f32[4,64,128]{2,1,0:T(8,128)S(1)}, f32[4,64,128]{2,1,0:T(8,128)S(1)}, u32[]{:S(2)}, u32[]{:S(2)}) collective-permute-start(f32[4,64,128]{2,1,0:T(8,128)S(1)} %dynamic-slice_bitcast_fusion.4), channel_id=1, source_target_pairs={{0,1},{1,0},{2,3},{3,2},{4,5},{5,4},{6,7},{7,6},{8,9},{9,8},{10,11... | collective-permute-start | bytes 393224 | tf_op jit(solution)/shard_map/ppermute | solution.py:44
  3.3 16.4 %copy-start.10 = (f32[1,16,2048]{2,1,0:T(8,128)}, f32[1,16,2048]{2,1,0:T(8,128)S(1)}, u32[]{:S(2)}) copy-start(f32[1,16,2048]{2,1,0:T(8,128)S(1)} %stack.117) | copy-start | bytes 393220
  3.3 28.7 %collective-permute-start = (f32[1,16,2048]{2,1,0:T(8,128)S(1)}, f32[1,16,2048]{2,1,0:T(8,128)}, u32[]{:S(2)}, u32[]{:S(2)}) collective-permute-start(f32[1,16,2048]{2,1,0:T(8,128)S(1)} %stack.117), channel_id=1, source_target_pairs={{0,8},{2,10},{4,12},{6,14},{8,0},{10,2},{12,4},{14,6},{1,9},{3,11}... | collective-permute-start | bytes 393224 | tf_op jit(solution)/shard_map/ppermute | solution.py:113
  6.9 10.6 %collective-permute-start.1 = (f32[1,16,64]{2,1,0:T(8,128)}, f32[1,16,64]{2,1,0:T(8,128)S(1)}, u32[]{:S(2)}, u32[]{:S(2)}) collective-permute-start(f32[1,16,64]{2,1,0:T(8,128)} %bitcast.145), channel_id=1, source_target_pairs={{0,8},{2,10},{4,12},{6,14},{8,0},{10,2},{12,4},{14,6},{1,9},{3,11}... | collective-permute-start | bytes 12296 | tf_op jit(solution)/shard_map/ppermute | solution.py:113
  14.4 40.1 %copy-start.12 = (f32[128]{0:T(128)}, f32[128]{0:T(128)S(1)}, u32[]{:S(2)}) copy-start(f32[128]{0:T(128)S(1)} %fusion.224) | copy-start | bytes 1540
  31.7 1.4 collective-permute-start.3
  48.6 5.0 %collective-permute-start.7 = (f32[4,64,128]{2,1,0:T(8,128)S(1)}, f32[4,64,128]{2,1,0:T(8,128)S(1)}, u32[]{:S(2)}, u32[]{:S(2)}) collective-permute-start(f32[4,64,128]{2,1,0:T(8,128)S(1)} %constant_dynamic-slice_fusion.6), channel_id=1, source_target_pairs={{0,1},{1,0},{2,3},{3,2},{4,5},{5,4},{6,7},{7,6},{8,9},{9,8},{10,11... | collective-permute-start | bytes 393224 | tf_op jit(solution)/shard_map/ppermute | solution.py:44
  49.0 4.6 %collective-permute-start.5 = (f32[2,16,64]{2,1,0:T(8,128)S(1)}, f32[2,16,64]{2,1,0:T(8,128)S(1)}, u32[]{:S(2)}, u32[]{:S(2)}) collective-permute-start(f32[2,16,64]{2,1,0:T(8,128)S(1)} %maximum_select_fusion.9), channel_id=1, source_target_pairs={{0,4},{2,6},{4,0},{6,2},{8,12},{10,14},{12,8},{14,10},{1,5},{3,7},... | collective-permute-start | bytes 24584 | tf_op jit(solution)/shard_map/ppermute | solution.py:113
  51.6 14.9 %collective-permute-start.6 = (f32[4,4,64,128]{3,2,1,0:T(8,128)}, f32[4,4,64,128]{3,2,1,0:T(8,128)}, u32[]{:S(2)}, u32[]{:S(2)}) collective-permute-start(f32[4,4,64,128]{3,2,1,0:T(8,128)} %dynamic-slice_bitcast_fusion.1), channel_id=1, source_target_pairs={{0,2},{2,0},{4,6},{6,4},{8,10},{10,8},{12,14},{14,12},{1,3},{3,1},... | collective-permute-start | bytes 1572872 | tf_op jit(solution)/shard_map/ppermute | solution.py:127
  53.1 12.3 %collective-permute-start.4 = (f32[2,16,2048]{2,1,0:T(8,128)S(1)}, f32[2,16,2048]{2,1,0:T(8,128)}, u32[]{:S(2)}, u32[]{:S(2)}) collective-permute-start(f32[2,16,2048]{2,1,0:T(8,128)S(1)} %maximum_select_fusion.4), channel_id=1, source_target_pairs={{0,4},{2,6},{4,0},{6,2},{8,12},{10,14},{12,8},{14,10},{1,5},{3,7},... | collective-permute-start | bytes 786440 | tf_op jit(solution)/shard_map/ppermute | solution.py:113
  67.9 14.0 %collective-permute-start.8 = (f32[4,16,2048]{2,1,0:T(8,128)S(1)}, f32[4,16,2048]{2,1,0:T(8,128)S(1)}, u32[]{:S(2)}, u32[]{:S(2)}) collective-permute-start(f32[4,16,2048]{2,1,0:T(8,128)S(1)} %bitcast.119), channel_id=1, source_target_pairs={{0,2},{2,0},{4,6},{6,4},{8,10},{10,8},{12,14},{14,12},{1,3},{3,1},... | collective-permute-start | bytes 1572872 | tf_op jit(solution)/shard_map/ppermute | solution.py:113
  68.8 13.0 %collective-permute-start.10 = (f32[2,4,64,128]{3,2,1,0:T(8,128)S(1)}, f32[2,4,64,128]{3,2,1,0:T(8,128)S(1)}, u32[]{:S(2)}, u32[]{:S(2)}) collective-permute-start(f32[2,4,64,128]{3,2,1,0:T(8,128)S(1)} %dynamic-slice_bitcast_fusion.3), channel_id=1, source_target_pairs={{0,4},{2,6},{4,0},{6,2},{8,12},{10,14},{12,8},{14,10},{1,5},{3,7},... | collective-permute-start | bytes 786440 | tf_op jit(solution)/shard_map/ppermute | solution.py:127
  70.5 11.4 %collective-permute-start.9 = (f32[4,16,64]{2,1,0:T(8,128)S(1)}, f32[4,16,64]{2,1,0:T(8,128)S(1)}, u32[]{:S(2)}, u32[]{:S(2)}) collective-permute-start(f32[4,16,64]{2,1,0:T(8,128)S(1)} %bitcast.138), channel_id=1, source_target_pairs={{0,2},{2,0},{4,6},{6,4},{8,10},{10,8},{12,14},{14,12},{1,3},{3,1},... | collective-permute-start | bytes 49160 | tf_op jit(solution)/shard_map/ppermute | solution.py:113
  82.4 5.2 %copy-start.6 = (f32[2048,128]{1,0:T(8,128)}, f32[2048,128]{1,0:T(8,128)S(1)}, u32[]{:S(2)}) copy-start(f32[2048,128]{1,0:T(8,128)S(1)} %copy.37) | copy-start | bytes 3145732
  84.3 3.4 %collective-permute-start.12 = (f32[4,64,128]{2,1,0:T(8,128)S(1)}, f32[4,64,128]{2,1,0:T(8,128)S(1)}, u32[]{:S(2)}, u32[]{:S(2)}) collective-permute-start(f32[4,64,128]{2,1,0:T(8,128)S(1)} %constant_dynamic-slice_fusion.4), channel_id=1, source_target_pairs={{0,1},{1,0},{2,3},{3,2},{4,5},{5,4},{6,7},{7,6},{8,9},{9,8},{10,11... | collective-permute-start | bytes 393224 | tf_op jit(solution)/shard_map/ppermute | solution.py:44
  85.1 16.1 %collective-permute-start.11 = (f32[1,4,64,128]{3,2,1,0:T(8,128)}, f32[1,4,64,128]{3,2,1,0:T(8,128)}, u32[]{:S(2)}, u32[]{:S(2)}) collective-permute-start(f32[1,4,64,128]{3,2,1,0:T(8,128)} %constant_dynamic-slice_fusion.5), channel_id=1, source_target_pairs={{0,8},{2,10},{4,12},{6,14},{8,0},{10,2},{12,4},{14,6},{1,9},{3,11}... | collective-permute-start | bytes 393224 | tf_op jit(solution)/shard_map/ppermute | solution.py:127
  103.6 4.4 %collective-permute-start.14 = (f32[4,64,128]{2,1,0:T(8,128)S(1)}, f32[4,64,128]{2,1,0:T(8,128)S(1)}, u32[]{:S(2)}, u32[]{:S(2)}) collective-permute-start(f32[4,64,128]{2,1,0:T(8,128)S(1)} %constant_dynamic-slice_fusion.3), channel_id=1, source_target_pairs={{0,1},{1,0},{2,3},{3,2},{4,5},{5,4},{6,7},{7,6},{8,9},{9,8},{10,11... | collective-permute-start | bytes 393224 | tf_op jit(solution)/shard_map/ppermute | solution.py:44
  107.5 14.4 %collective-permute-start.13 = (f32[4,4,64,128]{3,2,1,0:T(8,128)}, f32[4,4,64,128]{3,2,1,0:T(8,128)}, u32[]{:S(2)}, u32[]{:S(2)}) collective-permute-start(f32[4,4,64,128]{3,2,1,0:T(8,128)} %dynamic-slice_bitcast_fusion), channel_id=1, source_target_pairs={{0,2},{2,0},{4,6},{6,4},{8,10},{10,8},{12,14},{14,12},{1,3},{3,1},... | collective-permute-start | bytes 1572872 | tf_op jit(solution)/shard_map/ppermute | solution.py:127
  119.4 19.3 %copy-start.11 = (f32[1,4,64,128]{3,2,1,0:T(8,128)S(1)}, f32[1,4,64,128]{3,2,1,0:T(8,128)}, u32[]{:S(2)}) copy-start(f32[1,4,64,128]{3,2,1,0:T(8,128)} %dynamic-slice_add_fusion.1) | copy-start | bytes 393220
  123.2 7.7 %collective-permute-start.15 = (f32[2,4,64,128]{3,2,1,0:T(8,128)S(1)}, f32[2,4,64,128]{3,2,1,0:T(8,128)S(1)}, u32[]{:S(2)}, u32[]{:S(2)}) collective-permute-start(f32[2,4,64,128]{3,2,1,0:T(8,128)S(1)} %dynamic-slice_bitcast_fusion.2), channel_id=1, source_target_pairs={{0,4},{2,6},{4,0},{6,2},{8,12},{10,14},{12,8},{14,10},{1,5},{3,7},... | collective-permute-start | bytes 786440 | tf_op jit(solution)/shard_map/ppermute | solution.py:127
  130.9 23.4 %copy-start.16 = (s32[1,256]{1,0:T(1,128)S(1)}, s32[1,256]{1,0:T(1,128)}, u32[]{:S(2)}) copy-start(s32[1,256]{1,0:T(1,128)} %param.18) | copy-start | bytes 3076
  131.0 7.7 %collective-permute-start.16 = (f32[1,4,64,128]{3,2,1,0:T(8,128)S(1)}, f32[1,4,64,128]{3,2,1,0:T(8,128)S(1)}, u32[]{:S(2)}, u32[]{:S(2)}) collective-permute-start(f32[1,4,64,128]{3,2,1,0:T(8,128)S(1)} %constant_dynamic-slice_fusion.2), channel_id=1, source_target_pairs={{0,8},{2,10},{4,12},{6,14},{8,0},{10,2},{12,4},{14,6},{1,9},{3,11}... | collective-permute-start | bytes 393224 | tf_op jit(solution)/shard_map/ppermute | solution.py:127
  140.5 6.7 %collective-permute-start.17 = (f32[1,4,64,128]{3,2,1,0:T(8,128)S(1)}, f32[1,4,64,128]{3,2,1,0:T(8,128)S(1)}, u32[]{:S(2)}, u32[]{:S(2)}) collective-permute-start(f32[1,4,64,128]{3,2,1,0:T(8,128)S(1)} %bitcast.127), channel_id=1, source_target_pairs={{0,8},{2,10},{4,12},{6,14},{8,0},{10,2},{12,4},{14,6},{1,9},{3,11}... | collective-permute-start | bytes 393224 | tf_op jit(solution)/shard_map/ppermute | solution.py:113
  147.2 6.4 %collective-permute-start.18 = (f32[2,4,64,128]{3,2,1,0:T(8,128)S(1)}, f32[2,4,64,128]{3,2,1,0:T(8,128)S(1)}, u32[]{:S(2)}, u32[]{:S(2)}) collective-permute-start(f32[2,4,64,128]{3,2,1,0:T(8,128)S(1)} %maximum_select_fusion.6), channel_id=1, source_target_pairs={{0,4},{2,6},{4,0},{6,2},{8,12},{10,14},{12,8},{14,10},{1,5},{3,7},... | collective-permute-start | bytes 786440 | tf_op jit(solution)/shard_map/ppermute | solution.py:113
  153.7 11.3 %copy-start.7 = (f32[32,64,128]{2,1,0:T(8,128)S(1)}, f32[32,64,128]{2,1,0:T(8,128)}, u32[]{:S(2)}) copy-start(f32[32,64,128]{2,1,0:T(8,128)} %get-tuple-element.76) | copy-start | bytes 3145732
  153.8 10.0 %collective-permute-start.19 = (f32[4,4,64,128]{3,2,1,0:T(8,128)S(1)}, f32[4,4,64,128]{3,2,1,0:T(8,128)S(1)}, u32[]{:S(2)}, u32[]{:S(2)}) collective-permute-start(f32[4,4,64,128]{3,2,1,0:T(8,128)S(1)} %bitcast.121), channel_id=1, source_target_pairs={{0,2},{2,0},{4,6},{6,4},{8,10},{10,8},{12,14},{14,12},{1,3},{3,1},... | collective-permute-start | bytes 1572872 | tf_op jit(solution)/shard_map/ppermute | solution.py:113
  165.2 1.4 collective-permute-start.20
  168.8 13.2 %copy-start.17 = (s32[1,256]{1,0:T(1,128)S(1)}, s32[1,256]{1,0:T(1,128)}, u32[]{:S(2)}) copy-start(s32[1,256]{1,0:T(1,128)} %param.18) | copy-start | bytes 3076
  182.0 2.8 %collective-permute-start.21 = (f32[1,2,256]{2,1,0:T(2,128)S(1)}, f32[1,2,256]{2,1,0:T(2,128)S(1)}, u32[]{:S(2)}, u32[]{:S(2)}) collective-permute-start(f32[1,2,256]{2,1,0:T(2,128)S(1)} %maximum_bitcast_fusion), channel_id=1, source_target_pairs={{0,1},{1,0},{2,3},{3,2},{4,5},{5,4},{6,7},{7,6},{8,9},{9,8},{10,11... | collective-permute-start | bytes 6152 | tf_op jit(solution)/shard_map/ppermute | solution.py:274
  (9 other events, 21.1 us)

commit v5 on v4

--- a/solution.py
+++ b/solution.py
@@ -42,10 +42,9 @@
         me = lax.axis_index("space")
         piece = lax.dynamic_slice_in_dim(x, (1 - me) * (length - HALO), HALO, 0)
         got = lax.ppermute(piece, "space", [(0, 1), (1, 0)])
-        zero = jnp.zeros_like(got)
-        before = jnp.where(me == 1, got, zero)
-        after = jnp.where(me == 0, got, zero)
-        return jnp.concatenate([before, x, after], axis=0)
+        zeros = jnp.zeros((HALO,) + x.shape[1:], x.dtype)
+        padded = jnp.concatenate([zeros, x, zeros], axis=0)
+        return lax.dynamic_update_slice_in_dim(padded, got, (1 - me) * (length + HALO), 0)
     up = [(i, (i + 1) % size) for i in range(size - 1)]
     down = [(j, i) for i, j in up]
     before = lax.ppermute(x[length - HALO :], "space", up)

time: 186 us -> 158 us (0.85)
  other arithmetic: 94 us -> 40.5 us
  waiting for transfers between devices: 48.7 us -> 71.3 us
  local copies, waits for them, and re-layouts: 17 us -> 19.8 us
    add x3, other arithmetic: 33.5 us -> 11.7 us  [inject(): return field + jnp.where(hit, source_gain[0] * wavelet[0, moment], 0.0)]
    add x2, other arithmetic: 22.4 us -> 5.85 us  [born_second(): 2.0 * born + speed_term * laplace_x(with_halo(born)) - absorber * born]
    ppermute x6, waiting for transfers between devices: 15.5 us -> 30.8 us  [rs_step(): return keep + lax.ppermute(send, 'shot', [(i, i ^ k) for i in range(n)])]
    concatenate x6, other arithmetic: 9.9 us -> 0.92 us  [with_halo(): padded = jnp.concatenate([zeros, x, zeros], axis=0)]
    ppermute x9, waiting for transfers between devices: 32.6 us -> 39.9 us  [ag_step(): theirs = lax.ppermute(held, 'shot', [(i, i ^ k) for i in range(n)])]
    mul x1, other arithmetic: 10.5 us -> 3.24 us  [wave_step(): drive = speed_term * laplace_x(with_halo(current))]
    select_n x10, other arithmetic: 2.51 us -> 5.28 us  [ag_step(): jnp.where(low, jnp.stack([held, theirs], axis=1), jnp.stack([theirs, held...]
    select_n x5, local copies, waits for them, and re-layouts: 0.28 us -> 2.65 us  [ag_step(): jnp.where(low, jnp.stack([held, theirs], axis=1), jnp.stack([theirs, held...]
  transfers between devices with their start and end apart: 22 -> 22, of which waited for: 8 -> 11; matrix products, arithmetic and copies ran while one was open for 38% -> 24% of each run, Pallas kernels for 0% -> 0%
where the time goes in v5:
time: 158 us
  waiting for transfers between devices  71.3 us (45%)
  other arithmetic  40.5 us (26%)
  local copies, waits for them, and re-layouts  19.8 us (13%)
  starting transfers between devices  19.6 us (12%)
  between operations  4.59 us (3%)
  matrix products  1.7 us (1%)
    ppermute x9, waiting for transfers between devices, ag_step(): theirs = lax.ppermute(held, 'shot', [(i, i ^ k) for i in range(n)])  39.9 us
    ppermute x6, waiting for transfers between devices, rs_step(): return keep + lax.ppermute(send, 'shot', [(i, i ^ k) for i in range(n)])  30.8 us
    add x3, other arithmetic, inject(): return field + jnp.where(hit, source_gain[0] * wavelet[0, moment], 0.0)  11.7 us
    ppermute x9, starting transfers between devices, ag_step(): theirs = lax.ppermute(held, 'shot', [(i, i ^ k) for i in range(n)])  9.88 us
    ppermute x6, starting transfers between devices, rs_step(): return keep + lax.ppermute(send, 'shot', [(i, i ^ k) for i in range(n)])  7.88 us
    add x2, other arithmetic, born_second(): 2.0 * born + speed_term * laplace_x(with_halo(born)) - absorber * born  5.85 us
    select_n x10, other arithmetic, ag_step(): jnp.where(low, jnp.stack([held, theirs], axis=1), jnp.stack([theirs, held...  5.28 us
    add x3, other arithmetic, ramp(): return low_part * low_part + high_part * high_part  4.41 us
  transfers between devices with their start and end apart: 22, of which 11 were waited for; matrix products, arithmetic and copies ran while one was open for 24% of the time, Pallas kernels for 0%

profile of v5, /device:TPU:0, one launch (start us, length us, event | category | flops | bytes accessed | tf_op | source)
XLA Modules:
  0.0 157.5 jit_solution(615291174211906923)
XLA Ops:
  0.6 1.7 %dynamic-slice_bitcast_fusion.4 = f32[4,64,128]{2,1,0:T(8,128)} fusion(f32[1,32,64,128]{3,2,1,0:T(8,128)} %param.12, s32[]{:T(128)S(6)} %select_n.324), kind=kLoop, calls=%fused_computation.336 | loop fusion | bytes 262148 | tf_op jit(solution)/shard_map/dynamic_slice | solution.py:43
  4.6 3.6 %collective-permute-start = (f32[1,16,2048]{2,1,0:T(8,128)}, f32[1,16,2048]{2,1,0:T(8,128)}, u32[]{:S(2)}, u32[]{:S(2)}) collective-permute-start(f32[1,16,2048]{2,1,0:T(8,128)} %stack.117), channel_id=1, source_target_pairs={{0,8},{2,10},{4,12},{6,14},{8,0},{10,2},{12,4},{14,6},{1,9},{3,11}... | collective-permute-start | bytes 393224 | tf_op jit(solution)/shard_map/ppermute | solution.py:112
  12.8 1.3 fusion.186
  14.1 1.3 fusion.187
  15.4 1.9 %fusion.185 = f32[128]{0:T(128)} fusion(f32[]{:T(128)} %bitcast.11, f32[]{:T(128)} %bitcast.10), kind=kLoop, calls=%fused_computation.388 | loop fusion | flops 1280 | bytes 520 | tf_op jit(solution)/shard_map/add | solution.py:27
  17.3 1.4 dynamic-slice.7
  22.9 4.5 %fusion.1 = (f32[32,64,128]{2,1,0:T(8,128)S(1)}, f32[32,64,128]{2,1,0:T(8,128)S(1)}) fusion(f32[]{:T(128)S(6)} %mul.343, f32[128]{0:T(128)} %fusion.185, f32[32,64]{1,0:T(8,128)S(1)} %broadcast_add_fusion, pred[128]{0:T(512)(128)(4,1)} %iota_compare_fusion.1, pred[32,64]{1,0:T(8,128)(4,1)} %broadcast_and_fusion, f32[1,32,64,128]{3,2,1,0:T(8,128)} %param.11, ...), kind=kLoop, calls=%fused_computation.117 | loop fusion | flops 12058624 | bytes 16009860 | tf_op jit(solution)/shard_map/add | solution.py:166
  30.4 3.2 %fusion.2 = (f32[32,64,128]{2,1,0:T(8,128)S(1)}, f32[32,64,128]{2,1,0:T(8,128)S(1)}) fusion(f32[]{:T(128)S(6)} %mul.354, f32[]{:T(128)S(6)} %mul.343, f32[128]{0:T(128)S(1)} %copy-done.14, f32[32,64]{1,0:T(8,128)S(1)} %broadcast_add_fusion, f32[32,64,128]{2,1,0:T(8,128)S(1)} %get-tuple-element.61, pred[128]{0:T(512)(128)(4,1)S(1)} %copy-done.17, ...), kind=kLoop, calls=%fused_computation.118 | loop fusion | flops 14155776 | bytes 17060872 | tf_op jit(solution)/shard_map/add | solution.py:166
  34.3 1.9 %collective-permute-start.5 = (f32[2,16,64]{2,1,0:T(8,128)S(1)}, f32[2,16,64]{2,1,0:T(8,128)S(1)}, u32[]{:S(2)}, u32[]{:S(2)}) collective-permute-start(f32[2,16,64]{2,1,0:T(8,128)S(1)} %maximum_select_fusion.9), channel_id=1, source_target_pairs={{0,4},{2,6},{4,0},{6,2},{8,12},{10,14},{12,8},{14,10},{1,5},{3,7},... | collective-permute-start | bytes 24584 | tf_op jit(solution)/shard_map/ppermute | solution.py:112
  36.3 1.6 %collective-permute-start.6 = (f32[4,4,64,128]{3,2,1,0:T(8,128)S(1)}, f32[4,4,64,128]{3,2,1,0:T(8,128)S(1)}, u32[]{:S(2)}, u32[]{:S(2)}) collective-permute-start(f32[4,4,64,128]{3,2,1,0:T(8,128)S(1)} %dynamic-slice_bitcast_fusion.1), channel_id=1, source_target_pairs={{0,2},{2,0},{4,6},{6,4},{8,10},{10,8},{12,14},{14,12},{1,3},{3,1},... | collective-permute-start | bytes 1572872 | tf_op jit(solution)/shard_map/ppermute | solution.py:126
  38.9 4.0 %fusion.3 = (f32[32,64,128]{2,1,0:T(8,128)}, f32[32,64,128]{2,1,0:T(8,128)}) fusion(f32[32,64,128]{2,1,0:T(8,128)S(1)} %get-tuple-element.46, f32[32,64,128]{2,1,0:T(8,128)S(1)} %get-tuple-element.47, f32[]{:T(128)S(6)} %mul.363, f32[128]{0:T(128)S(1)} %copy-done.14, f32[32,64]{1,0:T(8,128)S(1)} %broadcast_add_fusion, pred[128]{0:T(512)(128)(4,1)S(1)} %copy-done.17, ...), kind=kLoop, calls=%fused_computation.119 | loop fusion | flops 12058624 | bytes 16012292 | tf_op jit(solution)/shard_map/add | solution.py:166
  42.9 2.6 %collective-permute-done.4 = f32[2,16,2048]{2,1,0:T(8,128)S(1)} collective-permute-done((f32[2,16,2048]{2,1,0:T(8,128)S(1)}, f32[2,16,2048]{2,1,0:T(8,128)S(1)}, u32[]{:S(2)}, u32[]{:S(2)}) %collective-permute-start.4) | collective-permute-done | bytes 262176 | tf_op jit(solution)/shard_map/ppermute | solution.py:112
  46.4 3.5 %collective-permute-done.6 = f32[4,4,64,128]{3,2,1,0:T(8,128)S(1)} collective-permute-done((f32[4,4,64,128]{3,2,1,0:T(8,128)S(1)}, f32[4,4,64,128]{3,2,1,0:T(8,128)S(1)}, u32[]{:S(2)}, u32[]{:S(2)}) %collective-permute-start.6) | collective-permute-done | bytes 524320 | tf_op jit(solution)/shard_map/ppermute | solution.py:126
  50.0 1.6 %collective-permute-start.8 = (f32[4,16,2048]{2,1,0:T(8,128)}, f32[4,16,2048]{2,1,0:T(8,128)}, u32[]{:S(2)}, u32[]{:S(2)}) collective-permute-start(f32[4,16,2048]{2,1,0:T(8,128)} %bitcast.20), channel_id=1, source_target_pairs={{0,2},{2,0},{4,6},{6,4},{8,10},{10,8},{12,14},{14,12},{1,3},{3,1},... | collective-permute-start | bytes 1572872 | tf_op jit(solution)/shard_map/ppermute | solution.py:112
  52.9 11.0 %collective-permute-done.9 = f32[4,16,64]{2,1,0:T(8,128)} collective-permute-done((f32[4,16,64]{2,1,0:T(8,128)}, f32[4,16,64]{2,1,0:T(8,128)}, u32[]{:S(2)}, u32[]{:S(2)}) %collective-permute-start.9) | collective-permute-done | bytes 16416 | tf_op jit(solution)/shard_map/ppermute | solution.py:112
  66.4 1.7 %maximum_select_fusion = f32[4,2,16,2048]{3,2,0,1:T(8,128)S(1)} fusion(f32[4,1,16,2048]{3,2,0,1:T(8,128)} %bitcast.29, f32[4,1,16,2048]{3,2,0,1:T(8,128)} %bitcast.28, pred[]{:T(512)S(6)} %eq.83), kind=kLoop, calls=%fused_computation.306 | loop fusion | flops 786432 | bytes 2097153 | tf_op jit(solution)/shard_map/jit(_where)/select_n | solution.py:114
  69.2 2.5 %copy.37 = f32[2048,128]{1,0:T(8,128)} copy(f32[2048,128]{0,1:T(8,128)} %bitcast.119) | data formatting | bytes 2097152 | tf_op jit(solution)/shard_map/transpose | solution.py:234
  71.7 1.4 mul.364
  73.2 2.7 %collective-permute-start.11 = (f32[1,4,64,128]{3,2,1,0:T(8,128)S(1)}, f32[1,4,64,128]{3,2,1,0:T(8,128)S(1)}, u32[]{:S(2)}, u32[]{:S(2)}) collective-permute-start(f32[1,4,64,128]{3,2,1,0:T(8,128)S(1)} %constant_dynamic-slice_fusion.5), channel_id=1, source_target_pairs={{0,8},{2,10},{4,12},{6,14},{8,0},{10,2},{12,4},{14,6},{1,9},{3,11}... | collective-permute-start | bytes 393224 | tf_op jit(solution)/shard_map/ppermute | solution.py:126
  76.1 2.9 %fusion.91 = f32[32,64,128]{2,1,0:T(8,128)S(1)} fusion(f32[40,64,128]{2,1,0:T(8,128)S(1)} %constant_dynamic-update-slice_fusion.2, f32[32,64,128]{2,1,0:T(8,128)S(1)} %bitcast.112, f32[32,64,128]{2,1,0:T(8,128)S(1)} %get-tuple-element.63, f32[32,64,128]{2,1,0:T(8,128)S(1)} %mul.364, f32[128]{0:T(128)S(1)} %copy-done.15, f32[32,64]{1,0:T(8,128)S(1)} %broadcast_add_fusion, ...), kind=kLoop, calls=%fused_computation.207 | loop fusion | flops 11272192 | bytes 16007680 | tf_op jit(solution)/shard_map/add | solution.py:177
  79.0 3.7 %collective-permute-done.11 = f32[1,4,64,128]{3,2,1,0:T(8,128)S(1)} collective-permute-done((f32[1,4,64,128]{3,2,1,0:T(8,128)S(1)}, f32[1,4,64,128]{3,2,1,0:T(8,128)S(1)}, u32[]{:S(2)}, u32[]{:S(2)}) %collective-permute-start.11) | collective-permute-done | bytes 131104 | tf_op jit(solution)/shard_map/ppermute | solution.py:126
  84.1 1.5 collective-permute-start.13
  85.9 3.2 %fusion.116 = f32[32,64,128]{2,1,0:T(8,128)} fusion(f32[40,64,128]{2,1,0:T(8,128)S(1)} %constant_dynamic-update-slice_fusion.1, s32[32,64,128]{2,1,0:T(8,128)S(1)} %copy-done), kind=kLoop, calls=%fused_computation.232 | loop fusion | flops 9175040 | bytes 12845056 | tf_op jit(solution)/shard_map/mul | solution.py:169
  89.1 9.3 %collective-permute-done.13 = f32[4,4,64,128]{3,2,1,0:T(8,128)S(1)} collective-permute-done((f32[4,4,64,128]{3,2,1,0:T(8,128)S(1)}, f32[4,4,64,128]{3,2,1,0:T(8,128)S(1)}, u32[]{:S(2)}, u32[]{:S(2)}) %collective-permute-start.13) | collective-permute-done | bytes 524320 | tf_op jit(solution)/shard_map/ppermute | solution.py:126
  98.6 7.8 %collective-permute-done.15 = f32[2,4,64,128]{3,2,1,0:T(8,128)S(1)} collective-permute-done((f32[2,4,64,128]{3,2,1,0:T(8,128)S(1)}, f32[2,4,64,128]{3,2,1,0:T(8,128)S(1)}, u32[]{:S(2)}, u32[]{:S(2)}) %collective-permute-start.15) | collective-permute-done | bytes 262176 | tf_op jit(solution)/shard_map/ppermute | solution.py:126
  106.5 1.5 collective-permute-start.16
  108.1 6.4 %collective-permute-done.16 = f32[1,4,64,128]{3,2,1,0:T(8,128)S(1)} collective-permute-done((f32[1,4,64,128]{3,2,1,0:T(8,128)S(1)}, f32[1,4,64,128]{3,2,1,0:T(8,128)S(1)}, u32[]{:S(2)}, u32[]{:S(2)}) %collective-permute-start.16) | collective-permute-done | bytes 131104 | tf_op jit(solution)/shard_map/ppermute | solution.py:126
  116.3 8.6 %collective-permute-done.17 = f32[1,4,64,128]{3,2,1,0:T(8,128)S(1)} collective-permute-done((f32[1,4,64,128]{3,2,1,0:T(8,128)S(1)}, f32[1,4,64,128]{3,2,1,0:T(8,128)S(1)}, u32[]{:S(2)}, u32[]{:S(2)}) %collective-permute-start.17) | collective-permute-done | bytes 131104 | tf_op jit(solution)/shard_map/ppermute | solution.py:112
  125.1 8.0 %collective-permute-done.18 = f32[2,4,64,128]{3,2,1,0:T(8,128)S(1)} collective-permute-done((f32[2,4,64,128]{3,2,1,0:T(8,128)S(1)}, f32[2,4,64,128]{3,2,1,0:T(8,128)S(1)}, u32[]{:S(2)}, u32[]{:S(2)}) %collective-permute-start.18) | collective-permute-done | bytes 262176 | tf_op jit(solution)/shard_map/ppermute | solution.py:112
  133.2 1.5 collective-permute-start.19
  136.5 9.7 %collective-permute-done.19 = f32[4,4,64,128]{3,2,1,0:T(8,128)S(1)} collective-permute-done((f32[4,4,64,128]{3,2,1,0:T(8,128)S(1)}, f32[4,4,64,128]{3,2,1,0:T(8,128)S(1)}, u32[]{:S(2)}, u32[]{:S(2)}) %collective-permute-start.19) | collective-permute-done | bytes 524320 | tf_op jit(solution)/shard_map/ppermute | solution.py:112
  150.8 2.9 %fusion.144 = f32[32,64,128]{2,1,0:T(8,128)S(1)} fusion(f32[40,64,128]{2,1,0:T(8,128)S(1)} %constant_dynamic-update-slice_fusion, f32[32,64,128]{2,1,0:T(8,128)S(1)} %copy-done.8, f32[128]{0:T(128)S(1)} %copy-done.16, f32[32,64]{1,0:T(8,128)S(1)} %broadcast_add_fusion, f32[4,2,4,64,128]{4,3,2,1,0:T(8,128)S(1)} %copy.43, f32[32,64,128]{2,1,0:T(8,128)S(1)} %copy-done.4, ...), kind=kLoop, calls=%fused_computation.260 | loop fusion | flops 11534336 | bytes 16007680 | tf_op jit(solution)/shard_map/add | solution.py:177
  (149 shorter events, 32.6 us)
Async XLA Ops:
  0.6 8.9 %copy-start = (s32[32,64,128]{2,1,0:T(8,128)S(1)}, s32[32,64,128]{2,1,0:T(8,128)}, u32[]{:S(2)}) copy-start(s32[32,64,128]{2,1,0:T(8,128)} %param.13) | copy-start | bytes 3145732
  2.3 19.7 %collective-permute-start.2 = (f32[4,64,128]{2,1,0:T(8,128)}, f32[4,64,128]{2,1,0:T(8,128)}, u32[]{:S(2)}, u32[]{:S(2)}) collective-permute-start(f32[4,64,128]{2,1,0:T(8,128)} %dynamic-slice_bitcast_fusion.4), channel_id=1, source_target_pairs={{0,1},{1,0},{2,3},{3,2},{4,5},{5,4},{6,7},{7,6},{8,9},{9,8},{10,11... | collective-permute-start | bytes 393224 | tf_op jit(solution)/shard_map/ppermute | solution.py:44
  3.8 6.9 %copy-start.18 = (f32[1,4]{1,0:T(1,128)S(1)}, f32[1,4]{1,0:T(1,128)}, u32[]{:S(2)}) copy-start(f32[1,4]{1,0:T(1,128)} %param.16) | copy-start | bytes 52
  3.8 7.5 %copy-start.23 = (s32[6]{0:T(128)S(1)}, s32[6]{0:T(128)}, u32[]{:S(2)}) copy-start(s32[6]{0:T(128)} %param.19) | copy-start | bytes 76
  3.8 8.8 %copy-start.1 = (f32[1,32,64,128]{3,2,1,0:T(8,128)S(1)}, f32[1,32,64,128]{3,2,1,0:T(8,128)}, u32[]{:S(2)}) copy-start(f32[1,32,64,128]{3,2,1,0:T(8,128)} %param.12) | copy-start | bytes 3145732
  4.6 23.1 %collective-permute-start = (f32[1,16,2048]{2,1,0:T(8,128)}, f32[1,16,2048]{2,1,0:T(8,128)}, u32[]{:S(2)}, u32[]{:S(2)}) collective-permute-start(f32[1,16,2048]{2,1,0:T(8,128)} %stack.117), channel_id=1, source_target_pairs={{0,8},{2,10},{4,12},{6,14},{8,0},{10,2},{12,4},{14,6},{1,9},{3,11}... | collective-permute-start | bytes 393224 | tf_op jit(solution)/shard_map/ppermute | solution.py:112
  8.2 13.0 %collective-permute-start.1 = (f32[1,16,64]{2,1,0:T(8,128)}, f32[1,16,64]{2,1,0:T(8,128)}, u32[]{:S(2)}, u32[]{:S(2)}) collective-permute-start(f32[1,16,64]{2,1,0:T(8,128)} %bitcast.141), channel_id=1, source_target_pairs={{0,8},{2,10},{4,12},{6,14},{8,0},{10,2},{12,4},{14,6},{1,9},{3,11}... | collective-permute-start | bytes 12296 | tf_op jit(solution)/shard_map/ppermute | solution.py:112
  27.4 1.6 %collective-permute-start.3 = (f32[4,64,128]{2,1,0:T(8,128)S(1)}, f32[4,64,128]{2,1,0:T(8,128)S(1)}, u32[]{:S(2)}, u32[]{:S(2)}) collective-permute-start(f32[4,64,128]{2,1,0:T(8,128)S(1)} %constant_dynamic-slice_fusion.7), channel_id=1, source_target_pairs={{0,1},{1,0},{2,3},{3,2},{4,5},{5,4},{6,7},{7,6},{8,9},{9,8},{10,11... | collective-permute-start | bytes 393224 | tf_op jit(solution)/shard_map/ppermute | solution.py:44
  34.0 4.9 %collective-permute-start.7 = (f32[4,64,128]{2,1,0:T(8,128)S(1)}, f32[4,64,128]{2,1,0:T(8,128)S(1)}, u32[]{:S(2)}, u32[]{:S(2)}) collective-permute-start(f32[4,64,128]{2,1,0:T(8,128)S(1)} %constant_dynamic-slice_fusion.6), channel_id=1, source_target_pairs={{0,1},{1,0},{2,3},{3,2},{4,5},{5,4},{6,7},{7,6},{8,9},{9,8},{10,11... | collective-permute-start | bytes 393224 | tf_op jit(solution)/shard_map/ppermute | solution.py:44
  34.3 4.0 %collective-permute-start.5 = (f32[2,16,64]{2,1,0:T(8,128)S(1)}, f32[2,16,64]{2,1,0:T(8,128)S(1)}, u32[]{:S(2)}, u32[]{:S(2)}) collective-permute-start(f32[2,16,64]{2,1,0:T(8,128)S(1)} %maximum_select_fusion.9), channel_id=1, source_target_pairs={{0,4},{2,6},{4,0},{6,2},{8,12},{10,14},{12,8},{14,10},{1,5},{3,7},... | collective-permute-start | bytes 24584 | tf_op jit(solution)/shard_map/ppermute | solution.py:112
  36.3 13.7 %collective-permute-start.6 = (f32[4,4,64,128]{3,2,1,0:T(8,128)S(1)}, f32[4,4,64,128]{3,2,1,0:T(8,128)S(1)}, u32[]{:S(2)}, u32[]{:S(2)}) collective-permute-start(f32[4,4,64,128]{3,2,1,0:T(8,128)S(1)} %dynamic-slice_bitcast_fusion.1), channel_id=1, source_target_pairs={{0,2},{2,0},{4,6},{6,4},{8,10},{10,8},{12,14},{14,12},{1,3},{3,1},... | collective-permute-start | bytes 1572872 | tf_op jit(solution)/shard_map/ppermute | solution.py:126
  37.8 7.7 %collective-permute-start.4 = (f32[2,16,2048]{2,1,0:T(8,128)S(1)}, f32[2,16,2048]{2,1,0:T(8,128)S(1)}, u32[]{:S(2)}, u32[]{:S(2)}) collective-permute-start(f32[2,16,2048]{2,1,0:T(8,128)S(1)} %maximum_select_fusion.4), channel_id=1, source_target_pairs={{0,4},{2,6},{4,0},{6,2},{8,12},{10,14},{12,8},{14,10},{1,5},{3,7},... | collective-permute-start | bytes 786440 | tf_op jit(solution)/shard_map/ppermute | solution.py:112
  50.0 16.4 %collective-permute-start.8 = (f32[4,16,2048]{2,1,0:T(8,128)}, f32[4,16,2048]{2,1,0:T(8,128)}, u32[]{:S(2)}, u32[]{:S(2)}) collective-permute-start(f32[4,16,2048]{2,1,0:T(8,128)} %bitcast.20), channel_id=1, source_target_pairs={{0,2},{2,0},{4,6},{6,4},{8,10},{10,8},{12,14},{14,12},{1,3},{3,1},... | collective-permute-start | bytes 1572872 | tf_op jit(solution)/shard_map/ppermute | solution.py:112
  51.7 13.7 %collective-permute-start.10 = (f32[2,4,64,128]{3,2,1,0:T(8,128)S(1)}, f32[2,4,64,128]{3,2,1,0:T(8,128)}, u32[]{:S(2)}, u32[]{:S(2)}) collective-permute-start(f32[2,4,64,128]{3,2,1,0:T(8,128)S(1)} %dynamic-slice_bitcast_fusion.3), channel_id=1, source_target_pairs={{0,4},{2,6},{4,0},{6,2},{8,12},{10,14},{12,8},{14,10},{1,5},{3,7},... | collective-permute-start | bytes 786440 | tf_op jit(solution)/shard_map/ppermute | solution.py:126
  52.2 11.7 %collective-permute-start.9 = (f32[4,16,64]{2,1,0:T(8,128)}, f32[4,16,64]{2,1,0:T(8,128)}, u32[]{:S(2)}, u32[]{:S(2)}) collective-permute-start(f32[4,16,64]{2,1,0:T(8,128)} %bitcast.23), channel_id=1, source_target_pairs={{0,2},{2,0},{4,6},{6,4},{8,10},{10,8},{12,14},{14,12},{1,3},{3,1},... | collective-permute-start | bytes 49160 | tf_op jit(solution)/shard_map/ppermute | solution.py:112
  73.1 2.9 %collective-permute-start.12 = (f32[4,64,128]{2,1,0:T(8,128)S(1)}, f32[4,64,128]{2,1,0:T(8,128)S(1)}, u32[]{:S(2)}, u32[]{:S(2)}) collective-permute-start(f32[4,64,128]{2,1,0:T(8,128)S(1)} %constant_dynamic-slice_fusion.4), channel_id=1, source_target_pairs={{0,1},{1,0},{2,3},{3,2},{4,5},{5,4},{6,7},{7,6},{8,9},{9,8},{10,11... | collective-permute-start | bytes 393224 | tf_op jit(solution)/shard_map/ppermute | solution.py:44
  73.2 9.6 %collective-permute-start.11 = (f32[1,4,64,128]{3,2,1,0:T(8,128)S(1)}, f32[1,4,64,128]{3,2,1,0:T(8,128)S(1)}, u32[]{:S(2)}, u32[]{:S(2)}) collective-permute-start(f32[1,4,64,128]{3,2,1,0:T(8,128)S(1)} %constant_dynamic-slice_fusion.5), channel_id=1, source_target_pairs={{0,8},{2,10},{4,12},{6,14},{8,0},{10,2},{12,4},{14,6},{1,9},{3,11}... | collective-permute-start | bytes 393224 | tf_op jit(solution)/shard_map/ppermute | solution.py:126
  76.1 7.4 %copy-start.6 = (f32[32,64,128]{2,1,0:T(8,128)S(1)}, f32[32,64,128]{2,1,0:T(8,128)}, u32[]{:S(2)}) copy-start(f32[32,64,128]{2,1,0:T(8,128)} %get-tuple-element.66) | copy-start | bytes 3145732
  83.5 2.3 %collective-permute-start.14 = (f32[4,64,128]{2,1,0:T(8,128)S(1)}, f32[4,64,128]{2,1,0:T(8,128)S(1)}, u32[]{:S(2)}, u32[]{:S(2)}) collective-permute-start(f32[4,64,128]{2,1,0:T(8,128)S(1)} %constant_dynamic-slice_fusion.3), channel_id=1, source_target_pairs={{0,1},{1,0},{2,3},{3,2},{4,5},{5,4},{6,7},{7,6},{8,9},{9,8},{10,11... | collective-permute-start | bytes 393224 | tf_op jit(solution)/shard_map/ppermute | solution.py:44
  84.1 14.3 %collective-permute-start.13 = (f32[4,4,64,128]{3,2,1,0:T(8,128)S(1)}, f32[4,4,64,128]{3,2,1,0:T(8,128)S(1)}, u32[]{:S(2)}, u32[]{:S(2)}) collective-permute-start(f32[4,4,64,128]{3,2,1,0:T(8,128)S(1)} %dynamic-slice_bitcast_fusion), channel_id=1, source_target_pairs={{0,2},{2,0},{4,6},{6,4},{8,10},{10,8},{12,14},{14,12},{1,3},{3,1},... | collective-permute-start | bytes 1572872 | tf_op jit(solution)/shard_map/ppermute | solution.py:126
  89.1 19.0 %copy-start.11 = (f32[4,2,16,64]{3,2,1,0:T(8,128)S(1)}, f32[4,2,16,64]{3,2,1,0:T(8,128)}, u32[]{:S(2)}) copy-start(f32[4,2,16,64]{3,2,1,0:T(8,128)} %copy.36) | copy-start | bytes 98308
  98.5 16.0 %copy-start.12 = (f32[1,4,64,128]{3,2,1,0:T(8,128)S(1)}, f32[1,4,64,128]{3,2,1,0:T(8,128)}, u32[]{:S(2)}) copy-start(f32[1,4,64,128]{3,2,1,0:T(8,128)} %dynamic-slice_add_fusion.1) | copy-start | bytes 393220
  98.6 7.9 %collective-permute-start.15 = (f32[2,4,64,128]{3,2,1,0:T(8,128)S(1)}, f32[2,4,64,128]{3,2,1,0:T(8,128)S(1)}, u32[]{:S(2)}, u32[]{:S(2)}) collective-permute-start(f32[2,4,64,128]{3,2,1,0:T(8,128)S(1)} %dynamic-slice_bitcast_fusion.2), channel_id=1, source_target_pairs={{0,4},{2,6},{4,0},{6,2},{8,12},{10,14},{12,8},{14,10},{1,5},{3,7},... | collective-permute-start | bytes 786440 | tf_op jit(solution)/shard_map/ppermute | solution.py:126
  106.5 7.9 %collective-permute-start.16 = (f32[1,4,64,128]{3,2,1,0:T(8,128)S(1)}, f32[1,4,64,128]{3,2,1,0:T(8,128)S(1)}, u32[]{:S(2)}, u32[]{:S(2)}) collective-permute-start(f32[1,4,64,128]{3,2,1,0:T(8,128)S(1)} %constant_dynamic-slice_fusion.2), channel_id=1, source_target_pairs={{0,8},{2,10},{4,12},{6,14},{8,0},{10,2},{12,4},{14,6},{1,9},{3,11}... | collective-permute-start | bytes 393224 | tf_op jit(solution)/shard_map/ppermute | solution.py:126
  114.5 10.5 %copy-start.20 = (s32[1,256]{1,0:T(1,128)S(1)}, s32[1,256]{1,0:T(1,128)}, u32[]{:S(2)}) copy-start(s32[1,256]{1,0:T(1,128)} %param.18) | copy-start | bytes 3076
  116.2 8.7 %collective-permute-start.17 = (f32[1,4,64,128]{3,2,1,0:T(8,128)S(1)}, f32[1,4,64,128]{3,2,1,0:T(8,128)S(1)}, u32[]{:S(2)}, u32[]{:S(2)}) collective-permute-start(f32[1,4,64,128]{3,2,1,0:T(8,128)S(1)} %bitcast.126), channel_id=1, source_target_pairs={{0,8},{2,10},{4,12},{6,14},{8,0},{10,2},{12,4},{14,6},{1,9},{3,11}... | collective-permute-start | bytes 393224 | tf_op jit(solution)/shard_map/ppermute | solution.py:112
  124.9 8.2 %collective-permute-start.18 = (f32[2,4,64,128]{3,2,1,0:T(8,128)S(1)}, f32[2,4,64,128]{3,2,1,0:T(8,128)S(1)}, u32[]{:S(2)}, u32[]{:S(2)}) collective-permute-start(f32[2,4,64,128]{3,2,1,0:T(8,128)S(1)} %maximum_select_fusion.6), channel_id=1, source_target_pairs={{0,4},{2,6},{4,0},{6,2},{8,12},{10,14},{12,8},{14,10},{1,5},{3,7},... | collective-permute-start | bytes 786440 | tf_op jit(solution)/shard_map/ppermute | solution.py:112
  133.2 12.9 %collective-permute-start.19 = (f32[4,4,64,128]{3,2,1,0:T(8,128)S(1)}, f32[4,4,64,128]{3,2,1,0:T(8,128)S(1)}, u32[]{:S(2)}, u32[]{:S(2)}) collective-permute-start(f32[4,4,64,128]{3,2,1,0:T(8,128)S(1)} %bitcast.120), channel_id=1, source_target_pairs={{0,2},{2,0},{4,6},{6,4},{8,10},{10,8},{12,14},{14,12},{1,3},{3,1},... | collective-permute-start | bytes 1572872 | tf_op jit(solution)/shard_map/ppermute | solution.py:112
  148.3 1.6 collective-permute-start.20
  150.8 3.9 %copy-start.19 = (s32[256]{0:T(256)S(1)}, s32[256]{0:T(256)}, u32[]{:S(2)}) copy-start(s32[256]{0:T(256)} %and_select_fusion.4) | copy-start | bytes 3076
  150.8 4.0 %copy-start.22 = (pred[256]{0:T(512)(128)(4,1)S(1)}, pred[256]{0:T(512)(128)(4,1)}, u32[]{:S(2)}) copy-start(pred[256]{0:T(512)(128)(4,1)} %get-tuple-element.103) | copy-start | bytes 772
  155.0 1.9 %collective-permute-start.21 = (f32[1,2,256]{2,1,0:T(2,128)S(1)}, f32[1,2,256]{2,1,0:T(2,128)S(1)}, u32[]{:S(2)}, u32[]{:S(2)}) collective-permute-start(f32[1,2,256]{2,1,0:T(2,128)S(1)} %maximum_bitcast_fusion), channel_id=1, source_target_pairs={{0,1},{1,0},{2,3},{3,2},{4,5},{5,4},{6,7},{7,6},{8,9},{9,8},{10,11... | collective-permute-start | bytes 6152 | tf_op jit(solution)/shard_map/ppermute | solution.py:273
  (14 other events, 23.7 us)

commit v6 on v3

--- a/solution.py
+++ b/solution.py
@@ -115,15 +115,17 @@
     return pair.reshape((-1,) + held.shape[1:])
 
 
-def rs_step(held, k):
+def rs_step(held, k, left):
     n = lax.axis_size("shot")
     me = lax.axis_index("shot")
-    m = held.shape[0] // 2
-    split = held.reshape((m, 2) + held.shape[1:])
+    low = 2 ** left.index(k)
+    high = held.shape[0] // (2 * low)
+    split = held.reshape((high, 2, low) + held.shape[1:])
     mine = (me // k) % 2
     keep = lax.dynamic_index_in_dim(split, mine, axis=1, keepdims=False)
     send = lax.dynamic_index_in_dim(split, 1 - mine, axis=1, keepdims=False)
-    return keep + lax.ppermute(send, "shot", [(i, i ^ k) for i in range(n)])
+    got = lax.ppermute(send, "shot", [(i, i ^ k) for i in range(n)])
+    return (keep + got).reshape((high * low,) + held.shape[1:])
 
 
 def body(
@@ -146,19 +148,27 @@
     speed_term = coefficient(velocity_code)
     positions = start_x.astype(jnp.float32) + jnp.arange(span_x, dtype=jnp.float32)
     absorber = damping(absorb_width, positions, total_x, span_y, span_z)
-    term_flat = speed_term.reshape(-1)
     cells = span_x * span_y * span_z
     offset = start_x * span_y * span_z
     source_local = source_index - offset
     source_owned = (source_local >= 0) & (source_local < cells)
     source_safe = jnp.clip(source_local, 0, cells - 1)
-    source_gain = jnp.where(source_owned, term_flat[source_safe], 0.0)
+    plane = span_y * span_z
+    sx = source_safe[0] // plane
+    sy = (source_safe[0] // span_z) % span_y
+    sz = source_safe[0] % span_z
+    source_code = lax.dynamic_slice(velocity_code, (sx, sy, sz), (1, 1, 1)).reshape(1)
+    source_gain = jnp.where(source_owned, coefficient(source_code), 0.0)
     barrier = lax.optimization_barrier
 
+    hit = (
+        (jnp.arange(span_x)[:, None, None] == sx)
+        & (jnp.arange(span_y)[None, :, None] == sy)
+        & (jnp.arange(span_z)[None, None, :] == sz)
+    )
+
     def inject(field, moment):
-        flat = field.reshape(1, -1)
-        flat = flat.at[jnp.arange(1), source_safe].add(source_gain * wavelet[:, moment])
-        return flat.reshape(field.shape)
+        return field + jnp.where(hit, source_gain[0] * wavelet[0, moment], 0.0)
 
     def wave_step(current, prior, moment, last):
         drive = speed_term * laplace_x(with_halo(current))
@@ -203,39 +213,56 @@
         return None
 
     def light_prep():
-        task_wave(2)()
+        task_wave(1)()
         st["light"] = st["drive0"] * st["drive0"] + st["drive1"] * st["drive1"]
 
     ag_bits = list(reversed(bits))
-    tasks = [task_wave(0), task_wave(1), light_prep]
-    for i, k in enumerate(ag_bits):
+    tasks = [task_wave(0), light_prep]
+    for i, k in enumerate(ag_bits[:-1]):
         model_held, gains_held = run_group(
             [(model_held, ag_step, k), (gains_held, ag_step, k)],
             tasks[i] if i < len(tasks) else nothing,
         )
-    for i in range(len(bits), len(tasks)):
+    for i in range(len(bits) - 1, len(tasks)):
         tasks[i]()
     light_held = st["light"].reshape(n_shot, slab, span_y, span_z)
+    light_order = bits[1:] + bits[:1]
+    light_left = list(bits)
+    model_held, gains_held, light_held = run_group(
+        [
+            (model_held, ag_step, ag_bits[-1]),
+            (gains_held, ag_step, ag_bits[-1]),
+            (light_held, lambda h, k: rs_step(h, k, light_left), light_order[0]),
+        ],
+        task_wave(2),
+    )
+    light_left.remove(light_order[0])
 
     def born_pass():
         model = model_held.reshape(span_z, span_x * span_y).T.reshape(span_x, span_y, span_z)
         st["born1"] = model * st["drive0"]
         st["born2"] = born_second(st["born1"], model, st["drive1"])
 
-    (light_held,) = run_group([(light_held, rs_step, bits[0])], born_pass)
+    light_rest = light_order[1:]
+    (light_held,) = run_group([(light_held, lambda h, k: rs_step(h, k, light_left), light_rest[0])], born_pass)
+    light_left.remove(light_rest[0])
+    light_rest = light_rest[1:]
     born1, born2 = st["born1"], st["born2"]
 
     image = st["drive0"] * born1 + st["drive1"] * born2
     image_held = image.reshape(n_shot, slab, span_y, span_z)
+    image_left = list(bits)
     tasks = [task_wave(3)]
     for i, k in enumerate(bits):
-        comm = [(image_held, rs_step, k)]
-        if i + 1 < len(bits):
-            comm.append((light_held, rs_step, bits[i + 1]))
+        comm = [(image_held, lambda h, kk: rs_step(h, kk, image_left), k)]
+        if i < len(light_rest):
+            comm.append((light_held, lambda h, kk: rs_step(h, kk, light_left), light_rest[i]))
         moved = run_group(comm, tasks[i] if i < len(tasks) else nothing)
         image_held = moved[0]
-        if i + 1 < len(bits):
+        image_left.remove(k)
+        if i < len(light_rest):
             light_held = moved[1]
+            light_left.remove(light_rest[i])
     for i in range(len(bits), len(tasks)):
         tasks[i]()
 

time: 160 us -> 151 us (0.944)
  local copies, waits for them, and re-layouts: 24.1 us -> 17.8 us
  between operations: 10.2 us -> 4.63 us
  waiting for transfers between devices: 66.1 us -> 71.3 us
  other arithmetic: 40.6 us -> 36.2 us
  starting transfers between devices: 16.9 us -> 19.2 us
    sub x3 -> x0, other arithmetic: 11.9 us -> none  [wave_step(): 2.0 * current - prior + drive - absorber * (current - prior)]
    add x9 -> x4, other arithmetic: 2.05 us -> 12.5 us  [the longest x3 11.6 us: inject(): return field + jnp.where(hit, source_gain[0] * wavelet[0, moment], 0.0)]
    ppermute x9, waiting for transfers between devices: 30 us -> 37.1 us  [ag_step(): theirs = lax.ppermute(held, 'shot', [(i, i ^ k) for i in range(n)])]
    select_n x10, other arithmetic: 6.15 us -> 2.27 us  [ag_step(): jnp.where(low, jnp.stack([held, theirs], axis=1), jnp.stack([theirs, held...]
    unnamed x53 -> x41, local copies, waits for them, and re-layouts: 6.14 us -> 3.06 us
    scatter-add x3 -> x0, local copies, waits for them, and re-layouts: 2.56 us -> none  [inject(): flat.at[jnp.arange(1), source_safe].add(source_gain * wavelet[:, moment])]
    ppermute x6, waiting for transfers between devices: 35.6 us -> 33.6 us  [rs_step(): got = lax.ppermute(send, 'shot', [(i, i ^ k) for i in range(n)])]
  transfers between devices with their start and end apart: 22 -> 22, of which waited for: 13 -> 13; matrix products, arithmetic and copies ran while one was open for 27% -> 25% of each run, Pallas kernels for 0% -> 0%
where the time goes in v6:
time: 151 us
  waiting for transfers between devices  71.3 us (47%)
  other arithmetic  36.2 us (24%)
  starting transfers between devices  19.2 us (13%)
  local copies, waits for them, and re-layouts  17.8 us (12%)
  between operations  4.63 us (3%)
  matrix products  1.69 us (1%)
    ppermute x9, waiting for transfers between devices, ag_step(): theirs = lax.ppermute(held, 'shot', [(i, i ^ k) for i in range(n)])  37.1 us
    ppermute x6, waiting for transfers between devices, rs_step(): got = lax.ppermute(send, 'shot', [(i, i ^ k) for i in range(n)])  33.6 us
    add x3, other arithmetic, inject(): return field + jnp.where(hit, source_gain[0] * wavelet[0, moment], 0.0)  11.6 us
    ppermute x9, starting transfers between devices, ag_step(): theirs = lax.ppermute(held, 'shot', [(i, i ^ k) for i in range(n)])  9.19 us
    ppermute x6, starting transfers between devices, rs_step(): got = lax.ppermute(send, 'shot', [(i, i ^ k) for i in range(n)])  8.49 us
    add x2, other arithmetic, born_second(): 2.0 * born + speed_term * laplace_x(with_halo(born)) - absorber * born  5.85 us
    add x3, other arithmetic, ramp(): return low_part * low_part + high_part * high_part  4.49 us
    mul x1, other arithmetic, wave_step(): drive = speed_term * laplace_x(with_halo(current))  3.24 us
  transfers between devices with their start and end apart: 22, of which 13 were waited for; matrix products, arithmetic and copies ran while one was open for 25% of the time, Pallas kernels for 0%

profile of v6, /device:TPU:0, one launch (start us, length us, event | category | flops | bytes accessed | tf_op | source)
XLA Modules:
  0.0 150.8 jit_solution(9024712956805467214)
XLA Ops:
  0.6 1.7 %dynamic-slice_bitcast_fusion.6 = f32[4,64,128]{2,1,0:T(8,128)} fusion(f32[1,32,64,128]{3,2,1,0:T(8,128)} %param.12, s32[]{:T(128)S(6)} %select_n.334), kind=kLoop, calls=%fused_computation.342 | loop fusion | bytes 262148 | tf_op jit(solution)/shard_map/dynamic_slice | solution.py:43
  4.6 3.6 %collective-permute-start = (f32[1,16,2048]{2,1,0:T(8,128)}, f32[1,16,2048]{2,1,0:T(8,128)}, u32[]{:S(2)}, u32[]{:S(2)}) collective-permute-start(f32[1,16,2048]{2,1,0:T(8,128)} %stack.117), channel_id=1, source_target_pairs={{0,8},{2,10},{4,12},{6,14},{8,0},{10,2},{12,4},{14,6},{1,9},{3,11}... | collective-permute-start | bytes 393224 | tf_op jit(solution)/shard_map/ppermute | solution.py:112
  8.9 1.4 fusion.209
  13.1 1.4 fusion.191
  14.5 1.3 fusion.192
  15.9 1.8 %fusion.190 = f32[128]{0:T(128)} fusion(f32[]{:T(128)} %bitcast.11, f32[]{:T(128)} %bitcast.10), kind=kLoop, calls=%fused_computation.392 | loop fusion | flops 1280 | bytes 520 | tf_op jit(solution)/shard_map/add | solution.py:27
  22.6 4.5 %fusion.1 = (f32[32,64,128]{2,1,0:T(8,128)S(1)}, f32[32,64,128]{2,1,0:T(8,128)S(1)}) fusion(f32[]{:T(128)S(6)} %mul.359, f32[128]{0:T(128)} %fusion.190, f32[32,64]{1,0:T(8,128)S(1)} %broadcast_add_fusion, pred[128]{0:T(512)(128)(4,1)} %iota_compare_fusion.1, pred[32,64]{1,0:T(8,128)(4,1)} %broadcast_and_fusion, f32[1,32,64,128]{3,2,1,0:T(8,128)} %param.11, ...), kind=kLoop, calls=%fused_computation.117 | loop fusion | flops 12058624 | bytes 16009860 | tf_op jit(solution)/shard_map/add | solution.py:171
  28.6 1.7 %collective-permute-start.4 = (f32[2,16,64]{2,1,0:T(8,128)S(1)}, f32[2,16,64]{2,1,0:T(8,128)S(1)}, u32[]{:S(2)}, u32[]{:S(2)}) collective-permute-start(f32[2,16,64]{2,1,0:T(8,128)S(1)} %maximum_select_fusion.9), channel_id=1, source_target_pairs={{0,4},{2,6},{4,0},{6,2},{8,12},{10,14},{12,8},{14,10},{1,5},{3,7},... | collective-permute-start | bytes 24584 | tf_op jit(solution)/shard_map/ppermute | solution.py:112
  30.9 1.5 collective-permute-done.4
  32.4 3.2 %fusion.2 = (f32[32,64,128]{2,1,0:T(8,128)S(1)}, f32[32,64,128]{2,1,0:T(8,128)S(1)}) fusion(f32[32,64,128]{2,1,0:T(8,128)S(1)} %get-tuple-element.51, f32[32,64,128]{2,1,0:T(8,128)S(1)} %bitcast.133, f32[]{:T(128)S(6)} %mul.370, f32[128]{0:T(128)S(1)} %copy-done.12, f32[32,64]{1,0:T(8,128)S(1)} %broadcast_add_fusion, pred[128]{0:T(512)(128)(4,1)S(1)} %copy-done.15, ...), kind=kLoop, calls=%fused_computation.118 | loop fusion | flops 12058624 | bytes 16012292 | tf_op jit(solution)/shard_map/add | solution.py:171
  35.8 3.2 %collective-permute-done.3 = f32[2,16,2048]{2,1,0:T(8,128)S(1)} collective-permute-done((f32[2,16,2048]{2,1,0:T(8,128)S(1)}, f32[2,16,2048]{2,1,0:T(8,128)S(1)}, u32[]{:S(2)}, u32[]{:S(2)}) %collective-permute-start.3) | collective-permute-done | bytes 262176 | tf_op jit(solution)/shard_map/ppermute | solution.py:112
  39.3 1.6 %collective-permute-start.7 = (f32[4,16,64]{2,1,0:T(8,128)S(1)}, f32[4,16,64]{2,1,0:T(8,128)S(1)}, u32[]{:S(2)}, u32[]{:S(2)}) collective-permute-start(f32[4,16,64]{2,1,0:T(8,128)S(1)} %bitcast.163), channel_id=1, source_target_pairs={{0,2},{2,0},{4,6},{6,4},{8,10},{10,8},{12,14},{14,12},{1,3},{3,1},... | collective-permute-start | bytes 49160 | tf_op jit(solution)/shard_map/ppermute | solution.py:112
  42.0 1.3 collective-permute-done.7
  44.0 4.0 %fusion.3 = (f32[32,64,128]{2,1,0:T(8,128)}, f32[32,64,128]{2,1,0:T(8,128)}) fusion(f32[32,64,128]{2,1,0:T(8,128)S(1)} %get-tuple-element.50, f32[32,64,128]{2,1,0:T(8,128)S(1)} %get-tuple-element.51, f32[]{:T(128)S(6)} %mul.379, f32[128]{0:T(128)S(1)} %copy-done.12, f32[32,64]{1,0:T(8,128)S(1)} %broadcast_add_fusion, pred[128]{0:T(512)(128)(4,1)S(1)} %copy-done.15, ...), kind=kLoop, calls=%fused_computation.119 | loop fusion | flops 12058624 | bytes 16012292 | tf_op jit(solution)/shard_map/add | solution.py:171
  47.9 7.4 %collective-permute-done.6 = f32[4,16,2048]{2,1,0:T(8,128)S(1)} collective-permute-done((f32[4,16,2048]{2,1,0:T(8,128)S(1)}, f32[4,16,2048]{2,1,0:T(8,128)S(1)}, u32[]{:S(2)}, u32[]{:S(2)}) %collective-permute-start.6) | collective-permute-done | bytes 524320 | tf_op jit(solution)/shard_map/ppermute | solution.py:112
  57.4 2.5 %copy.35 = f32[2048,128]{1,0:T(8,128)} copy(f32[2048,128]{0,1:T(8,128)} %bitcast.143) | data formatting | bytes 2097152 | tf_op jit(solution)/shard_map/transpose | solution.py:242
  59.9 1.4 mul.380
  61.5 2.7 %collective-permute-start.10 = (f32[1,2,4,64,128]{4,3,2,1,0:T(8,128)S(1)}, f32[1,2,4,64,128]{4,3,2,1,0:T(8,128)S(1)}, u32[]{:S(2)}, u32[]{:S(2)}) collective-permute-start(f32[1,2,4,64,128]{4,3,2,1,0:T(8,128)S(1)} %dynamic-slice_bitcast_fusion.3), channel_id=1, source_target_pairs={{0,8},{2,10},{4,12},{6,14},{8,0},{10,2},{12,4},{14,6},{1,9},{3,11}... | collective-permute-start | bytes 786440 | tf_op jit(solution)/shard_map/ppermute | solution.py:127
  64.4 2.9 %fusion.91 = f32[32,64,128]{2,1,0:T(8,128)S(1)} fusion(f32[40,64,128]{2,1,0:T(8,128)S(1)} %constant_dynamic-update-slice_fusion.2, f32[32,64,128]{2,1,0:T(8,128)S(1)} %bitcast.136, f32[32,64,128]{2,1,0:T(8,128)S(1)} %get-tuple-element.60, f32[32,64,128]{2,1,0:T(8,128)S(1)} %mul.380, f32[128]{0:T(128)S(1)} %copy-done.13, f32[32,64]{1,0:T(8,128)S(1)} %broadcast_add_fusion, ...), kind=kLoop, calls=%fused_computation.207 | loop fusion | flops 11272192 | bytes 16007680 | tf_op jit(solution)/shard_map/add | solution.py:182
  67.3 9.4 %collective-permute-done.10 = f32[1,2,4,64,128]{4,3,2,1,0:T(8,128)S(1)} collective-permute-done((f32[1,2,4,64,128]{4,3,2,1,0:T(8,128)S(1)}, f32[1,2,4,64,128]{4,3,2,1,0:T(8,128)S(1)}, u32[]{:S(2)}, u32[]{:S(2)}) %collective-permute-start.10) | collective-permute-done | bytes 262176 | tf_op jit(solution)/shard_map/ppermute | solution.py:127
  78.4 1.4 collective-permute-start.12
  79.8 3.7 %collective-permute-done.13 = f32[1,1,4,64,128]{4,3,2,1,0:T(8,128)S(1)} collective-permute-done((f32[1,1,4,64,128]{4,3,2,1,0:T(8,128)S(1)}, f32[1,1,4,64,128]{4,3,2,1,0:T(8,128)S(1)}, u32[]{:S(2)}, u32[]{:S(2)}) %collective-permute-start.13) | collective-permute-done | bytes 131104 | tf_op jit(solution)/shard_map/ppermute | solution.py:127
  83.5 3.2 %fusion.116 = f32[32,64,128]{2,1,0:T(8,128)} fusion(f32[40,64,128]{2,1,0:T(8,128)S(1)} %constant_dynamic-update-slice_fusion.1, s32[32,64,128]{2,1,0:T(8,128)S(1)} %copy-done), kind=kLoop, calls=%fused_computation.232 | loop fusion | flops 9175040 | bytes 12845056 | tf_op jit(solution)/shard_map/mul | solution.py:174
  86.7 7.6 %collective-permute-done.12 = f32[4,1,4,64,128]{4,3,2,0,1:T(8,128)S(1)} collective-permute-done((f32[4,1,4,64,128]{4,3,2,0,1:T(8,128)S(1)}, f32[4,1,4,64,128]{4,3,2,0,1:T(8,128)S(1)}, u32[]{:S(2)}, u32[]{:S(2)}) %collective-permute-start.12) | collective-permute-done | bytes 524320 | tf_op jit(solution)/shard_map/ppermute | solution.py:127
  95.1 7.3 %collective-permute-done.15 = f32[2,1,4,64,128]{4,3,2,0,1:T(8,128)S(1)} collective-permute-done((f32[2,1,4,64,128]{4,3,2,0,1:T(8,128)S(1)}, f32[2,1,4,64,128]{4,3,2,0,1:T(8,128)S(1)}, u32[]{:S(2)}, u32[]{:S(2)}) %collective-permute-start.15) | collective-permute-done | bytes 262176 | tf_op jit(solution)/shard_map/ppermute | solution.py:127
  102.5 2.3 %collective-permute-start.16 = (f32[1,1,4,64,128]{4,3,2,1,0:T(8,128)S(1)}, f32[1,1,4,64,128]{4,3,2,1,0:T(8,128)S(1)}, u32[]{:S(2)}, u32[]{:S(2)}) collective-permute-start(f32[1,1,4,64,128]{4,3,2,1,0:T(8,128)S(1)} %dynamic-slice_bitcast_fusion.4), channel_id=1, source_target_pairs={{0,8},{2,10},{4,12},{6,14},{8,0},{10,2},{12,4},{14,6},{1,9},{3,11}... | collective-permute-start | bytes 393224 | tf_op jit(solution)/shard_map/ppermute | solution.py:127
  104.8 5.6 %collective-permute-done.16 = f32[1,1,4,64,128]{4,3,2,1,0:T(8,128)S(1)} collective-permute-done((f32[1,1,4,64,128]{4,3,2,1,0:T(8,128)S(1)}, f32[1,1,4,64,128]{4,3,2,1,0:T(8,128)S(1)}, u32[]{:S(2)}, u32[]{:S(2)}) %collective-permute-start.16) | collective-permute-done | bytes 131104 | tf_op jit(solution)/shard_map/ppermute | solution.py:127
  112.5 8.1 %collective-permute-done.17 = f32[1,4,64,128]{3,2,1,0:T(8,128)S(1)} collective-permute-done((f32[1,4,64,128]{3,2,1,0:T(8,128)S(1)}, f32[1,4,64,128]{3,2,1,0:T(8,128)S(1)}, u32[]{:S(2)}, u32[]{:S(2)}) %collective-permute-start.17) | collective-permute-done | bytes 131104 | tf_op jit(solution)/shard_map/ppermute | solution.py:112
  120.7 6.9 %collective-permute-done.18 = f32[2,4,64,128]{3,2,1,0:T(8,128)S(1)} collective-permute-done((f32[2,4,64,128]{3,2,1,0:T(8,128)S(1)}, f32[2,4,64,128]{3,2,1,0:T(8,128)S(1)}, u32[]{:S(2)}, u32[]{:S(2)}) %collective-permute-start.18) | collective-permute-done | bytes 262176 | tf_op jit(solution)/shard_map/ppermute | solution.py:112
  127.7 1.2 collective-permute-start.19
  130.7 8.8 %collective-permute-done.19 = f32[4,4,64,128]{3,2,1,0:T(8,128)S(1)} collective-permute-done((f32[4,4,64,128]{3,2,1,0:T(8,128)S(1)}, f32[4,4,64,128]{3,2,1,0:T(8,128)S(1)}, u32[]{:S(2)}, u32[]{:S(2)}) %collective-permute-start.19) | collective-permute-done | bytes 524320 | tf_op jit(solution)/shard_map/ppermute | solution.py:112
  144.1 2.9 %fusion.144 = f32[32,64,128]{2,1,0:T(8,128)S(1)} fusion(f32[40,64,128]{2,1,0:T(8,128)S(1)} %constant_dynamic-update-slice_fusion, f32[32,64,128]{2,1,0:T(8,128)S(1)} %copy-done.7, f32[128]{0:T(128)S(1)} %copy-done.14, f32[32,64]{1,0:T(8,128)S(1)} %broadcast_add_fusion, f32[4,2,4,64,128]{4,3,2,1,0:T(8,128)S(1)} %copy.41, f32[32,64,128]{2,1,0:T(8,128)S(1)} %copy-done.4, ...), kind=kLoop, calls=%fused_computation.260 | loop fusion | flops 11534336 | bytes 16007680 | tf_op jit(solution)/shard_map/add | solution.py:182
  (140 shorter events, 28.7 us)
Async XLA Ops:
  0.6 12.3 %copy-start.1 = (f32[1,32,64,128]{3,2,1,0:T(8,128)S(1)}, f32[1,32,64,128]{3,2,1,0:T(8,128)}, u32[]{:S(2)}) copy-start(f32[1,32,64,128]{3,2,1,0:T(8,128)} %param.12) | copy-start | bytes 3145732
  2.3 19.4 %collective-permute-start.2 = (f32[4,64,128]{2,1,0:T(8,128)}, f32[4,64,128]{2,1,0:T(8,128)}, u32[]{:S(2)}, u32[]{:S(2)}) collective-permute-start(f32[4,64,128]{2,1,0:T(8,128)} %dynamic-slice_bitcast_fusion.6), channel_id=1, source_target_pairs={{0,1},{1,0},{2,3},{3,2},{4,5},{5,4},{6,7},{7,6},{8,9},{9,8},{10,11... | collective-permute-start | bytes 393224 | tf_op jit(solution)/shard_map/ppermute | solution.py:44
  4.6 22.5 %collective-permute-start = (f32[1,16,2048]{2,1,0:T(8,128)}, f32[1,16,2048]{2,1,0:T(8,128)}, u32[]{:S(2)}, u32[]{:S(2)}) collective-permute-start(f32[1,16,2048]{2,1,0:T(8,128)} %stack.117), channel_id=1, source_target_pairs={{0,8},{2,10},{4,12},{6,14},{8,0},{10,2},{12,4},{14,6},{1,9},{3,11}... | collective-permute-start | bytes 393224 | tf_op jit(solution)/shard_map/ppermute | solution.py:112
  8.2 12.7 %collective-permute-start.1 = (f32[1,16,64]{2,1,0:T(8,128)}, f32[1,16,64]{2,1,0:T(8,128)}, u32[]{:S(2)}, u32[]{:S(2)}) collective-permute-start(f32[1,16,64]{2,1,0:T(8,128)} %bitcast.170), channel_id=1, source_target_pairs={{0,8},{2,10},{4,12},{6,14},{8,0},{10,2},{12,4},{14,6},{1,9},{3,11}... | collective-permute-start | bytes 12296 | tf_op jit(solution)/shard_map/ppermute | solution.py:112
  12.9 4.8 %copy-start = (s32[32,64,128]{2,1,0:T(8,128)S(1)}, s32[32,64,128]{2,1,0:T(8,128)}, u32[]{:S(2)}) copy-start(s32[32,64,128]{2,1,0:T(8,128)} %param.13) | copy-start | bytes 3145732
  28.3 4.1 %copy-start.2 = (f32[1,32,64,128]{3,2,1,0:T(8,128)S(1)}, f32[1,32,64,128]{3,2,1,0:T(8,128)}, u32[]{:S(2)}) copy-start(f32[1,32,64,128]{3,2,1,0:T(8,128)} %param.12) | copy-start | bytes 3145732
  28.3 4.1 %copy-start.11 = (pred[32,64]{1,0:T(8,128)(4,1)S(1)}, pred[32,64]{1,0:T(8,128)(4,1)}, u32[]{:S(2)}) copy-start(pred[32,64]{1,0:T(8,128)(4,1)} %broadcast_and_fusion) | copy-start | bytes 6148
  28.3 4.1 %copy-start.12 = (f32[128]{0:T(128)S(1)}, f32[128]{0:T(128)}, u32[]{:S(2)}) copy-start(f32[128]{0:T(128)} %fusion.190) | copy-start | bytes 1540
  28.3 4.1 %copy-start.15 = (pred[128]{0:T(512)(128)(4,1)S(1)}, pred[128]{0:T(512)(128)(4,1)}, u32[]{:S(2)}) copy-start(pred[128]{0:T(512)(128)(4,1)} %iota_compare_fusion.1) | copy-start | bytes 388
  28.3 4.0 %collective-permute-start.5 = (f32[4,64,128]{2,1,0:T(8,128)S(1)}, f32[4,64,128]{2,1,0:T(8,128)S(1)}, u32[]{:S(2)}, u32[]{:S(2)}) collective-permute-start(f32[4,64,128]{2,1,0:T(8,128)S(1)} %constant_dynamic-slice_fusion.5), channel_id=1, source_target_pairs={{0,1},{1,0},{2,3},{3,2},{4,5},{5,4},{6,7},{7,6},{8,9},{9,8},{10,11... | collective-permute-start | bytes 393224 | tf_op jit(solution)/shard_map/ppermute | solution.py:44
  28.6 3.7 %collective-permute-start.4 = (f32[2,16,64]{2,1,0:T(8,128)S(1)}, f32[2,16,64]{2,1,0:T(8,128)S(1)}, u32[]{:S(2)}, u32[]{:S(2)}) collective-permute-start(f32[2,16,64]{2,1,0:T(8,128)S(1)} %maximum_select_fusion.9), channel_id=1, source_target_pairs={{0,4},{2,6},{4,0},{6,2},{8,12},{10,14},{12,8},{14,10},{1,5},{3,7},... | collective-permute-start | bytes 24584 | tf_op jit(solution)/shard_map/ppermute | solution.py:112
  30.5 8.4 %collective-permute-start.3 = (f32[2,16,2048]{2,1,0:T(8,128)S(1)}, f32[2,16,2048]{2,1,0:T(8,128)S(1)}, u32[]{:S(2)}, u32[]{:S(2)}) collective-permute-start(f32[2,16,2048]{2,1,0:T(8,128)S(1)} %maximum_select_fusion.4), channel_id=1, source_target_pairs={{0,4},{2,6},{4,0},{6,2},{8,12},{10,14},{12,8},{14,10},{1,5},{3,7},... | collective-permute-start | bytes 786440 | tf_op jit(solution)/shard_map/ppermute | solution.py:112
  39.2 4.7 %collective-permute-start.9 = (f32[4,64,128]{2,1,0:T(8,128)S(1)}, f32[4,64,128]{2,1,0:T(8,128)S(1)}, u32[]{:S(2)}, u32[]{:S(2)}) collective-permute-start(f32[4,64,128]{2,1,0:T(8,128)S(1)} %constant_dynamic-slice_fusion.4), channel_id=1, source_target_pairs={{0,1},{1,0},{2,3},{3,2},{4,5},{5,4},{6,7},{7,6},{8,9},{9,8},{10,11... | collective-permute-start | bytes 393224 | tf_op jit(solution)/shard_map/ppermute | solution.py:44
  39.3 4.0 %collective-permute-start.7 = (f32[4,16,64]{2,1,0:T(8,128)S(1)}, f32[4,16,64]{2,1,0:T(8,128)S(1)}, u32[]{:S(2)}, u32[]{:S(2)}) collective-permute-start(f32[4,16,64]{2,1,0:T(8,128)S(1)} %bitcast.163), channel_id=1, source_target_pairs={{0,2},{2,0},{4,6},{6,4},{8,10},{10,8},{12,14},{14,12},{1,3},{3,1},... | collective-permute-start | bytes 49160 | tf_op jit(solution)/shard_map/ppermute | solution.py:112
  41.0 15.6 %collective-permute-start.8 = (f32[2,2,4,64,128]{4,3,2,1,0:T(8,128)S(1)}, f32[2,2,4,64,128]{4,3,2,1,0:T(8,128)S(1)}, u32[]{:S(2)}, u32[]{:S(2)}) collective-permute-start(f32[2,2,4,64,128]{4,3,2,1,0:T(8,128)S(1)} %dynamic-slice_bitcast_fusion.1), channel_id=1, source_target_pairs={{0,4},{2,6},{4,0},{6,2},{8,12},{10,14},{12,8},{14,10},{1,5},{3,7},... | collective-permute-start | bytes 1572872 | tf_op jit(solution)/shard_map/ppermute | solution.py:127
  41.6 13.7 %collective-permute-start.6 = (f32[4,16,2048]{2,1,0:T(8,128)S(1)}, f32[4,16,2048]{2,1,0:T(8,128)S(1)}, u32[]{:S(2)}, u32[]{:S(2)}) collective-permute-start(f32[4,16,2048]{2,1,0:T(8,128)S(1)} %bitcast.144), channel_id=1, source_target_pairs={{0,2},{2,0},{4,6},{6,4},{8,10},{10,8},{12,14},{14,12},{1,3},{3,1},... | collective-permute-start | bytes 1572872 | tf_op jit(solution)/shard_map/ppermute | solution.py:112
  61.4 3.0 %collective-permute-start.11 = (f32[4,64,128]{2,1,0:T(8,128)S(1)}, f32[4,64,128]{2,1,0:T(8,128)S(1)}, u32[]{:S(2)}, u32[]{:S(2)}) collective-permute-start(f32[4,64,128]{2,1,0:T(8,128)S(1)} %constant_dynamic-slice_fusion.3), channel_id=1, source_target_pairs={{0,1},{1,0},{2,3},{3,2},{4,5},{5,4},{6,7},{7,6},{8,9},{9,8},{10,11... | collective-permute-start | bytes 393224 | tf_op jit(solution)/shard_map/ppermute | solution.py:44
  61.5 15.3 %collective-permute-start.10 = (f32[1,2,4,64,128]{4,3,2,1,0:T(8,128)S(1)}, f32[1,2,4,64,128]{4,3,2,1,0:T(8,128)S(1)}, u32[]{:S(2)}, u32[]{:S(2)}) collective-permute-start(f32[1,2,4,64,128]{4,3,2,1,0:T(8,128)S(1)} %dynamic-slice_bitcast_fusion.3), channel_id=1, source_target_pairs={{0,8},{2,10},{4,12},{6,14},{8,0},{10,2},{12,4},{14,6},{1,9},{3,11}... | collective-permute-start | bytes 786440 | tf_op jit(solution)/shard_map/ppermute | solution.py:127
  64.4 12.4 %copy-start.6 = (f32[32,64,128]{2,1,0:T(8,128)S(1)}, f32[32,64,128]{2,1,0:T(8,128)}, u32[]{:S(2)}) copy-start(f32[32,64,128]{2,1,0:T(8,128)} %get-tuple-element.64) | copy-start | bytes 3145732
  77.0 2.7 %collective-permute-start.14 = (f32[4,64,128]{2,1,0:T(8,128)S(1)}, f32[4,64,128]{2,1,0:T(8,128)S(1)}, u32[]{:S(2)}, u32[]{:S(2)}) collective-permute-start(f32[4,64,128]{2,1,0:T(8,128)S(1)} %constant_dynamic-slice_fusion.2), channel_id=1, source_target_pairs={{0,1},{1,0},{2,3},{3,2},{4,5},{5,4},{6,7},{7,6},{8,9},{9,8},{10,11... | collective-permute-start | bytes 393224 | tf_op jit(solution)/shard_map/ppermute | solution.py:44
  77.1 6.4 %collective-permute-start.13 = (f32[1,1,4,64,128]{4,3,2,1,0:T(8,128)S(1)}, f32[1,1,4,64,128]{4,3,2,1,0:T(8,128)S(1)}, u32[]{:S(2)}, u32[]{:S(2)}) collective-permute-start(f32[1,1,4,64,128]{4,3,2,1,0:T(8,128)S(1)} %dynamic-slice_bitcast_fusion.5), channel_id=1, source_target_pairs={{0,2},{2,0},{4,6},{6,4},{8,10},{10,8},{12,14},{14,12},{1,3},{3,1},... | collective-permute-start | bytes 393224 | tf_op jit(solution)/shard_map/ppermute | solution.py:127
  78.4 15.9 %collective-permute-start.12 = (f32[4,1,4,64,128]{4,3,2,0,1:T(8,128)S(1)}, f32[4,1,4,64,128]{4,3,2,0,1:T(8,128)S(1)}, u32[]{:S(2)}, u32[]{:S(2)}) collective-permute-start(f32[4,1,4,64,128]{4,3,2,0,1:T(8,128)S(1)} %dynamic-slice_bitcast_fusion), channel_id=1, source_target_pairs={{0,2},{2,0},{4,6},{6,4},{8,10},{10,8},{12,14},{14,12},{1,3},{3,1},... | collective-permute-start | bytes 1572872 | tf_op jit(solution)/shard_map/ppermute | solution.py:127
  86.7 18.0 %copy-start.10 = (f32[4,2,16,64]{3,2,1,0:T(8,128)S(1)}, f32[4,2,16,64]{3,2,1,0:T(8,128)}, u32[]{:S(2)}) copy-start(f32[4,2,16,64]{3,2,1,0:T(8,128)} %copy.34) | copy-start | bytes 98308
  94.4 8.0 %collective-permute-start.15 = (f32[2,1,4,64,128]{4,3,2,0,1:T(8,128)S(1)}, f32[2,1,4,64,128]{4,3,2,0,1:T(8,128)S(1)}, u32[]{:S(2)}, u32[]{:S(2)}) collective-permute-start(f32[2,1,4,64,128]{4,3,2,0,1:T(8,128)S(1)} %dynamic-slice_bitcast_fusion.2), channel_id=1, source_target_pairs={{0,4},{2,6},{4,0},{6,2},{8,12},{10,14},{12,8},{14,10},{1,5},{3,7},... | collective-permute-start | bytes 786440 | tf_op jit(solution)/shard_map/ppermute | solution.py:127
  102.5 8.0 %collective-permute-start.16 = (f32[1,1,4,64,128]{4,3,2,1,0:T(8,128)S(1)}, f32[1,1,4,64,128]{4,3,2,1,0:T(8,128)S(1)}, u32[]{:S(2)}, u32[]{:S(2)}) collective-permute-start(f32[1,1,4,64,128]{4,3,2,1,0:T(8,128)S(1)} %dynamic-slice_bitcast_fusion.4), channel_id=1, source_target_pairs={{0,8},{2,10},{4,12},{6,14},{8,0},{10,2},{12,4},{14,6},{1,9},{3,11}... | collective-permute-start | bytes 393224 | tf_op jit(solution)/shard_map/ppermute | solution.py:127
  110.5 10.2 %copy-start.17 = (s32[1,256]{1,0:T(1,128)S(1)}, s32[1,256]{1,0:T(1,128)}, u32[]{:S(2)}) copy-start(s32[1,256]{1,0:T(1,128)} %param.18) | copy-start | bytes 3076
  112.2 8.3 %collective-permute-start.17 = (f32[1,4,64,128]{3,2,1,0:T(8,128)S(1)}, f32[1,4,64,128]{3,2,1,0:T(8,128)S(1)}, u32[]{:S(2)}, u32[]{:S(2)}) collective-permute-start(f32[1,4,64,128]{3,2,1,0:T(8,128)S(1)} %bitcast.152), channel_id=1, source_target_pairs={{0,8},{2,10},{4,12},{6,14},{8,0},{10,2},{12,4},{14,6},{1,9},{3,11}... | collective-permute-start | bytes 393224 | tf_op jit(solution)/shard_map/ppermute | solution.py:112
  120.6 7.0 %collective-permute-start.18 = (f32[2,4,64,128]{3,2,1,0:T(8,128)S(1)}, f32[2,4,64,128]{3,2,1,0:T(8,128)S(1)}, u32[]{:S(2)}, u32[]{:S(2)}) collective-permute-start(f32[2,4,64,128]{3,2,1,0:T(8,128)S(1)} %maximum_select_fusion.6), channel_id=1, source_target_pairs={{0,4},{2,6},{4,0},{6,2},{8,12},{10,14},{12,8},{14,10},{1,5},{3,7},... | collective-permute-start | bytes 786440 | tf_op jit(solution)/shard_map/ppermute | solution.py:112
  127.7 11.7 %collective-permute-start.19 = (f32[4,4,64,128]{3,2,1,0:T(8,128)S(1)}, f32[4,4,64,128]{3,2,1,0:T(8,128)S(1)}, u32[]{:S(2)}, u32[]{:S(2)}) collective-permute-start(f32[4,4,64,128]{3,2,1,0:T(8,128)S(1)} %bitcast.146), channel_id=1, source_target_pairs={{0,2},{2,0},{4,6},{6,4},{8,10},{10,8},{12,14},{14,12},{1,3},{3,1},... | collective-permute-start | bytes 1572872 | tf_op jit(solution)/shard_map/ppermute | solution.py:112
  141.6 1.6 %collective-permute-start.20 = (f32[4,64,128]{2,1,0:T(8,128)}, f32[4,64,128]{2,1,0:T(8,128)S(1)}, u32[]{:S(2)}, u32[]{:S(2)}) collective-permute-start(f32[4,64,128]{2,1,0:T(8,128)} %constant_dynamic-slice_fusion), channel_id=1, source_target_pairs={{0,1},{1,0},{2,3},{3,2},{4,5},{5,4},{6,7},{7,6},{8,9},{9,8},{10,11... | collective-permute-start | bytes 393224 | tf_op jit(solution)/shard_map/ppermute | solution.py:44
  144.1 4.0 %copy-start.19 = (pred[256]{0:T(512)(128)(4,1)S(1)}, pred[256]{0:T(512)(128)(4,1)}, u32[]{:S(2)}) copy-start(pred[256]{0:T(512)(128)(4,1)} %get-tuple-element.90) | copy-start | bytes 772
  148.3 1.9 %collective-permute-start.21 = (f32[1,2,256]{2,1,0:T(2,128)S(1)}, f32[1,2,256]{2,1,0:T(2,128)S(1)}, u32[]{:S(2)}, u32[]{:S(2)}) collective-permute-start(f32[1,2,256]{2,1,0:T(2,128)S(1)} %maximum_bitcast_fusion), channel_id=1, source_target_pairs={{0,1},{1,0},{2,3},{3,2},{4,5},{5,4},{6,7},{7,6},{8,9},{9,8},{10,11... | collective-permute-start | bytes 6152 | tf_op jit(solution)/shard_map/ppermute | solution.py:293
  (10 other events, 20.3 us)

commit v7 on v6

--- a/solution.py
+++ b/solution.py
@@ -106,13 +106,45 @@
     return bits
 
 
-def ag_step(held, k):
+def ag_step(held, k, done):
     n = lax.axis_size("shot")
     me = lax.axis_index("shot")
     theirs = lax.ppermute(held, "shot", [(i, i ^ k) for i in range(n)])
-    low = (me // k) % 2 == 0
-    pair = jnp.where(low, jnp.stack([held, theirs], axis=1), jnp.stack([theirs, held], axis=1))
-    return pair.reshape((-1,) + held.shape[1:])
+    low = 2 ** sum(1 for b in done if b < k)
+    shape = (held.shape[0] // low, 1, low) + held.shape[1:]
+    mine, other = held.reshape(shape), theirs.reshape(shape)
+    first = (me // k) % 2 == 0
+    pair = jnp.where(first, jnp.concatenate([mine, other], axis=1), jnp.concatenate([other, mine], axis=1))
+    return pair.reshape((2 * held.shape[0],) + held.shape[1:])
+
+
+def swap_first(order):
+    return order[1:2] + order[:1] + order[2:]
+
+
+def swap_last(order):
+    return order[:-2] + order[-1:] + order[-2:-1] if len(order) > 1 else order
+
+
+def chain(held, kind, order):
+    return {"held": held, "kind": kind, "order": list(order), "i": 0, "bits": [] if kind == "ag" else sorted(order)}
+
+
+def chain_step(c):
+    k = c["order"][c["i"]]
+    if c["kind"] == "ag":
+        return ag_step(c["held"], k, c["bits"])
+    return rs_step(c["held"], k, c["bits"])
+
+
+def chain_commit(c, held):
+    k = c["order"][c["i"]]
+    c["held"] = held
+    c["i"] += 1
+    if c["kind"] == "ag":
+        c["bits"].append(k)
+    else:
+        c["bits"].remove(k)
 
 
 def rs_step(held, k, left):
@@ -201,13 +233,15 @@
                 st["w%d" % (i + 1)] = later
         return run
 
-    def run_group(comm, compute):
-        moved = [step(held, k) for held, step, k in comm]
+    def run_group(chains, compute):
+        chains = [c for c in chains if c["i"] < len(c["order"])]
+        moved = [chain_step(c) for c in chains]
         compute()
         keys = sorted(st.keys())
         out = barrier((moved, [st[n] for n in keys]))
         st.update(zip(keys, out[1]))
-        return out[0]
+        for c, held in zip(chains, out[0]):
+            chain_commit(c, held)
 
     def nothing():
         return None
@@ -216,62 +250,56 @@
         task_wave(1)()
         st["light"] = st["drive0"] * st["drive0"] + st["drive1"] * st["drive1"]
 
-    ag_bits = list(reversed(bits))
-    tasks = [task_wave(0), light_prep]
-    for i, k in enumerate(ag_bits[:-1]):
-        model_held, gains_held = run_group(
-            [(model_held, ag_step, k), (gains_held, ag_step, k)],
-            tasks[i] if i < len(tasks) else nothing,
-        )
-    for i in range(len(bits) - 1, len(tasks)):
+    def halves(x, axis):
+        h = x.shape[axis] // 2
+        return lax.slice_in_dim(x, 0, h, axis=axis), lax.slice_in_dim(x, h, x.shape[axis], axis=axis)
+
+    far_first = list(reversed(bits))
+    near_first = list(bits)
+
+    half_a, half_b = halves(model_held, 1)
+    model_a = chain(half_a, "ag", far_first)
+    model_b = chain(half_b, "ag", swap_last(far_first))
+    gains_c = chain(gains_held, "ag", far_first)
+    tasks = [task_wave(0), light_prep, task_wave(2)]
+    for i in range(len(bits)):
+        run_group([model_a, model_b, gains_c], tasks[i] if i < len(tasks) else nothing)
+    for i in range(len(bits), len(tasks)):
         tasks[i]()
-    light_held = st["light"].reshape(n_shot, slab, span_y, span_z)
-    light_order = bits[1:] + bits[:1]
-    light_left = list(bits)
-    model_held, gains_held, light_held = run_group(
-        [
-            (model_held, ag_step, ag_bits[-1]),
-            (gains_held, ag_step, ag_bits[-1]),
-            (light_held, lambda h, k: rs_step(h, k, light_left), light_order[0]),
-        ],
-        task_wave(2),
-    )
-    light_left.remove(light_order[0])
+    model_held = jnp.concatenate([model_a["held"], model_b["held"]], axis=1)
+    gains_held = gains_c["held"]
+    light_a, light_b = halves(st["light"].reshape(n_shot, slab, span_y, span_z), 2)
+    light_a = chain(light_a, "rs", near_first)
+    light_b = chain(light_b, "rs", swap_first(near_first))
 
     def born_pass():
         model = model_held.reshape(span_z, span_x * span_y).T.reshape(span_x, span_y, span_z)
         st["born1"] = model * st["drive0"]
         st["born2"] = born_second(st["born1"], model, st["drive1"])
 
-    light_rest = light_order[1:]
-    (light_held,) = run_group([(light_held, lambda h, k: rs_step(h, k, light_left), light_rest[0])], born_pass)
-    light_left.remove(light_rest[0])
-    light_rest = light_rest[1:]
+    run_group([light_a, light_b], born_pass)
     born1, born2 = st["born1"], st["born2"]
 
     image = st["drive0"] * born1 + st["drive1"] * born2
-    image_held = image.reshape(n_shot, slab, span_y, span_z)
-    image_left = list(bits)
+    image_a, image_b = halves(image.reshape(n_shot, slab, span_y, span_z), 2)
+    image_a = chain(image_a, "rs", near_first)
+    image_b = chain(image_b, "rs", swap_first(near_first))
     tasks = [task_wave(3)]
-    for i, k in enumerate(bits):
-        comm = [(image_held, lambda h, kk: rs_step(h, kk, image_left), k)]
-        if i < len(light_rest):
-            comm.append((light_held, lambda h, kk: rs_step(h, kk, light_left), light_rest[i]))
-        moved = run_group(comm, tasks[i] if i < len(tasks) else nothing)
-        image_held = moved[0]
-        image_left.remove(k)
-        if i < len(light_rest):
-            light_held = moved[1]
-            light_left.remove(light_rest[i])
+    for i in range(len(bits)):
+        run_group([image_a, image_b, light_a, light_b], tasks[i] if i < len(tasks) else nothing)
     for i in range(len(bits), len(tasks)):
         tasks[i]()
+    image_part = jnp.concatenate([image_a["held"][0], image_b["held"][0]], axis=1)
+    light_part = jnp.concatenate([light_a["held"][0], light_b["held"][0]], axis=1)
 
     table_all = gains_held.reshape(n_shot * gains.shape[0], gains.shape[1])
-    filt_part = lateral_filter(image_held[0] / (light_held[0] + eps), table_all)
-    filt_held = filt_part[None]
-    for k in reversed(bits):
-        filt_held = ag_step(filt_held, k)
-    new_model = filt_held.reshape(span_x, span_y, span_z)
+    filt_part = lateral_filter(image_part / (light_part + eps), table_all)
+    part_a, part_b = halves(filt_part[None], 2)
+    filt_a = chain(part_a, "ag", far_first)
+    filt_b = chain(part_b, "ag", swap_last(far_first))
+    for i in range(len(bits)):
+        run_group([filt_a, filt_b], nothing)
+    new_model = jnp.concatenate([filt_a["held"], filt_b["held"]], axis=2).reshape(span_x, span_y, span_z)
     filtered = lax.dynamic_slice_in_dim(new_model, me_shot * depth, depth, 2)
 
     b1 = new_model * st["drive2"]

time: 151 us -> 136 us (0.901)
  waiting for transfers between devices: 71.3 us -> 34.1 us
  starting transfers between devices: 19.2 us -> 36.7 us
  other arithmetic: 36.2 us -> 38.7 us
    ppermute x6 -> x12, waiting for transfers between devices: 33.6 us -> 13.1 us  [rs_step(): got = lax.ppermute(send, 'shot', [(i, i ^ k) for i in range(n)])]
    ppermute x9 -> x15, waiting for transfers between devices: 37.1 us -> 20.4 us  [ag_step(): theirs = lax.ppermute(held, 'shot', [(i, i ^ k) for i in range(n)])]
    ppermute x9 -> x15, starting transfers between devices: 9.19 us -> 20.2 us  [ag_step(): theirs = lax.ppermute(held, 'shot', [(i, i ^ k) for i in range(n)])]
    ppermute x6 -> x12, starting transfers between devices: 8.49 us -> 15.3 us  [rs_step(): got = lax.ppermute(send, 'shot', [(i, i ^ k) for i in range(n)])]
    unnamed x41 -> x57, local copies, waits for them, and re-layouts: 3.06 us -> 3.52 us
  transfers between devices with their start and end apart: 22 -> 34, of which waited for: 13 -> 17; matrix products, arithmetic and copies ran while one was open for 25% -> 25% of each run, Pallas kernels for 0% -> 0%
where the time goes in v7:
time: 136 us; the launch traced here: 135 us
  other arithmetic  38.7 us (28%)
  starting transfers between devices  36.7 us (27%)
  waiting for transfers between devices  34.1 us (25%)
  local copies, waits for them, and re-layouts  19.3 us (14%)
  between operations  4.77 us (4%)
  matrix products  1.7 us (1%)
    ppermute x15, waiting for transfers between devices, ag_step(): theirs = lax.ppermute(held, 'shot', [(i, i ^ k) for i in range(n)])  20.4 us
    ppermute x15, starting transfers between devices, ag_step(): theirs = lax.ppermute(held, 'shot', [(i, i ^ k) for i in range(n)])  20.2 us
    ppermute x12, starting transfers between devices, rs_step(): got = lax.ppermute(send, 'shot', [(i, i ^ k) for i in range(n)])  15.3 us
    ppermute x12, waiting for transfers between devices, rs_step(): got = lax.ppermute(send, 'shot', [(i, i ^ k) for i in range(n)])  13.1 us
    add x3, other arithmetic, inject(): return field + jnp.where(hit, source_gain[0] * wavelet[0, moment], 0.0)  11.7 us
    add x2, other arithmetic, born_second(): 2.0 * born + speed_term * laplace_x(with_halo(born)) - absorber * born  5.83 us
    add x3, other arithmetic, ramp(): return low_part * low_part + high_part * high_part  4.38 us
    unnamed x57, local copies, waits for them, and re-layouts  3.52 us
  transfers between devices with their start and end apart: 34, of which 17 were waited for; matrix products, arithmetic and copies ran while one was open for 25% of the time, Pallas kernels for 0%

profile of v7, /device:TPU:0, one launch (start us, length us, event | category | flops | bytes accessed | tf_op | source)
XLA Modules:
  0.0 135.2 jit_solution(16391190289192984448)
XLA Ops:
  0.7 1.7 %dynamic-slice_bitcast_fusion.8 = f32[4,64,128]{2,1,0:T(8,128)} fusion(f32[1,32,64,128]{3,2,1,0:T(8,128)} %param.12, s32[]{:T(128)S(6)} %select_n.435), kind=kLoop, calls=%fused_computation.354 | loop fusion | bytes 262148 | tf_op jit(solution)/shard_map/dynamic_slice | solution.py:43
  4.6 3.6 %collective-permute-start.1 = (f32[1,8,2048]{2,1,0:T(8,128)}, f32[1,8,2048]{2,1,0:T(8,128)}, u32[]{:S(2)}, u32[]{:S(2)}) collective-permute-start(f32[1,8,2048]{2,1,0:T(8,128)} %get-tuple-element.148), channel_id=1, source_target_pairs={{0,8},{2,10},{4,12},{6,14},{8,0},{10,2},{12,4},{14,6},{1,9},{3,11}... | collective-permute-start | bytes 196616 | tf_op jit(solution)/shard_map/ppermute | solution.py:112
  8.2 2.9 %collective-permute-start.2 = (f32[1,16,64]{2,1,0:T(8,128)}, f32[1,16,64]{2,1,0:T(8,128)}, u32[]{:S(2)}, u32[]{:S(2)}) collective-permute-start(f32[1,16,64]{2,1,0:T(8,128)} %bitcast.2), channel_id=1, source_target_pairs={{0,8},{2,10},{4,12},{6,14},{8,0},{10,2},{12,4},{14,6},{1,9},{3,11}... | collective-permute-start | bytes 12296 | tf_op jit(solution)/shard_map/ppermute | solution.py:112
  17.4 1.7 %fusion.194 = f32[128]{0:T(128)} fusion(f32[]{:T(128)} %bitcast.11, f32[]{:T(128)} %bitcast.10), kind=kLoop, calls=%fused_computation.416 | loop fusion | flops 1280 | bytes 520 | tf_op jit(solution)/shard_map/add | solution.py:27
  25.9 4.5 %fusion.2 = (f32[32,64,128]{2,1,0:T(8,128)S(1)}, f32[32,64,128]{2,1,0:T(8,128)S(1)}) fusion(f32[]{:T(128)S(6)} %mul.359, f32[128]{0:T(128)} %fusion.194, f32[32,64]{1,0:T(8,128)S(1)} %broadcast_add_fusion, pred[128]{0:T(512)(128)(4,1)} %iota_compare_fusion.1, pred[32,64]{1,0:T(8,128)(4,1)} %broadcast_and_fusion, f32[1,32,64,128]{3,2,1,0:T(8,128)} %param.11, ...), kind=kLoop, calls=%fused_computation.118 | loop fusion | flops 12058624 | bytes 16009860 | tf_op jit(solution)/shard_map/add | solution.py:203
  30.6 1.6 %collective-permute-start.6 = (f32[2,16,64]{2,1,0:T(8,128)S(1)}, f32[2,16,64]{2,1,0:T(8,128)S(1)}, u32[]{:S(2)}, u32[]{:S(2)}) collective-permute-start(f32[2,16,64]{2,1,0:T(8,128)S(1)} %maximum_select_fusion.14), channel_id=1, source_target_pairs={{0,4},{2,6},{4,0},{6,2},{8,12},{10,14},{12,8},{14,10},{1,5},{3,7},... | collective-permute-start | bytes 24584 | tf_op jit(solution)/shard_map/ppermute | solution.py:112
  32.2 1.5 %collective-permute-start.5 = (f32[2,8,2048]{2,1,0:T(8,128)S(1)}, f32[2,8,2048]{2,1,0:T(8,128)S(1)}, u32[]{:S(2)}, u32[]{:S(2)}) collective-permute-start(f32[2,8,2048]{2,1,0:T(8,128)S(1)} %maximum_select_fusion.9), channel_id=1, source_target_pairs={{0,2},{2,0},{4,6},{6,4},{8,10},{10,8},{12,14},{14,12},{1,3},{3,1},... | collective-permute-start | bytes 393224 | tf_op jit(solution)/shard_map/ppermute | solution.py:112
  34.4 2.8 %collective-permute-done.5 = f32[2,8,2048]{2,1,0:T(8,128)S(1)} collective-permute-done((f32[2,8,2048]{2,1,0:T(8,128)S(1)}, f32[2,8,2048]{2,1,0:T(8,128)S(1)}, u32[]{:S(2)}, u32[]{:S(2)}) %collective-permute-start.5) | collective-permute-done | bytes 131104 | tf_op jit(solution)/shard_map/ppermute | solution.py:112
  37.2 2.5 %collective-permute-done.4 = f32[2,8,2048]{2,1,0:T(8,128)S(1)} collective-permute-done((f32[2,8,2048]{2,1,0:T(8,128)S(1)}, f32[2,8,2048]{2,1,0:T(8,128)S(1)}, u32[]{:S(2)}, u32[]{:S(2)}) %collective-permute-start.4) | collective-permute-done | bytes 131104 | tf_op jit(solution)/shard_map/ppermute | solution.py:112
  39.9 3.2 %fusion.3 = (f32[32,64,128]{2,1,0:T(8,128)S(1)}, f32[32,64,128]{2,1,0:T(8,128)S(1)}) fusion(f32[32,64,128]{2,1,0:T(8,128)S(1)} %get-tuple-element.75, f32[32,64,128]{2,1,0:T(8,128)S(1)} %bitcast.209, f32[]{:T(128)S(6)} %mul.370, f32[128]{0:T(128)S(1)} %copy-done.18, f32[32,64]{1,0:T(8,128)S(1)} %broadcast_add_fusion, pred[128]{0:T(512)(128)(4,1)S(1)} %copy-done.21, ...), kind=kLoop, calls=%fused_computation.119 | loop fusion | flops 12058624 | bytes 16012292 | tf_op jit(solution)/shard_map/add | solution.py:203
  45.7 1.5 %collective-permute-start.8 = (f32[4,8,2048]{2,1,0:T(8,128)S(1)}, f32[4,8,2048]{2,1,0:T(8,128)S(1)}, u32[]{:S(2)}, u32[]{:S(2)}) collective-permute-start(f32[4,8,2048]{2,1,0:T(8,128)S(1)} %bitcast.232), channel_id=1, source_target_pairs={{0,2},{2,0},{4,6},{6,4},{8,10},{10,8},{12,14},{14,12},{1,3},{3,1},... | collective-permute-start | bytes 786440 | tf_op jit(solution)/shard_map/ppermute | solution.py:112
  47.2 1.5 %collective-permute-done.10 = f32[4,16,64]{2,1,0:T(8,128)S(1)} collective-permute-done((f32[4,16,64]{2,1,0:T(8,128)S(1)}, f32[4,16,64]{2,1,0:T(8,128)S(1)}, u32[]{:S(2)}, u32[]{:S(2)}) %collective-permute-start.10) | collective-permute-done | bytes 16416 | tf_op jit(solution)/shard_map/ppermute | solution.py:112
  49.4 4.0 %fusion.4 = (f32[32,64,128]{2,1,0:T(8,128)}, f32[32,64,128]{2,1,0:T(8,128)}) fusion(f32[32,64,128]{2,1,0:T(8,128)S(1)} %get-tuple-element.73, f32[32,64,128]{2,1,0:T(8,128)S(1)} %get-tuple-element.75, f32[]{:T(128)S(6)} %mul.379, f32[128]{0:T(128)S(1)} %copy-done.18, f32[32,64]{1,0:T(8,128)S(1)} %broadcast_add_fusion, pred[128]{0:T(512)(128)(4,1)S(1)} %copy-done.21, ...), kind=kLoop, calls=%fused_computation.120 | loop fusion | flops 12058624 | bytes 16012292 | tf_op jit(solution)/shard_map/add | solution.py:203
  60.0 1.6 %collective-permute-start.12 = (f32[4,1,4,32,128]{4,3,2,0,1:T(8,128)S(1)}, f32[4,1,4,32,128]{4,3,2,0,1:T(8,128)}, u32[]{:S(2)}, u32[]{:S(2)}) collective-permute-start(f32[4,1,4,32,128]{4,3,2,0,1:T(8,128)S(1)} %dynamic-slice_bitcast_fusion.3), channel_id=1, source_target_pairs={{0,2},{2,0},{4,6},{6,4},{8,10},{10,8},{12,14},{14,12},{1,3},{3,1},... | collective-permute-start | bytes 786440 | tf_op jit(solution)/shard_map/ppermute | solution.py:159
  61.5 1.5 %copy.50 = f32[128,64]{0,1:T(8,128)} copy(f32[128,64]{1,0:T(8,128)} %bitcast.251) | data formatting | bytes 65536 | tf_op jit(solution)/shard_map/mul | solution.py:92
  64.7 2.9 %fusion.92 = f32[32,64,128]{2,1,0:T(8,128)S(1)} fusion(f32[40,64,128]{2,1,0:T(8,128)S(1)} %constant_dynamic-update-slice_fusion.2, f32[32,64,128]{2,1,0:T(8,128)S(1)} %bitcast.212, f32[32,64,128]{2,1,0:T(8,128)S(1)} %copy-done.2, f32[32,64,128]{2,1,0:T(8,128)S(1)} %mul.380, f32[128]{0:T(128)S(1)} %copy-done.19, f32[32,64]{1,0:T(8,128)S(1)} %broadcast_add_fusion, ...), kind=kLoop, calls=%fused_computation.208 | loop fusion | flops 11272192 | bytes 16007680 | tf_op jit(solution)/shard_map/add | solution.py:214
  71.3 1.5 %collective-permute-start.17 = (f32[2,1,4,32,128]{4,3,2,0,1:T(8,128)S(1)}, f32[2,1,4,32,128]{4,3,2,0,1:T(8,128)S(1)}, u32[]{:S(2)}, u32[]{:S(2)}) collective-permute-start(f32[2,1,4,32,128]{4,3,2,0,1:T(8,128)S(1)} %dynamic-slice_bitcast_fusion.7), channel_id=1, source_target_pairs={{0,4},{2,6},{4,0},{6,2},{8,12},{10,14},{12,8},{14,10},{1,5},{3,7},... | collective-permute-start | bytes 393224 | tf_op jit(solution)/shard_map/ppermute | solution.py:159
  75.0 3.2 %fusion.117 = f32[32,64,128]{2,1,0:T(8,128)} fusion(f32[40,64,128]{2,1,0:T(8,128)S(1)} %constant_dynamic-update-slice_fusion.1, s32[32,64,128]{2,1,0:T(8,128)S(1)} %copy-done), kind=kLoop, calls=%fused_computation.233 | loop fusion | flops 9175040 | bytes 12845056 | tf_op jit(solution)/shard_map/mul | solution.py:206
  78.3 4.3 %collective-permute-done.16 = f32[2,2,4,32,128]{4,3,2,1,0:T(8,128)S(1)} collective-permute-done((f32[2,2,4,32,128]{4,3,2,1,0:T(8,128)S(1)}, f32[2,2,4,32,128]{4,3,2,1,0:T(8,128)S(1)}, u32[]{:S(2)}, u32[]{:S(2)}) %collective-permute-start.16) | collective-permute-done | bytes 262176 | tf_op jit(solution)/shard_map/ppermute | solution.py:159
  83.1 2.6 %collective-permute-start.22 = (f32[1,1,4,32,128]{4,3,2,1,0:T(8,128)S(1)}, f32[1,1,4,32,128]{4,3,2,1,0:T(8,128)S(1)}, u32[]{:S(2)}, u32[]{:S(2)}) collective-permute-start(f32[1,1,4,32,128]{4,3,2,1,0:T(8,128)S(1)} %dynamic-slice_bitcast_fusion.12), channel_id=1, source_target_pairs={{0,8},{2,10},{4,12},{6,14},{8,0},{10,2},{12,4},{14,6},{1,9},{3,11}... | collective-permute-start | bytes 196616 | tf_op jit(solution)/shard_map/ppermute | solution.py:159
  87.8 2.4 %collective-permute-done.23 = f32[1,1,4,32,128]{4,3,2,1,0:T(8,128)S(1)} collective-permute-done((f32[1,1,4,32,128]{4,3,2,1,0:T(8,128)S(1)}, f32[1,1,4,32,128]{4,3,2,1,0:T(8,128)S(1)}, u32[]{:S(2)}, u32[]{:S(2)}) %collective-permute-start.23) | collective-permute-done | bytes 65568 | tf_op jit(solution)/shard_map/ppermute | solution.py:159
  92.8 2.6 %collective-permute-start.24 = (f32[1,1,4,32,128]{4,3,2,1,0:T(8,128)S(1)}, f32[1,1,4,32,128]{4,3,2,1,0:T(8,128)S(1)}, u32[]{:S(2)}, u32[]{:S(2)}) collective-permute-start(f32[1,1,4,32,128]{4,3,2,1,0:T(8,128)S(1)} %dynamic-slice_bitcast_fusion.10), channel_id=1, source_target_pairs={{0,8},{2,10},{4,12},{6,14},{8,0},{10,2},{12,4},{14,6},{1,9},{3,11}... | collective-permute-start | bytes 196616 | tf_op jit(solution)/shard_map/ppermute | solution.py:159
  95.4 3.6 %collective-permute-done.25 = f32[1,1,4,32,128]{4,3,2,1,0:T(8,128)S(1)} collective-permute-done((f32[1,1,4,32,128]{4,3,2,1,0:T(8,128)S(1)}, f32[1,1,4,32,128]{4,3,2,1,0:T(8,128)S(1)}, u32[]{:S(2)}, u32[]{:S(2)}) %collective-permute-start.25) | collective-permute-done | bytes 65568 | tf_op jit(solution)/shard_map/ppermute | solution.py:159
  102.4 2.1 %collective-permute-start.26 = (f32[1,4,32,128]{3,2,1,0:T(8,128)S(1)}, f32[1,4,32,128]{3,2,1,0:T(8,128)S(1)}, u32[]{:S(2)}, u32[]{:S(2)}) collective-permute-start(f32[1,4,32,128]{3,2,1,0:T(8,128)S(1)} %get-tuple-element.147), channel_id=1, source_target_pairs={{0,8},{2,10},{4,12},{6,14},{8,0},{10,2},{12,4},{14,6},{1,9},{3,11}... | collective-permute-start | bytes 196616 | tf_op jit(solution)/shard_map/ppermute | solution.py:112
  104.5 2.2 %collective-permute-done.27 = f32[1,4,32,128]{3,2,1,0:T(8,128)S(1)} collective-permute-done((f32[1,4,32,128]{3,2,1,0:T(8,128)S(1)}, f32[1,4,32,128]{3,2,1,0:T(8,128)S(1)}, u32[]{:S(2)}, u32[]{:S(2)}) %collective-permute-start.27) | collective-permute-done | bytes 65568 | tf_op jit(solution)/shard_map/ppermute | solution.py:112
  106.8 1.5 %collective-permute-done.26 = f32[1,4,32,128]{3,2,1,0:T(8,128)S(1)} collective-permute-done((f32[1,4,32,128]{3,2,1,0:T(8,128)S(1)}, f32[1,4,32,128]{3,2,1,0:T(8,128)S(1)}, u32[]{:S(2)}, u32[]{:S(2)}) %collective-permute-start.26) | collective-permute-done | bytes 65568 | tf_op jit(solution)/shard_map/ppermute | solution.py:112
  109.1 1.8 %collective-permute-start.28 = (f32[2,4,32,128]{3,2,1,0:T(8,128)S(1)}, f32[2,4,32,128]{3,2,1,0:T(8,128)S(1)}, u32[]{:S(2)}, u32[]{:S(2)}) collective-permute-start(f32[2,4,32,128]{3,2,1,0:T(8,128)S(1)} %maximum_select_fusion.10), channel_id=1, source_target_pairs={{0,4},{2,6},{4,0},{6,2},{8,12},{10,14},{12,8},{14,10},{1,5},{3,7},... | collective-permute-start | bytes 393224 | tf_op jit(solution)/shard_map/ppermute | solution.py:112
  111.4 1.9 %collective-permute-done.29 = f32[2,4,32,128]{3,2,1,0:T(8,128)S(1)} collective-permute-done((f32[2,4,32,128]{3,2,1,0:T(8,128)S(1)}, f32[2,4,32,128]{3,2,1,0:T(8,128)S(1)}, u32[]{:S(2)}, u32[]{:S(2)}) %collective-permute-start.29) | collective-permute-done | bytes 131104 | tf_op jit(solution)/shard_map/ppermute | solution.py:112
  113.4 2.1 %collective-permute-done.28 = f32[2,4,32,128]{3,2,1,0:T(8,128)S(1)} collective-permute-done((f32[2,4,32,128]{3,2,1,0:T(8,128)S(1)}, f32[2,4,32,128]{3,2,1,0:T(8,128)S(1)}, u32[]{:S(2)}, u32[]{:S(2)}) %collective-permute-start.28) | collective-permute-done | bytes 131104 | tf_op jit(solution)/shard_map/ppermute | solution.py:112
  115.5 1.8 %collective-permute-start.31 = (f32[4,4,32,128]{3,2,1,0:T(8,128)S(1)}, f32[4,4,32,128]{3,2,1,0:T(8,128)S(1)}, u32[]{:S(2)}, u32[]{:S(2)}) collective-permute-start(f32[4,4,32,128]{3,2,1,0:T(8,128)S(1)} %bitcast.242), channel_id=1, source_target_pairs={{0,4},{2,6},{4,0},{6,2},{8,12},{10,14},{12,8},{14,10},{1,5},{3,7},... | collective-permute-start | bytes 786440 | tf_op jit(solution)/shard_map/ppermute | solution.py:112
  118.5 5.2 %collective-permute-done.30 = f32[4,4,32,128]{3,2,1,0:T(8,128)S(1)} collective-permute-done((f32[4,4,32,128]{3,2,1,0:T(8,128)S(1)}, f32[4,4,32,128]{3,2,1,0:T(8,128)S(1)}, u32[]{:S(2)}, u32[]{:S(2)}) %collective-permute-start.30) | collective-permute-done | bytes 262176 | tf_op jit(solution)/shard_map/ppermute | solution.py:112
  128.4 2.9 %fusion.145 = f32[32,64,128]{2,1,0:T(8,128)S(1)} fusion(f32[40,64,128]{2,1,0:T(8,128)S(1)} %constant_dynamic-update-slice_fusion, f32[32,64,128]{2,1,0:T(8,128)S(1)} %copy-done.9, f32[128]{0:T(128)S(1)} %copy-done.20, f32[32,64]{1,0:T(8,128)S(1)} %broadcast_add_fusion, f32[8,4,64,128]{3,2,1,0:T(8,128)S(1)} %pad_maximum_fusion.13, ...), kind=kLoop, calls=%fused_computation.261 | loop fusion | flops 11534336 | bytes 16007680 | tf_op jit(solution)/shard_map/add | solution.py:214
  (206 shorter events, 49.6 us)
Async XLA Ops:
  2.3 22.6 %collective-permute-start.3 = (f32[4,64,128]{2,1,0:T(8,128)}, f32[4,64,128]{2,1,0:T(8,128)}, u32[]{:S(2)}, u32[]{:S(2)}) collective-permute-start(f32[4,64,128]{2,1,0:T(8,128)} %dynamic-slice_bitcast_fusion.8), channel_id=1, source_target_pairs={{0,1},{1,0},{2,3},{3,2},{4,5},{5,4},{6,7},{7,6},{8,9},{9,8},{10,11... | collective-permute-start | bytes 393224 | tf_op jit(solution)/shard_map/ppermute | solution.py:44
  4.6 18.4 %collective-permute-start.1 = (f32[1,8,2048]{2,1,0:T(8,128)}, f32[1,8,2048]{2,1,0:T(8,128)}, u32[]{:S(2)}, u32[]{:S(2)}) collective-permute-start(f32[1,8,2048]{2,1,0:T(8,128)} %get-tuple-element.148), channel_id=1, source_target_pairs={{0,8},{2,10},{4,12},{6,14},{8,0},{10,2},{12,4},{14,6},{1,9},{3,11}... | collective-permute-start | bytes 196616 | tf_op jit(solution)/shard_map/ppermute | solution.py:112
  8.2 15.8 %collective-permute-start = (f32[1,8,2048]{2,1,0:T(8,128)}, f32[1,8,2048]{2,1,0:T(8,128)}, u32[]{:S(2)}, u32[]{:S(2)}) collective-permute-start(f32[1,8,2048]{2,1,0:T(8,128)} %get-tuple-element.149), channel_id=1, source_target_pairs={{0,8},{2,10},{4,12},{6,14},{8,0},{10,2},{12,4},{14,6},{1,9},{3,11}... | collective-permute-start | bytes 196616 | tf_op jit(solution)/shard_map/ppermute | solution.py:112
  8.2 14.0 %collective-permute-start.2 = (f32[1,16,64]{2,1,0:T(8,128)}, f32[1,16,64]{2,1,0:T(8,128)}, u32[]{:S(2)}, u32[]{:S(2)}) collective-permute-start(f32[1,16,64]{2,1,0:T(8,128)} %bitcast.2), channel_id=1, source_target_pairs={{0,8},{2,10},{4,12},{6,14},{8,0},{10,2},{12,4},{14,6},{1,9},{3,11}... | collective-permute-start | bytes 12296 | tf_op jit(solution)/shard_map/ppermute | solution.py:112
  30.6 3.8 %collective-permute-start.6 = (f32[2,16,64]{2,1,0:T(8,128)S(1)}, f32[2,16,64]{2,1,0:T(8,128)S(1)}, u32[]{:S(2)}, u32[]{:S(2)}) collective-permute-start(f32[2,16,64]{2,1,0:T(8,128)S(1)} %maximum_select_fusion.14), channel_id=1, source_target_pairs={{0,4},{2,6},{4,0},{6,2},{8,12},{10,14},{12,8},{14,10},{1,5},{3,7},... | collective-permute-start | bytes 24584 | tf_op jit(solution)/shard_map/ppermute | solution.py:112
  32.2 5.0 %collective-permute-start.5 = (f32[2,8,2048]{2,1,0:T(8,128)S(1)}, f32[2,8,2048]{2,1,0:T(8,128)S(1)}, u32[]{:S(2)}, u32[]{:S(2)}) collective-permute-start(f32[2,8,2048]{2,1,0:T(8,128)S(1)} %maximum_select_fusion.9), channel_id=1, source_target_pairs={{0,2},{2,0},{4,6},{6,4},{8,10},{10,8},{12,14},{14,12},{1,3},{3,1},... | collective-permute-start | bytes 393224 | tf_op jit(solution)/shard_map/ppermute | solution.py:112
  33.7 6.0 %collective-permute-start.7 = (f32[4,64,128]{2,1,0:T(8,128)S(1)}, f32[4,64,128]{2,1,0:T(8,128)S(1)}, u32[]{:S(2)}, u32[]{:S(2)}) collective-permute-start(f32[4,64,128]{2,1,0:T(8,128)S(1)} %constant_dynamic-slice_fusion.5), channel_id=1, source_target_pairs={{0,1},{1,0},{2,3},{3,2},{4,5},{5,4},{6,7},{7,6},{8,9},{9,8},{10,11... | collective-permute-start | bytes 393224 | tf_op jit(solution)/shard_map/ppermute | solution.py:44
  33.8 5.9 %collective-permute-start.4 = (f32[2,8,2048]{2,1,0:T(8,128)S(1)}, f32[2,8,2048]{2,1,0:T(8,128)S(1)}, u32[]{:S(2)}, u32[]{:S(2)}) collective-permute-start(f32[2,8,2048]{2,1,0:T(8,128)S(1)} %maximum_select_fusion.8), channel_id=1, source_target_pairs={{0,4},{2,6},{4,0},{6,2},{8,12},{10,14},{12,8},{14,10},{1,5},{3,7},... | collective-permute-start | bytes 393224 | tf_op jit(solution)/shard_map/ppermute | solution.py:112
  44.4 5.0 %collective-permute-start.11 = (f32[4,64,128]{2,1,0:T(8,128)S(1)}, f32[4,64,128]{2,1,0:T(8,128)S(1)}, u32[]{:S(2)}, u32[]{:S(2)}) collective-permute-start(f32[4,64,128]{2,1,0:T(8,128)S(1)} %constant_dynamic-slice_fusion.4), channel_id=1, source_target_pairs={{0,1},{1,0},{2,3},{3,2},{4,5},{5,4},{6,7},{7,6},{8,9},{9,8},{10,11... | collective-permute-start | bytes 393224 | tf_op jit(solution)/shard_map/ppermute | solution.py:44
  44.5 4.2 %collective-permute-start.10 = (f32[4,16,64]{2,1,0:T(8,128)S(1)}, f32[4,16,64]{2,1,0:T(8,128)S(1)}, u32[]{:S(2)}, u32[]{:S(2)}) collective-permute-start(f32[4,16,64]{2,1,0:T(8,128)S(1)} %bitcast.260), channel_id=1, source_target_pairs={{0,2},{2,0},{4,6},{6,4},{8,10},{10,8},{12,14},{14,12},{1,3},{3,1},... | collective-permute-start | bytes 49160 | tf_op jit(solution)/shard_map/ppermute | solution.py:112
  45.2 8.4 %collective-permute-start.9 = (f32[4,8,2048]{2,1,0:T(8,128)S(1)}, f32[4,8,2048]{2,1,0:T(8,128)S(1)}, u32[]{:S(2)}, u32[]{:S(2)}) collective-permute-start(f32[4,8,2048]{2,1,0:T(8,128)S(1)} %bitcast.230), channel_id=1, source_target_pairs={{0,4},{2,6},{4,0},{6,2},{8,12},{10,14},{12,8},{14,10},{1,5},{3,7},... | collective-permute-start | bytes 786440 | tf_op jit(solution)/shard_map/ppermute | solution.py:112
  45.7 8.3 %collective-permute-start.8 = (f32[4,8,2048]{2,1,0:T(8,128)S(1)}, f32[4,8,2048]{2,1,0:T(8,128)S(1)}, u32[]{:S(2)}, u32[]{:S(2)}) collective-permute-start(f32[4,8,2048]{2,1,0:T(8,128)S(1)} %bitcast.232), channel_id=1, source_target_pairs={{0,2},{2,0},{4,6},{6,4},{8,10},{10,8},{12,14},{14,12},{1,3},{3,1},... | collective-permute-start | bytes 786440 | tf_op jit(solution)/shard_map/ppermute | solution.py:112
  57.7 5.5 %collective-permute-start.14 = (f32[4,64,128]{2,1,0:T(8,128)}, f32[4,64,128]{2,1,0:T(8,128)}, u32[]{:S(2)}, u32[]{:S(2)}) collective-permute-start(f32[4,64,128]{2,1,0:T(8,128)} %constant_dynamic-slice_fusion.3), channel_id=1, source_target_pairs={{0,1},{1,0},{2,3},{3,2},{4,5},{5,4},{6,7},{7,6},{8,9},{9,8},{10,11... | collective-permute-start | bytes 393224 | tf_op jit(solution)/shard_map/ppermute | solution.py:44
  58.6 9.0 %collective-permute-start.13 = (f32[2,2,4,32,128]{4,3,2,1,0:T(8,128)}, f32[2,2,4,32,128]{4,3,2,1,0:T(8,128)}, u32[]{:S(2)}, u32[]{:S(2)}) collective-permute-start(f32[2,2,4,32,128]{4,3,2,1,0:T(8,128)} %dynamic-slice_bitcast_fusion.2), channel_id=1, source_target_pairs={{0,4},{2,6},{4,0},{6,2},{8,12},{10,14},{12,8},{14,10},{1,5},{3,7},... | collective-permute-start | bytes 786440 | tf_op jit(solution)/shard_map/ppermute | solution.py:159
  60.0 8.8 %collective-permute-start.12 = (f32[4,1,4,32,128]{4,3,2,0,1:T(8,128)S(1)}, f32[4,1,4,32,128]{4,3,2,0,1:T(8,128)}, u32[]{:S(2)}, u32[]{:S(2)}) collective-permute-start(f32[4,1,4,32,128]{4,3,2,0,1:T(8,128)S(1)} %dynamic-slice_bitcast_fusion.3), channel_id=1, source_target_pairs={{0,2},{2,0},{4,6},{6,4},{8,10},{10,8},{12,14},{14,12},{1,3},{3,1},... | collective-permute-start | bytes 786440 | tf_op jit(solution)/shard_map/ppermute | solution.py:159
  69.8 5.2 %collective-permute-start.19 = (f32[4,64,128]{2,1,0:T(8,128)S(1)}, f32[4,64,128]{2,1,0:T(8,128)S(1)}, u32[]{:S(2)}, u32[]{:S(2)}) collective-permute-start(f32[4,64,128]{2,1,0:T(8,128)S(1)} %constant_dynamic-slice_fusion.2), channel_id=1, source_target_pairs={{0,1},{1,0},{2,3},{3,2},{4,5},{5,4},{6,7},{7,6},{8,9},{9,8},{10,11... | collective-permute-start | bytes 393224 | tf_op jit(solution)/shard_map/ppermute | solution.py:44
  69.9 8.3 %collective-permute-start.18 = (f32[2,1,4,32,128]{4,3,2,0,1:T(8,128)S(1)}, f32[2,1,4,32,128]{4,3,2,0,1:T(8,128)S(1)}, u32[]{:S(2)}, u32[]{:S(2)}) collective-permute-start(f32[2,1,4,32,128]{4,3,2,0,1:T(8,128)S(1)} %dynamic-slice_bitcast_fusion.6), channel_id=1, source_target_pairs={{0,2},{2,0},{4,6},{6,4},{8,10},{10,8},{12,14},{14,12},{1,3},{3,1},... | collective-permute-start | bytes 393224 | tf_op jit(solution)/shard_map/ppermute | solution.py:159
  71.3 7.0 %collective-permute-start.17 = (f32[2,1,4,32,128]{4,3,2,0,1:T(8,128)S(1)}, f32[2,1,4,32,128]{4,3,2,0,1:T(8,128)S(1)}, u32[]{:S(2)}, u32[]{:S(2)}) collective-permute-start(f32[2,1,4,32,128]{4,3,2,0,1:T(8,128)S(1)} %dynamic-slice_bitcast_fusion.7), channel_id=1, source_target_pairs={{0,4},{2,6},{4,0},{6,2},{8,12},{10,14},{12,8},{14,10},{1,5},{3,7},... | collective-permute-start | bytes 393224 | tf_op jit(solution)/shard_map/ppermute | solution.py:159
  73.4 9.2 %collective-permute-start.16 = (f32[2,2,4,32,128]{4,3,2,1,0:T(8,128)S(1)}, f32[2,2,4,32,128]{4,3,2,1,0:T(8,128)S(1)}, u32[]{:S(2)}, u32[]{:S(2)}) collective-permute-start(f32[2,2,4,32,128]{4,3,2,1,0:T(8,128)S(1)} %dynamic-slice_bitcast_fusion), channel_id=1, source_target_pairs={{0,4},{2,6},{4,0},{6,2},{8,12},{10,14},{12,8},{14,10},{1,5},{3,7},... | collective-permute-start | bytes 786440 | tf_op jit(solution)/shard_map/ppermute | solution.py:159
  74.1 8.5 %collective-permute-start.15 = (f32[4,1,4,32,128]{4,3,2,0,1:T(8,128)S(1)}, f32[4,1,4,32,128]{4,3,2,0,1:T(8,128)S(1)}, u32[]{:S(2)}, u32[]{:S(2)}) collective-permute-start(f32[4,1,4,32,128]{4,3,2,0,1:T(8,128)S(1)} %dynamic-slice_bitcast_fusion.1), channel_id=1, source_target_pairs={{0,2},{2,0},{4,6},{6,4},{8,10},{10,8},{12,14},{14,12},{1,3},{3,1},... | collective-permute-start | bytes 786440 | tf_op jit(solution)/shard_map/ppermute | solution.py:159
  82.7 7.5 %collective-permute-start.23 = (f32[1,1,4,32,128]{4,3,2,1,0:T(8,128)S(1)}, f32[1,1,4,32,128]{4,3,2,1,0:T(8,128)S(1)}, u32[]{:S(2)}, u32[]{:S(2)}) collective-permute-start(f32[1,1,4,32,128]{4,3,2,1,0:T(8,128)S(1)} %dynamic-slice_bitcast_fusion.11), channel_id=1, source_target_pairs={{0,8},{2,10},{4,12},{6,14},{8,0},{10,2},{12,4},{14,6},{1,9},{3,11}... | collective-permute-start | bytes 196616 | tf_op jit(solution)/shard_map/ppermute | solution.py:159
  83.1 8.2 %collective-permute-start.22 = (f32[1,1,4,32,128]{4,3,2,1,0:T(8,128)S(1)}, f32[1,1,4,32,128]{4,3,2,1,0:T(8,128)S(1)}, u32[]{:S(2)}, u32[]{:S(2)}) collective-permute-start(f32[1,1,4,32,128]{4,3,2,1,0:T(8,128)S(1)} %dynamic-slice_bitcast_fusion.12), channel_id=1, source_target_pairs={{0,8},{2,10},{4,12},{6,14},{8,0},{10,2},{12,4},{14,6},{1,9},{3,11}... | collective-permute-start | bytes 196616 | tf_op jit(solution)/shard_map/ppermute | solution.py:159
  85.7 5.6 %collective-permute-start.21 = (f32[2,1,4,32,128]{4,3,2,0,1:T(8,128)S(1)}, f32[2,1,4,32,128]{4,3,2,0,1:T(8,128)S(1)}, u32[]{:S(2)}, u32[]{:S(2)}) collective-permute-start(f32[2,1,4,32,128]{4,3,2,0,1:T(8,128)S(1)} %dynamic-slice_bitcast_fusion.4), channel_id=1, source_target_pairs={{0,2},{2,0},{4,6},{6,4},{8,10},{10,8},{12,14},{14,12},{1,3},{3,1},... | collective-permute-start | bytes 393224 | tf_op jit(solution)/shard_map/ppermute | solution.py:159
  86.5 5.9 %collective-permute-start.20 = (f32[2,1,4,32,128]{4,3,2,0,1:T(8,128)S(1)}, f32[2,1,4,32,128]{4,3,2,0,1:T(8,128)S(1)}, u32[]{:S(2)}, u32[]{:S(2)}) collective-permute-start(f32[2,1,4,32,128]{4,3,2,0,1:T(8,128)S(1)} %dynamic-slice_bitcast_fusion.5), channel_id=1, source_target_pairs={{0,4},{2,6},{4,0},{6,2},{8,12},{10,14},{12,8},{14,10},{1,5},{3,7},... | collective-permute-start | bytes 393224 | tf_op jit(solution)/shard_map/ppermute | solution.py:159
  92.4 6.6 %collective-permute-start.25 = (f32[1,1,4,32,128]{4,3,2,1,0:T(8,128)S(1)}, f32[1,1,4,32,128]{4,3,2,1,0:T(8,128)S(1)}, u32[]{:S(2)}, u32[]{:S(2)}) collective-permute-start(f32[1,1,4,32,128]{4,3,2,1,0:T(8,128)S(1)} %dynamic-slice_bitcast_fusion.9), channel_id=1, source_target_pairs={{0,8},{2,10},{4,12},{6,14},{8,0},{10,2},{12,4},{14,6},{1,9},{3,11}... | collective-permute-start | bytes 196616 | tf_op jit(solution)/shard_map/ppermute | solution.py:159
  92.8 6.9 %collective-permute-start.24 = (f32[1,1,4,32,128]{4,3,2,1,0:T(8,128)S(1)}, f32[1,1,4,32,128]{4,3,2,1,0:T(8,128)S(1)}, u32[]{:S(2)}, u32[]{:S(2)}) collective-permute-start(f32[1,1,4,32,128]{4,3,2,1,0:T(8,128)S(1)} %dynamic-slice_bitcast_fusion.10), channel_id=1, source_target_pairs={{0,8},{2,10},{4,12},{6,14},{8,0},{10,2},{12,4},{14,6},{1,9},{3,11}... | collective-permute-start | bytes 196616 | tf_op jit(solution)/shard_map/ppermute | solution.py:159
  101.5 5.2 %collective-permute-start.27 = (f32[1,4,32,128]{3,2,1,0:T(8,128)S(1)}, f32[1,4,32,128]{3,2,1,0:T(8,128)S(1)}, u32[]{:S(2)}, u32[]{:S(2)}) collective-permute-start(f32[1,4,32,128]{3,2,1,0:T(8,128)S(1)} %get-tuple-element.146), channel_id=1, source_target_pairs={{0,8},{2,10},{4,12},{6,14},{8,0},{10,2},{12,4},{14,6},{1,9},{3,11}... | collective-permute-start | bytes 196616 | tf_op jit(solution)/shard_map/ppermute | solution.py:112
  102.4 5.9 %collective-permute-start.26 = (f32[1,4,32,128]{3,2,1,0:T(8,128)S(1)}, f32[1,4,32,128]{3,2,1,0:T(8,128)S(1)}, u32[]{:S(2)}, u32[]{:S(2)}) collective-permute-start(f32[1,4,32,128]{3,2,1,0:T(8,128)S(1)} %get-tuple-element.147), channel_id=1, source_target_pairs={{0,8},{2,10},{4,12},{6,14},{8,0},{10,2},{12,4},{14,6},{1,9},{3,11}... | collective-permute-start | bytes 196616 | tf_op jit(solution)/shard_map/ppermute | solution.py:112
  108.3 5.0 %collective-permute-start.29 = (f32[2,4,32,128]{3,2,1,0:T(8,128)S(1)}, f32[2,4,32,128]{3,2,1,0:T(8,128)S(1)}, u32[]{:S(2)}, u32[]{:S(2)}) collective-permute-start(f32[2,4,32,128]{3,2,1,0:T(8,128)S(1)} %maximum_select_fusion.11), channel_id=1, source_target_pairs={{0,2},{2,0},{4,6},{6,4},{8,10},{10,8},{12,14},{14,12},{1,3},{3,1},... | collective-permute-start | bytes 393224 | tf_op jit(solution)/shard_map/ppermute | solution.py:112
  109.1 6.4 %collective-permute-start.28 = (f32[2,4,32,128]{3,2,1,0:T(8,128)S(1)}, f32[2,4,32,128]{3,2,1,0:T(8,128)S(1)}, u32[]{:S(2)}, u32[]{:S(2)}) collective-permute-start(f32[2,4,32,128]{3,2,1,0:T(8,128)S(1)} %maximum_select_fusion.10), channel_id=1, source_target_pairs={{0,4},{2,6},{4,0},{6,2},{8,12},{10,14},{12,8},{14,10},{1,5},{3,7},... | collective-permute-start | bytes 393224 | tf_op jit(solution)/shard_map/ppermute | solution.py:112
  115.5 8.3 %collective-permute-start.31 = (f32[4,4,32,128]{3,2,1,0:T(8,128)S(1)}, f32[4,4,32,128]{3,2,1,0:T(8,128)S(1)}, u32[]{:S(2)}, u32[]{:S(2)}) collective-permute-start(f32[4,4,32,128]{3,2,1,0:T(8,128)S(1)} %bitcast.242), channel_id=1, source_target_pairs={{0,4},{2,6},{4,0},{6,2},{8,12},{10,14},{12,8},{14,10},{1,5},{3,7},... | collective-permute-start | bytes 786440 | tf_op jit(solution)/shard_map/ppermute | solution.py:112
  117.4 6.4 %collective-permute-start.30 = (f32[4,4,32,128]{3,2,1,0:T(8,128)S(1)}, f32[4,4,32,128]{3,2,1,0:T(8,128)S(1)}, u32[]{:S(2)}, u32[]{:S(2)}) collective-permute-start(f32[4,4,32,128]{3,2,1,0:T(8,128)S(1)} %bitcast.244), channel_id=1, source_target_pairs={{0,2},{2,0},{4,6},{6,4},{8,10},{10,8},{12,14},{14,12},{1,3},{3,1},... | collective-permute-start | bytes 786440 | tf_op jit(solution)/shard_map/ppermute | solution.py:112
  (30 other events, 141.4 us)

commit v8 on v7

--- a/solution.py
+++ b/solution.py
@@ -29,9 +29,17 @@
 
 def damping(widths, positions, count_x, count_y, count_z):
     edges = widths.astype(jnp.float32)
-    along_x = ramp(positions, count_x, edges[0], edges[1])
-    along_y = ramp(jnp.arange(count_y, dtype=jnp.float32), count_y, edges[2], edges[3])
-    along_z = ramp(jnp.arange(count_z, dtype=jnp.float32), count_z, edges[4], edges[5])
+    longest = max(positions.shape[0], count_y, count_z)
+    line = jnp.arange(longest, dtype=jnp.float32)
+    x_line = jnp.pad(positions, (0, longest - positions.shape[0]))
+    place = jnp.stack([x_line, line, line])
+    count = jnp.stack([jnp.asarray(count_x, jnp.float32), jnp.float32(count_y), jnp.float32(count_z)])[:, None]
+    lower = jnp.stack([edges[0], edges[2], edges[4]])[:, None]
+    upper = jnp.stack([edges[1], edges[3], edges[5]])[:, None]
+    ramps = ramp(place, count, lower, upper)
+    along_x = ramps[0, : positions.shape[0]]
+    along_y = ramps[1, :count_y]
+    along_z = ramps[2, :count_z]
     return damp_peak * (along_x[:, None, None] + along_y[None, :, None] + along_z[None, None, :])
 
 
@@ -126,8 +134,10 @@
     return order[:-2] + order[-1:] + order[-2:-1] if len(order) > 1 else order
 
 
-def chain(held, kind, order):
-    return {"held": held, "kind": kind, "order": list(order), "i": 0, "bits": [] if kind == "ag" else sorted(order)}
+def chain(held, kind, order, bits=None):
+    if bits is None:
+        bits = [] if kind == "ag" else sorted(order)
+    return {"held": held, "kind": kind, "order": list(order), "i": 0, "bits": list(bits)}
 
 
 def chain_step(c):
@@ -257,20 +267,23 @@
     far_first = list(reversed(bits))
     near_first = list(bits)
 
-    half_a, half_b = halves(model_held, 1)
-    model_a = chain(half_a, "ag", far_first)
-    model_b = chain(half_b, "ag", swap_last(far_first))
+    top = far_first[0]
+    model_c = chain(model_held, "ag", far_first[:1])
     gains_c = chain(gains_held, "ag", far_first)
     tasks = [task_wave(0), light_prep, task_wave(2)]
-    for i in range(len(bits)):
+    run_group([model_c, gains_c], tasks[0])
+    half_a, half_b = halves(model_c["held"], 1)
+    model_a = chain(half_a, "ag", far_first[1:], [top])
+    model_b = chain(half_b, "ag", swap_first(far_first[1:]), [top])
+    for i in range(1, len(bits)):
         run_group([model_a, model_b, gains_c], tasks[i] if i < len(tasks) else nothing)
     for i in range(len(bits), len(tasks)):
         tasks[i]()
     model_held = jnp.concatenate([model_a["held"], model_b["held"]], axis=1)
     gains_held = gains_c["held"]
     light_a, light_b = halves(st["light"].reshape(n_shot, slab, span_y, span_z), 2)
-    light_a = chain(light_a, "rs", near_first)
-    light_b = chain(light_b, "rs", swap_first(near_first))
+    light_a = chain(light_a, "rs", near_first[:-1], near_first)
+    light_b = chain(light_b, "rs", swap_first(near_first[:-1]), near_first)
 
     def born_pass():
         model = model_held.reshape(span_z, span_x * span_y).T.reshape(span_x, span_y, span_z)
@@ -282,22 +295,33 @@
 
     image = st["drive0"] * born1 + st["drive1"] * born2
     image_a, image_b = halves(image.reshape(n_shot, slab, span_y, span_z), 2)
-    image_a = chain(image_a, "rs", near_first)
-    image_b = chain(image_b, "rs", swap_first(near_first))
+    image_a = chain(image_a, "rs", near_first[:-1], near_first)
+    image_b = chain(image_b, "rs", swap_first(near_first[:-1]), near_first)
     tasks = [task_wave(3)]
-    for i in range(len(bits)):
+    for i in range(len(bits) - 1):
         run_group([image_a, image_b, light_a, light_b], tasks[i] if i < len(tasks) else nothing)
-    for i in range(len(bits), len(tasks)):
+    for i in range(len(bits) - 1, len(tasks)):
         tasks[i]()
-    image_part = jnp.concatenate([image_a["held"][0], image_b["held"][0]], axis=1)
-    light_part = jnp.concatenate([light_a["held"][0], light_b["held"][0]], axis=1)
+    both = jnp.concatenate(
+        [
+            jnp.concatenate([image_a["held"], image_b["held"]], axis=2),
+            jnp.concatenate([light_a["held"], light_b["held"]], axis=2),
+        ],
+        axis=1,
+    )
+    last = chain(both, "rs", near_first[-1:], near_first[-1:])
+    run_group([last], nothing)
+    image_part = last["held"][0, :slab]
+    light_part = last["held"][0, slab:]
 
     table_all = gains_held.reshape(n_shot * gains.shape[0], gains.shape[1])
     filt_part = lateral_filter(image_part / (light_part + eps), table_all)
-    part_a, part_b = halves(filt_part[None], 2)
-    filt_a = chain(part_a, "ag", far_first)
-    filt_b = chain(part_b, "ag", swap_last(far_first))
-    for i in range(len(bits)):
+    filt_c = chain(filt_part[None], "ag", far_first[:1])
+    run_group([filt_c], nothing)
+    part_a, part_b = halves(filt_c["held"], 2)
+    filt_a = chain(part_a, "ag", far_first[1:], [top])
+    filt_b = chain(part_b, "ag", swap_first(far_first[1:]), [top])
+    for i in range(1, len(bits)):
         run_group([filt_a, filt_b], nothing)
     new_model = jnp.concatenate([filt_a["held"], filt_b["held"]], axis=2).reshape(span_x, span_y, span_z)
     filtered = lax.dynamic_slice_in_dim(new_model, me_shot * depth, depth, 2)

time: 136 us -> 135 us (level)
  waiting for transfers between devices: 34.1 us -> 47.7 us
  starting transfers between devices: 36.7 us -> 25.5 us
  local copies, waits for them, and re-layouts: 19.3 us -> 17.2 us
  other arithmetic: 38.7 us -> 37.1 us
    ppermute x12 -> x9, waiting for transfers between devices: 13.1 us -> 22.7 us  [rs_step(): got = lax.ppermute(send, 'shot', [(i, i ^ k) for i in range(n)])]
    ppermute x15 -> x13, starting transfers between devices: 20.2 us -> 12.9 us  [ag_step(): theirs = lax.ppermute(held, 'shot', [(i, i ^ k) for i in range(n)])]
    add x3 -> x1, other arithmetic: 4.38 us -> 0.08 us  [ramp(): return low_part * low_part + high_part * high_part]
    ppermute x15 -> x13, waiting for transfers between devices: 20.4 us -> 24.5 us  [ag_step(): theirs = lax.ppermute(held, 'shot', [(i, i ^ k) for i in range(n)])]
    ppermute x12 -> x9, starting transfers between devices: 15.3 us -> 11.3 us  [rs_step(): got = lax.ppermute(send, 'shot', [(i, i ^ k) for i in range(n)])]
    another operation x0 -> x1, other arithmetic: none -> 3.86 us  [damping(): lower = jnp.stack([edges[0], edges[2], edges[4]])[:, None]]
    mul x1, local copies, waits for them, and re-layouts: 1.53 us -> 0.06 us  [lateral_filter(): real_part * weight]
    select_n x15 -> x13, other arithmetic: 2.97 us -> 2.21 us  [ag_step(): jnp.where(first, jnp.concatenate([mine, other], axis=1), jnp.concatenate(...]
  transfers between devices with their start and end apart: 34 -> 29, of which waited for: 17 -> 16; matrix products, arithmetic and copies ran while one was open for 25% -> 25% of each run, Pallas kernels for 0% -> 0%
where the time goes in v8:
time: 135 us; the launch traced here: 134 us
  waiting for transfers between devices  47.7 us (35%)
  other arithmetic  37.1 us (27%)
  starting transfers between devices  25.5 us (19%)
  local copies, waits for them, and re-layouts  17.2 us (13%)
  between operations  4.78 us (4%)
  matrix products  1.7 us (1%)
    ppermute x13, waiting for transfers between devices, ag_step(): theirs = lax.ppermute(held, 'shot', [(i, i ^ k) for i in range(n)])  24.5 us
    ppermute x9, waiting for transfers between devices, rs_step(): got = lax.ppermute(send, 'shot', [(i, i ^ k) for i in range(n)])  22.7 us
    ppermute x13, starting transfers between devices, ag_step(): theirs = lax.ppermute(held, 'shot', [(i, i ^ k) for i in range(n)])  12.9 us
    add x3, other arithmetic, inject(): return field + jnp.where(hit, source_gain[0] * wavelet[0, moment], 0.0)  11.7 us
    ppermute x9, starting transfers between devices, rs_step(): got = lax.ppermute(send, 'shot', [(i, i ^ k) for i in range(n)])  11.3 us
    add x2, other arithmetic, born_second(): 2.0 * born + speed_term * laplace_x(with_halo(born)) - absorber * born  5.85 us
    another operation x1, other arithmetic, damping(): lower = jnp.stack([edges[0], edges[2], edges[4]])[:, None]  3.86 us
    unnamed x45, local copies, waits for them, and re-layouts  3.56 us
  transfers between devices with their start and end apart: 29, of which 16 were waited for; matrix products, arithmetic and copies ran while one was open for 25% of the time, Pallas kernels for 0%

profile of v8, /device:TPU:0, one launch (start us, length us, event | category | flops | bytes accessed | tf_op | source)
XLA Modules:
  0.0 134.1 jit_solution(140480276296482432)
XLA Ops:
  0.7 1.7 %dynamic-slice_bitcast_fusion.9 = f32[4,64,128]{2,1,0:T(8,128)} fusion(f32[1,32,64,128]{3,2,1,0:T(8,128)} %param.12, s32[]{:T(128)S(6)} %select_n.399), kind=kLoop, calls=%fused_computation.357 | loop fusion | bytes 262148 | tf_op jit(solution)/shard_map/dynamic_slice | solution.py:51
  4.6 3.6 %collective-permute-start = (f32[1,16,2048]{2,1,0:T(8,128)}, f32[1,16,2048]{2,1,0:T(8,128)}, u32[]{:S(2)}, u32[]{:S(2)}) collective-permute-start(f32[1,16,2048]{2,1,0:T(8,128)} %concatenate.199), channel_id=1, source_target_pairs={{0,8},{2,10},{4,12},{6,14},{8,0},{10,2},{12,4},{14,6},{1,9},{3,11}... | collective-permute-start | bytes 393224 | tf_op jit(solution)/shard_map/ppermute | solution.py:120
  10.3 3.9 %pad_maximum_fusion.15 = (f32[3]{0:T(128)S(1)}, f32[3]{0:T(128)S(1)}) fusion(f32[1]{0:T(128)} %get-tuple-element.153, f32[1]{0:T(128)} %get-tuple-element.154, f32[1]{0:T(128)} %get-tuple-element.149, f32[1]{0:T(128)} %get-tuple-element.150, f32[1]{0:T(128)} %get-tuple-element.151, f32[1]{0:T(128)} %get-tuple-element.152), kind=kLoop, calls=%fused_computation.410 | loop fusion | flops 12 | bytes 48 | tf_op jit(solution)/shard_map/stack | solution.py:37
  22.3 4.5 %fusion.2 = (f32[32,64,128]{2,1,0:T(8,128)S(1)}, f32[32,64,128]{2,1,0:T(8,128)S(1)}) fusion(f32[]{:T(128)S(6)} %mul.319, f32[128]{0:T(128)} %slice_bitcast_fusion, f32[32,64]{1,0:T(8,128)S(1)} %broadcast_add_fusion, pred[128]{0:T(512)(128)(4,1)} %iota_compare_fusion.1, pred[32,64]{1,0:T(8,128)(4,1)} %broadcast_and_fusion, f32[1,32,64,128]{3,2,1,0:T(8,128)} %param.11, ...), kind=kLoop, calls=%fused_computation.118 | loop fusion | flops 12058624 | bytes 16009860 | tf_op jit(solution)/shard_map/add | solution.py:213
  28.1 1.9 %collective-permute-start.5 = (f32[2,16,64]{2,1,0:T(8,128)S(1)}, f32[2,16,64]{2,1,0:T(8,128)S(1)}, u32[]{:S(2)}, u32[]{:S(2)}) collective-permute-start(f32[2,16,64]{2,1,0:T(8,128)S(1)} %maximum_select_fusion.12), channel_id=1, source_target_pairs={{0,4},{2,6},{4,0},{6,2},{8,12},{10,14},{12,8},{14,10},{1,5},{3,7},... | collective-permute-start | bytes 24584 | tf_op jit(solution)/shard_map/ppermute | solution.py:120
  30.2 1.6 %collective-permute-start.4 = (f32[2,8,2048]{2,1,0:T(8,128)S(1)}, f32[2,8,2048]{2,1,0:T(8,128)S(1)}, u32[]{:S(2)}, u32[]{:S(2)}) collective-permute-start(f32[2,8,2048]{2,1,0:T(8,128)S(1)} %get-tuple-element.142), channel_id=1, source_target_pairs={{0,2},{2,0},{4,6},{6,4},{8,10},{10,8},{12,14},{14,12},{1,3},{3,1},... | collective-permute-start | bytes 393224 | tf_op jit(solution)/shard_map/ppermute | solution.py:120
  32.4 2.9 %collective-permute-done.4 = f32[2,8,2048]{2,1,0:T(8,128)S(1)} collective-permute-done((f32[2,8,2048]{2,1,0:T(8,128)S(1)}, f32[2,8,2048]{2,1,0:T(8,128)S(1)}, u32[]{:S(2)}, u32[]{:S(2)}) %collective-permute-start.4) | collective-permute-done | bytes 131104 | tf_op jit(solution)/shard_map/ppermute | solution.py:120
  35.3 2.4 %collective-permute-done.3 = f32[2,8,2048]{2,1,0:T(8,128)S(1)} collective-permute-done((f32[2,8,2048]{2,1,0:T(8,128)S(1)}, f32[2,8,2048]{2,1,0:T(8,128)S(1)}, u32[]{:S(2)}, u32[]{:S(2)}) %collective-permute-start.3) | collective-permute-done | bytes 131104 | tf_op jit(solution)/shard_map/ppermute | solution.py:120
  37.9 3.2 %fusion.3 = (f32[32,64,128]{2,1,0:T(8,128)S(1)}, f32[32,64,128]{2,1,0:T(8,128)S(1)}) fusion(f32[32,64,128]{2,1,0:T(8,128)S(1)} %get-tuple-element.69, f32[32,64,128]{2,1,0:T(8,128)S(1)} %bitcast.192, f32[]{:T(128)S(6)} %mul.330, f32[128]{0:T(128)S(1)} %copy-done.12, f32[32,64]{1,0:T(8,128)S(1)} %broadcast_add_fusion, pred[128]{0:T(512)(128)(4,1)S(1)} %copy-done.15, ...), kind=kLoop, calls=%fused_computation.119 | loop fusion | flops 12058624 | bytes 16012292 | tf_op jit(solution)/shard_map/add | solution.py:213
  41.0 1.1 multiply_add_fusion.1
  43.4 1.7 %collective-permute-start.7 = (f32[4,8,2048]{2,1,0:T(8,128)S(1)}, f32[4,8,2048]{2,1,0:T(8,128)S(1)}, u32[]{:S(2)}, u32[]{:S(2)}) collective-permute-start(f32[4,8,2048]{2,1,0:T(8,128)S(1)} %bitcast.215), channel_id=1, source_target_pairs={{0,2},{2,0},{4,6},{6,4},{8,10},{10,8},{12,14},{14,12},{1,3},{3,1},... | collective-permute-start | bytes 786440 | tf_op jit(solution)/shard_map/ppermute | solution.py:120
  45.1 1.5 %collective-permute-done.9 = f32[4,16,64]{2,1,0:T(8,128)S(1)} collective-permute-done((f32[4,16,64]{2,1,0:T(8,128)S(1)}, f32[4,16,64]{2,1,0:T(8,128)S(1)}, u32[]{:S(2)}, u32[]{:S(2)}) %collective-permute-start.9) | collective-permute-done | bytes 16416 | tf_op jit(solution)/shard_map/ppermute | solution.py:120
  47.3 4.0 %fusion.4 = (f32[32,64,128]{2,1,0:T(8,128)}, f32[32,64,128]{2,1,0:T(8,128)}) fusion(f32[32,64,128]{2,1,0:T(8,128)S(1)} %get-tuple-element.67, f32[32,64,128]{2,1,0:T(8,128)S(1)} %get-tuple-element.69, f32[]{:T(128)S(6)} %mul.339, f32[128]{0:T(128)S(1)} %copy-done.12, f32[32,64]{1,0:T(8,128)S(1)} %broadcast_add_fusion, pred[128]{0:T(512)(128)(4,1)S(1)} %copy-done.15, ...), kind=kLoop, calls=%fused_computation.120 | loop fusion | flops 12058624 | bytes 16012292 | tf_op jit(solution)/shard_map/add | solution.py:213
  53.0 2.5 %copy.46 = f32[2048,128]{1,0:T(8,128)} copy(f32[2048,128]{0,1:T(8,128)} %bitcast.200) | data formatting | bytes 2097152 | tf_op jit(solution)/shard_map/transpose | solution.py:289
  55.6 1.4 %mul.340 = f32[32,64,128]{2,1,0:T(8,128)S(1)} multiply(f32[32,64,128]{2,1,0:T(8,128)} %bitcast.194, f32[32,64,128]{2,1,0:T(8,128)S(1)} %get-tuple-element.77) | non-fusion elementwise | flops 262144 | bytes 3145728 | tf_op jit(solution)/shard_map/mul | solution.py:290
  57.3 1.4 %collective-permute-start.12 = (f32[2,2,4,32,128]{4,3,2,1,0:T(8,128)S(1)}, f32[2,2,4,32,128]{4,3,2,1,0:T(8,128)S(1)}, u32[]{:S(2)}, u32[]{:S(2)}) collective-permute-start(f32[2,2,4,32,128]{4,3,2,1,0:T(8,128)S(1)} %dynamic-slice_bitcast_fusion.3), channel_id=1, source_target_pairs={{0,4},{2,6},{4,0},{6,2},{8,12},{10,14},{12,8},{14,10},{1,5},{3,7},... | collective-permute-start | bytes 786440 | tf_op jit(solution)/shard_map/ppermute | solution.py:169
  58.7 1.6 %collective-permute-start.11 = (f32[4,1,4,32,128]{4,3,2,0,1:T(8,128)S(1)}, f32[4,1,4,32,128]{4,3,2,0,1:T(8,128)S(1)}, u32[]{:S(2)}, u32[]{:S(2)}) collective-permute-start(f32[4,1,4,32,128]{4,3,2,0,1:T(8,128)S(1)} %dynamic-slice_bitcast_fusion.4), channel_id=1, source_target_pairs={{0,2},{2,0},{4,6},{6,4},{8,10},{10,8},{12,14},{14,12},{1,3},{3,1},... | collective-permute-start | bytes 786440 | tf_op jit(solution)/shard_map/ppermute | solution.py:169
  60.5 2.9 %fusion.92 = f32[32,64,128]{2,1,0:T(8,128)S(1)} fusion(f32[40,64,128]{2,1,0:T(8,128)S(1)} %constant_dynamic-update-slice_fusion.2, f32[32,64,128]{2,1,0:T(8,128)S(1)} %bitcast.195, f32[32,64,128]{2,1,0:T(8,128)S(1)} %get-tuple-element.79, f32[32,64,128]{2,1,0:T(8,128)S(1)} %mul.340, f32[128]{0:T(128)S(1)} %copy-done.13, f32[32,64]{1,0:T(8,128)S(1)} %broadcast_add_fusion, ...), kind=kLoop, calls=%fused_computation.208 | loop fusion | flops 11272192 | bytes 16007680 | tf_op jit(solution)/shard_map/add | solution.py:224
  63.5 2.6 %collective-permute-done.12 = f32[2,2,4,32,128]{4,3,2,1,0:T(8,128)S(1)} collective-permute-done((f32[2,2,4,32,128]{4,3,2,1,0:T(8,128)S(1)}, f32[2,2,4,32,128]{4,3,2,1,0:T(8,128)S(1)}, u32[]{:S(2)}, u32[]{:S(2)}) %collective-permute-start.12) | collective-permute-done | bytes 262176 | tf_op jit(solution)/shard_map/ppermute | solution.py:169
  67.4 1.6 %collective-permute-start.17 = (f32[2,1,4,32,128]{4,3,2,0,1:T(8,128)S(1)}, f32[2,1,4,32,128]{4,3,2,0,1:T(8,128)S(1)}, u32[]{:S(2)}, u32[]{:S(2)}) collective-permute-start(f32[2,1,4,32,128]{4,3,2,0,1:T(8,128)S(1)} %dynamic-slice_bitcast_fusion.7), channel_id=1, source_target_pairs={{0,2},{2,0},{4,6},{6,4},{8,10},{10,8},{12,14},{14,12},{1,3},{3,1},... | collective-permute-start | bytes 393224 | tf_op jit(solution)/shard_map/ppermute | solution.py:169
  70.0 1.6 %collective-permute-start.15 = (f32[2,2,4,32,128]{4,3,2,1,0:T(8,128)S(1)}, f32[2,2,4,32,128]{4,3,2,1,0:T(8,128)S(1)}, u32[]{:S(2)}, u32[]{:S(2)}) collective-permute-start(f32[2,2,4,32,128]{4,3,2,1,0:T(8,128)S(1)} %dynamic-slice_bitcast_fusion.1), channel_id=1, source_target_pairs={{0,4},{2,6},{4,0},{6,2},{8,12},{10,14},{12,8},{14,10},{1,5},{3,7},... | collective-permute-start | bytes 786440 | tf_op jit(solution)/shard_map/ppermute | solution.py:169
  72.5 3.2 %fusion.117 = f32[32,64,128]{2,1,0:T(8,128)} fusion(f32[40,64,128]{2,1,0:T(8,128)S(1)} %constant_dynamic-update-slice_fusion.1, s32[32,64,128]{2,1,0:T(8,128)S(1)} %copy-done), kind=kLoop, calls=%fused_computation.233 | loop fusion | flops 9175040 | bytes 12845056 | tf_op jit(solution)/shard_map/mul | solution.py:216
  75.8 4.5 %collective-permute-done.15 = f32[2,2,4,32,128]{4,3,2,1,0:T(8,128)S(1)} collective-permute-done((f32[2,2,4,32,128]{4,3,2,1,0:T(8,128)S(1)}, f32[2,2,4,32,128]{4,3,2,1,0:T(8,128)S(1)}, u32[]{:S(2)}, u32[]{:S(2)}) %collective-permute-start.15) | collective-permute-done | bytes 262176 | tf_op jit(solution)/shard_map/ppermute | solution.py:169
  81.7 3.7 %collective-permute-done.20 = f32[2,1,4,32,128]{4,3,2,0,1:T(8,128)S(1)} collective-permute-done((f32[2,1,4,32,128]{4,3,2,0,1:T(8,128)S(1)}, f32[2,1,4,32,128]{4,3,2,0,1:T(8,128)S(1)}, u32[]{:S(2)}, u32[]{:S(2)}) %collective-permute-start.20) | collective-permute-done | bytes 131104 | tf_op jit(solution)/shard_map/ppermute | solution.py:169
  86.1 2.7 %collective-permute-start.21 = (f32[1,1,8,64,128]{4,3,2,1,0:T(8,128)S(1)}, f32[1,1,8,64,128]{4,3,2,1,0:T(8,128)S(1)}, u32[]{:S(2)}, u32[]{:S(2)}) collective-permute-start(f32[1,1,8,64,128]{4,3,2,1,0:T(8,128)S(1)} %dynamic-slice_bitcast_fusion), channel_id=1, source_target_pairs={{0,8},{2,10},{4,12},{6,14},{8,0},{10,2},{12,4},{14,6},{1,9},{3,11}... | collective-permute-start | bytes 786440 | tf_op jit(solution)/shard_map/ppermute | solution.py:169
  88.8 10.3 %collective-permute-done.21 = f32[1,1,8,64,128]{4,3,2,1,0:T(8,128)S(1)} collective-permute-done((f32[1,1,8,64,128]{4,3,2,1,0:T(8,128)S(1)}, f32[1,1,8,64,128]{4,3,2,1,0:T(8,128)S(1)}, u32[]{:S(2)}, u32[]{:S(2)}) %collective-permute-start.21) | collective-permute-done | bytes 262176 | tf_op jit(solution)/shard_map/ppermute | solution.py:169
  101.0 8.3 %collective-permute-done.22 = f32[1,4,64,128]{3,2,1,0:T(8,128)S(1)} collective-permute-done((f32[1,4,64,128]{3,2,1,0:T(8,128)S(1)}, f32[1,4,64,128]{3,2,1,0:T(8,128)S(1)}, u32[]{:S(2)}, u32[]{:S(2)}) %collective-permute-start.22) | collective-permute-done | bytes 131104 | tf_op jit(solution)/shard_map/ppermute | solution.py:120
  111.1 3.8 %collective-permute-done.24 = f32[2,4,32,128]{3,2,1,0:T(8,128)S(1)} collective-permute-done((f32[2,4,32,128]{3,2,1,0:T(8,128)S(1)}, f32[2,4,32,128]{3,2,1,0:T(8,128)S(1)}, u32[]{:S(2)}, u32[]{:S(2)}) %collective-permute-start.24) | collective-permute-done | bytes 131104 | tf_op jit(solution)/shard_map/ppermute | solution.py:120
  115.8 1.2 collective-permute-start.25
  118.2 4.4 %collective-permute-done.25 = f32[4,4,32,128]{3,2,1,0:T(8,128)S(1)} collective-permute-done((f32[4,4,32,128]{3,2,1,0:T(8,128)S(1)}, f32[4,4,32,128]{3,2,1,0:T(8,128)S(1)}, u32[]{:S(2)}, u32[]{:S(2)}) %collective-permute-start.25) | collective-permute-done | bytes 262176 | tf_op jit(solution)/shard_map/ppermute | solution.py:120
  122.9 1.1 copy-done.3
  127.3 2.9 %fusion.145 = f32[32,64,128]{2,1,0:T(8,128)S(1)} fusion(f32[40,64,128]{2,1,0:T(8,128)S(1)} %constant_dynamic-update-slice_fusion, f32[32,64,128]{2,1,0:T(8,128)S(1)} %copy-done.7, f32[128]{0:T(128)S(1)} %copy-done.14, f32[32,64]{1,0:T(8,128)S(1)} %broadcast_add_fusion, f32[8,4,64,128]{3,2,1,0:T(8,128)S(1)} %pad_maximum_fusion.13, ...), kind=kLoop, calls=%fused_computation.261 | loop fusion | flops 11534336 | bytes 16007680 | tf_op jit(solution)/shard_map/add | solution.py:224
  (182 shorter events, 33.4 us)
Async XLA Ops:
  0.6 13.5 %copy-start.21 = (f32[3]{0:T(128)S(1)}, f32[3]{0:T(128)}, u32[]{:S(2)}) copy-start(f32[3]{0:T(128)} %constant.319.clone.1) | copy-start | bytes 40
  0.6 15.5 %copy-start.1 = (f32[1,32,64,128]{3,2,1,0:T(8,128)S(1)}, f32[1,32,64,128]{3,2,1,0:T(8,128)}, u32[]{:S(2)}) copy-start(f32[1,32,64,128]{3,2,1,0:T(8,128)} %param.12) | copy-start | bytes 3145732
  0.7 14.1 %copy-start.16 = (f32[1,4]{1,0:T(1,128)S(1)}, f32[1,4]{1,0:T(1,128)}, u32[]{:S(2)}) copy-start(f32[1,4]{1,0:T(1,128)} %param.16) | copy-start | bytes 52
  2.3 19.1 %collective-permute-start.2 = (f32[4,64,128]{2,1,0:T(8,128)}, f32[4,64,128]{2,1,0:T(8,128)}, u32[]{:S(2)}, u32[]{:S(2)}) collective-permute-start(f32[4,64,128]{2,1,0:T(8,128)} %dynamic-slice_bitcast_fusion.9), channel_id=1, source_target_pairs={{0,1},{1,0},{2,3},{3,2},{4,5},{5,4},{6,7},{7,6},{8,9},{9,8},{10,11... | collective-permute-start | bytes 393224 | tf_op jit(solution)/shard_map/ppermute | solution.py:52
  4.6 22.2 %collective-permute-start = (f32[1,16,2048]{2,1,0:T(8,128)}, f32[1,16,2048]{2,1,0:T(8,128)}, u32[]{:S(2)}, u32[]{:S(2)}) collective-permute-start(f32[1,16,2048]{2,1,0:T(8,128)} %concatenate.199), channel_id=1, source_target_pairs={{0,8},{2,10},{4,12},{6,14},{8,0},{10,2},{12,4},{14,6},{1,9},{3,11}... | collective-permute-start | bytes 393224 | tf_op jit(solution)/shard_map/ppermute | solution.py:120
  8.2 12.4 %collective-permute-start.1 = (f32[1,16,64]{2,1,0:T(8,128)}, f32[1,16,64]{2,1,0:T(8,128)}, u32[]{:S(2)}, u32[]{:S(2)}) collective-permute-start(f32[1,16,64]{2,1,0:T(8,128)} %bitcast.246), channel_id=1, source_target_pairs={{0,8},{2,10},{4,12},{6,14},{8,0},{10,2},{12,4},{14,6},{1,9},{3,11}... | collective-permute-start | bytes 12296 | tf_op jit(solution)/shard_map/ppermute | solution.py:120
  28.1 4.2 %collective-permute-start.5 = (f32[2,16,64]{2,1,0:T(8,128)S(1)}, f32[2,16,64]{2,1,0:T(8,128)S(1)}, u32[]{:S(2)}, u32[]{:S(2)}) collective-permute-start(f32[2,16,64]{2,1,0:T(8,128)S(1)} %maximum_select_fusion.12), channel_id=1, source_target_pairs={{0,4},{2,6},{4,0},{6,2},{8,12},{10,14},{12,8},{14,10},{1,5},{3,7},... | collective-permute-start | bytes 24584 | tf_op jit(solution)/shard_map/ppermute | solution.py:120
  30.2 5.1 %collective-permute-start.4 = (f32[2,8,2048]{2,1,0:T(8,128)S(1)}, f32[2,8,2048]{2,1,0:T(8,128)S(1)}, u32[]{:S(2)}, u32[]{:S(2)}) collective-permute-start(f32[2,8,2048]{2,1,0:T(8,128)S(1)} %get-tuple-element.142), channel_id=1, source_target_pairs={{0,2},{2,0},{4,6},{6,4},{8,10},{10,8},{12,14},{14,12},{1,3},{3,1},... | collective-permute-start | bytes 393224 | tf_op jit(solution)/shard_map/ppermute | solution.py:120
  31.8 6.0 %collective-permute-start.6 = (f32[4,64,128]{2,1,0:T(8,128)S(1)}, f32[4,64,128]{2,1,0:T(8,128)S(1)}, u32[]{:S(2)}, u32[]{:S(2)}) collective-permute-start(f32[4,64,128]{2,1,0:T(8,128)S(1)} %constant_dynamic-slice_fusion.5), channel_id=1, source_target_pairs={{0,1},{1,0},{2,3},{3,2},{4,5},{5,4},{6,7},{7,6},{8,9},{9,8},{10,11... | collective-permute-start | bytes 393224 | tf_op jit(solution)/shard_map/ppermute | solution.py:52
  31.8 5.9 %collective-permute-start.3 = (f32[2,8,2048]{2,1,0:T(8,128)S(1)}, f32[2,8,2048]{2,1,0:T(8,128)S(1)}, u32[]{:S(2)}, u32[]{:S(2)}) collective-permute-start(f32[2,8,2048]{2,1,0:T(8,128)S(1)} %get-tuple-element.143), channel_id=1, source_target_pairs={{0,4},{2,6},{4,0},{6,2},{8,12},{10,14},{12,8},{14,10},{1,5},{3,7},... | collective-permute-start | bytes 393224 | tf_op jit(solution)/shard_map/ppermute | solution.py:120
  42.2 5.0 %collective-permute-start.10 = (f32[4,64,128]{2,1,0:T(8,128)S(1)}, f32[4,64,128]{2,1,0:T(8,128)S(1)}, u32[]{:S(2)}, u32[]{:S(2)}) collective-permute-start(f32[4,64,128]{2,1,0:T(8,128)S(1)} %constant_dynamic-slice_fusion.4), channel_id=1, source_target_pairs={{0,1},{1,0},{2,3},{3,2},{4,5},{5,4},{6,7},{7,6},{8,9},{9,8},{10,11... | collective-permute-start | bytes 393224 | tf_op jit(solution)/shard_map/ppermute | solution.py:52
  42.3 4.3 %collective-permute-start.9 = (f32[4,16,64]{2,1,0:T(8,128)S(1)}, f32[4,16,64]{2,1,0:T(8,128)S(1)}, u32[]{:S(2)}, u32[]{:S(2)}) collective-permute-start(f32[4,16,64]{2,1,0:T(8,128)S(1)} %bitcast.239), channel_id=1, source_target_pairs={{0,2},{2,0},{4,6},{6,4},{8,10},{10,8},{12,14},{14,12},{1,3},{3,1},... | collective-permute-start | bytes 49160 | tf_op jit(solution)/shard_map/ppermute | solution.py:120
  43.0 8.4 %collective-permute-start.8 = (f32[4,8,2048]{2,1,0:T(8,128)S(1)}, f32[4,8,2048]{2,1,0:T(8,128)S(1)}, u32[]{:S(2)}, u32[]{:S(2)}) collective-permute-start(f32[4,8,2048]{2,1,0:T(8,128)S(1)} %bitcast.213), channel_id=1, source_target_pairs={{0,4},{2,6},{4,0},{6,2},{8,12},{10,14},{12,8},{14,10},{1,5},{3,7},... | collective-permute-start | bytes 786440 | tf_op jit(solution)/shard_map/ppermute | solution.py:120
  43.4 8.5 %collective-permute-start.7 = (f32[4,8,2048]{2,1,0:T(8,128)S(1)}, f32[4,8,2048]{2,1,0:T(8,128)S(1)}, u32[]{:S(2)}, u32[]{:S(2)}) collective-permute-start(f32[4,8,2048]{2,1,0:T(8,128)S(1)} %bitcast.215), channel_id=1, source_target_pairs={{0,2},{2,0},{4,6},{6,4},{8,10},{10,8},{12,14},{14,12},{1,3},{3,1},... | collective-permute-start | bytes 786440 | tf_op jit(solution)/shard_map/ppermute | solution.py:120
  57.1 3.4 %collective-permute-start.13 = (f32[4,64,128]{2,1,0:T(8,128)S(1)}, f32[4,64,128]{2,1,0:T(8,128)S(1)}, u32[]{:S(2)}, u32[]{:S(2)}) collective-permute-start(f32[4,64,128]{2,1,0:T(8,128)S(1)} %constant_dynamic-slice_fusion.3), channel_id=1, source_target_pairs={{0,1},{1,0},{2,3},{3,2},{4,5},{5,4},{6,7},{7,6},{8,9},{9,8},{10,11... | collective-permute-start | bytes 393224 | tf_op jit(solution)/shard_map/ppermute | solution.py:52
  57.3 8.8 %collective-permute-start.12 = (f32[2,2,4,32,128]{4,3,2,1,0:T(8,128)S(1)}, f32[2,2,4,32,128]{4,3,2,1,0:T(8,128)S(1)}, u32[]{:S(2)}, u32[]{:S(2)}) collective-permute-start(f32[2,2,4,32,128]{4,3,2,1,0:T(8,128)S(1)} %dynamic-slice_bitcast_fusion.3), channel_id=1, source_target_pairs={{0,4},{2,6},{4,0},{6,2},{8,12},{10,14},{12,8},{14,10},{1,5},{3,7},... | collective-permute-start | bytes 786440 | tf_op jit(solution)/shard_map/ppermute | solution.py:169
  58.7 8.5 %collective-permute-start.11 = (f32[4,1,4,32,128]{4,3,2,0,1:T(8,128)S(1)}, f32[4,1,4,32,128]{4,3,2,0,1:T(8,128)S(1)}, u32[]{:S(2)}, u32[]{:S(2)}) collective-permute-start(f32[4,1,4,32,128]{4,3,2,0,1:T(8,128)S(1)} %dynamic-slice_bitcast_fusion.4), channel_id=1, source_target_pairs={{0,2},{2,0},{4,6},{6,4},{8,10},{10,8},{12,14},{14,12},{1,3},{3,1},... | collective-permute-start | bytes 786440 | tf_op jit(solution)/shard_map/ppermute | solution.py:169
  67.3 5.2 %collective-permute-start.18 = (f32[4,64,128]{2,1,0:T(8,128)S(1)}, f32[4,64,128]{2,1,0:T(8,128)S(1)}, u32[]{:S(2)}, u32[]{:S(2)}) collective-permute-start(f32[4,64,128]{2,1,0:T(8,128)S(1)} %constant_dynamic-slice_fusion.2), channel_id=1, source_target_pairs={{0,1},{1,0},{2,3},{3,2},{4,5},{5,4},{6,7},{7,6},{8,9},{9,8},{10,11... | collective-permute-start | bytes 393224 | tf_op jit(solution)/shard_map/ppermute | solution.py:52
  67.4 8.4 %collective-permute-start.17 = (f32[2,1,4,32,128]{4,3,2,0,1:T(8,128)S(1)}, f32[2,1,4,32,128]{4,3,2,0,1:T(8,128)S(1)}, u32[]{:S(2)}, u32[]{:S(2)}) collective-permute-start(f32[2,1,4,32,128]{4,3,2,0,1:T(8,128)S(1)} %dynamic-slice_bitcast_fusion.7), channel_id=1, source_target_pairs={{0,2},{2,0},{4,6},{6,4},{8,10},{10,8},{12,14},{14,12},{1,3},{3,1},... | collective-permute-start | bytes 393224 | tf_op jit(solution)/shard_map/ppermute | solution.py:169
  69.0 6.8 %collective-permute-start.16 = (f32[2,1,4,32,128]{4,3,2,0,1:T(8,128)S(1)}, f32[2,1,4,32,128]{4,3,2,0,1:T(8,128)S(1)}, u32[]{:S(2)}, u32[]{:S(2)}) collective-permute-start(f32[2,1,4,32,128]{4,3,2,0,1:T(8,128)S(1)} %dynamic-slice_bitcast_fusion.8), channel_id=1, source_target_pairs={{0,4},{2,6},{4,0},{6,2},{8,12},{10,14},{12,8},{14,10},{1,5},{3,7},... | collective-permute-start | bytes 393224 | tf_op jit(solution)/shard_map/ppermute | solution.py:169
  70.0 10.2 %collective-permute-start.15 = (f32[2,2,4,32,128]{4,3,2,1,0:T(8,128)S(1)}, f32[2,2,4,32,128]{4,3,2,1,0:T(8,128)S(1)}, u32[]{:S(2)}, u32[]{:S(2)}) collective-permute-start(f32[2,2,4,32,128]{4,3,2,1,0:T(8,128)S(1)} %dynamic-slice_bitcast_fusion.1), channel_id=1, source_target_pairs={{0,4},{2,6},{4,0},{6,2},{8,12},{10,14},{12,8},{14,10},{1,5},{3,7},... | collective-permute-start | bytes 786440 | tf_op jit(solution)/shard_map/ppermute | solution.py:169
  71.7 8.6 %collective-permute-start.14 = (f32[4,1,4,32,128]{4,3,2,0,1:T(8,128)S(1)}, f32[4,1,4,32,128]{4,3,2,0,1:T(8,128)S(1)}, u32[]{:S(2)}, u32[]{:S(2)}) collective-permute-start(f32[4,1,4,32,128]{4,3,2,0,1:T(8,128)S(1)} %dynamic-slice_bitcast_fusion.2), channel_id=1, source_target_pairs={{0,2},{2,0},{4,6},{6,4},{8,10},{10,8},{12,14},{14,12},{1,3},{3,1},... | collective-permute-start | bytes 786440 | tf_op jit(solution)/shard_map/ppermute | solution.py:169
  80.4 5.0 %collective-permute-start.20 = (f32[2,1,4,32,128]{4,3,2,0,1:T(8,128)S(1)}, f32[2,1,4,32,128]{4,3,2,0,1:T(8,128)S(1)}, u32[]{:S(2)}, u32[]{:S(2)}) collective-permute-start(f32[2,1,4,32,128]{4,3,2,0,1:T(8,128)S(1)} %dynamic-slice_bitcast_fusion.5), channel_id=1, source_target_pairs={{0,2},{2,0},{4,6},{6,4},{8,10},{10,8},{12,14},{14,12},{1,3},{3,1},... | collective-permute-start | bytes 393224 | tf_op jit(solution)/shard_map/ppermute | solution.py:169
  81.0 5.0 %collective-permute-start.19 = (f32[2,1,4,32,128]{4,3,2,0,1:T(8,128)S(1)}, f32[2,1,4,32,128]{4,3,2,0,1:T(8,128)S(1)}, u32[]{:S(2)}, u32[]{:S(2)}) collective-permute-start(f32[2,1,4,32,128]{4,3,2,0,1:T(8,128)S(1)} %dynamic-slice_bitcast_fusion.6), channel_id=1, source_target_pairs={{0,4},{2,6},{4,0},{6,2},{8,12},{10,14},{12,8},{14,10},{1,5},{3,7},... | collective-permute-start | bytes 393224 | tf_op jit(solution)/shard_map/ppermute | solution.py:169
  86.1 13.0 %collective-permute-start.21 = (f32[1,1,8,64,128]{4,3,2,1,0:T(8,128)S(1)}, f32[1,1,8,64,128]{4,3,2,1,0:T(8,128)S(1)}, u32[]{:S(2)}, u32[]{:S(2)}) collective-permute-start(f32[1,1,8,64,128]{4,3,2,1,0:T(8,128)S(1)} %dynamic-slice_bitcast_fusion), channel_id=1, source_target_pairs={{0,8},{2,10},{4,12},{6,14},{8,0},{10,2},{12,4},{14,6},{1,9},{3,11}... | collective-permute-start | bytes 786440 | tf_op jit(solution)/shard_map/ppermute | solution.py:169
  100.9 8.4 %collective-permute-start.22 = (f32[1,4,64,128]{3,2,1,0:T(8,128)S(1)}, f32[1,4,64,128]{3,2,1,0:T(8,128)S(1)}, u32[]{:S(2)}, u32[]{:S(2)}) collective-permute-start(f32[1,4,64,128]{3,2,1,0:T(8,128)S(1)} %fusion.1), channel_id=1, source_target_pairs={{0,8},{2,10},{4,12},{6,14},{8,0},{10,2},{12,4},{14,6},{1,9},{3,11}... | collective-permute-start | bytes 393224 | tf_op jit(solution)/shard_map/ppermute | solution.py:120
  109.4 5.5 %collective-permute-start.24 = (f32[2,4,32,128]{3,2,1,0:T(8,128)S(1)}, f32[2,4,32,128]{3,2,1,0:T(8,128)S(1)}, u32[]{:S(2)}, u32[]{:S(2)}) collective-permute-start(f32[2,4,32,128]{3,2,1,0:T(8,128)S(1)} %get-tuple-element.138), channel_id=1, source_target_pairs={{0,2},{2,0},{4,6},{6,4},{8,10},{10,8},{12,14},{14,12},{1,3},{3,1},... | collective-permute-start | bytes 393224 | tf_op jit(solution)/shard_map/ppermute | solution.py:120
  110.5 5.0 %collective-permute-start.23 = (f32[2,4,32,128]{3,2,1,0:T(8,128)S(1)}, f32[2,4,32,128]{3,2,1,0:T(8,128)S(1)}, u32[]{:S(2)}, u32[]{:S(2)}) collective-permute-start(f32[2,4,32,128]{3,2,1,0:T(8,128)S(1)} %get-tuple-element.139), channel_id=1, source_target_pairs={{0,4},{2,6},{4,0},{6,2},{8,12},{10,14},{12,8},{14,10},{1,5},{3,7},... | collective-permute-start | bytes 393224 | tf_op jit(solution)/shard_map/ppermute | solution.py:120
  115.5 7.2 %collective-permute-start.26 = (f32[4,4,32,128]{3,2,1,0:T(8,128)S(1)}, f32[4,4,32,128]{3,2,1,0:T(8,128)S(1)}, u32[]{:S(2)}, u32[]{:S(2)}) collective-permute-start(f32[4,4,32,128]{3,2,1,0:T(8,128)S(1)} %bitcast.221), channel_id=1, source_target_pairs={{0,4},{2,6},{4,0},{6,2},{8,12},{10,14},{12,8},{14,10},{1,5},{3,7},... | collective-permute-start | bytes 786440 | tf_op jit(solution)/shard_map/ppermute | solution.py:120
  115.8 6.8 %collective-permute-start.25 = (f32[4,4,32,128]{3,2,1,0:T(8,128)S(1)}, f32[4,4,32,128]{3,2,1,0:T(8,128)S(1)}, u32[]{:S(2)}, u32[]{:S(2)}) collective-permute-start(f32[4,4,32,128]{3,2,1,0:T(8,128)S(1)} %bitcast.227), channel_id=1, source_target_pairs={{0,2},{2,0},{4,6},{6,4},{8,10},{10,8},{12,14},{14,12},{1,3},{3,1},... | collective-permute-start | bytes 786440 | tf_op jit(solution)/shard_map/ppermute | solution.py:120
  124.9 1.6 %collective-permute-start.27 = (f32[4,64,128]{2,1,0:T(8,128)}, f32[4,64,128]{2,1,0:T(8,128)S(1)}, u32[]{:S(2)}, u32[]{:S(2)}) collective-permute-start(f32[4,64,128]{2,1,0:T(8,128)} %constant_dynamic-slice_fusion), channel_id=1, source_target_pairs={{0,1},{1,0},{2,3},{3,2},{4,5},{5,4},{6,7},{7,6},{8,9},{9,8},{10,11... | collective-permute-start | bytes 393224 | tf_op jit(solution)/shard_map/ppermute | solution.py:52
  131.6 1.9 %collective-permute-start.28 = (f32[1,2,256]{2,1,0:T(2,128)S(1)}, f32[1,2,256]{2,1,0:T(2,128)S(1)}, u32[]{:S(2)}, u32[]{:S(2)}) collective-permute-start(f32[1,2,256]{2,1,0:T(2,128)S(1)} %maximum_bitcast_fusion), channel_id=1, source_target_pairs={{0,1},{1,0},{2,3},{3,2},{4,5},{5,4},{6,7},{7,6},{8,9},{9,8},{10,11... | collective-permute-start | bytes 6152 | tf_op jit(solution)/shard_map/ppermute | solution.py:345
  (19 other events, 78.0 us)

commit v9 on v8

--- a/solution.py
+++ b/solution.py
@@ -298,21 +298,29 @@
     image_a = chain(image_a, "rs", near_first[:-1], near_first)
     image_b = chain(image_b, "rs", swap_first(near_first[:-1]), near_first)
     tasks = [task_wave(3)]
+    light_c = None
     for i in range(len(bits) - 1):
-        run_group([image_a, image_b, light_a, light_b], tasks[i] if i < len(tasks) else nothing)
+        group = [image_a, image_b]
+        if light_a["i"] < len(light_a["order"]):
+            group += [light_a, light_b]
+        elif light_c is None:
+            light_c = chain(
+                jnp.concatenate([light_a["held"], light_b["held"]], axis=2), "rs", near_first[-1:], near_first[-1:]
+            )
+            group.append(light_c)
+        run_group(group, tasks[i] if i < len(tasks) else nothing)
     for i in range(len(bits) - 1, len(tasks)):
         tasks[i]()
-    both = jnp.concatenate(
-        [
-            jnp.concatenate([image_a["held"], image_b["held"]], axis=2),
-            jnp.concatenate([light_a["held"], light_b["held"]], axis=2),
-        ],
-        axis=1,
-    )
-    last = chain(both, "rs", near_first[-1:], near_first[-1:])
-    run_group([last], nothing)
-    image_part = last["held"][0, :slab]
-    light_part = last["held"][0, slab:]
+    if light_c is None:
+        light_c = chain(
+            jnp.concatenate([light_a["held"], light_b["held"]], axis=2), "rs", near_first[-1:], near_first[-1:]
+        )
+    last = chain(
+        jnp.concatenate([image_a["held"], image_b["held"]], axis=2), "rs", near_first[-1:], near_first[-1:]
+    )
+    run_group([last, light_c], nothing)
+    image_part = last["held"][0]
+    light_part = light_c["held"][0]
 
     table_all = gains_held.reshape(n_shot * gains.shape[0], gains.shape[1])
     filt_part = lateral_filter(image_part / (light_part + eps), table_all)

time: 135 us -> 133 us (0.985)
  waiting for transfers between devices: 47.7 us -> 46 us
    ppermute x9 -> x10, waiting for transfers between devices: 22.7 us -> 21.3 us  [rs_step(): got = lax.ppermute(send, 'shot', [(i, i ^ k) for i in range(n)])]
    unnamed x45 -> x47, local copies, waits for them, and re-layouts: 3.56 us -> 3.65 us
    ppermute x9 -> x10, starting transfers between devices: 11.3 us -> 11.4 us  [rs_step(): got = lax.ppermute(send, 'shot', [(i, i ^ k) for i in range(n)])]
  transfers between devices with their start and end apart: 29 -> 30, of which waited for: 16 -> 16; matrix products, arithmetic and copies ran while one was open for 25% -> 25% of each run, Pallas kernels for 0% -> 0%
where the time goes in v9:
time: 133 us; the launch traced here: 132 us
  waiting for transfers between devices  46 us (35%)
  other arithmetic  36.9 us (28%)
  starting transfers between devices  25 us (19%)
  local copies, waits for them, and re-layouts  17.4 us (13%)
  between operations  4.92 us (4%)
  matrix products  1.7 us (1%)
    ppermute x13, waiting for transfers between devices, ag_step(): theirs = lax.ppermute(held, 'shot', [(i, i ^ k) for i in range(n)])  24.1 us
    ppermute x10, waiting for transfers between devices, rs_step(): got = lax.ppermute(send, 'shot', [(i, i ^ k) for i in range(n)])  21.3 us
    ppermute x13, starting transfers between devices, ag_step(): theirs = lax.ppermute(held, 'shot', [(i, i ^ k) for i in range(n)])  12.4 us
    add x3, other arithmetic, inject(): return field + jnp.where(hit, source_gain[0] * wavelet[0, moment], 0.0)  11.6 us
    ppermute x10, starting transfers between devices, rs_step(): got = lax.ppermute(send, 'shot', [(i, i ^ k) for i in range(n)])  11.4 us
    add x2, other arithmetic, born_second(): 2.0 * born + speed_term * laplace_x(with_halo(born)) - absorber * born  5.85 us
    another operation x1, other arithmetic, damping(): lower = jnp.stack([edges[0], edges[2], edges[4]])[:, None]  3.92 us
    unnamed x47, local copies, waits for them, and re-layouts  3.65 us
  transfers between devices with their start and end apart: 30, of which 16 were waited for; matrix products, arithmetic and copies ran while one was open for 25% of the time, Pallas kernels for 0%

profile of v9, /device:TPU:0, one launch (start us, length us, event | category | flops | bytes accessed | tf_op | source)
XLA Modules:
  0.0 132.0 jit_solution(5849483923818614190)
XLA Ops:
  0.7 1.7 %dynamic-slice_bitcast_fusion.10 = f32[4,64,128]{2,1,0:T(8,128)} fusion(f32[1,32,64,128]{3,2,1,0:T(8,128)} %param.12, s32[]{:T(128)S(6)} %select_n.404), kind=kLoop, calls=%fused_computation.359 | loop fusion | bytes 262148 | tf_op jit(solution)/shard_map/dynamic_slice | solution.py:51
  4.6 3.6 %collective-permute-start = (f32[1,16,2048]{2,1,0:T(8,128)}, f32[1,16,2048]{2,1,0:T(8,128)}, u32[]{:S(2)}, u32[]{:S(2)}) collective-permute-start(f32[1,16,2048]{2,1,0:T(8,128)} %concatenate.196), channel_id=1, source_target_pairs={{0,8},{2,10},{4,12},{6,14},{8,0},{10,2},{12,4},{14,6},{1,9},{3,11}... | collective-permute-start | bytes 393224 | tf_op jit(solution)/shard_map/ppermute | solution.py:120
  10.2 3.9 %pad_maximum_fusion.15 = (f32[3]{0:T(128)S(1)}, f32[3]{0:T(128)S(1)}) fusion(f32[1]{0:T(128)} %get-tuple-element.155, f32[1]{0:T(128)} %get-tuple-element.156, f32[1]{0:T(128)} %get-tuple-element.151, f32[1]{0:T(128)} %get-tuple-element.152, f32[1]{0:T(128)} %get-tuple-element.153, f32[1]{0:T(128)} %get-tuple-element.154), kind=kLoop, calls=%fused_computation.416 | loop fusion | flops 12 | bytes 48 | tf_op jit(solution)/shard_map/stack | solution.py:37
  22.5 4.5 %fusion.2 = (f32[32,64,128]{2,1,0:T(8,128)S(1)}, f32[32,64,128]{2,1,0:T(8,128)S(1)}) fusion(f32[]{:T(128)S(6)} %mul.319, f32[128]{0:T(128)} %slice_bitcast_fusion, f32[32,64]{1,0:T(8,128)S(1)} %broadcast_add_fusion, pred[128]{0:T(512)(128)(4,1)} %iota_compare_fusion.1, pred[32,64]{1,0:T(8,128)(4,1)} %broadcast_and_fusion, f32[1,32,64,128]{3,2,1,0:T(8,128)} %param.11, ...), kind=kLoop, calls=%fused_computation.118 | loop fusion | flops 12058624 | bytes 16009860 | tf_op jit(solution)/shard_map/add | solution.py:213
  28.3 1.9 %collective-permute-start.5 = (f32[2,16,64]{2,1,0:T(8,128)S(1)}, f32[2,16,64]{2,1,0:T(8,128)S(1)}, u32[]{:S(2)}, u32[]{:S(2)}) collective-permute-start(f32[2,16,64]{2,1,0:T(8,128)S(1)} %maximum_select_fusion.12), channel_id=1, source_target_pairs={{0,4},{2,6},{4,0},{6,2},{8,12},{10,14},{12,8},{14,10},{1,5},{3,7},... | collective-permute-start | bytes 24584 | tf_op jit(solution)/shard_map/ppermute | solution.py:120
  30.3 1.6 %collective-permute-start.4 = (f32[2,8,2048]{2,1,0:T(8,128)S(1)}, f32[2,8,2048]{2,1,0:T(8,128)S(1)}, u32[]{:S(2)}, u32[]{:S(2)}) collective-permute-start(f32[2,8,2048]{2,1,0:T(8,128)S(1)} %get-tuple-element.144), channel_id=1, source_target_pairs={{0,2},{2,0},{4,6},{6,4},{8,10},{10,8},{12,14},{14,12},{1,3},{3,1},... | collective-permute-start | bytes 393224 | tf_op jit(solution)/shard_map/ppermute | solution.py:120
  32.5 2.9 %collective-permute-done.4 = f32[2,8,2048]{2,1,0:T(8,128)S(1)} collective-permute-done((f32[2,8,2048]{2,1,0:T(8,128)S(1)}, f32[2,8,2048]{2,1,0:T(8,128)S(1)}, u32[]{:S(2)}, u32[]{:S(2)}) %collective-permute-start.4) | collective-permute-done | bytes 131104 | tf_op jit(solution)/shard_map/ppermute | solution.py:120
  35.5 2.4 %collective-permute-done.3 = f32[2,8,2048]{2,1,0:T(8,128)S(1)} collective-permute-done((f32[2,8,2048]{2,1,0:T(8,128)S(1)}, f32[2,8,2048]{2,1,0:T(8,128)S(1)}, u32[]{:S(2)}, u32[]{:S(2)}) %collective-permute-start.3) | collective-permute-done | bytes 131104 | tf_op jit(solution)/shard_map/ppermute | solution.py:120
  38.0 3.2 %fusion.3 = (f32[32,64,128]{2,1,0:T(8,128)S(1)}, f32[32,64,128]{2,1,0:T(8,128)S(1)}) fusion(f32[32,64,128]{2,1,0:T(8,128)S(1)} %get-tuple-element.70, f32[32,64,128]{2,1,0:T(8,128)S(1)} %bitcast.200, f32[]{:T(128)S(6)} %mul.330, f32[128]{0:T(128)S(1)} %copy-done.12, f32[32,64]{1,0:T(8,128)S(1)} %broadcast_add_fusion, pred[128]{0:T(512)(128)(4,1)S(1)} %copy-done.15, ...), kind=kLoop, calls=%fused_computation.119 | loop fusion | flops 12058624 | bytes 16012292 | tf_op jit(solution)/shard_map/add | solution.py:213
  41.2 1.2 multiply_add_fusion.1
  43.5 1.7 %collective-permute-start.7 = (f32[4,8,2048]{2,1,0:T(8,128)S(1)}, f32[4,8,2048]{2,1,0:T(8,128)S(1)}, u32[]{:S(2)}, u32[]{:S(2)}) collective-permute-start(f32[4,8,2048]{2,1,0:T(8,128)S(1)} %bitcast.223), channel_id=1, source_target_pairs={{0,2},{2,0},{4,6},{6,4},{8,10},{10,8},{12,14},{14,12},{1,3},{3,1},... | collective-permute-start | bytes 786440 | tf_op jit(solution)/shard_map/ppermute | solution.py:120
  45.2 1.5 %collective-permute-done.9 = f32[4,16,64]{2,1,0:T(8,128)S(1)} collective-permute-done((f32[4,16,64]{2,1,0:T(8,128)S(1)}, f32[4,16,64]{2,1,0:T(8,128)S(1)}, u32[]{:S(2)}, u32[]{:S(2)}) %collective-permute-start.9) | collective-permute-done | bytes 16416 | tf_op jit(solution)/shard_map/ppermute | solution.py:120
  47.4 4.0 %fusion.4 = (f32[32,64,128]{2,1,0:T(8,128)}, f32[32,64,128]{2,1,0:T(8,128)}) fusion(f32[32,64,128]{2,1,0:T(8,128)S(1)} %get-tuple-element.68, f32[32,64,128]{2,1,0:T(8,128)S(1)} %get-tuple-element.70, f32[]{:T(128)S(6)} %mul.339, f32[128]{0:T(128)S(1)} %copy-done.12, f32[32,64]{1,0:T(8,128)S(1)} %broadcast_add_fusion, pred[128]{0:T(512)(128)(4,1)S(1)} %copy-done.15, ...), kind=kLoop, calls=%fused_computation.120 | loop fusion | flops 12058624 | bytes 16012292 | tf_op jit(solution)/shard_map/add | solution.py:213
  53.2 2.5 %copy.46 = f32[2048,128]{1,0:T(8,128)} copy(f32[2048,128]{0,1:T(8,128)} %bitcast.208) | data formatting | bytes 2097152 | tf_op jit(solution)/shard_map/transpose | solution.py:289
  55.7 1.4 %mul.340 = f32[32,64,128]{2,1,0:T(8,128)S(1)} multiply(f32[32,64,128]{2,1,0:T(8,128)} %bitcast.202, f32[32,64,128]{2,1,0:T(8,128)S(1)} %get-tuple-element.78) | non-fusion elementwise | flops 262144 | bytes 3145728 | tf_op jit(solution)/shard_map/mul | solution.py:290
  57.4 1.4 %collective-permute-start.12 = (f32[2,2,4,32,128]{4,3,2,1,0:T(8,128)S(1)}, f32[2,2,4,32,128]{4,3,2,1,0:T(8,128)S(1)}, u32[]{:S(2)}, u32[]{:S(2)}) collective-permute-start(f32[2,2,4,32,128]{4,3,2,1,0:T(8,128)S(1)} %dynamic-slice_bitcast_fusion.2), channel_id=1, source_target_pairs={{0,4},{2,6},{4,0},{6,2},{8,12},{10,14},{12,8},{14,10},{1,5},{3,7},... | collective-permute-start | bytes 786440 | tf_op jit(solution)/shard_map/ppermute | solution.py:169
  58.9 1.6 %collective-permute-start.11 = (f32[4,1,4,32,128]{4,3,2,0,1:T(8,128)S(1)}, f32[4,1,4,32,128]{4,3,2,0,1:T(8,128)S(1)}, u32[]{:S(2)}, u32[]{:S(2)}) collective-permute-start(f32[4,1,4,32,128]{4,3,2,0,1:T(8,128)S(1)} %dynamic-slice_bitcast_fusion.3), channel_id=1, source_target_pairs={{0,2},{2,0},{4,6},{6,4},{8,10},{10,8},{12,14},{14,12},{1,3},{3,1},... | collective-permute-start | bytes 786440 | tf_op jit(solution)/shard_map/ppermute | solution.py:169
  60.7 2.9 %fusion.92 = f32[32,64,128]{2,1,0:T(8,128)S(1)} fusion(f32[40,64,128]{2,1,0:T(8,128)S(1)} %constant_dynamic-update-slice_fusion.2, f32[32,64,128]{2,1,0:T(8,128)S(1)} %bitcast.203, f32[32,64,128]{2,1,0:T(8,128)S(1)} %get-tuple-element.80, f32[32,64,128]{2,1,0:T(8,128)S(1)} %mul.340, f32[128]{0:T(128)S(1)} %copy-done.13, f32[32,64]{1,0:T(8,128)S(1)} %broadcast_add_fusion, ...), kind=kLoop, calls=%fused_computation.208 | loop fusion | flops 11272192 | bytes 16007680 | tf_op jit(solution)/shard_map/add | solution.py:224
  63.6 2.6 %collective-permute-done.12 = f32[2,2,4,32,128]{4,3,2,1,0:T(8,128)S(1)} collective-permute-done((f32[2,2,4,32,128]{4,3,2,1,0:T(8,128)S(1)}, f32[2,2,4,32,128]{4,3,2,1,0:T(8,128)S(1)}, u32[]{:S(2)}, u32[]{:S(2)}) %collective-permute-start.12) | collective-permute-done | bytes 262176 | tf_op jit(solution)/shard_map/ppermute | solution.py:169
  67.5 1.6 %collective-permute-start.17 = (f32[2,1,4,32,128]{4,3,2,0,1:T(8,128)S(1)}, f32[2,1,4,32,128]{4,3,2,0,1:T(8,128)S(1)}, u32[]{:S(2)}, u32[]{:S(2)}) collective-permute-start(f32[2,1,4,32,128]{4,3,2,0,1:T(8,128)S(1)} %dynamic-slice_bitcast_fusion.8), channel_id=1, source_target_pairs={{0,2},{2,0},{4,6},{6,4},{8,10},{10,8},{12,14},{14,12},{1,3},{3,1},... | collective-permute-start | bytes 393224 | tf_op jit(solution)/shard_map/ppermute | solution.py:169
  70.2 1.6 %collective-permute-start.15 = (f32[2,2,4,32,128]{4,3,2,1,0:T(8,128)S(1)}, f32[2,2,4,32,128]{4,3,2,1,0:T(8,128)S(1)}, u32[]{:S(2)}, u32[]{:S(2)}) collective-permute-start(f32[2,2,4,32,128]{4,3,2,1,0:T(8,128)S(1)} %dynamic-slice_bitcast_fusion), channel_id=1, source_target_pairs={{0,4},{2,6},{4,0},{6,2},{8,12},{10,14},{12,8},{14,10},{1,5},{3,7},... | collective-permute-start | bytes 786440 | tf_op jit(solution)/shard_map/ppermute | solution.py:169
  72.6 3.2 %fusion.117 = f32[32,64,128]{2,1,0:T(8,128)} fusion(f32[40,64,128]{2,1,0:T(8,128)S(1)} %constant_dynamic-update-slice_fusion.1, s32[32,64,128]{2,1,0:T(8,128)S(1)} %copy-done), kind=kLoop, calls=%fused_computation.233 | loop fusion | flops 9175040 | bytes 12845056 | tf_op jit(solution)/shard_map/mul | solution.py:216
  75.9 4.5 %collective-permute-done.15 = f32[2,2,4,32,128]{4,3,2,1,0:T(8,128)S(1)} collective-permute-done((f32[2,2,4,32,128]{4,3,2,1,0:T(8,128)S(1)}, f32[2,2,4,32,128]{4,3,2,1,0:T(8,128)S(1)}, u32[]{:S(2)}, u32[]{:S(2)}) %collective-permute-start.15) | collective-permute-done | bytes 262176 | tf_op jit(solution)/shard_map/ppermute | solution.py:169
  81.2 2.7 %collective-permute-start.21 = (f32[1,1,4,64,128]{4,3,2,1,0:T(8,128)S(1)}, f32[1,1,4,64,128]{4,3,2,1,0:T(8,128)S(1)}, u32[]{:S(2)}, u32[]{:S(2)}) collective-permute-start(f32[1,1,4,64,128]{4,3,2,1,0:T(8,128)S(1)} %dynamic-slice_bitcast_fusion.5), channel_id=1, source_target_pairs={{0,8},{2,10},{4,12},{6,14},{8,0},{10,2},{12,4},{14,6},{1,9},{3,11}... | collective-permute-start | bytes 393224 | tf_op jit(solution)/shard_map/ppermute | solution.py:169
  85.6 5.1 %collective-permute-done.19 = f32[2,1,4,32,128]{4,3,2,0,1:T(8,128)S(1)} collective-permute-done((f32[2,1,4,32,128]{4,3,2,0,1:T(8,128)S(1)}, f32[2,1,4,32,128]{4,3,2,0,1:T(8,128)S(1)}, u32[]{:S(2)}, u32[]{:S(2)}) %collective-permute-start.19) | collective-permute-done | bytes 131104 | tf_op jit(solution)/shard_map/ppermute | solution.py:169
  91.0 7.1 %collective-permute-done.22 = f32[1,1,4,64,128]{4,3,2,1,0:T(8,128)S(1)} collective-permute-done((f32[1,1,4,64,128]{4,3,2,1,0:T(8,128)S(1)}, f32[1,1,4,64,128]{4,3,2,1,0:T(8,128)S(1)}, u32[]{:S(2)}, u32[]{:S(2)}) %collective-permute-start.22) | collective-permute-done | bytes 131104 | tf_op jit(solution)/shard_map/ppermute | solution.py:169
  100.0 6.1 %collective-permute-done.23 = f32[1,4,64,128]{3,2,1,0:T(8,128)S(1)} collective-permute-done((f32[1,4,64,128]{3,2,1,0:T(8,128)S(1)}, f32[1,4,64,128]{3,2,1,0:T(8,128)S(1)}, u32[]{:S(2)}, u32[]{:S(2)}) %collective-permute-start.23) | collective-permute-done | bytes 131104 | tf_op jit(solution)/shard_map/ppermute | solution.py:120
  106.1 1.4 %collective-permute-start.25 = (f32[2,4,32,128]{3,2,1,0:T(8,128)S(1)}, f32[2,4,32,128]{3,2,1,0:T(8,128)S(1)}, u32[]{:S(2)}, u32[]{:S(2)}) collective-permute-start(f32[2,4,32,128]{3,2,1,0:T(8,128)S(1)} %get-tuple-element.140), channel_id=1, source_target_pairs={{0,2},{2,0},{4,6},{6,4},{8,10},{10,8},{12,14},{14,12},{1,3},{3,1},... | collective-permute-start | bytes 393224 | tf_op jit(solution)/shard_map/ppermute | solution.py:120
  108.1 3.1 %collective-permute-done.25 = f32[2,4,32,128]{3,2,1,0:T(8,128)S(1)} collective-permute-done((f32[2,4,32,128]{3,2,1,0:T(8,128)S(1)}, f32[2,4,32,128]{3,2,1,0:T(8,128)S(1)}, u32[]{:S(2)}, u32[]{:S(2)}) %collective-permute-start.25) | collective-permute-done | bytes 131104 | tf_op jit(solution)/shard_map/ppermute | solution.py:120
  111.2 2.7 %collective-permute-done.24 = f32[2,4,32,128]{3,2,1,0:T(8,128)S(1)} collective-permute-done((f32[2,4,32,128]{3,2,1,0:T(8,128)S(1)}, f32[2,4,32,128]{3,2,1,0:T(8,128)S(1)}, u32[]{:S(2)}, u32[]{:S(2)}) %collective-permute-start.24) | collective-permute-done | bytes 131104 | tf_op jit(solution)/shard_map/ppermute | solution.py:120
  115.8 4.8 %collective-permute-done.26 = f32[4,4,32,128]{3,2,1,0:T(8,128)S(1)} collective-permute-done((f32[4,4,32,128]{3,2,1,0:T(8,128)S(1)}, f32[4,4,32,128]{3,2,1,0:T(8,128)S(1)}, u32[]{:S(2)}, u32[]{:S(2)}) %collective-permute-start.26) | collective-permute-done | bytes 262176 | tf_op jit(solution)/shard_map/ppermute | solution.py:120
  125.2 2.9 %fusion.145 = f32[32,64,128]{2,1,0:T(8,128)S(1)} fusion(f32[40,64,128]{2,1,0:T(8,128)S(1)} %constant_dynamic-update-slice_fusion, f32[32,64,128]{2,1,0:T(8,128)S(1)} %copy-done.7, f32[128]{0:T(128)S(1)} %copy-done.14, f32[32,64]{1,0:T(8,128)S(1)} %broadcast_add_fusion, f32[8,4,64,128]{3,2,1,0:T(8,128)S(1)} %pad_maximum_fusion.13, ...), kind=kLoop, calls=%fused_computation.261 | loop fusion | flops 11534336 | bytes 16007680 | tf_op jit(solution)/shard_map/add | solution.py:224
  (189 shorter events, 33.7 us)
Async XLA Ops:
  0.6 15.6 %copy-start.1 = (f32[1,32,64,128]{3,2,1,0:T(8,128)S(1)}, f32[1,32,64,128]{3,2,1,0:T(8,128)}, u32[]{:S(2)}) copy-start(f32[1,32,64,128]{3,2,1,0:T(8,128)} %param.12) | copy-start | bytes 3145732
  0.7 14.2 %copy-start.16 = (f32[1,4]{1,0:T(1,128)S(1)}, f32[1,4]{1,0:T(1,128)}, u32[]{:S(2)}) copy-start(f32[1,4]{1,0:T(1,128)} %param.16) | copy-start | bytes 52
  2.3 19.2 %collective-permute-start.2 = (f32[4,64,128]{2,1,0:T(8,128)}, f32[4,64,128]{2,1,0:T(8,128)}, u32[]{:S(2)}, u32[]{:S(2)}) collective-permute-start(f32[4,64,128]{2,1,0:T(8,128)} %dynamic-slice_bitcast_fusion.10), channel_id=1, source_target_pairs={{0,1},{1,0},{2,3},{3,2},{4,5},{5,4},{6,7},{7,6},{8,9},{9,8},{10,11... | collective-permute-start | bytes 393224 | tf_op jit(solution)/shard_map/ppermute | solution.py:52
  4.6 22.4 %collective-permute-start = (f32[1,16,2048]{2,1,0:T(8,128)}, f32[1,16,2048]{2,1,0:T(8,128)}, u32[]{:S(2)}, u32[]{:S(2)}) collective-permute-start(f32[1,16,2048]{2,1,0:T(8,128)} %concatenate.196), channel_id=1, source_target_pairs={{0,8},{2,10},{4,12},{6,14},{8,0},{10,2},{12,4},{14,6},{1,9},{3,11}... | collective-permute-start | bytes 393224 | tf_op jit(solution)/shard_map/ppermute | solution.py:120
  8.2 12.6 %collective-permute-start.1 = (f32[1,16,64]{2,1,0:T(8,128)}, f32[1,16,64]{2,1,0:T(8,128)}, u32[]{:S(2)}, u32[]{:S(2)}) collective-permute-start(f32[1,16,64]{2,1,0:T(8,128)} %bitcast.254), channel_id=1, source_target_pairs={{0,8},{2,10},{4,12},{6,14},{8,0},{10,2},{12,4},{14,6},{1,9},{3,11}... | collective-permute-start | bytes 12296 | tf_op jit(solution)/shard_map/ppermute | solution.py:120
  28.3 4.2 %collective-permute-start.5 = (f32[2,16,64]{2,1,0:T(8,128)S(1)}, f32[2,16,64]{2,1,0:T(8,128)S(1)}, u32[]{:S(2)}, u32[]{:S(2)}) collective-permute-start(f32[2,16,64]{2,1,0:T(8,128)S(1)} %maximum_select_fusion.12), channel_id=1, source_target_pairs={{0,4},{2,6},{4,0},{6,2},{8,12},{10,14},{12,8},{14,10},{1,5},{3,7},... | collective-permute-start | bytes 24584 | tf_op jit(solution)/shard_map/ppermute | solution.py:120
  30.3 5.1 %collective-permute-start.4 = (f32[2,8,2048]{2,1,0:T(8,128)S(1)}, f32[2,8,2048]{2,1,0:T(8,128)S(1)}, u32[]{:S(2)}, u32[]{:S(2)}) collective-permute-start(f32[2,8,2048]{2,1,0:T(8,128)S(1)} %get-tuple-element.144), channel_id=1, source_target_pairs={{0,2},{2,0},{4,6},{6,4},{8,10},{10,8},{12,14},{14,12},{1,3},{3,1},... | collective-permute-start | bytes 393224 | tf_op jit(solution)/shard_map/ppermute | solution.py:120
  31.9 6.0 %collective-permute-start.6 = (f32[4,64,128]{2,1,0:T(8,128)S(1)}, f32[4,64,128]{2,1,0:T(8,128)S(1)}, u32[]{:S(2)}, u32[]{:S(2)}) collective-permute-start(f32[4,64,128]{2,1,0:T(8,128)S(1)} %constant_dynamic-slice_fusion.5), channel_id=1, source_target_pairs={{0,1},{1,0},{2,3},{3,2},{4,5},{5,4},{6,7},{7,6},{8,9},{9,8},{10,11... | collective-permute-start | bytes 393224 | tf_op jit(solution)/shard_map/ppermute | solution.py:52
  32.0 5.9 %collective-permute-start.3 = (f32[2,8,2048]{2,1,0:T(8,128)S(1)}, f32[2,8,2048]{2,1,0:T(8,128)S(1)}, u32[]{:S(2)}, u32[]{:S(2)}) collective-permute-start(f32[2,8,2048]{2,1,0:T(8,128)S(1)} %get-tuple-element.145), channel_id=1, source_target_pairs={{0,4},{2,6},{4,0},{6,2},{8,12},{10,14},{12,8},{14,10},{1,5},{3,7},... | collective-permute-start | bytes 393224 | tf_op jit(solution)/shard_map/ppermute | solution.py:120
  42.4 5.0 %collective-permute-start.10 = (f32[4,64,128]{2,1,0:T(8,128)S(1)}, f32[4,64,128]{2,1,0:T(8,128)S(1)}, u32[]{:S(2)}, u32[]{:S(2)}) collective-permute-start(f32[4,64,128]{2,1,0:T(8,128)S(1)} %constant_dynamic-slice_fusion.4), channel_id=1, source_target_pairs={{0,1},{1,0},{2,3},{3,2},{4,5},{5,4},{6,7},{7,6},{8,9},{9,8},{10,11... | collective-permute-start | bytes 393224 | tf_op jit(solution)/shard_map/ppermute | solution.py:52
  42.5 4.3 %collective-permute-start.9 = (f32[4,16,64]{2,1,0:T(8,128)S(1)}, f32[4,16,64]{2,1,0:T(8,128)S(1)}, u32[]{:S(2)}, u32[]{:S(2)}) collective-permute-start(f32[4,16,64]{2,1,0:T(8,128)S(1)} %bitcast.247), channel_id=1, source_target_pairs={{0,2},{2,0},{4,6},{6,4},{8,10},{10,8},{12,14},{14,12},{1,3},{3,1},... | collective-permute-start | bytes 49160 | tf_op jit(solution)/shard_map/ppermute | solution.py:120
  43.2 8.4 %collective-permute-start.8 = (f32[4,8,2048]{2,1,0:T(8,128)S(1)}, f32[4,8,2048]{2,1,0:T(8,128)S(1)}, u32[]{:S(2)}, u32[]{:S(2)}) collective-permute-start(f32[4,8,2048]{2,1,0:T(8,128)S(1)} %bitcast.221), channel_id=1, source_target_pairs={{0,4},{2,6},{4,0},{6,2},{8,12},{10,14},{12,8},{14,10},{1,5},{3,7},... | collective-permute-start | bytes 786440 | tf_op jit(solution)/shard_map/ppermute | solution.py:120
  43.5 8.5 %collective-permute-start.7 = (f32[4,8,2048]{2,1,0:T(8,128)S(1)}, f32[4,8,2048]{2,1,0:T(8,128)S(1)}, u32[]{:S(2)}, u32[]{:S(2)}) collective-permute-start(f32[4,8,2048]{2,1,0:T(8,128)S(1)} %bitcast.223), channel_id=1, source_target_pairs={{0,2},{2,0},{4,6},{6,4},{8,10},{10,8},{12,14},{14,12},{1,3},{3,1},... | collective-permute-start | bytes 786440 | tf_op jit(solution)/shard_map/ppermute | solution.py:120
  57.2 3.4 %collective-permute-start.13 = (f32[4,64,128]{2,1,0:T(8,128)S(1)}, f32[4,64,128]{2,1,0:T(8,128)S(1)}, u32[]{:S(2)}, u32[]{:S(2)}) collective-permute-start(f32[4,64,128]{2,1,0:T(8,128)S(1)} %constant_dynamic-slice_fusion.3), channel_id=1, source_target_pairs={{0,1},{1,0},{2,3},{3,2},{4,5},{5,4},{6,7},{7,6},{8,9},{9,8},{10,11... | collective-permute-start | bytes 393224 | tf_op jit(solution)/shard_map/ppermute | solution.py:52
  57.4 8.8 %collective-permute-start.12 = (f32[2,2,4,32,128]{4,3,2,1,0:T(8,128)S(1)}, f32[2,2,4,32,128]{4,3,2,1,0:T(8,128)S(1)}, u32[]{:S(2)}, u32[]{:S(2)}) collective-permute-start(f32[2,2,4,32,128]{4,3,2,1,0:T(8,128)S(1)} %dynamic-slice_bitcast_fusion.2), channel_id=1, source_target_pairs={{0,4},{2,6},{4,0},{6,2},{8,12},{10,14},{12,8},{14,10},{1,5},{3,7},... | collective-permute-start | bytes 786440 | tf_op jit(solution)/shard_map/ppermute | solution.py:169
  58.9 8.5 %collective-permute-start.11 = (f32[4,1,4,32,128]{4,3,2,0,1:T(8,128)S(1)}, f32[4,1,4,32,128]{4,3,2,0,1:T(8,128)S(1)}, u32[]{:S(2)}, u32[]{:S(2)}) collective-permute-start(f32[4,1,4,32,128]{4,3,2,0,1:T(8,128)S(1)} %dynamic-slice_bitcast_fusion.3), channel_id=1, source_target_pairs={{0,2},{2,0},{4,6},{6,4},{8,10},{10,8},{12,14},{14,12},{1,3},{3,1},... | collective-permute-start | bytes 786440 | tf_op jit(solution)/shard_map/ppermute | solution.py:169
  67.4 5.2 %collective-permute-start.18 = (f32[4,64,128]{2,1,0:T(8,128)S(1)}, f32[4,64,128]{2,1,0:T(8,128)S(1)}, u32[]{:S(2)}, u32[]{:S(2)}) collective-permute-start(f32[4,64,128]{2,1,0:T(8,128)S(1)} %constant_dynamic-slice_fusion.2), channel_id=1, source_target_pairs={{0,1},{1,0},{2,3},{3,2},{4,5},{5,4},{6,7},{7,6},{8,9},{9,8},{10,11... | collective-permute-start | bytes 393224 | tf_op jit(solution)/shard_map/ppermute | solution.py:52
  67.5 8.4 %collective-permute-start.17 = (f32[2,1,4,32,128]{4,3,2,0,1:T(8,128)S(1)}, f32[2,1,4,32,128]{4,3,2,0,1:T(8,128)S(1)}, u32[]{:S(2)}, u32[]{:S(2)}) collective-permute-start(f32[2,1,4,32,128]{4,3,2,0,1:T(8,128)S(1)} %dynamic-slice_bitcast_fusion.8), channel_id=1, source_target_pairs={{0,2},{2,0},{4,6},{6,4},{8,10},{10,8},{12,14},{14,12},{1,3},{3,1},... | collective-permute-start | bytes 393224 | tf_op jit(solution)/shard_map/ppermute | solution.py:169
  69.1 6.8 %collective-permute-start.16 = (f32[2,1,4,32,128]{4,3,2,0,1:T(8,128)S(1)}, f32[2,1,4,32,128]{4,3,2,0,1:T(8,128)S(1)}, u32[]{:S(2)}, u32[]{:S(2)}) collective-permute-start(f32[2,1,4,32,128]{4,3,2,0,1:T(8,128)S(1)} %dynamic-slice_bitcast_fusion.9), channel_id=1, source_target_pairs={{0,4},{2,6},{4,0},{6,2},{8,12},{10,14},{12,8},{14,10},{1,5},{3,7},... | collective-permute-start | bytes 393224 | tf_op jit(solution)/shard_map/ppermute | solution.py:169
  70.2 10.2 %collective-permute-start.15 = (f32[2,2,4,32,128]{4,3,2,1,0:T(8,128)S(1)}, f32[2,2,4,32,128]{4,3,2,1,0:T(8,128)S(1)}, u32[]{:S(2)}, u32[]{:S(2)}) collective-permute-start(f32[2,2,4,32,128]{4,3,2,1,0:T(8,128)S(1)} %dynamic-slice_bitcast_fusion), channel_id=1, source_target_pairs={{0,4},{2,6},{4,0},{6,2},{8,12},{10,14},{12,8},{14,10},{1,5},{3,7},... | collective-permute-start | bytes 786440 | tf_op jit(solution)/shard_map/ppermute | solution.py:169
  71.9 8.6 %collective-permute-start.14 = (f32[4,1,4,32,128]{4,3,2,0,1:T(8,128)S(1)}, f32[4,1,4,32,128]{4,3,2,0,1:T(8,128)S(1)}, u32[]{:S(2)}, u32[]{:S(2)}) collective-permute-start(f32[4,1,4,32,128]{4,3,2,0,1:T(8,128)S(1)} %dynamic-slice_bitcast_fusion.1), channel_id=1, source_target_pairs={{0,2},{2,0},{4,6},{6,4},{8,10},{10,8},{12,14},{14,12},{1,3},{3,1},... | collective-permute-start | bytes 786440 | tf_op jit(solution)/shard_map/ppermute | solution.py:169
  80.6 5.0 %collective-permute-start.20 = (f32[2,1,4,32,128]{4,3,2,0,1:T(8,128)S(1)}, f32[2,1,4,32,128]{4,3,2,0,1:T(8,128)S(1)}, u32[]{:S(2)}, u32[]{:S(2)}) collective-permute-start(f32[2,1,4,32,128]{4,3,2,0,1:T(8,128)S(1)} %dynamic-slice_bitcast_fusion.6), channel_id=1, source_target_pairs={{0,2},{2,0},{4,6},{6,4},{8,10},{10,8},{12,14},{14,12},{1,3},{3,1},... | collective-permute-start | bytes 393224 | tf_op jit(solution)/shard_map/ppermute | solution.py:169
  81.2 9.6 %collective-permute-start.21 = (f32[1,1,4,64,128]{4,3,2,1,0:T(8,128)S(1)}, f32[1,1,4,64,128]{4,3,2,1,0:T(8,128)S(1)}, u32[]{:S(2)}, u32[]{:S(2)}) collective-permute-start(f32[1,1,4,64,128]{4,3,2,1,0:T(8,128)S(1)} %dynamic-slice_bitcast_fusion.5), channel_id=1, source_target_pairs={{0,8},{2,10},{4,12},{6,14},{8,0},{10,2},{12,4},{14,6},{1,9},{3,11}... | collective-permute-start | bytes 393224 | tf_op jit(solution)/shard_map/ppermute | solution.py:169
  83.9 6.9 %collective-permute-start.19 = (f32[2,1,4,32,128]{4,3,2,0,1:T(8,128)S(1)}, f32[2,1,4,32,128]{4,3,2,0,1:T(8,128)S(1)}, u32[]{:S(2)}, u32[]{:S(2)}) collective-permute-start(f32[2,1,4,32,128]{4,3,2,0,1:T(8,128)S(1)} %dynamic-slice_bitcast_fusion.7), channel_id=1, source_target_pairs={{0,4},{2,6},{4,0},{6,2},{8,12},{10,14},{12,8},{14,10},{1,5},{3,7},... | collective-permute-start | bytes 393224 | tf_op jit(solution)/shard_map/ppermute | solution.py:169
  90.9 7.3 %collective-permute-start.22 = (f32[1,1,4,64,128]{4,3,2,1,0:T(8,128)S(1)}, f32[1,1,4,64,128]{4,3,2,1,0:T(8,128)S(1)}, u32[]{:S(2)}, u32[]{:S(2)}) collective-permute-start(f32[1,1,4,64,128]{4,3,2,1,0:T(8,128)S(1)} %dynamic-slice_bitcast_fusion.4), channel_id=1, source_target_pairs={{0,8},{2,10},{4,12},{6,14},{8,0},{10,2},{12,4},{14,6},{1,9},{3,11}... | collective-permute-start | bytes 393224 | tf_op jit(solution)/shard_map/ppermute | solution.py:169
  99.9 6.2 %collective-permute-start.23 = (f32[1,4,64,128]{3,2,1,0:T(8,128)S(1)}, f32[1,4,64,128]{3,2,1,0:T(8,128)S(1)}, u32[]{:S(2)}, u32[]{:S(2)}) collective-permute-start(f32[1,4,64,128]{3,2,1,0:T(8,128)S(1)} %fusion.1), channel_id=1, source_target_pairs={{0,8},{2,10},{4,12},{6,14},{8,0},{10,2},{12,4},{14,6},{1,9},{3,11}... | collective-permute-start | bytes 393224 | tf_op jit(solution)/shard_map/ppermute | solution.py:120
  106.1 5.0 %collective-permute-start.25 = (f32[2,4,32,128]{3,2,1,0:T(8,128)S(1)}, f32[2,4,32,128]{3,2,1,0:T(8,128)S(1)}, u32[]{:S(2)}, u32[]{:S(2)}) collective-permute-start(f32[2,4,32,128]{3,2,1,0:T(8,128)S(1)} %get-tuple-element.140), channel_id=1, source_target_pairs={{0,2},{2,0},{4,6},{6,4},{8,10},{10,8},{12,14},{14,12},{1,3},{3,1},... | collective-permute-start | bytes 393224 | tf_op jit(solution)/shard_map/ppermute | solution.py:120
  107.6 6.4 %collective-permute-start.24 = (f32[2,4,32,128]{3,2,1,0:T(8,128)S(1)}, f32[2,4,32,128]{3,2,1,0:T(8,128)S(1)}, u32[]{:S(2)}, u32[]{:S(2)}) collective-permute-start(f32[2,4,32,128]{3,2,1,0:T(8,128)S(1)} %get-tuple-element.141), channel_id=1, source_target_pairs={{0,4},{2,6},{4,0},{6,2},{8,12},{10,14},{12,8},{14,10},{1,5},{3,7},... | collective-permute-start | bytes 393224 | tf_op jit(solution)/shard_map/ppermute | solution.py:120
  114.0 6.6 %collective-permute-start.27 = (f32[4,4,32,128]{3,2,1,0:T(8,128)S(1)}, f32[4,4,32,128]{3,2,1,0:T(8,128)S(1)}, u32[]{:S(2)}, u32[]{:S(2)}) collective-permute-start(f32[4,4,32,128]{3,2,1,0:T(8,128)S(1)} %bitcast.229), channel_id=1, source_target_pairs={{0,4},{2,6},{4,0},{6,2},{8,12},{10,14},{12,8},{14,10},{1,5},{3,7},... | collective-permute-start | bytes 786440 | tf_op jit(solution)/shard_map/ppermute | solution.py:120
  114.1 6.4 %collective-permute-start.26 = (f32[4,4,32,128]{3,2,1,0:T(8,128)S(1)}, f32[4,4,32,128]{3,2,1,0:T(8,128)S(1)}, u32[]{:S(2)}, u32[]{:S(2)}) collective-permute-start(f32[4,4,32,128]{3,2,1,0:T(8,128)S(1)} %bitcast.235), channel_id=1, source_target_pairs={{0,2},{2,0},{4,6},{6,4},{8,10},{10,8},{12,14},{14,12},{1,3},{3,1},... | collective-permute-start | bytes 786440 | tf_op jit(solution)/shard_map/ppermute | solution.py:120
  122.8 1.6 %collective-permute-start.28 = (f32[4,64,128]{2,1,0:T(8,128)}, f32[4,64,128]{2,1,0:T(8,128)S(1)}, u32[]{:S(2)}, u32[]{:S(2)}) collective-permute-start(f32[4,64,128]{2,1,0:T(8,128)} %constant_dynamic-slice_fusion), channel_id=1, source_target_pairs={{0,1},{1,0},{2,3},{3,2},{4,5},{5,4},{6,7},{7,6},{8,9},{9,8},{10,11... | collective-permute-start | bytes 393224 | tf_op jit(solution)/shard_map/ppermute | solution.py:52
  129.4 1.9 %collective-permute-start.29 = (f32[1,2,256]{2,1,0:T(2,128)S(1)}, f32[1,2,256]{2,1,0:T(2,128)S(1)}, u32[]{:S(2)}, u32[]{:S(2)}) collective-permute-start(f32[1,2,256]{2,1,0:T(2,128)S(1)} %maximum_bitcast_fusion), channel_id=1, source_target_pairs={{0,1},{1,0},{2,3},{3,2},{4,5},{5,4},{6,7},{7,6},{8,9},{9,8},{10,11... | collective-permute-start | bytes 6152 | tf_op jit(solution)/shard_map/ppermute | solution.py:353
  (20 other events, 90.4 us)

commit v10 on v9

--- a/solution.py
+++ b/solution.py
@@ -140,8 +140,15 @@
     return {"held": held, "kind": kind, "order": list(order), "i": 0, "bits": list(bits)}
 
 
+def swap_sum(held, k):
+    n = lax.axis_size("shot")
+    return held + lax.ppermute(held, "shot", [(i, i ^ k) for i in range(n)])
+
+
 def chain_step(c):
     k = c["order"][c["i"]]
+    if c["kind"] == "sum":
+        return swap_sum(c["held"], k)
     if c["kind"] == "ag":
         return ag_step(c["held"], k, c["bits"])
     return rs_step(c["held"], k, c["bits"])
@@ -153,7 +160,7 @@
     c["i"] += 1
     if c["kind"] == "ag":
         c["bits"].append(k)
-    else:
+    elif c["kind"] == "rs":
         c["bits"].remove(k)
 
 
@@ -304,29 +311,22 @@
         if light_a["i"] < len(light_a["order"]):
             group += [light_a, light_b]
         elif light_c is None:
-            light_c = chain(
-                jnp.concatenate([light_a["held"], light_b["held"]], axis=2), "rs", near_first[-1:], near_first[-1:]
-            )
+            light_c = chain(jnp.concatenate([light_a["held"], light_b["held"]], axis=2), "sum", near_first[-1:])
             group.append(light_c)
         run_group(group, tasks[i] if i < len(tasks) else nothing)
     for i in range(len(bits) - 1, len(tasks)):
         tasks[i]()
     if light_c is None:
-        light_c = chain(
-            jnp.concatenate([light_a["held"], light_b["held"]], axis=2), "rs", near_first[-1:], near_first[-1:]
-        )
-    last = chain(
-        jnp.concatenate([image_a["held"], image_b["held"]], axis=2), "rs", near_first[-1:], near_first[-1:]
-    )
+        light_c = chain(jnp.concatenate([light_a["held"], light_b["held"]], axis=2), "sum", near_first[-1:])
+    last = chain(jnp.concatenate([image_a["held"], image_b["held"]], axis=2), "sum", near_first[-1:])
     run_group([last, light_c], nothing)
-    image_part = last["held"][0]
-    light_part = light_c["held"][0]
+    image_part = last["held"].reshape((-1,) + last["held"].shape[2:])
+    light_part = light_c["held"].reshape((-1,) + light_c["held"].shape[2:])
 
     table_all = gains_held.reshape(n_shot * gains.shape[0], gains.shape[1])
     filt_part = lateral_filter(image_part / (light_part + eps), table_all)
-    filt_c = chain(filt_part[None], "ag", far_first[:1])
-    run_group([filt_c], nothing)
-    part_a, part_b = halves(filt_c["held"], 2)
+    pair_held = filt_part.reshape((2, slab) + filt_part.shape[1:])
+    part_a, part_b = halves(pair_held, 2)
     filt_a = chain(part_a, "ag", far_first[1:], [top])
     filt_b = chain(part_b, "ag", swap_first(far_first[1:]), [top])
     for i in range(1, len(bits)):

time: 133 us -> 137 us (1.030)
  waiting for transfers between devices: 46 us -> 50 us
    ppermute x0 -> x2, waiting for transfers between devices: none -> 17.4 us  [swap_sum(): return held + lax.ppermute(held, 'shot', [(i, i ^ k) for i in range(n)])]
    ppermute x13 -> x12, waiting for transfers between devices: 24.1 us -> 17 us  [ag_step(): theirs = lax.ppermute(held, 'shot', [(i, i ^ k) for i in range(n)])]
    ppermute x10 -> x8, waiting for transfers between devices: 21.3 us -> 15 us  [rs_step(): got = lax.ppermute(send, 'shot', [(i, i ^ k) for i in range(n)])]
    ppermute x0 -> x2, starting transfers between devices: none -> 2.73 us  [swap_sum(): return held + lax.ppermute(held, 'shot', [(i, i ^ k) for i in range(n)])]
    ppermute x10 -> x8, starting transfers between devices: 11.4 us -> 8.63 us  [rs_step(): got = lax.ppermute(send, 'shot', [(i, i ^ k) for i in range(n)])]
    ppermute x13 -> x12, starting transfers between devices: 12.4 us -> 12.7 us  [ag_step(): theirs = lax.ppermute(held, 'shot', [(i, i ^ k) for i in range(n)])]
  transfers between devices with their start and end apart: 30 -> 29, of which waited for: 16 -> 16; matrix products, arithmetic and copies ran while one was open for 25% -> 24% of each run, Pallas kernels for 0% -> 0%
where the time goes in v10:
time: 137 us
  waiting for transfers between devices  50 us (36%)
  other arithmetic  37.1 us (27%)
  starting transfers between devices  25.4 us (19%)
  local copies, waits for them, and re-layouts  17.2 us (13%)
  between operations  4.8 us (4%)
  matrix products  2.12 us (2%)
    ppermute x2, waiting for transfers between devices, swap_sum(): return held + lax.ppermute(held, 'shot', [(i, i ^ k) for i in range(n)])  17.4 us
    ppermute x12, waiting for transfers between devices, ag_step(): theirs = lax.ppermute(held, 'shot', [(i, i ^ k) for i in range(n)])  17 us
    ppermute x8, waiting for transfers between devices, rs_step(): got = lax.ppermute(send, 'shot', [(i, i ^ k) for i in range(n)])  15 us
    ppermute x12, starting transfers between devices, ag_step(): theirs = lax.ppermute(held, 'shot', [(i, i ^ k) for i in range(n)])  12.7 us
    add x3, other arithmetic, inject(): return field + jnp.where(hit, source_gain[0] * wavelet[0, moment], 0.0)  11.7 us
    ppermute x8, starting transfers between devices, rs_step(): got = lax.ppermute(send, 'shot', [(i, i ^ k) for i in range(n)])  8.63 us
    add x2, other arithmetic, born_second(): 2.0 * born + speed_term * laplace_x(with_halo(born)) - absorber * born  5.85 us
    another operation x1, other arithmetic, damping(): lower = jnp.stack([edges[0], edges[2], edges[4]])[:, None]  3.86 us
  transfers between devices with their start and end apart: 29, of which 16 were waited for; matrix products, arithmetic and copies ran while one was open for 24% of the time, Pallas kernels for 0%

profile of v10, /device:TPU:0, one launch (start us, length us, event | category | flops | bytes accessed | tf_op | source)
XLA Modules:
  0.0 136.6 jit_solution(12129091113984801101)
XLA Ops:
  0.7 1.7 %dynamic-slice_bitcast_fusion.8 = f32[4,64,128]{2,1,0:T(8,128)} fusion(f32[1,32,64,128]{3,2,1,0:T(8,128)} %param.12, s32[]{:T(128)S(6)} %select_n.374), kind=kLoop, calls=%fused_computation.349 | loop fusion | bytes 262148 | tf_op jit(solution)/shard_map/dynamic_slice | solution.py:51
  4.6 3.6 %collective-permute-start = (f32[1,16,2048]{2,1,0:T(8,128)}, f32[1,16,2048]{2,1,0:T(8,128)}, u32[]{:S(2)}, u32[]{:S(2)}) collective-permute-start(f32[1,16,2048]{2,1,0:T(8,128)} %concatenate.182), channel_id=1, source_target_pairs={{0,8},{2,10},{4,12},{6,14},{8,0},{10,2},{12,4},{14,6},{1,9},{3,11}... | collective-permute-start | bytes 393224 | tf_op jit(solution)/shard_map/ppermute | solution.py:120
  10.3 3.9 %pad_maximum_fusion.15 = (f32[3]{0:T(128)S(1)}, f32[3]{0:T(128)S(1)}) fusion(f32[1]{0:T(128)} %get-tuple-element.149, f32[1]{0:T(128)} %get-tuple-element.150, f32[1]{0:T(128)} %get-tuple-element.145, f32[1]{0:T(128)} %get-tuple-element.146, f32[1]{0:T(128)} %get-tuple-element.147, f32[1]{0:T(128)} %get-tuple-element.148), kind=kLoop, calls=%fused_computation.406 | loop fusion | flops 12 | bytes 48 | tf_op jit(solution)/shard_map/stack | solution.py:37
  22.3 4.5 %fusion.1 = (f32[32,64,128]{2,1,0:T(8,128)S(1)}, f32[32,64,128]{2,1,0:T(8,128)S(1)}) fusion(f32[]{:T(128)S(6)} %mul.319, f32[128]{0:T(128)} %slice_bitcast_fusion, f32[32,64]{1,0:T(8,128)S(1)} %broadcast_add_fusion, pred[128]{0:T(512)(128)(4,1)} %iota_compare_fusion.1, pred[32,64]{1,0:T(8,128)(4,1)} %broadcast_and_fusion, f32[1,32,64,128]{3,2,1,0:T(8,128)} %param.11, ...), kind=kLoop, calls=%fused_computation.117 | loop fusion | flops 12058624 | bytes 16009860 | tf_op jit(solution)/shard_map/add | solution.py:220
  28.1 1.9 %collective-permute-start.5 = (f32[2,16,64]{2,1,0:T(8,128)S(1)}, f32[2,16,64]{2,1,0:T(8,128)S(1)}, u32[]{:S(2)}, u32[]{:S(2)}) collective-permute-start(f32[2,16,64]{2,1,0:T(8,128)S(1)} %maximum_select_fusion.11), channel_id=1, source_target_pairs={{0,4},{2,6},{4,0},{6,2},{8,12},{10,14},{12,8},{14,10},{1,5},{3,7},... | collective-permute-start | bytes 24584 | tf_op jit(solution)/shard_map/ppermute | solution.py:120
  30.2 1.6 %collective-permute-start.4 = (f32[2,8,2048]{2,1,0:T(8,128)S(1)}, f32[2,8,2048]{2,1,0:T(8,128)S(1)}, u32[]{:S(2)}, u32[]{:S(2)}) collective-permute-start(f32[2,8,2048]{2,1,0:T(8,128)S(1)} %get-tuple-element.138), channel_id=1, source_target_pairs={{0,2},{2,0},{4,6},{6,4},{8,10},{10,8},{12,14},{14,12},{1,3},{3,1},... | collective-permute-start | bytes 393224 | tf_op jit(solution)/shard_map/ppermute | solution.py:120
  32.4 2.9 %collective-permute-done.4 = f32[2,8,2048]{2,1,0:T(8,128)S(1)} collective-permute-done((f32[2,8,2048]{2,1,0:T(8,128)S(1)}, f32[2,8,2048]{2,1,0:T(8,128)S(1)}, u32[]{:S(2)}, u32[]{:S(2)}) %collective-permute-start.4) | collective-permute-done | bytes 131104 | tf_op jit(solution)/shard_map/ppermute | solution.py:120
  35.3 2.4 %collective-permute-done.3 = f32[2,8,2048]{2,1,0:T(8,128)S(1)} collective-permute-done((f32[2,8,2048]{2,1,0:T(8,128)S(1)}, f32[2,8,2048]{2,1,0:T(8,128)S(1)}, u32[]{:S(2)}, u32[]{:S(2)}) %collective-permute-start.3) | collective-permute-done | bytes 131104 | tf_op jit(solution)/shard_map/ppermute | solution.py:120
  37.9 3.2 %fusion.2 = (f32[32,64,128]{2,1,0:T(8,128)S(1)}, f32[32,64,128]{2,1,0:T(8,128)S(1)}) fusion(f32[32,64,128]{2,1,0:T(8,128)S(1)} %get-tuple-element.67, f32[32,64,128]{2,1,0:T(8,128)S(1)} %bitcast.181, f32[]{:T(128)S(6)} %mul.330, f32[128]{0:T(128)S(1)} %copy-done.12, f32[32,64]{1,0:T(8,128)S(1)} %broadcast_add_fusion, pred[128]{0:T(512)(128)(4,1)S(1)} %copy-done.15, ...), kind=kLoop, calls=%fused_computation.118 | loop fusion | flops 12058624 | bytes 16012292 | tf_op jit(solution)/shard_map/add | solution.py:220
  41.0 1.2 multiply_add_fusion.1
  43.4 1.7 %collective-permute-start.7 = (f32[4,8,2048]{2,1,0:T(8,128)S(1)}, f32[4,8,2048]{2,1,0:T(8,128)S(1)}, u32[]{:S(2)}, u32[]{:S(2)}) collective-permute-start(f32[4,8,2048]{2,1,0:T(8,128)S(1)} %bitcast.209), channel_id=1, source_target_pairs={{0,2},{2,0},{4,6},{6,4},{8,10},{10,8},{12,14},{14,12},{1,3},{3,1},... | collective-permute-start | bytes 786440 | tf_op jit(solution)/shard_map/ppermute | solution.py:120
  45.1 1.5 %collective-permute-done.9 = f32[4,16,64]{2,1,0:T(8,128)S(1)} collective-permute-done((f32[4,16,64]{2,1,0:T(8,128)S(1)}, f32[4,16,64]{2,1,0:T(8,128)S(1)}, u32[]{:S(2)}, u32[]{:S(2)}) %collective-permute-start.9) | collective-permute-done | bytes 16416 | tf_op jit(solution)/shard_map/ppermute | solution.py:120
  47.3 4.0 %fusion.3 = (f32[32,64,128]{2,1,0:T(8,128)}, f32[32,64,128]{2,1,0:T(8,128)}) fusion(f32[32,64,128]{2,1,0:T(8,128)S(1)} %get-tuple-element.65, f32[32,64,128]{2,1,0:T(8,128)S(1)} %get-tuple-element.67, f32[]{:T(128)S(6)} %mul.339, f32[128]{0:T(128)S(1)} %copy-done.12, f32[32,64]{1,0:T(8,128)S(1)} %broadcast_add_fusion, pred[128]{0:T(512)(128)(4,1)S(1)} %copy-done.15, ...), kind=kLoop, calls=%fused_computation.119 | loop fusion | flops 12058624 | bytes 16012292 | tf_op jit(solution)/shard_map/add | solution.py:220
  53.0 2.5 %copy.44 = f32[2048,128]{1,0:T(8,128)} copy(f32[2048,128]{0,1:T(8,128)} %bitcast.189) | data formatting | bytes 2097152 | tf_op jit(solution)/shard_map/transpose | solution.py:296
  55.6 1.4 %mul.340 = f32[32,64,128]{2,1,0:T(8,128)S(1)} multiply(f32[32,64,128]{2,1,0:T(8,128)} %bitcast.183, f32[32,64,128]{2,1,0:T(8,128)S(1)} %get-tuple-element.75) | non-fusion elementwise | flops 262144 | bytes 3145728 | tf_op jit(solution)/shard_map/mul | solution.py:297
  57.3 1.4 %collective-permute-start.12 = (f32[2,2,4,32,128]{4,3,2,1,0:T(8,128)S(1)}, f32[2,2,4,32,128]{4,3,2,1,0:T(8,128)S(1)}, u32[]{:S(2)}, u32[]{:S(2)}) collective-permute-start(f32[2,2,4,32,128]{4,3,2,1,0:T(8,128)S(1)} %dynamic-slice_bitcast_fusion.2), channel_id=1, source_target_pairs={{0,4},{2,6},{4,0},{6,2},{8,12},{10,14},{12,8},{14,10},{1,5},{3,7},... | collective-permute-start | bytes 786440 | tf_op jit(solution)/shard_map/ppermute | solution.py:176
  58.7 1.6 %collective-permute-start.11 = (f32[4,1,4,32,128]{4,3,2,0,1:T(8,128)S(1)}, f32[4,1,4,32,128]{4,3,2,0,1:T(8,128)S(1)}, u32[]{:S(2)}, u32[]{:S(2)}) collective-permute-start(f32[4,1,4,32,128]{4,3,2,0,1:T(8,128)S(1)} %dynamic-slice_bitcast_fusion.3), channel_id=1, source_target_pairs={{0,2},{2,0},{4,6},{6,4},{8,10},{10,8},{12,14},{14,12},{1,3},{3,1},... | collective-permute-start | bytes 786440 | tf_op jit(solution)/shard_map/ppermute | solution.py:176
  60.5 2.9 %fusion.91 = f32[32,64,128]{2,1,0:T(8,128)S(1)} fusion(f32[40,64,128]{2,1,0:T(8,128)S(1)} %constant_dynamic-update-slice_fusion.6, f32[32,64,128]{2,1,0:T(8,128)S(1)} %bitcast.184, f32[32,64,128]{2,1,0:T(8,128)S(1)} %get-tuple-element.77, f32[32,64,128]{2,1,0:T(8,128)S(1)} %mul.340, f32[128]{0:T(128)S(1)} %copy-done.13, f32[32,64]{1,0:T(8,128)S(1)} %broadcast_add_fusion, ...), kind=kLoop, calls=%fused_computation.207 | loop fusion | flops 11272192 | bytes 16007680 | tf_op jit(solution)/shard_map/add | solution.py:231
  63.5 2.6 %collective-permute-done.12 = f32[2,2,4,32,128]{4,3,2,1,0:T(8,128)S(1)} collective-permute-done((f32[2,2,4,32,128]{4,3,2,1,0:T(8,128)S(1)}, f32[2,2,4,32,128]{4,3,2,1,0:T(8,128)S(1)}, u32[]{:S(2)}, u32[]{:S(2)}) %collective-permute-start.12) | collective-permute-done | bytes 262176 | tf_op jit(solution)/shard_map/ppermute | solution.py:176
  67.4 1.6 %collective-permute-start.17 = (f32[2,1,4,32,128]{4,3,2,0,1:T(8,128)S(1)}, f32[2,1,4,32,128]{4,3,2,0,1:T(8,128)S(1)}, u32[]{:S(2)}, u32[]{:S(2)}) collective-permute-start(f32[2,1,4,32,128]{4,3,2,0,1:T(8,128)S(1)} %dynamic-slice_bitcast_fusion.6), channel_id=1, source_target_pairs={{0,2},{2,0},{4,6},{6,4},{8,10},{10,8},{12,14},{14,12},{1,3},{3,1},... | collective-permute-start | bytes 393224 | tf_op jit(solution)/shard_map/ppermute | solution.py:176
  70.0 1.6 %collective-permute-start.15 = (f32[2,2,4,32,128]{4,3,2,1,0:T(8,128)S(1)}, f32[2,2,4,32,128]{4,3,2,1,0:T(8,128)S(1)}, u32[]{:S(2)}, u32[]{:S(2)}) collective-permute-start(f32[2,2,4,32,128]{4,3,2,1,0:T(8,128)S(1)} %dynamic-slice_bitcast_fusion), channel_id=1, source_target_pairs={{0,4},{2,6},{4,0},{6,2},{8,12},{10,14},{12,8},{14,10},{1,5},{3,7},... | collective-permute-start | bytes 786440 | tf_op jit(solution)/shard_map/ppermute | solution.py:176
  72.5 3.2 %fusion.116 = f32[32,64,128]{2,1,0:T(8,128)} fusion(f32[40,64,128]{2,1,0:T(8,128)S(1)} %constant_dynamic-update-slice_fusion.5, s32[32,64,128]{2,1,0:T(8,128)S(1)} %copy-done), kind=kLoop, calls=%fused_computation.232 | loop fusion | flops 9175040 | bytes 12845056 | tf_op jit(solution)/shard_map/mul | solution.py:223
  75.8 4.5 %collective-permute-done.15 = f32[2,2,4,32,128]{4,3,2,1,0:T(8,128)S(1)} collective-permute-done((f32[2,2,4,32,128]{4,3,2,1,0:T(8,128)S(1)}, f32[2,2,4,32,128]{4,3,2,1,0:T(8,128)S(1)}, u32[]{:S(2)}, u32[]{:S(2)}) %collective-permute-start.15) | collective-permute-done | bytes 262176 | tf_op jit(solution)/shard_map/ppermute | solution.py:176
  81.0 2.7 %collective-permute-start.21 = (f32[2,4,64,128]{3,2,1,0:T(8,128)S(1)}, f32[2,4,64,128]{3,2,1,0:T(8,128)S(1)}, u32[]{:S(2)}, u32[]{:S(2)}) collective-permute-start(f32[2,4,64,128]{3,2,1,0:T(8,128)S(1)} %constant_dynamic-update-slice_fusion), channel_id=1, source_target_pairs={{0,8},{2,10},{4,12},{6,14},{8,0},{10,2},{12,4},{14,6},{1,9},{3,11}... | collective-permute-start | bytes 786440 | tf_op jit(solution)/shard_map/ppermute | solution.py:145
  85.5 5.9 %collective-permute-done.19 = f32[2,1,4,32,128]{4,3,2,0,1:T(8,128)S(1)} collective-permute-done((f32[2,1,4,32,128]{4,3,2,0,1:T(8,128)S(1)}, f32[2,1,4,32,128]{4,3,2,0,1:T(8,128)S(1)}, u32[]{:S(2)}, u32[]{:S(2)}) %collective-permute-start.19) | collective-permute-done | bytes 131104 | tf_op jit(solution)/shard_map/ppermute | solution.py:176
  91.4 3.5 %collective-permute-done.21 = f32[2,4,64,128]{3,2,1,0:T(8,128)S(1)} collective-permute-done((f32[2,4,64,128]{3,2,1,0:T(8,128)S(1)}, f32[2,4,64,128]{3,2,1,0:T(8,128)S(1)}, u32[]{:S(2)}, u32[]{:S(2)}) %collective-permute-start.21) | collective-permute-done | bytes 262176 | tf_op jit(solution)/shard_map/ppermute | solution.py:145
  95.2 13.9 %collective-permute-done.22 = f32[2,4,64,128]{3,2,1,0:T(8,128)S(1)} collective-permute-done((f32[2,4,64,128]{3,2,1,0:T(8,128)S(1)}, f32[2,4,64,128]{3,2,1,0:T(8,128)S(1)}, u32[]{:S(2)}, u32[]{:S(2)}) %collective-permute-start.22) | collective-permute-done | bytes 262176 | tf_op jit(solution)/shard_map/ppermute | solution.py:145
  111.3 1.2 collective-permute-start.24
  113.1 3.7 %collective-permute-done.24 = f32[2,4,32,128]{3,2,1,0:T(8,128)S(1)} collective-permute-done((f32[2,4,32,128]{3,2,1,0:T(8,128)S(1)}, f32[2,4,32,128]{3,2,1,0:T(8,128)S(1)}, u32[]{:S(2)}, u32[]{:S(2)}) %collective-permute-start.24) | collective-permute-done | bytes 131104 | tf_op jit(solution)/shard_map/ppermute | solution.py:120
  120.1 5.0 %collective-permute-done.25 = f32[4,4,32,128]{3,2,1,0:T(8,128)S(1)} collective-permute-done((f32[4,4,32,128]{3,2,1,0:T(8,128)S(1)}, f32[4,4,32,128]{3,2,1,0:T(8,128)S(1)}, u32[]{:S(2)}, u32[]{:S(2)}) %collective-permute-start.25) | collective-permute-done | bytes 262176 | tf_op jit(solution)/shard_map/ppermute | solution.py:120
  125.4 1.1 copy-done.3
  129.8 2.9 %fusion.144 = f32[32,64,128]{2,1,0:T(8,128)S(1)} fusion(f32[40,64,128]{2,1,0:T(8,128)S(1)} %constant_dynamic-update-slice_fusion.4, f32[32,64,128]{2,1,0:T(8,128)S(1)} %copy-done.7, f32[128]{0:T(128)S(1)} %copy-done.14, f32[32,64]{1,0:T(8,128)S(1)} %broadcast_add_fusion, f32[8,4,64,128]{3,2,1,0:T(8,128)S(1)} %pad_maximum_fusion.13, ...), kind=kLoop, calls=%fused_computation.260 | loop fusion | flops 11534336 | bytes 16007680 | tf_op jit(solution)/shard_map/add | solution.py:231
  (184 shorter events, 34.5 us)
Async XLA Ops:
  0.6 15.5 %copy-start.1 = (f32[1,32,64,128]{3,2,1,0:T(8,128)S(1)}, f32[1,32,64,128]{3,2,1,0:T(8,128)}, u32[]{:S(2)}) copy-start(f32[1,32,64,128]{3,2,1,0:T(8,128)} %param.12) | copy-start | bytes 3145732
  2.3 19.1 %collective-permute-start.2 = (f32[4,64,128]{2,1,0:T(8,128)}, f32[4,64,128]{2,1,0:T(8,128)}, u32[]{:S(2)}, u32[]{:S(2)}) collective-permute-start(f32[4,64,128]{2,1,0:T(8,128)} %dynamic-slice_bitcast_fusion.8), channel_id=1, source_target_pairs={{0,1},{1,0},{2,3},{3,2},{4,5},{5,4},{6,7},{7,6},{8,9},{9,8},{10,11... | collective-permute-start | bytes 393224 | tf_op jit(solution)/shard_map/ppermute | solution.py:52
  4.6 22.2 %collective-permute-start = (f32[1,16,2048]{2,1,0:T(8,128)}, f32[1,16,2048]{2,1,0:T(8,128)}, u32[]{:S(2)}, u32[]{:S(2)}) collective-permute-start(f32[1,16,2048]{2,1,0:T(8,128)} %concatenate.182), channel_id=1, source_target_pairs={{0,8},{2,10},{4,12},{6,14},{8,0},{10,2},{12,4},{14,6},{1,9},{3,11}... | collective-permute-start | bytes 393224 | tf_op jit(solution)/shard_map/ppermute | solution.py:120
  8.2 12.4 %collective-permute-start.1 = (f32[1,16,64]{2,1,0:T(8,128)}, f32[1,16,64]{2,1,0:T(8,128)}, u32[]{:S(2)}, u32[]{:S(2)}) collective-permute-start(f32[1,16,64]{2,1,0:T(8,128)} %bitcast.238), channel_id=1, source_target_pairs={{0,8},{2,10},{4,12},{6,14},{8,0},{10,2},{12,4},{14,6},{1,9},{3,11}... | collective-permute-start | bytes 12296 | tf_op jit(solution)/shard_map/ppermute | solution.py:120
  28.1 4.2 %collective-permute-start.5 = (f32[2,16,64]{2,1,0:T(8,128)S(1)}, f32[2,16,64]{2,1,0:T(8,128)S(1)}, u32[]{:S(2)}, u32[]{:S(2)}) collective-permute-start(f32[2,16,64]{2,1,0:T(8,128)S(1)} %maximum_select_fusion.11), channel_id=1, source_target_pairs={{0,4},{2,6},{4,0},{6,2},{8,12},{10,14},{12,8},{14,10},{1,5},{3,7},... | collective-permute-start | bytes 24584 | tf_op jit(solution)/shard_map/ppermute | solution.py:120
  30.2 5.1 %collective-permute-start.4 = (f32[2,8,2048]{2,1,0:T(8,128)S(1)}, f32[2,8,2048]{2,1,0:T(8,128)S(1)}, u32[]{:S(2)}, u32[]{:S(2)}) collective-permute-start(f32[2,8,2048]{2,1,0:T(8,128)S(1)} %get-tuple-element.138), channel_id=1, source_target_pairs={{0,2},{2,0},{4,6},{6,4},{8,10},{10,8},{12,14},{14,12},{1,3},{3,1},... | collective-permute-start | bytes 393224 | tf_op jit(solution)/shard_map/ppermute | solution.py:120
  31.8 6.0 %collective-permute-start.6 = (f32[4,64,128]{2,1,0:T(8,128)S(1)}, f32[4,64,128]{2,1,0:T(8,128)S(1)}, u32[]{:S(2)}, u32[]{:S(2)}) collective-permute-start(f32[4,64,128]{2,1,0:T(8,128)S(1)} %constant_dynamic-slice_fusion.5), channel_id=1, source_target_pairs={{0,1},{1,0},{2,3},{3,2},{4,5},{5,4},{6,7},{7,6},{8,9},{9,8},{10,11... | collective-permute-start | bytes 393224 | tf_op jit(solution)/shard_map/ppermute | solution.py:52
  31.8 5.9 %collective-permute-start.3 = (f32[2,8,2048]{2,1,0:T(8,128)S(1)}, f32[2,8,2048]{2,1,0:T(8,128)S(1)}, u32[]{:S(2)}, u32[]{:S(2)}) collective-permute-start(f32[2,8,2048]{2,1,0:T(8,128)S(1)} %get-tuple-element.139), channel_id=1, source_target_pairs={{0,4},{2,6},{4,0},{6,2},{8,12},{10,14},{12,8},{14,10},{1,5},{3,7},... | collective-permute-start | bytes 393224 | tf_op jit(solution)/shard_map/ppermute | solution.py:120
  42.2 5.0 %collective-permute-start.10 = (f32[4,64,128]{2,1,0:T(8,128)S(1)}, f32[4,64,128]{2,1,0:T(8,128)S(1)}, u32[]{:S(2)}, u32[]{:S(2)}) collective-permute-start(f32[4,64,128]{2,1,0:T(8,128)S(1)} %constant_dynamic-slice_fusion.4), channel_id=1, source_target_pairs={{0,1},{1,0},{2,3},{3,2},{4,5},{5,4},{6,7},{7,6},{8,9},{9,8},{10,11... | collective-permute-start | bytes 393224 | tf_op jit(solution)/shard_map/ppermute | solution.py:52
  42.3 4.3 %collective-permute-start.9 = (f32[4,16,64]{2,1,0:T(8,128)S(1)}, f32[4,16,64]{2,1,0:T(8,128)S(1)}, u32[]{:S(2)}, u32[]{:S(2)}) collective-permute-start(f32[4,16,64]{2,1,0:T(8,128)S(1)} %bitcast.231), channel_id=1, source_target_pairs={{0,2},{2,0},{4,6},{6,4},{8,10},{10,8},{12,14},{14,12},{1,3},{3,1},... | collective-permute-start | bytes 49160 | tf_op jit(solution)/shard_map/ppermute | solution.py:120
  43.0 8.4 %collective-permute-start.8 = (f32[4,8,2048]{2,1,0:T(8,128)S(1)}, f32[4,8,2048]{2,1,0:T(8,128)S(1)}, u32[]{:S(2)}, u32[]{:S(2)}) collective-permute-start(f32[4,8,2048]{2,1,0:T(8,128)S(1)} %bitcast.207), channel_id=1, source_target_pairs={{0,4},{2,6},{4,0},{6,2},{8,12},{10,14},{12,8},{14,10},{1,5},{3,7},... | collective-permute-start | bytes 786440 | tf_op jit(solution)/shard_map/ppermute | solution.py:120
  43.4 8.5 %collective-permute-start.7 = (f32[4,8,2048]{2,1,0:T(8,128)S(1)}, f32[4,8,2048]{2,1,0:T(8,128)S(1)}, u32[]{:S(2)}, u32[]{:S(2)}) collective-permute-start(f32[4,8,2048]{2,1,0:T(8,128)S(1)} %bitcast.209), channel_id=1, source_target_pairs={{0,2},{2,0},{4,6},{6,4},{8,10},{10,8},{12,14},{14,12},{1,3},{3,1},... | collective-permute-start | bytes 786440 | tf_op jit(solution)/shard_map/ppermute | solution.py:120
  57.1 3.4 %collective-permute-start.13 = (f32[4,64,128]{2,1,0:T(8,128)S(1)}, f32[4,64,128]{2,1,0:T(8,128)S(1)}, u32[]{:S(2)}, u32[]{:S(2)}) collective-permute-start(f32[4,64,128]{2,1,0:T(8,128)S(1)} %constant_dynamic-slice_fusion.3), channel_id=1, source_target_pairs={{0,1},{1,0},{2,3},{3,2},{4,5},{5,4},{6,7},{7,6},{8,9},{9,8},{10,11... | collective-permute-start | bytes 393224 | tf_op jit(solution)/shard_map/ppermute | solution.py:52
  57.3 8.8 %collective-permute-start.12 = (f32[2,2,4,32,128]{4,3,2,1,0:T(8,128)S(1)}, f32[2,2,4,32,128]{4,3,2,1,0:T(8,128)S(1)}, u32[]{:S(2)}, u32[]{:S(2)}) collective-permute-start(f32[2,2,4,32,128]{4,3,2,1,0:T(8,128)S(1)} %dynamic-slice_bitcast_fusion.2), channel_id=1, source_target_pairs={{0,4},{2,6},{4,0},{6,2},{8,12},{10,14},{12,8},{14,10},{1,5},{3,7},... | collective-permute-start | bytes 786440 | tf_op jit(solution)/shard_map/ppermute | solution.py:176
  58.7 8.5 %collective-permute-start.11 = (f32[4,1,4,32,128]{4,3,2,0,1:T(8,128)S(1)}, f32[4,1,4,32,128]{4,3,2,0,1:T(8,128)S(1)}, u32[]{:S(2)}, u32[]{:S(2)}) collective-permute-start(f32[4,1,4,32,128]{4,3,2,0,1:T(8,128)S(1)} %dynamic-slice_bitcast_fusion.3), channel_id=1, source_target_pairs={{0,2},{2,0},{4,6},{6,4},{8,10},{10,8},{12,14},{14,12},{1,3},{3,1},... | collective-permute-start | bytes 786440 | tf_op jit(solution)/shard_map/ppermute | solution.py:176
  67.3 5.2 %collective-permute-start.18 = (f32[4,64,128]{2,1,0:T(8,128)S(1)}, f32[4,64,128]{2,1,0:T(8,128)S(1)}, u32[]{:S(2)}, u32[]{:S(2)}) collective-permute-start(f32[4,64,128]{2,1,0:T(8,128)S(1)} %constant_dynamic-slice_fusion.2), channel_id=1, source_target_pairs={{0,1},{1,0},{2,3},{3,2},{4,5},{5,4},{6,7},{7,6},{8,9},{9,8},{10,11... | collective-permute-start | bytes 393224 | tf_op jit(solution)/shard_map/ppermute | solution.py:52
  67.4 8.4 %collective-permute-start.17 = (f32[2,1,4,32,128]{4,3,2,0,1:T(8,128)S(1)}, f32[2,1,4,32,128]{4,3,2,0,1:T(8,128)S(1)}, u32[]{:S(2)}, u32[]{:S(2)}) collective-permute-start(f32[2,1,4,32,128]{4,3,2,0,1:T(8,128)S(1)} %dynamic-slice_bitcast_fusion.6), channel_id=1, source_target_pairs={{0,2},{2,0},{4,6},{6,4},{8,10},{10,8},{12,14},{14,12},{1,3},{3,1},... | collective-permute-start | bytes 393224 | tf_op jit(solution)/shard_map/ppermute | solution.py:176
  69.0 6.8 %collective-permute-start.16 = (f32[2,1,4,32,128]{4,3,2,0,1:T(8,128)S(1)}, f32[2,1,4,32,128]{4,3,2,0,1:T(8,128)S(1)}, u32[]{:S(2)}, u32[]{:S(2)}) collective-permute-start(f32[2,1,4,32,128]{4,3,2,0,1:T(8,128)S(1)} %dynamic-slice_bitcast_fusion.7), channel_id=1, source_target_pairs={{0,4},{2,6},{4,0},{6,2},{8,12},{10,14},{12,8},{14,10},{1,5},{3,7},... | collective-permute-start | bytes 393224 | tf_op jit(solution)/shard_map/ppermute | solution.py:176
  70.0 10.2 %collective-permute-start.15 = (f32[2,2,4,32,128]{4,3,2,1,0:T(8,128)S(1)}, f32[2,2,4,32,128]{4,3,2,1,0:T(8,128)S(1)}, u32[]{:S(2)}, u32[]{:S(2)}) collective-permute-start(f32[2,2,4,32,128]{4,3,2,1,0:T(8,128)S(1)} %dynamic-slice_bitcast_fusion), channel_id=1, source_target_pairs={{0,4},{2,6},{4,0},{6,2},{8,12},{10,14},{12,8},{14,10},{1,5},{3,7},... | collective-permute-start | bytes 786440 | tf_op jit(solution)/shard_map/ppermute | solution.py:176
  71.7 8.6 %collective-permute-start.14 = (f32[4,1,4,32,128]{4,3,2,0,1:T(8,128)S(1)}, f32[4,1,4,32,128]{4,3,2,0,1:T(8,128)S(1)}, u32[]{:S(2)}, u32[]{:S(2)}) collective-permute-start(f32[4,1,4,32,128]{4,3,2,0,1:T(8,128)S(1)} %dynamic-slice_bitcast_fusion.1), channel_id=1, source_target_pairs={{0,2},{2,0},{4,6},{6,4},{8,10},{10,8},{12,14},{14,12},{1,3},{3,1},... | collective-permute-start | bytes 786440 | tf_op jit(solution)/shard_map/ppermute | solution.py:176
  80.4 14.7 %copy-start.18 = (s32[1,256]{1,0:T(1,128)S(1)}, s32[1,256]{1,0:T(1,128)}, u32[]{:S(2)}) copy-start(s32[1,256]{1,0:T(1,128)} %param.18) | copy-start | bytes 3076
  80.4 14.7 %copy-start.10 = (f32[4,2,1,16,64]{4,3,1,0,2:T(8,128)S(1)}, f32[4,2,1,16,64]{4,3,1,0,2:T(8,128)}, u32[]{:S(2)}) copy-start(f32[4,2,1,16,64]{4,3,1,0,2:T(8,128)} %copy.41) | copy-start | bytes 98308
  80.4 5.0 %collective-permute-start.20 = (f32[2,1,4,32,128]{4,3,2,0,1:T(8,128)S(1)}, f32[2,1,4,32,128]{4,3,2,0,1:T(8,128)S(1)}, u32[]{:S(2)}, u32[]{:S(2)}) collective-permute-start(f32[2,1,4,32,128]{4,3,2,0,1:T(8,128)S(1)} %dynamic-slice_bitcast_fusion.4), channel_id=1, source_target_pairs={{0,2},{2,0},{4,6},{6,4},{8,10},{10,8},{12,14},{14,12},{1,3},{3,1},... | collective-permute-start | bytes 393224 | tf_op jit(solution)/shard_map/ppermute | solution.py:176
  81.0 13.9 %collective-permute-start.21 = (f32[2,4,64,128]{3,2,1,0:T(8,128)S(1)}, f32[2,4,64,128]{3,2,1,0:T(8,128)S(1)}, u32[]{:S(2)}, u32[]{:S(2)}) collective-permute-start(f32[2,4,64,128]{3,2,1,0:T(8,128)S(1)} %constant_dynamic-update-slice_fusion), channel_id=1, source_target_pairs={{0,8},{2,10},{4,12},{6,14},{8,0},{10,2},{12,4},{14,6},{1,9},{3,11}... | collective-permute-start | bytes 786440 | tf_op jit(solution)/shard_map/ppermute | solution.py:145
  83.7 7.7 %collective-permute-start.19 = (f32[2,1,4,32,128]{4,3,2,0,1:T(8,128)S(1)}, f32[2,1,4,32,128]{4,3,2,0,1:T(8,128)S(1)}, u32[]{:S(2)}, u32[]{:S(2)}) collective-permute-start(f32[2,1,4,32,128]{4,3,2,0,1:T(8,128)S(1)} %dynamic-slice_bitcast_fusion.5), channel_id=1, source_target_pairs={{0,4},{2,6},{4,0},{6,2},{8,12},{10,14},{12,8},{14,10},{1,5},{3,7},... | collective-permute-start | bytes 393224 | tf_op jit(solution)/shard_map/ppermute | solution.py:176
  95.0 14.1 %collective-permute-start.22 = (f32[2,4,64,128]{3,2,1,0:T(8,128)S(1)}, f32[2,4,64,128]{3,2,1,0:T(8,128)S(1)}, u32[]{:S(2)}, u32[]{:S(2)}) collective-permute-start(f32[2,4,64,128]{3,2,1,0:T(8,128)S(1)} %constant_dynamic-update-slice_fusion.2), channel_id=1, source_target_pairs={{0,8},{2,10},{4,12},{6,14},{8,0},{10,2},{12,4},{14,6},{1,9},{3,11}... | collective-permute-start | bytes 786440 | tf_op jit(solution)/shard_map/ppermute | solution.py:145
  111.3 5.5 %collective-permute-start.24 = (f32[2,4,32,128]{3,2,1,0:T(8,128)S(1)}, f32[2,4,32,128]{3,2,1,0:T(8,128)S(1)}, u32[]{:S(2)}, u32[]{:S(2)}) collective-permute-start(f32[2,4,32,128]{3,2,1,0:T(8,128)S(1)} %get-tuple-element.134), channel_id=1, source_target_pairs={{0,2},{2,0},{4,6},{6,4},{8,10},{10,8},{12,14},{14,12},{1,3},{3,1},... | collective-permute-start | bytes 393224 | tf_op jit(solution)/shard_map/ppermute | solution.py:120
  112.5 5.1 %collective-permute-start.23 = (f32[2,4,32,128]{3,2,1,0:T(8,128)S(1)}, f32[2,4,32,128]{3,2,1,0:T(8,128)S(1)}, u32[]{:S(2)}, u32[]{:S(2)}) collective-permute-start(f32[2,4,32,128]{3,2,1,0:T(8,128)S(1)} %get-tuple-element.135), channel_id=1, source_target_pairs={{0,4},{2,6},{4,0},{6,2},{8,12},{10,14},{12,8},{14,10},{1,5},{3,7},... | collective-permute-start | bytes 393224 | tf_op jit(solution)/shard_map/ppermute | solution.py:120
  117.7 7.6 %collective-permute-start.26 = (f32[4,4,32,128]{3,2,1,0:T(8,128)S(1)}, f32[4,4,32,128]{3,2,1,0:T(8,128)S(1)}, u32[]{:S(2)}, u32[]{:S(2)}) collective-permute-start(f32[4,4,32,128]{3,2,1,0:T(8,128)S(1)} %bitcast.215), channel_id=1, source_target_pairs={{0,4},{2,6},{4,0},{6,2},{8,12},{10,14},{12,8},{14,10},{1,5},{3,7},... | collective-permute-start | bytes 786440 | tf_op jit(solution)/shard_map/ppermute | solution.py:120
  118.0 7.1 %collective-permute-start.25 = (f32[4,4,32,128]{3,2,1,0:T(8,128)S(1)}, f32[4,4,32,128]{3,2,1,0:T(8,128)S(1)}, u32[]{:S(2)}, u32[]{:S(2)}) collective-permute-start(f32[4,4,32,128]{3,2,1,0:T(8,128)S(1)} %bitcast.205), channel_id=1, source_target_pairs={{0,2},{2,0},{4,6},{6,4},{8,10},{10,8},{12,14},{14,12},{1,3},{3,1},... | collective-permute-start | bytes 786440 | tf_op jit(solution)/shard_map/ppermute | solution.py:120
  127.4 1.6 %collective-permute-start.27 = (f32[4,64,128]{2,1,0:T(8,128)}, f32[4,64,128]{2,1,0:T(8,128)S(1)}, u32[]{:S(2)}, u32[]{:S(2)}) collective-permute-start(f32[4,64,128]{2,1,0:T(8,128)} %constant_dynamic-slice_fusion), channel_id=1, source_target_pairs={{0,1},{1,0},{2,3},{3,2},{4,5},{5,4},{6,7},{7,6},{8,9},{9,8},{10,11... | collective-permute-start | bytes 393224 | tf_op jit(solution)/shard_map/ppermute | solution.py:52
  134.1 1.9 %collective-permute-start.28 = (f32[1,2,256]{2,1,0:T(2,128)S(1)}, f32[1,2,256]{2,1,0:T(2,128)S(1)}, u32[]{:S(2)}, u32[]{:S(2)}) collective-permute-start(f32[1,2,256]{2,1,0:T(2,128)S(1)} %maximum_bitcast_fusion), channel_id=1, source_target_pairs={{0,1},{1,0},{2,3},{3,2},{4,5},{5,4},{6,7},{7,6},{8,9},{9,8},{10,11... | collective-permute-start | bytes 6152 | tf_op jit(solution)/shard_map/ppermute | solution.py:353
  (19 other events, 85.6 us)

commit v11 on v9

--- a/solution.py
+++ b/solution.py
@@ -271,7 +271,7 @@
     model_c = chain(model_held, "ag", far_first[:1])
     gains_c = chain(gains_held, "ag", far_first)
     tasks = [task_wave(0), light_prep, task_wave(2)]
-    run_group([model_c, gains_c], tasks[0])
+    run_group([model_c], tasks[0])
     half_a, half_b = halves(model_c["held"], 1)
     model_a = chain(half_a, "ag", far_first[1:], [top])
     model_b = chain(half_b, "ag", swap_first(far_first[1:]), [top])
@@ -280,7 +280,6 @@
     for i in range(len(bits), len(tasks)):
         tasks[i]()
     model_held = jnp.concatenate([model_a["held"], model_b["held"]], axis=1)
-    gains_held = gains_c["held"]
     light_a, light_b = halves(st["light"].reshape(n_shot, slab, span_y, span_z), 2)
     light_a = chain(light_a, "rs", near_first[:-1], near_first)
     light_b = chain(light_b, "rs", swap_first(near_first[:-1]), near_first)
@@ -290,8 +289,9 @@
         st["born1"] = model * st["drive0"]
         st["born2"] = born_second(st["born1"], model, st["drive1"])
 
-    run_group([light_a, light_b], born_pass)
+    run_group([light_a, light_b, gains_c], born_pass)
     born1, born2 = st["born1"], st["born2"]
+    gains_held = gains_c["held"]
 
     image = st["drive0"] * born1 + st["drive1"] * born2
     image_a, image_b = halves(image.reshape(n_shot, slab, span_y, span_z), 2)
@@ -335,7 +335,14 @@
     filtered = lax.dynamic_slice_in_dim(new_model, me_shot * depth, depth, 2)
 
     b1 = new_model * st["drive2"]
-    b2 = born_second(b1, new_model, st["drive3"])
+    b1_padded = with_halo(b1)
+    filtered, b1_padded = barrier((filtered, b1_padded))
+    b2 = (
+        2.0 * b1
+        + speed_term * laplace_x(b1_padded)
+        - absorber * b1
+        + new_model * st["drive3"]
+    )
 
     receiver_local = receiver_index[0] - offset
     receiver_owned = (receiver_local >= 0) & (receiver_local < cells)

time: 133 us -> 136 us (1.023)
  local copies, waits for them, and re-layouts: 17.4 us -> 21.6 us
  waiting for transfers between devices: 46 us -> 41.8 us
  other arithmetic: 36.9 us -> 38.8 us
    add x0 -> x1, other arithmetic: none -> 3.58 us  [body(): 2.0 * b1 + speed_term * laplace_x(b1_padded) - absorber * b1]
    add x2 -> x1, other arithmetic: 5.85 us -> 2.94 us  [born_second(): 2.0 * born + speed_term * laplace_x(with_halo(born)) - absorber * born]
    ppermute x13, waiting for transfers between devices: 24.1 us -> 21.7 us  [ag_step(): theirs = lax.ppermute(held, 'shot', [(i, i ^ k) for i in range(n)])]
    gather x2, local copies, waits for them, and re-layouts: 1.87 us -> 4.26 us  [sample(): rows = jnp.take(field.reshape(span_x * span_y, span_z), row, axis=0)]
  transfers between devices with their start and end apart: 30 -> 30, of which waited for: 16 -> 15; matrix products, arithmetic and copies ran while one was open for 25% -> 27% of each run, Pallas kernels for 0% -> 0%
where the time goes in v11:
time: 136 us; the launch traced here: 135 us
  waiting for transfers between devices  41.8 us (31%)
  other arithmetic  38.8 us (29%)
  starting transfers between devices  25.9 us (19%)
  local copies, waits for them, and re-layouts  21.6 us (16%)
  between operations  4.89 us (4%)
  matrix products  1.7 us (1%)
    ppermute x13, waiting for transfers between devices, ag_step(): theirs = lax.ppermute(held, 'shot', [(i, i ^ k) for i in range(n)])  21.7 us
    ppermute x10, waiting for transfers between devices, rs_step(): got = lax.ppermute(send, 'shot', [(i, i ^ k) for i in range(n)])  20 us
    ppermute x13, starting transfers between devices, ag_step(): theirs = lax.ppermute(held, 'shot', [(i, i ^ k) for i in range(n)])  12.7 us
    ppermute x10, starting transfers between devices, rs_step(): got = lax.ppermute(send, 'shot', [(i, i ^ k) for i in range(n)])  11.7 us
    add x3, other arithmetic, inject(): return field + jnp.where(hit, source_gain[0] * wavelet[0, moment], 0.0)  11.6 us
    gather x2, local copies, waits for them, and re-layouts, sample(): rows = jnp.take(field.reshape(span_x * span_y, span_z), row, axis=0)  4.26 us
    another operation x1, other arithmetic, damping(): lower = jnp.stack([edges[0], edges[2], edges[4]])[:, None]  3.92 us
    add x1, other arithmetic, body(): 2.0 * b1 + speed_term * laplace_x(b1_padded) - absorber * b1  3.58 us
  transfers between devices with their start and end apart: 30, of which 15 were waited for; matrix products, arithmetic and copies ran while one was open for 27% of the time, Pallas kernels for 0%

profile of v11, /device:TPU:0, one launch (start us, length us, event | category | flops | bytes accessed | tf_op | source)
XLA Modules:
  0.0 134.7 jit_solution(14970638418621446961)
XLA Ops:
  0.7 1.7 %dynamic-slice_bitcast_fusion.10 = f32[4,64,128]{2,1,0:T(8,128)} fusion(f32[1,32,64,128]{3,2,1,0:T(8,128)} %param.12, s32[]{:T(128)S(6)} %select_n.402), kind=kLoop, calls=%fused_computation.354 | loop fusion | bytes 262148 | tf_op jit(solution)/shard_map/dynamic_slice | solution.py:51
  4.6 3.6 %collective-permute-start = (f32[1,16,2048]{2,1,0:T(8,128)}, f32[1,16,2048]{2,1,0:T(8,128)}, u32[]{:S(2)}, u32[]{:S(2)}) collective-permute-start(f32[1,16,2048]{2,1,0:T(8,128)} %concatenate.196), channel_id=1, source_target_pairs={{0,8},{2,10},{4,12},{6,14},{8,0},{10,2},{12,4},{14,6},{1,9},{3,11}... | collective-permute-start | bytes 393224 | tf_op jit(solution)/shard_map/ppermute | solution.py:120
  10.2 3.9 %pad_maximum_fusion.15 = (f32[3]{0:T(128)S(1)}, f32[3]{0:T(128)S(1)}) fusion(f32[1]{0:T(128)} %get-tuple-element.159, f32[1]{0:T(128)} %get-tuple-element.160, f32[1]{0:T(128)} %get-tuple-element.155, f32[1]{0:T(128)} %get-tuple-element.156, f32[1]{0:T(128)} %get-tuple-element.157, f32[1]{0:T(128)} %get-tuple-element.158), kind=kLoop, calls=%fused_computation.411 | loop fusion | flops 12 | bytes 48 | tf_op jit(solution)/shard_map/stack | solution.py:37
  22.5 4.5 %fusion.2 = (f32[32,64,128]{2,1,0:T(8,128)S(1)}, f32[32,64,128]{2,1,0:T(8,128)S(1)}) fusion(f32[]{:T(128)S(6)} %mul.319, f32[128]{0:T(128)} %slice_bitcast_fusion, f32[32,64]{1,0:T(8,128)S(1)} %broadcast_add_fusion, pred[128]{0:T(512)(128)(4,1)} %iota_compare_fusion.1, pred[32,64]{1,0:T(8,128)(4,1)} %broadcast_and_fusion, f32[1,32,64,128]{3,2,1,0:T(8,128)} %param.11, ...), kind=kLoop, calls=%fused_computation.118 | loop fusion | flops 12058624 | bytes 16009860 | tf_op jit(solution)/shard_map/add | solution.py:213
  28.5 1.7 %collective-permute-start.3 = (f32[2,8,2048]{2,1,0:T(8,128)S(1)}, f32[2,8,2048]{2,1,0:T(8,128)S(1)}, u32[]{:S(2)}, u32[]{:S(2)}) collective-permute-start(f32[2,8,2048]{2,1,0:T(8,128)S(1)} %get-tuple-element.148), channel_id=1, source_target_pairs={{0,2},{2,0},{4,6},{6,4},{8,10},{10,8},{12,14},{14,12},{1,3},{3,1},... | collective-permute-start | bytes 393224 | tf_op jit(solution)/shard_map/ppermute | solution.py:120
  30.2 1.6 %collective-permute-start.2 = (f32[2,8,2048]{2,1,0:T(8,128)S(1)}, f32[2,8,2048]{2,1,0:T(8,128)S(1)}, u32[]{:S(2)}, u32[]{:S(2)}) collective-permute-start(f32[2,8,2048]{2,1,0:T(8,128)S(1)} %get-tuple-element.149), channel_id=1, source_target_pairs={{0,4},{2,6},{4,0},{6,2},{8,12},{10,14},{12,8},{14,10},{1,5},{3,7},... | collective-permute-start | bytes 393224 | tf_op jit(solution)/shard_map/ppermute | solution.py:120
  32.0 2.4 %collective-permute-done.3 = f32[2,8,2048]{2,1,0:T(8,128)S(1)} collective-permute-done((f32[2,8,2048]{2,1,0:T(8,128)S(1)}, f32[2,8,2048]{2,1,0:T(8,128)S(1)}, u32[]{:S(2)}, u32[]{:S(2)}) %collective-permute-start.3) | collective-permute-done | bytes 131104 | tf_op jit(solution)/shard_map/ppermute | solution.py:120
  34.4 1.4 %collective-permute-done.2 = f32[2,8,2048]{2,1,0:T(8,128)S(1)} collective-permute-done((f32[2,8,2048]{2,1,0:T(8,128)S(1)}, f32[2,8,2048]{2,1,0:T(8,128)S(1)}, u32[]{:S(2)}, u32[]{:S(2)}) %collective-permute-start.2) | collective-permute-done | bytes 131104 | tf_op jit(solution)/shard_map/ppermute | solution.py:120
  35.9 3.2 %fusion.3 = (f32[32,64,128]{2,1,0:T(8,128)S(1)}, f32[32,64,128]{2,1,0:T(8,128)S(1)}) fusion(f32[32,64,128]{2,1,0:T(8,128)S(1)} %get-tuple-element.71, f32[32,64,128]{2,1,0:T(8,128)S(1)} %bitcast.200, f32[]{:T(128)S(6)} %mul.330, f32[128]{0:T(128)S(1)} %copy-done.14, f32[32,64]{1,0:T(8,128)S(1)} %broadcast_add_fusion, pred[128]{0:T(512)(128)(4,1)S(1)} %copy-done.17, ...), kind=kLoop, calls=%fused_computation.119 | loop fusion | flops 12058624 | bytes 16012292 | tf_op jit(solution)/shard_map/add | solution.py:213
  40.3 1.6 %collective-permute-start.8 = (f32[2,16,64]{2,1,0:T(8,128)S(1)}, f32[2,16,64]{2,1,0:T(8,128)S(1)}, u32[]{:S(2)}, u32[]{:S(2)}) collective-permute-start(f32[2,16,64]{2,1,0:T(8,128)S(1)} %maximum_select_fusion.12), channel_id=1, source_target_pairs={{0,4},{2,6},{4,0},{6,2},{8,12},{10,14},{12,8},{14,10},{1,5},{3,7},... | collective-permute-start | bytes 24584 | tf_op jit(solution)/shard_map/ppermute | solution.py:120
  44.8 4.0 %fusion.4 = (f32[32,64,128]{2,1,0:T(8,128)}, f32[32,64,128]{2,1,0:T(8,128)}) fusion(f32[32,64,128]{2,1,0:T(8,128)S(1)} %get-tuple-element.69, f32[32,64,128]{2,1,0:T(8,128)S(1)} %get-tuple-element.71, f32[]{:T(128)S(6)} %mul.339, f32[128]{0:T(128)S(1)} %copy-done.14, f32[32,64]{1,0:T(8,128)S(1)} %broadcast_add_fusion, pred[128]{0:T(512)(128)(4,1)S(1)} %copy-done.17, ...), kind=kLoop, calls=%fused_computation.120 | loop fusion | flops 12058624 | bytes 16012292 | tf_op jit(solution)/shard_map/add | solution.py:213
  48.8 1.8 %collective-permute-done.7 = f32[4,8,2048]{2,1,0:T(8,128)S(1)} collective-permute-done((f32[4,8,2048]{2,1,0:T(8,128)S(1)}, f32[4,8,2048]{2,1,0:T(8,128)S(1)}, u32[]{:S(2)}, u32[]{:S(2)}) %collective-permute-start.7) | collective-permute-done | bytes 262176 | tf_op jit(solution)/shard_map/ppermute | solution.py:120
  51.9 2.5 %copy.46 = f32[2048,128]{1,0:T(8,128)} copy(f32[2048,128]{0,1:T(8,128)} %bitcast.208) | data formatting | bytes 2097152 | tf_op jit(solution)/shard_map/transpose | solution.py:288
  54.4 1.4 %mul.340 = f32[32,64,128]{2,1,0:T(8,128)S(1)} multiply(f32[32,64,128]{2,1,0:T(8,128)} %bitcast.202, f32[32,64,128]{2,1,0:T(8,128)S(1)} %get-tuple-element.80) | non-fusion elementwise | flops 262144 | bytes 3145728 | tf_op jit(solution)/shard_map/mul | solution.py:289
  57.2 1.7 %collective-permute-start.11 = (f32[2,2,4,32,128]{4,3,2,1,0:T(8,128)S(1)}, f32[2,2,4,32,128]{4,3,2,1,0:T(8,128)S(1)}, u32[]{:S(2)}, u32[]{:S(2)}) collective-permute-start(f32[2,2,4,32,128]{4,3,2,1,0:T(8,128)S(1)} %dynamic-slice_bitcast_fusion.2), channel_id=1, source_target_pairs={{0,4},{2,6},{4,0},{6,2},{8,12},{10,14},{12,8},{14,10},{1,5},{3,7},... | collective-permute-start | bytes 786440 | tf_op jit(solution)/shard_map/ppermute | solution.py:169
  58.9 1.6 %collective-permute-start.10 = (f32[4,1,4,32,128]{4,3,2,0,1:T(8,128)S(1)}, f32[4,1,4,32,128]{4,3,2,0,1:T(8,128)S(1)}, u32[]{:S(2)}, u32[]{:S(2)}) collective-permute-start(f32[4,1,4,32,128]{4,3,2,0,1:T(8,128)S(1)} %dynamic-slice_bitcast_fusion.3), channel_id=1, source_target_pairs={{0,2},{2,0},{4,6},{6,4},{8,10},{10,8},{12,14},{14,12},{1,3},{3,1},... | collective-permute-start | bytes 786440 | tf_op jit(solution)/shard_map/ppermute | solution.py:169
  61.2 2.9 %fusion.92 = f32[32,64,128]{2,1,0:T(8,128)S(1)} fusion(f32[40,64,128]{2,1,0:T(8,128)S(1)} %constant_dynamic-update-slice_fusion.2, f32[32,64,128]{2,1,0:T(8,128)S(1)} %bitcast.203, f32[32,64,128]{2,1,0:T(8,128)S(1)} %get-tuple-element.82, f32[32,64,128]{2,1,0:T(8,128)S(1)} %mul.340, f32[128]{0:T(128)S(1)} %copy-done.15, f32[32,64]{1,0:T(8,128)S(1)} %broadcast_add_fusion, ...), kind=kLoop, calls=%fused_computation.208 | loop fusion | flops 11272192 | bytes 16007680 | tf_op jit(solution)/shard_map/add | solution.py:224
  65.2 1.4 %collective-permute-done.10 = f32[4,1,4,32,128]{4,3,2,0,1:T(8,128)S(1)} collective-permute-done((f32[4,1,4,32,128]{4,3,2,0,1:T(8,128)S(1)}, f32[4,1,4,32,128]{4,3,2,0,1:T(8,128)S(1)}, u32[]{:S(2)}, u32[]{:S(2)}) %collective-permute-start.10) | collective-permute-done | bytes 262176 | tf_op jit(solution)/shard_map/ppermute | solution.py:169
  66.8 1.6 %collective-permute-start.17 = (f32[2,1,4,32,128]{4,3,2,0,1:T(8,128)S(1)}, f32[2,1,4,32,128]{4,3,2,0,1:T(8,128)S(1)}, u32[]{:S(2)}, u32[]{:S(2)}) collective-permute-start(f32[2,1,4,32,128]{4,3,2,0,1:T(8,128)S(1)} %dynamic-slice_bitcast_fusion.8), channel_id=1, source_target_pairs={{0,2},{2,0},{4,6},{6,4},{8,10},{10,8},{12,14},{14,12},{1,3},{3,1},... | collective-permute-start | bytes 393224 | tf_op jit(solution)/shard_map/ppermute | solution.py:169
  69.5 1.6 %collective-permute-start.15 = (f32[2,2,4,32,128]{4,3,2,1,0:T(8,128)S(1)}, f32[2,2,4,32,128]{4,3,2,1,0:T(8,128)S(1)}, u32[]{:S(2)}, u32[]{:S(2)}) collective-permute-start(f32[2,2,4,32,128]{4,3,2,1,0:T(8,128)S(1)} %dynamic-slice_bitcast_fusion), channel_id=1, source_target_pairs={{0,4},{2,6},{4,0},{6,2},{8,12},{10,14},{12,8},{14,10},{1,5},{3,7},... | collective-permute-start | bytes 786440 | tf_op jit(solution)/shard_map/ppermute | solution.py:169
  71.9 3.2 %fusion.117 = f32[32,64,128]{2,1,0:T(8,128)} fusion(f32[40,64,128]{2,1,0:T(8,128)S(1)} %constant_dynamic-update-slice_fusion.1, s32[32,64,128]{2,1,0:T(8,128)S(1)} %copy-done), kind=kLoop, calls=%fused_computation.233 | loop fusion | flops 9175040 | bytes 12845056 | tf_op jit(solution)/shard_map/mul | solution.py:216
  75.2 4.5 %collective-permute-done.15 = f32[2,2,4,32,128]{4,3,2,1,0:T(8,128)S(1)} collective-permute-done((f32[2,2,4,32,128]{4,3,2,1,0:T(8,128)S(1)}, f32[2,2,4,32,128]{4,3,2,1,0:T(8,128)S(1)}, u32[]{:S(2)}, u32[]{:S(2)}) %collective-permute-start.15) | collective-permute-done | bytes 262176 | tf_op jit(solution)/shard_map/ppermute | solution.py:169
  80.5 2.7 %collective-permute-start.21 = (f32[1,1,4,64,128]{4,3,2,1,0:T(8,128)S(1)}, f32[1,1,4,64,128]{4,3,2,1,0:T(8,128)S(1)}, u32[]{:S(2)}, u32[]{:S(2)}) collective-permute-start(f32[1,1,4,64,128]{4,3,2,1,0:T(8,128)S(1)} %dynamic-slice_bitcast_fusion.5), channel_id=1, source_target_pairs={{0,8},{2,10},{4,12},{6,14},{8,0},{10,2},{12,4},{14,6},{1,9},{3,11}... | collective-permute-start | bytes 393224 | tf_op jit(solution)/shard_map/ppermute | solution.py:169
  84.9 5.0 %collective-permute-done.19 = f32[2,1,4,32,128]{4,3,2,0,1:T(8,128)S(1)} collective-permute-done((f32[2,1,4,32,128]{4,3,2,0,1:T(8,128)S(1)}, f32[2,1,4,32,128]{4,3,2,0,1:T(8,128)S(1)}, u32[]{:S(2)}, u32[]{:S(2)}) %collective-permute-start.19) | collective-permute-done | bytes 131104 | tf_op jit(solution)/shard_map/ppermute | solution.py:169
  90.2 7.2 %collective-permute-done.22 = f32[1,1,4,64,128]{4,3,2,1,0:T(8,128)S(1)} collective-permute-done((f32[1,1,4,64,128]{4,3,2,1,0:T(8,128)S(1)}, f32[1,1,4,64,128]{4,3,2,1,0:T(8,128)S(1)}, u32[]{:S(2)}, u32[]{:S(2)}) %collective-permute-start.22) | collective-permute-done | bytes 131104 | tf_op jit(solution)/shard_map/ppermute | solution.py:169
  99.2 7.0 %collective-permute-done.23 = f32[1,4,64,128]{3,2,1,0:T(8,128)S(1)} collective-permute-done((f32[1,4,64,128]{3,2,1,0:T(8,128)S(1)}, f32[1,4,64,128]{3,2,1,0:T(8,128)S(1)}, u32[]{:S(2)}, u32[]{:S(2)}) %collective-permute-start.23) | collective-permute-done | bytes 131104 | tf_op jit(solution)/shard_map/ppermute | solution.py:120
  107.4 4.0 %collective-permute-done.25 = f32[2,4,32,128]{3,2,1,0:T(8,128)S(1)} collective-permute-done((f32[2,4,32,128]{3,2,1,0:T(8,128)S(1)}, f32[2,4,32,128]{3,2,1,0:T(8,128)S(1)}, u32[]{:S(2)}, u32[]{:S(2)}) %collective-permute-start.25) | collective-permute-done | bytes 131104 | tf_op jit(solution)/shard_map/ppermute | solution.py:120
  111.9 2.2 %collective-permute-start.26 = (f32[4,4,32,128]{3,2,1,0:T(8,128)S(1)}, f32[4,4,32,128]{3,2,1,0:T(8,128)S(1)}, u32[]{:S(2)}, u32[]{:S(2)}) collective-permute-start(f32[4,4,32,128]{3,2,1,0:T(8,128)S(1)} %bitcast.235), channel_id=1, source_target_pairs={{0,2},{2,0},{4,6},{6,4},{8,10},{10,8},{12,14},{14,12},{1,3},{3,1},... | collective-permute-start | bytes 786440 | tf_op jit(solution)/shard_map/ppermute | solution.py:120
  115.3 3.5 %collective-permute-done.26 = f32[4,4,32,128]{3,2,1,0:T(8,128)S(1)} collective-permute-done((f32[4,4,32,128]{3,2,1,0:T(8,128)S(1)}, f32[4,4,32,128]{3,2,1,0:T(8,128)S(1)}, u32[]{:S(2)}, u32[]{:S(2)}) %collective-permute-start.26) | collective-permute-done | bytes 262176 | tf_op jit(solution)/shard_map/ppermute | solution.py:120
  121.4 2.1 %gather_fusion = f32[256,128]{1,0:T(8,128)S(1)} fusion(f32[2048,128]{1,0:T(8,128)} %bitcast.201, s32[1024]{0:T(1024)} %pad_clamp_fusion), kind=kCustom, calls=%fused_computation.clone | custom fusion | bytes 263168 | tf_op jit(solution)/shard_map/jit(_take)/gather | solution.py:355
  125.8 3.6 %fusion.145 = f32[32,64,128]{2,1,0:T(8,128)} fusion(f32[40,64,128]{2,1,0:T(8,128)S(1)} %constant_dynamic-update-slice_fusion, f32[32,64,128]{2,1,0:T(8,128)S(1)} %copy-done.8, f32[128]{0:T(128)S(1)} %copy-done.16, f32[32,64]{1,0:T(8,128)S(1)} %broadcast_add_fusion, f32[8,4,64,128]{3,2,1,0:T(8,128)S(1)} %pad_maximum_fusion.13, ...), kind=kLoop, calls=%fused_computation.261 | loop fusion | flops 11534336 | bytes 16007680 | tf_op jit(solution)/shard_map/add | solution.py:341
  129.4 2.2 %gather_fusion.1 = f32[256,128]{1,0:T(8,128)S(1)} fusion(f32[2048,128]{1,0:T(8,128)} %bitcast.205, s32[1024]{0:T(1024)} %pad_clamp_fusion), kind=kCustom, calls=%fused_computation.1.clone | custom fusion | bytes 263168 | tf_op jit(solution)/shard_map/jit(_take)/gather | solution.py:355
  (189 shorter events, 36.7 us)
Async XLA Ops:
  0.6 15.6 %copy-start.1 = (f32[1,32,64,128]{3,2,1,0:T(8,128)S(1)}, f32[1,32,64,128]{3,2,1,0:T(8,128)}, u32[]{:S(2)}) copy-start(f32[1,32,64,128]{3,2,1,0:T(8,128)} %param.12) | copy-start | bytes 3145732
  0.7 14.2 %copy-start.18 = (f32[1,4]{1,0:T(1,128)S(1)}, f32[1,4]{1,0:T(1,128)}, u32[]{:S(2)}) copy-start(f32[1,4]{1,0:T(1,128)} %param.16) | copy-start | bytes 52
  2.3 19.2 %collective-permute-start.1 = (f32[4,64,128]{2,1,0:T(8,128)}, f32[4,64,128]{2,1,0:T(8,128)}, u32[]{:S(2)}, u32[]{:S(2)}) collective-permute-start(f32[4,64,128]{2,1,0:T(8,128)} %dynamic-slice_bitcast_fusion.10), channel_id=1, source_target_pairs={{0,1},{1,0},{2,3},{3,2},{4,5},{5,4},{6,7},{7,6},{8,9},{9,8},{10,11... | collective-permute-start | bytes 393224 | tf_op jit(solution)/shard_map/ppermute | solution.py:52
  4.6 22.4 %collective-permute-start = (f32[1,16,2048]{2,1,0:T(8,128)}, f32[1,16,2048]{2,1,0:T(8,128)}, u32[]{:S(2)}, u32[]{:S(2)}) collective-permute-start(f32[1,16,2048]{2,1,0:T(8,128)} %concatenate.196), channel_id=1, source_target_pairs={{0,8},{2,10},{4,12},{6,14},{8,0},{10,2},{12,4},{14,6},{1,9},{3,11}... | collective-permute-start | bytes 393224 | tf_op jit(solution)/shard_map/ppermute | solution.py:120
  8.2 12.6 %collective-permute-start.4 = (f32[1,16,64]{2,1,0:T(8,128)}, f32[1,16,64]{2,1,0:T(8,128)}, u32[]{:S(2)}, u32[]{:S(2)}) collective-permute-start(f32[1,16,64]{2,1,0:T(8,128)} %bitcast.254), channel_id=1, source_target_pairs={{0,8},{2,10},{4,12},{6,14},{8,0},{10,2},{12,4},{14,6},{1,9},{3,11}... | collective-permute-start | bytes 12296 | tf_op jit(solution)/shard_map/ppermute | solution.py:120
  28.2 7.7 %collective-permute-start.5 = (f32[4,64,128]{2,1,0:T(8,128)S(1)}, f32[4,64,128]{2,1,0:T(8,128)S(1)}, u32[]{:S(2)}, u32[]{:S(2)}) collective-permute-start(f32[4,64,128]{2,1,0:T(8,128)S(1)} %constant_dynamic-slice_fusion.5), channel_id=1, source_target_pairs={{0,1},{1,0},{2,3},{3,2},{4,5},{5,4},{6,7},{7,6},{8,9},{9,8},{10,11... | collective-permute-start | bytes 393224 | tf_op jit(solution)/shard_map/ppermute | solution.py:52
  28.5 5.8 %collective-permute-start.3 = (f32[2,8,2048]{2,1,0:T(8,128)S(1)}, f32[2,8,2048]{2,1,0:T(8,128)S(1)}, u32[]{:S(2)}, u32[]{:S(2)}) collective-permute-start(f32[2,8,2048]{2,1,0:T(8,128)S(1)} %get-tuple-element.148), channel_id=1, source_target_pairs={{0,2},{2,0},{4,6},{6,4},{8,10},{10,8},{12,14},{14,12},{1,3},{3,1},... | collective-permute-start | bytes 393224 | tf_op jit(solution)/shard_map/ppermute | solution.py:120
  30.2 5.6 %collective-permute-start.2 = (f32[2,8,2048]{2,1,0:T(8,128)S(1)}, f32[2,8,2048]{2,1,0:T(8,128)S(1)}, u32[]{:S(2)}, u32[]{:S(2)}) collective-permute-start(f32[2,8,2048]{2,1,0:T(8,128)S(1)} %get-tuple-element.149), channel_id=1, source_target_pairs={{0,4},{2,6},{4,0},{6,2},{8,12},{10,14},{12,8},{14,10},{1,5},{3,7},... | collective-permute-start | bytes 393224 | tf_op jit(solution)/shard_map/ppermute | solution.py:120
  40.3 4.5 %collective-permute-start.9 = (f32[4,64,128]{2,1,0:T(8,128)S(1)}, f32[4,64,128]{2,1,0:T(8,128)S(1)}, u32[]{:S(2)}, u32[]{:S(2)}) collective-permute-start(f32[4,64,128]{2,1,0:T(8,128)S(1)} %constant_dynamic-slice_fusion.4), channel_id=1, source_target_pairs={{0,1},{1,0},{2,3},{3,2},{4,5},{5,4},{6,7},{7,6},{8,9},{9,8},{10,11... | collective-permute-start | bytes 393224 | tf_op jit(solution)/shard_map/ppermute | solution.py:52
  40.3 3.8 %collective-permute-start.8 = (f32[2,16,64]{2,1,0:T(8,128)S(1)}, f32[2,16,64]{2,1,0:T(8,128)S(1)}, u32[]{:S(2)}, u32[]{:S(2)}) collective-permute-start(f32[2,16,64]{2,1,0:T(8,128)S(1)} %maximum_select_fusion.12), channel_id=1, source_target_pairs={{0,4},{2,6},{4,0},{6,2},{8,12},{10,14},{12,8},{14,10},{1,5},{3,7},... | collective-permute-start | bytes 24584 | tf_op jit(solution)/shard_map/ppermute | solution.py:120
  42.1 8.4 %collective-permute-start.7 = (f32[4,8,2048]{2,1,0:T(8,128)S(1)}, f32[4,8,2048]{2,1,0:T(8,128)S(1)}, u32[]{:S(2)}, u32[]{:S(2)}) collective-permute-start(f32[4,8,2048]{2,1,0:T(8,128)S(1)} %bitcast.221), channel_id=1, source_target_pairs={{0,4},{2,6},{4,0},{6,2},{8,12},{10,14},{12,8},{14,10},{1,5},{3,7},... | collective-permute-start | bytes 786440 | tf_op jit(solution)/shard_map/ppermute | solution.py:120
  42.7 8.1 %collective-permute-start.6 = (f32[4,8,2048]{2,1,0:T(8,128)S(1)}, f32[4,8,2048]{2,1,0:T(8,128)S(1)}, u32[]{:S(2)}, u32[]{:S(2)}) collective-permute-start(f32[4,8,2048]{2,1,0:T(8,128)S(1)} %bitcast.223), channel_id=1, source_target_pairs={{0,2},{2,0},{4,6},{6,4},{8,10},{10,8},{12,14},{14,12},{1,3},{3,1},... | collective-permute-start | bytes 786440 | tf_op jit(solution)/shard_map/ppermute | solution.py:120
  56.0 5.1 %collective-permute-start.13 = (f32[4,64,128]{2,1,0:T(8,128)S(1)}, f32[4,64,128]{2,1,0:T(8,128)S(1)}, u32[]{:S(2)}, u32[]{:S(2)}) collective-permute-start(f32[4,64,128]{2,1,0:T(8,128)S(1)} %constant_dynamic-slice_fusion.3), channel_id=1, source_target_pairs={{0,1},{1,0},{2,3},{3,2},{4,5},{5,4},{6,7},{7,6},{8,9},{9,8},{10,11... | collective-permute-start | bytes 393224 | tf_op jit(solution)/shard_map/ppermute | solution.py:52
  56.6 3.9 %collective-permute-start.12 = (f32[4,16,64]{2,1,0:T(8,128)S(1)}, f32[4,16,64]{2,1,0:T(8,128)S(1)}, u32[]{:S(2)}, u32[]{:S(2)}) collective-permute-start(f32[4,16,64]{2,1,0:T(8,128)S(1)} %bitcast.247), channel_id=1, source_target_pairs={{0,2},{2,0},{4,6},{6,4},{8,10},{10,8},{12,14},{14,12},{1,3},{3,1},... | collective-permute-start | bytes 49160 | tf_op jit(solution)/shard_map/ppermute | solution.py:120
  57.2 8.0 %collective-permute-start.11 = (f32[2,2,4,32,128]{4,3,2,1,0:T(8,128)S(1)}, f32[2,2,4,32,128]{4,3,2,1,0:T(8,128)S(1)}, u32[]{:S(2)}, u32[]{:S(2)}) collective-permute-start(f32[2,2,4,32,128]{4,3,2,1,0:T(8,128)S(1)} %dynamic-slice_bitcast_fusion.2), channel_id=1, source_target_pairs={{0,4},{2,6},{4,0},{6,2},{8,12},{10,14},{12,8},{14,10},{1,5},{3,7},... | collective-permute-start | bytes 786440 | tf_op jit(solution)/shard_map/ppermute | solution.py:169
  58.9 7.7 %collective-permute-start.10 = (f32[4,1,4,32,128]{4,3,2,0,1:T(8,128)S(1)}, f32[4,1,4,32,128]{4,3,2,0,1:T(8,128)S(1)}, u32[]{:S(2)}, u32[]{:S(2)}) collective-permute-start(f32[4,1,4,32,128]{4,3,2,0,1:T(8,128)S(1)} %dynamic-slice_bitcast_fusion.3), channel_id=1, source_target_pairs={{0,2},{2,0},{4,6},{6,4},{8,10},{10,8},{12,14},{14,12},{1,3},{3,1},... | collective-permute-start | bytes 786440 | tf_op jit(solution)/shard_map/ppermute | solution.py:169
  66.7 5.2 %collective-permute-start.18 = (f32[4,64,128]{2,1,0:T(8,128)S(1)}, f32[4,64,128]{2,1,0:T(8,128)S(1)}, u32[]{:S(2)}, u32[]{:S(2)}) collective-permute-start(f32[4,64,128]{2,1,0:T(8,128)S(1)} %constant_dynamic-slice_fusion.2), channel_id=1, source_target_pairs={{0,1},{1,0},{2,3},{3,2},{4,5},{5,4},{6,7},{7,6},{8,9},{9,8},{10,11... | collective-permute-start | bytes 393224 | tf_op jit(solution)/shard_map/ppermute | solution.py:52
  66.8 8.3 %collective-permute-start.17 = (f32[2,1,4,32,128]{4,3,2,0,1:T(8,128)S(1)}, f32[2,1,4,32,128]{4,3,2,0,1:T(8,128)S(1)}, u32[]{:S(2)}, u32[]{:S(2)}) collective-permute-start(f32[2,1,4,32,128]{4,3,2,0,1:T(8,128)S(1)} %dynamic-slice_bitcast_fusion.8), channel_id=1, source_target_pairs={{0,2},{2,0},{4,6},{6,4},{8,10},{10,8},{12,14},{14,12},{1,3},{3,1},... | collective-permute-start | bytes 393224 | tf_op jit(solution)/shard_map/ppermute | solution.py:169
  68.4 6.8 %collective-permute-start.16 = (f32[2,1,4,32,128]{4,3,2,0,1:T(8,128)S(1)}, f32[2,1,4,32,128]{4,3,2,0,1:T(8,128)S(1)}, u32[]{:S(2)}, u32[]{:S(2)}) collective-permute-start(f32[2,1,4,32,128]{4,3,2,0,1:T(8,128)S(1)} %dynamic-slice_bitcast_fusion.9), channel_id=1, source_target_pairs={{0,4},{2,6},{4,0},{6,2},{8,12},{10,14},{12,8},{14,10},{1,5},{3,7},... | collective-permute-start | bytes 393224 | tf_op jit(solution)/shard_map/ppermute | solution.py:169
  69.5 10.2 %collective-permute-start.15 = (f32[2,2,4,32,128]{4,3,2,1,0:T(8,128)S(1)}, f32[2,2,4,32,128]{4,3,2,1,0:T(8,128)S(1)}, u32[]{:S(2)}, u32[]{:S(2)}) collective-permute-start(f32[2,2,4,32,128]{4,3,2,1,0:T(8,128)S(1)} %dynamic-slice_bitcast_fusion), channel_id=1, source_target_pairs={{0,4},{2,6},{4,0},{6,2},{8,12},{10,14},{12,8},{14,10},{1,5},{3,7},... | collective-permute-start | bytes 786440 | tf_op jit(solution)/shard_map/ppermute | solution.py:169
  71.1 8.6 %collective-permute-start.14 = (f32[4,1,4,32,128]{4,3,2,0,1:T(8,128)S(1)}, f32[4,1,4,32,128]{4,3,2,0,1:T(8,128)S(1)}, u32[]{:S(2)}, u32[]{:S(2)}) collective-permute-start(f32[4,1,4,32,128]{4,3,2,0,1:T(8,128)S(1)} %dynamic-slice_bitcast_fusion.1), channel_id=1, source_target_pairs={{0,2},{2,0},{4,6},{6,4},{8,10},{10,8},{12,14},{14,12},{1,3},{3,1},... | collective-permute-start | bytes 786440 | tf_op jit(solution)/shard_map/ppermute | solution.py:169
  79.8 5.0 %collective-permute-start.20 = (f32[2,1,4,32,128]{4,3,2,0,1:T(8,128)S(1)}, f32[2,1,4,32,128]{4,3,2,0,1:T(8,128)S(1)}, u32[]{:S(2)}, u32[]{:S(2)}) collective-permute-start(f32[2,1,4,32,128]{4,3,2,0,1:T(8,128)S(1)} %dynamic-slice_bitcast_fusion.6), channel_id=1, source_target_pairs={{0,2},{2,0},{4,6},{6,4},{8,10},{10,8},{12,14},{14,12},{1,3},{3,1},... | collective-permute-start | bytes 393224 | tf_op jit(solution)/shard_map/ppermute | solution.py:169
  80.5 9.5 %collective-permute-start.21 = (f32[1,1,4,64,128]{4,3,2,1,0:T(8,128)S(1)}, f32[1,1,4,64,128]{4,3,2,1,0:T(8,128)S(1)}, u32[]{:S(2)}, u32[]{:S(2)}) collective-permute-start(f32[1,1,4,64,128]{4,3,2,1,0:T(8,128)S(1)} %dynamic-slice_bitcast_fusion.5), channel_id=1, source_target_pairs={{0,8},{2,10},{4,12},{6,14},{8,0},{10,2},{12,4},{14,6},{1,9},{3,11}... | collective-permute-start | bytes 393224 | tf_op jit(solution)/shard_map/ppermute | solution.py:169
  83.1 6.8 %collective-permute-start.19 = (f32[2,1,4,32,128]{4,3,2,0,1:T(8,128)S(1)}, f32[2,1,4,32,128]{4,3,2,0,1:T(8,128)S(1)}, u32[]{:S(2)}, u32[]{:S(2)}) collective-permute-start(f32[2,1,4,32,128]{4,3,2,0,1:T(8,128)S(1)} %dynamic-slice_bitcast_fusion.7), channel_id=1, source_target_pairs={{0,4},{2,6},{4,0},{6,2},{8,12},{10,14},{12,8},{14,10},{1,5},{3,7},... | collective-permute-start | bytes 393224 | tf_op jit(solution)/shard_map/ppermute | solution.py:169
  90.1 7.3 %collective-permute-start.22 = (f32[1,1,4,64,128]{4,3,2,1,0:T(8,128)S(1)}, f32[1,1,4,64,128]{4,3,2,1,0:T(8,128)S(1)}, u32[]{:S(2)}, u32[]{:S(2)}) collective-permute-start(f32[1,1,4,64,128]{4,3,2,1,0:T(8,128)S(1)} %dynamic-slice_bitcast_fusion.4), channel_id=1, source_target_pairs={{0,8},{2,10},{4,12},{6,14},{8,0},{10,2},{12,4},{14,6},{1,9},{3,11}... | collective-permute-start | bytes 393224 | tf_op jit(solution)/shard_map/ppermute | solution.py:169
  99.1 7.2 %collective-permute-start.23 = (f32[1,4,64,128]{3,2,1,0:T(8,128)S(1)}, f32[1,4,64,128]{3,2,1,0:T(8,128)S(1)}, u32[]{:S(2)}, u32[]{:S(2)}) collective-permute-start(f32[1,4,64,128]{3,2,1,0:T(8,128)S(1)} %fusion.1), channel_id=1, source_target_pairs={{0,8},{2,10},{4,12},{6,14},{8,0},{10,2},{12,4},{14,6},{1,9},{3,11}... | collective-permute-start | bytes 393224 | tf_op jit(solution)/shard_map/ppermute | solution.py:120
  106.4 5.0 %collective-permute-start.25 = (f32[2,4,32,128]{3,2,1,0:T(8,128)S(1)}, f32[2,4,32,128]{3,2,1,0:T(8,128)S(1)}, u32[]{:S(2)}, u32[]{:S(2)}) collective-permute-start(f32[2,4,32,128]{3,2,1,0:T(8,128)S(1)} %get-tuple-element.144), channel_id=1, source_target_pairs={{0,2},{2,0},{4,6},{6,4},{8,10},{10,8},{12,14},{14,12},{1,3},{3,1},... | collective-permute-start | bytes 393224 | tf_op jit(solution)/shard_map/ppermute | solution.py:120
  106.8 5.0 %collective-permute-start.24 = (f32[2,4,32,128]{3,2,1,0:T(8,128)S(1)}, f32[2,4,32,128]{3,2,1,0:T(8,128)S(1)}, u32[]{:S(2)}, u32[]{:S(2)}) collective-permute-start(f32[2,4,32,128]{3,2,1,0:T(8,128)S(1)} %get-tuple-element.145), channel_id=1, source_target_pairs={{0,4},{2,6},{4,0},{6,2},{8,12},{10,14},{12,8},{14,10},{1,5},{3,7},... | collective-permute-start | bytes 393224 | tf_op jit(solution)/shard_map/ppermute | solution.py:120
  111.9 7.0 %collective-permute-start.27 = (f32[4,4,32,128]{3,2,1,0:T(8,128)S(1)}, f32[4,4,32,128]{3,2,1,0:T(8,128)S(1)}, u32[]{:S(2)}, u32[]{:S(2)}) collective-permute-start(f32[4,4,32,128]{3,2,1,0:T(8,128)S(1)} %bitcast.229), channel_id=1, source_target_pairs={{0,4},{2,6},{4,0},{6,2},{8,12},{10,14},{12,8},{14,10},{1,5},{3,7},... | collective-permute-start | bytes 786440 | tf_op jit(solution)/shard_map/ppermute | solution.py:120
  111.9 6.9 %collective-permute-start.26 = (f32[4,4,32,128]{3,2,1,0:T(8,128)S(1)}, f32[4,4,32,128]{3,2,1,0:T(8,128)S(1)}, u32[]{:S(2)}, u32[]{:S(2)}) collective-permute-start(f32[4,4,32,128]{3,2,1,0:T(8,128)S(1)} %bitcast.235), channel_id=1, source_target_pairs={{0,2},{2,0},{4,6},{6,4},{8,10},{10,8},{12,14},{14,12},{1,3},{3,1},... | collective-permute-start | bytes 786440 | tf_op jit(solution)/shard_map/ppermute | solution.py:120
  121.4 3.4 %collective-permute-start.28 = (f32[4,64,128]{2,1,0:T(8,128)}, f32[4,64,128]{2,1,0:T(8,128)}, u32[]{:S(2)}, u32[]{:S(2)}) collective-permute-start(f32[4,64,128]{2,1,0:T(8,128)} %constant_dynamic-slice_fusion), channel_id=1, source_target_pairs={{0,1},{1,0},{2,3},{3,2},{4,5},{5,4},{6,7},{7,6},{8,9},{9,8},{10,11... | collective-permute-start | bytes 393224 | tf_op jit(solution)/shard_map/ppermute | solution.py:52
  132.5 1.6 %collective-permute-start.29 = (f32[1,2,256]{2,1,0:T(2,128)S(1)}, f32[1,2,256]{2,1,0:T(2,128)S(1)}, u32[]{:S(2)}, u32[]{:S(2)}) collective-permute-start(f32[1,2,256]{2,1,0:T(2,128)S(1)} %maximum_bitcast_fusion), channel_id=1, source_target_pairs={{0,1},{1,0},{2,3},{3,2},{4,5},{5,4},{6,7},{7,6},{8,9},{9,8},{10,11... | collective-permute-start | bytes 6152 | tf_op jit(solution)/shard_map/ppermute | solution.py:360
  (20 other events, 78.0 us)

commit v12 on v8

--- a/solution.py
+++ b/solution.py
@@ -270,27 +270,32 @@
     top = far_first[0]
     model_c = chain(model_held, "ag", far_first[:1])
     gains_c = chain(gains_held, "ag", far_first)
-    tasks = [task_wave(0), light_prep, task_wave(2)]
+    def first_steps():
+        task_wave(0)()
+        light_prep()
+
+    tasks = [first_steps, task_wave(2)]
     run_group([model_c, gains_c], tasks[0])
     half_a, half_b = halves(model_c["held"], 1)
     model_a = chain(half_a, "ag", far_first[1:], [top])
     model_b = chain(half_b, "ag", swap_first(far_first[1:]), [top])
+    light_a, light_b = halves(st["light"].reshape(n_shot, slab, span_y, span_z), 2)
+    light_a = chain(light_a, "rs", near_first[:-1], near_first)
+    light_b = chain(light_b, "rs", swap_first(near_first[:-1]), near_first)
     for i in range(1, len(bits)):
-        run_group([model_a, model_b, gains_c], tasks[i] if i < len(tasks) else nothing)
+        run_group([model_a, model_b, gains_c, light_a, light_b], tasks[i] if i < len(tasks) else nothing)
     for i in range(len(bits), len(tasks)):
         tasks[i]()
     model_held = jnp.concatenate([model_a["held"], model_b["held"]], axis=1)
     gains_held = gains_c["held"]
-    light_a, light_b = halves(st["light"].reshape(n_shot, slab, span_y, span_z), 2)
-    light_a = chain(light_a, "rs", near_first[:-1], near_first)
-    light_b = chain(light_b, "rs", swap_first(near_first[:-1]), near_first)
+    light_c = chain(jnp.concatenate([light_a["held"], light_b["held"]], axis=2), "rs", near_first[-1:], near_first[-1:])
 
     def born_pass():
         model = model_held.reshape(span_z, span_x * span_y).T.reshape(span_x, span_y, span_z)
         st["born1"] = model * st["drive0"]
         st["born2"] = born_second(st["born1"], model, st["drive1"])
 
-    run_group([light_a, light_b], born_pass)
+    run_group([light_c], born_pass)
     born1, born2 = st["born1"], st["born2"]
 
     image = st["drive0"] * born1 + st["drive1"] * born2
@@ -299,20 +304,15 @@
     image_b = chain(image_b, "rs", swap_first(near_first[:-1]), near_first)
     tasks = [task_wave(3)]
     for i in range(len(bits) - 1):
-        run_group([image_a, image_b, light_a, light_b], tasks[i] if i < len(tasks) else nothing)
+        run_group([image_a, image_b], tasks[i] if i < len(tasks) else nothing)
     for i in range(len(bits) - 1, len(tasks)):
         tasks[i]()
-    both = jnp.concatenate(
-        [
-            jnp.concatenate([image_a["held"], image_b["held"]], axis=2),
-            jnp.concatenate([light_a["held"], light_b["held"]], axis=2),
-        ],
-        axis=1,
-    )
-    last = chain(both, "rs", near_first[-1:], near_first[-1:])
+    last = chain(
+        jnp.concatenate([image_a["held"], image_b["held"]], axis=2), "rs", near_first[-1:], near_first[-1:]
+    )
     run_group([last], nothing)
-    image_part = last["held"][0, :slab]
-    light_part = last["held"][0, slab:]
+    image_part = last["held"][0]
+    light_part = light_c["held"][0]
 
     table_all = gains_held.reshape(n_shot * gains.shape[0], gains.shape[1])
     filt_part = lateral_filter(image_part / (light_part + eps), table_all)

time: 135 us -> 134 us (level)
  waiting for transfers between devices: 47.7 us -> 39.7 us
  starting transfers between devices: 25.5 us -> 30.9 us
  local copies, waits for them, and re-layouts: 17.2 us -> 18.7 us
    ppermute x9 -> x10, waiting for transfers between devices: 22.7 us -> 16.6 us  [rs_step(): got = lax.ppermute(send, 'shot', [(i, i ^ k) for i in range(n)])]
    ppermute x9 -> x10, starting transfers between devices: 11.3 us -> 16.5 us  [rs_step(): got = lax.ppermute(send, 'shot', [(i, i ^ k) for i in range(n)])]
    reshape x7 -> x8, other arithmetic: 0.18 us -> 2.14 us  [rs_step(): return (keep + got).reshape((high * low,) + held.shape[1:])]
    ppermute x13, waiting for transfers between devices: 24.5 us -> 22.6 us  [ag_step(): theirs = lax.ppermute(held, 'shot', [(i, i ^ k) for i in range(n)])]
    unnamed x45 -> x53, local copies, waits for them, and re-layouts: 3.56 us -> 4.94 us
  transfers between devices with their start and end apart: 29 -> 30, of which waited for: 16 -> 15; matrix products, arithmetic and copies ran while one was open for 25% -> 27% of each run, Pallas kernels for 0% -> 0%
where the time goes in v12:
time: 134 us
  waiting for transfers between devices  39.7 us (30%)
  other arithmetic  37.9 us (28%)
  starting transfers between devices  30.9 us (23%)
  local copies, waits for them, and re-layouts  18.7 us (14%)
  between operations  4.82 us (4%)
  matrix products  1.7 us (1%)
    ppermute x13, waiting for transfers between devices, ag_step(): theirs = lax.ppermute(held, 'shot', [(i, i ^ k) for i in range(n)])  22.6 us
    ppermute x10, waiting for transfers between devices, rs_step(): got = lax.ppermute(send, 'shot', [(i, i ^ k) for i in range(n)])  16.6 us
    ppermute x10, starting transfers between devices, rs_step(): got = lax.ppermute(send, 'shot', [(i, i ^ k) for i in range(n)])  16.5 us
    ppermute x13, starting transfers between devices, ag_step(): theirs = lax.ppermute(held, 'shot', [(i, i ^ k) for i in range(n)])  12.6 us
    add x3, other arithmetic, inject(): return field + jnp.where(hit, source_gain[0] * wavelet[0, moment], 0.0)  11.8 us
    add x2, other arithmetic, born_second(): 2.0 * born + speed_term * laplace_x(with_halo(born)) - absorber * born  5.85 us
    unnamed x53, local copies, waits for them, and re-layouts  4.94 us
    another operation x1, other arithmetic, damping(): lower = jnp.stack([edges[0], edges[2], edges[4]])[:, None]  3.85 us
  transfers between devices with their start and end apart: 30, of which 15 were waited for; matrix products, arithmetic and copies ran while one was open for 27% of the time, Pallas kernels for 0%

profile of v12, /device:TPU:0, one launch (start us, length us, event | category | flops | bytes accessed | tf_op | source)
XLA Modules:
  0.0 133.7 jit_solution(319447324381519406)
XLA Ops:
  0.7 1.7 %dynamic-slice_bitcast_fusion.10 = f32[4,64,128]{2,1,0:T(8,128)} fusion(f32[1,32,64,128]{3,2,1,0:T(8,128)} %param.12, s32[]{:T(128)S(6)} %select_n.404), kind=kLoop, calls=%fused_computation.360 | loop fusion | bytes 262148 | tf_op jit(solution)/shard_map/dynamic_slice | solution.py:51
  4.6 3.6 %collective-permute-start = (f32[1,16,2048]{2,1,0:T(8,128)}, f32[1,16,2048]{2,1,0:T(8,128)}, u32[]{:S(2)}, u32[]{:S(2)}) collective-permute-start(f32[1,16,2048]{2,1,0:T(8,128)} %concatenate.196), channel_id=1, source_target_pairs={{0,8},{2,10},{4,12},{6,14},{8,0},{10,2},{12,4},{14,6},{1,9},{3,11}... | collective-permute-start | bytes 393224 | tf_op jit(solution)/shard_map/ppermute | solution.py:120
  10.2 3.9 %pad_maximum_fusion.15 = (f32[3]{0:T(128)S(1)}, f32[3]{0:T(128)S(1)}) fusion(f32[1]{0:T(128)} %get-tuple-element.158, f32[1]{0:T(128)} %get-tuple-element.159, f32[1]{0:T(128)} %get-tuple-element.154, f32[1]{0:T(128)} %get-tuple-element.155, f32[1]{0:T(128)} %get-tuple-element.156, f32[1]{0:T(128)} %get-tuple-element.157), kind=kLoop, calls=%fused_computation.417 | loop fusion | flops 12 | bytes 48 | tf_op jit(solution)/shard_map/stack | solution.py:37
  22.3 4.5 %fusion.2 = (f32[32,64,128]{2,1,0:T(8,128)S(1)}, f32[32,64,128]{2,1,0:T(8,128)S(1)}) fusion(f32[]{:T(128)S(6)} %mul.319, f32[128]{0:T(128)} %slice_bitcast_fusion, f32[32,64]{1,0:T(8,128)S(1)} %broadcast_add_fusion, pred[128]{0:T(512)(128)(4,1)} %iota_compare_fusion.1, pred[32,64]{1,0:T(8,128)(4,1)} %broadcast_and_fusion, f32[1,32,64,128]{3,2,1,0:T(8,128)} %param.11, ...), kind=kLoop, calls=%fused_computation.118 | loop fusion | flops 12058624 | bytes 16009860 | tf_op jit(solution)/shard_map/add | solution.py:213
  29.8 3.2 %fusion.3 = (f32[32,64,128]{2,1,0:T(8,128)S(1)}, f32[32,64,128]{2,1,0:T(8,128)S(1)}) fusion(f32[]{:T(128)S(6)} %mul.330, f32[]{:T(128)S(6)} %mul.319, f32[128]{0:T(128)S(1)} %copy-done.15, f32[32,64]{1,0:T(8,128)S(1)} %broadcast_add_fusion, f32[32,64,128]{2,1,0:T(8,128)S(1)} %get-tuple-element.82, pred[128]{0:T(512)(128)(4,1)S(1)} %copy-done.18, ...), kind=kLoop, calls=%fused_computation.119 | loop fusion | flops 14155776 | bytes 17060872 | tf_op jit(solution)/shard_map/add | solution.py:213
  33.8 1.9 %collective-permute-start.8 = (f32[2,2,4,32,128]{4,3,2,1,0:T(8,128)S(1)}, f32[2,2,4,32,128]{4,3,2,1,0:T(8,128)S(1)}, u32[]{:S(2)}, u32[]{:S(2)}) collective-permute-start(f32[2,2,4,32,128]{4,3,2,1,0:T(8,128)S(1)} %dynamic-slice_bitcast_fusion.2), channel_id=1, source_target_pairs={{0,4},{2,6},{4,0},{6,2},{8,12},{10,14},{12,8},{14,10},{1,5},{3,7},... | collective-permute-start | bytes 786440 | tf_op jit(solution)/shard_map/ppermute | solution.py:169
  35.8 1.6 %collective-permute-start.7 = (f32[4,1,4,32,128]{4,3,2,0,1:T(8,128)S(1)}, f32[4,1,4,32,128]{4,3,2,0,1:T(8,128)S(1)}, u32[]{:S(2)}, u32[]{:S(2)}) collective-permute-start(f32[4,1,4,32,128]{4,3,2,0,1:T(8,128)S(1)} %dynamic-slice_bitcast_fusion.3), channel_id=1, source_target_pairs={{0,2},{2,0},{4,6},{6,4},{8,10},{10,8},{12,14},{14,12},{1,3},{3,1},... | collective-permute-start | bytes 786440 | tf_op jit(solution)/shard_map/ppermute | solution.py:169
  38.1 4.5 %collective-permute-done.6 = f32[2,16,64]{2,1,0:T(8,128)S(1)} collective-permute-done((f32[2,16,64]{2,1,0:T(8,128)S(1)}, f32[2,16,64]{2,1,0:T(8,128)S(1)}, u32[]{:S(2)}, u32[]{:S(2)}) %collective-permute-start.6) | collective-permute-done | bytes 8224 | tf_op jit(solution)/shard_map/ppermute | solution.py:120
  42.7 1.7 %collective-permute-start.4 = (f32[2,8,2048]{2,1,0:T(8,128)S(1)}, f32[2,8,2048]{2,1,0:T(8,128)S(1)}, u32[]{:S(2)}, u32[]{:S(2)}) collective-permute-start(f32[2,8,2048]{2,1,0:T(8,128)S(1)} %get-tuple-element.148), channel_id=1, source_target_pairs={{0,4},{2,6},{4,0},{6,2},{8,12},{10,14},{12,8},{14,10},{1,5},{3,7},... | collective-permute-start | bytes 393224 | tf_op jit(solution)/shard_map/ppermute | solution.py:120
  44.4 4.0 %fusion.4 = (f32[32,64,128]{2,1,0:T(8,128)}, f32[32,64,128]{2,1,0:T(8,128)}) fusion(f32[32,64,128]{2,1,0:T(8,128)S(1)} %get-tuple-element.63, f32[32,64,128]{2,1,0:T(8,128)S(1)} %get-tuple-element.64, f32[]{:T(128)S(6)} %mul.339, f32[128]{0:T(128)S(1)} %copy-done.15, f32[32,64]{1,0:T(8,128)S(1)} %broadcast_add_fusion, pred[128]{0:T(512)(128)(4,1)S(1)} %copy-done.18, ...), kind=kLoop, calls=%fused_computation.120 | loop fusion | flops 12058624 | bytes 16012292 | tf_op jit(solution)/shard_map/add | solution.py:213
  48.7 1.6 %collective-permute-start.14 = (f32[2,1,4,32,128]{4,3,2,0,1:T(8,128)S(1)}, f32[2,1,4,32,128]{4,3,2,0,1:T(8,128)S(1)}, u32[]{:S(2)}, u32[]{:S(2)}) collective-permute-start(f32[2,1,4,32,128]{4,3,2,0,1:T(8,128)S(1)} %dynamic-slice_bitcast_fusion.8), channel_id=1, source_target_pairs={{0,2},{2,0},{4,6},{6,4},{8,10},{10,8},{12,14},{14,12},{1,3},{3,1},... | collective-permute-start | bytes 393224 | tf_op jit(solution)/shard_map/ppermute | solution.py:169
  52.9 1.5 %collective-permute-start.10 = (f32[4,8,2048]{2,1,0:T(8,128)S(1)}, f32[4,8,2048]{2,1,0:T(8,128)S(1)}, u32[]{:S(2)}, u32[]{:S(2)}) collective-permute-start(f32[4,8,2048]{2,1,0:T(8,128)S(1)} %bitcast.218), channel_id=1, source_target_pairs={{0,2},{2,0},{4,6},{6,4},{8,10},{10,8},{12,14},{14,12},{1,3},{3,1},... | collective-permute-start | bytes 786440 | tf_op jit(solution)/shard_map/ppermute | solution.py:120
  58.0 2.2 %collective-permute-done.11 = f32[4,8,2048]{2,1,0:T(8,128)S(1)} collective-permute-done((f32[4,8,2048]{2,1,0:T(8,128)S(1)}, f32[4,8,2048]{2,1,0:T(8,128)S(1)}, u32[]{:S(2)}, u32[]{:S(2)}) %collective-permute-start.11) | collective-permute-done | bytes 262176 | tf_op jit(solution)/shard_map/ppermute | solution.py:120
  61.5 2.5 %copy.66 = f32[2048,128]{1,0:T(8,128)} copy(f32[2048,128]{0,1:T(8,128)} %bitcast.205) | data formatting | bytes 2097152 | tf_op jit(solution)/shard_map/transpose | solution.py:294
  64.0 1.4 %mul.340 = f32[32,64,128]{2,1,0:T(8,128)S(1)} multiply(f32[32,64,128]{2,1,0:T(8,128)} %bitcast.199, f32[32,64,128]{2,1,0:T(8,128)S(1)} %get-tuple-element.82) | non-fusion elementwise | flops 262144 | bytes 3145728 | tf_op jit(solution)/shard_map/mul | solution.py:295
  65.6 2.7 %collective-permute-start.15 = (f32[1,1,4,64,128]{4,3,2,1,0:T(8,128)S(1)}, f32[1,1,4,64,128]{4,3,2,1,0:T(8,128)S(1)}, u32[]{:S(2)}, u32[]{:S(2)}) collective-permute-start(f32[1,1,4,64,128]{4,3,2,1,0:T(8,128)S(1)} %dynamic-slice_bitcast_fusion.7), channel_id=1, source_target_pairs={{0,8},{2,10},{4,12},{6,14},{8,0},{10,2},{12,4},{14,6},{1,9},{3,11}... | collective-permute-start | bytes 393224 | tf_op jit(solution)/shard_map/ppermute | solution.py:169
  68.5 2.9 %fusion.92 = f32[32,64,128]{2,1,0:T(8,128)S(1)} fusion(f32[40,64,128]{2,1,0:T(8,128)S(1)} %constant_dynamic-update-slice_fusion.2, f32[32,64,128]{2,1,0:T(8,128)S(1)} %bitcast.200, f32[32,64,128]{2,1,0:T(8,128)S(1)} %get-tuple-element.84, f32[32,64,128]{2,1,0:T(8,128)S(1)} %mul.340, f32[128]{0:T(128)S(1)} %copy-done.16, f32[32,64]{1,0:T(8,128)S(1)} %broadcast_add_fusion, ...), kind=kLoop, calls=%fused_computation.208 | loop fusion | flops 11272192 | bytes 16007680 | tf_op jit(solution)/shard_map/add | solution.py:224
  71.5 3.8 %collective-permute-done.15 = f32[1,1,4,64,128]{4,3,2,1,0:T(8,128)S(1)} collective-permute-done((f32[1,1,4,64,128]{4,3,2,1,0:T(8,128)S(1)}, f32[1,1,4,64,128]{4,3,2,1,0:T(8,128)S(1)}, u32[]{:S(2)}, u32[]{:S(2)}) %collective-permute-start.15) | collective-permute-done | bytes 131104 | tf_op jit(solution)/shard_map/ppermute | solution.py:169
  76.7 1.5 %collective-permute-start.17 = (f32[4,1,4,32,128]{4,3,2,0,1:T(8,128)S(1)}, f32[4,1,4,32,128]{4,3,2,0,1:T(8,128)S(1)}, u32[]{:S(2)}, u32[]{:S(2)}) collective-permute-start(f32[4,1,4,32,128]{4,3,2,0,1:T(8,128)S(1)} %dynamic-slice_bitcast_fusion.1), channel_id=1, source_target_pairs={{0,2},{2,0},{4,6},{6,4},{8,10},{10,8},{12,14},{14,12},{1,3},{3,1},... | collective-permute-start | bytes 786440 | tf_op jit(solution)/shard_map/ppermute | solution.py:169
  78.4 3.2 %fusion.117 = f32[32,64,128]{2,1,0:T(8,128)} fusion(f32[40,64,128]{2,1,0:T(8,128)S(1)} %constant_dynamic-update-slice_fusion.1, s32[32,64,128]{2,1,0:T(8,128)S(1)} %copy-done), kind=kLoop, calls=%fused_computation.233 | loop fusion | flops 9175040 | bytes 12845056 | tf_op jit(solution)/shard_map/mul | solution.py:216
  81.7 3.7 %collective-permute-done.18 = f32[2,2,4,32,128]{4,3,2,1,0:T(8,128)S(1)} collective-permute-done((f32[2,2,4,32,128]{4,3,2,1,0:T(8,128)S(1)}, f32[2,2,4,32,128]{4,3,2,1,0:T(8,128)S(1)}, u32[]{:S(2)}, u32[]{:S(2)}) %collective-permute-start.18) | collective-permute-done | bytes 262176 | tf_op jit(solution)/shard_map/ppermute | solution.py:169
  85.6 1.5 %collective-permute-start.21 = (f32[2,1,4,32,128]{4,3,2,0,1:T(8,128)S(1)}, f32[2,1,4,32,128]{4,3,2,0,1:T(8,128)S(1)}, u32[]{:S(2)}, u32[]{:S(2)}) collective-permute-start(f32[2,1,4,32,128]{4,3,2,0,1:T(8,128)S(1)} %dynamic-slice_bitcast_fusion.5), channel_id=1, source_target_pairs={{0,2},{2,0},{4,6},{6,4},{8,10},{10,8},{12,14},{14,12},{1,3},{3,1},... | collective-permute-start | bytes 393224 | tf_op jit(solution)/shard_map/ppermute | solution.py:169
  87.0 1.8 %collective-permute-start.20 = (f32[2,1,4,32,128]{4,3,2,0,1:T(8,128)S(1)}, f32[2,1,4,32,128]{4,3,2,0,1:T(8,128)S(1)}, u32[]{:S(2)}, u32[]{:S(2)}) collective-permute-start(f32[2,1,4,32,128]{4,3,2,0,1:T(8,128)S(1)} %dynamic-slice_bitcast_fusion.6), channel_id=1, source_target_pairs={{0,4},{2,6},{4,0},{6,2},{8,12},{10,14},{12,8},{14,10},{1,5},{3,7},... | collective-permute-start | bytes 393224 | tf_op jit(solution)/shard_map/ppermute | solution.py:169
  88.8 1.9 %collective-permute-done.21 = f32[2,1,4,32,128]{4,3,2,0,1:T(8,128)S(1)} collective-permute-done((f32[2,1,4,32,128]{4,3,2,0,1:T(8,128)S(1)}, f32[2,1,4,32,128]{4,3,2,0,1:T(8,128)S(1)}, u32[]{:S(2)}, u32[]{:S(2)}) %collective-permute-start.21) | collective-permute-done | bytes 131104 | tf_op jit(solution)/shard_map/ppermute | solution.py:169
  90.8 1.3 collective-permute-done.20
  92.2 2.9 %collective-permute-start.22 = (f32[1,1,4,64,128]{4,3,2,1,0:T(8,128)S(1)}, f32[1,1,4,64,128]{4,3,2,1,0:T(8,128)S(1)}, u32[]{:S(2)}, u32[]{:S(2)}) collective-permute-start(f32[1,1,4,64,128]{4,3,2,1,0:T(8,128)S(1)} %dynamic-slice_bitcast_fusion.4), channel_id=1, source_target_pairs={{0,8},{2,10},{4,12},{6,14},{8,0},{10,2},{12,4},{14,6},{1,9},{3,11}... | collective-permute-start | bytes 393224 | tf_op jit(solution)/shard_map/ppermute | solution.py:169
  95.2 4.7 %collective-permute-done.22 = f32[1,1,4,64,128]{4,3,2,1,0:T(8,128)S(1)} collective-permute-done((f32[1,1,4,64,128]{4,3,2,1,0:T(8,128)S(1)}, f32[1,1,4,64,128]{4,3,2,1,0:T(8,128)S(1)}, u32[]{:S(2)}, u32[]{:S(2)}) %collective-permute-start.22) | collective-permute-done | bytes 131104 | tf_op jit(solution)/shard_map/ppermute | solution.py:169
  102.9 5.8 %collective-permute-done.23 = f32[1,4,64,128]{3,2,1,0:T(8,128)S(1)} collective-permute-done((f32[1,4,64,128]{3,2,1,0:T(8,128)S(1)}, f32[1,4,64,128]{3,2,1,0:T(8,128)S(1)}, u32[]{:S(2)}, u32[]{:S(2)}) %collective-permute-start.23) | collective-permute-done | bytes 131104 | tf_op jit(solution)/shard_map/ppermute | solution.py:120
  109.9 5.1 %collective-permute-done.25 = f32[2,4,32,128]{3,2,1,0:T(8,128)S(1)} collective-permute-done((f32[2,4,32,128]{3,2,1,0:T(8,128)S(1)}, f32[2,4,32,128]{3,2,1,0:T(8,128)S(1)}, u32[]{:S(2)}, u32[]{:S(2)}) %collective-permute-start.25) | collective-permute-done | bytes 131104 | tf_op jit(solution)/shard_map/ppermute | solution.py:120
  115.8 1.6 %collective-permute-start.26 = (f32[4,4,32,128]{3,2,1,0:T(8,128)S(1)}, f32[4,4,32,128]{3,2,1,0:T(8,128)S(1)}, u32[]{:S(2)}, u32[]{:S(2)}) collective-permute-start(f32[4,4,32,128]{3,2,1,0:T(8,128)S(1)} %bitcast.228), channel_id=1, source_target_pairs={{0,2},{2,0},{4,6},{6,4},{8,10},{10,8},{12,14},{14,12},{1,3},{3,1},... | collective-permute-start | bytes 786440 | tf_op jit(solution)/shard_map/ppermute | solution.py:120
  118.6 3.7 %collective-permute-done.26 = f32[4,4,32,128]{3,2,1,0:T(8,128)S(1)} collective-permute-done((f32[4,4,32,128]{3,2,1,0:T(8,128)S(1)}, f32[4,4,32,128]{3,2,1,0:T(8,128)S(1)}, u32[]{:S(2)}, u32[]{:S(2)}) %collective-permute-start.26) | collective-permute-done | bytes 262176 | tf_op jit(solution)/shard_map/ppermute | solution.py:120
  127.0 2.9 %fusion.145 = f32[32,64,128]{2,1,0:T(8,128)S(1)} fusion(f32[40,64,128]{2,1,0:T(8,128)S(1)} %constant_dynamic-update-slice_fusion, f32[32,64,128]{2,1,0:T(8,128)S(1)} %copy-done.8, f32[128]{0:T(128)S(1)} %copy-done.17, f32[32,64]{1,0:T(8,128)S(1)} %broadcast_add_fusion, f32[8,4,64,128]{3,2,1,0:T(8,128)S(1)} %pad_maximum_fusion.13, ...), kind=kLoop, calls=%fused_computation.261 | loop fusion | flops 11534336 | bytes 16007680 | tf_op jit(solution)/shard_map/add | solution.py:224
  (195 shorter events, 37.9 us)
Async XLA Ops:
  0.6 15.5 %copy-start.1 = (f32[1,32,64,128]{3,2,1,0:T(8,128)S(1)}, f32[1,32,64,128]{3,2,1,0:T(8,128)}, u32[]{:S(2)}) copy-start(f32[1,32,64,128]{3,2,1,0:T(8,128)} %param.12) | copy-start | bytes 3145732
  2.3 19.0 %collective-permute-start.2 = (f32[4,64,128]{2,1,0:T(8,128)}, f32[4,64,128]{2,1,0:T(8,128)}, u32[]{:S(2)}, u32[]{:S(2)}) collective-permute-start(f32[4,64,128]{2,1,0:T(8,128)} %dynamic-slice_bitcast_fusion.10), channel_id=1, source_target_pairs={{0,1},{1,0},{2,3},{3,2},{4,5},{5,4},{6,7},{7,6},{8,9},{9,8},{10,11... | collective-permute-start | bytes 393224 | tf_op jit(solution)/shard_map/ppermute | solution.py:52
  4.6 22.5 %collective-permute-start = (f32[1,16,2048]{2,1,0:T(8,128)}, f32[1,16,2048]{2,1,0:T(8,128)}, u32[]{:S(2)}, u32[]{:S(2)}) collective-permute-start(f32[1,16,2048]{2,1,0:T(8,128)} %concatenate.196), channel_id=1, source_target_pairs={{0,8},{2,10},{4,12},{6,14},{8,0},{10,2},{12,4},{14,6},{1,9},{3,11}... | collective-permute-start | bytes 393224 | tf_op jit(solution)/shard_map/ppermute | solution.py:120
  8.2 12.4 %collective-permute-start.1 = (f32[1,16,64]{2,1,0:T(8,128)}, f32[1,16,64]{2,1,0:T(8,128)}, u32[]{:S(2)}, u32[]{:S(2)}) collective-permute-start(f32[1,16,64]{2,1,0:T(8,128)} %bitcast.251), channel_id=1, source_target_pairs={{0,8},{2,10},{4,12},{6,14},{8,0},{10,2},{12,4},{14,6},{1,9},{3,11}... | collective-permute-start | bytes 12296 | tf_op jit(solution)/shard_map/ppermute | solution.py:120
  26.8 1.6 %collective-permute-start.3 = (f32[4,64,128]{2,1,0:T(8,128)S(1)}, f32[4,64,128]{2,1,0:T(8,128)S(1)}, u32[]{:S(2)}, u32[]{:S(2)}) collective-permute-start(f32[4,64,128]{2,1,0:T(8,128)S(1)} %constant_dynamic-slice_fusion.5), channel_id=1, source_target_pairs={{0,1},{1,0},{2,3},{3,2},{4,5},{5,4},{6,7},{7,6},{8,9},{9,8},{10,11... | collective-permute-start | bytes 393224 | tf_op jit(solution)/shard_map/ppermute | solution.py:52
  33.3 11.0 %collective-permute-start.9 = (f32[4,64,128]{2,1,0:T(8,128)S(1)}, f32[4,64,128]{2,1,0:T(8,128)S(1)}, u32[]{:S(2)}, u32[]{:S(2)}) collective-permute-start(f32[4,64,128]{2,1,0:T(8,128)S(1)} %constant_dynamic-slice_fusion.4), channel_id=1, source_target_pairs={{0,1},{1,0},{2,3},{3,2},{4,5},{5,4},{6,7},{7,6},{8,9},{9,8},{10,11... | collective-permute-start | bytes 393224 | tf_op jit(solution)/shard_map/ppermute | solution.py:52
  33.8 14.7 %collective-permute-start.8 = (f32[2,2,4,32,128]{4,3,2,1,0:T(8,128)S(1)}, f32[2,2,4,32,128]{4,3,2,1,0:T(8,128)S(1)}, u32[]{:S(2)}, u32[]{:S(2)}) collective-permute-start(f32[2,2,4,32,128]{4,3,2,1,0:T(8,128)S(1)} %dynamic-slice_bitcast_fusion.2), channel_id=1, source_target_pairs={{0,4},{2,6},{4,0},{6,2},{8,12},{10,14},{12,8},{14,10},{1,5},{3,7},... | collective-permute-start | bytes 786440 | tf_op jit(solution)/shard_map/ppermute | solution.py:169
  35.8 12.8 %collective-permute-start.7 = (f32[4,1,4,32,128]{4,3,2,0,1:T(8,128)S(1)}, f32[4,1,4,32,128]{4,3,2,0,1:T(8,128)S(1)}, u32[]{:S(2)}, u32[]{:S(2)}) collective-permute-start(f32[4,1,4,32,128]{4,3,2,0,1:T(8,128)S(1)} %dynamic-slice_bitcast_fusion.3), channel_id=1, source_target_pairs={{0,2},{2,0},{4,6},{6,4},{8,10},{10,8},{12,14},{14,12},{1,3},{3,1},... | collective-permute-start | bytes 786440 | tf_op jit(solution)/shard_map/ppermute | solution.py:169
  37.4 5.3 %collective-permute-start.6 = (f32[2,16,64]{2,1,0:T(8,128)S(1)}, f32[2,16,64]{2,1,0:T(8,128)S(1)}, u32[]{:S(2)}, u32[]{:S(2)}) collective-permute-start(f32[2,16,64]{2,1,0:T(8,128)S(1)} %maximum_select_fusion.12), channel_id=1, source_target_pairs={{0,4},{2,6},{4,0},{6,2},{8,12},{10,14},{12,8},{14,10},{1,5},{3,7},... | collective-permute-start | bytes 24584 | tf_op jit(solution)/shard_map/ppermute | solution.py:120
  37.8 10.6 %collective-permute-start.5 = (f32[2,8,2048]{2,1,0:T(8,128)S(1)}, f32[2,8,2048]{2,1,0:T(8,128)S(1)}, u32[]{:S(2)}, u32[]{:S(2)}) collective-permute-start(f32[2,8,2048]{2,1,0:T(8,128)S(1)} %get-tuple-element.147), channel_id=1, source_target_pairs={{0,2},{2,0},{4,6},{6,4},{8,10},{10,8},{12,14},{14,12},{1,3},{3,1},... | collective-permute-start | bytes 393224 | tf_op jit(solution)/shard_map/ppermute | solution.py:120
  42.7 5.8 %collective-permute-start.4 = (f32[2,8,2048]{2,1,0:T(8,128)S(1)}, f32[2,8,2048]{2,1,0:T(8,128)S(1)}, u32[]{:S(2)}, u32[]{:S(2)}) collective-permute-start(f32[2,8,2048]{2,1,0:T(8,128)S(1)} %get-tuple-element.148), channel_id=1, source_target_pairs={{0,4},{2,6},{4,0},{6,2},{8,12},{10,14},{12,8},{14,10},{1,5},{3,7},... | collective-permute-start | bytes 393224 | tf_op jit(solution)/shard_map/ppermute | solution.py:120
  48.7 6.9 %collective-permute-start.14 = (f32[2,1,4,32,128]{4,3,2,0,1:T(8,128)S(1)}, f32[2,1,4,32,128]{4,3,2,0,1:T(8,128)S(1)}, u32[]{:S(2)}, u32[]{:S(2)}) collective-permute-start(f32[2,1,4,32,128]{4,3,2,0,1:T(8,128)S(1)} %dynamic-slice_bitcast_fusion.8), channel_id=1, source_target_pairs={{0,2},{2,0},{4,6},{6,4},{8,10},{10,8},{12,14},{14,12},{1,3},{3,1},... | collective-permute-start | bytes 393224 | tf_op jit(solution)/shard_map/ppermute | solution.py:169
  50.3 4.6 %collective-permute-start.12 = (f32[4,16,64]{2,1,0:T(8,128)S(1)}, f32[4,16,64]{2,1,0:T(8,128)S(1)}, u32[]{:S(2)}, u32[]{:S(2)}) collective-permute-start(f32[4,16,64]{2,1,0:T(8,128)S(1)} %bitcast.244), channel_id=1, source_target_pairs={{0,2},{2,0},{4,6},{6,4},{8,10},{10,8},{12,14},{14,12},{1,3},{3,1},... | collective-permute-start | bytes 49160 | tf_op jit(solution)/shard_map/ppermute | solution.py:120
  50.8 6.5 %collective-permute-start.13 = (f32[2,1,4,32,128]{4,3,2,0,1:T(8,128)S(1)}, f32[2,1,4,32,128]{4,3,2,0,1:T(8,128)S(1)}, u32[]{:S(2)}, u32[]{:S(2)}) collective-permute-start(f32[2,1,4,32,128]{4,3,2,0,1:T(8,128)S(1)} %dynamic-slice_bitcast_fusion.9), channel_id=1, source_target_pairs={{0,4},{2,6},{4,0},{6,2},{8,12},{10,14},{12,8},{14,10},{1,5},{3,7},... | collective-permute-start | bytes 393224 | tf_op jit(solution)/shard_map/ppermute | solution.py:169
  51.7 8.5 %collective-permute-start.11 = (f32[4,8,2048]{2,1,0:T(8,128)S(1)}, f32[4,8,2048]{2,1,0:T(8,128)S(1)}, u32[]{:S(2)}, u32[]{:S(2)}) collective-permute-start(f32[4,8,2048]{2,1,0:T(8,128)S(1)} %bitcast.220), channel_id=1, source_target_pairs={{0,4},{2,6},{4,0},{6,2},{8,12},{10,14},{12,8},{14,10},{1,5},{3,7},... | collective-permute-start | bytes 786440 | tf_op jit(solution)/shard_map/ppermute | solution.py:120
  52.9 7.4 %collective-permute-start.10 = (f32[4,8,2048]{2,1,0:T(8,128)S(1)}, f32[4,8,2048]{2,1,0:T(8,128)S(1)}, u32[]{:S(2)}, u32[]{:S(2)}) collective-permute-start(f32[4,8,2048]{2,1,0:T(8,128)S(1)} %bitcast.218), channel_id=1, source_target_pairs={{0,2},{2,0},{4,6},{6,4},{8,10},{10,8},{12,14},{14,12},{1,3},{3,1},... | collective-permute-start | bytes 786440 | tf_op jit(solution)/shard_map/ppermute | solution.py:120
  65.4 3.0 %collective-permute-start.16 = (f32[4,64,128]{2,1,0:T(8,128)S(1)}, f32[4,64,128]{2,1,0:T(8,128)S(1)}, u32[]{:S(2)}, u32[]{:S(2)}) collective-permute-start(f32[4,64,128]{2,1,0:T(8,128)S(1)} %constant_dynamic-slice_fusion.3), channel_id=1, source_target_pairs={{0,1},{1,0},{2,3},{3,2},{4,5},{5,4},{6,7},{7,6},{8,9},{9,8},{10,11... | collective-permute-start | bytes 393224 | tf_op jit(solution)/shard_map/ppermute | solution.py:52
  65.6 9.7 %collective-permute-start.15 = (f32[1,1,4,64,128]{4,3,2,1,0:T(8,128)S(1)}, f32[1,1,4,64,128]{4,3,2,1,0:T(8,128)S(1)}, u32[]{:S(2)}, u32[]{:S(2)}) collective-permute-start(f32[1,1,4,64,128]{4,3,2,1,0:T(8,128)S(1)} %dynamic-slice_bitcast_fusion.7), channel_id=1, source_target_pairs={{0,8},{2,10},{4,12},{6,14},{8,0},{10,2},{12,4},{14,6},{1,9},{3,11}... | collective-permute-start | bytes 393224 | tf_op jit(solution)/shard_map/ppermute | solution.py:169
  76.0 2.4 %collective-permute-start.19 = (f32[4,64,128]{2,1,0:T(8,128)S(1)}, f32[4,64,128]{2,1,0:T(8,128)S(1)}, u32[]{:S(2)}, u32[]{:S(2)}) collective-permute-start(f32[4,64,128]{2,1,0:T(8,128)S(1)} %constant_dynamic-slice_fusion.2), channel_id=1, source_target_pairs={{0,1},{1,0},{2,3},{3,2},{4,5},{5,4},{6,7},{7,6},{8,9},{9,8},{10,11... | collective-permute-start | bytes 393224 | tf_op jit(solution)/shard_map/ppermute | solution.py:52
  76.6 8.8 %collective-permute-start.18 = (f32[2,2,4,32,128]{4,3,2,1,0:T(8,128)S(1)}, f32[2,2,4,32,128]{4,3,2,1,0:T(8,128)S(1)}, u32[]{:S(2)}, u32[]{:S(2)}) collective-permute-start(f32[2,2,4,32,128]{4,3,2,1,0:T(8,128)S(1)} %dynamic-slice_bitcast_fusion), channel_id=1, source_target_pairs={{0,4},{2,6},{4,0},{6,2},{8,12},{10,14},{12,8},{14,10},{1,5},{3,7},... | collective-permute-start | bytes 786440 | tf_op jit(solution)/shard_map/ppermute | solution.py:169
  76.7 8.8 %collective-permute-start.17 = (f32[4,1,4,32,128]{4,3,2,0,1:T(8,128)S(1)}, f32[4,1,4,32,128]{4,3,2,0,1:T(8,128)S(1)}, u32[]{:S(2)}, u32[]{:S(2)}) collective-permute-start(f32[4,1,4,32,128]{4,3,2,0,1:T(8,128)S(1)} %dynamic-slice_bitcast_fusion.1), channel_id=1, source_target_pairs={{0,2},{2,0},{4,6},{6,4},{8,10},{10,8},{12,14},{14,12},{1,3},{3,1},... | collective-permute-start | bytes 786440 | tf_op jit(solution)/shard_map/ppermute | solution.py:169
  85.5 14.4 %copy-start.13 = (f32[1,4,64,128]{3,2,1,0:T(8,128)S(1)}, f32[1,4,64,128]{3,2,1,0:T(8,128)}, u32[]{:S(2)}) copy-start(f32[1,4,64,128]{3,2,1,0:T(8,128)} %fusion.168) | copy-start | bytes 393220
  85.6 5.2 %collective-permute-start.21 = (f32[2,1,4,32,128]{4,3,2,0,1:T(8,128)S(1)}, f32[2,1,4,32,128]{4,3,2,0,1:T(8,128)S(1)}, u32[]{:S(2)}, u32[]{:S(2)}) collective-permute-start(f32[2,1,4,32,128]{4,3,2,0,1:T(8,128)S(1)} %dynamic-slice_bitcast_fusion.5), channel_id=1, source_target_pairs={{0,2},{2,0},{4,6},{6,4},{8,10},{10,8},{12,14},{14,12},{1,3},{3,1},... | collective-permute-start | bytes 393224 | tf_op jit(solution)/shard_map/ppermute | solution.py:169
  87.0 5.0 %collective-permute-start.20 = (f32[2,1,4,32,128]{4,3,2,0,1:T(8,128)S(1)}, f32[2,1,4,32,128]{4,3,2,0,1:T(8,128)S(1)}, u32[]{:S(2)}, u32[]{:S(2)}) collective-permute-start(f32[2,1,4,32,128]{4,3,2,0,1:T(8,128)S(1)} %dynamic-slice_bitcast_fusion.6), channel_id=1, source_target_pairs={{0,4},{2,6},{4,0},{6,2},{8,12},{10,14},{12,8},{14,10},{1,5},{3,7},... | collective-permute-start | bytes 393224 | tf_op jit(solution)/shard_map/ppermute | solution.py:169
  92.2 7.7 %collective-permute-start.22 = (f32[1,1,4,64,128]{4,3,2,1,0:T(8,128)S(1)}, f32[1,1,4,64,128]{4,3,2,1,0:T(8,128)S(1)}, u32[]{:S(2)}, u32[]{:S(2)}) collective-permute-start(f32[1,1,4,64,128]{4,3,2,1,0:T(8,128)S(1)} %dynamic-slice_bitcast_fusion.4), channel_id=1, source_target_pairs={{0,8},{2,10},{4,12},{6,14},{8,0},{10,2},{12,4},{14,6},{1,9},{3,11}... | collective-permute-start | bytes 393224 | tf_op jit(solution)/shard_map/ppermute | solution.py:169
  101.6 7.1 %collective-permute-start.23 = (f32[1,4,64,128]{3,2,1,0:T(8,128)S(1)}, f32[1,4,64,128]{3,2,1,0:T(8,128)S(1)}, u32[]{:S(2)}, u32[]{:S(2)}) collective-permute-start(f32[1,4,64,128]{3,2,1,0:T(8,128)S(1)} %fusion.1), channel_id=1, source_target_pairs={{0,8},{2,10},{4,12},{6,14},{8,0},{10,2},{12,4},{14,6},{1,9},{3,11}... | collective-permute-start | bytes 393224 | tf_op jit(solution)/shard_map/ppermute | solution.py:120
  108.8 6.2 %collective-permute-start.25 = (f32[2,4,32,128]{3,2,1,0:T(8,128)S(1)}, f32[2,4,32,128]{3,2,1,0:T(8,128)S(1)}, u32[]{:S(2)}, u32[]{:S(2)}) collective-permute-start(f32[2,4,32,128]{3,2,1,0:T(8,128)S(1)} %get-tuple-element.143), channel_id=1, source_target_pairs={{0,2},{2,0},{4,6},{6,4},{8,10},{10,8},{12,14},{14,12},{1,3},{3,1},... | collective-permute-start | bytes 393224 | tf_op jit(solution)/shard_map/ppermute | solution.py:120
  109.3 6.4 %collective-permute-start.24 = (f32[2,4,32,128]{3,2,1,0:T(8,128)S(1)}, f32[2,4,32,128]{3,2,1,0:T(8,128)S(1)}, u32[]{:S(2)}, u32[]{:S(2)}) collective-permute-start(f32[2,4,32,128]{3,2,1,0:T(8,128)S(1)} %get-tuple-element.144), channel_id=1, source_target_pairs={{0,4},{2,6},{4,0},{6,2},{8,12},{10,14},{12,8},{14,10},{1,5},{3,7},... | collective-permute-start | bytes 393224 | tf_op jit(solution)/shard_map/ppermute | solution.py:120
  115.8 6.6 %collective-permute-start.27 = (f32[4,4,32,128]{3,2,1,0:T(8,128)S(1)}, f32[4,4,32,128]{3,2,1,0:T(8,128)S(1)}, u32[]{:S(2)}, u32[]{:S(2)}) collective-permute-start(f32[4,4,32,128]{3,2,1,0:T(8,128)S(1)} %bitcast.222), channel_id=1, source_target_pairs={{0,4},{2,6},{4,0},{6,2},{8,12},{10,14},{12,8},{14,10},{1,5},{3,7},... | collective-permute-start | bytes 786440 | tf_op jit(solution)/shard_map/ppermute | solution.py:120
  115.8 6.4 %collective-permute-start.26 = (f32[4,4,32,128]{3,2,1,0:T(8,128)S(1)}, f32[4,4,32,128]{3,2,1,0:T(8,128)S(1)}, u32[]{:S(2)}, u32[]{:S(2)}) collective-permute-start(f32[4,4,32,128]{3,2,1,0:T(8,128)S(1)} %bitcast.228), channel_id=1, source_target_pairs={{0,2},{2,0},{4,6},{6,4},{8,10},{10,8},{12,14},{14,12},{1,3},{3,1},... | collective-permute-start | bytes 786440 | tf_op jit(solution)/shard_map/ppermute | solution.py:120
  124.5 1.6 %collective-permute-start.28 = (f32[4,64,128]{2,1,0:T(8,128)}, f32[4,64,128]{2,1,0:T(8,128)S(1)}, u32[]{:S(2)}, u32[]{:S(2)}) collective-permute-start(f32[4,64,128]{2,1,0:T(8,128)} %constant_dynamic-slice_fusion), channel_id=1, source_target_pairs={{0,1},{1,0},{2,3},{3,2},{4,5},{5,4},{6,7},{7,6},{8,9},{9,8},{10,11... | collective-permute-start | bytes 393224 | tf_op jit(solution)/shard_map/ppermute | solution.py:52
  131.2 1.9 %collective-permute-start.29 = (f32[1,2,256]{2,1,0:T(2,128)S(1)}, f32[1,2,256]{2,1,0:T(2,128)S(1)}, u32[]{:S(2)}, u32[]{:S(2)}) collective-permute-start(f32[1,2,256]{2,1,0:T(2,128)S(1)} %maximum_bitcast_fusion), channel_id=1, source_target_pairs={{0,1},{1,0},{2,3},{3,2},{4,5},{5,4},{6,7},{7,6},{8,9},{9,8},{10,11... | collective-permute-start | bytes 6152 | tf_op jit(solution)/shard_map/ppermute | solution.py:345
  (23 other events, 89.7 us)

commit v13 on v12

--- a/solution.py
+++ b/solution.py
@@ -282,20 +282,31 @@
     light_a, light_b = halves(st["light"].reshape(n_shot, slab, span_y, span_z), 2)
     light_a = chain(light_a, "rs", near_first[:-1], near_first)
     light_b = chain(light_b, "rs", swap_first(near_first[:-1]), near_first)
+    light_c = {}
+
+    def light_next():
+        if light_a["i"] < len(light_a["order"]):
+            return [light_a, light_b]
+        if not light_c:
+            light_c.update(
+                chain(jnp.concatenate([light_a["held"], light_b["held"]], axis=2), "rs", near_first[-1:], near_first[-1:])
+            )
+        return [light_c]
+
     for i in range(1, len(bits)):
-        run_group([model_a, model_b, gains_c, light_a, light_b], tasks[i] if i < len(tasks) else nothing)
+        extra = light_next() if i == len(bits) - 1 else []
+        run_group([model_a, model_b, gains_c] + extra, tasks[i] if i < len(tasks) else nothing)
     for i in range(len(bits), len(tasks)):
         tasks[i]()
     model_held = jnp.concatenate([model_a["held"], model_b["held"]], axis=1)
     gains_held = gains_c["held"]
-    light_c = chain(jnp.concatenate([light_a["held"], light_b["held"]], axis=2), "rs", near_first[-1:], near_first[-1:])
 
     def born_pass():
         model = model_held.reshape(span_z, span_x * span_y).T.reshape(span_x, span_y, span_z)
         st["born1"] = model * st["drive0"]
         st["born2"] = born_second(st["born1"], model, st["drive1"])
 
-    run_group([light_c], born_pass)
+    run_group(light_next(), born_pass)
     born1, born2 = st["born1"], st["born2"]
 
     image = st["drive0"] * born1 + st["drive1"] * born2
@@ -304,13 +315,13 @@
     image_b = chain(image_b, "rs", swap_first(near_first[:-1]), near_first)
     tasks = [task_wave(3)]
     for i in range(len(bits) - 1):
-        run_group([image_a, image_b], tasks[i] if i < len(tasks) else nothing)
+        run_group([image_a, image_b] + light_next(), tasks[i] if i < len(tasks) else nothing)
     for i in range(len(bits) - 1, len(tasks)):
         tasks[i]()
     last = chain(
         jnp.concatenate([image_a["held"], image_b["held"]], axis=2), "rs", near_first[-1:], near_first[-1:]
     )
-    run_group([last], nothing)
+    run_group([last] + light_next(), nothing)
     image_part = last["held"][0]
     light_part = light_c["held"][0]
 

time: 134 us -> 135 us (level)
  waiting for transfers between devices: 39.7 us -> 43 us
  starting transfers between devices: 30.9 us -> 29.5 us
    ppermute x10, waiting for transfers between devices: 16.6 us -> 19.7 us  [rs_step(): got = lax.ppermute(send, 'shot', [(i, i ^ k) for i in range(n)])]
    ppermute x10, starting transfers between devices: 16.5 us -> 13.8 us  [rs_step(): got = lax.ppermute(send, 'shot', [(i, i ^ k) for i in range(n)])]
    ppermute x13, starting transfers between devices: 12.6 us -> 14 us  [ag_step(): theirs = lax.ppermute(held, 'shot', [(i, i ^ k) for i in range(n)])]
    unnamed x53 -> x49, local copies, waits for them, and re-layouts: 4.94 us -> 4.86 us
  transfers between devices with their start and end apart: 30 -> 30, of which waited for: 15 -> 14; matrix products, arithmetic and copies ran while one was open for 27% -> 26% of each run, Pallas kernels for 0% -> 0%
where the time goes in v13:
time: 135 us; the launch traced here: 134 us
  waiting for transfers between devices  43 us (32%)
  other arithmetic  36.8 us (27%)
  starting transfers between devices  29.5 us (22%)
  local copies, waits for them, and re-layouts  18.7 us (14%)
  between operations  4.83 us (4%)
  matrix products  1.7 us (1%)
    ppermute x13, waiting for transfers between devices, ag_step(): theirs = lax.ppermute(held, 'shot', [(i, i ^ k) for i in range(n)])  22.7 us
    ppermute x10, waiting for transfers between devices, rs_step(): got = lax.ppermute(send, 'shot', [(i, i ^ k) for i in range(n)])  19.7 us
    ppermute x13, starting transfers between devices, ag_step(): theirs = lax.ppermute(held, 'shot', [(i, i ^ k) for i in range(n)])  14 us
    ppermute x10, starting transfers between devices, rs_step(): got = lax.ppermute(send, 'shot', [(i, i ^ k) for i in range(n)])  13.8 us
    add x3, other arithmetic, inject(): return field + jnp.where(hit, source_gain[0] * wavelet[0, moment], 0.0)  11.7 us
    add x2, other arithmetic, born_second(): 2.0 * born + speed_term * laplace_x(with_halo(born)) - absorber * born  5.85 us
    unnamed x49, local copies, waits for them, and re-layouts  4.86 us
    another operation x1, other arithmetic, damping(): lower = jnp.stack([edges[0], edges[2], edges[4]])[:, None]  3.9 us
  transfers between devices with their start and end apart: 30, of which 14 were waited for; matrix products, arithmetic and copies ran while one was open for 26% of the time, Pallas kernels for 0%

profile of v13, /device:TPU:0, one launch (start us, length us, event | category | flops | bytes accessed | tf_op | source)
XLA Modules:
  0.0 134.4 jit_solution(13533673006621355232)
XLA Ops:
  0.7 1.7 %dynamic-slice_bitcast_fusion.10 = f32[4,64,128]{2,1,0:T(8,128)} fusion(f32[1,32,64,128]{3,2,1,0:T(8,128)} %param.12, s32[]{:T(128)S(6)} %select_n.404), kind=kLoop, calls=%fused_computation.360 | loop fusion | bytes 262148 | tf_op jit(solution)/shard_map/dynamic_slice | solution.py:51
  4.6 3.6 %collective-permute-start = (f32[1,16,2048]{2,1,0:T(8,128)}, f32[1,16,2048]{2,1,0:T(8,128)}, u32[]{:S(2)}, u32[]{:S(2)}) collective-permute-start(f32[1,16,2048]{2,1,0:T(8,128)} %concatenate.196), channel_id=1, source_target_pairs={{0,8},{2,10},{4,12},{6,14},{8,0},{10,2},{12,4},{14,6},{1,9},{3,11}... | collective-permute-start | bytes 393224 | tf_op jit(solution)/shard_map/ppermute | solution.py:120
  10.2 3.9 %pad_maximum_fusion.15 = (f32[3]{0:T(128)S(1)}, f32[3]{0:T(128)S(1)}) fusion(f32[1]{0:T(128)} %get-tuple-element.158, f32[1]{0:T(128)} %get-tuple-element.159, f32[1]{0:T(128)} %get-tuple-element.154, f32[1]{0:T(128)} %get-tuple-element.155, f32[1]{0:T(128)} %get-tuple-element.156, f32[1]{0:T(128)} %get-tuple-element.157), kind=kLoop, calls=%fused_computation.417 | loop fusion | flops 12 | bytes 48 | tf_op jit(solution)/shard_map/stack | solution.py:37
  22.5 4.5 %fusion.2 = (f32[32,64,128]{2,1,0:T(8,128)S(1)}, f32[32,64,128]{2,1,0:T(8,128)S(1)}) fusion(f32[]{:T(128)S(6)} %mul.319, f32[128]{0:T(128)} %slice_bitcast_fusion, f32[32,64]{1,0:T(8,128)S(1)} %broadcast_add_fusion, pred[128]{0:T(512)(128)(4,1)} %iota_compare_fusion.1, pred[32,64]{1,0:T(8,128)(4,1)} %broadcast_and_fusion, f32[1,32,64,128]{3,2,1,0:T(8,128)} %param.11, ...), kind=kLoop, calls=%fused_computation.118 | loop fusion | flops 12058624 | bytes 16009860 | tf_op jit(solution)/shard_map/add | solution.py:213
  30.0 3.2 %fusion.3 = (f32[32,64,128]{2,1,0:T(8,128)S(1)}, f32[32,64,128]{2,1,0:T(8,128)S(1)}) fusion(f32[]{:T(128)S(6)} %mul.330, f32[]{:T(128)S(6)} %mul.319, f32[128]{0:T(128)S(1)} %copy-done.13, f32[32,64]{1,0:T(8,128)S(1)} %broadcast_add_fusion, f32[32,64,128]{2,1,0:T(8,128)S(1)} %get-tuple-element.80, pred[128]{0:T(512)(128)(4,1)S(1)} %copy-done.16, ...), kind=kLoop, calls=%fused_computation.119 | loop fusion | flops 14155776 | bytes 17060872 | tf_op jit(solution)/shard_map/add | solution.py:213
  33.7 1.7 %collective-permute-start.12 = (f32[2,2,4,32,128]{4,3,2,1,0:T(8,128)S(1)}, f32[2,2,4,32,128]{4,3,2,1,0:T(8,128)S(1)}, u32[]{:S(2)}, u32[]{:S(2)}) collective-permute-start(f32[2,2,4,32,128]{4,3,2,1,0:T(8,128)S(1)} %dynamic-slice_bitcast_fusion.2), channel_id=1, source_target_pairs={{0,4},{2,6},{4,0},{6,2},{8,12},{10,14},{12,8},{14,10},{1,5},{3,7},... | collective-permute-start | bytes 786440 | tf_op jit(solution)/shard_map/ppermute | solution.py:169
  36.0 1.7 %collective-permute-start.5 = (f32[2,8,2048]{2,1,0:T(8,128)S(1)}, f32[2,8,2048]{2,1,0:T(8,128)S(1)}, u32[]{:S(2)}, u32[]{:S(2)}) collective-permute-start(f32[2,8,2048]{2,1,0:T(8,128)S(1)} %get-tuple-element.147), channel_id=1, source_target_pairs={{0,2},{2,0},{4,6},{6,4},{8,10},{10,8},{12,14},{14,12},{1,3},{3,1},... | collective-permute-start | bytes 393224 | tf_op jit(solution)/shard_map/ppermute | solution.py:120
  37.7 1.6 %collective-permute-start.4 = (f32[2,8,2048]{2,1,0:T(8,128)S(1)}, f32[2,8,2048]{2,1,0:T(8,128)S(1)}, u32[]{:S(2)}, u32[]{:S(2)}) collective-permute-start(f32[2,8,2048]{2,1,0:T(8,128)S(1)} %get-tuple-element.148), channel_id=1, source_target_pairs={{0,4},{2,6},{4,0},{6,2},{8,12},{10,14},{12,8},{14,10},{1,5},{3,7},... | collective-permute-start | bytes 393224 | tf_op jit(solution)/shard_map/ppermute | solution.py:120
  39.2 3.9 %collective-permute-done.6 = f32[2,16,64]{2,1,0:T(8,128)S(1)} collective-permute-done((f32[2,16,64]{2,1,0:T(8,128)S(1)}, f32[2,16,64]{2,1,0:T(8,128)S(1)}, u32[]{:S(2)}, u32[]{:S(2)}) %collective-permute-start.6) | collective-permute-done | bytes 8224 | tf_op jit(solution)/shard_map/ppermute | solution.py:120
  43.2 4.0 %fusion.4 = (f32[32,64,128]{2,1,0:T(8,128)}, f32[32,64,128]{2,1,0:T(8,128)}) fusion(f32[32,64,128]{2,1,0:T(8,128)S(1)} %get-tuple-element.62, f32[32,64,128]{2,1,0:T(8,128)S(1)} %get-tuple-element.64, f32[]{:T(128)S(6)} %mul.339, f32[128]{0:T(128)S(1)} %copy-done.13, f32[32,64]{1,0:T(8,128)S(1)} %broadcast_add_fusion, pred[128]{0:T(512)(128)(4,1)S(1)} %copy-done.16, ...), kind=kLoop, calls=%fused_computation.120 | loop fusion | flops 12058624 | bytes 16012292 | tf_op jit(solution)/shard_map/add | solution.py:213
  47.3 1.7 %collective-permute-start.10 = (f32[4,16,64]{2,1,0:T(8,128)S(1)}, f32[4,16,64]{2,1,0:T(8,128)S(1)}, u32[]{:S(2)}, u32[]{:S(2)}) collective-permute-start(f32[4,16,64]{2,1,0:T(8,128)S(1)} %bitcast.244), channel_id=1, source_target_pairs={{0,2},{2,0},{4,6},{6,4},{8,10},{10,8},{12,14},{14,12},{1,3},{3,1},... | collective-permute-start | bytes 49160 | tf_op jit(solution)/shard_map/ppermute | solution.py:120
  49.5 1.7 %collective-permute-start.9 = (f32[4,8,2048]{2,1,0:T(8,128)S(1)}, f32[4,8,2048]{2,1,0:T(8,128)S(1)}, u32[]{:S(2)}, u32[]{:S(2)}) collective-permute-start(f32[4,8,2048]{2,1,0:T(8,128)S(1)} %bitcast.224), channel_id=1, source_target_pairs={{0,4},{2,6},{4,0},{6,2},{8,12},{10,14},{12,8},{14,10},{1,5},{3,7},... | collective-permute-start | bytes 786440 | tf_op jit(solution)/shard_map/ppermute | solution.py:120
  51.2 1.5 %collective-permute-start.8 = (f32[4,8,2048]{2,1,0:T(8,128)S(1)}, f32[4,8,2048]{2,1,0:T(8,128)S(1)}, u32[]{:S(2)}, u32[]{:S(2)}) collective-permute-start(f32[4,8,2048]{2,1,0:T(8,128)S(1)} %bitcast.222), channel_id=1, source_target_pairs={{0,2},{2,0},{4,6},{6,4},{8,10},{10,8},{12,14},{14,12},{1,3},{3,1},... | collective-permute-start | bytes 786440 | tf_op jit(solution)/shard_map/ppermute | solution.py:120
  53.4 5.0 %collective-permute-done.11 = f32[4,1,4,32,128]{4,3,2,0,1:T(8,128)S(1)} collective-permute-done((f32[4,1,4,32,128]{4,3,2,0,1:T(8,128)S(1)}, f32[4,1,4,32,128]{4,3,2,0,1:T(8,128)S(1)}, u32[]{:S(2)}, u32[]{:S(2)}) %collective-permute-start.11) | collective-permute-done | bytes 262176 | tf_op jit(solution)/shard_map/ppermute | solution.py:169
  59.2 3.1 %collective-permute-done.8 = f32[4,8,2048]{2,1,0:T(8,128)S(1)} collective-permute-done((f32[4,8,2048]{2,1,0:T(8,128)S(1)}, f32[4,8,2048]{2,1,0:T(8,128)S(1)}, u32[]{:S(2)}, u32[]{:S(2)}) %collective-permute-start.8) | collective-permute-done | bytes 262176 | tf_op jit(solution)/shard_map/ppermute | solution.py:120
  63.4 2.5 %copy.66 = f32[2048,128]{1,0:T(8,128)} copy(f32[2048,128]{0,1:T(8,128)} %bitcast.205) | data formatting | bytes 2097152 | tf_op jit(solution)/shard_map/transpose | solution.py:305
  66.0 1.4 %mul.340 = f32[32,64,128]{2,1,0:T(8,128)S(1)} multiply(f32[32,64,128]{2,1,0:T(8,128)} %bitcast.199, f32[32,64,128]{2,1,0:T(8,128)S(1)} %get-tuple-element.80) | non-fusion elementwise | flops 262144 | bytes 3145728 | tf_op jit(solution)/shard_map/mul | solution.py:306
  68.2 1.6 %collective-permute-start.13 = (f32[2,1,4,32,128]{4,3,2,0,1:T(8,128)S(1)}, f32[2,1,4,32,128]{4,3,2,0,1:T(8,128)S(1)}, u32[]{:S(2)}, u32[]{:S(2)}) collective-permute-start(f32[2,1,4,32,128]{4,3,2,0,1:T(8,128)S(1)} %dynamic-slice_bitcast_fusion.9), channel_id=1, source_target_pairs={{0,4},{2,6},{4,0},{6,2},{8,12},{10,14},{12,8},{14,10},{1,5},{3,7},... | collective-permute-start | bytes 393224 | tf_op jit(solution)/shard_map/ppermute | solution.py:169
  70.0 2.9 %fusion.92 = f32[32,64,128]{2,1,0:T(8,128)S(1)} fusion(f32[40,64,128]{2,1,0:T(8,128)S(1)} %constant_dynamic-update-slice_fusion.2, f32[32,64,128]{2,1,0:T(8,128)S(1)} %bitcast.200, f32[32,64,128]{2,1,0:T(8,128)S(1)} %get-tuple-element.82, f32[32,64,128]{2,1,0:T(8,128)S(1)} %mul.340, f32[128]{0:T(128)S(1)} %copy-done.14, f32[32,64]{1,0:T(8,128)S(1)} %broadcast_add_fusion, ...), kind=kLoop, calls=%fused_computation.208 | loop fusion | flops 11272192 | bytes 16007680 | tf_op jit(solution)/shard_map/add | solution.py:224
  74.0 2.7 %collective-permute-start.18 = (f32[1,1,4,64,128]{4,3,2,1,0:T(8,128)S(1)}, f32[1,1,4,64,128]{4,3,2,1,0:T(8,128)S(1)}, u32[]{:S(2)}, u32[]{:S(2)}) collective-permute-start(f32[1,1,4,64,128]{4,3,2,1,0:T(8,128)S(1)} %dynamic-slice_bitcast_fusion.7), channel_id=1, source_target_pairs={{0,8},{2,10},{4,12},{6,14},{8,0},{10,2},{12,4},{14,6},{1,9},{3,11}... | collective-permute-start | bytes 393224 | tf_op jit(solution)/shard_map/ppermute | solution.py:169
  77.2 1.6 %collective-permute-start.17 = (f32[2,2,4,32,128]{4,3,2,1,0:T(8,128)S(1)}, f32[2,2,4,32,128]{4,3,2,1,0:T(8,128)S(1)}, u32[]{:S(2)}, u32[]{:S(2)}) collective-permute-start(f32[2,2,4,32,128]{4,3,2,1,0:T(8,128)S(1)} %dynamic-slice_bitcast_fusion), channel_id=1, source_target_pairs={{0,4},{2,6},{4,0},{6,2},{8,12},{10,14},{12,8},{14,10},{1,5},{3,7},... | collective-permute-start | bytes 786440 | tf_op jit(solution)/shard_map/ppermute | solution.py:169
  78.9 1.5 %collective-permute-start.16 = (f32[4,1,4,32,128]{4,3,2,0,1:T(8,128)S(1)}, f32[4,1,4,32,128]{4,3,2,0,1:T(8,128)S(1)}, u32[]{:S(2)}, u32[]{:S(2)}) collective-permute-start(f32[4,1,4,32,128]{4,3,2,0,1:T(8,128)S(1)} %dynamic-slice_bitcast_fusion.1), channel_id=1, source_target_pairs={{0,2},{2,0},{4,6},{6,4},{8,10},{10,8},{12,14},{14,12},{1,3},{3,1},... | collective-permute-start | bytes 786440 | tf_op jit(solution)/shard_map/ppermute | solution.py:169
  80.7 3.2 %fusion.117 = f32[32,64,128]{2,1,0:T(8,128)} fusion(f32[40,64,128]{2,1,0:T(8,128)S(1)} %constant_dynamic-update-slice_fusion.1, s32[32,64,128]{2,1,0:T(8,128)S(1)} %copy-done), kind=kLoop, calls=%fused_computation.233 | loop fusion | flops 9175040 | bytes 12845056 | tf_op jit(solution)/shard_map/mul | solution.py:216
  83.9 3.5 %collective-permute-done.17 = f32[2,2,4,32,128]{4,3,2,1,0:T(8,128)S(1)} collective-permute-done((f32[2,2,4,32,128]{4,3,2,1,0:T(8,128)S(1)}, f32[2,2,4,32,128]{4,3,2,1,0:T(8,128)S(1)}, u32[]{:S(2)}, u32[]{:S(2)}) %collective-permute-start.17) | collective-permute-done | bytes 262176 | tf_op jit(solution)/shard_map/ppermute | solution.py:169
  87.6 1.5 %collective-permute-start.21 = (f32[2,1,4,32,128]{4,3,2,0,1:T(8,128)S(1)}, f32[2,1,4,32,128]{4,3,2,0,1:T(8,128)S(1)}, u32[]{:S(2)}, u32[]{:S(2)}) collective-permute-start(f32[2,1,4,32,128]{4,3,2,0,1:T(8,128)S(1)} %dynamic-slice_bitcast_fusion.5), channel_id=1, source_target_pairs={{0,2},{2,0},{4,6},{6,4},{8,10},{10,8},{12,14},{14,12},{1,3},{3,1},... | collective-permute-start | bytes 393224 | tf_op jit(solution)/shard_map/ppermute | solution.py:169
  90.0 2.6 %collective-permute-done.21 = f32[2,1,4,32,128]{4,3,2,0,1:T(8,128)S(1)} collective-permute-done((f32[2,1,4,32,128]{4,3,2,0,1:T(8,128)S(1)}, f32[2,1,4,32,128]{4,3,2,0,1:T(8,128)S(1)}, u32[]{:S(2)}, u32[]{:S(2)}) %collective-permute-start.21) | collective-permute-done | bytes 131104 | tf_op jit(solution)/shard_map/ppermute | solution.py:169
  92.6 1.5 %collective-permute-done.20 = f32[2,1,4,32,128]{4,3,2,0,1:T(8,128)S(1)} collective-permute-done((f32[2,1,4,32,128]{4,3,2,0,1:T(8,128)S(1)}, f32[2,1,4,32,128]{4,3,2,0,1:T(8,128)S(1)}, u32[]{:S(2)}, u32[]{:S(2)}) %collective-permute-start.20) | collective-permute-done | bytes 131104 | tf_op jit(solution)/shard_map/ppermute | solution.py:169
  95.4 6.3 %collective-permute-done.22 = f32[1,1,4,64,128]{4,3,2,1,0:T(8,128)S(1)} collective-permute-done((f32[1,1,4,64,128]{4,3,2,1,0:T(8,128)S(1)}, f32[1,1,4,64,128]{4,3,2,1,0:T(8,128)S(1)}, u32[]{:S(2)}, u32[]{:S(2)}) %collective-permute-start.22) | collective-permute-done | bytes 131104 | tf_op jit(solution)/shard_map/ppermute | solution.py:169
  103.5 6.4 %collective-permute-done.23 = f32[1,4,64,128]{3,2,1,0:T(8,128)S(1)} collective-permute-done((f32[1,4,64,128]{3,2,1,0:T(8,128)S(1)}, f32[1,4,64,128]{3,2,1,0:T(8,128)S(1)}, u32[]{:S(2)}, u32[]{:S(2)}) %collective-permute-start.23) | collective-permute-done | bytes 131104 | tf_op jit(solution)/shard_map/ppermute | solution.py:120
  111.4 3.7 %collective-permute-done.25 = f32[2,4,32,128]{3,2,1,0:T(8,128)S(1)} collective-permute-done((f32[2,4,32,128]{3,2,1,0:T(8,128)S(1)}, f32[2,4,32,128]{3,2,1,0:T(8,128)S(1)}, u32[]{:S(2)}, u32[]{:S(2)}) %collective-permute-start.25) | collective-permute-done | bytes 131104 | tf_op jit(solution)/shard_map/ppermute | solution.py:120
  118.7 4.3 %collective-permute-done.26 = f32[4,4,32,128]{3,2,1,0:T(8,128)S(1)} collective-permute-done((f32[4,4,32,128]{3,2,1,0:T(8,128)S(1)}, f32[4,4,32,128]{3,2,1,0:T(8,128)S(1)}, u32[]{:S(2)}, u32[]{:S(2)}) %collective-permute-start.26) | collective-permute-done | bytes 262176 | tf_op jit(solution)/shard_map/ppermute | solution.py:120
  127.7 2.9 %fusion.145 = f32[32,64,128]{2,1,0:T(8,128)S(1)} fusion(f32[40,64,128]{2,1,0:T(8,128)S(1)} %constant_dynamic-update-slice_fusion, f32[32,64,128]{2,1,0:T(8,128)S(1)} %copy-done.8, f32[128]{0:T(128)S(1)} %copy-done.15, f32[32,64]{1,0:T(8,128)S(1)} %broadcast_add_fusion, f32[8,4,64,128]{3,2,1,0:T(8,128)S(1)} %pad_maximum_fusion.13, ...), kind=kLoop, calls=%fused_computation.261 | loop fusion | flops 11534336 | bytes 16007680 | tf_op jit(solution)/shard_map/add | solution.py:224
  (191 shorter events, 36.6 us)
Async XLA Ops:
  0.6 15.6 %copy-start.1 = (f32[1,32,64,128]{3,2,1,0:T(8,128)S(1)}, f32[1,32,64,128]{3,2,1,0:T(8,128)}, u32[]{:S(2)}) copy-start(f32[1,32,64,128]{3,2,1,0:T(8,128)} %param.12) | copy-start | bytes 3145732
  0.7 14.2 %copy-start.17 = (f32[1,4]{1,0:T(1,128)S(1)}, f32[1,4]{1,0:T(1,128)}, u32[]{:S(2)}) copy-start(f32[1,4]{1,0:T(1,128)} %param.16) | copy-start | bytes 52
  2.3 19.2 %collective-permute-start.2 = (f32[4,64,128]{2,1,0:T(8,128)}, f32[4,64,128]{2,1,0:T(8,128)}, u32[]{:S(2)}, u32[]{:S(2)}) collective-permute-start(f32[4,64,128]{2,1,0:T(8,128)} %dynamic-slice_bitcast_fusion.10), channel_id=1, source_target_pairs={{0,1},{1,0},{2,3},{3,2},{4,5},{5,4},{6,7},{7,6},{8,9},{9,8},{10,11... | collective-permute-start | bytes 393224 | tf_op jit(solution)/shard_map/ppermute | solution.py:52
  4.6 22.7 %collective-permute-start = (f32[1,16,2048]{2,1,0:T(8,128)}, f32[1,16,2048]{2,1,0:T(8,128)}, u32[]{:S(2)}, u32[]{:S(2)}) collective-permute-start(f32[1,16,2048]{2,1,0:T(8,128)} %concatenate.196), channel_id=1, source_target_pairs={{0,8},{2,10},{4,12},{6,14},{8,0},{10,2},{12,4},{14,6},{1,9},{3,11}... | collective-permute-start | bytes 393224 | tf_op jit(solution)/shard_map/ppermute | solution.py:120
  8.2 12.6 %collective-permute-start.1 = (f32[1,16,64]{2,1,0:T(8,128)}, f32[1,16,64]{2,1,0:T(8,128)}, u32[]{:S(2)}, u32[]{:S(2)}) collective-permute-start(f32[1,16,64]{2,1,0:T(8,128)} %bitcast.251), channel_id=1, source_target_pairs={{0,8},{2,10},{4,12},{6,14},{8,0},{10,2},{12,4},{14,6},{1,9},{3,11}... | collective-permute-start | bytes 12296 | tf_op jit(solution)/shard_map/ppermute | solution.py:120
  27.0 1.6 %collective-permute-start.3 = (f32[4,64,128]{2,1,0:T(8,128)S(1)}, f32[4,64,128]{2,1,0:T(8,128)S(1)}, u32[]{:S(2)}, u32[]{:S(2)}) collective-permute-start(f32[4,64,128]{2,1,0:T(8,128)S(1)} %constant_dynamic-slice_fusion.5), channel_id=1, source_target_pairs={{0,1},{1,0},{2,3},{3,2},{4,5},{5,4},{6,7},{7,6},{8,9},{9,8},{10,11... | collective-permute-start | bytes 393224 | tf_op jit(solution)/shard_map/ppermute | solution.py:52
  33.7 19.7 %collective-permute-start.12 = (f32[2,2,4,32,128]{4,3,2,1,0:T(8,128)S(1)}, f32[2,2,4,32,128]{4,3,2,1,0:T(8,128)S(1)}, u32[]{:S(2)}, u32[]{:S(2)}) collective-permute-start(f32[2,2,4,32,128]{4,3,2,1,0:T(8,128)S(1)} %dynamic-slice_bitcast_fusion.2), channel_id=1, source_target_pairs={{0,4},{2,6},{4,0},{6,2},{8,12},{10,14},{12,8},{14,10},{1,5},{3,7},... | collective-permute-start | bytes 786440 | tf_op jit(solution)/shard_map/ppermute | solution.py:169
  35.4 7.8 %collective-permute-start.7 = (f32[4,64,128]{2,1,0:T(8,128)S(1)}, f32[4,64,128]{2,1,0:T(8,128)S(1)}, u32[]{:S(2)}, u32[]{:S(2)}) collective-permute-start(f32[4,64,128]{2,1,0:T(8,128)S(1)} %constant_dynamic-slice_fusion.4), channel_id=1, source_target_pairs={{0,1},{1,0},{2,3},{3,2},{4,5},{5,4},{6,7},{7,6},{8,9},{9,8},{10,11... | collective-permute-start | bytes 393224 | tf_op jit(solution)/shard_map/ppermute | solution.py:52
  35.6 7.6 %collective-permute-start.6 = (f32[2,16,64]{2,1,0:T(8,128)S(1)}, f32[2,16,64]{2,1,0:T(8,128)S(1)}, u32[]{:S(2)}, u32[]{:S(2)}) collective-permute-start(f32[2,16,64]{2,1,0:T(8,128)S(1)} %maximum_select_fusion.12), channel_id=1, source_target_pairs={{0,4},{2,6},{4,0},{6,2},{8,12},{10,14},{12,8},{14,10},{1,5},{3,7},... | collective-permute-start | bytes 24584 | tf_op jit(solution)/shard_map/ppermute | solution.py:120
  36.0 11.2 %collective-permute-start.5 = (f32[2,8,2048]{2,1,0:T(8,128)S(1)}, f32[2,8,2048]{2,1,0:T(8,128)S(1)}, u32[]{:S(2)}, u32[]{:S(2)}) collective-permute-start(f32[2,8,2048]{2,1,0:T(8,128)S(1)} %get-tuple-element.147), channel_id=1, source_target_pairs={{0,2},{2,0},{4,6},{6,4},{8,10},{10,8},{12,14},{14,12},{1,3},{3,1},... | collective-permute-start | bytes 393224 | tf_op jit(solution)/shard_map/ppermute | solution.py:120
  37.7 9.5 %collective-permute-start.4 = (f32[2,8,2048]{2,1,0:T(8,128)S(1)}, f32[2,8,2048]{2,1,0:T(8,128)S(1)}, u32[]{:S(2)}, u32[]{:S(2)}) collective-permute-start(f32[2,8,2048]{2,1,0:T(8,128)S(1)} %get-tuple-element.148), channel_id=1, source_target_pairs={{0,4},{2,6},{4,0},{6,2},{8,12},{10,14},{12,8},{14,10},{1,5},{3,7},... | collective-permute-start | bytes 393224 | tf_op jit(solution)/shard_map/ppermute | solution.py:120
  47.3 5.4 %collective-permute-start.10 = (f32[4,16,64]{2,1,0:T(8,128)S(1)}, f32[4,16,64]{2,1,0:T(8,128)S(1)}, u32[]{:S(2)}, u32[]{:S(2)}) collective-permute-start(f32[4,16,64]{2,1,0:T(8,128)S(1)} %bitcast.244), channel_id=1, source_target_pairs={{0,2},{2,0},{4,6},{6,4},{8,10},{10,8},{12,14},{14,12},{1,3},{3,1},... | collective-permute-start | bytes 49160 | tf_op jit(solution)/shard_map/ppermute | solution.py:120
  49.0 9.3 %collective-permute-start.11 = (f32[4,1,4,32,128]{4,3,2,0,1:T(8,128)S(1)}, f32[4,1,4,32,128]{4,3,2,0,1:T(8,128)S(1)}, u32[]{:S(2)}, u32[]{:S(2)}) collective-permute-start(f32[4,1,4,32,128]{4,3,2,0,1:T(8,128)S(1)} %dynamic-slice_bitcast_fusion.3), channel_id=1, source_target_pairs={{0,2},{2,0},{4,6},{6,4},{8,10},{10,8},{12,14},{14,12},{1,3},{3,1},... | collective-permute-start | bytes 786440 | tf_op jit(solution)/shard_map/ppermute | solution.py:169
  49.5 9.6 %collective-permute-start.9 = (f32[4,8,2048]{2,1,0:T(8,128)S(1)}, f32[4,8,2048]{2,1,0:T(8,128)S(1)}, u32[]{:S(2)}, u32[]{:S(2)}) collective-permute-start(f32[4,8,2048]{2,1,0:T(8,128)S(1)} %bitcast.224), channel_id=1, source_target_pairs={{0,4},{2,6},{4,0},{6,2},{8,12},{10,14},{12,8},{14,10},{1,5},{3,7},... | collective-permute-start | bytes 786440 | tf_op jit(solution)/shard_map/ppermute | solution.py:120
  51.2 11.1 %collective-permute-start.8 = (f32[4,8,2048]{2,1,0:T(8,128)S(1)}, f32[4,8,2048]{2,1,0:T(8,128)S(1)}, u32[]{:S(2)}, u32[]{:S(2)}) collective-permute-start(f32[4,8,2048]{2,1,0:T(8,128)S(1)} %bitcast.222), channel_id=1, source_target_pairs={{0,2},{2,0},{4,6},{6,4},{8,10},{10,8},{12,14},{14,12},{1,3},{3,1},... | collective-permute-start | bytes 786440 | tf_op jit(solution)/shard_map/ppermute | solution.py:120
  67.4 2.6 %collective-permute-start.15 = (f32[4,64,128]{2,1,0:T(8,128)S(1)}, f32[4,64,128]{2,1,0:T(8,128)S(1)}, u32[]{:S(2)}, u32[]{:S(2)}) collective-permute-start(f32[4,64,128]{2,1,0:T(8,128)S(1)} %constant_dynamic-slice_fusion.3), channel_id=1, source_target_pairs={{0,1},{1,0},{2,3},{3,2},{4,5},{5,4},{6,7},{7,6},{8,9},{9,8},{10,11... | collective-permute-start | bytes 393224 | tf_op jit(solution)/shard_map/ppermute | solution.py:52
  67.5 6.0 %collective-permute-start.14 = (f32[2,1,4,32,128]{4,3,2,0,1:T(8,128)S(1)}, f32[2,1,4,32,128]{4,3,2,0,1:T(8,128)S(1)}, u32[]{:S(2)}, u32[]{:S(2)}) collective-permute-start(f32[2,1,4,32,128]{4,3,2,0,1:T(8,128)S(1)} %dynamic-slice_bitcast_fusion.8), channel_id=1, source_target_pairs={{0,2},{2,0},{4,6},{6,4},{8,10},{10,8},{12,14},{14,12},{1,3},{3,1},... | collective-permute-start | bytes 393224 | tf_op jit(solution)/shard_map/ppermute | solution.py:169
  68.2 5.7 %collective-permute-start.13 = (f32[2,1,4,32,128]{4,3,2,0,1:T(8,128)S(1)}, f32[2,1,4,32,128]{4,3,2,0,1:T(8,128)S(1)}, u32[]{:S(2)}, u32[]{:S(2)}) collective-permute-start(f32[2,1,4,32,128]{4,3,2,0,1:T(8,128)S(1)} %dynamic-slice_bitcast_fusion.9), channel_id=1, source_target_pairs={{0,4},{2,6},{4,0},{6,2},{8,12},{10,14},{12,8},{14,10},{1,5},{3,7},... | collective-permute-start | bytes 393224 | tf_op jit(solution)/shard_map/ppermute | solution.py:169
  73.9 6.7 %collective-permute-start.19 = (f32[4,64,128]{2,1,0:T(8,128)S(1)}, f32[4,64,128]{2,1,0:T(8,128)S(1)}, u32[]{:S(2)}, u32[]{:S(2)}) collective-permute-start(f32[4,64,128]{2,1,0:T(8,128)S(1)} %constant_dynamic-slice_fusion.2), channel_id=1, source_target_pairs={{0,1},{1,0},{2,3},{3,2},{4,5},{5,4},{6,7},{7,6},{8,9},{9,8},{10,11... | collective-permute-start | bytes 393224 | tf_op jit(solution)/shard_map/ppermute | solution.py:52
  74.0 9.9 %collective-permute-start.18 = (f32[1,1,4,64,128]{4,3,2,1,0:T(8,128)S(1)}, f32[1,1,4,64,128]{4,3,2,1,0:T(8,128)S(1)}, u32[]{:S(2)}, u32[]{:S(2)}) collective-permute-start(f32[1,1,4,64,128]{4,3,2,1,0:T(8,128)S(1)} %dynamic-slice_bitcast_fusion.7), channel_id=1, source_target_pairs={{0,8},{2,10},{4,12},{6,14},{8,0},{10,2},{12,4},{14,6},{1,9},{3,11}... | collective-permute-start | bytes 393224 | tf_op jit(solution)/shard_map/ppermute | solution.py:169
  77.2 10.2 %collective-permute-start.17 = (f32[2,2,4,32,128]{4,3,2,1,0:T(8,128)S(1)}, f32[2,2,4,32,128]{4,3,2,1,0:T(8,128)S(1)}, u32[]{:S(2)}, u32[]{:S(2)}) collective-permute-start(f32[2,2,4,32,128]{4,3,2,1,0:T(8,128)S(1)} %dynamic-slice_bitcast_fusion), channel_id=1, source_target_pairs={{0,4},{2,6},{4,0},{6,2},{8,12},{10,14},{12,8},{14,10},{1,5},{3,7},... | collective-permute-start | bytes 786440 | tf_op jit(solution)/shard_map/ppermute | solution.py:169
  78.9 8.6 %collective-permute-start.16 = (f32[4,1,4,32,128]{4,3,2,0,1:T(8,128)S(1)}, f32[4,1,4,32,128]{4,3,2,0,1:T(8,128)S(1)}, u32[]{:S(2)}, u32[]{:S(2)}) collective-permute-start(f32[4,1,4,32,128]{4,3,2,0,1:T(8,128)S(1)} %dynamic-slice_bitcast_fusion.1), channel_id=1, source_target_pairs={{0,2},{2,0},{4,6},{6,4},{8,10},{10,8},{12,14},{14,12},{1,3},{3,1},... | collective-permute-start | bytes 786440 | tf_op jit(solution)/shard_map/ppermute | solution.py:169
  87.6 5.0 %collective-permute-start.21 = (f32[2,1,4,32,128]{4,3,2,0,1:T(8,128)S(1)}, f32[2,1,4,32,128]{4,3,2,0,1:T(8,128)S(1)}, u32[]{:S(2)}, u32[]{:S(2)}) collective-permute-start(f32[2,1,4,32,128]{4,3,2,0,1:T(8,128)S(1)} %dynamic-slice_bitcast_fusion.5), channel_id=1, source_target_pairs={{0,2},{2,0},{4,6},{6,4},{8,10},{10,8},{12,14},{14,12},{1,3},{3,1},... | collective-permute-start | bytes 393224 | tf_op jit(solution)/shard_map/ppermute | solution.py:169
  89.1 5.0 %collective-permute-start.20 = (f32[2,1,4,32,128]{4,3,2,0,1:T(8,128)S(1)}, f32[2,1,4,32,128]{4,3,2,0,1:T(8,128)S(1)}, u32[]{:S(2)}, u32[]{:S(2)}) collective-permute-start(f32[2,1,4,32,128]{4,3,2,0,1:T(8,128)S(1)} %dynamic-slice_bitcast_fusion.6), channel_id=1, source_target_pairs={{0,4},{2,6},{4,0},{6,2},{8,12},{10,14},{12,8},{14,10},{1,5},{3,7},... | collective-permute-start | bytes 393224 | tf_op jit(solution)/shard_map/ppermute | solution.py:169
  94.2 7.4 %collective-permute-start.22 = (f32[1,1,4,64,128]{4,3,2,1,0:T(8,128)S(1)}, f32[1,1,4,64,128]{4,3,2,1,0:T(8,128)S(1)}, u32[]{:S(2)}, u32[]{:S(2)}) collective-permute-start(f32[1,1,4,64,128]{4,3,2,1,0:T(8,128)S(1)} %dynamic-slice_bitcast_fusion.4), channel_id=1, source_target_pairs={{0,8},{2,10},{4,12},{6,14},{8,0},{10,2},{12,4},{14,6},{1,9},{3,11}... | collective-permute-start | bytes 393224 | tf_op jit(solution)/shard_map/ppermute | solution.py:169
  103.4 6.5 %collective-permute-start.23 = (f32[1,4,64,128]{3,2,1,0:T(8,128)S(1)}, f32[1,4,64,128]{3,2,1,0:T(8,128)S(1)}, u32[]{:S(2)}, u32[]{:S(2)}) collective-permute-start(f32[1,4,64,128]{3,2,1,0:T(8,128)S(1)} %fusion.1), channel_id=1, source_target_pairs={{0,8},{2,10},{4,12},{6,14},{8,0},{10,2},{12,4},{14,6},{1,9},{3,11}... | collective-permute-start | bytes 393224 | tf_op jit(solution)/shard_map/ppermute | solution.py:120
  110.0 5.0 %collective-permute-start.25 = (f32[2,4,32,128]{3,2,1,0:T(8,128)S(1)}, f32[2,4,32,128]{3,2,1,0:T(8,128)S(1)}, u32[]{:S(2)}, u32[]{:S(2)}) collective-permute-start(f32[2,4,32,128]{3,2,1,0:T(8,128)S(1)} %get-tuple-element.143), channel_id=1, source_target_pairs={{0,2},{2,0},{4,6},{6,4},{8,10},{10,8},{12,14},{14,12},{1,3},{3,1},... | collective-permute-start | bytes 393224 | tf_op jit(solution)/shard_map/ppermute | solution.py:120
  110.8 5.6 %collective-permute-start.24 = (f32[2,4,32,128]{3,2,1,0:T(8,128)S(1)}, f32[2,4,32,128]{3,2,1,0:T(8,128)S(1)}, u32[]{:S(2)}, u32[]{:S(2)}) collective-permute-start(f32[2,4,32,128]{3,2,1,0:T(8,128)S(1)} %get-tuple-element.144), channel_id=1, source_target_pairs={{0,4},{2,6},{4,0},{6,2},{8,12},{10,14},{12,8},{14,10},{1,5},{3,7},... | collective-permute-start | bytes 393224 | tf_op jit(solution)/shard_map/ppermute | solution.py:120
  116.5 6.6 %collective-permute-start.27 = (f32[4,4,32,128]{3,2,1,0:T(8,128)S(1)}, f32[4,4,32,128]{3,2,1,0:T(8,128)S(1)}, u32[]{:S(2)}, u32[]{:S(2)}) collective-permute-start(f32[4,4,32,128]{3,2,1,0:T(8,128)S(1)} %bitcast.226), channel_id=1, source_target_pairs={{0,4},{2,6},{4,0},{6,2},{8,12},{10,14},{12,8},{14,10},{1,5},{3,7},... | collective-permute-start | bytes 786440 | tf_op jit(solution)/shard_map/ppermute | solution.py:120
  116.5 6.4 %collective-permute-start.26 = (f32[4,4,32,128]{3,2,1,0:T(8,128)S(1)}, f32[4,4,32,128]{3,2,1,0:T(8,128)S(1)}, u32[]{:S(2)}, u32[]{:S(2)}) collective-permute-start(f32[4,4,32,128]{3,2,1,0:T(8,128)S(1)} %bitcast.228), channel_id=1, source_target_pairs={{0,2},{2,0},{4,6},{6,4},{8,10},{10,8},{12,14},{14,12},{1,3},{3,1},... | collective-permute-start | bytes 786440 | tf_op jit(solution)/shard_map/ppermute | solution.py:120
  125.2 1.6 %collective-permute-start.28 = (f32[4,64,128]{2,1,0:T(8,128)}, f32[4,64,128]{2,1,0:T(8,128)S(1)}, u32[]{:S(2)}, u32[]{:S(2)}) collective-permute-start(f32[4,64,128]{2,1,0:T(8,128)} %constant_dynamic-slice_fusion), channel_id=1, source_target_pairs={{0,1},{1,0},{2,3},{3,2},{4,5},{5,4},{6,7},{7,6},{8,9},{9,8},{10,11... | collective-permute-start | bytes 393224 | tf_op jit(solution)/shard_map/ppermute | solution.py:52
  131.9 1.9 %collective-permute-start.29 = (f32[1,2,256]{2,1,0:T(2,128)S(1)}, f32[1,2,256]{2,1,0:T(2,128)S(1)}, u32[]{:S(2)}, u32[]{:S(2)}) collective-permute-start(f32[1,2,256]{2,1,0:T(2,128)S(1)} %maximum_bitcast_fusion), channel_id=1, source_target_pairs={{0,1},{1,0},{2,3},{3,2},{4,5},{5,4},{6,7},{7,6},{8,9},{9,8},{10,11... | collective-permute-start | bytes 6152 | tf_op jit(solution)/shard_map/ppermute | solution.py:356
  (21 other events, 65.9 us)

commit v14 on v9

--- a/solution.py
+++ b/solution.py
@@ -213,7 +213,17 @@
         return field + jnp.where(hit, source_gain[0] * wavelet[0, moment], 0.0)
 
     def wave_step(current, prior, moment, last):
-        drive = speed_term * laplace_x(with_halo(current))
+        if moment == 0:
+            inner = barrier(laplace_x(current))
+            padded = with_halo(current)
+            edge = 2 * HALO
+            lap = jnp.concatenate(
+                [laplace_x(padded[: edge + HALO]), inner, laplace_x(padded[padded.shape[0] - edge - HALO :])],
+                axis=0,
+            )
+            drive = speed_term * lap
+        else:
+            drive = speed_term * laplace_x(with_halo(current))
         if last:
             return None, drive
         later = inject(2.0 * current - prior + drive - absorber * (current - prior), moment)

time: 133 us -> 132 us (level)
    add x3, other arithmetic: 11.6 us -> 8.08 us  [inject(): return field + jnp.where(hit, source_gain[0] * wavelet[0, moment], 0.0)]
    add x0 -> x3, other arithmetic: none -> 3.24 us  [laplace_x(): total = total + STENCIL[reach] * beside_all]
    unnamed x47 -> x51, local copies, waits for them, and re-layouts: 3.65 us -> 4.8 us
  transfers between devices with their start and end apart: 30 -> 30, of which waited for: 16 -> 16; matrix products, arithmetic and copies ran while one was open for 25% -> 26% of each run, Pallas kernels for 0% -> 0%
where the time goes in v14:
time: 132 us; the launch traced here: 131 us
  waiting for transfers between devices  45 us (34%)
  other arithmetic  36.2 us (27%)
  starting transfers between devices  25 us (19%)
  local copies, waits for them, and re-layouts  18.7 us (14%)
  between operations  4.83 us (4%)
  matrix products  1.7 us (1%)
    ppermute x13, waiting for transfers between devices, ag_step(): theirs = lax.ppermute(held, 'shot', [(i, i ^ k) for i in range(n)])  24 us
    ppermute x10, waiting for transfers between devices, rs_step(): got = lax.ppermute(send, 'shot', [(i, i ^ k) for i in range(n)])  20.4 us
    ppermute x13, starting transfers between devices, ag_step(): theirs = lax.ppermute(held, 'shot', [(i, i ^ k) for i in range(n)])  12.3 us
    ppermute x10, starting transfers between devices, rs_step(): got = lax.ppermute(send, 'shot', [(i, i ^ k) for i in range(n)])  11.4 us
    add x3, other arithmetic, inject(): return field + jnp.where(hit, source_gain[0] * wavelet[0, moment], 0.0)  8.08 us
    add x2, other arithmetic, born_second(): 2.0 * born + speed_term * laplace_x(with_halo(born)) - absorber * born  5.83 us
    unnamed x51, local copies, waits for them, and re-layouts  4.8 us
    another operation x1, other arithmetic, damping(): lower = jnp.stack([edges[0], edges[2], edges[4]])[:, None]  3.87 us
  transfers between devices with their start and end apart: 30, of which 16 were waited for; matrix products, arithmetic and copies ran while one was open for 26% of the time, Pallas kernels for 0%

profile of v14, /device:TPU:0, one launch (start us, length us, event | category | flops | bytes accessed | tf_op | source)
XLA Modules:
  0.0 131.4 jit_solution(7878284020946426037)
XLA Ops:
  0.7 1.7 %dynamic-slice_bitcast_fusion.10 = f32[4,64,128]{2,1,0:T(8,128)} fusion(f32[1,32,64,128]{3,2,1,0:T(8,128)} %param.12, s32[]{:T(128)S(6)} %select_n.404), kind=kLoop, calls=%fused_computation.444 | loop fusion | bytes 262148 | tf_op jit(solution)/shard_map/dynamic_slice | solution.py:51
  4.6 3.6 %collective-permute-start = (f32[1,16,2048]{2,1,0:T(8,128)}, f32[1,16,2048]{2,1,0:T(8,128)}, u32[]{:S(2)}, u32[]{:S(2)}) collective-permute-start(f32[1,16,2048]{2,1,0:T(8,128)} %concatenate.199), channel_id=1, source_target_pairs={{0,8},{2,10},{4,12},{6,14},{8,0},{10,2},{12,4},{14,6},{1,9},{3,11}... | collective-permute-start | bytes 393224 | tf_op jit(solution)/shard_map/ppermute | solution.py:120
  10.2 3.9 %pad_maximum_fusion.15 = (f32[3]{0:T(128)S(1)}, f32[3]{0:T(128)S(1)}) fusion(f32[1]{0:T(128)} %get-tuple-element.157, f32[1]{0:T(128)} %get-tuple-element.158, f32[1]{0:T(128)} %get-tuple-element.153, f32[1]{0:T(128)} %get-tuple-element.154, f32[1]{0:T(128)} %get-tuple-element.155, f32[1]{0:T(128)} %get-tuple-element.156), kind=kLoop, calls=%fused_computation.501 | loop fusion | flops 12 | bytes 48 | tf_op jit(solution)/shard_map/stack | solution.py:37
  16.5 2.6 %fusion.144 = f32[24,64,128]{2,1,0:T(8,128)} fusion(f32[32,64,128]{2,1,0:T(8,128)S(1)} %bitcast.208, f32[1,32,64,128]{3,2,1,0:T(8,128)S(1)} %copy-done), kind=kLoop, calls=%fused_computation.324 | loop fusion | flops 5701632 | bytes 8912896 | tf_op jit(solution)/shard_map/add | solution.py:86
  29.9 1.9 %collective-permute-start.5 = (f32[2,16,64]{2,1,0:T(8,128)S(1)}, f32[2,16,64]{2,1,0:T(8,128)S(1)}, u32[]{:S(2)}, u32[]{:S(2)}) collective-permute-start(f32[2,16,64]{2,1,0:T(8,128)S(1)} %maximum_select_fusion.12), channel_id=1, source_target_pairs={{0,4},{2,6},{4,0},{6,2},{8,12},{10,14},{12,8},{14,10},{1,5},{3,7},... | collective-permute-start | bytes 24584 | tf_op jit(solution)/shard_map/ppermute | solution.py:120
  31.9 1.6 %collective-permute-start.4 = (f32[2,8,2048]{2,1,0:T(8,128)S(1)}, f32[2,8,2048]{2,1,0:T(8,128)S(1)}, u32[]{:S(2)}, u32[]{:S(2)}) collective-permute-start(f32[2,8,2048]{2,1,0:T(8,128)S(1)} %get-tuple-element.146), channel_id=1, source_target_pairs={{0,2},{2,0},{4,6},{6,4},{8,10},{10,8},{12,14},{14,12},{1,3},{3,1},... | collective-permute-start | bytes 393224 | tf_op jit(solution)/shard_map/ppermute | solution.py:120
  34.1 2.9 %collective-permute-done.4 = f32[2,8,2048]{2,1,0:T(8,128)S(1)} collective-permute-done((f32[2,8,2048]{2,1,0:T(8,128)S(1)}, f32[2,8,2048]{2,1,0:T(8,128)S(1)}, u32[]{:S(2)}, u32[]{:S(2)}) %collective-permute-start.4) | collective-permute-done | bytes 131104 | tf_op jit(solution)/shard_map/ppermute | solution.py:120
  37.1 2.4 %collective-permute-done.3 = f32[2,8,2048]{2,1,0:T(8,128)S(1)} collective-permute-done((f32[2,8,2048]{2,1,0:T(8,128)S(1)}, f32[2,8,2048]{2,1,0:T(8,128)S(1)}, u32[]{:S(2)}, u32[]{:S(2)}) %collective-permute-start.3) | collective-permute-done | bytes 131104 | tf_op jit(solution)/shard_map/ppermute | solution.py:120
  39.5 3.2 %fusion.3 = (f32[32,64,128]{2,1,0:T(8,128)S(1)}, f32[32,64,128]{2,1,0:T(8,128)S(1)}) fusion(f32[32,64,128]{2,1,0:T(8,128)S(1)} %get-tuple-element.70, f32[32,64,128]{2,1,0:T(8,128)S(1)} %bitcast.210, f32[]{:T(128)S(6)} %mul.394, f32[128]{0:T(128)S(1)} %copy-done.14, f32[32,64]{1,0:T(8,128)S(1)} %broadcast_add_fusion, pred[128]{0:T(512)(128)(4,1)S(1)} %copy-done.17, ...), kind=kLoop, calls=%fused_computation.151 | loop fusion | flops 12058624 | bytes 16012292 | tf_op jit(solution)/shard_map/add | solution.py:213
  42.7 1.3 %multiply_add_fusion.1 = f32[32,64,128]{2,1,0:T(8,128)} fusion(f32[32,64,128]{2,1,0:T(8,128)S(1)} %get-tuple-element.80, f32[32,64,128]{2,1,0:T(8,128)S(1)} %get-tuple-element.78), kind=kLoop, calls=%fused_computation.313 | loop fusion | flops 786432 | bytes 3145728 | tf_op jit(solution)/shard_map/add | solution.py:271
  45.2 1.7 %collective-permute-start.7 = (f32[4,8,2048]{2,1,0:T(8,128)S(1)}, f32[4,8,2048]{2,1,0:T(8,128)S(1)}, u32[]{:S(2)}, u32[]{:S(2)}) collective-permute-start(f32[4,8,2048]{2,1,0:T(8,128)S(1)} %bitcast.234), channel_id=1, source_target_pairs={{0,2},{2,0},{4,6},{6,4},{8,10},{10,8},{12,14},{14,12},{1,3},{3,1},... | collective-permute-start | bytes 786440 | tf_op jit(solution)/shard_map/ppermute | solution.py:120
  46.9 1.6 %collective-permute-done.9 = f32[4,16,64]{2,1,0:T(8,128)S(1)} collective-permute-done((f32[4,16,64]{2,1,0:T(8,128)S(1)}, f32[4,16,64]{2,1,0:T(8,128)S(1)}, u32[]{:S(2)}, u32[]{:S(2)}) %collective-permute-start.9) | collective-permute-done | bytes 16416 | tf_op jit(solution)/shard_map/ppermute | solution.py:120
  49.1 4.0 %fusion.4 = (f32[32,64,128]{2,1,0:T(8,128)}, f32[32,64,128]{2,1,0:T(8,128)}) fusion(f32[32,64,128]{2,1,0:T(8,128)S(1)} %get-tuple-element.68, f32[32,64,128]{2,1,0:T(8,128)S(1)} %get-tuple-element.70, f32[]{:T(128)S(6)} %mul.403, f32[128]{0:T(128)S(1)} %copy-done.14, f32[32,64]{1,0:T(8,128)S(1)} %broadcast_add_fusion, pred[128]{0:T(512)(128)(4,1)S(1)} %copy-done.17, ...), kind=kLoop, calls=%fused_computation.152 | loop fusion | flops 12058624 | bytes 16012292 | tf_op jit(solution)/shard_map/add | solution.py:213
  54.9 1.5 %copy.46 = f32[2048,128]{1,0:T(8,128)S(1)} copy(f32[2048,128]{0,1:T(8,128)} %bitcast.219) | data formatting | bytes 2097152 | tf_op jit(solution)/shard_map/transpose | solution.py:299
  57.8 1.4 %collective-permute-start.12 = (f32[2,2,4,32,128]{4,3,2,1,0:T(8,128)S(1)}, f32[2,2,4,32,128]{4,3,2,1,0:T(8,128)S(1)}, u32[]{:S(2)}, u32[]{:S(2)}) collective-permute-start(f32[2,2,4,32,128]{4,3,2,1,0:T(8,128)S(1)} %dynamic-slice_bitcast_fusion.2), channel_id=1, source_target_pairs={{0,4},{2,6},{4,0},{6,2},{8,12},{10,14},{12,8},{14,10},{1,5},{3,7},... | collective-permute-start | bytes 786440 | tf_op jit(solution)/shard_map/ppermute | solution.py:169
  59.3 1.6 %collective-permute-start.11 = (f32[4,1,4,32,128]{4,3,2,0,1:T(8,128)S(1)}, f32[4,1,4,32,128]{4,3,2,0,1:T(8,128)S(1)}, u32[]{:S(2)}, u32[]{:S(2)}) collective-permute-start(f32[4,1,4,32,128]{4,3,2,0,1:T(8,128)S(1)} %dynamic-slice_bitcast_fusion.3), channel_id=1, source_target_pairs={{0,2},{2,0},{4,6},{6,4},{8,10},{10,8},{12,14},{14,12},{1,3},{3,1},... | collective-permute-start | bytes 786440 | tf_op jit(solution)/shard_map/ppermute | solution.py:169
  61.1 2.9 %fusion.67 = f32[32,64,128]{2,1,0:T(8,128)S(1)} fusion(f32[40,64,128]{2,1,0:T(8,128)S(1)} %constant_dynamic-update-slice_fusion.2, f32[32,64,128]{2,1,0:T(8,128)S(1)} %bitcast.214, f32[32,64,128]{2,1,0:T(8,128)S(1)} %copy-done.3, f32[32,64,128]{2,1,0:T(8,128)S(1)} %mul.404, f32[128]{0:T(128)S(1)} %copy-done.15, f32[32,64]{1,0:T(8,128)S(1)} %broadcast_add_fusion, ...), kind=kLoop, calls=%fused_computation.215 | loop fusion | flops 11272192 | bytes 16007680 | tf_op jit(solution)/shard_map/add | solution.py:234
  64.0 1.6 %collective-permute-done.12 = f32[2,2,4,32,128]{4,3,2,1,0:T(8,128)S(1)} collective-permute-done((f32[2,2,4,32,128]{4,3,2,1,0:T(8,128)S(1)}, f32[2,2,4,32,128]{4,3,2,1,0:T(8,128)S(1)}, u32[]{:S(2)}, u32[]{:S(2)}) %collective-permute-start.12) | collective-permute-done | bytes 262176 | tf_op jit(solution)/shard_map/ppermute | solution.py:169
  67.0 1.6 %collective-permute-start.17 = (f32[2,1,4,32,128]{4,3,2,0,1:T(8,128)S(1)}, f32[2,1,4,32,128]{4,3,2,0,1:T(8,128)S(1)}, u32[]{:S(2)}, u32[]{:S(2)}) collective-permute-start(f32[2,1,4,32,128]{4,3,2,0,1:T(8,128)S(1)} %dynamic-slice_bitcast_fusion.8), channel_id=1, source_target_pairs={{0,2},{2,0},{4,6},{6,4},{8,10},{10,8},{12,14},{14,12},{1,3},{3,1},... | collective-permute-start | bytes 393224 | tf_op jit(solution)/shard_map/ppermute | solution.py:169
  69.7 1.6 %collective-permute-start.15 = (f32[2,2,4,32,128]{4,3,2,1,0:T(8,128)S(1)}, f32[2,2,4,32,128]{4,3,2,1,0:T(8,128)S(1)}, u32[]{:S(2)}, u32[]{:S(2)}) collective-permute-start(f32[2,2,4,32,128]{4,3,2,1,0:T(8,128)S(1)} %dynamic-slice_bitcast_fusion), channel_id=1, source_target_pairs={{0,4},{2,6},{4,0},{6,2},{8,12},{10,14},{12,8},{14,10},{1,5},{3,7},... | collective-permute-start | bytes 786440 | tf_op jit(solution)/shard_map/ppermute | solution.py:169
  72.1 3.2 %fusion.92 = f32[32,64,128]{2,1,0:T(8,128)} fusion(f32[40,64,128]{2,1,0:T(8,128)S(1)} %constant_dynamic-update-slice_fusion.1, s32[32,64,128]{2,1,0:T(8,128)S(1)} %copy-done.1), kind=kLoop, calls=%fused_computation.240 | loop fusion | flops 9175040 | bytes 12845056 | tf_op jit(solution)/shard_map/mul | solution.py:226
  75.4 4.5 %collective-permute-done.15 = f32[2,2,4,32,128]{4,3,2,1,0:T(8,128)S(1)} collective-permute-done((f32[2,2,4,32,128]{4,3,2,1,0:T(8,128)S(1)}, f32[2,2,4,32,128]{4,3,2,1,0:T(8,128)S(1)}, u32[]{:S(2)}, u32[]{:S(2)}) %collective-permute-start.15) | collective-permute-done | bytes 262176 | tf_op jit(solution)/shard_map/ppermute | solution.py:169
  80.6 2.7 %collective-permute-start.21 = (f32[1,1,4,64,128]{4,3,2,1,0:T(8,128)S(1)}, f32[1,1,4,64,128]{4,3,2,1,0:T(8,128)S(1)}, u32[]{:S(2)}, u32[]{:S(2)}) collective-permute-start(f32[1,1,4,64,128]{4,3,2,1,0:T(8,128)S(1)} %dynamic-slice_bitcast_fusion.5), channel_id=1, source_target_pairs={{0,8},{2,10},{4,12},{6,14},{8,0},{10,2},{12,4},{14,6},{1,9},{3,11}... | collective-permute-start | bytes 393224 | tf_op jit(solution)/shard_map/ppermute | solution.py:169
  85.1 5.1 %collective-permute-done.19 = f32[2,1,4,32,128]{4,3,2,0,1:T(8,128)S(1)} collective-permute-done((f32[2,1,4,32,128]{4,3,2,0,1:T(8,128)S(1)}, f32[2,1,4,32,128]{4,3,2,0,1:T(8,128)S(1)}, u32[]{:S(2)}, u32[]{:S(2)}) %collective-permute-start.19) | collective-permute-done | bytes 131104 | tf_op jit(solution)/shard_map/ppermute | solution.py:169
  90.5 7.1 %collective-permute-done.22 = f32[1,1,4,64,128]{4,3,2,1,0:T(8,128)S(1)} collective-permute-done((f32[1,1,4,64,128]{4,3,2,1,0:T(8,128)S(1)}, f32[1,1,4,64,128]{4,3,2,1,0:T(8,128)S(1)}, u32[]{:S(2)}, u32[]{:S(2)}) %collective-permute-start.22) | collective-permute-done | bytes 131104 | tf_op jit(solution)/shard_map/ppermute | solution.py:169
  99.4 6.1 %collective-permute-done.23 = f32[1,4,64,128]{3,2,1,0:T(8,128)S(1)} collective-permute-done((f32[1,4,64,128]{3,2,1,0:T(8,128)S(1)}, f32[1,4,64,128]{3,2,1,0:T(8,128)S(1)}, u32[]{:S(2)}, u32[]{:S(2)}) %collective-permute-start.23) | collective-permute-done | bytes 131104 | tf_op jit(solution)/shard_map/ppermute | solution.py:120
  105.6 1.4 %collective-permute-start.25 = (f32[2,4,32,128]{3,2,1,0:T(8,128)S(1)}, f32[2,4,32,128]{3,2,1,0:T(8,128)S(1)}, u32[]{:S(2)}, u32[]{:S(2)}) collective-permute-start(f32[2,4,32,128]{3,2,1,0:T(8,128)S(1)} %get-tuple-element.142), channel_id=1, source_target_pairs={{0,2},{2,0},{4,6},{6,4},{8,10},{10,8},{12,14},{14,12},{1,3},{3,1},... | collective-permute-start | bytes 393224 | tf_op jit(solution)/shard_map/ppermute | solution.py:120
  107.5 3.1 %collective-permute-done.25 = f32[2,4,32,128]{3,2,1,0:T(8,128)S(1)} collective-permute-done((f32[2,4,32,128]{3,2,1,0:T(8,128)S(1)}, f32[2,4,32,128]{3,2,1,0:T(8,128)S(1)}, u32[]{:S(2)}, u32[]{:S(2)}) %collective-permute-start.25) | collective-permute-done | bytes 131104 | tf_op jit(solution)/shard_map/ppermute | solution.py:120
  110.7 2.7 %collective-permute-done.24 = f32[2,4,32,128]{3,2,1,0:T(8,128)S(1)} collective-permute-done((f32[2,4,32,128]{3,2,1,0:T(8,128)S(1)}, f32[2,4,32,128]{3,2,1,0:T(8,128)S(1)}, u32[]{:S(2)}, u32[]{:S(2)}) %collective-permute-start.24) | collective-permute-done | bytes 131104 | tf_op jit(solution)/shard_map/ppermute | solution.py:120
  115.2 4.7 %collective-permute-done.26 = f32[4,4,32,128]{3,2,1,0:T(8,128)S(1)} collective-permute-done((f32[4,4,32,128]{3,2,1,0:T(8,128)S(1)}, f32[4,4,32,128]{3,2,1,0:T(8,128)S(1)}, u32[]{:S(2)}, u32[]{:S(2)}) %collective-permute-start.26) | collective-permute-done | bytes 262176 | tf_op jit(solution)/shard_map/ppermute | solution.py:120
  120.2 1.1 copy-done.4
  124.6 2.9 %fusion.120 = f32[32,64,128]{2,1,0:T(8,128)S(1)} fusion(f32[40,64,128]{2,1,0:T(8,128)S(1)} %constant_dynamic-update-slice_fusion, f32[32,64,128]{2,1,0:T(8,128)S(1)} %copy-done.7, f32[128]{0:T(128)S(1)} %copy-done.16, f32[32,64]{1,0:T(8,128)S(1)} %broadcast_add_fusion, f32[8,4,64,128]{3,2,1,0:T(8,128)S(1)} %pad_maximum_fusion.13, ...), kind=kLoop, calls=%fused_computation.268 | loop fusion | flops 11534336 | bytes 16007680 | tf_op jit(solution)/shard_map/add | solution.py:234
  (197 shorter events, 37.3 us)
Async XLA Ops:
  0.6 15.9 %copy-start = (f32[1,32,64,128]{3,2,1,0:T(8,128)S(1)}, f32[1,32,64,128]{3,2,1,0:T(8,128)}, u32[]{:S(2)}) copy-start(f32[1,32,64,128]{3,2,1,0:T(8,128)} %param.12) | copy-start | bytes 3145732
  0.7 15.2 %copy-start.18 = (f32[1,4]{1,0:T(1,128)S(1)}, f32[1,4]{1,0:T(1,128)}, u32[]{:S(2)}) copy-start(f32[1,4]{1,0:T(1,128)} %param.16) | copy-start | bytes 52
  2.3 22.9 %collective-permute-start.2 = (f32[4,64,128]{2,1,0:T(8,128)}, f32[4,64,128]{2,1,0:T(8,128)}, u32[]{:S(2)}, u32[]{:S(2)}) collective-permute-start(f32[4,64,128]{2,1,0:T(8,128)} %dynamic-slice_bitcast_fusion.10), channel_id=1, source_target_pairs={{0,1},{1,0},{2,3},{3,2},{4,5},{5,4},{6,7},{7,6},{8,9},{9,8},{10,11... | collective-permute-start | bytes 393224 | tf_op jit(solution)/shard_map/ppermute | solution.py:52
  4.6 24.0 %collective-permute-start = (f32[1,16,2048]{2,1,0:T(8,128)}, f32[1,16,2048]{2,1,0:T(8,128)}, u32[]{:S(2)}, u32[]{:S(2)}) collective-permute-start(f32[1,16,2048]{2,1,0:T(8,128)} %concatenate.199), channel_id=1, source_target_pairs={{0,8},{2,10},{4,12},{6,14},{8,0},{10,2},{12,4},{14,6},{1,9},{3,11}... | collective-permute-start | bytes 393224 | tf_op jit(solution)/shard_map/ppermute | solution.py:120
  8.2 16.2 %collective-permute-start.1 = (f32[1,16,64]{2,1,0:T(8,128)}, f32[1,16,64]{2,1,0:T(8,128)}, u32[]{:S(2)}, u32[]{:S(2)}) collective-permute-start(f32[1,16,64]{2,1,0:T(8,128)} %bitcast.265), channel_id=1, source_target_pairs={{0,8},{2,10},{4,12},{6,14},{8,0},{10,2},{12,4},{14,6},{1,9},{3,11}... | collective-permute-start | bytes 12296 | tf_op jit(solution)/shard_map/ppermute | solution.py:120
  29.9 4.2 %collective-permute-start.5 = (f32[2,16,64]{2,1,0:T(8,128)S(1)}, f32[2,16,64]{2,1,0:T(8,128)S(1)}, u32[]{:S(2)}, u32[]{:S(2)}) collective-permute-start(f32[2,16,64]{2,1,0:T(8,128)S(1)} %maximum_select_fusion.12), channel_id=1, source_target_pairs={{0,4},{2,6},{4,0},{6,2},{8,12},{10,14},{12,8},{14,10},{1,5},{3,7},... | collective-permute-start | bytes 24584 | tf_op jit(solution)/shard_map/ppermute | solution.py:120
  31.9 5.1 %collective-permute-start.4 = (f32[2,8,2048]{2,1,0:T(8,128)S(1)}, f32[2,8,2048]{2,1,0:T(8,128)S(1)}, u32[]{:S(2)}, u32[]{:S(2)}) collective-permute-start(f32[2,8,2048]{2,1,0:T(8,128)S(1)} %get-tuple-element.146), channel_id=1, source_target_pairs={{0,2},{2,0},{4,6},{6,4},{8,10},{10,8},{12,14},{14,12},{1,3},{3,1},... | collective-permute-start | bytes 393224 | tf_op jit(solution)/shard_map/ppermute | solution.py:120
  33.5 6.0 %collective-permute-start.6 = (f32[4,64,128]{2,1,0:T(8,128)S(1)}, f32[4,64,128]{2,1,0:T(8,128)S(1)}, u32[]{:S(2)}, u32[]{:S(2)}) collective-permute-start(f32[4,64,128]{2,1,0:T(8,128)S(1)} %constant_dynamic-slice_fusion.5), channel_id=1, source_target_pairs={{0,1},{1,0},{2,3},{3,2},{4,5},{5,4},{6,7},{7,6},{8,9},{9,8},{10,11... | collective-permute-start | bytes 393224 | tf_op jit(solution)/shard_map/ppermute | solution.py:52
  33.5 5.9 %collective-permute-start.3 = (f32[2,8,2048]{2,1,0:T(8,128)S(1)}, f32[2,8,2048]{2,1,0:T(8,128)S(1)}, u32[]{:S(2)}, u32[]{:S(2)}) collective-permute-start(f32[2,8,2048]{2,1,0:T(8,128)S(1)} %get-tuple-element.147), channel_id=1, source_target_pairs={{0,4},{2,6},{4,0},{6,2},{8,12},{10,14},{12,8},{14,10},{1,5},{3,7},... | collective-permute-start | bytes 393224 | tf_op jit(solution)/shard_map/ppermute | solution.py:120
  44.1 5.0 %collective-permute-start.10 = (f32[4,64,128]{2,1,0:T(8,128)S(1)}, f32[4,64,128]{2,1,0:T(8,128)S(1)}, u32[]{:S(2)}, u32[]{:S(2)}) collective-permute-start(f32[4,64,128]{2,1,0:T(8,128)S(1)} %constant_dynamic-slice_fusion.4), channel_id=1, source_target_pairs={{0,1},{1,0},{2,3},{3,2},{4,5},{5,4},{6,7},{7,6},{8,9},{9,8},{10,11... | collective-permute-start | bytes 393224 | tf_op jit(solution)/shard_map/ppermute | solution.py:52
  44.1 4.3 %collective-permute-start.9 = (f32[4,16,64]{2,1,0:T(8,128)S(1)}, f32[4,16,64]{2,1,0:T(8,128)S(1)}, u32[]{:S(2)}, u32[]{:S(2)}) collective-permute-start(f32[4,16,64]{2,1,0:T(8,128)S(1)} %bitcast.258), channel_id=1, source_target_pairs={{0,2},{2,0},{4,6},{6,4},{8,10},{10,8},{12,14},{14,12},{1,3},{3,1},... | collective-permute-start | bytes 49160 | tf_op jit(solution)/shard_map/ppermute | solution.py:120
  44.9 8.4 %collective-permute-start.8 = (f32[4,8,2048]{2,1,0:T(8,128)S(1)}, f32[4,8,2048]{2,1,0:T(8,128)S(1)}, u32[]{:S(2)}, u32[]{:S(2)}) collective-permute-start(f32[4,8,2048]{2,1,0:T(8,128)S(1)} %bitcast.232), channel_id=1, source_target_pairs={{0,4},{2,6},{4,0},{6,2},{8,12},{10,14},{12,8},{14,10},{1,5},{3,7},... | collective-permute-start | bytes 786440 | tf_op jit(solution)/shard_map/ppermute | solution.py:120
  45.2 8.5 %collective-permute-start.7 = (f32[4,8,2048]{2,1,0:T(8,128)S(1)}, f32[4,8,2048]{2,1,0:T(8,128)S(1)}, u32[]{:S(2)}, u32[]{:S(2)}) collective-permute-start(f32[4,8,2048]{2,1,0:T(8,128)S(1)} %bitcast.234), channel_id=1, source_target_pairs={{0,2},{2,0},{4,6},{6,4},{8,10},{10,8},{12,14},{14,12},{1,3},{3,1},... | collective-permute-start | bytes 786440 | tf_op jit(solution)/shard_map/ppermute | solution.py:120
  56.7 4.3 %collective-permute-start.13 = (f32[4,64,128]{2,1,0:T(8,128)S(1)}, f32[4,64,128]{2,1,0:T(8,128)S(1)}, u32[]{:S(2)}, u32[]{:S(2)}) collective-permute-start(f32[4,64,128]{2,1,0:T(8,128)S(1)} %constant_dynamic-slice_fusion.3), channel_id=1, source_target_pairs={{0,1},{1,0},{2,3},{3,2},{4,5},{5,4},{6,7},{7,6},{8,9},{9,8},{10,11... | collective-permute-start | bytes 393224 | tf_op jit(solution)/shard_map/ppermute | solution.py:52
  57.8 7.8 %collective-permute-start.12 = (f32[2,2,4,32,128]{4,3,2,1,0:T(8,128)S(1)}, f32[2,2,4,32,128]{4,3,2,1,0:T(8,128)S(1)}, u32[]{:S(2)}, u32[]{:S(2)}) collective-permute-start(f32[2,2,4,32,128]{4,3,2,1,0:T(8,128)S(1)} %dynamic-slice_bitcast_fusion.2), channel_id=1, source_target_pairs={{0,4},{2,6},{4,0},{6,2},{8,12},{10,14},{12,8},{14,10},{1,5},{3,7},... | collective-permute-start | bytes 786440 | tf_op jit(solution)/shard_map/ppermute | solution.py:169
  59.3 7.5 %collective-permute-start.11 = (f32[4,1,4,32,128]{4,3,2,0,1:T(8,128)S(1)}, f32[4,1,4,32,128]{4,3,2,0,1:T(8,128)S(1)}, u32[]{:S(2)}, u32[]{:S(2)}) collective-permute-start(f32[4,1,4,32,128]{4,3,2,0,1:T(8,128)S(1)} %dynamic-slice_bitcast_fusion.3), channel_id=1, source_target_pairs={{0,2},{2,0},{4,6},{6,4},{8,10},{10,8},{12,14},{14,12},{1,3},{3,1},... | collective-permute-start | bytes 786440 | tf_op jit(solution)/shard_map/ppermute | solution.py:169
  66.9 5.2 %collective-permute-start.18 = (f32[4,64,128]{2,1,0:T(8,128)S(1)}, f32[4,64,128]{2,1,0:T(8,128)S(1)}, u32[]{:S(2)}, u32[]{:S(2)}) collective-permute-start(f32[4,64,128]{2,1,0:T(8,128)S(1)} %constant_dynamic-slice_fusion.2), channel_id=1, source_target_pairs={{0,1},{1,0},{2,3},{3,2},{4,5},{5,4},{6,7},{7,6},{8,9},{9,8},{10,11... | collective-permute-start | bytes 393224 | tf_op jit(solution)/shard_map/ppermute | solution.py:52
  67.0 8.4 %collective-permute-start.17 = (f32[2,1,4,32,128]{4,3,2,0,1:T(8,128)S(1)}, f32[2,1,4,32,128]{4,3,2,0,1:T(8,128)S(1)}, u32[]{:S(2)}, u32[]{:S(2)}) collective-permute-start(f32[2,1,4,32,128]{4,3,2,0,1:T(8,128)S(1)} %dynamic-slice_bitcast_fusion.8), channel_id=1, source_target_pairs={{0,2},{2,0},{4,6},{6,4},{8,10},{10,8},{12,14},{14,12},{1,3},{3,1},... | collective-permute-start | bytes 393224 | tf_op jit(solution)/shard_map/ppermute | solution.py:169
  68.6 6.8 %collective-permute-start.16 = (f32[2,1,4,32,128]{4,3,2,0,1:T(8,128)S(1)}, f32[2,1,4,32,128]{4,3,2,0,1:T(8,128)S(1)}, u32[]{:S(2)}, u32[]{:S(2)}) collective-permute-start(f32[2,1,4,32,128]{4,3,2,0,1:T(8,128)S(1)} %dynamic-slice_bitcast_fusion.9), channel_id=1, source_target_pairs={{0,4},{2,6},{4,0},{6,2},{8,12},{10,14},{12,8},{14,10},{1,5},{3,7},... | collective-permute-start | bytes 393224 | tf_op jit(solution)/shard_map/ppermute | solution.py:169
  69.7 10.2 %collective-permute-start.15 = (f32[2,2,4,32,128]{4,3,2,1,0:T(8,128)S(1)}, f32[2,2,4,32,128]{4,3,2,1,0:T(8,128)S(1)}, u32[]{:S(2)}, u32[]{:S(2)}) collective-permute-start(f32[2,2,4,32,128]{4,3,2,1,0:T(8,128)S(1)} %dynamic-slice_bitcast_fusion), channel_id=1, source_target_pairs={{0,4},{2,6},{4,0},{6,2},{8,12},{10,14},{12,8},{14,10},{1,5},{3,7},... | collective-permute-start | bytes 786440 | tf_op jit(solution)/shard_map/ppermute | solution.py:169
  71.3 8.6 %collective-permute-start.14 = (f32[4,1,4,32,128]{4,3,2,0,1:T(8,128)S(1)}, f32[4,1,4,32,128]{4,3,2,0,1:T(8,128)S(1)}, u32[]{:S(2)}, u32[]{:S(2)}) collective-permute-start(f32[4,1,4,32,128]{4,3,2,0,1:T(8,128)S(1)} %dynamic-slice_bitcast_fusion.1), channel_id=1, source_target_pairs={{0,2},{2,0},{4,6},{6,4},{8,10},{10,8},{12,14},{14,12},{1,3},{3,1},... | collective-permute-start | bytes 786440 | tf_op jit(solution)/shard_map/ppermute | solution.py:169
  80.0 5.0 %collective-permute-start.20 = (f32[2,1,4,32,128]{4,3,2,0,1:T(8,128)S(1)}, f32[2,1,4,32,128]{4,3,2,0,1:T(8,128)S(1)}, u32[]{:S(2)}, u32[]{:S(2)}) collective-permute-start(f32[2,1,4,32,128]{4,3,2,0,1:T(8,128)S(1)} %dynamic-slice_bitcast_fusion.6), channel_id=1, source_target_pairs={{0,2},{2,0},{4,6},{6,4},{8,10},{10,8},{12,14},{14,12},{1,3},{3,1},... | collective-permute-start | bytes 393224 | tf_op jit(solution)/shard_map/ppermute | solution.py:169
  80.6 9.6 %collective-permute-start.21 = (f32[1,1,4,64,128]{4,3,2,1,0:T(8,128)S(1)}, f32[1,1,4,64,128]{4,3,2,1,0:T(8,128)S(1)}, u32[]{:S(2)}, u32[]{:S(2)}) collective-permute-start(f32[1,1,4,64,128]{4,3,2,1,0:T(8,128)S(1)} %dynamic-slice_bitcast_fusion.5), channel_id=1, source_target_pairs={{0,8},{2,10},{4,12},{6,14},{8,0},{10,2},{12,4},{14,6},{1,9},{3,11}... | collective-permute-start | bytes 393224 | tf_op jit(solution)/shard_map/ppermute | solution.py:169
  83.3 6.9 %collective-permute-start.19 = (f32[2,1,4,32,128]{4,3,2,0,1:T(8,128)S(1)}, f32[2,1,4,32,128]{4,3,2,0,1:T(8,128)S(1)}, u32[]{:S(2)}, u32[]{:S(2)}) collective-permute-start(f32[2,1,4,32,128]{4,3,2,0,1:T(8,128)S(1)} %dynamic-slice_bitcast_fusion.7), channel_id=1, source_target_pairs={{0,4},{2,6},{4,0},{6,2},{8,12},{10,14},{12,8},{14,10},{1,5},{3,7},... | collective-permute-start | bytes 393224 | tf_op jit(solution)/shard_map/ppermute | solution.py:169
  90.3 7.3 %collective-permute-start.22 = (f32[1,1,4,64,128]{4,3,2,1,0:T(8,128)S(1)}, f32[1,1,4,64,128]{4,3,2,1,0:T(8,128)S(1)}, u32[]{:S(2)}, u32[]{:S(2)}) collective-permute-start(f32[1,1,4,64,128]{4,3,2,1,0:T(8,128)S(1)} %dynamic-slice_bitcast_fusion.4), channel_id=1, source_target_pairs={{0,8},{2,10},{4,12},{6,14},{8,0},{10,2},{12,4},{14,6},{1,9},{3,11}... | collective-permute-start | bytes 393224 | tf_op jit(solution)/shard_map/ppermute | solution.py:169
  99.3 6.2 %collective-permute-start.23 = (f32[1,4,64,128]{3,2,1,0:T(8,128)S(1)}, f32[1,4,64,128]{3,2,1,0:T(8,128)S(1)}, u32[]{:S(2)}, u32[]{:S(2)}) collective-permute-start(f32[1,4,64,128]{3,2,1,0:T(8,128)S(1)} %fusion.1), channel_id=1, source_target_pairs={{0,8},{2,10},{4,12},{6,14},{8,0},{10,2},{12,4},{14,6},{1,9},{3,11}... | collective-permute-start | bytes 393224 | tf_op jit(solution)/shard_map/ppermute | solution.py:120
  105.6 5.0 %collective-permute-start.25 = (f32[2,4,32,128]{3,2,1,0:T(8,128)S(1)}, f32[2,4,32,128]{3,2,1,0:T(8,128)S(1)}, u32[]{:S(2)}, u32[]{:S(2)}) collective-permute-start(f32[2,4,32,128]{3,2,1,0:T(8,128)S(1)} %get-tuple-element.142), channel_id=1, source_target_pairs={{0,2},{2,0},{4,6},{6,4},{8,10},{10,8},{12,14},{14,12},{1,3},{3,1},... | collective-permute-start | bytes 393224 | tf_op jit(solution)/shard_map/ppermute | solution.py:120
  107.0 6.4 %collective-permute-start.24 = (f32[2,4,32,128]{3,2,1,0:T(8,128)S(1)}, f32[2,4,32,128]{3,2,1,0:T(8,128)S(1)}, u32[]{:S(2)}, u32[]{:S(2)}) collective-permute-start(f32[2,4,32,128]{3,2,1,0:T(8,128)S(1)} %get-tuple-element.143), channel_id=1, source_target_pairs={{0,4},{2,6},{4,0},{6,2},{8,12},{10,14},{12,8},{14,10},{1,5},{3,7},... | collective-permute-start | bytes 393224 | tf_op jit(solution)/shard_map/ppermute | solution.py:120
  113.4 6.6 %collective-permute-start.27 = (f32[4,4,32,128]{3,2,1,0:T(8,128)S(1)}, f32[4,4,32,128]{3,2,1,0:T(8,128)S(1)}, u32[]{:S(2)}, u32[]{:S(2)}) collective-permute-start(f32[4,4,32,128]{3,2,1,0:T(8,128)S(1)} %bitcast.240), channel_id=1, source_target_pairs={{0,4},{2,6},{4,0},{6,2},{8,12},{10,14},{12,8},{14,10},{1,5},{3,7},... | collective-permute-start | bytes 786440 | tf_op jit(solution)/shard_map/ppermute | solution.py:120
  113.5 6.4 %collective-permute-start.26 = (f32[4,4,32,128]{3,2,1,0:T(8,128)S(1)}, f32[4,4,32,128]{3,2,1,0:T(8,128)S(1)}, u32[]{:S(2)}, u32[]{:S(2)}) collective-permute-start(f32[4,4,32,128]{3,2,1,0:T(8,128)S(1)} %bitcast.246), channel_id=1, source_target_pairs={{0,2},{2,0},{4,6},{6,4},{8,10},{10,8},{12,14},{14,12},{1,3},{3,1},... | collective-permute-start | bytes 786440 | tf_op jit(solution)/shard_map/ppermute | solution.py:120
  122.2 1.6 %collective-permute-start.28 = (f32[4,64,128]{2,1,0:T(8,128)}, f32[4,64,128]{2,1,0:T(8,128)S(1)}, u32[]{:S(2)}, u32[]{:S(2)}) collective-permute-start(f32[4,64,128]{2,1,0:T(8,128)} %constant_dynamic-slice_fusion), channel_id=1, source_target_pairs={{0,1},{1,0},{2,3},{3,2},{4,5},{5,4},{6,7},{7,6},{8,9},{9,8},{10,11... | collective-permute-start | bytes 393224 | tf_op jit(solution)/shard_map/ppermute | solution.py:52
  128.9 1.9 %collective-permute-start.29 = (f32[1,2,256]{2,1,0:T(2,128)S(1)}, f32[1,2,256]{2,1,0:T(2,128)S(1)}, u32[]{:S(2)}, u32[]{:S(2)}) collective-permute-start(f32[1,2,256]{2,1,0:T(2,128)S(1)} %maximum_bitcast_fusion), channel_id=1, source_target_pairs={{0,1},{1,0},{2,3},{3,2},{4,5},{5,4},{6,7},{7,6},{8,9},{9,8},{10,11... | collective-permute-start | bytes 6152 | tf_op jit(solution)/shard_map/ppermute | solution.py:363
  (22 other events, 67.5 us)

commit v15 on v14

--- a/solution.py
+++ b/solution.py
@@ -140,8 +140,24 @@
     return {"held": held, "kind": kind, "order": list(order), "i": 0, "bits": list(bits)}
 
 
+def split_step(held, k, left):
+    me = lax.axis_index("shot")
+    low = 2 ** left.index(k)
+    high = held.shape[0] // (2 * low)
+    split = held.reshape((high, 2, low) + held.shape[1:])
+    mine = (me // k) % 2
+    keep = lax.dynamic_index_in_dim(split, mine, axis=1, keepdims=False)
+    send = lax.dynamic_index_in_dim(split, 1 - mine, axis=1, keepdims=False)
+    shape = (high * low,) + held.shape[1:]
+    return keep.reshape(shape), send.reshape(shape)
+
+
 def chain_step(c):
     k = c["order"][c["i"]]
+    if c["kind"] == "pre":
+        n = lax.axis_size("shot")
+        keep, send = c["slices"]()
+        return keep + lax.ppermute(send, "shot", [(i, i ^ k) for i in range(n)])
     if c["kind"] == "ag":
         return ag_step(c["held"], k, c["bits"])
     return rs_step(c["held"], k, c["bits"])
@@ -154,6 +170,7 @@
     if c["kind"] == "ag":
         c["bits"].append(k)
     else:
+        c["kind"] = "rs"
         c["bits"].remove(k)
 
 
@@ -280,7 +297,15 @@
     top = far_first[0]
     model_c = chain(model_held, "ag", far_first[:1])
     gains_c = chain(gains_held, "ag", far_first)
-    tasks = [task_wave(0), light_prep, task_wave(2)]
+    light_orders = {"la": near_first[:-1], "lb": swap_first(near_first[:-1])}
+
+    def wave_and_split():
+        task_wave(2)()
+        pieces = halves(st["light"].reshape(n_shot, slab, span_y, span_z), 2)
+        for (name, order), piece in zip(sorted(light_orders.items()), pieces):
+            st[name + "_keep"], st[name + "_send"] = split_step(piece, order[0], list(near_first))
+
+    tasks = [task_wave(0), light_prep, wave_and_split]
     run_group([model_c, gains_c], tasks[0])
     half_a, half_b = halves(model_c["held"], 1)
     model_a = chain(half_a, "ag", far_first[1:], [top])
@@ -291,9 +316,10 @@
         tasks[i]()
     model_held = jnp.concatenate([model_a["held"], model_b["held"]], axis=1)
     gains_held = gains_c["held"]
-    light_a, light_b = halves(st["light"].reshape(n_shot, slab, span_y, span_z), 2)
-    light_a = chain(light_a, "rs", near_first[:-1], near_first)
-    light_b = chain(light_b, "rs", swap_first(near_first[:-1]), near_first)
+    light_a = chain(None, "pre", light_orders["la"], near_first)
+    light_b = chain(None, "pre", light_orders["lb"], near_first)
+    light_a["slices"] = lambda: (st["la_keep"], st["la_send"])
+    light_b["slices"] = lambda: (st["lb_keep"], st["lb_send"])
 
     def born_pass():
         model = model_held.reshape(span_z, span_x * span_y).T.reshape(span_x, span_y, span_z)

time: 132 us -> 130 us (0.985)
  waiting for transfers between devices: 45 us -> 41.9 us
  local copies, waits for them, and re-layouts: 18.7 us -> 20.7 us
  other arithmetic: 36.2 us -> 34.8 us
    ppermute x13, waiting for transfers between devices: 24 us -> 20.8 us  [ag_step(): theirs = lax.ppermute(held, 'shot', [(i, i ^ k) for i in range(n)])]
    ppermute x0 -> x2, waiting for transfers between devices: none -> 3.04 us  [chain_step(): return keep + lax.ppermute(send, 'shot', [(i, i ^ k) for i in range(n)])]
    ppermute x10 -> x8, starting transfers between devices: 11.4 us -> 8.48 us  [rs_step(): got = lax.ppermute(send, 'shot', [(i, i ^ k) for i in range(n)])]
    ppermute x10 -> x8, waiting for transfers between devices: 20.4 us -> 17.6 us  [rs_step(): got = lax.ppermute(send, 'shot', [(i, i ^ k) for i in range(n)])]
    ppermute x0 -> x2, starting transfers between devices: none -> 2.79 us  [chain_step(): return keep + lax.ppermute(send, 'shot', [(i, i ^ k) for i in range(n)])]
    unnamed x51 -> x55, local copies, waits for them, and re-layouts: 4.8 us -> 5.27 us
  transfers between devices with their start and end apart: 30 -> 30, of which waited for: 16 -> 15; matrix products, arithmetic and copies ran while one was open for 26% -> 28% of each run, Pallas kernels for 0% -> 0%
where the time goes in v15:
time: 130 us; the launch traced here: 129 us
  waiting for transfers between devices  41.9 us (32%)
  other arithmetic  34.8 us (27%)
  starting transfers between devices  25.6 us (20%)
  local copies, waits for them, and re-layouts  20.7 us (16%)
  between operations  4.71 us (4%)
  matrix products  1.7 us (1%)
    ppermute x13, waiting for transfers between devices, ag_step(): theirs = lax.ppermute(held, 'shot', [(i, i ^ k) for i in range(n)])  20.8 us
    ppermute x8, waiting for transfers between devices, rs_step(): got = lax.ppermute(send, 'shot', [(i, i ^ k) for i in range(n)])  17.6 us
    ppermute x13, starting transfers between devices, ag_step(): theirs = lax.ppermute(held, 'shot', [(i, i ^ k) for i in range(n)])  13 us
    ppermute x8, starting transfers between devices, rs_step(): got = lax.ppermute(send, 'shot', [(i, i ^ k) for i in range(n)])  8.48 us
    add x3, other arithmetic, inject(): return field + jnp.where(hit, source_gain[0] * wavelet[0, moment], 0.0)  8.05 us
    add x2, other arithmetic, born_second(): 2.0 * born + speed_term * laplace_x(with_halo(born)) - absorber * born  5.83 us
    unnamed x55, local copies, waits for them, and re-layouts  5.27 us
    another operation x1, other arithmetic, damping(): lower = jnp.stack([edges[0], edges[2], edges[4]])[:, None]  3.74 us
  transfers between devices with their start and end apart: 30, of which 15 were waited for; matrix products, arithmetic and copies ran while one was open for 28% of the time, Pallas kernels for 0%

profile of v15, /device:TPU:0, one launch (start us, length us, event | category | flops | bytes accessed | tf_op | source)
XLA Modules:
  0.0 129.4 jit_solution(4659868927207910406)
XLA Ops:
  0.7 1.7 %dynamic-slice_bitcast_fusion.10 = f32[4,64,128]{2,1,0:T(8,128)} fusion(f32[1,32,64,128]{3,2,1,0:T(8,128)} %param.12, s32[]{:T(128)S(6)} %select_n.404), kind=kLoop, calls=%fused_computation.441 | loop fusion | bytes 262148 | tf_op jit(solution)/shard_map/dynamic_slice | solution.py:51
  2.8 1.0 copy.38
  4.6 3.6 %collective-permute-start = (f32[1,16,2048]{2,1,0:T(8,128)}, f32[1,16,2048]{2,1,0:T(8,128)}, u32[]{:S(2)}, u32[]{:S(2)}) collective-permute-start(f32[1,16,2048]{2,1,0:T(8,128)} %concatenate.199), channel_id=1, source_target_pairs={{0,8},{2,10},{4,12},{6,14},{8,0},{10,2},{12,4},{14,6},{1,9},{3,11}... | collective-permute-start | bytes 393224 | tf_op jit(solution)/shard_map/ppermute | solution.py:120
  10.2 3.7 %pad_maximum_fusion.15 = (f32[3]{0:T(128)S(1)}, f32[3]{0:T(128)S(1)}) fusion(f32[1]{0:T(128)} %get-tuple-element.167, f32[1]{0:T(128)} %get-tuple-element.168, f32[1]{0:T(128)} %get-tuple-element.163, f32[1]{0:T(128)} %get-tuple-element.164, f32[1]{0:T(128)} %get-tuple-element.165, f32[1]{0:T(128)} %get-tuple-element.166), kind=kLoop, calls=%fused_computation.500 | loop fusion | flops 12 | bytes 48 | tf_op jit(solution)/shard_map/stack | solution.py:37
  16.3 2.6 %fusion.144 = f32[24,64,128]{2,1,0:T(8,128)} fusion(f32[32,64,128]{2,1,0:T(8,128)S(1)} %bitcast.205, f32[1,32,64,128]{3,2,1,0:T(8,128)S(1)} %copy-done), kind=kLoop, calls=%fused_computation.324 | loop fusion | flops 5701632 | bytes 8912896 | tf_op jit(solution)/shard_map/add | solution.py:86
  28.2 1.1 maximum_select_fusion.4
  29.5 1.9 %collective-permute-start.5 = (f32[2,16,64]{2,1,0:T(8,128)S(1)}, f32[2,16,64]{2,1,0:T(8,128)S(1)}, u32[]{:S(2)}, u32[]{:S(2)}) collective-permute-start(f32[2,16,64]{2,1,0:T(8,128)S(1)} %maximum_select_fusion.12), channel_id=1, source_target_pairs={{0,4},{2,6},{4,0},{6,2},{8,12},{10,14},{12,8},{14,10},{1,5},{3,7},... | collective-permute-start | bytes 24584 | tf_op jit(solution)/shard_map/ppermute | solution.py:120
  31.5 1.6 %collective-permute-start.4 = (f32[2,8,2048]{2,1,0:T(8,128)S(1)}, f32[2,8,2048]{2,1,0:T(8,128)S(1)}, u32[]{:S(2)}, u32[]{:S(2)}) collective-permute-start(f32[2,8,2048]{2,1,0:T(8,128)S(1)} %get-tuple-element.156), channel_id=1, source_target_pairs={{0,2},{2,0},{4,6},{6,4},{8,10},{10,8},{12,14},{14,12},{1,3},{3,1},... | collective-permute-start | bytes 393224 | tf_op jit(solution)/shard_map/ppermute | solution.py:120
  33.7 2.9 %collective-permute-done.4 = f32[2,8,2048]{2,1,0:T(8,128)S(1)} collective-permute-done((f32[2,8,2048]{2,1,0:T(8,128)S(1)}, f32[2,8,2048]{2,1,0:T(8,128)S(1)}, u32[]{:S(2)}, u32[]{:S(2)}) %collective-permute-start.4) | collective-permute-done | bytes 131104 | tf_op jit(solution)/shard_map/ppermute | solution.py:120
  36.6 2.4 %collective-permute-done.3 = f32[2,8,2048]{2,1,0:T(8,128)S(1)} collective-permute-done((f32[2,8,2048]{2,1,0:T(8,128)S(1)}, f32[2,8,2048]{2,1,0:T(8,128)S(1)}, u32[]{:S(2)}, u32[]{:S(2)}) %collective-permute-start.3) | collective-permute-done | bytes 131104 | tf_op jit(solution)/shard_map/ppermute | solution.py:120
  39.1 3.2 %fusion.3 = (f32[32,64,128]{2,1,0:T(8,128)S(1)}, f32[32,64,128]{2,1,0:T(8,128)S(1)}) fusion(f32[32,64,128]{2,1,0:T(8,128)S(1)} %get-tuple-element.73, f32[32,64,128]{2,1,0:T(8,128)S(1)} %bitcast.207, f32[]{:T(128)S(6)} %mul.394, f32[128]{0:T(128)S(1)} %copy-done.16, f32[32,64]{1,0:T(8,128)S(1)} %broadcast_add_fusion, pred[128]{0:T(512)(128)(4,1)S(1)} %copy-done.19, ...), kind=kLoop, calls=%fused_computation.151 | loop fusion | flops 12058624 | bytes 16012292 | tf_op jit(solution)/shard_map/add | solution.py:230
  44.5 1.7 %collective-permute-start.7 = (f32[4,8,2048]{2,1,0:T(8,128)S(1)}, f32[4,8,2048]{2,1,0:T(8,128)S(1)}, u32[]{:S(2)}, u32[]{:S(2)}) collective-permute-start(f32[4,8,2048]{2,1,0:T(8,128)S(1)} %bitcast.234), channel_id=1, source_target_pairs={{0,2},{2,0},{4,6},{6,4},{8,10},{10,8},{12,14},{14,12},{1,3},{3,1},... | collective-permute-start | bytes 786440 | tf_op jit(solution)/shard_map/ppermute | solution.py:120
  48.6 4.0 %fusion.4 = (f32[32,64,128]{2,1,0:T(8,128)}, f32[32,64,128]{2,1,0:T(8,128)}) fusion(f32[32,64,128]{2,1,0:T(8,128)S(1)} %get-tuple-element.71, f32[32,64,128]{2,1,0:T(8,128)S(1)} %get-tuple-element.73, f32[]{:T(128)S(6)} %mul.403, f32[128]{0:T(128)S(1)} %copy-done.16, f32[32,64]{1,0:T(8,128)S(1)} %broadcast_add_fusion, pred[128]{0:T(512)(128)(4,1)S(1)} %copy-done.19, ...), kind=kLoop, calls=%fused_computation.152 | loop fusion | flops 12058624 | bytes 16012292 | tf_op jit(solution)/shard_map/add | solution.py:230
  53.2 1.1 pad_maximum_fusion.12
  54.2 1.5 %copy.48 = f32[2048,128]{1,0:T(8,128)S(1)} copy(f32[2048,128]{0,1:T(8,128)} %bitcast.216) | data formatting | bytes 2097152 | tf_op jit(solution)/shard_map/transpose | solution.py:325
  56.7 1.3 collective-permute-start.12
  58.0 1.5 %collective-permute-start.11 = (f32[4,4,32,128]{3,2,1,0:T(8,128)S(1)}, f32[4,4,32,128]{3,2,1,0:T(8,128)S(1)}, u32[]{:S(2)}, u32[]{:S(2)}) collective-permute-start(f32[4,4,32,128]{3,2,1,0:T(8,128)S(1)} %copy-done.12), channel_id=1, source_target_pairs={{0,2},{2,0},{4,6},{6,4},{8,10},{10,8},{12,14},{14,12},{1,3},{3,1},... | collective-permute-start | bytes 786440 | tf_op jit(solution)/shard_map/ppermute | solution.py:160
  59.8 2.9 %fusion.67 = f32[32,64,128]{2,1,0:T(8,128)S(1)} fusion(f32[40,64,128]{2,1,0:T(8,128)S(1)} %constant_dynamic-update-slice_fusion.2, f32[32,64,128]{2,1,0:T(8,128)S(1)} %bitcast.211, f32[32,64,128]{2,1,0:T(8,128)S(1)} %copy-done.3, f32[32,64,128]{2,1,0:T(8,128)S(1)} %mul.404, f32[128]{0:T(128)S(1)} %copy-done.17, f32[32,64]{1,0:T(8,128)S(1)} %broadcast_add_fusion, ...), kind=kLoop, calls=%fused_computation.215 | loop fusion | flops 11272192 | bytes 16007680 | tf_op jit(solution)/shard_map/add | solution.py:251
  62.7 2.1 %collective-permute-done.12 = f32[4,4,32,128]{3,2,1,0:T(8,128)S(1)} collective-permute-done((f32[4,4,32,128]{3,2,1,0:T(8,128)S(1)}, f32[4,4,32,128]{3,2,1,0:T(8,128)S(1)}, u32[]{:S(2)}, u32[]{:S(2)}) %collective-permute-start.12) | collective-permute-done | bytes 262176 | tf_op jit(solution)/shard_map/ppermute | solution.py:160
  66.0 1.6 %collective-permute-start.17 = (f32[2,1,4,32,128]{4,3,2,0,1:T(8,128)S(1)}, f32[2,1,4,32,128]{4,3,2,0,1:T(8,128)S(1)}, u32[]{:S(2)}, u32[]{:S(2)}) collective-permute-start(f32[2,1,4,32,128]{4,3,2,0,1:T(8,128)S(1)} %dynamic-slice_bitcast_fusion.8), channel_id=1, source_target_pairs={{0,2},{2,0},{4,6},{6,4},{8,10},{10,8},{12,14},{14,12},{1,3},{3,1},... | collective-permute-start | bytes 393224 | tf_op jit(solution)/shard_map/ppermute | solution.py:186
  68.7 1.6 %collective-permute-start.15 = (f32[2,2,4,32,128]{4,3,2,1,0:T(8,128)S(1)}, f32[2,2,4,32,128]{4,3,2,1,0:T(8,128)S(1)}, u32[]{:S(2)}, u32[]{:S(2)}) collective-permute-start(f32[2,2,4,32,128]{4,3,2,1,0:T(8,128)S(1)} %dynamic-slice_bitcast_fusion), channel_id=1, source_target_pairs={{0,4},{2,6},{4,0},{6,2},{8,12},{10,14},{12,8},{14,10},{1,5},{3,7},... | collective-permute-start | bytes 786440 | tf_op jit(solution)/shard_map/ppermute | solution.py:186
  71.0 3.2 %fusion.92 = f32[32,64,128]{2,1,0:T(8,128)} fusion(f32[40,64,128]{2,1,0:T(8,128)S(1)} %constant_dynamic-update-slice_fusion.1, s32[32,64,128]{2,1,0:T(8,128)S(1)} %copy-done.1), kind=kLoop, calls=%fused_computation.240 | loop fusion | flops 9175040 | bytes 12845056 | tf_op jit(solution)/shard_map/mul | solution.py:243
  74.4 4.5 %collective-permute-done.15 = f32[2,2,4,32,128]{4,3,2,1,0:T(8,128)S(1)} collective-permute-done((f32[2,2,4,32,128]{4,3,2,1,0:T(8,128)S(1)}, f32[2,2,4,32,128]{4,3,2,1,0:T(8,128)S(1)}, u32[]{:S(2)}, u32[]{:S(2)}) %collective-permute-start.15) | collective-permute-done | bytes 262176 | tf_op jit(solution)/shard_map/ppermute | solution.py:186
  79.6 2.7 %collective-permute-start.21 = (f32[1,1,4,64,128]{4,3,2,1,0:T(8,128)S(1)}, f32[1,1,4,64,128]{4,3,2,1,0:T(8,128)S(1)}, u32[]{:S(2)}, u32[]{:S(2)}) collective-permute-start(f32[1,1,4,64,128]{4,3,2,1,0:T(8,128)S(1)} %dynamic-slice_bitcast_fusion.5), channel_id=1, source_target_pairs={{0,8},{2,10},{4,12},{6,14},{8,0},{10,2},{12,4},{14,6},{1,9},{3,11}... | collective-permute-start | bytes 393224 | tf_op jit(solution)/shard_map/ppermute | solution.py:186
  84.1 5.0 %collective-permute-done.19 = f32[2,1,4,32,128]{4,3,2,0,1:T(8,128)S(1)} collective-permute-done((f32[2,1,4,32,128]{4,3,2,0,1:T(8,128)S(1)}, f32[2,1,4,32,128]{4,3,2,0,1:T(8,128)S(1)}, u32[]{:S(2)}, u32[]{:S(2)}) %collective-permute-start.19) | collective-permute-done | bytes 131104 | tf_op jit(solution)/shard_map/ppermute | solution.py:186
  89.4 7.2 %collective-permute-done.22 = f32[1,1,4,64,128]{4,3,2,1,0:T(8,128)S(1)} collective-permute-done((f32[1,1,4,64,128]{4,3,2,1,0:T(8,128)S(1)}, f32[1,1,4,64,128]{4,3,2,1,0:T(8,128)S(1)}, u32[]{:S(2)}, u32[]{:S(2)}) %collective-permute-start.22) | collective-permute-done | bytes 131104 | tf_op jit(solution)/shard_map/ppermute | solution.py:186
  98.4 7.0 %collective-permute-done.23 = f32[1,4,64,128]{3,2,1,0:T(8,128)S(1)} collective-permute-done((f32[1,4,64,128]{3,2,1,0:T(8,128)S(1)}, f32[1,4,64,128]{3,2,1,0:T(8,128)S(1)}, u32[]{:S(2)}, u32[]{:S(2)}) %collective-permute-start.23) | collective-permute-done | bytes 131104 | tf_op jit(solution)/shard_map/ppermute | solution.py:120
  106.6 4.0 %collective-permute-done.25 = f32[2,4,32,128]{3,2,1,0:T(8,128)S(1)} collective-permute-done((f32[2,4,32,128]{3,2,1,0:T(8,128)S(1)}, f32[2,4,32,128]{3,2,1,0:T(8,128)S(1)}, u32[]{:S(2)}, u32[]{:S(2)}) %collective-permute-start.25) | collective-permute-done | bytes 131104 | tf_op jit(solution)/shard_map/ppermute | solution.py:120
  111.1 2.2 %collective-permute-start.26 = (f32[4,4,32,128]{3,2,1,0:T(8,128)S(1)}, f32[4,4,32,128]{3,2,1,0:T(8,128)S(1)}, u32[]{:S(2)}, u32[]{:S(2)}) collective-permute-start(f32[4,4,32,128]{3,2,1,0:T(8,128)S(1)} %bitcast.242), channel_id=1, source_target_pairs={{0,2},{2,0},{4,6},{6,4},{8,10},{10,8},{12,14},{14,12},{1,3},{3,1},... | collective-permute-start | bytes 786440 | tf_op jit(solution)/shard_map/ppermute | solution.py:120
  114.5 3.5 %collective-permute-done.26 = f32[4,4,32,128]{3,2,1,0:T(8,128)S(1)} collective-permute-done((f32[4,4,32,128]{3,2,1,0:T(8,128)S(1)}, f32[4,4,32,128]{3,2,1,0:T(8,128)S(1)}, u32[]{:S(2)}, u32[]{:S(2)}) %collective-permute-start.26) | collective-permute-done | bytes 262176 | tf_op jit(solution)/shard_map/ppermute | solution.py:120
  118.2 1.1 copy-done.4
  122.6 2.9 %fusion.120 = f32[32,64,128]{2,1,0:T(8,128)S(1)} fusion(f32[40,64,128]{2,1,0:T(8,128)S(1)} %constant_dynamic-update-slice_fusion, f32[32,64,128]{2,1,0:T(8,128)S(1)} %copy-done.7, f32[128]{0:T(128)S(1)} %copy-done.18, f32[32,64]{1,0:T(8,128)S(1)} %broadcast_add_fusion, f32[8,4,64,128]{3,2,1,0:T(8,128)S(1)} %pad_maximum_fusion.13, ...), kind=kLoop, calls=%fused_computation.268 | loop fusion | flops 11534336 | bytes 16007680 | tf_op jit(solution)/shard_map/add | solution.py:251
  (201 shorter events, 36.2 us)
Async XLA Ops:
  0.6 15.7 %copy-start = (f32[1,32,64,128]{3,2,1,0:T(8,128)S(1)}, f32[1,32,64,128]{3,2,1,0:T(8,128)}, u32[]{:S(2)}) copy-start(f32[1,32,64,128]{3,2,1,0:T(8,128)} %param.12) | copy-start | bytes 3145732
  0.7 15.1 %copy-start.20 = (f32[1,4]{1,0:T(1,128)S(1)}, f32[1,4]{1,0:T(1,128)}, u32[]{:S(2)}) copy-start(f32[1,4]{1,0:T(1,128)} %param.16) | copy-start | bytes 52
  2.3 22.5 %collective-permute-start.2 = (f32[4,64,128]{2,1,0:T(8,128)}, f32[4,64,128]{2,1,0:T(8,128)}, u32[]{:S(2)}, u32[]{:S(2)}) collective-permute-start(f32[4,64,128]{2,1,0:T(8,128)} %dynamic-slice_bitcast_fusion.10), channel_id=1, source_target_pairs={{0,1},{1,0},{2,3},{3,2},{4,5},{5,4},{6,7},{7,6},{8,9},{9,8},{10,11... | collective-permute-start | bytes 393224 | tf_op jit(solution)/shard_map/ppermute | solution.py:52
  4.6 23.6 %collective-permute-start = (f32[1,16,2048]{2,1,0:T(8,128)}, f32[1,16,2048]{2,1,0:T(8,128)}, u32[]{:S(2)}, u32[]{:S(2)}) collective-permute-start(f32[1,16,2048]{2,1,0:T(8,128)} %concatenate.199), channel_id=1, source_target_pairs={{0,8},{2,10},{4,12},{6,14},{8,0},{10,2},{12,4},{14,6},{1,9},{3,11}... | collective-permute-start | bytes 393224 | tf_op jit(solution)/shard_map/ppermute | solution.py:120
  8.2 15.8 %collective-permute-start.1 = (f32[1,16,64]{2,1,0:T(8,128)}, f32[1,16,64]{2,1,0:T(8,128)}, u32[]{:S(2)}, u32[]{:S(2)}) collective-permute-start(f32[1,16,64]{2,1,0:T(8,128)} %bitcast.262), channel_id=1, source_target_pairs={{0,8},{2,10},{4,12},{6,14},{8,0},{10,2},{12,4},{14,6},{1,9},{3,11}... | collective-permute-start | bytes 12296 | tf_op jit(solution)/shard_map/ppermute | solution.py:120
  29.5 4.2 %collective-permute-start.5 = (f32[2,16,64]{2,1,0:T(8,128)S(1)}, f32[2,16,64]{2,1,0:T(8,128)S(1)}, u32[]{:S(2)}, u32[]{:S(2)}) collective-permute-start(f32[2,16,64]{2,1,0:T(8,128)S(1)} %maximum_select_fusion.12), channel_id=1, source_target_pairs={{0,4},{2,6},{4,0},{6,2},{8,12},{10,14},{12,8},{14,10},{1,5},{3,7},... | collective-permute-start | bytes 24584 | tf_op jit(solution)/shard_map/ppermute | solution.py:120
  31.5 5.1 %collective-permute-start.4 = (f32[2,8,2048]{2,1,0:T(8,128)S(1)}, f32[2,8,2048]{2,1,0:T(8,128)S(1)}, u32[]{:S(2)}, u32[]{:S(2)}) collective-permute-start(f32[2,8,2048]{2,1,0:T(8,128)S(1)} %get-tuple-element.156), channel_id=1, source_target_pairs={{0,2},{2,0},{4,6},{6,4},{8,10},{10,8},{12,14},{14,12},{1,3},{3,1},... | collective-permute-start | bytes 393224 | tf_op jit(solution)/shard_map/ppermute | solution.py:120
  33.1 6.0 %collective-permute-start.6 = (f32[4,64,128]{2,1,0:T(8,128)S(1)}, f32[4,64,128]{2,1,0:T(8,128)S(1)}, u32[]{:S(2)}, u32[]{:S(2)}) collective-permute-start(f32[4,64,128]{2,1,0:T(8,128)S(1)} %constant_dynamic-slice_fusion.7), channel_id=1, source_target_pairs={{0,1},{1,0},{2,3},{3,2},{4,5},{5,4},{6,7},{7,6},{8,9},{9,8},{10,11... | collective-permute-start | bytes 393224 | tf_op jit(solution)/shard_map/ppermute | solution.py:52
  33.1 5.9 %collective-permute-start.3 = (f32[2,8,2048]{2,1,0:T(8,128)S(1)}, f32[2,8,2048]{2,1,0:T(8,128)S(1)}, u32[]{:S(2)}, u32[]{:S(2)}) collective-permute-start(f32[2,8,2048]{2,1,0:T(8,128)S(1)} %get-tuple-element.157), channel_id=1, source_target_pairs={{0,4},{2,6},{4,0},{6,2},{8,12},{10,14},{12,8},{14,10},{1,5},{3,7},... | collective-permute-start | bytes 393224 | tf_op jit(solution)/shard_map/ppermute | solution.py:120
  43.6 5.0 %collective-permute-start.10 = (f32[4,64,128]{2,1,0:T(8,128)S(1)}, f32[4,64,128]{2,1,0:T(8,128)S(1)}, u32[]{:S(2)}, u32[]{:S(2)}) collective-permute-start(f32[4,64,128]{2,1,0:T(8,128)S(1)} %constant_dynamic-slice_fusion.6), channel_id=1, source_target_pairs={{0,1},{1,0},{2,3},{3,2},{4,5},{5,4},{6,7},{7,6},{8,9},{9,8},{10,11... | collective-permute-start | bytes 393224 | tf_op jit(solution)/shard_map/ppermute | solution.py:52
  43.6 4.3 %collective-permute-start.9 = (f32[4,16,64]{2,1,0:T(8,128)S(1)}, f32[4,16,64]{2,1,0:T(8,128)S(1)}, u32[]{:S(2)}, u32[]{:S(2)}) collective-permute-start(f32[4,16,64]{2,1,0:T(8,128)S(1)} %bitcast.255), channel_id=1, source_target_pairs={{0,2},{2,0},{4,6},{6,4},{8,10},{10,8},{12,14},{14,12},{1,3},{3,1},... | collective-permute-start | bytes 49160 | tf_op jit(solution)/shard_map/ppermute | solution.py:120
  44.2 8.4 %collective-permute-start.8 = (f32[4,8,2048]{2,1,0:T(8,128)S(1)}, f32[4,8,2048]{2,1,0:T(8,128)S(1)}, u32[]{:S(2)}, u32[]{:S(2)}) collective-permute-start(f32[4,8,2048]{2,1,0:T(8,128)S(1)} %bitcast.232), channel_id=1, source_target_pairs={{0,4},{2,6},{4,0},{6,2},{8,12},{10,14},{12,8},{14,10},{1,5},{3,7},... | collective-permute-start | bytes 786440 | tf_op jit(solution)/shard_map/ppermute | solution.py:120
  44.5 8.6 %collective-permute-start.7 = (f32[4,8,2048]{2,1,0:T(8,128)S(1)}, f32[4,8,2048]{2,1,0:T(8,128)S(1)}, u32[]{:S(2)}, u32[]{:S(2)}) collective-permute-start(f32[4,8,2048]{2,1,0:T(8,128)S(1)} %bitcast.234), channel_id=1, source_target_pairs={{0,2},{2,0},{4,6},{6,4},{8,10},{10,8},{12,14},{14,12},{1,3},{3,1},... | collective-permute-start | bytes 786440 | tf_op jit(solution)/shard_map/ppermute | solution.py:120
  56.0 3.7 %collective-permute-start.13 = (f32[4,64,128]{2,1,0:T(8,128)S(1)}, f32[4,64,128]{2,1,0:T(8,128)S(1)}, u32[]{:S(2)}, u32[]{:S(2)}) collective-permute-start(f32[4,64,128]{2,1,0:T(8,128)S(1)} %constant_dynamic-slice_fusion.3), channel_id=1, source_target_pairs={{0,1},{1,0},{2,3},{3,2},{4,5},{5,4},{6,7},{7,6},{8,9},{9,8},{10,11... | collective-permute-start | bytes 393224 | tf_op jit(solution)/shard_map/ppermute | solution.py:52
  56.7 8.0 %collective-permute-start.12 = (f32[4,4,32,128]{3,2,1,0:T(8,128)S(1)}, f32[4,4,32,128]{3,2,1,0:T(8,128)S(1)}, u32[]{:S(2)}, u32[]{:S(2)}) collective-permute-start(f32[4,4,32,128]{3,2,1,0:T(8,128)S(1)} %bitcast.244), channel_id=1, source_target_pairs={{0,4},{2,6},{4,0},{6,2},{8,12},{10,14},{12,8},{14,10},{1,5},{3,7},... | collective-permute-start | bytes 786440 | tf_op jit(solution)/shard_map/ppermute | solution.py:160
  58.0 7.8 %collective-permute-start.11 = (f32[4,4,32,128]{3,2,1,0:T(8,128)S(1)}, f32[4,4,32,128]{3,2,1,0:T(8,128)S(1)}, u32[]{:S(2)}, u32[]{:S(2)}) collective-permute-start(f32[4,4,32,128]{3,2,1,0:T(8,128)S(1)} %copy-done.12), channel_id=1, source_target_pairs={{0,2},{2,0},{4,6},{6,4},{8,10},{10,8},{12,14},{14,12},{1,3},{3,1},... | collective-permute-start | bytes 786440 | tf_op jit(solution)/shard_map/ppermute | solution.py:160
  65.9 5.1 %collective-permute-start.18 = (f32[4,64,128]{2,1,0:T(8,128)S(1)}, f32[4,64,128]{2,1,0:T(8,128)S(1)}, u32[]{:S(2)}, u32[]{:S(2)}) collective-permute-start(f32[4,64,128]{2,1,0:T(8,128)S(1)} %constant_dynamic-slice_fusion.2), channel_id=1, source_target_pairs={{0,1},{1,0},{2,3},{3,2},{4,5},{5,4},{6,7},{7,6},{8,9},{9,8},{10,11... | collective-permute-start | bytes 393224 | tf_op jit(solution)/shard_map/ppermute | solution.py:52
  66.0 8.3 %collective-permute-start.17 = (f32[2,1,4,32,128]{4,3,2,0,1:T(8,128)S(1)}, f32[2,1,4,32,128]{4,3,2,0,1:T(8,128)S(1)}, u32[]{:S(2)}, u32[]{:S(2)}) collective-permute-start(f32[2,1,4,32,128]{4,3,2,0,1:T(8,128)S(1)} %dynamic-slice_bitcast_fusion.8), channel_id=1, source_target_pairs={{0,2},{2,0},{4,6},{6,4},{8,10},{10,8},{12,14},{14,12},{1,3},{3,1},... | collective-permute-start | bytes 393224 | tf_op jit(solution)/shard_map/ppermute | solution.py:186
  67.6 6.7 %collective-permute-start.16 = (f32[2,1,4,32,128]{4,3,2,0,1:T(8,128)S(1)}, f32[2,1,4,32,128]{4,3,2,0,1:T(8,128)S(1)}, u32[]{:S(2)}, u32[]{:S(2)}) collective-permute-start(f32[2,1,4,32,128]{4,3,2,0,1:T(8,128)S(1)} %dynamic-slice_bitcast_fusion.9), channel_id=1, source_target_pairs={{0,4},{2,6},{4,0},{6,2},{8,12},{10,14},{12,8},{14,10},{1,5},{3,7},... | collective-permute-start | bytes 393224 | tf_op jit(solution)/shard_map/ppermute | solution.py:186
  68.7 10.2 %collective-permute-start.15 = (f32[2,2,4,32,128]{4,3,2,1,0:T(8,128)S(1)}, f32[2,2,4,32,128]{4,3,2,1,0:T(8,128)S(1)}, u32[]{:S(2)}, u32[]{:S(2)}) collective-permute-start(f32[2,2,4,32,128]{4,3,2,1,0:T(8,128)S(1)} %dynamic-slice_bitcast_fusion), channel_id=1, source_target_pairs={{0,4},{2,6},{4,0},{6,2},{8,12},{10,14},{12,8},{14,10},{1,5},{3,7},... | collective-permute-start | bytes 786440 | tf_op jit(solution)/shard_map/ppermute | solution.py:186
  70.3 8.6 %collective-permute-start.14 = (f32[4,1,4,32,128]{4,3,2,0,1:T(8,128)S(1)}, f32[4,1,4,32,128]{4,3,2,0,1:T(8,128)S(1)}, u32[]{:S(2)}, u32[]{:S(2)}) collective-permute-start(f32[4,1,4,32,128]{4,3,2,0,1:T(8,128)S(1)} %dynamic-slice_bitcast_fusion.1), channel_id=1, source_target_pairs={{0,2},{2,0},{4,6},{6,4},{8,10},{10,8},{12,14},{14,12},{1,3},{3,1},... | collective-permute-start | bytes 786440 | tf_op jit(solution)/shard_map/ppermute | solution.py:186
  79.0 5.0 %collective-permute-start.20 = (f32[2,1,4,32,128]{4,3,2,0,1:T(8,128)S(1)}, f32[2,1,4,32,128]{4,3,2,0,1:T(8,128)S(1)}, u32[]{:S(2)}, u32[]{:S(2)}) collective-permute-start(f32[2,1,4,32,128]{4,3,2,0,1:T(8,128)S(1)} %dynamic-slice_bitcast_fusion.6), channel_id=1, source_target_pairs={{0,2},{2,0},{4,6},{6,4},{8,10},{10,8},{12,14},{14,12},{1,3},{3,1},... | collective-permute-start | bytes 393224 | tf_op jit(solution)/shard_map/ppermute | solution.py:186
  79.6 9.5 %collective-permute-start.21 = (f32[1,1,4,64,128]{4,3,2,1,0:T(8,128)S(1)}, f32[1,1,4,64,128]{4,3,2,1,0:T(8,128)S(1)}, u32[]{:S(2)}, u32[]{:S(2)}) collective-permute-start(f32[1,1,4,64,128]{4,3,2,1,0:T(8,128)S(1)} %dynamic-slice_bitcast_fusion.5), channel_id=1, source_target_pairs={{0,8},{2,10},{4,12},{6,14},{8,0},{10,2},{12,4},{14,6},{1,9},{3,11}... | collective-permute-start | bytes 393224 | tf_op jit(solution)/shard_map/ppermute | solution.py:186
  82.3 6.8 %collective-permute-start.19 = (f32[2,1,4,32,128]{4,3,2,0,1:T(8,128)S(1)}, f32[2,1,4,32,128]{4,3,2,0,1:T(8,128)S(1)}, u32[]{:S(2)}, u32[]{:S(2)}) collective-permute-start(f32[2,1,4,32,128]{4,3,2,0,1:T(8,128)S(1)} %dynamic-slice_bitcast_fusion.7), channel_id=1, source_target_pairs={{0,4},{2,6},{4,0},{6,2},{8,12},{10,14},{12,8},{14,10},{1,5},{3,7},... | collective-permute-start | bytes 393224 | tf_op jit(solution)/shard_map/ppermute | solution.py:186
  89.2 7.3 %collective-permute-start.22 = (f32[1,1,4,64,128]{4,3,2,1,0:T(8,128)S(1)}, f32[1,1,4,64,128]{4,3,2,1,0:T(8,128)S(1)}, u32[]{:S(2)}, u32[]{:S(2)}) collective-permute-start(f32[1,1,4,64,128]{4,3,2,1,0:T(8,128)S(1)} %dynamic-slice_bitcast_fusion.4), channel_id=1, source_target_pairs={{0,8},{2,10},{4,12},{6,14},{8,0},{10,2},{12,4},{14,6},{1,9},{3,11}... | collective-permute-start | bytes 393224 | tf_op jit(solution)/shard_map/ppermute | solution.py:186
  98.3 7.2 %collective-permute-start.23 = (f32[1,4,64,128]{3,2,1,0:T(8,128)S(1)}, f32[1,4,64,128]{3,2,1,0:T(8,128)S(1)}, u32[]{:S(2)}, u32[]{:S(2)}) collective-permute-start(f32[1,4,64,128]{3,2,1,0:T(8,128)S(1)} %fusion.1), channel_id=1, source_target_pairs={{0,8},{2,10},{4,12},{6,14},{8,0},{10,2},{12,4},{14,6},{1,9},{3,11}... | collective-permute-start | bytes 393224 | tf_op jit(solution)/shard_map/ppermute | solution.py:120
  105.5 5.0 %collective-permute-start.25 = (f32[2,4,32,128]{3,2,1,0:T(8,128)S(1)}, f32[2,4,32,128]{3,2,1,0:T(8,128)S(1)}, u32[]{:S(2)}, u32[]{:S(2)}) collective-permute-start(f32[2,4,32,128]{3,2,1,0:T(8,128)S(1)} %get-tuple-element.152), channel_id=1, source_target_pairs={{0,2},{2,0},{4,6},{6,4},{8,10},{10,8},{12,14},{14,12},{1,3},{3,1},... | collective-permute-start | bytes 393224 | tf_op jit(solution)/shard_map/ppermute | solution.py:120
  106.0 5.0 %collective-permute-start.24 = (f32[2,4,32,128]{3,2,1,0:T(8,128)S(1)}, f32[2,4,32,128]{3,2,1,0:T(8,128)S(1)}, u32[]{:S(2)}, u32[]{:S(2)}) collective-permute-start(f32[2,4,32,128]{3,2,1,0:T(8,128)S(1)} %get-tuple-element.153), channel_id=1, source_target_pairs={{0,4},{2,6},{4,0},{6,2},{8,12},{10,14},{12,8},{14,10},{1,5},{3,7},... | collective-permute-start | bytes 393224 | tf_op jit(solution)/shard_map/ppermute | solution.py:120
  111.0 7.1 %collective-permute-start.27 = (f32[4,4,32,128]{3,2,1,0:T(8,128)S(1)}, f32[4,4,32,128]{3,2,1,0:T(8,128)S(1)}, u32[]{:S(2)}, u32[]{:S(2)}) collective-permute-start(f32[4,4,32,128]{3,2,1,0:T(8,128)S(1)} %bitcast.236), channel_id=1, source_target_pairs={{0,4},{2,6},{4,0},{6,2},{8,12},{10,14},{12,8},{14,10},{1,5},{3,7},... | collective-permute-start | bytes 786440 | tf_op jit(solution)/shard_map/ppermute | solution.py:120
  111.1 6.9 %collective-permute-start.26 = (f32[4,4,32,128]{3,2,1,0:T(8,128)S(1)}, f32[4,4,32,128]{3,2,1,0:T(8,128)S(1)}, u32[]{:S(2)}, u32[]{:S(2)}) collective-permute-start(f32[4,4,32,128]{3,2,1,0:T(8,128)S(1)} %bitcast.242), channel_id=1, source_target_pairs={{0,2},{2,0},{4,6},{6,4},{8,10},{10,8},{12,14},{14,12},{1,3},{3,1},... | collective-permute-start | bytes 786440 | tf_op jit(solution)/shard_map/ppermute | solution.py:120
  120.2 1.6 %collective-permute-start.28 = (f32[4,64,128]{2,1,0:T(8,128)}, f32[4,64,128]{2,1,0:T(8,128)S(1)}, u32[]{:S(2)}, u32[]{:S(2)}) collective-permute-start(f32[4,64,128]{2,1,0:T(8,128)} %constant_dynamic-slice_fusion), channel_id=1, source_target_pairs={{0,1},{1,0},{2,3},{3,2},{4,5},{5,4},{6,7},{7,6},{8,9},{9,8},{10,11... | collective-permute-start | bytes 393224 | tf_op jit(solution)/shard_map/ppermute | solution.py:52
  126.9 1.9 %collective-permute-start.29 = (f32[1,2,256]{2,1,0:T(2,128)S(1)}, f32[1,2,256]{2,1,0:T(2,128)S(1)}, u32[]{:S(2)}, u32[]{:S(2)}) collective-permute-start(f32[1,2,256]{2,1,0:T(2,128)S(1)} %maximum_bitcast_fusion), channel_id=1, source_target_pairs={{0,1},{1,0},{2,3},{3,2},{4,5},{5,4},{6,7},{7,6},{8,9},{9,8},{10,11... | collective-permute-start | bytes 6152 | tf_op jit(solution)/shard_map/ppermute | solution.py:389
  (24 other events, 78.0 us)

commit v16 on v15

--- a/solution.py
+++ b/solution.py
@@ -306,16 +306,15 @@
             st[name + "_keep"], st[name + "_send"] = split_step(piece, order[0], list(near_first))
 
     tasks = [task_wave(0), light_prep, wave_and_split]
-    run_group([model_c, gains_c], tasks[0])
+    run_group([model_c], tasks[0])
     half_a, half_b = halves(model_c["held"], 1)
     model_a = chain(half_a, "ag", far_first[1:], [top])
     model_b = chain(half_b, "ag", swap_first(far_first[1:]), [top])
     for i in range(1, len(bits)):
-        run_group([model_a, model_b, gains_c], tasks[i] if i < len(tasks) else nothing)
+        run_group([model_a, model_b], tasks[i] if i < len(tasks) else nothing)
     for i in range(len(bits), len(tasks)):
         tasks[i]()
     model_held = jnp.concatenate([model_a["held"], model_b["held"]], axis=1)
-    gains_held = gains_c["held"]
     light_a = chain(None, "pre", light_orders["la"], near_first)
     light_b = chain(None, "pre", light_orders["lb"], near_first)
     light_a["slices"] = lambda: (st["la_keep"], st["la_send"])
@@ -336,7 +335,7 @@
     tasks = [task_wave(3)]
     light_c = None
     for i in range(len(bits) - 1):
-        group = [image_a, image_b]
+        group = [image_a, image_b, gains_c]
         if light_a["i"] < len(light_a["order"]):
             group += [light_a, light_b]
         elif light_c is None:
@@ -354,7 +353,10 @@
     last = chain(
         jnp.concatenate([image_a["held"], image_b["held"]], axis=2), "rs", near_first[-1:], near_first[-1:]
     )
-    run_group([last, light_c], nothing)
+    run_group([last, light_c, gains_c], nothing)
+    while gains_c["i"] < len(gains_c["order"]):
+        run_group([gains_c], nothing)
+    gains_held = gains_c["held"]
     image_part = last["held"][0]
     light_part = light_c["held"][0]
 

time: 130 us -> 131 us (level)
    ppermute x13, waiting for transfers between devices: 20.8 us -> 27.1 us  [ag_step(): theirs = lax.ppermute(held, 'shot', [(i, i ^ k) for i in range(n)])]
    ppermute x8, waiting for transfers between devices: 17.6 us -> 11.3 us  [rs_step(): got = lax.ppermute(send, 'shot', [(i, i ^ k) for i in range(n)])]
    ppermute x2, starting transfers between devices: 2.79 us -> 0.9 us  [chain_step(): return keep + lax.ppermute(send, 'shot', [(i, i ^ k) for i in range(n)])]
  transfers between devices with their start and end apart: 30 -> 30, of which waited for: 15 -> 16; matrix products, arithmetic and copies ran while one was open for 28% -> 27% of each run, Pallas kernels for 0% -> 0%
where the time goes in v16:
time: 131 us; the launch traced here: 130 us
  waiting for transfers between devices  43.1 us (33%)
  other arithmetic  35.4 us (27%)
  starting transfers between devices  25.3 us (19%)
  local copies, waits for them, and re-layouts  20 us (15%)
  between operations  4.68 us (4%)
  matrix products  1.72 us (1%)
    ppermute x13, waiting for transfers between devices, ag_step(): theirs = lax.ppermute(held, 'shot', [(i, i ^ k) for i in range(n)])  27.1 us
    ppermute x13, starting transfers between devices, ag_step(): theirs = lax.ppermute(held, 'shot', [(i, i ^ k) for i in range(n)])  13.5 us
    ppermute x8, waiting for transfers between devices, rs_step(): got = lax.ppermute(send, 'shot', [(i, i ^ k) for i in range(n)])  11.3 us
    ppermute x8, starting transfers between devices, rs_step(): got = lax.ppermute(send, 'shot', [(i, i ^ k) for i in range(n)])  9.42 us
    add x3, other arithmetic, inject(): return field + jnp.where(hit, source_gain[0] * wavelet[0, moment], 0.0)  8.05 us
    add x2, other arithmetic, born_second(): 2.0 * born + speed_term * laplace_x(with_halo(born)) - absorber * born  5.83 us
    unnamed x55, local copies, waits for them, and re-layouts  5.27 us
    ppermute x2, waiting for transfers between devices, chain_step(): return keep + lax.ppermute(send, 'shot', [(i, i ^ k) for i in range(n)])  4.11 us
  transfers between devices with their start and end apart: 30, of which 16 were waited for; matrix products, arithmetic and copies ran while one was open for 27% of the time, Pallas kernels for 0%

profile of v16, /device:TPU:0, one launch (start us, length us, event | category | flops | bytes accessed | tf_op | source)
XLA Modules:
  0.0 130.2 jit_solution(14335011941744187224)
XLA Ops:
  0.7 1.7 %dynamic-slice_bitcast_fusion.10 = f32[4,64,128]{2,1,0:T(8,128)} fusion(f32[1,32,64,128]{3,2,1,0:T(8,128)} %param.12, s32[]{:T(128)S(6)} %select_n.402), kind=kLoop, calls=%fused_computation.441 | loop fusion | bytes 262148 | tf_op jit(solution)/shard_map/dynamic_slice | solution.py:51
  4.6 3.6 %collective-permute-start = (f32[1,16,2048]{2,1,0:T(8,128)}, f32[1,16,2048]{2,1,0:T(8,128)}, u32[]{:S(2)}, u32[]{:S(2)}) collective-permute-start(f32[1,16,2048]{2,1,0:T(8,128)} %concatenate.199), channel_id=1, source_target_pairs={{0,8},{2,10},{4,12},{6,14},{8,0},{10,2},{12,4},{14,6},{1,9},{3,11}... | collective-permute-start | bytes 393224 | tf_op jit(solution)/shard_map/ppermute | solution.py:120
  10.2 3.7 %pad_maximum_fusion.15 = (f32[3]{0:T(128)S(1)}, f32[3]{0:T(128)S(1)}) fusion(f32[1]{0:T(128)} %get-tuple-element.167, f32[1]{0:T(128)} %get-tuple-element.168, f32[1]{0:T(128)} %get-tuple-element.163, f32[1]{0:T(128)} %get-tuple-element.164, f32[1]{0:T(128)} %get-tuple-element.165, f32[1]{0:T(128)} %get-tuple-element.166), kind=kLoop, calls=%fused_computation.500 | loop fusion | flops 12 | bytes 48 | tf_op jit(solution)/shard_map/stack | solution.py:37
  16.3 2.6 %fusion.144 = f32[24,64,128]{2,1,0:T(8,128)} fusion(f32[32,64,128]{2,1,0:T(8,128)S(1)} %bitcast.205, f32[1,32,64,128]{3,2,1,0:T(8,128)S(1)} %copy-done), kind=kLoop, calls=%fused_computation.324 | loop fusion | flops 5701632 | bytes 8912896 | tf_op jit(solution)/shard_map/add | solution.py:86
  24.0 1.4 %maximum_select_fusion.12 = f32[2,16,64]{2,1,0:T(8,128)} fusion(f32[1,16,64]{2,1,0:T(8,128)} %collective-permute-done.13, f32[1,16,64]{2,1,0:T(8,128)} %bitcast.263, pred[]{:T(512)S(6)} %eq.97), kind=kLoop, calls=%fused_computation.458 | loop fusion | flops 6144 | bytes 16385 | tf_op jit(solution)/shard_map/jit(_where)/select_n | solution.py:125
  30.2 1.7 %collective-permute-start.3 = (f32[2,8,2048]{2,1,0:T(8,128)S(1)}, f32[2,8,2048]{2,1,0:T(8,128)S(1)}, u32[]{:S(2)}, u32[]{:S(2)}) collective-permute-start(f32[2,8,2048]{2,1,0:T(8,128)S(1)} %get-tuple-element.156), channel_id=1, source_target_pairs={{0,2},{2,0},{4,6},{6,4},{8,10},{10,8},{12,14},{14,12},{1,3},{3,1},... | collective-permute-start | bytes 393224 | tf_op jit(solution)/shard_map/ppermute | solution.py:120
  31.9 1.6 %collective-permute-start.2 = (f32[2,8,2048]{2,1,0:T(8,128)S(1)}, f32[2,8,2048]{2,1,0:T(8,128)S(1)}, u32[]{:S(2)}, u32[]{:S(2)}) collective-permute-start(f32[2,8,2048]{2,1,0:T(8,128)S(1)} %get-tuple-element.157), channel_id=1, source_target_pairs={{0,4},{2,6},{4,0},{6,2},{8,12},{10,14},{12,8},{14,10},{1,5},{3,7},... | collective-permute-start | bytes 393224 | tf_op jit(solution)/shard_map/ppermute | solution.py:120
  33.6 2.4 %collective-permute-done.3 = f32[2,8,2048]{2,1,0:T(8,128)S(1)} collective-permute-done((f32[2,8,2048]{2,1,0:T(8,128)S(1)}, f32[2,8,2048]{2,1,0:T(8,128)S(1)}, u32[]{:S(2)}, u32[]{:S(2)}) %collective-permute-start.3) | collective-permute-done | bytes 131104 | tf_op jit(solution)/shard_map/ppermute | solution.py:120
  36.1 1.4 %collective-permute-done.2 = f32[2,8,2048]{2,1,0:T(8,128)S(1)} collective-permute-done((f32[2,8,2048]{2,1,0:T(8,128)S(1)}, f32[2,8,2048]{2,1,0:T(8,128)S(1)}, u32[]{:S(2)}, u32[]{:S(2)}) %collective-permute-start.2) | collective-permute-done | bytes 131104 | tf_op jit(solution)/shard_map/ppermute | solution.py:120
  37.6 3.2 %fusion.3 = (f32[32,64,128]{2,1,0:T(8,128)S(1)}, f32[32,64,128]{2,1,0:T(8,128)S(1)}) fusion(f32[32,64,128]{2,1,0:T(8,128)S(1)} %get-tuple-element.71, f32[32,64,128]{2,1,0:T(8,128)S(1)} %bitcast.207, f32[]{:T(128)S(6)} %mul.394, f32[128]{0:T(128)S(1)} %copy-done.16, f32[32,64]{1,0:T(8,128)S(1)} %broadcast_add_fusion, pred[128]{0:T(512)(128)(4,1)S(1)} %copy-done.19, ...), kind=kLoop, calls=%fused_computation.151 | loop fusion | flops 12058624 | bytes 16012292 | tf_op jit(solution)/shard_map/add | solution.py:230
  42.1 1.6 %collective-permute-start.6 = (f32[4,8,2048]{2,1,0:T(8,128)S(1)}, f32[4,8,2048]{2,1,0:T(8,128)S(1)}, u32[]{:S(2)}, u32[]{:S(2)}) collective-permute-start(f32[4,8,2048]{2,1,0:T(8,128)S(1)} %bitcast.232), channel_id=1, source_target_pairs={{0,4},{2,6},{4,0},{6,2},{8,12},{10,14},{12,8},{14,10},{1,5},{3,7},... | collective-permute-start | bytes 786440 | tf_op jit(solution)/shard_map/ppermute | solution.py:120
  45.9 4.0 %fusion.4 = (f32[32,64,128]{2,1,0:T(8,128)}, f32[32,64,128]{2,1,0:T(8,128)}) fusion(f32[32,64,128]{2,1,0:T(8,128)S(1)} %get-tuple-element.69, f32[32,64,128]{2,1,0:T(8,128)S(1)} %get-tuple-element.71, f32[]{:T(128)S(6)} %mul.403, f32[128]{0:T(128)S(1)} %copy-done.16, f32[32,64]{1,0:T(8,128)S(1)} %broadcast_add_fusion, pred[128]{0:T(512)(128)(4,1)S(1)} %copy-done.19, ...), kind=kLoop, calls=%fused_computation.152 | loop fusion | flops 12058624 | bytes 16012292 | tf_op jit(solution)/shard_map/add | solution.py:230
  50.9 1.2 collective-permute-done.5
  53.3 1.5 %copy.47 = f32[2048,128]{1,0:T(8,128)S(1)} copy(f32[2048,128]{0,1:T(8,128)} %bitcast.216) | data formatting | bytes 2097152 | tf_op jit(solution)/shard_map/transpose | solution.py:324
  56.9 2.9 %fusion.67 = f32[32,64,128]{2,1,0:T(8,128)S(1)} fusion(f32[40,64,128]{2,1,0:T(8,128)S(1)} %constant_dynamic-update-slice_fusion.2, f32[32,64,128]{2,1,0:T(8,128)S(1)} %bitcast.211, f32[32,64,128]{2,1,0:T(8,128)S(1)} %copy-done.3, f32[32,64,128]{2,1,0:T(8,128)S(1)} %mul.404, f32[128]{0:T(128)S(1)} %copy-done.17, f32[32,64]{1,0:T(8,128)S(1)} %broadcast_add_fusion, ...), kind=kLoop, calls=%fused_computation.215 | loop fusion | flops 11272192 | bytes 16007680 | tf_op jit(solution)/shard_map/add | solution.py:251
  59.9 4.0 %collective-permute-done.9 = f32[4,4,32,128]{3,2,1,0:T(8,128)S(1)} collective-permute-done((f32[4,4,32,128]{3,2,1,0:T(8,128)S(1)}, f32[4,4,32,128]{3,2,1,0:T(8,128)S(1)}, u32[]{:S(2)}, u32[]{:S(2)}) %collective-permute-start.9) | collective-permute-done | bytes 262176 | tf_op jit(solution)/shard_map/ppermute | solution.py:160
  64.7 1.7 %collective-permute-start.14 = (f32[2,1,4,32,128]{4,3,2,0,1:T(8,128)S(1)}, f32[2,1,4,32,128]{4,3,2,0,1:T(8,128)S(1)}, u32[]{:S(2)}, u32[]{:S(2)}) collective-permute-start(f32[2,1,4,32,128]{4,3,2,0,1:T(8,128)S(1)} %dynamic-slice_bitcast_fusion.9), channel_id=1, source_target_pairs={{0,4},{2,6},{4,0},{6,2},{8,12},{10,14},{12,8},{14,10},{1,5},{3,7},... | collective-permute-start | bytes 393224 | tf_op jit(solution)/shard_map/ppermute | solution.py:186
  67.5 1.6 %collective-permute-start.11 = (f32[4,1,4,32,128]{4,3,2,0,1:T(8,128)S(1)}, f32[4,1,4,32,128]{4,3,2,0,1:T(8,128)S(1)}, u32[]{:S(2)}, u32[]{:S(2)}) collective-permute-start(f32[4,1,4,32,128]{4,3,2,0,1:T(8,128)S(1)} %dynamic-slice_bitcast_fusion.1), channel_id=1, source_target_pairs={{0,2},{2,0},{4,6},{6,4},{8,10},{10,8},{12,14},{14,12},{1,3},{3,1},... | collective-permute-start | bytes 786440 | tf_op jit(solution)/shard_map/ppermute | solution.py:186
  69.3 3.2 %fusion.92 = f32[32,64,128]{2,1,0:T(8,128)} fusion(f32[40,64,128]{2,1,0:T(8,128)S(1)} %constant_dynamic-update-slice_fusion.1, s32[32,64,128]{2,1,0:T(8,128)S(1)} %copy-done.1), kind=kLoop, calls=%fused_computation.240 | loop fusion | flops 9175040 | bytes 12845056 | tf_op jit(solution)/shard_map/mul | solution.py:243
  72.6 3.4 %collective-permute-done.12 = f32[2,2,4,32,128]{4,3,2,1,0:T(8,128)S(1)} collective-permute-done((f32[2,2,4,32,128]{4,3,2,1,0:T(8,128)S(1)}, f32[2,2,4,32,128]{4,3,2,1,0:T(8,128)S(1)}, u32[]{:S(2)}, u32[]{:S(2)}) %collective-permute-start.12) | collective-permute-done | bytes 262176 | tf_op jit(solution)/shard_map/ppermute | solution.py:186
  76.2 2.7 %collective-permute-start.20 = (f32[1,1,4,64,128]{4,3,2,1,0:T(8,128)S(1)}, f32[1,1,4,64,128]{4,3,2,1,0:T(8,128)S(1)}, u32[]{:S(2)}, u32[]{:S(2)}) collective-permute-start(f32[1,1,4,64,128]{4,3,2,1,0:T(8,128)S(1)} %dynamic-slice_bitcast_fusion.5), channel_id=1, source_target_pairs={{0,8},{2,10},{4,12},{6,14},{8,0},{10,2},{12,4},{14,6},{1,9},{3,11}... | collective-permute-start | bytes 393224 | tf_op jit(solution)/shard_map/ppermute | solution.py:186
  78.9 1.6 %collective-permute-start.19 = (f32[2,16,64]{2,1,0:T(8,128)S(1)}, f32[2,16,64]{2,1,0:T(8,128)S(1)}, u32[]{:S(2)}, u32[]{:S(2)}) collective-permute-start(f32[2,16,64]{2,1,0:T(8,128)S(1)} %copy-done.15), channel_id=1, source_target_pairs={{0,4},{2,6},{4,0},{6,2},{8,12},{10,14},{12,8},{14,10},{1,5},{3,7},... | collective-permute-start | bytes 24584 | tf_op jit(solution)/shard_map/ppermute | solution.py:120
  80.5 1.6 %collective-permute-start.18 = (f32[2,1,4,32,128]{4,3,2,0,1:T(8,128)S(1)}, f32[2,1,4,32,128]{4,3,2,0,1:T(8,128)S(1)}, u32[]{:S(2)}, u32[]{:S(2)}) collective-permute-start(f32[2,1,4,32,128]{4,3,2,0,1:T(8,128)S(1)} %dynamic-slice_bitcast_fusion.6), channel_id=1, source_target_pairs={{0,2},{2,0},{4,6},{6,4},{8,10},{10,8},{12,14},{14,12},{1,3},{3,1},... | collective-permute-start | bytes 393224 | tf_op jit(solution)/shard_map/ppermute | solution.py:186
  82.6 2.9 %collective-permute-done.18 = f32[2,1,4,32,128]{4,3,2,0,1:T(8,128)S(1)} collective-permute-done((f32[2,1,4,32,128]{4,3,2,0,1:T(8,128)S(1)}, f32[2,1,4,32,128]{4,3,2,0,1:T(8,128)S(1)}, u32[]{:S(2)}, u32[]{:S(2)}) %collective-permute-start.18) | collective-permute-done | bytes 131104 | tf_op jit(solution)/shard_map/ppermute | solution.py:186
  85.5 2.0 %collective-permute-done.17 = f32[2,1,4,32,128]{4,3,2,0,1:T(8,128)S(1)} collective-permute-done((f32[2,1,4,32,128]{4,3,2,0,1:T(8,128)S(1)}, f32[2,1,4,32,128]{4,3,2,0,1:T(8,128)S(1)}, u32[]{:S(2)}, u32[]{:S(2)}) %collective-permute-start.17) | collective-permute-done | bytes 131104 | tf_op jit(solution)/shard_map/ppermute | solution.py:186
  88.5 3.3 %collective-permute-done.22 = f32[4,16,64]{2,1,0:T(8,128)S(1)} collective-permute-done((f32[4,16,64]{2,1,0:T(8,128)S(1)}, f32[4,16,64]{2,1,0:T(8,128)S(1)}, u32[]{:S(2)}, u32[]{:S(2)}) %collective-permute-start.22) | collective-permute-done | bytes 16416 | tf_op jit(solution)/shard_map/ppermute | solution.py:120
  91.9 3.0 %collective-permute-done.21 = f32[1,1,4,64,128]{4,3,2,1,0:T(8,128)S(1)} collective-permute-done((f32[1,1,4,64,128]{4,3,2,1,0:T(8,128)S(1)}, f32[1,1,4,64,128]{4,3,2,1,0:T(8,128)S(1)}, u32[]{:S(2)}, u32[]{:S(2)}) %collective-permute-start.21) | collective-permute-done | bytes 131104 | tf_op jit(solution)/shard_map/ppermute | solution.py:186
  96.8 8.0 %collective-permute-done.23 = f32[1,4,64,128]{3,2,1,0:T(8,128)S(1)} collective-permute-done((f32[1,4,64,128]{3,2,1,0:T(8,128)S(1)}, f32[1,4,64,128]{3,2,1,0:T(8,128)S(1)}, u32[]{:S(2)}, u32[]{:S(2)}) %collective-permute-start.23) | collective-permute-done | bytes 131104 | tf_op jit(solution)/shard_map/ppermute | solution.py:120
  104.9 1.2 collective-permute-start.25
  106.7 3.5 %collective-permute-done.25 = f32[2,4,32,128]{3,2,1,0:T(8,128)S(1)} collective-permute-done((f32[2,4,32,128]{3,2,1,0:T(8,128)S(1)}, f32[2,4,32,128]{3,2,1,0:T(8,128)S(1)}, u32[]{:S(2)}, u32[]{:S(2)}) %collective-permute-start.25) | collective-permute-done | bytes 131104 | tf_op jit(solution)/shard_map/ppermute | solution.py:120
  113.5 5.3 %collective-permute-done.26 = f32[4,4,32,128]{3,2,1,0:T(8,128)S(1)} collective-permute-done((f32[4,4,32,128]{3,2,1,0:T(8,128)S(1)}, f32[4,4,32,128]{3,2,1,0:T(8,128)S(1)}, u32[]{:S(2)}, u32[]{:S(2)}) %collective-permute-start.26) | collective-permute-done | bytes 262176 | tf_op jit(solution)/shard_map/ppermute | solution.py:120
  123.4 2.9 %fusion.120 = f32[32,64,128]{2,1,0:T(8,128)S(1)} fusion(f32[40,64,128]{2,1,0:T(8,128)S(1)} %constant_dynamic-update-slice_fusion, f32[32,64,128]{2,1,0:T(8,128)S(1)} %copy-done.7, f32[128]{0:T(128)S(1)} %copy-done.18, f32[32,64]{1,0:T(8,128)S(1)} %broadcast_add_fusion, f32[8,4,64,128]{3,2,1,0:T(8,128)S(1)} %pad_maximum_fusion.13, ...), kind=kLoop, calls=%fused_computation.268 | loop fusion | flops 11534336 | bytes 16007680 | tf_op jit(solution)/shard_map/add | solution.py:251
  (201 shorter events, 39.1 us)
Async XLA Ops:
  0.6 15.6 %copy-start = (f32[1,32,64,128]{3,2,1,0:T(8,128)S(1)}, f32[1,32,64,128]{3,2,1,0:T(8,128)}, u32[]{:S(2)}) copy-start(f32[1,32,64,128]{3,2,1,0:T(8,128)} %param.12) | copy-start | bytes 3145732
  0.7 15.0 %copy-start.20 = (f32[1,4]{1,0:T(1,128)S(1)}, f32[1,4]{1,0:T(1,128)}, u32[]{:S(2)}) copy-start(f32[1,4]{1,0:T(1,128)} %param.16) | copy-start | bytes 52
  2.3 23.0 %collective-permute-start.1 = (f32[4,64,128]{2,1,0:T(8,128)}, f32[4,64,128]{2,1,0:T(8,128)}, u32[]{:S(2)}, u32[]{:S(2)}) collective-permute-start(f32[4,64,128]{2,1,0:T(8,128)} %dynamic-slice_bitcast_fusion.10), channel_id=1, source_target_pairs={{0,1},{1,0},{2,3},{3,2},{4,5},{5,4},{6,7},{7,6},{8,9},{9,8},{10,11... | collective-permute-start | bytes 393224 | tf_op jit(solution)/shard_map/ppermute | solution.py:52
  4.6 24.1 %collective-permute-start = (f32[1,16,2048]{2,1,0:T(8,128)}, f32[1,16,2048]{2,1,0:T(8,128)}, u32[]{:S(2)}, u32[]{:S(2)}) collective-permute-start(f32[1,16,2048]{2,1,0:T(8,128)} %concatenate.199), channel_id=1, source_target_pairs={{0,8},{2,10},{4,12},{6,14},{8,0},{10,2},{12,4},{14,6},{1,9},{3,11}... | collective-permute-start | bytes 393224 | tf_op jit(solution)/shard_map/ppermute | solution.py:120
  8.2 15.8 %collective-permute-start.13 = (f32[1,16,64]{2,1,0:T(8,128)}, f32[1,16,64]{2,1,0:T(8,128)}, u32[]{:S(2)}, u32[]{:S(2)}) collective-permute-start(f32[1,16,64]{2,1,0:T(8,128)} %bitcast.262), channel_id=1, source_target_pairs={{0,8},{2,10},{4,12},{6,14},{8,0},{10,2},{12,4},{14,6},{1,9},{3,11}... | collective-permute-start | bytes 12296 | tf_op jit(solution)/shard_map/ppermute | solution.py:120
  29.9 7.7 %collective-permute-start.4 = (f32[4,64,128]{2,1,0:T(8,128)S(1)}, f32[4,64,128]{2,1,0:T(8,128)S(1)}, u32[]{:S(2)}, u32[]{:S(2)}) collective-permute-start(f32[4,64,128]{2,1,0:T(8,128)S(1)} %constant_dynamic-slice_fusion.7), channel_id=1, source_target_pairs={{0,1},{1,0},{2,3},{3,2},{4,5},{5,4},{6,7},{7,6},{8,9},{9,8},{10,11... | collective-permute-start | bytes 393224 | tf_op jit(solution)/shard_map/ppermute | solution.py:52
  30.2 5.8 %collective-permute-start.3 = (f32[2,8,2048]{2,1,0:T(8,128)S(1)}, f32[2,8,2048]{2,1,0:T(8,128)S(1)}, u32[]{:S(2)}, u32[]{:S(2)}) collective-permute-start(f32[2,8,2048]{2,1,0:T(8,128)S(1)} %get-tuple-element.156), channel_id=1, source_target_pairs={{0,2},{2,0},{4,6},{6,4},{8,10},{10,8},{12,14},{14,12},{1,3},{3,1},... | collective-permute-start | bytes 393224 | tf_op jit(solution)/shard_map/ppermute | solution.py:120
  31.9 5.6 %collective-permute-start.2 = (f32[2,8,2048]{2,1,0:T(8,128)S(1)}, f32[2,8,2048]{2,1,0:T(8,128)S(1)}, u32[]{:S(2)}, u32[]{:S(2)}) collective-permute-start(f32[2,8,2048]{2,1,0:T(8,128)S(1)} %get-tuple-element.157), channel_id=1, source_target_pairs={{0,4},{2,6},{4,0},{6,2},{8,12},{10,14},{12,8},{14,10},{1,5},{3,7},... | collective-permute-start | bytes 393224 | tf_op jit(solution)/shard_map/ppermute | solution.py:120
  42.0 3.8 %collective-permute-start.7 = (f32[4,64,128]{2,1,0:T(8,128)S(1)}, f32[4,64,128]{2,1,0:T(8,128)S(1)}, u32[]{:S(2)}, u32[]{:S(2)}) collective-permute-start(f32[4,64,128]{2,1,0:T(8,128)S(1)} %constant_dynamic-slice_fusion.6), channel_id=1, source_target_pairs={{0,1},{1,0},{2,3},{3,2},{4,5},{5,4},{6,7},{7,6},{8,9},{9,8},{10,11... | collective-permute-start | bytes 393224 | tf_op jit(solution)/shard_map/ppermute | solution.py:52
  42.1 8.7 %collective-permute-start.6 = (f32[4,8,2048]{2,1,0:T(8,128)S(1)}, f32[4,8,2048]{2,1,0:T(8,128)S(1)}, u32[]{:S(2)}, u32[]{:S(2)}) collective-permute-start(f32[4,8,2048]{2,1,0:T(8,128)S(1)} %bitcast.232), channel_id=1, source_target_pairs={{0,4},{2,6},{4,0},{6,2},{8,12},{10,14},{12,8},{14,10},{1,5},{3,7},... | collective-permute-start | bytes 786440 | tf_op jit(solution)/shard_map/ppermute | solution.py:120
  43.7 8.4 %collective-permute-start.5 = (f32[4,8,2048]{2,1,0:T(8,128)S(1)}, f32[4,8,2048]{2,1,0:T(8,128)S(1)}, u32[]{:S(2)}, u32[]{:S(2)}) collective-permute-start(f32[4,8,2048]{2,1,0:T(8,128)S(1)} %bitcast.234), channel_id=1, source_target_pairs={{0,2},{2,0},{4,6},{6,4},{8,10},{10,8},{12,14},{14,12},{1,3},{3,1},... | collective-permute-start | bytes 786440 | tf_op jit(solution)/shard_map/ppermute | solution.py:120
  55.0 1.8 %collective-permute-start.10 = (f32[4,64,128]{2,1,0:T(8,128)S(1)}, f32[4,64,128]{2,1,0:T(8,128)S(1)}, u32[]{:S(2)}, u32[]{:S(2)}) collective-permute-start(f32[4,64,128]{2,1,0:T(8,128)S(1)} %constant_dynamic-slice_fusion.3), channel_id=1, source_target_pairs={{0,1},{1,0},{2,3},{3,2},{4,5},{5,4},{6,7},{7,6},{8,9},{9,8},{10,11... | collective-permute-start | bytes 393224 | tf_op jit(solution)/shard_map/ppermute | solution.py:52
  55.8 8.0 %collective-permute-start.9 = (f32[4,4,32,128]{3,2,1,0:T(8,128)S(1)}, f32[4,4,32,128]{3,2,1,0:T(8,128)S(1)}, u32[]{:S(2)}, u32[]{:S(2)}) collective-permute-start(f32[4,4,32,128]{3,2,1,0:T(8,128)S(1)} %bitcast.244), channel_id=1, source_target_pairs={{0,4},{2,6},{4,0},{6,2},{8,12},{10,14},{12,8},{14,10},{1,5},{3,7},... | collective-permute-start | bytes 786440 | tf_op jit(solution)/shard_map/ppermute | solution.py:160
  56.2 7.8 %collective-permute-start.8 = (f32[4,4,32,128]{3,2,1,0:T(8,128)S(1)}, f32[4,4,32,128]{3,2,1,0:T(8,128)S(1)}, u32[]{:S(2)}, u32[]{:S(2)}) collective-permute-start(f32[4,4,32,128]{3,2,1,0:T(8,128)S(1)} %copy-done.12), channel_id=1, source_target_pairs={{0,2},{2,0},{4,6},{6,4},{8,10},{10,8},{12,14},{14,12},{1,3},{3,1},... | collective-permute-start | bytes 786440 | tf_op jit(solution)/shard_map/ppermute | solution.py:160
  64.1 5.1 %collective-permute-start.16 = (f32[4,64,128]{2,1,0:T(8,128)S(1)}, f32[4,64,128]{2,1,0:T(8,128)S(1)}, u32[]{:S(2)}, u32[]{:S(2)}) collective-permute-start(f32[4,64,128]{2,1,0:T(8,128)S(1)} %constant_dynamic-slice_fusion.2), channel_id=1, source_target_pairs={{0,1},{1,0},{2,3},{3,2},{4,5},{5,4},{6,7},{7,6},{8,9},{9,8},{10,11... | collective-permute-start | bytes 393224 | tf_op jit(solution)/shard_map/ppermute | solution.py:52
  64.2 8.3 %collective-permute-start.15 = (f32[2,1,4,32,128]{4,3,2,0,1:T(8,128)S(1)}, f32[2,1,4,32,128]{4,3,2,0,1:T(8,128)S(1)}, u32[]{:S(2)}, u32[]{:S(2)}) collective-permute-start(f32[2,1,4,32,128]{4,3,2,0,1:T(8,128)S(1)} %dynamic-slice_bitcast_fusion.8), channel_id=1, source_target_pairs={{0,2},{2,0},{4,6},{6,4},{8,10},{10,8},{12,14},{14,12},{1,3},{3,1},... | collective-permute-start | bytes 393224 | tf_op jit(solution)/shard_map/ppermute | solution.py:186
  64.7 7.8 %collective-permute-start.14 = (f32[2,1,4,32,128]{4,3,2,0,1:T(8,128)S(1)}, f32[2,1,4,32,128]{4,3,2,0,1:T(8,128)S(1)}, u32[]{:S(2)}, u32[]{:S(2)}) collective-permute-start(f32[2,1,4,32,128]{4,3,2,0,1:T(8,128)S(1)} %dynamic-slice_bitcast_fusion.9), channel_id=1, source_target_pairs={{0,4},{2,6},{4,0},{6,2},{8,12},{10,14},{12,8},{14,10},{1,5},{3,7},... | collective-permute-start | bytes 393224 | tf_op jit(solution)/shard_map/ppermute | solution.py:186
  67.0 9.0 %collective-permute-start.12 = (f32[2,2,4,32,128]{4,3,2,1,0:T(8,128)S(1)}, f32[2,2,4,32,128]{4,3,2,1,0:T(8,128)S(1)}, u32[]{:S(2)}, u32[]{:S(2)}) collective-permute-start(f32[2,2,4,32,128]{4,3,2,1,0:T(8,128)S(1)} %dynamic-slice_bitcast_fusion), channel_id=1, source_target_pairs={{0,4},{2,6},{4,0},{6,2},{8,12},{10,14},{12,8},{14,10},{1,5},{3,7},... | collective-permute-start | bytes 786440 | tf_op jit(solution)/shard_map/ppermute | solution.py:186
  67.5 8.6 %collective-permute-start.11 = (f32[4,1,4,32,128]{4,3,2,0,1:T(8,128)S(1)}, f32[4,1,4,32,128]{4,3,2,0,1:T(8,128)S(1)}, u32[]{:S(2)}, u32[]{:S(2)}) collective-permute-start(f32[4,1,4,32,128]{4,3,2,0,1:T(8,128)S(1)} %dynamic-slice_bitcast_fusion.1), channel_id=1, source_target_pairs={{0,2},{2,0},{4,6},{6,4},{8,10},{10,8},{12,14},{14,12},{1,3},{3,1},... | collective-permute-start | bytes 786440 | tf_op jit(solution)/shard_map/ppermute | solution.py:186
  76.2 11.4 %collective-permute-start.20 = (f32[1,1,4,64,128]{4,3,2,1,0:T(8,128)S(1)}, f32[1,1,4,64,128]{4,3,2,1,0:T(8,128)S(1)}, u32[]{:S(2)}, u32[]{:S(2)}) collective-permute-start(f32[1,1,4,64,128]{4,3,2,1,0:T(8,128)S(1)} %dynamic-slice_bitcast_fusion.5), channel_id=1, source_target_pairs={{0,8},{2,10},{4,12},{6,14},{8,0},{10,2},{12,4},{14,6},{1,9},{3,11}... | collective-permute-start | bytes 393224 | tf_op jit(solution)/shard_map/ppermute | solution.py:186
  78.9 3.7 %collective-permute-start.19 = (f32[2,16,64]{2,1,0:T(8,128)S(1)}, f32[2,16,64]{2,1,0:T(8,128)S(1)}, u32[]{:S(2)}, u32[]{:S(2)}) collective-permute-start(f32[2,16,64]{2,1,0:T(8,128)S(1)} %copy-done.15), channel_id=1, source_target_pairs={{0,4},{2,6},{4,0},{6,2},{8,12},{10,14},{12,8},{14,10},{1,5},{3,7},... | collective-permute-start | bytes 24584 | tf_op jit(solution)/shard_map/ppermute | solution.py:120
  80.5 5.0 %collective-permute-start.18 = (f32[2,1,4,32,128]{4,3,2,0,1:T(8,128)S(1)}, f32[2,1,4,32,128]{4,3,2,0,1:T(8,128)S(1)}, u32[]{:S(2)}, u32[]{:S(2)}) collective-permute-start(f32[2,1,4,32,128]{4,3,2,0,1:T(8,128)S(1)} %dynamic-slice_bitcast_fusion.6), channel_id=1, source_target_pairs={{0,2},{2,0},{4,6},{6,4},{8,10},{10,8},{12,14},{14,12},{1,3},{3,1},... | collective-permute-start | bytes 393224 | tf_op jit(solution)/shard_map/ppermute | solution.py:186
  82.1 5.5 %collective-permute-start.17 = (f32[2,1,4,32,128]{4,3,2,0,1:T(8,128)S(1)}, f32[2,1,4,32,128]{4,3,2,0,1:T(8,128)S(1)}, u32[]{:S(2)}, u32[]{:S(2)}) collective-permute-start(f32[2,1,4,32,128]{4,3,2,0,1:T(8,128)S(1)} %dynamic-slice_bitcast_fusion.7), channel_id=1, source_target_pairs={{0,4},{2,6},{4,0},{6,2},{8,12},{10,14},{12,8},{14,10},{1,5},{3,7},... | collective-permute-start | bytes 393224 | tf_op jit(solution)/shard_map/ppermute | solution.py:186
  87.6 7.2 %collective-permute-start.21 = (f32[1,1,4,64,128]{4,3,2,1,0:T(8,128)S(1)}, f32[1,1,4,64,128]{4,3,2,1,0:T(8,128)S(1)}, u32[]{:S(2)}, u32[]{:S(2)}) collective-permute-start(f32[1,1,4,64,128]{4,3,2,1,0:T(8,128)S(1)} %dynamic-slice_bitcast_fusion.4), channel_id=1, source_target_pairs={{0,8},{2,10},{4,12},{6,14},{8,0},{10,2},{12,4},{14,6},{1,9},{3,11}... | collective-permute-start | bytes 393224 | tf_op jit(solution)/shard_map/ppermute | solution.py:186
  87.9 3.9 %collective-permute-start.22 = (f32[4,16,64]{2,1,0:T(8,128)S(1)}, f32[4,16,64]{2,1,0:T(8,128)S(1)}, u32[]{:S(2)}, u32[]{:S(2)}) collective-permute-start(f32[4,16,64]{2,1,0:T(8,128)S(1)} %bitcast.255), channel_id=1, source_target_pairs={{0,2},{2,0},{4,6},{6,4},{8,10},{10,8},{12,14},{14,12},{1,3},{3,1},... | collective-permute-start | bytes 49160 | tf_op jit(solution)/shard_map/ppermute | solution.py:120
  96.7 8.1 %collective-permute-start.23 = (f32[1,4,64,128]{3,2,1,0:T(8,128)S(1)}, f32[1,4,64,128]{3,2,1,0:T(8,128)S(1)}, u32[]{:S(2)}, u32[]{:S(2)}) collective-permute-start(f32[1,4,64,128]{3,2,1,0:T(8,128)S(1)} %fusion.1), channel_id=1, source_target_pairs={{0,8},{2,10},{4,12},{6,14},{8,0},{10,2},{12,4},{14,6},{1,9},{3,11}... | collective-permute-start | bytes 393224 | tf_op jit(solution)/shard_map/ppermute | solution.py:120
  104.9 5.3 %collective-permute-start.25 = (f32[2,4,32,128]{3,2,1,0:T(8,128)S(1)}, f32[2,4,32,128]{3,2,1,0:T(8,128)S(1)}, u32[]{:S(2)}, u32[]{:S(2)}) collective-permute-start(f32[2,4,32,128]{3,2,1,0:T(8,128)S(1)} %get-tuple-element.152), channel_id=1, source_target_pairs={{0,2},{2,0},{4,6},{6,4},{8,10},{10,8},{12,14},{14,12},{1,3},{3,1},... | collective-permute-start | bytes 393224 | tf_op jit(solution)/shard_map/ppermute | solution.py:120
  106.1 5.1 %collective-permute-start.24 = (f32[2,4,32,128]{3,2,1,0:T(8,128)S(1)}, f32[2,4,32,128]{3,2,1,0:T(8,128)S(1)}, u32[]{:S(2)}, u32[]{:S(2)}) collective-permute-start(f32[2,4,32,128]{3,2,1,0:T(8,128)S(1)} %get-tuple-element.153), channel_id=1, source_target_pairs={{0,4},{2,6},{4,0},{6,2},{8,12},{10,14},{12,8},{14,10},{1,5},{3,7},... | collective-permute-start | bytes 393224 | tf_op jit(solution)/shard_map/ppermute | solution.py:120
  111.3 7.6 %collective-permute-start.27 = (f32[4,4,32,128]{3,2,1,0:T(8,128)S(1)}, f32[4,4,32,128]{3,2,1,0:T(8,128)S(1)}, u32[]{:S(2)}, u32[]{:S(2)}) collective-permute-start(f32[4,4,32,128]{3,2,1,0:T(8,128)S(1)} %bitcast.238), channel_id=1, source_target_pairs={{0,4},{2,6},{4,0},{6,2},{8,12},{10,14},{12,8},{14,10},{1,5},{3,7},... | collective-permute-start | bytes 786440 | tf_op jit(solution)/shard_map/ppermute | solution.py:120
  111.6 7.1 %collective-permute-start.26 = (f32[4,4,32,128]{3,2,1,0:T(8,128)S(1)}, f32[4,4,32,128]{3,2,1,0:T(8,128)S(1)}, u32[]{:S(2)}, u32[]{:S(2)}) collective-permute-start(f32[4,4,32,128]{3,2,1,0:T(8,128)S(1)} %bitcast.242), channel_id=1, source_target_pairs={{0,2},{2,0},{4,6},{6,4},{8,10},{10,8},{12,14},{14,12},{1,3},{3,1},... | collective-permute-start | bytes 786440 | tf_op jit(solution)/shard_map/ppermute | solution.py:120
  121.0 1.6 %collective-permute-start.28 = (f32[4,64,128]{2,1,0:T(8,128)}, f32[4,64,128]{2,1,0:T(8,128)S(1)}, u32[]{:S(2)}, u32[]{:S(2)}) collective-permute-start(f32[4,64,128]{2,1,0:T(8,128)} %constant_dynamic-slice_fusion), channel_id=1, source_target_pairs={{0,1},{1,0},{2,3},{3,2},{4,5},{5,4},{6,7},{7,6},{8,9},{9,8},{10,11... | collective-permute-start | bytes 393224 | tf_op jit(solution)/shard_map/ppermute | solution.py:52
  127.7 1.9 %collective-permute-start.29 = (f32[1,2,256]{2,1,0:T(2,128)S(1)}, f32[1,2,256]{2,1,0:T(2,128)S(1)}, u32[]{:S(2)}, u32[]{:S(2)}) collective-permute-start(f32[1,2,256]{2,1,0:T(2,128)S(1)} %maximum_bitcast_fusion), channel_id=1, source_target_pairs={{0,1},{1,0},{2,3},{3,2},{4,5},{5,4},{6,7},{7,6},{8,9},{9,8},{10,11... | collective-permute-start | bytes 6152 | tf_op jit(solution)/shard_map/ppermute | solution.py:391
  (24 other events, 68.7 us)

commit v17 on v15

--- a/solution.py
+++ b/solution.py
@@ -300,7 +300,6 @@
     light_orders = {"la": near_first[:-1], "lb": swap_first(near_first[:-1])}
 
     def wave_and_split():
-        task_wave(2)()
         pieces = halves(st["light"].reshape(n_shot, slab, span_y, span_z), 2)
         for (name, order), piece in zip(sorted(light_orders.items()), pieces):
             st[name + "_keep"], st[name + "_send"] = split_step(piece, order[0], list(near_first))
@@ -333,7 +332,7 @@
     image_a, image_b = halves(image.reshape(n_shot, slab, span_y, span_z), 2)
     image_a = chain(image_a, "rs", near_first[:-1], near_first)
     image_b = chain(image_b, "rs", swap_first(near_first[:-1]), near_first)
-    tasks = [task_wave(3)]
+    tasks = [task_wave(2), task_wave(3)]
     light_c = None
     for i in range(len(bits) - 1):
         group = [image_a, image_b]

time: 130 us -> 135 us (1.038)
  other arithmetic: 34.8 us -> 40.9 us
  waiting for transfers between devices: 41.9 us -> 36.2 us
  starting transfers between devices: 25.6 us -> 29.1 us
    ppermute x8, waiting for transfers between devices: 17.6 us -> 10.2 us  [rs_step(): got = lax.ppermute(send, 'shot', [(i, i ^ k) for i in range(n)])]
    ppermute x6, waiting for transfers between devices: 0.54 us -> 4.08 us  [with_halo(): got = lax.ppermute(piece, 'space', [(0, 1), (1, 0)])]
    ppermute x2, waiting for transfers between devices: 3.04 us -> 0.01 us  [chain_step(): return keep + lax.ppermute(send, 'shot', [(i, i ^ k) for i in range(n)])]
    ppermute x13, starting transfers between devices: 13 us -> 15.3 us  [ag_step(): theirs = lax.ppermute(held, 'shot', [(i, i ^ k) for i in range(n)])]
    add x2, other arithmetic: 0.08 us -> 1.98 us  [chain_step(): return keep + lax.ppermute(send, 'shot', [(i, i ^ k) for i in range(n)])]
    ppermute x8, starting transfers between devices: 8.48 us -> 9.99 us  [rs_step(): got = lax.ppermute(send, 'shot', [(i, i ^ k) for i in range(n)])]
    unnamed x55 -> x61, local copies, waits for them, and re-layouts: 5.27 us -> 4.74 us
  transfers between devices with their start and end apart: 30 -> 30, of which waited for: 15 -> 14; matrix products, arithmetic and copies ran while one was open for 28% -> 32% of each run, Pallas kernels for 0% -> 0%
where the time goes in v17:
time: 135 us; the launch traced here: 134 us
  other arithmetic  40.9 us (30%)
  waiting for transfers between devices  36.2 us (27%)
  starting transfers between devices  29.1 us (22%)
  local copies, waits for them, and re-layouts  21.3 us (16%)
  between operations  4.89 us (4%)
  matrix products  1.7 us (1%)
    ppermute x13, waiting for transfers between devices, ag_step(): theirs = lax.ppermute(held, 'shot', [(i, i ^ k) for i in range(n)])  22 us
    ppermute x13, starting transfers between devices, ag_step(): theirs = lax.ppermute(held, 'shot', [(i, i ^ k) for i in range(n)])  15.3 us
    ppermute x8, waiting for transfers between devices, rs_step(): got = lax.ppermute(send, 'shot', [(i, i ^ k) for i in range(n)])  10.2 us
    ppermute x8, starting transfers between devices, rs_step(): got = lax.ppermute(send, 'shot', [(i, i ^ k) for i in range(n)])  9.99 us
    add x3, other arithmetic, inject(): return field + jnp.where(hit, source_gain[0] * wavelet[0, moment], 0.0)  8.65 us
    add x2, other arithmetic, born_second(): 2.0 * born + speed_term * laplace_x(with_halo(born)) - absorber * born  5.8 us
    unnamed x61, local copies, waits for them, and re-layouts  4.74 us
    ppermute x6, waiting for transfers between devices, with_halo(): got = lax.ppermute(piece, 'space', [(0, 1), (1, 0)])  4.08 us
  transfers between devices with their start and end apart: 30, of which 14 were waited for; matrix products, arithmetic and copies ran while one was open for 32% of the time, Pallas kernels for 0%

profile of v17, /device:TPU:0, one launch (start us, length us, event | category | flops | bytes accessed | tf_op | source)
XLA Modules:
  0.0 134.1 jit_solution(4159161107746960430)
XLA Ops:
  2.6 4.0 %collective-permute-start = (f32[1,16,2048]{2,1,0:T(8,128)}, f32[1,16,2048]{2,1,0:T(8,128)}, u32[]{:S(2)}, u32[]{:S(2)}) collective-permute-start(f32[1,16,2048]{2,1,0:T(8,128)} %concatenate.199), channel_id=1, source_target_pairs={{0,8},{2,10},{4,12},{6,14},{8,0},{10,2},{12,4},{14,6},{1,9},{3,11}... | collective-permute-start | bytes 393224 | tf_op jit(solution)/shard_map/ppermute | solution.py:120
  6.6 1.6 %dynamic-slice_bitcast_fusion.10 = f32[4,64,128]{2,1,0:T(8,128)} fusion(f32[1,32,64,128]{3,2,1,0:T(8,128)} %param.12, s32[]{:T(128)S(6)} %select_n.404), kind=kLoop, calls=%fused_computation.441 | loop fusion | bytes 262148 | tf_op jit(solution)/shard_map/dynamic_slice | solution.py:51
  10.3 4.0 %pad_maximum_fusion.15 = (f32[3]{0:T(128)S(1)}, f32[3]{0:T(128)S(1)}) fusion(f32[1]{0:T(128)} %get-tuple-element.167, f32[1]{0:T(128)} %get-tuple-element.168, f32[1]{0:T(128)} %get-tuple-element.163, f32[1]{0:T(128)} %get-tuple-element.164, f32[1]{0:T(128)} %get-tuple-element.165, f32[1]{0:T(128)} %get-tuple-element.166), kind=kLoop, calls=%fused_computation.500 | loop fusion | flops 12 | bytes 48 | tf_op jit(solution)/shard_map/stack | solution.py:37
  17.7 2.6 %fusion.144 = f32[24,64,128]{2,1,0:T(8,128)} fusion(f32[32,64,128]{2,1,0:T(8,128)S(1)} %bitcast.205, f32[1,32,64,128]{3,2,1,0:T(8,128)S(1)} %copy-done), kind=kLoop, calls=%fused_computation.324 | loop fusion | flops 5701632 | bytes 8912896 | tf_op jit(solution)/shard_map/add | solution.py:86
  21.3 1.3 broadcast_and_fusion
  30.6 1.5 %maximum_select_fusion.4 = f32[2,16,2048]{2,1,0:T(8,128)S(1)} fusion(f32[1,16,2048]{2,1,0:T(8,128)} %collective-permute-done, f32[1,16,2048]{2,1,0:T(8,128)} %concatenate.199, pred[]{:T(512)S(6)} %eq.97), kind=kLoop, calls=%fused_computation.344 | loop fusion | flops 196608 | bytes 524289 | tf_op jit(solution)/shard_map/jit(_where)/select_n | solution.py:125
  32.1 1.9 %collective-permute-start.3 = (f32[2,8,2048]{2,1,0:T(8,128)S(1)}, f32[2,8,2048]{2,1,0:T(8,128)S(1)}, u32[]{:S(2)}, u32[]{:S(2)}) collective-permute-start(f32[2,8,2048]{2,1,0:T(8,128)S(1)} %get-tuple-element.157), channel_id=1, source_target_pairs={{0,4},{2,6},{4,0},{6,2},{8,12},{10,14},{12,8},{14,10},{1,5},{3,7},... | collective-permute-start | bytes 393224 | tf_op jit(solution)/shard_map/ppermute | solution.py:120
  34.4 1.9 %collective-permute-start.4 = (f32[2,8,2048]{2,1,0:T(8,128)S(1)}, f32[2,8,2048]{2,1,0:T(8,128)S(1)}, u32[]{:S(2)}, u32[]{:S(2)}) collective-permute-start(f32[2,8,2048]{2,1,0:T(8,128)S(1)} %get-tuple-element.156), channel_id=1, source_target_pairs={{0,2},{2,0},{4,6},{6,4},{8,10},{10,8},{12,14},{14,12},{1,3},{3,1},... | collective-permute-start | bytes 393224 | tf_op jit(solution)/shard_map/ppermute | solution.py:120
  36.3 2.3 %collective-permute-done.5 = f32[2,16,64]{2,1,0:T(8,128)S(1)} collective-permute-done((f32[2,16,64]{2,1,0:T(8,128)S(1)}, f32[2,16,64]{2,1,0:T(8,128)S(1)}, u32[]{:S(2)}, u32[]{:S(2)}) %collective-permute-start.5) | collective-permute-done | bytes 8224 | tf_op jit(solution)/shard_map/ppermute | solution.py:120
  38.7 1.3 %collective-permute-done.4 = f32[2,8,2048]{2,1,0:T(8,128)S(1)} collective-permute-done((f32[2,8,2048]{2,1,0:T(8,128)S(1)}, f32[2,8,2048]{2,1,0:T(8,128)S(1)}, u32[]{:S(2)}, u32[]{:S(2)}) %collective-permute-start.4) | collective-permute-done | bytes 131104 | tf_op jit(solution)/shard_map/ppermute | solution.py:120
  40.1 3.9 %fusion.3 = (f32[32,64,128]{2,1,0:T(8,128)}, f32[32,64,128]{2,1,0:T(8,128)S(1)}) fusion(f32[32,64,128]{2,1,0:T(8,128)S(1)} %get-tuple-element.91, f32[32,64,128]{2,1,0:T(8,128)S(1)} %bitcast.207, f32[]{:T(128)S(6)} %mul.394, f32[128]{0:T(128)S(1)} %copy-done.18, f32[32,64]{1,0:T(8,128)S(1)} %broadcast_add_fusion, pred[128]{0:T(512)(128)(4,1)S(1)} %copy-done.21, ...), kind=kLoop, calls=%fused_computation.151 | loop fusion | flops 12058624 | bytes 16012292 | tf_op jit(solution)/shard_map/add | solution.py:230
  45.0 1.6 %collective-permute-start.7 = (f32[4,8,2048]{2,1,0:T(8,128)S(1)}, f32[4,8,2048]{2,1,0:T(8,128)S(1)}, u32[]{:S(2)}, u32[]{:S(2)}) collective-permute-start(f32[4,8,2048]{2,1,0:T(8,128)S(1)} %bitcast.232), channel_id=1, source_target_pairs={{0,2},{2,0},{4,6},{6,4},{8,10},{10,8},{12,14},{14,12},{1,3},{3,1},... | collective-permute-start | bytes 786440 | tf_op jit(solution)/shard_map/ppermute | solution.py:120
  46.6 1.6 %collective-permute-start.8 = (f32[4,8,2048]{2,1,0:T(8,128)S(1)}, f32[4,8,2048]{2,1,0:T(8,128)S(1)}, u32[]{:S(2)}, u32[]{:S(2)}) collective-permute-start(f32[4,8,2048]{2,1,0:T(8,128)S(1)} %bitcast.234), channel_id=1, source_target_pairs={{0,4},{2,6},{4,0},{6,2},{8,12},{10,14},{12,8},{14,10},{1,5},{3,7},... | collective-permute-start | bytes 786440 | tf_op jit(solution)/shard_map/ppermute | solution.py:120
  50.3 2.9 %collective-permute-done.9 = f32[4,16,64]{2,1,0:T(8,128)S(1)} collective-permute-done((f32[4,16,64]{2,1,0:T(8,128)S(1)}, f32[4,16,64]{2,1,0:T(8,128)S(1)}, u32[]{:S(2)}, u32[]{:S(2)}) %collective-permute-start.9) | collective-permute-done | bytes 16416 | tf_op jit(solution)/shard_map/ppermute | solution.py:120
  54.0 1.5 %collective-permute-start.10 = (f32[4,4,32,128]{3,2,1,0:T(8,128)}, f32[4,4,32,128]{3,2,1,0:T(8,128)}, u32[]{:S(2)}, u32[]{:S(2)}) collective-permute-start(f32[4,4,32,128]{3,2,1,0:T(8,128)} %get-tuple-element.75), channel_id=1, source_target_pairs={{0,2},{2,0},{4,6},{6,4},{8,10},{10,8},{12,14},{14,12},{1,3},{3,1},... | collective-permute-start | bytes 786440 | tf_op jit(solution)/shard_map/ppermute | solution.py:160
  55.5 1.6 %collective-permute-start.11 = (f32[4,4,32,128]{3,2,1,0:T(8,128)}, f32[4,4,32,128]{3,2,1,0:T(8,128)}, u32[]{:S(2)}, u32[]{:S(2)}) collective-permute-start(f32[4,4,32,128]{3,2,1,0:T(8,128)} %bitcast.45), channel_id=1, source_target_pairs={{0,4},{2,6},{4,0},{6,2},{8,12},{10,14},{12,8},{14,10},{1,5},{3,7},... | collective-permute-start | bytes 786440 | tf_op jit(solution)/shard_map/ppermute | solution.py:160
  58.1 2.6 %copy.48 = f32[2048,128]{1,0:T(8,128)} copy(f32[2048,128]{0,1:T(8,128)} %bitcast.216) | data formatting | bytes 2097152 | tf_op jit(solution)/shard_map/transpose | solution.py:324
  60.8 1.4 %mul.395 = f32[32,64,128]{2,1,0:T(8,128)S(1)} multiply(f32[32,64,128]{2,1,0:T(8,128)} %bitcast.210, f32[32,64,128]{2,1,0:T(8,128)S(1)} %copy-done.3) | non-fusion elementwise | flops 262144 | bytes 3145728 | tf_op jit(solution)/shard_map/mul | solution.py:325
  63.7 2.9 %fusion.42 = f32[32,64,128]{2,1,0:T(8,128)S(1)} fusion(f32[40,64,128]{2,1,0:T(8,128)S(1)} %constant_dynamic-update-slice_fusion.3, f32[32,64,128]{2,1,0:T(8,128)S(1)} %bitcast.211, f32[32,64,128]{2,1,0:T(8,128)S(1)} %copy-done.5, f32[32,64,128]{2,1,0:T(8,128)S(1)} %mul.395, f32[128]{0:T(128)S(1)} %copy-done.19, f32[32,64]{1,0:T(8,128)S(1)} %broadcast_add_fusion, ...), kind=kLoop, calls=%fused_computation.190 | loop fusion | flops 11272192 | bytes 16007680 | tf_op jit(solution)/shard_map/add | solution.py:251
  70.5 1.5 %collective-permute-start.15 = (f32[2,1,4,32,128]{4,3,2,0,1:T(8,128)S(1)}, f32[2,1,4,32,128]{4,3,2,0,1:T(8,128)S(1)}, u32[]{:S(2)}, u32[]{:S(2)}) collective-permute-start(f32[2,1,4,32,128]{4,3,2,0,1:T(8,128)S(1)} %dynamic-slice_bitcast_fusion.9), channel_id=1, source_target_pairs={{0,4},{2,6},{4,0},{6,2},{8,12},{10,14},{12,8},{14,10},{1,5},{3,7},... | collective-permute-start | bytes 393224 | tf_op jit(solution)/shard_map/ppermute | solution.py:186
  72.0 1.6 %collective-permute-start.16 = (f32[2,1,4,32,128]{4,3,2,0,1:T(8,128)S(1)}, f32[2,1,4,32,128]{4,3,2,0,1:T(8,128)S(1)}, u32[]{:S(2)}, u32[]{:S(2)}) collective-permute-start(f32[2,1,4,32,128]{4,3,2,0,1:T(8,128)S(1)} %dynamic-slice_bitcast_fusion.8), channel_id=1, source_target_pairs={{0,2},{2,0},{4,6},{6,4},{8,10},{10,8},{12,14},{14,12},{1,3},{3,1},... | collective-permute-start | bytes 393224 | tf_op jit(solution)/shard_map/ppermute | solution.py:186
  75.1 3.9 %fusion.4 = (f32[32,64,128]{2,1,0:T(8,128)S(1)}, f32[32,64,128]{2,1,0:T(8,128)}) fusion(f32[32,64,128]{2,1,0:T(8,128)S(1)} %copy-done.6, f32[32,64,128]{2,1,0:T(8,128)S(1)} %get-tuple-element.91, f32[]{:T(128)S(6)} %mul.415, f32[128]{0:T(128)S(1)} %copy-done.19, f32[32,64]{1,0:T(8,128)S(1)} %broadcast_add_fusion, pred[128]{0:T(512)(128)(4,1)S(1)} %copy-done.22, ...), kind=kLoop, calls=%fused_computation.152 | loop fusion | flops 12058624 | bytes 16012292 | tf_op jit(solution)/shard_map/add | solution.py:230
  78.9 1.8 %collective-permute-done.15 = f32[2,1,4,32,128]{4,3,2,0,1:T(8,128)S(1)} collective-permute-done((f32[2,1,4,32,128]{4,3,2,0,1:T(8,128)S(1)}, f32[2,1,4,32,128]{4,3,2,0,1:T(8,128)S(1)}, u32[]{:S(2)}, u32[]{:S(2)}) %collective-permute-start.15) | collective-permute-done | bytes 131104 | tf_op jit(solution)/shard_map/ppermute | solution.py:186
  81.6 1.5 %collective-permute-start.19 = (f32[2,1,4,32,128]{4,3,2,0,1:T(8,128)S(1)}, f32[2,1,4,32,128]{4,3,2,0,1:T(8,128)S(1)}, u32[]{:S(2)}, u32[]{:S(2)}) collective-permute-start(f32[2,1,4,32,128]{4,3,2,0,1:T(8,128)S(1)} %dynamic-slice_bitcast_fusion.6), channel_id=1, source_target_pairs={{0,2},{2,0},{4,6},{6,4},{8,10},{10,8},{12,14},{14,12},{1,3},{3,1},... | collective-permute-start | bytes 393224 | tf_op jit(solution)/shard_map/ppermute | solution.py:186
  83.1 2.7 %collective-permute-start.20 = (f32[1,1,4,64,128]{4,3,2,1,0:T(8,128)S(1)}, f32[1,1,4,64,128]{4,3,2,1,0:T(8,128)S(1)}, u32[]{:S(2)}, u32[]{:S(2)}) collective-permute-start(f32[1,1,4,64,128]{4,3,2,1,0:T(8,128)S(1)} %dynamic-slice_bitcast_fusion.5), channel_id=1, source_target_pairs={{0,8},{2,10},{4,12},{6,14},{8,0},{10,2},{12,4},{14,6},{1,9},{3,11}... | collective-permute-start | bytes 393224 | tf_op jit(solution)/shard_map/ppermute | solution.py:186
  87.2 3.2 %fusion.92 = f32[32,64,128]{2,1,0:T(8,128)} fusion(f32[40,64,128]{2,1,0:T(8,128)S(1)} %constant_dynamic-update-slice_fusion.1, s32[32,64,128]{2,1,0:T(8,128)S(1)} %copy-done.1), kind=kLoop, calls=%fused_computation.240 | loop fusion | flops 9175040 | bytes 12845056 | tf_op jit(solution)/shard_map/mul | solution.py:243
  92.0 8.0 %collective-permute-done.22 = f32[1,1,4,64,128]{4,3,2,1,0:T(8,128)S(1)} collective-permute-done((f32[1,1,4,64,128]{4,3,2,1,0:T(8,128)S(1)}, f32[1,1,4,64,128]{4,3,2,1,0:T(8,128)S(1)}, u32[]{:S(2)}, u32[]{:S(2)}) %collective-permute-start.22) | collective-permute-done | bytes 131104 | tf_op jit(solution)/shard_map/ppermute | solution.py:186
  101.8 7.3 %collective-permute-done.23 = f32[1,4,64,128]{3,2,1,0:T(8,128)S(1)} collective-permute-done((f32[1,4,64,128]{3,2,1,0:T(8,128)S(1)}, f32[1,4,64,128]{3,2,1,0:T(8,128)S(1)}, u32[]{:S(2)}, u32[]{:S(2)}) %collective-permute-start.23) | collective-permute-done | bytes 131104 | tf_op jit(solution)/shard_map/ppermute | solution.py:120
  110.7 4.0 %collective-permute-done.24 = f32[2,4,32,128]{3,2,1,0:T(8,128)S(1)} collective-permute-done((f32[2,4,32,128]{3,2,1,0:T(8,128)S(1)}, f32[2,4,32,128]{3,2,1,0:T(8,128)S(1)}, u32[]{:S(2)}, u32[]{:S(2)}) %collective-permute-start.24) | collective-permute-done | bytes 131104 | tf_op jit(solution)/shard_map/ppermute | solution.py:120
  115.6 1.7 %collective-permute-start.27 = (f32[4,4,32,128]{3,2,1,0:T(8,128)S(1)}, f32[4,4,32,128]{3,2,1,0:T(8,128)S(1)}, u32[]{:S(2)}, u32[]{:S(2)}) collective-permute-start(f32[4,4,32,128]{3,2,1,0:T(8,128)S(1)} %bitcast.242), channel_id=1, source_target_pairs={{0,4},{2,6},{4,0},{6,2},{8,12},{10,14},{12,8},{14,10},{1,5},{3,7},... | collective-permute-start | bytes 786440 | tf_op jit(solution)/shard_map/ppermute | solution.py:120
  118.5 3.7 %collective-permute-done.26 = f32[4,4,32,128]{3,2,1,0:T(8,128)S(1)} collective-permute-done((f32[4,4,32,128]{3,2,1,0:T(8,128)S(1)}, f32[4,4,32,128]{3,2,1,0:T(8,128)S(1)}, u32[]{:S(2)}, u32[]{:S(2)}) %collective-permute-start.26) | collective-permute-done | bytes 262176 | tf_op jit(solution)/shard_map/ppermute | solution.py:120
  127.3 2.9 %fusion.120 = f32[32,64,128]{2,1,0:T(8,128)S(1)} fusion(f32[40,64,128]{2,1,0:T(8,128)S(1)} %constant_dynamic-update-slice_fusion, f32[32,64,128]{2,1,0:T(8,128)S(1)} %copy-done.10, f32[128]{0:T(128)S(1)} %copy-done.20, f32[32,64]{1,0:T(8,128)S(1)} %broadcast_add_fusion, f32[8,4,64,128]{3,2,1,0:T(8,128)S(1)} %pad_maximum_fusion.13, ...), kind=kLoop, calls=%fused_computation.268 | loop fusion | flops 11534336 | bytes 16007680 | tf_op jit(solution)/shard_map/add | solution.py:251
  (207 shorter events, 43.2 us)
Async XLA Ops:
  0.6 17.1 %copy-start = (f32[1,32,64,128]{3,2,1,0:T(8,128)S(1)}, f32[1,32,64,128]{3,2,1,0:T(8,128)}, u32[]{:S(2)}) copy-start(f32[1,32,64,128]{3,2,1,0:T(8,128)} %param.12) | copy-start | bytes 3145732
  0.7 15.4 %copy-start.23 = (f32[1,4]{1,0:T(1,128)S(1)}, f32[1,4]{1,0:T(1,128)}, u32[]{:S(2)}) copy-start(f32[1,4]{1,0:T(1,128)} %param.16) | copy-start | bytes 52
  2.6 28.0 %collective-permute-start = (f32[1,16,2048]{2,1,0:T(8,128)}, f32[1,16,2048]{2,1,0:T(8,128)}, u32[]{:S(2)}, u32[]{:S(2)}) collective-permute-start(f32[1,16,2048]{2,1,0:T(8,128)} %concatenate.199), channel_id=1, source_target_pairs={{0,8},{2,10},{4,12},{6,14},{8,0},{10,2},{12,4},{14,6},{1,9},{3,11}... | collective-permute-start | bytes 393224 | tf_op jit(solution)/shard_map/ppermute | solution.py:120
  6.6 19.8 %collective-permute-start.1 = (f32[1,16,64]{2,1,0:T(8,128)}, f32[1,16,64]{2,1,0:T(8,128)}, u32[]{:S(2)}, u32[]{:S(2)}) collective-permute-start(f32[1,16,64]{2,1,0:T(8,128)} %bitcast.261), channel_id=1, source_target_pairs={{0,8},{2,10},{4,12},{6,14},{8,0},{10,2},{12,4},{14,6},{1,9},{3,11}... | collective-permute-start | bytes 12296 | tf_op jit(solution)/shard_map/ppermute | solution.py:120
  8.2 19.0 %collective-permute-start.2 = (f32[4,64,128]{2,1,0:T(8,128)}, f32[4,64,128]{2,1,0:T(8,128)}, u32[]{:S(2)}, u32[]{:S(2)}) collective-permute-start(f32[4,64,128]{2,1,0:T(8,128)} %dynamic-slice_bitcast_fusion.10), channel_id=1, source_target_pairs={{0,1},{1,0},{2,3},{3,2},{4,5},{5,4},{6,7},{7,6},{8,9},{9,8},{10,11... | collective-permute-start | bytes 393224 | tf_op jit(solution)/shard_map/ppermute | solution.py:52
  32.1 6.5 %collective-permute-start.3 = (f32[2,8,2048]{2,1,0:T(8,128)S(1)}, f32[2,8,2048]{2,1,0:T(8,128)S(1)}, u32[]{:S(2)}, u32[]{:S(2)}) collective-permute-start(f32[2,8,2048]{2,1,0:T(8,128)S(1)} %get-tuple-element.157), channel_id=1, source_target_pairs={{0,4},{2,6},{4,0},{6,2},{8,12},{10,14},{12,8},{14,10},{1,5},{3,7},... | collective-permute-start | bytes 393224 | tf_op jit(solution)/shard_map/ppermute | solution.py:120
  34.1 4.5 %collective-permute-start.5 = (f32[2,16,64]{2,1,0:T(8,128)S(1)}, f32[2,16,64]{2,1,0:T(8,128)S(1)}, u32[]{:S(2)}, u32[]{:S(2)}) collective-permute-start(f32[2,16,64]{2,1,0:T(8,128)S(1)} %maximum_select_fusion.12), channel_id=1, source_target_pairs={{0,4},{2,6},{4,0},{6,2},{8,12},{10,14},{12,8},{14,10},{1,5},{3,7},... | collective-permute-start | bytes 24584 | tf_op jit(solution)/shard_map/ppermute | solution.py:120
  34.4 5.6 %collective-permute-start.4 = (f32[2,8,2048]{2,1,0:T(8,128)S(1)}, f32[2,8,2048]{2,1,0:T(8,128)S(1)}, u32[]{:S(2)}, u32[]{:S(2)}) collective-permute-start(f32[2,8,2048]{2,1,0:T(8,128)S(1)} %get-tuple-element.156), channel_id=1, source_target_pairs={{0,2},{2,0},{4,6},{6,4},{8,10},{10,8},{12,14},{14,12},{1,3},{3,1},... | collective-permute-start | bytes 393224 | tf_op jit(solution)/shard_map/ppermute | solution.py:120
  36.3 3.8 %collective-permute-start.6 = (f32[4,64,128]{2,1,0:T(8,128)S(1)}, f32[4,64,128]{2,1,0:T(8,128)S(1)}, u32[]{:S(2)}, u32[]{:S(2)}) collective-permute-start(f32[4,64,128]{2,1,0:T(8,128)S(1)} %constant_dynamic-slice_fusion.7), channel_id=1, source_target_pairs={{0,1},{1,0},{2,3},{3,2},{4,5},{5,4},{6,7},{7,6},{8,9},{9,8},{10,11... | collective-permute-start | bytes 393224 | tf_op jit(solution)/shard_map/ppermute | solution.py:52
  45.0 8.9 %collective-permute-start.7 = (f32[4,8,2048]{2,1,0:T(8,128)S(1)}, f32[4,8,2048]{2,1,0:T(8,128)S(1)}, u32[]{:S(2)}, u32[]{:S(2)}) collective-permute-start(f32[4,8,2048]{2,1,0:T(8,128)S(1)} %bitcast.232), channel_id=1, source_target_pairs={{0,2},{2,0},{4,6},{6,4},{8,10},{10,8},{12,14},{14,12},{1,3},{3,1},... | collective-permute-start | bytes 786440 | tf_op jit(solution)/shard_map/ppermute | solution.py:120
  46.6 7.4 %collective-permute-start.8 = (f32[4,8,2048]{2,1,0:T(8,128)S(1)}, f32[4,8,2048]{2,1,0:T(8,128)S(1)}, u32[]{:S(2)}, u32[]{:S(2)}) collective-permute-start(f32[4,8,2048]{2,1,0:T(8,128)S(1)} %bitcast.234), channel_id=1, source_target_pairs={{0,4},{2,6},{4,0},{6,2},{8,12},{10,14},{12,8},{14,10},{1,5},{3,7},... | collective-permute-start | bytes 786440 | tf_op jit(solution)/shard_map/ppermute | solution.py:120
  48.2 5.0 %collective-permute-start.9 = (f32[4,16,64]{2,1,0:T(8,128)S(1)}, f32[4,16,64]{2,1,0:T(8,128)S(1)}, u32[]{:S(2)}, u32[]{:S(2)}) collective-permute-start(f32[4,16,64]{2,1,0:T(8,128)S(1)} %bitcast.254), channel_id=1, source_target_pairs={{0,2},{2,0},{4,6},{6,4},{8,10},{10,8},{12,14},{14,12},{1,3},{3,1},... | collective-permute-start | bytes 49160 | tf_op jit(solution)/shard_map/ppermute | solution.py:120
  54.0 12.6 %collective-permute-start.10 = (f32[4,4,32,128]{3,2,1,0:T(8,128)}, f32[4,4,32,128]{3,2,1,0:T(8,128)}, u32[]{:S(2)}, u32[]{:S(2)}) collective-permute-start(f32[4,4,32,128]{3,2,1,0:T(8,128)} %get-tuple-element.75), channel_id=1, source_target_pairs={{0,2},{2,0},{4,6},{6,4},{8,10},{10,8},{12,14},{14,12},{1,3},{3,1},... | collective-permute-start | bytes 786440 | tf_op jit(solution)/shard_map/ppermute | solution.py:160
  55.5 12.1 %collective-permute-start.11 = (f32[4,4,32,128]{3,2,1,0:T(8,128)}, f32[4,4,32,128]{3,2,1,0:T(8,128)}, u32[]{:S(2)}, u32[]{:S(2)}) collective-permute-start(f32[4,4,32,128]{3,2,1,0:T(8,128)} %bitcast.45), channel_id=1, source_target_pairs={{0,4},{2,6},{4,0},{6,2},{8,12},{10,14},{12,8},{14,10},{1,5},{3,7},... | collective-permute-start | bytes 786440 | tf_op jit(solution)/shard_map/ppermute | solution.py:160
  62.2 1.4 %collective-permute-start.12 = (f32[4,64,128]{2,1,0:T(8,128)S(1)}, f32[4,64,128]{2,1,0:T(8,128)S(1)}, u32[]{:S(2)}, u32[]{:S(2)}) collective-permute-start(f32[4,64,128]{2,1,0:T(8,128)S(1)} %constant_dynamic-slice_fusion.4), channel_id=1, source_target_pairs={{0,1},{1,0},{2,3},{3,2},{4,5},{5,4},{6,7},{7,6},{8,9},{9,8},{10,11... | collective-permute-start | bytes 393224 | tf_op jit(solution)/shard_map/ppermute | solution.py:52
  69.2 11.6 %collective-permute-start.13 = (f32[4,1,4,32,128]{4,3,2,0,1:T(8,128)S(1)}, f32[4,1,4,32,128]{4,3,2,0,1:T(8,128)S(1)}, u32[]{:S(2)}, u32[]{:S(2)}) collective-permute-start(f32[4,1,4,32,128]{4,3,2,0,1:T(8,128)S(1)} %dynamic-slice_bitcast_fusion.1), channel_id=1, source_target_pairs={{0,2},{2,0},{4,6},{6,4},{8,10},{10,8},{12,14},{14,12},{1,3},{3,1},... | collective-permute-start | bytes 786440 | tf_op jit(solution)/shard_map/ppermute | solution.py:186
  69.8 11.1 %collective-permute-start.14 = (f32[2,2,4,32,128]{4,3,2,1,0:T(8,128)S(1)}, f32[2,2,4,32,128]{4,3,2,1,0:T(8,128)S(1)}, u32[]{:S(2)}, u32[]{:S(2)}) collective-permute-start(f32[2,2,4,32,128]{4,3,2,1,0:T(8,128)S(1)} %dynamic-slice_bitcast_fusion), channel_id=1, source_target_pairs={{0,4},{2,6},{4,0},{6,2},{8,12},{10,14},{12,8},{14,10},{1,5},{3,7},... | collective-permute-start | bytes 786440 | tf_op jit(solution)/shard_map/ppermute | solution.py:186
  70.5 10.3 %collective-permute-start.15 = (f32[2,1,4,32,128]{4,3,2,0,1:T(8,128)S(1)}, f32[2,1,4,32,128]{4,3,2,0,1:T(8,128)S(1)}, u32[]{:S(2)}, u32[]{:S(2)}) collective-permute-start(f32[2,1,4,32,128]{4,3,2,0,1:T(8,128)S(1)} %dynamic-slice_bitcast_fusion.9), channel_id=1, source_target_pairs={{0,4},{2,6},{4,0},{6,2},{8,12},{10,14},{12,8},{14,10},{1,5},{3,7},... | collective-permute-start | bytes 393224 | tf_op jit(solution)/shard_map/ppermute | solution.py:186
  72.0 8.8 %collective-permute-start.16 = (f32[2,1,4,32,128]{4,3,2,0,1:T(8,128)S(1)}, f32[2,1,4,32,128]{4,3,2,0,1:T(8,128)S(1)}, u32[]{:S(2)}, u32[]{:S(2)}) collective-permute-start(f32[2,1,4,32,128]{4,3,2,0,1:T(8,128)S(1)} %dynamic-slice_bitcast_fusion.8), channel_id=1, source_target_pairs={{0,2},{2,0},{4,6},{6,4},{8,10},{10,8},{12,14},{14,12},{1,3},{3,1},... | collective-permute-start | bytes 393224 | tf_op jit(solution)/shard_map/ppermute | solution.py:186
  73.6 1.4 %collective-permute-start.17 = (f32[4,64,128]{2,1,0:T(8,128)S(1)}, f32[4,64,128]{2,1,0:T(8,128)S(1)}, u32[]{:S(2)}, u32[]{:S(2)}) collective-permute-start(f32[4,64,128]{2,1,0:T(8,128)S(1)} %constant_dynamic-slice_fusion.3), channel_id=1, source_target_pairs={{0,1},{1,0},{2,3},{3,2},{4,5},{5,4},{6,7},{7,6},{8,9},{9,8},{10,11... | collective-permute-start | bytes 393224 | tf_op jit(solution)/shard_map/ppermute | solution.py:52
  80.9 9.5 %collective-permute-start.18 = (f32[2,1,4,32,128]{4,3,2,0,1:T(8,128)S(1)}, f32[2,1,4,32,128]{4,3,2,0,1:T(8,128)S(1)}, u32[]{:S(2)}, u32[]{:S(2)}) collective-permute-start(f32[2,1,4,32,128]{4,3,2,0,1:T(8,128)S(1)} %dynamic-slice_bitcast_fusion.7), channel_id=1, source_target_pairs={{0,4},{2,6},{4,0},{6,2},{8,12},{10,14},{12,8},{14,10},{1,5},{3,7},... | collective-permute-start | bytes 393224 | tf_op jit(solution)/shard_map/ppermute | solution.py:186
  81.6 8.9 %collective-permute-start.19 = (f32[2,1,4,32,128]{4,3,2,0,1:T(8,128)S(1)}, f32[2,1,4,32,128]{4,3,2,0,1:T(8,128)S(1)}, u32[]{:S(2)}, u32[]{:S(2)}) collective-permute-start(f32[2,1,4,32,128]{4,3,2,0,1:T(8,128)S(1)} %dynamic-slice_bitcast_fusion.6), channel_id=1, source_target_pairs={{0,2},{2,0},{4,6},{6,4},{8,10},{10,8},{12,14},{14,12},{1,3},{3,1},... | collective-permute-start | bytes 393224 | tf_op jit(solution)/shard_map/ppermute | solution.py:186
  83.1 7.8 %collective-permute-start.20 = (f32[1,1,4,64,128]{4,3,2,1,0:T(8,128)S(1)}, f32[1,1,4,64,128]{4,3,2,1,0:T(8,128)S(1)}, u32[]{:S(2)}, u32[]{:S(2)}) collective-permute-start(f32[1,1,4,64,128]{4,3,2,1,0:T(8,128)S(1)} %dynamic-slice_bitcast_fusion.5), channel_id=1, source_target_pairs={{0,8},{2,10},{4,12},{6,14},{8,0},{10,2},{12,4},{14,6},{1,9},{3,11}... | collective-permute-start | bytes 393224 | tf_op jit(solution)/shard_map/ppermute | solution.py:186
  85.8 1.4 %collective-permute-start.21 = (f32[4,64,128]{2,1,0:T(8,128)S(1)}, f32[4,64,128]{2,1,0:T(8,128)S(1)}, u32[]{:S(2)}, u32[]{:S(2)}) collective-permute-start(f32[4,64,128]{2,1,0:T(8,128)S(1)} %constant_dynamic-slice_fusion.2), channel_id=1, source_target_pairs={{0,1},{1,0},{2,3},{3,2},{4,5},{5,4},{6,7},{7,6},{8,9},{9,8},{10,11... | collective-permute-start | bytes 393224 | tf_op jit(solution)/shard_map/ppermute | solution.py:52
  91.0 9.0 %collective-permute-start.22 = (f32[1,1,4,64,128]{4,3,2,1,0:T(8,128)S(1)}, f32[1,1,4,64,128]{4,3,2,1,0:T(8,128)S(1)}, u32[]{:S(2)}, u32[]{:S(2)}) collective-permute-start(f32[1,1,4,64,128]{4,3,2,1,0:T(8,128)S(1)} %dynamic-slice_bitcast_fusion.4), channel_id=1, source_target_pairs={{0,8},{2,10},{4,12},{6,14},{8,0},{10,2},{12,4},{14,6},{1,9},{3,11}... | collective-permute-start | bytes 393224 | tf_op jit(solution)/shard_map/ppermute | solution.py:186
  101.7 7.4 %collective-permute-start.23 = (f32[1,4,64,128]{3,2,1,0:T(8,128)S(1)}, f32[1,4,64,128]{3,2,1,0:T(8,128)S(1)}, u32[]{:S(2)}, u32[]{:S(2)}) collective-permute-start(f32[1,4,64,128]{3,2,1,0:T(8,128)S(1)} %fusion.1), channel_id=1, source_target_pairs={{0,8},{2,10},{4,12},{6,14},{8,0},{10,2},{12,4},{14,6},{1,9},{3,11}... | collective-permute-start | bytes 393224 | tf_op jit(solution)/shard_map/ppermute | solution.py:120
  109.2 5.5 %collective-permute-start.24 = (f32[2,4,32,128]{3,2,1,0:T(8,128)S(1)}, f32[2,4,32,128]{3,2,1,0:T(8,128)S(1)}, u32[]{:S(2)}, u32[]{:S(2)}) collective-permute-start(f32[2,4,32,128]{3,2,1,0:T(8,128)S(1)} %get-tuple-element.153), channel_id=1, source_target_pairs={{0,4},{2,6},{4,0},{6,2},{8,12},{10,14},{12,8},{14,10},{1,5},{3,7},... | collective-permute-start | bytes 393224 | tf_op jit(solution)/shard_map/ppermute | solution.py:120
  109.2 5.5 %collective-permute-start.25 = (f32[2,4,32,128]{3,2,1,0:T(8,128)S(1)}, f32[2,4,32,128]{3,2,1,0:T(8,128)S(1)}, u32[]{:S(2)}, u32[]{:S(2)}) collective-permute-start(f32[2,4,32,128]{3,2,1,0:T(8,128)S(1)} %get-tuple-element.152), channel_id=1, source_target_pairs={{0,2},{2,0},{4,6},{6,4},{8,10},{10,8},{12,14},{14,12},{1,3},{3,1},... | collective-permute-start | bytes 393224 | tf_op jit(solution)/shard_map/ppermute | solution.py:120
  114.8 7.4 %collective-permute-start.26 = (f32[4,4,32,128]{3,2,1,0:T(8,128)S(1)}, f32[4,4,32,128]{3,2,1,0:T(8,128)S(1)}, u32[]{:S(2)}, u32[]{:S(2)}) collective-permute-start(f32[4,4,32,128]{3,2,1,0:T(8,128)S(1)} %bitcast.240), channel_id=1, source_target_pairs={{0,2},{2,0},{4,6},{6,4},{8,10},{10,8},{12,14},{14,12},{1,3},{3,1},... | collective-permute-start | bytes 786440 | tf_op jit(solution)/shard_map/ppermute | solution.py:120
  115.6 7.1 %collective-permute-start.27 = (f32[4,4,32,128]{3,2,1,0:T(8,128)S(1)}, f32[4,4,32,128]{3,2,1,0:T(8,128)S(1)}, u32[]{:S(2)}, u32[]{:S(2)}) collective-permute-start(f32[4,4,32,128]{3,2,1,0:T(8,128)S(1)} %bitcast.242), channel_id=1, source_target_pairs={{0,4},{2,6},{4,0},{6,2},{8,12},{10,14},{12,8},{14,10},{1,5},{3,7},... | collective-permute-start | bytes 786440 | tf_op jit(solution)/shard_map/ppermute | solution.py:120
  124.9 1.6 %collective-permute-start.28 = (f32[4,64,128]{2,1,0:T(8,128)}, f32[4,64,128]{2,1,0:T(8,128)S(1)}, u32[]{:S(2)}, u32[]{:S(2)}) collective-permute-start(f32[4,64,128]{2,1,0:T(8,128)} %constant_dynamic-slice_fusion), channel_id=1, source_target_pairs={{0,1},{1,0},{2,3},{3,2},{4,5},{5,4},{6,7},{7,6},{8,9},{9,8},{10,11... | collective-permute-start | bytes 393224 | tf_op jit(solution)/shard_map/ppermute | solution.py:52
  131.5 1.9 %collective-permute-start.29 = (f32[1,2,256]{2,1,0:T(2,128)S(1)}, f32[1,2,256]{2,1,0:T(2,128)S(1)}, u32[]{:S(2)}, u32[]{:S(2)}) collective-permute-start(f32[1,2,256]{2,1,0:T(2,128)S(1)} %maximum_bitcast_fusion), channel_id=1, source_target_pairs={{0,1},{1,0},{2,3},{3,2},{4,5},{5,4},{6,7},{7,6},{8,9},{9,8},{10,11... | collective-permute-start | bytes 6152 | tf_op jit(solution)/shard_map/ppermute | solution.py:388
  (27 other events, 84.4 us)

commit v18 on v15

--- a/solution.py
+++ b/solution.py
@@ -307,14 +307,14 @@
 
     tasks = [task_wave(0), light_prep, wave_and_split]
     run_group([model_c, gains_c], tasks[0])
-    half_a, half_b = halves(model_c["held"], 1)
+    half_a, half_b = halves(model_c["held"], 2)
     model_a = chain(half_a, "ag", far_first[1:], [top])
     model_b = chain(half_b, "ag", swap_first(far_first[1:]), [top])
     for i in range(1, len(bits)):
         run_group([model_a, model_b, gains_c], tasks[i] if i < len(tasks) else nothing)
     for i in range(len(bits), len(tasks)):
         tasks[i]()
-    model_held = jnp.concatenate([model_a["held"], model_b["held"]], axis=1)
+    model_lo, model_hi = model_a["held"], model_b["held"]
     gains_held = gains_c["held"]
     light_a = chain(None, "pre", light_orders["la"], near_first)
     light_b = chain(None, "pre", light_orders["lb"], near_first)
@@ -322,7 +322,9 @@
     light_b["slices"] = lambda: (st["lb_keep"], st["lb_send"])
 
     def born_pass():
-        model = model_held.reshape(span_z, span_x * span_y).T.reshape(span_x, span_y, span_z)
+        model = jnp.concatenate(
+            [m.reshape(span_z, m.shape[2]).T for m in (model_lo, model_hi)], axis=0
+        ).reshape(span_x, span_y, span_z)
         st["born1"] = model * st["drive0"]
         st["born2"] = born_second(st["born1"], model, st["drive1"])
 

time: 130 us -> 130 us (level)
    transpose x1 -> x0, local copies, waits for them, and re-layouts: 1.55 us -> none  [born_pass(): model_held.reshape(span_z, span_x * span_y)]
    concatenate x0 -> x1, local copies, waits for them, and re-layouts: none -> 1.55 us  [born_pass(): jnp.concatenate([m.reshape(span_z, m.shape[2]).T for m in (model_lo, mode...]
where the time goes in v18:
time: 130 us; the launch traced here: 129 us
  waiting for transfers between devices  41.9 us (32%)
  other arithmetic  34.8 us (27%)
  starting transfers between devices  25.6 us (20%)
  local copies, waits for them, and re-layouts  20.7 us (16%)
  between operations  4.71 us (4%)
  matrix products  1.69 us (1%)
    ppermute x13, waiting for transfers between devices, ag_step(): theirs = lax.ppermute(held, 'shot', [(i, i ^ k) for i in range(n)])  20.8 us
    ppermute x8, waiting for transfers between devices, rs_step(): got = lax.ppermute(send, 'shot', [(i, i ^ k) for i in range(n)])  17.6 us
    ppermute x13, starting transfers between devices, ag_step(): theirs = lax.ppermute(held, 'shot', [(i, i ^ k) for i in range(n)])  13 us
    ppermute x8, starting transfers between devices, rs_step(): got = lax.ppermute(send, 'shot', [(i, i ^ k) for i in range(n)])  8.48 us
    add x3, other arithmetic, inject(): return field + jnp.where(hit, source_gain[0] * wavelet[0, moment], 0.0)  8.05 us
    add x2, other arithmetic, born_second(): 2.0 * born + speed_term * laplace_x(with_halo(born)) - absorber * born  5.83 us
    unnamed x55, local copies, waits for them, and re-layouts  5.27 us
    another operation x1, other arithmetic, damping(): lower = jnp.stack([edges[0], edges[2], edges[4]])[:, None]  3.74 us
  transfers between devices with their start and end apart: 30, of which 15 were waited for; matrix products, arithmetic and copies ran while one was open for 28% of the time, Pallas kernels for 0%

profile of v18, /device:TPU:0, one launch (start us, length us, event | category | flops | bytes accessed | tf_op | source)
XLA Modules:
  0.0 129.4 jit_solution(6104242003252866091)
XLA Ops:
  0.7 1.7 %dynamic-slice_bitcast_fusion.10 = f32[4,64,128]{2,1,0:T(8,128)} fusion(f32[1,32,64,128]{3,2,1,0:T(8,128)} %param.12, s32[]{:T(128)S(6)} %select_n.404), kind=kLoop, calls=%fused_computation.441 | loop fusion | bytes 262148 | tf_op jit(solution)/shard_map/dynamic_slice | solution.py:51
  2.8 1.0 copy.38
  4.6 3.6 %collective-permute-start = (f32[1,16,2048]{2,1,0:T(8,128)}, f32[1,16,2048]{2,1,0:T(8,128)}, u32[]{:S(2)}, u32[]{:S(2)}) collective-permute-start(f32[1,16,2048]{2,1,0:T(8,128)} %concatenate.199), channel_id=1, source_target_pairs={{0,8},{2,10},{4,12},{6,14},{8,0},{10,2},{12,4},{14,6},{1,9},{3,11}... | collective-permute-start | bytes 393224 | tf_op jit(solution)/shard_map/ppermute | solution.py:120
  10.2 3.7 %pad_maximum_fusion.15 = (f32[3]{0:T(128)S(1)}, f32[3]{0:T(128)S(1)}) fusion(f32[1]{0:T(128)} %get-tuple-element.167, f32[1]{0:T(128)} %get-tuple-element.168, f32[1]{0:T(128)} %get-tuple-element.163, f32[1]{0:T(128)} %get-tuple-element.164, f32[1]{0:T(128)} %get-tuple-element.165, f32[1]{0:T(128)} %get-tuple-element.166), kind=kLoop, calls=%fused_computation.500 | loop fusion | flops 12 | bytes 48 | tf_op jit(solution)/shard_map/stack | solution.py:37
  16.3 2.6 %fusion.144 = f32[24,64,128]{2,1,0:T(8,128)} fusion(f32[32,64,128]{2,1,0:T(8,128)S(1)} %bitcast.208, f32[1,32,64,128]{3,2,1,0:T(8,128)S(1)} %copy-done), kind=kLoop, calls=%fused_computation.324 | loop fusion | flops 5701632 | bytes 8912896 | tf_op jit(solution)/shard_map/add | solution.py:86
  28.2 1.1 maximum_select_fusion.4
  29.5 1.9 %collective-permute-start.5 = (f32[2,16,64]{2,1,0:T(8,128)S(1)}, f32[2,16,64]{2,1,0:T(8,128)S(1)}, u32[]{:S(2)}, u32[]{:S(2)}) collective-permute-start(f32[2,16,64]{2,1,0:T(8,128)S(1)} %maximum_select_fusion.12), channel_id=1, source_target_pairs={{0,4},{2,6},{4,0},{6,2},{8,12},{10,14},{12,8},{14,10},{1,5},{3,7},... | collective-permute-start | bytes 24584 | tf_op jit(solution)/shard_map/ppermute | solution.py:120
  31.5 1.6 %collective-permute-start.4 = (f32[2,16,1024]{2,1,0:T(8,128)S(1)}, f32[2,16,1024]{2,1,0:T(8,128)S(1)}, u32[]{:S(2)}, u32[]{:S(2)}) collective-permute-start(f32[2,16,1024]{2,1,0:T(8,128)S(1)} %get-tuple-element.156), channel_id=1, source_target_pairs={{0,2},{2,0},{4,6},{6,4},{8,10},{10,8},{12,14},{14,12},{1,3},{3,1},... | collective-permute-start | bytes 393224 | tf_op jit(solution)/shard_map/ppermute | solution.py:120
  33.7 2.9 %collective-permute-done.4 = f32[2,16,1024]{2,1,0:T(8,128)S(1)} collective-permute-done((f32[2,16,1024]{2,1,0:T(8,128)S(1)}, f32[2,16,1024]{2,1,0:T(8,128)S(1)}, u32[]{:S(2)}, u32[]{:S(2)}) %collective-permute-start.4) | collective-permute-done | bytes 131104 | tf_op jit(solution)/shard_map/ppermute | solution.py:120
  36.6 2.4 %collective-permute-done.3 = f32[2,16,1024]{2,1,0:T(8,128)S(1)} collective-permute-done((f32[2,16,1024]{2,1,0:T(8,128)S(1)}, f32[2,16,1024]{2,1,0:T(8,128)S(1)}, u32[]{:S(2)}, u32[]{:S(2)}) %collective-permute-start.3) | collective-permute-done | bytes 131104 | tf_op jit(solution)/shard_map/ppermute | solution.py:120
  39.1 3.2 %fusion.3 = (f32[32,64,128]{2,1,0:T(8,128)S(1)}, f32[32,64,128]{2,1,0:T(8,128)S(1)}) fusion(f32[32,64,128]{2,1,0:T(8,128)S(1)} %get-tuple-element.73, f32[32,64,128]{2,1,0:T(8,128)S(1)} %bitcast.210, f32[]{:T(128)S(6)} %mul.394, f32[128]{0:T(128)S(1)} %copy-done.16, f32[32,64]{1,0:T(8,128)S(1)} %broadcast_add_fusion, pred[128]{0:T(512)(128)(4,1)S(1)} %copy-done.19, ...), kind=kLoop, calls=%fused_computation.151 | loop fusion | flops 12058624 | bytes 16012292 | tf_op jit(solution)/shard_map/add | solution.py:230
  44.5 1.7 %collective-permute-start.7 = (f32[4,16,1024]{2,1,0:T(8,128)S(1)}, f32[4,16,1024]{2,1,0:T(8,128)S(1)}, u32[]{:S(2)}, u32[]{:S(2)}) collective-permute-start(f32[4,16,1024]{2,1,0:T(8,128)S(1)} %bitcast.236), channel_id=1, source_target_pairs={{0,2},{2,0},{4,6},{6,4},{8,10},{10,8},{12,14},{14,12},{1,3},{3,1},... | collective-permute-start | bytes 786440 | tf_op jit(solution)/shard_map/ppermute | solution.py:120
  48.6 4.0 %fusion.4 = (f32[32,64,128]{2,1,0:T(8,128)}, f32[32,64,128]{2,1,0:T(8,128)}) fusion(f32[32,64,128]{2,1,0:T(8,128)S(1)} %get-tuple-element.71, f32[32,64,128]{2,1,0:T(8,128)S(1)} %get-tuple-element.73, f32[]{:T(128)S(6)} %mul.403, f32[128]{0:T(128)S(1)} %copy-done.16, f32[32,64]{1,0:T(8,128)S(1)} %broadcast_add_fusion, pred[128]{0:T(512)(128)(4,1)S(1)} %copy-done.19, ...), kind=kLoop, calls=%fused_computation.152 | loop fusion | flops 12058624 | bytes 16012292 | tf_op jit(solution)/shard_map/add | solution.py:230
  53.2 1.1 pad_maximum_fusion.12
  54.2 1.5 %copy.48 = f32[2048,128]{1,0:T(8,128)S(1)} copy(f32[2048,128]{0,1:T(8,128)} %pad_maximum_fusion.12) | data formatting | bytes 2097152 | tf_op jit(solution)/shard_map/concatenate | solution.py:325
  56.7 1.3 collective-permute-start.12
  58.0 1.5 %collective-permute-start.11 = (f32[4,4,32,128]{3,2,1,0:T(8,128)S(1)}, f32[4,4,32,128]{3,2,1,0:T(8,128)S(1)}, u32[]{:S(2)}, u32[]{:S(2)}) collective-permute-start(f32[4,4,32,128]{3,2,1,0:T(8,128)S(1)} %copy-done.12), channel_id=1, source_target_pairs={{0,2},{2,0},{4,6},{6,4},{8,10},{10,8},{12,14},{14,12},{1,3},{3,1},... | collective-permute-start | bytes 786440 | tf_op jit(solution)/shard_map/ppermute | solution.py:160
  59.8 2.9 %fusion.67 = f32[32,64,128]{2,1,0:T(8,128)S(1)} fusion(f32[40,64,128]{2,1,0:T(8,128)S(1)} %constant_dynamic-update-slice_fusion.2, f32[32,64,128]{2,1,0:T(8,128)S(1)} %bitcast.214, f32[32,64,128]{2,1,0:T(8,128)S(1)} %copy-done.3, f32[32,64,128]{2,1,0:T(8,128)S(1)} %mul.404, f32[128]{0:T(128)S(1)} %copy-done.17, f32[32,64]{1,0:T(8,128)S(1)} %broadcast_add_fusion, ...), kind=kLoop, calls=%fused_computation.215 | loop fusion | flops 11272192 | bytes 16007680 | tf_op jit(solution)/shard_map/add | solution.py:251
  62.7 2.1 %collective-permute-done.12 = f32[4,4,32,128]{3,2,1,0:T(8,128)S(1)} collective-permute-done((f32[4,4,32,128]{3,2,1,0:T(8,128)S(1)}, f32[4,4,32,128]{3,2,1,0:T(8,128)S(1)}, u32[]{:S(2)}, u32[]{:S(2)}) %collective-permute-start.12) | collective-permute-done | bytes 262176 | tf_op jit(solution)/shard_map/ppermute | solution.py:160
  66.0 1.6 %collective-permute-start.17 = (f32[2,1,4,32,128]{4,3,2,0,1:T(8,128)S(1)}, f32[2,1,4,32,128]{4,3,2,0,1:T(8,128)S(1)}, u32[]{:S(2)}, u32[]{:S(2)}) collective-permute-start(f32[2,1,4,32,128]{4,3,2,0,1:T(8,128)S(1)} %dynamic-slice_bitcast_fusion.8), channel_id=1, source_target_pairs={{0,2},{2,0},{4,6},{6,4},{8,10},{10,8},{12,14},{14,12},{1,3},{3,1},... | collective-permute-start | bytes 393224 | tf_op jit(solution)/shard_map/ppermute | solution.py:186
  68.6 1.6 %collective-permute-start.15 = (f32[2,2,4,32,128]{4,3,2,1,0:T(8,128)S(1)}, f32[2,2,4,32,128]{4,3,2,1,0:T(8,128)S(1)}, u32[]{:S(2)}, u32[]{:S(2)}) collective-permute-start(f32[2,2,4,32,128]{4,3,2,1,0:T(8,128)S(1)} %dynamic-slice_bitcast_fusion), channel_id=1, source_target_pairs={{0,4},{2,6},{4,0},{6,2},{8,12},{10,14},{12,8},{14,10},{1,5},{3,7},... | collective-permute-start | bytes 786440 | tf_op jit(solution)/shard_map/ppermute | solution.py:186
  71.0 3.2 %fusion.92 = f32[32,64,128]{2,1,0:T(8,128)} fusion(f32[40,64,128]{2,1,0:T(8,128)S(1)} %constant_dynamic-update-slice_fusion.1, s32[32,64,128]{2,1,0:T(8,128)S(1)} %copy-done.1), kind=kLoop, calls=%fused_computation.240 | loop fusion | flops 9175040 | bytes 12845056 | tf_op jit(solution)/shard_map/mul | solution.py:243
  74.3 4.5 %collective-permute-done.15 = f32[2,2,4,32,128]{4,3,2,1,0:T(8,128)S(1)} collective-permute-done((f32[2,2,4,32,128]{4,3,2,1,0:T(8,128)S(1)}, f32[2,2,4,32,128]{4,3,2,1,0:T(8,128)S(1)}, u32[]{:S(2)}, u32[]{:S(2)}) %collective-permute-start.15) | collective-permute-done | bytes 262176 | tf_op jit(solution)/shard_map/ppermute | solution.py:186
  79.6 2.7 %collective-permute-start.21 = (f32[1,1,4,64,128]{4,3,2,1,0:T(8,128)S(1)}, f32[1,1,4,64,128]{4,3,2,1,0:T(8,128)S(1)}, u32[]{:S(2)}, u32[]{:S(2)}) collective-permute-start(f32[1,1,4,64,128]{4,3,2,1,0:T(8,128)S(1)} %dynamic-slice_bitcast_fusion.5), channel_id=1, source_target_pairs={{0,8},{2,10},{4,12},{6,14},{8,0},{10,2},{12,4},{14,6},{1,9},{3,11}... | collective-permute-start | bytes 393224 | tf_op jit(solution)/shard_map/ppermute | solution.py:186
  84.0 5.0 %collective-permute-done.19 = f32[2,1,4,32,128]{4,3,2,0,1:T(8,128)S(1)} collective-permute-done((f32[2,1,4,32,128]{4,3,2,0,1:T(8,128)S(1)}, f32[2,1,4,32,128]{4,3,2,0,1:T(8,128)S(1)}, u32[]{:S(2)}, u32[]{:S(2)}) %collective-permute-start.19) | collective-permute-done | bytes 131104 | tf_op jit(solution)/shard_map/ppermute | solution.py:186
  89.4 7.2 %collective-permute-done.22 = f32[1,1,4,64,128]{4,3,2,1,0:T(8,128)S(1)} collective-permute-done((f32[1,1,4,64,128]{4,3,2,1,0:T(8,128)S(1)}, f32[1,1,4,64,128]{4,3,2,1,0:T(8,128)S(1)}, u32[]{:S(2)}, u32[]{:S(2)}) %collective-permute-start.22) | collective-permute-done | bytes 131104 | tf_op jit(solution)/shard_map/ppermute | solution.py:186
  98.4 7.0 %collective-permute-done.23 = f32[1,4,64,128]{3,2,1,0:T(8,128)S(1)} collective-permute-done((f32[1,4,64,128]{3,2,1,0:T(8,128)S(1)}, f32[1,4,64,128]{3,2,1,0:T(8,128)S(1)}, u32[]{:S(2)}, u32[]{:S(2)}) %collective-permute-start.23) | collective-permute-done | bytes 131104 | tf_op jit(solution)/shard_map/ppermute | solution.py:120
  106.5 4.0 %collective-permute-done.25 = f32[2,4,32,128]{3,2,1,0:T(8,128)S(1)} collective-permute-done((f32[2,4,32,128]{3,2,1,0:T(8,128)S(1)}, f32[2,4,32,128]{3,2,1,0:T(8,128)S(1)}, u32[]{:S(2)}, u32[]{:S(2)}) %collective-permute-start.25) | collective-permute-done | bytes 131104 | tf_op jit(solution)/shard_map/ppermute | solution.py:120
  111.1 2.2 %collective-permute-start.26 = (f32[4,4,32,128]{3,2,1,0:T(8,128)S(1)}, f32[4,4,32,128]{3,2,1,0:T(8,128)S(1)}, u32[]{:S(2)}, u32[]{:S(2)}) collective-permute-start(f32[4,4,32,128]{3,2,1,0:T(8,128)S(1)} %bitcast.244), channel_id=1, source_target_pairs={{0,2},{2,0},{4,6},{6,4},{8,10},{10,8},{12,14},{14,12},{1,3},{3,1},... | collective-permute-start | bytes 786440 | tf_op jit(solution)/shard_map/ppermute | solution.py:120
  114.5 3.5 %collective-permute-done.26 = f32[4,4,32,128]{3,2,1,0:T(8,128)S(1)} collective-permute-done((f32[4,4,32,128]{3,2,1,0:T(8,128)S(1)}, f32[4,4,32,128]{3,2,1,0:T(8,128)S(1)}, u32[]{:S(2)}, u32[]{:S(2)}) %collective-permute-start.26) | collective-permute-done | bytes 262176 | tf_op jit(solution)/shard_map/ppermute | solution.py:120
  118.2 1.1 copy-done.4
  122.6 2.9 %fusion.120 = f32[32,64,128]{2,1,0:T(8,128)S(1)} fusion(f32[40,64,128]{2,1,0:T(8,128)S(1)} %constant_dynamic-update-slice_fusion, f32[32,64,128]{2,1,0:T(8,128)S(1)} %copy-done.7, f32[128]{0:T(128)S(1)} %copy-done.18, f32[32,64]{1,0:T(8,128)S(1)} %broadcast_add_fusion, f32[8,4,64,128]{3,2,1,0:T(8,128)S(1)} %pad_maximum_fusion.13, ...), kind=kLoop, calls=%fused_computation.268 | loop fusion | flops 11534336 | bytes 16007680 | tf_op jit(solution)/shard_map/add | solution.py:251
  (201 shorter events, 36.2 us)
Async XLA Ops:
  0.6 15.7 %copy-start = (f32[1,32,64,128]{3,2,1,0:T(8,128)S(1)}, f32[1,32,64,128]{3,2,1,0:T(8,128)}, u32[]{:S(2)}) copy-start(f32[1,32,64,128]{3,2,1,0:T(8,128)} %param.12) | copy-start | bytes 3145732
  0.7 15.1 %copy-start.20 = (f32[1,4]{1,0:T(1,128)S(1)}, f32[1,4]{1,0:T(1,128)}, u32[]{:S(2)}) copy-start(f32[1,4]{1,0:T(1,128)} %param.16) | copy-start | bytes 52
  2.3 22.5 %collective-permute-start.2 = (f32[4,64,128]{2,1,0:T(8,128)}, f32[4,64,128]{2,1,0:T(8,128)}, u32[]{:S(2)}, u32[]{:S(2)}) collective-permute-start(f32[4,64,128]{2,1,0:T(8,128)} %dynamic-slice_bitcast_fusion.10), channel_id=1, source_target_pairs={{0,1},{1,0},{2,3},{3,2},{4,5},{5,4},{6,7},{7,6},{8,9},{9,8},{10,11... | collective-permute-start | bytes 393224 | tf_op jit(solution)/shard_map/ppermute | solution.py:52
  4.6 23.6 %collective-permute-start = (f32[1,16,2048]{2,1,0:T(8,128)}, f32[1,16,2048]{2,1,0:T(8,128)}, u32[]{:S(2)}, u32[]{:S(2)}) collective-permute-start(f32[1,16,2048]{2,1,0:T(8,128)} %concatenate.199), channel_id=1, source_target_pairs={{0,8},{2,10},{4,12},{6,14},{8,0},{10,2},{12,4},{14,6},{1,9},{3,11}... | collective-permute-start | bytes 393224 | tf_op jit(solution)/shard_map/ppermute | solution.py:120
  8.2 15.8 %collective-permute-start.1 = (f32[1,16,64]{2,1,0:T(8,128)}, f32[1,16,64]{2,1,0:T(8,128)}, u32[]{:S(2)}, u32[]{:S(2)}) collective-permute-start(f32[1,16,64]{2,1,0:T(8,128)} %bitcast.264), channel_id=1, source_target_pairs={{0,8},{2,10},{4,12},{6,14},{8,0},{10,2},{12,4},{14,6},{1,9},{3,11}... | collective-permute-start | bytes 12296 | tf_op jit(solution)/shard_map/ppermute | solution.py:120
  29.5 4.2 %collective-permute-start.5 = (f32[2,16,64]{2,1,0:T(8,128)S(1)}, f32[2,16,64]{2,1,0:T(8,128)S(1)}, u32[]{:S(2)}, u32[]{:S(2)}) collective-permute-start(f32[2,16,64]{2,1,0:T(8,128)S(1)} %maximum_select_fusion.12), channel_id=1, source_target_pairs={{0,4},{2,6},{4,0},{6,2},{8,12},{10,14},{12,8},{14,10},{1,5},{3,7},... | collective-permute-start | bytes 24584 | tf_op jit(solution)/shard_map/ppermute | solution.py:120
  31.5 5.1 %collective-permute-start.4 = (f32[2,16,1024]{2,1,0:T(8,128)S(1)}, f32[2,16,1024]{2,1,0:T(8,128)S(1)}, u32[]{:S(2)}, u32[]{:S(2)}) collective-permute-start(f32[2,16,1024]{2,1,0:T(8,128)S(1)} %get-tuple-element.156), channel_id=1, source_target_pairs={{0,2},{2,0},{4,6},{6,4},{8,10},{10,8},{12,14},{14,12},{1,3},{3,1},... | collective-permute-start | bytes 393224 | tf_op jit(solution)/shard_map/ppermute | solution.py:120
  33.1 6.0 %collective-permute-start.6 = (f32[4,64,128]{2,1,0:T(8,128)S(1)}, f32[4,64,128]{2,1,0:T(8,128)S(1)}, u32[]{:S(2)}, u32[]{:S(2)}) collective-permute-start(f32[4,64,128]{2,1,0:T(8,128)S(1)} %constant_dynamic-slice_fusion.7), channel_id=1, source_target_pairs={{0,1},{1,0},{2,3},{3,2},{4,5},{5,4},{6,7},{7,6},{8,9},{9,8},{10,11... | collective-permute-start | bytes 393224 | tf_op jit(solution)/shard_map/ppermute | solution.py:52
  33.1 5.9 %collective-permute-start.3 = (f32[2,16,1024]{2,1,0:T(8,128)S(1)}, f32[2,16,1024]{2,1,0:T(8,128)S(1)}, u32[]{:S(2)}, u32[]{:S(2)}) collective-permute-start(f32[2,16,1024]{2,1,0:T(8,128)S(1)} %get-tuple-element.157), channel_id=1, source_target_pairs={{0,4},{2,6},{4,0},{6,2},{8,12},{10,14},{12,8},{14,10},{1,5},{3,7},... | collective-permute-start | bytes 393224 | tf_op jit(solution)/shard_map/ppermute | solution.py:120
  43.6 5.0 %collective-permute-start.10 = (f32[4,64,128]{2,1,0:T(8,128)S(1)}, f32[4,64,128]{2,1,0:T(8,128)S(1)}, u32[]{:S(2)}, u32[]{:S(2)}) collective-permute-start(f32[4,64,128]{2,1,0:T(8,128)S(1)} %constant_dynamic-slice_fusion.6), channel_id=1, source_target_pairs={{0,1},{1,0},{2,3},{3,2},{4,5},{5,4},{6,7},{7,6},{8,9},{9,8},{10,11... | collective-permute-start | bytes 393224 | tf_op jit(solution)/shard_map/ppermute | solution.py:52
  43.6 4.3 %collective-permute-start.9 = (f32[4,16,64]{2,1,0:T(8,128)S(1)}, f32[4,16,64]{2,1,0:T(8,128)S(1)}, u32[]{:S(2)}, u32[]{:S(2)}) collective-permute-start(f32[4,16,64]{2,1,0:T(8,128)S(1)} %bitcast.257), channel_id=1, source_target_pairs={{0,2},{2,0},{4,6},{6,4},{8,10},{10,8},{12,14},{14,12},{1,3},{3,1},... | collective-permute-start | bytes 49160 | tf_op jit(solution)/shard_map/ppermute | solution.py:120
  44.2 8.4 %collective-permute-start.8 = (f32[4,16,1024]{2,1,0:T(8,128)S(1)}, f32[4,16,1024]{2,1,0:T(8,128)S(1)}, u32[]{:S(2)}, u32[]{:S(2)}) collective-permute-start(f32[4,16,1024]{2,1,0:T(8,128)S(1)} %bitcast.234), channel_id=1, source_target_pairs={{0,4},{2,6},{4,0},{6,2},{8,12},{10,14},{12,8},{14,10},{1,5},{3,7},... | collective-permute-start | bytes 786440 | tf_op jit(solution)/shard_map/ppermute | solution.py:120
  44.5 8.6 %collective-permute-start.7 = (f32[4,16,1024]{2,1,0:T(8,128)S(1)}, f32[4,16,1024]{2,1,0:T(8,128)S(1)}, u32[]{:S(2)}, u32[]{:S(2)}) collective-permute-start(f32[4,16,1024]{2,1,0:T(8,128)S(1)} %bitcast.236), channel_id=1, source_target_pairs={{0,2},{2,0},{4,6},{6,4},{8,10},{10,8},{12,14},{14,12},{1,3},{3,1},... | collective-permute-start | bytes 786440 | tf_op jit(solution)/shard_map/ppermute | solution.py:120
  56.0 3.7 %collective-permute-start.13 = (f32[4,64,128]{2,1,0:T(8,128)S(1)}, f32[4,64,128]{2,1,0:T(8,128)S(1)}, u32[]{:S(2)}, u32[]{:S(2)}) collective-permute-start(f32[4,64,128]{2,1,0:T(8,128)S(1)} %constant_dynamic-slice_fusion.3), channel_id=1, source_target_pairs={{0,1},{1,0},{2,3},{3,2},{4,5},{5,4},{6,7},{7,6},{8,9},{9,8},{10,11... | collective-permute-start | bytes 393224 | tf_op jit(solution)/shard_map/ppermute | solution.py:52
  56.7 8.0 %collective-permute-start.12 = (f32[4,4,32,128]{3,2,1,0:T(8,128)S(1)}, f32[4,4,32,128]{3,2,1,0:T(8,128)S(1)}, u32[]{:S(2)}, u32[]{:S(2)}) collective-permute-start(f32[4,4,32,128]{3,2,1,0:T(8,128)S(1)} %bitcast.246), channel_id=1, source_target_pairs={{0,4},{2,6},{4,0},{6,2},{8,12},{10,14},{12,8},{14,10},{1,5},{3,7},... | collective-permute-start | bytes 786440 | tf_op jit(solution)/shard_map/ppermute | solution.py:160
  58.0 7.8 %collective-permute-start.11 = (f32[4,4,32,128]{3,2,1,0:T(8,128)S(1)}, f32[4,4,32,128]{3,2,1,0:T(8,128)S(1)}, u32[]{:S(2)}, u32[]{:S(2)}) collective-permute-start(f32[4,4,32,128]{3,2,1,0:T(8,128)S(1)} %copy-done.12), channel_id=1, source_target_pairs={{0,2},{2,0},{4,6},{6,4},{8,10},{10,8},{12,14},{14,12},{1,3},{3,1},... | collective-permute-start | bytes 786440 | tf_op jit(solution)/shard_map/ppermute | solution.py:160
  65.9 5.1 %collective-permute-start.18 = (f32[4,64,128]{2,1,0:T(8,128)S(1)}, f32[4,64,128]{2,1,0:T(8,128)S(1)}, u32[]{:S(2)}, u32[]{:S(2)}) collective-permute-start(f32[4,64,128]{2,1,0:T(8,128)S(1)} %constant_dynamic-slice_fusion.2), channel_id=1, source_target_pairs={{0,1},{1,0},{2,3},{3,2},{4,5},{5,4},{6,7},{7,6},{8,9},{9,8},{10,11... | collective-permute-start | bytes 393224 | tf_op jit(solution)/shard_map/ppermute | solution.py:52
  66.0 8.3 %collective-permute-start.17 = (f32[2,1,4,32,128]{4,3,2,0,1:T(8,128)S(1)}, f32[2,1,4,32,128]{4,3,2,0,1:T(8,128)S(1)}, u32[]{:S(2)}, u32[]{:S(2)}) collective-permute-start(f32[2,1,4,32,128]{4,3,2,0,1:T(8,128)S(1)} %dynamic-slice_bitcast_fusion.8), channel_id=1, source_target_pairs={{0,2},{2,0},{4,6},{6,4},{8,10},{10,8},{12,14},{14,12},{1,3},{3,1},... | collective-permute-start | bytes 393224 | tf_op jit(solution)/shard_map/ppermute | solution.py:186
  67.6 6.7 %collective-permute-start.16 = (f32[2,1,4,32,128]{4,3,2,0,1:T(8,128)S(1)}, f32[2,1,4,32,128]{4,3,2,0,1:T(8,128)S(1)}, u32[]{:S(2)}, u32[]{:S(2)}) collective-permute-start(f32[2,1,4,32,128]{4,3,2,0,1:T(8,128)S(1)} %dynamic-slice_bitcast_fusion.9), channel_id=1, source_target_pairs={{0,4},{2,6},{4,0},{6,2},{8,12},{10,14},{12,8},{14,10},{1,5},{3,7},... | collective-permute-start | bytes 393224 | tf_op jit(solution)/shard_map/ppermute | solution.py:186
  68.6 10.2 %collective-permute-start.15 = (f32[2,2,4,32,128]{4,3,2,1,0:T(8,128)S(1)}, f32[2,2,4,32,128]{4,3,2,1,0:T(8,128)S(1)}, u32[]{:S(2)}, u32[]{:S(2)}) collective-permute-start(f32[2,2,4,32,128]{4,3,2,1,0:T(8,128)S(1)} %dynamic-slice_bitcast_fusion), channel_id=1, source_target_pairs={{0,4},{2,6},{4,0},{6,2},{8,12},{10,14},{12,8},{14,10},{1,5},{3,7},... | collective-permute-start | bytes 786440 | tf_op jit(solution)/shard_map/ppermute | solution.py:186
  70.3 8.6 %collective-permute-start.14 = (f32[4,1,4,32,128]{4,3,2,0,1:T(8,128)S(1)}, f32[4,1,4,32,128]{4,3,2,0,1:T(8,128)S(1)}, u32[]{:S(2)}, u32[]{:S(2)}) collective-permute-start(f32[4,1,4,32,128]{4,3,2,0,1:T(8,128)S(1)} %dynamic-slice_bitcast_fusion.1), channel_id=1, source_target_pairs={{0,2},{2,0},{4,6},{6,4},{8,10},{10,8},{12,14},{14,12},{1,3},{3,1},... | collective-permute-start | bytes 786440 | tf_op jit(solution)/shard_map/ppermute | solution.py:186
  79.0 5.0 %collective-permute-start.20 = (f32[2,1,4,32,128]{4,3,2,0,1:T(8,128)S(1)}, f32[2,1,4,32,128]{4,3,2,0,1:T(8,128)S(1)}, u32[]{:S(2)}, u32[]{:S(2)}) collective-permute-start(f32[2,1,4,32,128]{4,3,2,0,1:T(8,128)S(1)} %dynamic-slice_bitcast_fusion.6), channel_id=1, source_target_pairs={{0,2},{2,0},{4,6},{6,4},{8,10},{10,8},{12,14},{14,12},{1,3},{3,1},... | collective-permute-start | bytes 393224 | tf_op jit(solution)/shard_map/ppermute | solution.py:186
  79.6 9.5 %collective-permute-start.21 = (f32[1,1,4,64,128]{4,3,2,1,0:T(8,128)S(1)}, f32[1,1,4,64,128]{4,3,2,1,0:T(8,128)S(1)}, u32[]{:S(2)}, u32[]{:S(2)}) collective-permute-start(f32[1,1,4,64,128]{4,3,2,1,0:T(8,128)S(1)} %dynamic-slice_bitcast_fusion.5), channel_id=1, source_target_pairs={{0,8},{2,10},{4,12},{6,14},{8,0},{10,2},{12,4},{14,6},{1,9},{3,11}... | collective-permute-start | bytes 393224 | tf_op jit(solution)/shard_map/ppermute | solution.py:186
  82.3 6.8 %collective-permute-start.19 = (f32[2,1,4,32,128]{4,3,2,0,1:T(8,128)S(1)}, f32[2,1,4,32,128]{4,3,2,0,1:T(8,128)S(1)}, u32[]{:S(2)}, u32[]{:S(2)}) collective-permute-start(f32[2,1,4,32,128]{4,3,2,0,1:T(8,128)S(1)} %dynamic-slice_bitcast_fusion.7), channel_id=1, source_target_pairs={{0,4},{2,6},{4,0},{6,2},{8,12},{10,14},{12,8},{14,10},{1,5},{3,7},... | collective-permute-start | bytes 393224 | tf_op jit(solution)/shard_map/ppermute | solution.py:186
  89.2 7.3 %collective-permute-start.22 = (f32[1,1,4,64,128]{4,3,2,1,0:T(8,128)S(1)}, f32[1,1,4,64,128]{4,3,2,1,0:T(8,128)S(1)}, u32[]{:S(2)}, u32[]{:S(2)}) collective-permute-start(f32[1,1,4,64,128]{4,3,2,1,0:T(8,128)S(1)} %dynamic-slice_bitcast_fusion.4), channel_id=1, source_target_pairs={{0,8},{2,10},{4,12},{6,14},{8,0},{10,2},{12,4},{14,6},{1,9},{3,11}... | collective-permute-start | bytes 393224 | tf_op jit(solution)/shard_map/ppermute | solution.py:186
  98.3 7.2 %collective-permute-start.23 = (f32[1,4,64,128]{3,2,1,0:T(8,128)S(1)}, f32[1,4,64,128]{3,2,1,0:T(8,128)S(1)}, u32[]{:S(2)}, u32[]{:S(2)}) collective-permute-start(f32[1,4,64,128]{3,2,1,0:T(8,128)S(1)} %fusion.1), channel_id=1, source_target_pairs={{0,8},{2,10},{4,12},{6,14},{8,0},{10,2},{12,4},{14,6},{1,9},{3,11}... | collective-permute-start | bytes 393224 | tf_op jit(solution)/shard_map/ppermute | solution.py:120
  105.5 5.0 %collective-permute-start.25 = (f32[2,4,32,128]{3,2,1,0:T(8,128)S(1)}, f32[2,4,32,128]{3,2,1,0:T(8,128)S(1)}, u32[]{:S(2)}, u32[]{:S(2)}) collective-permute-start(f32[2,4,32,128]{3,2,1,0:T(8,128)S(1)} %get-tuple-element.152), channel_id=1, source_target_pairs={{0,2},{2,0},{4,6},{6,4},{8,10},{10,8},{12,14},{14,12},{1,3},{3,1},... | collective-permute-start | bytes 393224 | tf_op jit(solution)/shard_map/ppermute | solution.py:120
  106.0 5.0 %collective-permute-start.24 = (f32[2,4,32,128]{3,2,1,0:T(8,128)S(1)}, f32[2,4,32,128]{3,2,1,0:T(8,128)S(1)}, u32[]{:S(2)}, u32[]{:S(2)}) collective-permute-start(f32[2,4,32,128]{3,2,1,0:T(8,128)S(1)} %get-tuple-element.153), channel_id=1, source_target_pairs={{0,4},{2,6},{4,0},{6,2},{8,12},{10,14},{12,8},{14,10},{1,5},{3,7},... | collective-permute-start | bytes 393224 | tf_op jit(solution)/shard_map/ppermute | solution.py:120
  111.0 7.1 %collective-permute-start.27 = (f32[4,4,32,128]{3,2,1,0:T(8,128)S(1)}, f32[4,4,32,128]{3,2,1,0:T(8,128)S(1)}, u32[]{:S(2)}, u32[]{:S(2)}) collective-permute-start(f32[4,4,32,128]{3,2,1,0:T(8,128)S(1)} %bitcast.238), channel_id=1, source_target_pairs={{0,4},{2,6},{4,0},{6,2},{8,12},{10,14},{12,8},{14,10},{1,5},{3,7},... | collective-permute-start | bytes 786440 | tf_op jit(solution)/shard_map/ppermute | solution.py:120
  111.1 6.9 %collective-permute-start.26 = (f32[4,4,32,128]{3,2,1,0:T(8,128)S(1)}, f32[4,4,32,128]{3,2,1,0:T(8,128)S(1)}, u32[]{:S(2)}, u32[]{:S(2)}) collective-permute-start(f32[4,4,32,128]{3,2,1,0:T(8,128)S(1)} %bitcast.244), channel_id=1, source_target_pairs={{0,2},{2,0},{4,6},{6,4},{8,10},{10,8},{12,14},{14,12},{1,3},{3,1},... | collective-permute-start | bytes 786440 | tf_op jit(solution)/shard_map/ppermute | solution.py:120
  120.2 1.6 %collective-permute-start.28 = (f32[4,64,128]{2,1,0:T(8,128)}, f32[4,64,128]{2,1,0:T(8,128)S(1)}, u32[]{:S(2)}, u32[]{:S(2)}) collective-permute-start(f32[4,64,128]{2,1,0:T(8,128)} %constant_dynamic-slice_fusion), channel_id=1, source_target_pairs={{0,1},{1,0},{2,3},{3,2},{4,5},{5,4},{6,7},{7,6},{8,9},{9,8},{10,11... | collective-permute-start | bytes 393224 | tf_op jit(solution)/shard_map/ppermute | solution.py:52
  126.9 1.9 %collective-permute-start.29 = (f32[1,2,256]{2,1,0:T(2,128)S(1)}, f32[1,2,256]{2,1,0:T(2,128)S(1)}, u32[]{:S(2)}, u32[]{:S(2)}) collective-permute-start(f32[1,2,256]{2,1,0:T(2,128)S(1)} %maximum_bitcast_fusion), channel_id=1, source_target_pairs={{0,1},{1,0},{2,3},{3,2},{4,5},{5,4},{6,7},{7,6},{8,9},{9,8},{10,11... | collective-permute-start | bytes 6152 | tf_op jit(solution)/shard_map/ppermute | solution.py:391
  (24 other events, 78.0 us)

commit v19 on v15

--- a/solution.py
+++ b/solution.py
@@ -121,8 +121,10 @@
     low = 2 ** sum(1 for b in done if b < k)
     shape = (held.shape[0] // low, 1, low) + held.shape[1:]
     mine, other = held.reshape(shape), theirs.reshape(shape)
-    first = (me // k) % 2 == 0
-    pair = jnp.where(first, jnp.concatenate([mine, other], axis=1), jnp.concatenate([other, mine], axis=1))
+    at = (me // k) % 2
+    pair = jnp.zeros((shape[0], 2) + shape[2:], held.dtype)
+    pair = lax.dynamic_update_slice_in_dim(pair, mine, at, axis=1)
+    pair = lax.dynamic_update_slice_in_dim(pair, other, 1 - at, axis=1)
     return pair.reshape((2 * held.shape[0],) + held.shape[1:])
 
 

time: 130 us -> 137 us (1.054)
  local copies, waits for them, and re-layouts: 20.7 us -> 30.1 us
  waiting for transfers between devices: 41.9 us -> 38.3 us
    dynamic_update_slice x0 -> x26, local copies, waits for them, and re-layouts: none -> 7.89 us  [the longest x13 4.86 us: ag_step(): pair = lax.dynamic_update_slice_in_dim(pair, mine, at, axis=1)]
    ppermute x8, waiting for transfers between devices: 17.6 us -> 15.2 us  [rs_step(): got = lax.ppermute(send, 'shot', [(i, i ^ k) for i in range(n)])]
    select_n x13 -> x0, other arithmetic: 2.21 us -> none  [ag_step(): jnp.where(first, jnp.concatenate([mine, other], axis=1), jnp.concatenate(...]
    reshape x0 -> x4, local copies, waits for them, and re-layouts: none -> 2.11 us  [ag_step(): return pair.reshape((2 * held.shape[0],) + held.shape[1:])]
    ppermute x13, waiting for transfers between devices: 20.8 us -> 19.2 us  [ag_step(): theirs = lax.ppermute(held, 'shot', [(i, i ^ k) for i in range(n)])]
    unnamed x55 -> x61, local copies, waits for them, and re-layouts: 5.27 us -> 4.94 us
  transfers between devices with their start and end apart: 30 -> 30, of which waited for: 15 -> 14; matrix products, arithmetic and copies ran while one was open for 28% -> 36% of each run, Pallas kernels for 0% -> 0%
where the time goes in v19:
time: 137 us; the launch traced here: 136 us
  waiting for transfers between devices  38.3 us (28%)
  other arithmetic  34.6 us (25%)
  local copies, waits for them, and re-layouts  30.1 us (22%)
  starting transfers between devices  26.6 us (19%)
  between operations  4.94 us (4%)
  matrix products  1.71 us (1%)
    ppermute x13, waiting for transfers between devices, ag_step(): theirs = lax.ppermute(held, 'shot', [(i, i ^ k) for i in range(n)])  19.2 us
    ppermute x8, waiting for transfers between devices, rs_step(): got = lax.ppermute(send, 'shot', [(i, i ^ k) for i in range(n)])  15.2 us
    ppermute x13, starting transfers between devices, ag_step(): theirs = lax.ppermute(held, 'shot', [(i, i ^ k) for i in range(n)])  13.3 us
    ppermute x8, starting transfers between devices, rs_step(): got = lax.ppermute(send, 'shot', [(i, i ^ k) for i in range(n)])  9.84 us
    add x3, other arithmetic, inject(): return field + jnp.where(hit, source_gain[0] * wavelet[0, moment], 0.0)  8.03 us
    add x2, other arithmetic, born_second(): 2.0 * born + speed_term * laplace_x(with_halo(born)) - absorber * born  5.83 us
    unnamed x61, local copies, waits for them, and re-layouts  4.94 us
    dynamic_update_slice x13, local copies, waits for them, and re-layouts, ag_step(): pair = lax.dynamic_update_slice_in_dim(pair, mine, at, axis=1)  4.86 us
  transfers between devices with their start and end apart: 30, of which 14 were waited for; matrix products, arithmetic and copies ran while one was open for 36% of the time, Pallas kernels for 0%

profile of v19, /device:TPU:0, one launch (start us, length us, event | category | flops | bytes accessed | tf_op | source)
XLA Modules:
  0.0 136.2 jit_solution(11766178085560770762)
XLA Ops:
  0.7 1.7 %dynamic-slice_bitcast_fusion.10 = f32[4,64,128]{2,1,0:T(8,128)} fusion(f32[1,32,64,128]{3,2,1,0:T(8,128)} %param.12, s32[]{:T(128)S(6)} %select_n.255), kind=kLoop, calls=%fused_computation.443 | loop fusion | bytes 262148 | tf_op jit(solution)/shard_map/dynamic_slice | solution.py:51
  2.8 3.6 %collective-permute-start.1 = (f32[1,16,64]{2,1,0:T(8,128)}, f32[1,16,64]{2,1,0:T(8,128)}, u32[]{:S(2)}, u32[]{:S(2)}) collective-permute-start(f32[1,16,64]{2,1,0:T(8,128)} %bitcast.294), channel_id=1, source_target_pairs={{0,8},{2,10},{4,12},{6,14},{8,0},{10,2},{12,4},{14,6},{1,9},{3,11}... | collective-permute-start | bytes 12296 | tf_op jit(solution)/shard_map/ppermute | solution.py:120
  10.2 4.0 %pad_maximum_fusion.15 = (f32[3]{0:T(128)S(1)}, f32[3]{0:T(128)S(1)}) fusion(f32[1]{0:T(128)} %get-tuple-element.163, f32[1]{0:T(128)} %get-tuple-element.164, f32[1]{0:T(128)} %get-tuple-element.159, f32[1]{0:T(128)} %get-tuple-element.160, f32[1]{0:T(128)} %get-tuple-element.161, f32[1]{0:T(128)} %get-tuple-element.162), kind=kLoop, calls=%fused_computation.513 | loop fusion | flops 12 | bytes 48 | tf_op jit(solution)/shard_map/stack | solution.py:37
  17.1 2.6 %fusion.144 = f32[24,64,128]{2,1,0:T(8,128)} fusion(f32[32,64,128]{2,1,0:T(8,128)S(1)} %bitcast.246, f32[1,32,64,128]{3,2,1,0:T(8,128)S(1)} %copy-done), kind=kLoop, calls=%fused_computation.324 | loop fusion | flops 5701632 | bytes 8912896 | tf_op jit(solution)/shard_map/add | solution.py:86
  21.7 1.6 %constant_dynamic-update-slice_fusion.15 = f32[2,16,2048]{2,1,0:T(8,128)} fusion(f32[2,16,2048]{2,1,0:T(8,128)} %reshape.373, f32[1,16,2048]{2,1,0:T(8,128)} %reshape.374, s32[]{:T(128)S(6)} %select_n.253), kind=kLoop, calls=%fused_computation.490 | loop fusion | bytes 262148 | tf_op jit(solution)/shard_map/dynamic_update_slice | solution.py:126
  23.9 1.3 broadcast_and_fusion
  29.7 1.3 constant_dynamic-update-slice_fusion.12
  34.4 1.6 %constant_dynamic-update-slice_fusion.14 = f32[2,16,2048]{2,1,0:T(8,128)} fusion(f32[2,16,2048]{2,1,0:T(8,128)} %constant_dynamic-update-slice_fusion.15, f32[1,16,2048]{2,1,0:T(8,128)} %collective-permute-done, s32[]{:T(128)S(6)} %select_n.254), kind=kLoop, calls=%fused_computation.489 | loop fusion | bytes 262148 | tf_op jit(solution)/shard_map/dynamic_update_slice | solution.py:127
  36.3 1.8 %collective-permute-start.5 = (f32[2,16,64]{2,1,0:T(8,128)}, f32[2,16,64]{2,1,0:T(8,128)S(1)}, u32[]{:S(2)}, u32[]{:S(2)}) collective-permute-start(f32[2,16,64]{2,1,0:T(8,128)} %constant_dynamic-update-slice_fusion.12), channel_id=1, source_target_pairs={{0,4},{2,6},{4,0},{6,2},{8,12},{10,14},{12,8},{14,10},{1,5},{3,7},... | collective-permute-start | bytes 24584 | tf_op jit(solution)/shard_map/ppermute | solution.py:120
  39.0 1.6 %collective-permute-start.4 = (f32[2,8,2048]{2,1,0:T(8,128)S(1)}, f32[2,8,2048]{2,1,0:T(8,128)S(1)}, u32[]{:S(2)}, u32[]{:S(2)}) collective-permute-start(f32[2,8,2048]{2,1,0:T(8,128)S(1)} %get-tuple-element.152), channel_id=1, source_target_pairs={{0,2},{2,0},{4,6},{6,4},{8,10},{10,8},{12,14},{14,12},{1,3},{3,1},... | collective-permute-start | bytes 393224 | tf_op jit(solution)/shard_map/ppermute | solution.py:120
  43.9 3.2 %fusion.3 = (f32[32,64,128]{2,1,0:T(8,128)S(1)}, f32[32,64,128]{2,1,0:T(8,128)S(1)}) fusion(f32[32,64,128]{2,1,0:T(8,128)S(1)} %get-tuple-element.73, f32[32,64,128]{2,1,0:T(8,128)S(1)} %bitcast.248, f32[]{:T(128)S(6)} %mul.394, f32[128]{0:T(128)S(1)} %copy-done.17, f32[32,64]{1,0:T(8,128)S(1)} %broadcast_add_fusion, pred[128]{0:T(512)(128)(4,1)S(1)} %copy-done.22, ...), kind=kLoop, calls=%fused_computation.151 | loop fusion | flops 12058624 | bytes 16012292 | tf_op jit(solution)/shard_map/add | solution.py:232
  49.6 1.8 %collective-permute-start.8 = (f32[4,8,2048]{2,1,0:T(8,128)S(1)}, f32[4,8,2048]{2,1,0:T(8,128)S(1)}, u32[]{:S(2)}, u32[]{:S(2)}) collective-permute-start(f32[4,8,2048]{2,1,0:T(8,128)S(1)} %bitcast.273), channel_id=1, source_target_pairs={{0,4},{2,6},{4,0},{6,2},{8,12},{10,14},{12,8},{14,10},{1,5},{3,7},... | collective-permute-start | bytes 786440 | tf_op jit(solution)/shard_map/ppermute | solution.py:120
  51.4 1.5 %collective-permute-start.7 = (f32[4,8,2048]{2,1,0:T(8,128)S(1)}, f32[4,8,2048]{2,1,0:T(8,128)S(1)}, u32[]{:S(2)}, u32[]{:S(2)}) collective-permute-start(f32[4,8,2048]{2,1,0:T(8,128)S(1)} %bitcast.277), channel_id=1, source_target_pairs={{0,2},{2,0},{4,6},{6,4},{8,10},{10,8},{12,14},{14,12},{1,3},{3,1},... | collective-permute-start | bytes 786440 | tf_op jit(solution)/shard_map/ppermute | solution.py:120
  54.0 4.0 %fusion.4 = (f32[32,64,128]{2,1,0:T(8,128)}, f32[32,64,128]{2,1,0:T(8,128)}) fusion(f32[32,64,128]{2,1,0:T(8,128)S(1)} %get-tuple-element.71, f32[32,64,128]{2,1,0:T(8,128)S(1)} %get-tuple-element.73, f32[]{:T(128)S(6)} %mul.403, f32[128]{0:T(128)S(1)} %copy-done.17, f32[32,64]{1,0:T(8,128)S(1)} %broadcast_add_fusion, pred[128]{0:T(512)(128)(4,1)S(1)} %copy-done.22, ...), kind=kLoop, calls=%fused_computation.152 | loop fusion | flops 12058624 | bytes 16012292 | tf_op jit(solution)/shard_map/add | solution.py:232
  58.1 1.4 %collective-permute-done.7 = f32[4,8,2048]{2,1,0:T(8,128)S(1)} collective-permute-done((f32[4,8,2048]{2,1,0:T(8,128)S(1)}, f32[4,8,2048]{2,1,0:T(8,128)S(1)}, u32[]{:S(2)}, u32[]{:S(2)}) %collective-permute-start.7) | collective-permute-done | bytes 262176 | tf_op jit(solution)/shard_map/ppermute | solution.py:120
  60.6 1.5 %copy.72 = f32[2048,128]{1,0:T(8,128)S(1)} copy(f32[2048,128]{0,1:T(8,128)} %bitcast.257) | data formatting | bytes 2097152 | tf_op jit(solution)/shard_map/transpose | solution.py:327
  63.9 1.3 collective-permute-start.11
  65.4 2.9 %fusion.67 = f32[32,64,128]{2,1,0:T(8,128)S(1)} fusion(f32[40,64,128]{2,1,0:T(8,128)S(1)} %constant_dynamic-update-slice_fusion.6, f32[32,64,128]{2,1,0:T(8,128)S(1)} %bitcast.252, f32[32,64,128]{2,1,0:T(8,128)S(1)} %copy-done.3, f32[32,64,128]{2,1,0:T(8,128)S(1)} %mul.404, f32[128]{0:T(128)S(1)} %copy-done.18, f32[32,64]{1,0:T(8,128)S(1)} %broadcast_add_fusion, ...), kind=kLoop, calls=%fused_computation.215 | loop fusion | flops 11272192 | bytes 16007680 | tf_op jit(solution)/shard_map/add | solution.py:253
  68.3 2.9 %collective-permute-done.12 = f32[4,4,32,128]{3,2,1,0:T(8,128)S(1)} collective-permute-done((f32[4,4,32,128]{3,2,1,0:T(8,128)S(1)}, f32[4,4,32,128]{3,2,1,0:T(8,128)S(1)}, u32[]{:S(2)}, u32[]{:S(2)}) %collective-permute-start.12) | collective-permute-done | bytes 262176 | tf_op jit(solution)/shard_map/ppermute | solution.py:162
  71.8 1.3 collective-permute-start.17
  73.2 1.6 %collective-permute-start.16 = (f32[2,1,4,32,128]{4,3,2,0,1:T(8,128)S(1)}, f32[2,1,4,32,128]{4,3,2,0,1:T(8,128)S(1)}, u32[]{:S(2)}, u32[]{:S(2)}) collective-permute-start(f32[2,1,4,32,128]{4,3,2,0,1:T(8,128)S(1)} %dynamic-slice_bitcast_fusion.9), channel_id=1, source_target_pairs={{0,4},{2,6},{4,0},{6,2},{8,12},{10,14},{12,8},{14,10},{1,5},{3,7},... | collective-permute-start | bytes 393224 | tf_op jit(solution)/shard_map/ppermute | solution.py:188
  76.9 3.2 %fusion.92 = f32[32,64,128]{2,1,0:T(8,128)} fusion(f32[40,64,128]{2,1,0:T(8,128)S(1)} %constant_dynamic-update-slice_fusion.5, s32[32,64,128]{2,1,0:T(8,128)S(1)} %copy-done.1), kind=kLoop, calls=%fused_computation.240 | loop fusion | flops 9175040 | bytes 12845056 | tf_op jit(solution)/shard_map/mul | solution.py:245
  80.2 4.2 %collective-permute-done.15 = f32[2,2,4,32,128]{4,3,2,1,0:T(8,128)S(1)} collective-permute-done((f32[2,2,4,32,128]{4,3,2,1,0:T(8,128)S(1)}, f32[2,2,4,32,128]{4,3,2,1,0:T(8,128)S(1)}, u32[]{:S(2)}, u32[]{:S(2)}) %collective-permute-start.15) | collective-permute-done | bytes 262176 | tf_op jit(solution)/shard_map/ppermute | solution.py:188
  84.6 2.7 %collective-permute-start.21 = (f32[1,1,4,64,128]{4,3,2,1,0:T(8,128)S(1)}, f32[1,1,4,64,128]{4,3,2,1,0:T(8,128)S(1)}, u32[]{:S(2)}, u32[]{:S(2)}) collective-permute-start(f32[1,1,4,64,128]{4,3,2,1,0:T(8,128)S(1)} %dynamic-slice_bitcast_fusion.5), channel_id=1, source_target_pairs={{0,8},{2,10},{4,12},{6,14},{8,0},{10,2},{12,4},{14,6},{1,9},{3,11}... | collective-permute-start | bytes 393224 | tf_op jit(solution)/shard_map/ppermute | solution.py:188
  88.2 1.3 collective-permute-start.19
  89.5 3.7 %collective-permute-done.21 = f32[1,1,4,64,128]{4,3,2,1,0:T(8,128)S(1)} collective-permute-done((f32[1,1,4,64,128]{4,3,2,1,0:T(8,128)S(1)}, f32[1,1,4,64,128]{4,3,2,1,0:T(8,128)S(1)}, u32[]{:S(2)}, u32[]{:S(2)}) %collective-permute-start.21) | collective-permute-done | bytes 131104 | tf_op jit(solution)/shard_map/ppermute | solution.py:188
  95.6 6.3 %collective-permute-done.22 = f32[1,1,4,64,128]{4,3,2,1,0:T(8,128)S(1)} collective-permute-done((f32[1,1,4,64,128]{4,3,2,1,0:T(8,128)S(1)}, f32[1,1,4,64,128]{4,3,2,1,0:T(8,128)S(1)}, u32[]{:S(2)}, u32[]{:S(2)}) %collective-permute-start.22) | collective-permute-done | bytes 131104 | tf_op jit(solution)/shard_map/ppermute | solution.py:188
  105.0 6.5 %collective-permute-done.23 = f32[1,4,64,128]{3,2,1,0:T(8,128)S(1)} collective-permute-done((f32[1,4,64,128]{3,2,1,0:T(8,128)S(1)}, f32[1,4,64,128]{3,2,1,0:T(8,128)S(1)}, u32[]{:S(2)}, u32[]{:S(2)}) %collective-permute-start.23) | collective-permute-done | bytes 131104 | tf_op jit(solution)/shard_map/ppermute | solution.py:120
  111.6 1.2 collective-permute-start.25
  112.9 3.7 %collective-permute-done.25 = f32[2,4,32,128]{3,2,1,0:T(8,128)S(1)} collective-permute-done((f32[2,4,32,128]{3,2,1,0:T(8,128)S(1)}, f32[2,4,32,128]{3,2,1,0:T(8,128)S(1)}, u32[]{:S(2)}, u32[]{:S(2)}) %collective-permute-start.25) | collective-permute-done | bytes 131104 | tf_op jit(solution)/shard_map/ppermute | solution.py:120
  119.0 5.9 %collective-permute-done.27 = f32[4,4,32,128]{3,2,1,0:T(8,128)S(1)} collective-permute-done((f32[4,4,32,128]{3,2,1,0:T(8,128)S(1)}, f32[4,4,32,128]{3,2,1,0:T(8,128)S(1)}, u32[]{:S(2)}, u32[]{:S(2)}) %collective-permute-start.27) | collective-permute-done | bytes 262176 | tf_op jit(solution)/shard_map/ppermute | solution.py:120
  129.4 2.9 %fusion.120 = f32[32,64,128]{2,1,0:T(8,128)S(1)} fusion(f32[40,64,128]{2,1,0:T(8,128)S(1)} %constant_dynamic-update-slice_fusion, f32[32,64,128]{2,1,0:T(8,128)S(1)} %copy-done.7, f32[128]{0:T(128)S(1)} %copy-done.19, f32[32,64]{1,0:T(8,128)S(1)} %broadcast_add_fusion, f32[8,4,64,128]{3,2,1,0:T(8,128)S(1)} %pad_maximum_fusion.13, ...), kind=kLoop, calls=%fused_computation.268 | loop fusion | flops 11534336 | bytes 16007680 | tf_op jit(solution)/shard_map/add | solution.py:253
  (225 shorter events, 45.1 us)
Async XLA Ops:
  0.6 16.5 %copy-start = (f32[1,32,64,128]{3,2,1,0:T(8,128)S(1)}, f32[1,32,64,128]{3,2,1,0:T(8,128)}, u32[]{:S(2)}) copy-start(f32[1,32,64,128]{3,2,1,0:T(8,128)} %param.12) | copy-start | bytes 3145732
  0.7 15.3 %copy-start.23 = (f32[1,4]{1,0:T(1,128)S(1)}, f32[1,4]{1,0:T(1,128)}, u32[]{:S(2)}) copy-start(f32[1,4]{1,0:T(1,128)} %param.16) | copy-start | bytes 52
  2.3 28.7 %collective-permute-start.2 = (f32[4,64,128]{2,1,0:T(8,128)}, f32[4,64,128]{2,1,0:T(8,128)}, u32[]{:S(2)}, u32[]{:S(2)}) collective-permute-start(f32[4,64,128]{2,1,0:T(8,128)} %dynamic-slice_bitcast_fusion.10), channel_id=1, source_target_pairs={{0,1},{1,0},{2,3},{3,2},{4,5},{5,4},{6,7},{7,6},{8,9},{9,8},{10,11... | collective-permute-start | bytes 393224 | tf_op jit(solution)/shard_map/ppermute | solution.py:52
  2.8 26.9 %collective-permute-start.1 = (f32[1,16,64]{2,1,0:T(8,128)}, f32[1,16,64]{2,1,0:T(8,128)}, u32[]{:S(2)}, u32[]{:S(2)}) collective-permute-start(f32[1,16,64]{2,1,0:T(8,128)} %bitcast.294), channel_id=1, source_target_pairs={{0,8},{2,10},{4,12},{6,14},{8,0},{10,2},{12,4},{14,6},{1,9},{3,11}... | collective-permute-start | bytes 12296 | tf_op jit(solution)/shard_map/ppermute | solution.py:120
  8.2 26.2 %collective-permute-start = (f32[1,16,2048]{2,1,0:T(8,128)}, f32[1,16,2048]{2,1,0:T(8,128)}, u32[]{:S(2)}, u32[]{:S(2)}) collective-permute-start(f32[1,16,2048]{2,1,0:T(8,128)} %reshape.374), channel_id=1, source_target_pairs={{0,8},{2,10},{4,12},{6,14},{8,0},{10,2},{12,4},{14,6},{1,9},{3,11}... | collective-permute-start | bytes 393224 | tf_op jit(solution)/shard_map/ppermute | solution.py:120
  36.0 7.9 %collective-permute-start.6 = (f32[4,64,128]{2,1,0:T(8,128)S(1)}, f32[4,64,128]{2,1,0:T(8,128)S(1)}, u32[]{:S(2)}, u32[]{:S(2)}) collective-permute-start(f32[4,64,128]{2,1,0:T(8,128)S(1)} %constant_dynamic-slice_fusion.7), channel_id=1, source_target_pairs={{0,1},{1,0},{2,3},{3,2},{4,5},{5,4},{6,7},{7,6},{8,9},{9,8},{10,11... | collective-permute-start | bytes 393224 | tf_op jit(solution)/shard_map/ppermute | solution.py:52
  36.3 7.6 %collective-permute-start.5 = (f32[2,16,64]{2,1,0:T(8,128)}, f32[2,16,64]{2,1,0:T(8,128)S(1)}, u32[]{:S(2)}, u32[]{:S(2)}) collective-permute-start(f32[2,16,64]{2,1,0:T(8,128)} %constant_dynamic-update-slice_fusion.12), channel_id=1, source_target_pairs={{0,4},{2,6},{4,0},{6,2},{8,12},{10,14},{12,8},{14,10},{1,5},{3,7},... | collective-permute-start | bytes 24584 | tf_op jit(solution)/shard_map/ppermute | solution.py:120
  39.0 9.0 %collective-permute-start.4 = (f32[2,8,2048]{2,1,0:T(8,128)S(1)}, f32[2,8,2048]{2,1,0:T(8,128)S(1)}, u32[]{:S(2)}, u32[]{:S(2)}) collective-permute-start(f32[2,8,2048]{2,1,0:T(8,128)S(1)} %get-tuple-element.152), channel_id=1, source_target_pairs={{0,2},{2,0},{4,6},{6,4},{8,10},{10,8},{12,14},{14,12},{1,3},{3,1},... | collective-permute-start | bytes 393224 | tf_op jit(solution)/shard_map/ppermute | solution.py:120
  40.6 6.5 %collective-permute-start.3 = (f32[2,8,2048]{2,1,0:T(8,128)S(1)}, f32[2,8,2048]{2,1,0:T(8,128)S(1)}, u32[]{:S(2)}, u32[]{:S(2)}) collective-permute-start(f32[2,8,2048]{2,1,0:T(8,128)S(1)} %get-tuple-element.153), channel_id=1, source_target_pairs={{0,4},{2,6},{4,0},{6,2},{8,12},{10,14},{12,8},{14,10},{1,5},{3,7},... | collective-permute-start | bytes 393224 | tf_op jit(solution)/shard_map/ppermute | solution.py:120
  48.3 5.7 %collective-permute-start.10 = (f32[4,64,128]{2,1,0:T(8,128)S(1)}, f32[4,64,128]{2,1,0:T(8,128)S(1)}, u32[]{:S(2)}, u32[]{:S(2)}) collective-permute-start(f32[4,64,128]{2,1,0:T(8,128)S(1)} %constant_dynamic-slice_fusion.6), channel_id=1, source_target_pairs={{0,1},{1,0},{2,3},{3,2},{4,5},{5,4},{6,7},{7,6},{8,9},{9,8},{10,11... | collective-permute-start | bytes 393224 | tf_op jit(solution)/shard_map/ppermute | solution.py:52
  49.2 4.7 %collective-permute-start.9 = (f32[4,16,64]{2,1,0:T(8,128)S(1)}, f32[4,16,64]{2,1,0:T(8,128)S(1)}, u32[]{:S(2)}, u32[]{:S(2)}) collective-permute-start(f32[4,16,64]{2,1,0:T(8,128)S(1)} %bitcast.290), channel_id=1, source_target_pairs={{0,2},{2,0},{4,6},{6,4},{8,10},{10,8},{12,14},{14,12},{1,3},{3,1},... | collective-permute-start | bytes 49160 | tf_op jit(solution)/shard_map/ppermute | solution.py:120
  49.6 8.5 %collective-permute-start.8 = (f32[4,8,2048]{2,1,0:T(8,128)S(1)}, f32[4,8,2048]{2,1,0:T(8,128)S(1)}, u32[]{:S(2)}, u32[]{:S(2)}) collective-permute-start(f32[4,8,2048]{2,1,0:T(8,128)S(1)} %bitcast.273), channel_id=1, source_target_pairs={{0,4},{2,6},{4,0},{6,2},{8,12},{10,14},{12,8},{14,10},{1,5},{3,7},... | collective-permute-start | bytes 786440 | tf_op jit(solution)/shard_map/ppermute | solution.py:120
  51.4 8.1 %collective-permute-start.7 = (f32[4,8,2048]{2,1,0:T(8,128)S(1)}, f32[4,8,2048]{2,1,0:T(8,128)S(1)}, u32[]{:S(2)}, u32[]{:S(2)}) collective-permute-start(f32[4,8,2048]{2,1,0:T(8,128)S(1)} %bitcast.277), channel_id=1, source_target_pairs={{0,2},{2,0},{4,6},{6,4},{8,10},{10,8},{12,14},{14,12},{1,3},{3,1},... | collective-permute-start | bytes 786440 | tf_op jit(solution)/shard_map/ppermute | solution.py:120
  62.4 2.9 %collective-permute-start.13 = (f32[4,64,128]{2,1,0:T(8,128)S(1)}, f32[4,64,128]{2,1,0:T(8,128)S(1)}, u32[]{:S(2)}, u32[]{:S(2)}) collective-permute-start(f32[4,64,128]{2,1,0:T(8,128)S(1)} %constant_dynamic-slice_fusion.3), channel_id=1, source_target_pairs={{0,1},{1,0},{2,3},{3,2},{4,5},{5,4},{6,7},{7,6},{8,9},{9,8},{10,11... | collective-permute-start | bytes 393224 | tf_op jit(solution)/shard_map/ppermute | solution.py:52
  63.2 8.0 %collective-permute-start.12 = (f32[4,4,32,128]{3,2,1,0:T(8,128)S(1)}, f32[4,4,32,128]{3,2,1,0:T(8,128)S(1)}, u32[]{:S(2)}, u32[]{:S(2)}) collective-permute-start(f32[4,4,32,128]{3,2,1,0:T(8,128)S(1)} %bitcast.285), channel_id=1, source_target_pairs={{0,4},{2,6},{4,0},{6,2},{8,12},{10,14},{12,8},{14,10},{1,5},{3,7},... | collective-permute-start | bytes 786440 | tf_op jit(solution)/shard_map/ppermute | solution.py:162
  63.9 7.8 %collective-permute-start.11 = (f32[4,4,32,128]{3,2,1,0:T(8,128)S(1)}, f32[4,4,32,128]{3,2,1,0:T(8,128)S(1)}, u32[]{:S(2)}, u32[]{:S(2)}) collective-permute-start(f32[4,4,32,128]{3,2,1,0:T(8,128)S(1)} %copy-done.13), channel_id=1, source_target_pairs={{0,2},{2,0},{4,6},{6,4},{8,10},{10,8},{12,14},{14,12},{1,3},{3,1},... | collective-permute-start | bytes 786440 | tf_op jit(solution)/shard_map/ppermute | solution.py:162
  71.7 5.1 %collective-permute-start.18 = (f32[4,64,128]{2,1,0:T(8,128)S(1)}, f32[4,64,128]{2,1,0:T(8,128)S(1)}, u32[]{:S(2)}, u32[]{:S(2)}) collective-permute-start(f32[4,64,128]{2,1,0:T(8,128)S(1)} %constant_dynamic-slice_fusion.2), channel_id=1, source_target_pairs={{0,1},{1,0},{2,3},{3,2},{4,5},{5,4},{6,7},{7,6},{8,9},{9,8},{10,11... | collective-permute-start | bytes 393224 | tf_op jit(solution)/shard_map/ppermute | solution.py:52
  71.8 8.3 %collective-permute-start.17 = (f32[2,1,4,32,128]{4,3,2,0,1:T(8,128)S(1)}, f32[2,1,4,32,128]{4,3,2,0,1:T(8,128)S(1)}, u32[]{:S(2)}, u32[]{:S(2)}) collective-permute-start(f32[2,1,4,32,128]{4,3,2,0,1:T(8,128)S(1)} %dynamic-slice_bitcast_fusion.8), channel_id=1, source_target_pairs={{0,2},{2,0},{4,6},{6,4},{8,10},{10,8},{12,14},{14,12},{1,3},{3,1},... | collective-permute-start | bytes 393224 | tf_op jit(solution)/shard_map/ppermute | solution.py:188
  73.2 7.0 %collective-permute-start.16 = (f32[2,1,4,32,128]{4,3,2,0,1:T(8,128)S(1)}, f32[2,1,4,32,128]{4,3,2,0,1:T(8,128)S(1)}, u32[]{:S(2)}, u32[]{:S(2)}) collective-permute-start(f32[2,1,4,32,128]{4,3,2,0,1:T(8,128)S(1)} %dynamic-slice_bitcast_fusion.9), channel_id=1, source_target_pairs={{0,4},{2,6},{4,0},{6,2},{8,12},{10,14},{12,8},{14,10},{1,5},{3,7},... | collective-permute-start | bytes 393224 | tf_op jit(solution)/shard_map/ppermute | solution.py:188
  75.4 9.1 %collective-permute-start.15 = (f32[2,2,4,32,128]{4,3,2,1,0:T(8,128)S(1)}, f32[2,2,4,32,128]{4,3,2,1,0:T(8,128)S(1)}, u32[]{:S(2)}, u32[]{:S(2)}) collective-permute-start(f32[2,2,4,32,128]{4,3,2,1,0:T(8,128)S(1)} %dynamic-slice_bitcast_fusion), channel_id=1, source_target_pairs={{0,4},{2,6},{4,0},{6,2},{8,12},{10,14},{12,8},{14,10},{1,5},{3,7},... | collective-permute-start | bytes 786440 | tf_op jit(solution)/shard_map/ppermute | solution.py:188
  75.9 8.6 %collective-permute-start.14 = (f32[4,1,4,32,128]{4,3,2,0,1:T(8,128)S(1)}, f32[4,1,4,32,128]{4,3,2,0,1:T(8,128)S(1)}, u32[]{:S(2)}, u32[]{:S(2)}) collective-permute-start(f32[4,1,4,32,128]{4,3,2,0,1:T(8,128)S(1)} %dynamic-slice_bitcast_fusion.1), channel_id=1, source_target_pairs={{0,2},{2,0},{4,6},{6,4},{8,10},{10,8},{12,14},{14,12},{1,3},{3,1},... | collective-permute-start | bytes 786440 | tf_op jit(solution)/shard_map/ppermute | solution.py:188
  84.6 8.6 %collective-permute-start.21 = (f32[1,1,4,64,128]{4,3,2,1,0:T(8,128)S(1)}, f32[1,1,4,64,128]{4,3,2,1,0:T(8,128)S(1)}, u32[]{:S(2)}, u32[]{:S(2)}) collective-permute-start(f32[1,1,4,64,128]{4,3,2,1,0:T(8,128)S(1)} %dynamic-slice_bitcast_fusion.5), channel_id=1, source_target_pairs={{0,8},{2,10},{4,12},{6,14},{8,0},{10,2},{12,4},{14,6},{1,9},{3,11}... | collective-permute-start | bytes 393224 | tf_op jit(solution)/shard_map/ppermute | solution.py:188
  87.3 5.9 %collective-permute-start.20 = (f32[2,1,4,32,128]{4,3,2,0,1:T(8,128)S(1)}, f32[2,1,4,32,128]{4,3,2,0,1:T(8,128)S(1)}, u32[]{:S(2)}, u32[]{:S(2)}) collective-permute-start(f32[2,1,4,32,128]{4,3,2,0,1:T(8,128)S(1)} %dynamic-slice_bitcast_fusion.6), channel_id=1, source_target_pairs={{0,2},{2,0},{4,6},{6,4},{8,10},{10,8},{12,14},{14,12},{1,3},{3,1},... | collective-permute-start | bytes 393224 | tf_op jit(solution)/shard_map/ppermute | solution.py:188
  88.2 6.0 %collective-permute-start.19 = (f32[2,1,4,32,128]{4,3,2,0,1:T(8,128)S(1)}, f32[2,1,4,32,128]{4,3,2,0,1:T(8,128)S(1)}, u32[]{:S(2)}, u32[]{:S(2)}) collective-permute-start(f32[2,1,4,32,128]{4,3,2,0,1:T(8,128)S(1)} %dynamic-slice_bitcast_fusion.7), channel_id=1, source_target_pairs={{0,4},{2,6},{4,0},{6,2},{8,12},{10,14},{12,8},{14,10},{1,5},{3,7},... | collective-permute-start | bytes 393224 | tf_op jit(solution)/shard_map/ppermute | solution.py:188
  94.3 7.7 %collective-permute-start.22 = (f32[1,1,4,64,128]{4,3,2,1,0:T(8,128)S(1)}, f32[1,1,4,64,128]{4,3,2,1,0:T(8,128)S(1)}, u32[]{:S(2)}, u32[]{:S(2)}) collective-permute-start(f32[1,1,4,64,128]{4,3,2,1,0:T(8,128)S(1)} %dynamic-slice_bitcast_fusion.4), channel_id=1, source_target_pairs={{0,8},{2,10},{4,12},{6,14},{8,0},{10,2},{12,4},{14,6},{1,9},{3,11}... | collective-permute-start | bytes 393224 | tf_op jit(solution)/shard_map/ppermute | solution.py:188
  103.8 7.7 %collective-permute-start.23 = (f32[1,4,64,128]{3,2,1,0:T(8,128)S(1)}, f32[1,4,64,128]{3,2,1,0:T(8,128)S(1)}, u32[]{:S(2)}, u32[]{:S(2)}) collective-permute-start(f32[1,4,64,128]{3,2,1,0:T(8,128)S(1)} %get-tuple-element.166), channel_id=1, source_target_pairs={{0,8},{2,10},{4,12},{6,14},{8,0},{10,2},{12,4},{14,6},{1,9},{3,11}... | collective-permute-start | bytes 393224 | tf_op jit(solution)/shard_map/ppermute | solution.py:120
  111.6 5.0 %collective-permute-start.25 = (f32[2,4,32,128]{3,2,1,0:T(8,128)S(1)}, f32[2,4,32,128]{3,2,1,0:T(8,128)S(1)}, u32[]{:S(2)}, u32[]{:S(2)}) collective-permute-start(f32[2,4,32,128]{3,2,1,0:T(8,128)S(1)} %get-tuple-element.150), channel_id=1, source_target_pairs={{0,2},{2,0},{4,6},{6,4},{8,10},{10,8},{12,14},{14,12},{1,3},{3,1},... | collective-permute-start | bytes 393224 | tf_op jit(solution)/shard_map/ppermute | solution.py:120
  112.8 5.0 %collective-permute-start.24 = (f32[2,4,32,128]{3,2,1,0:T(8,128)S(1)}, f32[2,4,32,128]{3,2,1,0:T(8,128)S(1)}, u32[]{:S(2)}, u32[]{:S(2)}) collective-permute-start(f32[2,4,32,128]{3,2,1,0:T(8,128)S(1)} %get-tuple-element.151), channel_id=1, source_target_pairs={{0,4},{2,6},{4,0},{6,2},{8,12},{10,14},{12,8},{14,10},{1,5},{3,7},... | collective-permute-start | bytes 393224 | tf_op jit(solution)/shard_map/ppermute | solution.py:120
  117.9 7.0 %collective-permute-start.27 = (f32[4,4,32,128]{3,2,1,0:T(8,128)S(1)}, f32[4,4,32,128]{3,2,1,0:T(8,128)S(1)}, u32[]{:S(2)}, u32[]{:S(2)}) collective-permute-start(f32[4,4,32,128]{3,2,1,0:T(8,128)S(1)} %bitcast.279), channel_id=1, source_target_pairs={{0,4},{2,6},{4,0},{6,2},{8,12},{10,14},{12,8},{14,10},{1,5},{3,7},... | collective-permute-start | bytes 786440 | tf_op jit(solution)/shard_map/ppermute | solution.py:120
  118.2 7.0 %collective-permute-start.26 = (f32[4,4,32,128]{3,2,1,0:T(8,128)S(1)}, f32[4,4,32,128]{3,2,1,0:T(8,128)S(1)}, u32[]{:S(2)}, u32[]{:S(2)}) collective-permute-start(f32[4,4,32,128]{3,2,1,0:T(8,128)S(1)} %bitcast.275), channel_id=1, source_target_pairs={{0,2},{2,0},{4,6},{6,4},{8,10},{10,8},{12,14},{14,12},{1,3},{3,1},... | collective-permute-start | bytes 786440 | tf_op jit(solution)/shard_map/ppermute | solution.py:120
  127.0 1.6 %collective-permute-start.28 = (f32[4,64,128]{2,1,0:T(8,128)}, f32[4,64,128]{2,1,0:T(8,128)S(1)}, u32[]{:S(2)}, u32[]{:S(2)}) collective-permute-start(f32[4,64,128]{2,1,0:T(8,128)} %constant_dynamic-slice_fusion), channel_id=1, source_target_pairs={{0,1},{1,0},{2,3},{3,2},{4,5},{5,4},{6,7},{7,6},{8,9},{9,8},{10,11... | collective-permute-start | bytes 393224 | tf_op jit(solution)/shard_map/ppermute | solution.py:52
  133.6 1.9 %collective-permute-start.29 = (f32[1,2,256]{2,1,0:T(2,128)S(1)}, f32[1,2,256]{2,1,0:T(2,128)S(1)}, u32[]{:S(2)}, u32[]{:S(2)}) collective-permute-start(f32[1,2,256]{2,1,0:T(2,128)S(1)} %maximum_bitcast_fusion), channel_id=1, source_target_pairs={{0,1},{1,0},{2,3},{3,2},{4,5},{5,4},{6,7},{7,6},{8,9},{9,8},{10,11... | collective-permute-start | bytes 6152 | tf_op jit(solution)/shard_map/ppermute | solution.py:391
  (27 other events, 93.1 us)

commit v20 on v15

--- a/solution.py
+++ b/solution.py
@@ -321,12 +321,16 @@
     light_a["slices"] = lambda: (st["la_keep"], st["la_send"])
     light_b["slices"] = lambda: (st["lb_keep"], st["lb_send"])
 
-    def born_pass():
+    def born_first():
         model = model_held.reshape(span_z, span_x * span_y).T.reshape(span_x, span_y, span_z)
+        st["model"] = model
         st["born1"] = model * st["drive0"]
-        st["born2"] = born_second(st["born1"], model, st["drive1"])
-
-    run_group([light_a, light_b], born_pass)
+
+    def born_next():
+        st["born2"] = born_second(st["born1"], st["model"], st["drive1"])
+
+    run_group([light_a, light_b], born_first)
+    run_group([light_a, light_b], born_next)
     born1, born2 = st["born1"], st["born2"]
 
     image = st["drive0"] * born1 + st["drive1"] * born2

time: 130 us -> 135 us (1.038)
  starting transfers between devices: 25.6 us -> 30.3 us
  other arithmetic: 34.8 us -> 38.6 us
  waiting for transfers between devices: 41.9 us -> 38.8 us
    ppermute x8, waiting for transfers between devices: 17.6 us -> 13.2 us  [rs_step(): got = lax.ppermute(send, 'shot', [(i, i ^ k) for i in range(n)])]
    ppermute x8, starting transfers between devices: 8.48 us -> 11.2 us  [rs_step(): got = lax.ppermute(send, 'shot', [(i, i ^ k) for i in range(n)])]
    ppermute x13, starting transfers between devices: 13 us -> 15.4 us  [ag_step(): theirs = lax.ppermute(held, 'shot', [(i, i ^ k) for i in range(n)])]
    ppermute x6, waiting for transfers between devices: 0.54 us -> 2.87 us  [with_halo(): got = lax.ppermute(piece, 'space', [(0, 1), (1, 0)])]
    add x2, other arithmetic: 0.08 us -> 1.98 us  [chain_step(): return keep + lax.ppermute(send, 'shot', [(i, i ^ k) for i in range(n)])]
    ppermute x2, waiting for transfers between devices: 3.04 us -> 1.33 us  [chain_step(): return keep + lax.ppermute(send, 'shot', [(i, i ^ k) for i in range(n)])]
    unnamed x55 -> x51, local copies, waits for them, and re-layouts: 5.27 us -> 4.6 us
  transfers between devices with their start and end apart: 30 -> 30, of which waited for: 15 -> 18; matrix products, arithmetic and copies ran while one was open for 28% -> 30% of each run, Pallas kernels for 0% -> 0%
where the time goes in v20:
time: 135 us; the launch traced here: 134 us
  waiting for transfers between devices  38.8 us (29%)
  other arithmetic  38.6 us (29%)
  starting transfers between devices  30.3 us (22%)
  local copies, waits for them, and re-layouts  20 us (15%)
  between operations  4.76 us (4%)
  matrix products  1.7 us (1%)
    ppermute x13, waiting for transfers between devices, ag_step(): theirs = lax.ppermute(held, 'shot', [(i, i ^ k) for i in range(n)])  21.4 us
    ppermute x13, starting transfers between devices, ag_step(): theirs = lax.ppermute(held, 'shot', [(i, i ^ k) for i in range(n)])  15.4 us
    ppermute x8, waiting for transfers between devices, rs_step(): got = lax.ppermute(send, 'shot', [(i, i ^ k) for i in range(n)])  13.2 us
    ppermute x8, starting transfers between devices, rs_step(): got = lax.ppermute(send, 'shot', [(i, i ^ k) for i in range(n)])  11.2 us
    add x3, other arithmetic, inject(): return field + jnp.where(hit, source_gain[0] * wavelet[0, moment], 0.0)  8.05 us
    add x2, other arithmetic, born_second(): 2.0 * born + speed_term * laplace_x(with_halo(born)) - absorber * born  5.83 us
    unnamed x51, local copies, waits for them, and re-layouts  4.6 us
    another operation x1, other arithmetic, damping(): lower = jnp.stack([edges[0], edges[2], edges[4]])[:, None]  3.86 us
  transfers between devices with their start and end apart: 30, of which 18 were waited for; matrix products, arithmetic and copies ran while one was open for 30% of the time, Pallas kernels for 0%

profile of v20, /device:TPU:0, one launch (start us, length us, event | category | flops | bytes accessed | tf_op | source)
XLA Modules:
  0.0 134.2 jit_solution(11798300621362970062)
XLA Ops:
  2.6 4.0 %collective-permute-start = (f32[1,16,2048]{2,1,0:T(8,128)}, f32[1,16,2048]{2,1,0:T(8,128)}, u32[]{:S(2)}, u32[]{:S(2)}) collective-permute-start(f32[1,16,2048]{2,1,0:T(8,128)} %concatenate.199), channel_id=1, source_target_pairs={{0,8},{2,10},{4,12},{6,14},{8,0},{10,2},{12,4},{14,6},{1,9},{3,11}... | collective-permute-start | bytes 393224 | tf_op jit(solution)/shard_map/ppermute | solution.py:120
  6.6 1.6 %dynamic-slice_bitcast_fusion.10 = f32[4,64,128]{2,1,0:T(8,128)} fusion(f32[1,32,64,128]{3,2,1,0:T(8,128)} %param.12, s32[]{:T(128)S(6)} %select_n.404), kind=kLoop, calls=%fused_computation.441 | loop fusion | bytes 262148 | tf_op jit(solution)/shard_map/dynamic_slice | solution.py:51
  10.2 3.9 %pad_maximum_fusion.15 = (f32[3]{0:T(128)S(1)}, f32[3]{0:T(128)S(1)}) fusion(f32[1]{0:T(128)} %get-tuple-element.179, f32[1]{0:T(128)} %get-tuple-element.180, f32[1]{0:T(128)} %get-tuple-element.175, f32[1]{0:T(128)} %get-tuple-element.176, f32[1]{0:T(128)} %get-tuple-element.177, f32[1]{0:T(128)} %get-tuple-element.178), kind=kLoop, calls=%fused_computation.500 | loop fusion | flops 12 | bytes 48 | tf_op jit(solution)/shard_map/stack | solution.py:37
  17.4 2.6 %fusion.144 = f32[24,64,128]{2,1,0:T(8,128)} fusion(f32[32,64,128]{2,1,0:T(8,128)S(1)} %bitcast.205, f32[1,32,64,128]{3,2,1,0:T(8,128)S(1)} %copy-done), kind=kLoop, calls=%fused_computation.324 | loop fusion | flops 5701632 | bytes 8912896 | tf_op jit(solution)/shard_map/add | solution.py:86
  21.0 1.3 broadcast_and_fusion
  31.3 1.9 %collective-permute-start.3 = (f32[2,8,2048]{2,1,0:T(8,128)S(1)}, f32[2,8,2048]{2,1,0:T(8,128)S(1)}, u32[]{:S(2)}, u32[]{:S(2)}) collective-permute-start(f32[2,8,2048]{2,1,0:T(8,128)S(1)} %get-tuple-element.169), channel_id=1, source_target_pairs={{0,4},{2,6},{4,0},{6,2},{8,12},{10,14},{12,8},{14,10},{1,5},{3,7},... | collective-permute-start | bytes 393224 | tf_op jit(solution)/shard_map/ppermute | solution.py:120
  33.6 1.9 %collective-permute-start.4 = (f32[2,8,2048]{2,1,0:T(8,128)S(1)}, f32[2,8,2048]{2,1,0:T(8,128)S(1)}, u32[]{:S(2)}, u32[]{:S(2)}) collective-permute-start(f32[2,8,2048]{2,1,0:T(8,128)S(1)} %get-tuple-element.168), channel_id=1, source_target_pairs={{0,2},{2,0},{4,6},{6,4},{8,10},{10,8},{12,14},{14,12},{1,3},{3,1},... | collective-permute-start | bytes 393224 | tf_op jit(solution)/shard_map/ppermute | solution.py:120
  35.5 2.3 %collective-permute-done.5 = f32[2,16,64]{2,1,0:T(8,128)S(1)} collective-permute-done((f32[2,16,64]{2,1,0:T(8,128)S(1)}, f32[2,16,64]{2,1,0:T(8,128)S(1)}, u32[]{:S(2)}, u32[]{:S(2)}) %collective-permute-start.5) | collective-permute-done | bytes 8224 | tf_op jit(solution)/shard_map/ppermute | solution.py:120
  37.8 1.4 %collective-permute-done.4 = f32[2,8,2048]{2,1,0:T(8,128)S(1)} collective-permute-done((f32[2,8,2048]{2,1,0:T(8,128)S(1)}, f32[2,8,2048]{2,1,0:T(8,128)S(1)}, u32[]{:S(2)}, u32[]{:S(2)}) %collective-permute-start.4) | collective-permute-done | bytes 131104 | tf_op jit(solution)/shard_map/ppermute | solution.py:120
  39.3 3.2 %fusion.3 = (f32[32,64,128]{2,1,0:T(8,128)S(1)}, f32[32,64,128]{2,1,0:T(8,128)S(1)}) fusion(f32[32,64,128]{2,1,0:T(8,128)S(1)} %get-tuple-element.79, f32[32,64,128]{2,1,0:T(8,128)S(1)} %bitcast.207, f32[]{:T(128)S(6)} %mul.394, f32[128]{0:T(128)S(1)} %copy-done.14, f32[32,64]{1,0:T(8,128)S(1)} %broadcast_add_fusion, pred[128]{0:T(512)(128)(4,1)S(1)} %copy-done.17, ...), kind=kLoop, calls=%fused_computation.151 | loop fusion | flops 12058624 | bytes 16012292 | tf_op jit(solution)/shard_map/add | solution.py:230
  43.6 1.7 %collective-permute-start.7 = (f32[4,8,2048]{2,1,0:T(8,128)S(1)}, f32[4,8,2048]{2,1,0:T(8,128)S(1)}, u32[]{:S(2)}, u32[]{:S(2)}) collective-permute-start(f32[4,8,2048]{2,1,0:T(8,128)S(1)} %bitcast.232), channel_id=1, source_target_pairs={{0,2},{2,0},{4,6},{6,4},{8,10},{10,8},{12,14},{14,12},{1,3},{3,1},... | collective-permute-start | bytes 786440 | tf_op jit(solution)/shard_map/ppermute | solution.py:120
  45.3 1.6 %collective-permute-start.8 = (f32[4,8,2048]{2,1,0:T(8,128)S(1)}, f32[4,8,2048]{2,1,0:T(8,128)S(1)}, u32[]{:S(2)}, u32[]{:S(2)}) collective-permute-start(f32[4,8,2048]{2,1,0:T(8,128)S(1)} %bitcast.234), channel_id=1, source_target_pairs={{0,4},{2,6},{4,0},{6,2},{8,12},{10,14},{12,8},{14,10},{1,5},{3,7},... | collective-permute-start | bytes 786440 | tf_op jit(solution)/shard_map/ppermute | solution.py:120
  49.1 2.9 %collective-permute-done.9 = f32[4,16,64]{2,1,0:T(8,128)S(1)} collective-permute-done((f32[4,16,64]{2,1,0:T(8,128)S(1)}, f32[4,16,64]{2,1,0:T(8,128)S(1)}, u32[]{:S(2)}, u32[]{:S(2)}) %collective-permute-start.9) | collective-permute-done | bytes 16416 | tf_op jit(solution)/shard_map/ppermute | solution.py:120
  52.6 4.0 %fusion.4 = (f32[32,64,128]{2,1,0:T(8,128)}, f32[32,64,128]{2,1,0:T(8,128)}) fusion(f32[32,64,128]{2,1,0:T(8,128)S(1)} %get-tuple-element.77, f32[32,64,128]{2,1,0:T(8,128)S(1)} %get-tuple-element.79, f32[]{:T(128)S(6)} %mul.403, f32[128]{0:T(128)S(1)} %copy-done.14, f32[32,64]{1,0:T(8,128)S(1)} %broadcast_add_fusion, pred[128]{0:T(512)(128)(4,1)S(1)} %copy-done.17, ...), kind=kLoop, calls=%fused_computation.152 | loop fusion | flops 12058624 | bytes 16012292 | tf_op jit(solution)/shard_map/add | solution.py:230
  56.8 1.5 %collective-permute-start.11 = (f32[4,4,32,128]{3,2,1,0:T(8,128)}, f32[4,4,32,128]{3,2,1,0:T(8,128)}, u32[]{:S(2)}, u32[]{:S(2)}) collective-permute-start(f32[4,4,32,128]{3,2,1,0:T(8,128)} %get-tuple-element.81), channel_id=1, source_target_pairs={{0,2},{2,0},{4,6},{6,4},{8,10},{10,8},{12,14},{14,12},{1,3},{3,1},... | collective-permute-start | bytes 786440 | tf_op jit(solution)/shard_map/ppermute | solution.py:160
  58.3 1.6 %collective-permute-start.12 = (f32[4,4,32,128]{3,2,1,0:T(8,128)}, f32[4,4,32,128]{3,2,1,0:T(8,128)}, u32[]{:S(2)}, u32[]{:S(2)}) collective-permute-start(f32[4,4,32,128]{3,2,1,0:T(8,128)} %bitcast.45), channel_id=1, source_target_pairs={{0,4},{2,6},{4,0},{6,2},{8,12},{10,14},{12,8},{14,10},{1,5},{3,7},... | collective-permute-start | bytes 786440 | tf_op jit(solution)/shard_map/ppermute | solution.py:160
  60.9 1.5 %copy.48 = f32[2048,128]{1,0:T(8,128)S(1)} copy(f32[2048,128]{0,1:T(8,128)} %bitcast.216) | data formatting | bytes 2097152 | tf_op jit(solution)/shard_map/transpose | solution.py:325
  66.0 1.6 %collective-permute-start.13 = (f32[2,1,4,32,128]{4,3,2,0,1:T(8,128)S(1)}, f32[2,1,4,32,128]{4,3,2,0,1:T(8,128)S(1)}, u32[]{:S(2)}, u32[]{:S(2)}) collective-permute-start(f32[2,1,4,32,128]{4,3,2,0,1:T(8,128)S(1)} %dynamic-slice_bitcast_fusion.9), channel_id=1, source_target_pairs={{0,4},{2,6},{4,0},{6,2},{8,12},{10,14},{12,8},{14,10},{1,5},{3,7},... | collective-permute-start | bytes 393224 | tf_op jit(solution)/shard_map/ppermute | solution.py:186
  69.0 1.2 collective-permute-done.15
  70.2 2.9 %fusion.67 = f32[32,64,128]{2,1,0:T(8,128)S(1)} fusion(f32[40,64,128]{2,1,0:T(8,128)S(1)} %constant_dynamic-update-slice_fusion.2, f32[32,64,128]{2,1,0:T(8,128)S(1)} %bitcast.211, f32[32,64,128]{2,1,0:T(8,128)S(1)} %copy-done.3, f32[32,64,128]{2,1,0:T(8,128)S(1)} %mul.404, f32[128]{0:T(128)S(1)} %copy-done.15, f32[32,64]{1,0:T(8,128)S(1)} %broadcast_add_fusion, ...), kind=kLoop, calls=%fused_computation.215 | loop fusion | flops 11272192 | bytes 16007680 | tf_op jit(solution)/shard_map/add | solution.py:251
  75.5 2.7 %collective-permute-start.18 = (f32[1,1,4,64,128]{4,3,2,1,0:T(8,128)S(1)}, f32[1,1,4,64,128]{4,3,2,1,0:T(8,128)S(1)}, u32[]{:S(2)}, u32[]{:S(2)}) collective-permute-start(f32[1,1,4,64,128]{4,3,2,1,0:T(8,128)S(1)} %dynamic-slice_bitcast_fusion.7), channel_id=1, source_target_pairs={{0,8},{2,10},{4,12},{6,14},{8,0},{10,2},{12,4},{14,6},{1,9},{3,11}... | collective-permute-start | bytes 393224 | tf_op jit(solution)/shard_map/ppermute | solution.py:186
  79.6 3.2 %fusion.92 = f32[32,64,128]{2,1,0:T(8,128)} fusion(f32[40,64,128]{2,1,0:T(8,128)S(1)} %constant_dynamic-update-slice_fusion.1, s32[32,64,128]{2,1,0:T(8,128)S(1)} %copy-done.1), kind=kLoop, calls=%fused_computation.240 | loop fusion | flops 9175040 | bytes 12845056 | tf_op jit(solution)/shard_map/mul | solution.py:243
  83.9 1.9 %collective-permute-done.17 = f32[2,2,4,32,128]{4,3,2,1,0:T(8,128)S(1)} collective-permute-done((f32[2,2,4,32,128]{4,3,2,1,0:T(8,128)S(1)}, f32[2,2,4,32,128]{4,3,2,1,0:T(8,128)S(1)}, u32[]{:S(2)}, u32[]{:S(2)}) %collective-permute-start.17) | collective-permute-done | bytes 262176 | tf_op jit(solution)/shard_map/ppermute | solution.py:186
  85.9 2.8 %collective-permute-start.20 = (f32[2,1,4,32,128]{4,3,2,0,1:T(8,128)S(1)}, f32[2,1,4,32,128]{4,3,2,0,1:T(8,128)S(1)}, u32[]{:S(2)}, u32[]{:S(2)}) collective-permute-start(f32[2,1,4,32,128]{4,3,2,0,1:T(8,128)S(1)} %dynamic-slice_bitcast_fusion.6), channel_id=1, source_target_pairs={{0,4},{2,6},{4,0},{6,2},{8,12},{10,14},{12,8},{14,10},{1,5},{3,7},... | collective-permute-start | bytes 393224 | tf_op jit(solution)/shard_map/ppermute | solution.py:186
  89.8 1.9 %collective-permute-done.20 = f32[2,1,4,32,128]{4,3,2,0,1:T(8,128)S(1)} collective-permute-done((f32[2,1,4,32,128]{4,3,2,0,1:T(8,128)S(1)}, f32[2,1,4,32,128]{4,3,2,0,1:T(8,128)S(1)}, u32[]{:S(2)}, u32[]{:S(2)}) %collective-permute-start.20) | collective-permute-done | bytes 131104 | tf_op jit(solution)/shard_map/ppermute | solution.py:186
  91.6 2.1 %collective-permute-done.21 = f32[2,1,4,32,128]{4,3,2,0,1:T(8,128)S(1)} collective-permute-done((f32[2,1,4,32,128]{4,3,2,0,1:T(8,128)S(1)}, f32[2,1,4,32,128]{4,3,2,0,1:T(8,128)S(1)}, u32[]{:S(2)}, u32[]{:S(2)}) %collective-permute-start.21) | collective-permute-done | bytes 131104 | tf_op jit(solution)/shard_map/ppermute | solution.py:186
  94.3 6.3 %collective-permute-done.22 = f32[1,1,4,64,128]{4,3,2,1,0:T(8,128)S(1)} collective-permute-done((f32[1,1,4,64,128]{4,3,2,1,0:T(8,128)S(1)}, f32[1,1,4,64,128]{4,3,2,1,0:T(8,128)S(1)}, u32[]{:S(2)}, u32[]{:S(2)}) %collective-permute-start.22) | collective-permute-done | bytes 131104 | tf_op jit(solution)/shard_map/ppermute | solution.py:186
  102.5 6.3 %collective-permute-done.23 = f32[1,4,64,128]{3,2,1,0:T(8,128)S(1)} collective-permute-done((f32[1,4,64,128]{3,2,1,0:T(8,128)S(1)}, f32[1,4,64,128]{3,2,1,0:T(8,128)S(1)}, u32[]{:S(2)}, u32[]{:S(2)}) %collective-permute-start.23) | collective-permute-done | bytes 131104 | tf_op jit(solution)/shard_map/ppermute | solution.py:120
  110.6 4.4 %collective-permute-done.24 = f32[2,4,32,128]{3,2,1,0:T(8,128)S(1)} collective-permute-done((f32[2,4,32,128]{3,2,1,0:T(8,128)S(1)}, f32[2,4,32,128]{3,2,1,0:T(8,128)S(1)}, u32[]{:S(2)}, u32[]{:S(2)}) %collective-permute-start.24) | collective-permute-done | bytes 131104 | tf_op jit(solution)/shard_map/ppermute | solution.py:120
  116.5 1.3 collective-permute-start.27
  118.9 2.9 %collective-permute-done.26 = f32[4,4,32,128]{3,2,1,0:T(8,128)S(1)} collective-permute-done((f32[4,4,32,128]{3,2,1,0:T(8,128)S(1)}, f32[4,4,32,128]{3,2,1,0:T(8,128)S(1)}, u32[]{:S(2)}, u32[]{:S(2)}) %collective-permute-start.26) | collective-permute-done | bytes 262176 | tf_op jit(solution)/shard_map/ppermute | solution.py:120
  127.4 2.9 %fusion.120 = f32[32,64,128]{2,1,0:T(8,128)S(1)} fusion(f32[40,64,128]{2,1,0:T(8,128)S(1)} %constant_dynamic-update-slice_fusion, f32[32,64,128]{2,1,0:T(8,128)S(1)} %copy-done.7, f32[128]{0:T(128)S(1)} %copy-done.16, f32[32,64]{1,0:T(8,128)S(1)} %broadcast_add_fusion, f32[8,4,64,128]{3,2,1,0:T(8,128)S(1)} %pad_maximum_fusion.13, ...), kind=kLoop, calls=%fused_computation.268 | loop fusion | flops 11534336 | bytes 16007680 | tf_op jit(solution)/shard_map/add | solution.py:251
  (197 shorter events, 46.3 us)
Async XLA Ops:
  0.6 16.8 %copy-start = (f32[1,32,64,128]{3,2,1,0:T(8,128)S(1)}, f32[1,32,64,128]{3,2,1,0:T(8,128)}, u32[]{:S(2)}) copy-start(f32[1,32,64,128]{3,2,1,0:T(8,128)} %param.12) | copy-start | bytes 3145732
  0.7 15.1 %copy-start.18 = (f32[1,4]{1,0:T(1,128)S(1)}, f32[1,4]{1,0:T(1,128)}, u32[]{:S(2)}) copy-start(f32[1,4]{1,0:T(1,128)} %param.16) | copy-start | bytes 52
  2.6 27.6 %collective-permute-start = (f32[1,16,2048]{2,1,0:T(8,128)}, f32[1,16,2048]{2,1,0:T(8,128)}, u32[]{:S(2)}, u32[]{:S(2)}) collective-permute-start(f32[1,16,2048]{2,1,0:T(8,128)} %concatenate.199), channel_id=1, source_target_pairs={{0,8},{2,10},{4,12},{6,14},{8,0},{10,2},{12,4},{14,6},{1,9},{3,11}... | collective-permute-start | bytes 393224 | tf_op jit(solution)/shard_map/ppermute | solution.py:120
  6.6 19.4 %collective-permute-start.1 = (f32[1,16,64]{2,1,0:T(8,128)}, f32[1,16,64]{2,1,0:T(8,128)}, u32[]{:S(2)}, u32[]{:S(2)}) collective-permute-start(f32[1,16,64]{2,1,0:T(8,128)} %bitcast.261), channel_id=1, source_target_pairs={{0,8},{2,10},{4,12},{6,14},{8,0},{10,2},{12,4},{14,6},{1,9},{3,11}... | collective-permute-start | bytes 12296 | tf_op jit(solution)/shard_map/ppermute | solution.py:120
  8.2 18.6 %collective-permute-start.2 = (f32[4,64,128]{2,1,0:T(8,128)}, f32[4,64,128]{2,1,0:T(8,128)}, u32[]{:S(2)}, u32[]{:S(2)}) collective-permute-start(f32[4,64,128]{2,1,0:T(8,128)} %dynamic-slice_bitcast_fusion.10), channel_id=1, source_target_pairs={{0,1},{1,0},{2,3},{3,2},{4,5},{5,4},{6,7},{7,6},{8,9},{9,8},{10,11... | collective-permute-start | bytes 393224 | tf_op jit(solution)/shard_map/ppermute | solution.py:52
  31.3 6.5 %collective-permute-start.3 = (f32[2,8,2048]{2,1,0:T(8,128)S(1)}, f32[2,8,2048]{2,1,0:T(8,128)S(1)}, u32[]{:S(2)}, u32[]{:S(2)}) collective-permute-start(f32[2,8,2048]{2,1,0:T(8,128)S(1)} %get-tuple-element.169), channel_id=1, source_target_pairs={{0,4},{2,6},{4,0},{6,2},{8,12},{10,14},{12,8},{14,10},{1,5},{3,7},... | collective-permute-start | bytes 393224 | tf_op jit(solution)/shard_map/ppermute | solution.py:120
  33.3 4.5 %collective-permute-start.5 = (f32[2,16,64]{2,1,0:T(8,128)S(1)}, f32[2,16,64]{2,1,0:T(8,128)S(1)}, u32[]{:S(2)}, u32[]{:S(2)}) collective-permute-start(f32[2,16,64]{2,1,0:T(8,128)S(1)} %maximum_select_fusion.12), channel_id=1, source_target_pairs={{0,4},{2,6},{4,0},{6,2},{8,12},{10,14},{12,8},{14,10},{1,5},{3,7},... | collective-permute-start | bytes 24584 | tf_op jit(solution)/shard_map/ppermute | solution.py:120
  33.6 5.6 %collective-permute-start.4 = (f32[2,8,2048]{2,1,0:T(8,128)S(1)}, f32[2,8,2048]{2,1,0:T(8,128)S(1)}, u32[]{:S(2)}, u32[]{:S(2)}) collective-permute-start(f32[2,8,2048]{2,1,0:T(8,128)S(1)} %get-tuple-element.168), channel_id=1, source_target_pairs={{0,2},{2,0},{4,6},{6,4},{8,10},{10,8},{12,14},{14,12},{1,3},{3,1},... | collective-permute-start | bytes 393224 | tf_op jit(solution)/shard_map/ppermute | solution.py:120
  35.5 3.8 %collective-permute-start.6 = (f32[4,64,128]{2,1,0:T(8,128)S(1)}, f32[4,64,128]{2,1,0:T(8,128)S(1)}, u32[]{:S(2)}, u32[]{:S(2)}) collective-permute-start(f32[4,64,128]{2,1,0:T(8,128)S(1)} %constant_dynamic-slice_fusion.7), channel_id=1, source_target_pairs={{0,1},{1,0},{2,3},{3,2},{4,5},{5,4},{6,7},{7,6},{8,9},{9,8},{10,11... | collective-permute-start | bytes 393224 | tf_op jit(solution)/shard_map/ppermute | solution.py:52
  43.6 13.0 %collective-permute-start.7 = (f32[4,8,2048]{2,1,0:T(8,128)S(1)}, f32[4,8,2048]{2,1,0:T(8,128)S(1)}, u32[]{:S(2)}, u32[]{:S(2)}) collective-permute-start(f32[4,8,2048]{2,1,0:T(8,128)S(1)} %bitcast.232), channel_id=1, source_target_pairs={{0,2},{2,0},{4,6},{6,4},{8,10},{10,8},{12,14},{14,12},{1,3},{3,1},... | collective-permute-start | bytes 786440 | tf_op jit(solution)/shard_map/ppermute | solution.py:120
  45.3 11.4 %collective-permute-start.8 = (f32[4,8,2048]{2,1,0:T(8,128)S(1)}, f32[4,8,2048]{2,1,0:T(8,128)S(1)}, u32[]{:S(2)}, u32[]{:S(2)}) collective-permute-start(f32[4,8,2048]{2,1,0:T(8,128)S(1)} %bitcast.234), channel_id=1, source_target_pairs={{0,4},{2,6},{4,0},{6,2},{8,12},{10,14},{12,8},{14,10},{1,5},{3,7},... | collective-permute-start | bytes 786440 | tf_op jit(solution)/shard_map/ppermute | solution.py:120
  46.9 5.0 %collective-permute-start.9 = (f32[4,16,64]{2,1,0:T(8,128)S(1)}, f32[4,16,64]{2,1,0:T(8,128)S(1)}, u32[]{:S(2)}, u32[]{:S(2)}) collective-permute-start(f32[4,16,64]{2,1,0:T(8,128)S(1)} %bitcast.254), channel_id=1, source_target_pairs={{0,2},{2,0},{4,6},{6,4},{8,10},{10,8},{12,14},{14,12},{1,3},{3,1},... | collective-permute-start | bytes 49160 | tf_op jit(solution)/shard_map/ppermute | solution.py:120
  47.4 5.2 %collective-permute-start.10 = (f32[4,64,128]{2,1,0:T(8,128)S(1)}, f32[4,64,128]{2,1,0:T(8,128)S(1)}, u32[]{:S(2)}, u32[]{:S(2)}) collective-permute-start(f32[4,64,128]{2,1,0:T(8,128)S(1)} %constant_dynamic-slice_fusion.6), channel_id=1, source_target_pairs={{0,1},{1,0},{2,3},{3,2},{4,5},{5,4},{6,7},{7,6},{8,9},{9,8},{10,11... | collective-permute-start | bytes 393224 | tf_op jit(solution)/shard_map/ppermute | solution.py:52
  56.8 7.0 %collective-permute-start.11 = (f32[4,4,32,128]{3,2,1,0:T(8,128)}, f32[4,4,32,128]{3,2,1,0:T(8,128)}, u32[]{:S(2)}, u32[]{:S(2)}) collective-permute-start(f32[4,4,32,128]{3,2,1,0:T(8,128)} %get-tuple-element.81), channel_id=1, source_target_pairs={{0,2},{2,0},{4,6},{6,4},{8,10},{10,8},{12,14},{14,12},{1,3},{3,1},... | collective-permute-start | bytes 786440 | tf_op jit(solution)/shard_map/ppermute | solution.py:160
  58.3 6.7 %collective-permute-start.12 = (f32[4,4,32,128]{3,2,1,0:T(8,128)}, f32[4,4,32,128]{3,2,1,0:T(8,128)}, u32[]{:S(2)}, u32[]{:S(2)}) collective-permute-start(f32[4,4,32,128]{3,2,1,0:T(8,128)} %bitcast.45), channel_id=1, source_target_pairs={{0,4},{2,6},{4,0},{6,2},{8,12},{10,14},{12,8},{14,10},{1,5},{3,7},... | collective-permute-start | bytes 786440 | tf_op jit(solution)/shard_map/ppermute | solution.py:160
  66.0 7.2 %collective-permute-start.13 = (f32[2,1,4,32,128]{4,3,2,0,1:T(8,128)S(1)}, f32[2,1,4,32,128]{4,3,2,0,1:T(8,128)S(1)}, u32[]{:S(2)}, u32[]{:S(2)}) collective-permute-start(f32[2,1,4,32,128]{4,3,2,0,1:T(8,128)S(1)} %dynamic-slice_bitcast_fusion.9), channel_id=1, source_target_pairs={{0,4},{2,6},{4,0},{6,2},{8,12},{10,14},{12,8},{14,10},{1,5},{3,7},... | collective-permute-start | bytes 393224 | tf_op jit(solution)/shard_map/ppermute | solution.py:186
  67.6 5.5 %collective-permute-start.14 = (f32[2,1,4,32,128]{4,3,2,0,1:T(8,128)S(1)}, f32[2,1,4,32,128]{4,3,2,0,1:T(8,128)S(1)}, u32[]{:S(2)}, u32[]{:S(2)}) collective-permute-start(f32[2,1,4,32,128]{4,3,2,0,1:T(8,128)S(1)} %dynamic-slice_bitcast_fusion.8), channel_id=1, source_target_pairs={{0,2},{2,0},{4,6},{6,4},{8,10},{10,8},{12,14},{14,12},{1,3},{3,1},... | collective-permute-start | bytes 393224 | tf_op jit(solution)/shard_map/ppermute | solution.py:186
  68.7 1.4 %collective-permute-start.15 = (f32[4,64,128]{2,1,0:T(8,128)S(1)}, f32[4,64,128]{2,1,0:T(8,128)S(1)}, u32[]{:S(2)}, u32[]{:S(2)}) collective-permute-start(f32[4,64,128]{2,1,0:T(8,128)S(1)} %constant_dynamic-slice_fusion.3), channel_id=1, source_target_pairs={{0,1},{1,0},{2,3},{3,2},{4,5},{5,4},{6,7},{7,6},{8,9},{9,8},{10,11... | collective-permute-start | bytes 393224 | tf_op jit(solution)/shard_map/ppermute | solution.py:52
  73.8 10.0 %collective-permute-start.16 = (f32[4,1,4,32,128]{4,3,2,0,1:T(8,128)S(1)}, f32[4,1,4,32,128]{4,3,2,0,1:T(8,128)S(1)}, u32[]{:S(2)}, u32[]{:S(2)}) collective-permute-start(f32[4,1,4,32,128]{4,3,2,0,1:T(8,128)S(1)} %dynamic-slice_bitcast_fusion.1), channel_id=1, source_target_pairs={{0,2},{2,0},{4,6},{6,4},{8,10},{10,8},{12,14},{14,12},{1,3},{3,1},... | collective-permute-start | bytes 786440 | tf_op jit(solution)/shard_map/ppermute | solution.py:186
  74.9 11.0 %collective-permute-start.17 = (f32[2,2,4,32,128]{4,3,2,1,0:T(8,128)S(1)}, f32[2,2,4,32,128]{4,3,2,1,0:T(8,128)S(1)}, u32[]{:S(2)}, u32[]{:S(2)}) collective-permute-start(f32[2,2,4,32,128]{4,3,2,1,0:T(8,128)S(1)} %dynamic-slice_bitcast_fusion), channel_id=1, source_target_pairs={{0,4},{2,6},{4,0},{6,2},{8,12},{10,14},{12,8},{14,10},{1,5},{3,7},... | collective-permute-start | bytes 786440 | tf_op jit(solution)/shard_map/ppermute | solution.py:186
  75.5 8.3 %collective-permute-start.18 = (f32[1,1,4,64,128]{4,3,2,1,0:T(8,128)S(1)}, f32[1,1,4,64,128]{4,3,2,1,0:T(8,128)S(1)}, u32[]{:S(2)}, u32[]{:S(2)}) collective-permute-start(f32[1,1,4,64,128]{4,3,2,1,0:T(8,128)S(1)} %dynamic-slice_bitcast_fusion.7), channel_id=1, source_target_pairs={{0,8},{2,10},{4,12},{6,14},{8,0},{10,2},{12,4},{14,6},{1,9},{3,11}... | collective-permute-start | bytes 393224 | tf_op jit(solution)/shard_map/ppermute | solution.py:186
  78.1 1.4 %collective-permute-start.19 = (f32[4,64,128]{2,1,0:T(8,128)S(1)}, f32[4,64,128]{2,1,0:T(8,128)S(1)}, u32[]{:S(2)}, u32[]{:S(2)}) collective-permute-start(f32[4,64,128]{2,1,0:T(8,128)S(1)} %constant_dynamic-slice_fusion.2), channel_id=1, source_target_pairs={{0,1},{1,0},{2,3},{3,2},{4,5},{5,4},{6,7},{7,6},{8,9},{9,8},{10,11... | collective-permute-start | bytes 393224 | tf_op jit(solution)/shard_map/ppermute | solution.py:52
  85.9 5.7 %collective-permute-start.20 = (f32[2,1,4,32,128]{4,3,2,0,1:T(8,128)S(1)}, f32[2,1,4,32,128]{4,3,2,0,1:T(8,128)S(1)}, u32[]{:S(2)}, u32[]{:S(2)}) collective-permute-start(f32[2,1,4,32,128]{4,3,2,0,1:T(8,128)S(1)} %dynamic-slice_bitcast_fusion.6), channel_id=1, source_target_pairs={{0,4},{2,6},{4,0},{6,2},{8,12},{10,14},{12,8},{14,10},{1,5},{3,7},... | collective-permute-start | bytes 393224 | tf_op jit(solution)/shard_map/ppermute | solution.py:186
  88.7 5.0 %collective-permute-start.21 = (f32[2,1,4,32,128]{4,3,2,0,1:T(8,128)S(1)}, f32[2,1,4,32,128]{4,3,2,0,1:T(8,128)S(1)}, u32[]{:S(2)}, u32[]{:S(2)}) collective-permute-start(f32[2,1,4,32,128]{4,3,2,0,1:T(8,128)S(1)} %dynamic-slice_bitcast_fusion.5), channel_id=1, source_target_pairs={{0,2},{2,0},{4,6},{6,4},{8,10},{10,8},{12,14},{14,12},{1,3},{3,1},... | collective-permute-start | bytes 393224 | tf_op jit(solution)/shard_map/ppermute | solution.py:186
  93.8 6.8 %collective-permute-start.22 = (f32[1,1,4,64,128]{4,3,2,1,0:T(8,128)S(1)}, f32[1,1,4,64,128]{4,3,2,1,0:T(8,128)S(1)}, u32[]{:S(2)}, u32[]{:S(2)}) collective-permute-start(f32[1,1,4,64,128]{4,3,2,1,0:T(8,128)S(1)} %dynamic-slice_bitcast_fusion.4), channel_id=1, source_target_pairs={{0,8},{2,10},{4,12},{6,14},{8,0},{10,2},{12,4},{14,6},{1,9},{3,11}... | collective-permute-start | bytes 393224 | tf_op jit(solution)/shard_map/ppermute | solution.py:186
  102.4 6.4 %collective-permute-start.23 = (f32[1,4,64,128]{3,2,1,0:T(8,128)S(1)}, f32[1,4,64,128]{3,2,1,0:T(8,128)S(1)}, u32[]{:S(2)}, u32[]{:S(2)}) collective-permute-start(f32[1,4,64,128]{3,2,1,0:T(8,128)S(1)} %fusion.1), channel_id=1, source_target_pairs={{0,8},{2,10},{4,12},{6,14},{8,0},{10,2},{12,4},{14,6},{1,9},{3,11}... | collective-permute-start | bytes 393224 | tf_op jit(solution)/shard_map/ppermute | solution.py:120
  108.9 6.1 %collective-permute-start.24 = (f32[2,4,32,128]{3,2,1,0:T(8,128)S(1)}, f32[2,4,32,128]{3,2,1,0:T(8,128)S(1)}, u32[]{:S(2)}, u32[]{:S(2)}) collective-permute-start(f32[2,4,32,128]{3,2,1,0:T(8,128)S(1)} %get-tuple-element.165), channel_id=1, source_target_pairs={{0,4},{2,6},{4,0},{6,2},{8,12},{10,14},{12,8},{14,10},{1,5},{3,7},... | collective-permute-start | bytes 393224 | tf_op jit(solution)/shard_map/ppermute | solution.py:120
  109.0 6.4 %collective-permute-start.25 = (f32[2,4,32,128]{3,2,1,0:T(8,128)S(1)}, f32[2,4,32,128]{3,2,1,0:T(8,128)S(1)}, u32[]{:S(2)}, u32[]{:S(2)}) collective-permute-start(f32[2,4,32,128]{3,2,1,0:T(8,128)S(1)} %get-tuple-element.164), channel_id=1, source_target_pairs={{0,2},{2,0},{4,6},{6,4},{8,10},{10,8},{12,14},{14,12},{1,3},{3,1},... | collective-permute-start | bytes 393224 | tf_op jit(solution)/shard_map/ppermute | solution.py:120
  115.4 6.4 %collective-permute-start.26 = (f32[4,4,32,128]{3,2,1,0:T(8,128)S(1)}, f32[4,4,32,128]{3,2,1,0:T(8,128)S(1)}, u32[]{:S(2)}, u32[]{:S(2)}) collective-permute-start(f32[4,4,32,128]{3,2,1,0:T(8,128)S(1)} %bitcast.236), channel_id=1, source_target_pairs={{0,2},{2,0},{4,6},{6,4},{8,10},{10,8},{12,14},{14,12},{1,3},{3,1},... | collective-permute-start | bytes 786440 | tf_op jit(solution)/shard_map/ppermute | solution.py:120
  116.5 6.4 %collective-permute-start.27 = (f32[4,4,32,128]{3,2,1,0:T(8,128)S(1)}, f32[4,4,32,128]{3,2,1,0:T(8,128)S(1)}, u32[]{:S(2)}, u32[]{:S(2)}) collective-permute-start(f32[4,4,32,128]{3,2,1,0:T(8,128)S(1)} %bitcast.238), channel_id=1, source_target_pairs={{0,4},{2,6},{4,0},{6,2},{8,12},{10,14},{12,8},{14,10},{1,5},{3,7},... | collective-permute-start | bytes 786440 | tf_op jit(solution)/shard_map/ppermute | solution.py:120
  125.0 1.6 %collective-permute-start.28 = (f32[4,64,128]{2,1,0:T(8,128)}, f32[4,64,128]{2,1,0:T(8,128)S(1)}, u32[]{:S(2)}, u32[]{:S(2)}) collective-permute-start(f32[4,64,128]{2,1,0:T(8,128)} %constant_dynamic-slice_fusion), channel_id=1, source_target_pairs={{0,1},{1,0},{2,3},{3,2},{4,5},{5,4},{6,7},{7,6},{8,9},{9,8},{10,11... | collective-permute-start | bytes 393224 | tf_op jit(solution)/shard_map/ppermute | solution.py:52
  131.7 1.9 %collective-permute-start.29 = (f32[1,2,256]{2,1,0:T(2,128)S(1)}, f32[1,2,256]{2,1,0:T(2,128)S(1)}, u32[]{:S(2)}, u32[]{:S(2)}) collective-permute-start(f32[1,2,256]{2,1,0:T(2,128)S(1)} %maximum_bitcast_fusion), channel_id=1, source_target_pairs={{0,1},{1,0},{2,3},{3,2},{4,5},{5,4},{6,7},{7,6},{8,9},{9,8},{10,11... | collective-permute-start | bytes 6152 | tf_op jit(solution)/shard_map/ppermute | solution.py:393
  (22 other events, 68.7 us)

commit v21 on v15

--- a/solution.py
+++ b/solution.py
@@ -230,17 +230,7 @@
         return field + jnp.where(hit, source_gain[0] * wavelet[0, moment], 0.0)
 
     def wave_step(current, prior, moment, last):
-        if moment == 0:
-            inner = barrier(laplace_x(current))
-            padded = with_halo(current)
-            edge = 2 * HALO
-            lap = jnp.concatenate(
-                [laplace_x(padded[: edge + HALO]), inner, laplace_x(padded[padded.shape[0] - edge - HALO :])],
-                axis=0,
-            )
-            drive = speed_term * lap
-        else:
-            drive = speed_term * laplace_x(with_halo(current))
+        drive = speed_term * laplace_x(with_halo(current))
         if last:
             return None, drive
         later = inject(2.0 * current - prior + drive - absorber * (current - prior), moment)

time: 130 us -> 130 us (level)
  local copies, waits for them, and re-layouts: 20.7 us -> 18.9 us
    add x3, other arithmetic: 8.05 us -> 11.7 us  [inject(): return field + jnp.where(hit, source_gain[0] * wavelet[0, moment], 0.0)]
    add x3 -> x0, other arithmetic: 3.24 us -> none  [laplace_x(): total = total + STENCIL[reach] * beside_all]
    unnamed x55 -> x51, local copies, waits for them, and re-layouts: 5.27 us -> 3.59 us
  transfers between devices with their start and end apart: 30 -> 30, of which waited for: 15 -> 15; matrix products, arithmetic and copies ran while one was open for 28% -> 27% of each run, Pallas kernels for 0% -> 0%
where the time goes in v21:
time: 130 us
  waiting for transfers between devices  42.5 us (33%)
  other arithmetic  36 us (28%)
  starting transfers between devices  25.7 us (20%)
  local copies, waits for them, and re-layouts  18.9 us (15%)
  between operations  4.82 us (4%)
  matrix products  1.7 us (1%)
    ppermute x13, waiting for transfers between devices, ag_step(): theirs = lax.ppermute(held, 'shot', [(i, i ^ k) for i in range(n)])  20.8 us
    ppermute x8, waiting for transfers between devices, rs_step(): got = lax.ppermute(send, 'shot', [(i, i ^ k) for i in range(n)])  17.6 us
    ppermute x13, starting transfers between devices, ag_step(): theirs = lax.ppermute(held, 'shot', [(i, i ^ k) for i in range(n)])  13 us
    add x3, other arithmetic, inject(): return field + jnp.where(hit, source_gain[0] * wavelet[0, moment], 0.0)  11.7 us
    ppermute x8, starting transfers between devices, rs_step(): got = lax.ppermute(send, 'shot', [(i, i ^ k) for i in range(n)])  8.48 us
    add x2, other arithmetic, born_second(): 2.0 * born + speed_term * laplace_x(with_halo(born)) - absorber * born  5.85 us
    another operation x1, other arithmetic, damping(): lower = jnp.stack([edges[0], edges[2], edges[4]])[:, None]  3.86 us
    ppermute x2, waiting for transfers between devices, chain_step(): return keep + lax.ppermute(send, 'shot', [(i, i ^ k) for i in range(n)])  3.62 us
  transfers between devices with their start and end apart: 30, of which 15 were waited for; matrix products, arithmetic and copies ran while one was open for 27% of the time, Pallas kernels for 0%

profile of v21, /device:TPU:0, one launch (start us, length us, event | category | flops | bytes accessed | tf_op | source)
XLA Modules:
  0.0 129.6 jit_solution(6436935382056743507)
XLA Ops:
  0.7 1.7 %dynamic-slice_bitcast_fusion.10 = f32[4,64,128]{2,1,0:T(8,128)} fusion(f32[1,32,64,128]{3,2,1,0:T(8,128)} %param.12, s32[]{:T(128)S(6)} %select_n.404), kind=kLoop, calls=%fused_computation.356 | loop fusion | bytes 262148 | tf_op jit(solution)/shard_map/dynamic_slice | solution.py:51
  4.6 3.6 %collective-permute-start = (f32[1,16,2048]{2,1,0:T(8,128)}, f32[1,16,2048]{2,1,0:T(8,128)}, u32[]{:S(2)}, u32[]{:S(2)}) collective-permute-start(f32[1,16,2048]{2,1,0:T(8,128)} %concatenate.196), channel_id=1, source_target_pairs={{0,8},{2,10},{4,12},{6,14},{8,0},{10,2},{12,4},{14,6},{1,9},{3,11}... | collective-permute-start | bytes 393224 | tf_op jit(solution)/shard_map/ppermute | solution.py:120
  10.2 3.9 %pad_maximum_fusion.15 = (f32[3]{0:T(128)S(1)}, f32[3]{0:T(128)S(1)}) fusion(f32[1]{0:T(128)} %get-tuple-element.165, f32[1]{0:T(128)} %get-tuple-element.166, f32[1]{0:T(128)} %get-tuple-element.161, f32[1]{0:T(128)} %get-tuple-element.162, f32[1]{0:T(128)} %get-tuple-element.163, f32[1]{0:T(128)} %get-tuple-element.164), kind=kLoop, calls=%fused_computation.415 | loop fusion | flops 12 | bytes 48 | tf_op jit(solution)/shard_map/stack | solution.py:37
  22.3 4.5 %fusion.2 = (f32[32,64,128]{2,1,0:T(8,128)S(1)}, f32[32,64,128]{2,1,0:T(8,128)S(1)}) fusion(f32[]{:T(128)S(6)} %mul.319, f32[128]{0:T(128)} %slice_bitcast_fusion, f32[32,64]{1,0:T(8,128)S(1)} %broadcast_add_fusion, pred[128]{0:T(512)(128)(4,1)} %iota_compare_fusion.1, pred[32,64]{1,0:T(8,128)(4,1)} %broadcast_and_fusion, f32[1,32,64,128]{3,2,1,0:T(8,128)} %param.11, ...), kind=kLoop, calls=%fused_computation.118 | loop fusion | flops 12058624 | bytes 16009860 | tf_op jit(solution)/shard_map/add | solution.py:230
  26.8 1.1 maximum_select_fusion.4
  28.1 1.9 %collective-permute-start.5 = (f32[2,16,64]{2,1,0:T(8,128)S(1)}, f32[2,16,64]{2,1,0:T(8,128)S(1)}, u32[]{:S(2)}, u32[]{:S(2)}) collective-permute-start(f32[2,16,64]{2,1,0:T(8,128)S(1)} %maximum_select_fusion.12), channel_id=1, source_target_pairs={{0,4},{2,6},{4,0},{6,2},{8,12},{10,14},{12,8},{14,10},{1,5},{3,7},... | collective-permute-start | bytes 24584 | tf_op jit(solution)/shard_map/ppermute | solution.py:120
  30.1 1.6 %collective-permute-start.4 = (f32[2,8,2048]{2,1,0:T(8,128)S(1)}, f32[2,8,2048]{2,1,0:T(8,128)S(1)}, u32[]{:S(2)}, u32[]{:S(2)}) collective-permute-start(f32[2,8,2048]{2,1,0:T(8,128)S(1)} %get-tuple-element.154), channel_id=1, source_target_pairs={{0,2},{2,0},{4,6},{6,4},{8,10},{10,8},{12,14},{14,12},{1,3},{3,1},... | collective-permute-start | bytes 393224 | tf_op jit(solution)/shard_map/ppermute | solution.py:120
  32.3 2.9 %collective-permute-done.4 = f32[2,8,2048]{2,1,0:T(8,128)S(1)} collective-permute-done((f32[2,8,2048]{2,1,0:T(8,128)S(1)}, f32[2,8,2048]{2,1,0:T(8,128)S(1)}, u32[]{:S(2)}, u32[]{:S(2)}) %collective-permute-start.4) | collective-permute-done | bytes 131104 | tf_op jit(solution)/shard_map/ppermute | solution.py:120
  35.3 2.4 %collective-permute-done.3 = f32[2,8,2048]{2,1,0:T(8,128)S(1)} collective-permute-done((f32[2,8,2048]{2,1,0:T(8,128)S(1)}, f32[2,8,2048]{2,1,0:T(8,128)S(1)}, u32[]{:S(2)}, u32[]{:S(2)}) %collective-permute-start.3) | collective-permute-done | bytes 131104 | tf_op jit(solution)/shard_map/ppermute | solution.py:120
  37.8 3.2 %fusion.3 = (f32[32,64,128]{2,1,0:T(8,128)S(1)}, f32[32,64,128]{2,1,0:T(8,128)S(1)}) fusion(f32[32,64,128]{2,1,0:T(8,128)S(1)} %get-tuple-element.73, f32[32,64,128]{2,1,0:T(8,128)S(1)} %bitcast.197, f32[]{:T(128)S(6)} %mul.330, f32[128]{0:T(128)S(1)} %copy-done.14, f32[32,64]{1,0:T(8,128)S(1)} %broadcast_add_fusion, pred[128]{0:T(512)(128)(4,1)S(1)} %copy-done.17, ...), kind=kLoop, calls=%fused_computation.119 | loop fusion | flops 12058624 | bytes 16012292 | tf_op jit(solution)/shard_map/add | solution.py:230
  42.4 1.7 %collective-permute-start.7 = (f32[4,8,2048]{2,1,0:T(8,128)S(1)}, f32[4,8,2048]{2,1,0:T(8,128)S(1)}, u32[]{:S(2)}, u32[]{:S(2)}) collective-permute-start(f32[4,8,2048]{2,1,0:T(8,128)S(1)} %bitcast.223), channel_id=1, source_target_pairs={{0,2},{2,0},{4,6},{6,4},{8,10},{10,8},{12,14},{14,12},{1,3},{3,1},... | collective-permute-start | bytes 786440 | tf_op jit(solution)/shard_map/ppermute | solution.py:120
  46.4 4.0 %fusion.4 = (f32[32,64,128]{2,1,0:T(8,128)}, f32[32,64,128]{2,1,0:T(8,128)}) fusion(f32[32,64,128]{2,1,0:T(8,128)S(1)} %get-tuple-element.71, f32[32,64,128]{2,1,0:T(8,128)S(1)} %get-tuple-element.73, f32[]{:T(128)S(6)} %mul.339, f32[128]{0:T(128)S(1)} %copy-done.14, f32[32,64]{1,0:T(8,128)S(1)} %broadcast_add_fusion, pred[128]{0:T(512)(128)(4,1)S(1)} %copy-done.17, ...), kind=kLoop, calls=%fused_computation.120 | loop fusion | flops 12058624 | bytes 16012292 | tf_op jit(solution)/shard_map/add | solution.py:230
  51.0 1.1 pad_maximum_fusion.12
  52.1 2.5 %copy.48 = f32[2048,128]{1,0:T(8,128)} copy(f32[2048,128]{0,1:T(8,128)} %bitcast.205) | data formatting | bytes 2097152 | tf_op jit(solution)/shard_map/transpose | solution.py:315
  54.7 1.4 %mul.340 = f32[32,64,128]{2,1,0:T(8,128)S(1)} multiply(f32[32,64,128]{2,1,0:T(8,128)} %bitcast.199, f32[32,64,128]{2,1,0:T(8,128)S(1)} %get-tuple-element.84) | non-fusion elementwise | flops 262144 | bytes 3145728 | tf_op jit(solution)/shard_map/mul | solution.py:316
  56.2 1.3 %collective-permute-start.12 = (f32[4,4,32,128]{3,2,1,0:T(8,128)S(1)}, f32[4,4,32,128]{3,2,1,0:T(8,128)S(1)}, u32[]{:S(2)}, u32[]{:S(2)}) collective-permute-start(f32[4,4,32,128]{3,2,1,0:T(8,128)S(1)} %bitcast.233), channel_id=1, source_target_pairs={{0,4},{2,6},{4,0},{6,2},{8,12},{10,14},{12,8},{14,10},{1,5},{3,7},... | collective-permute-start | bytes 786440 | tf_op jit(solution)/shard_map/ppermute | solution.py:160
  57.5 1.5 %collective-permute-start.11 = (f32[4,4,32,128]{3,2,1,0:T(8,128)S(1)}, f32[4,4,32,128]{3,2,1,0:T(8,128)S(1)}, u32[]{:S(2)}, u32[]{:S(2)}) collective-permute-start(f32[4,4,32,128]{3,2,1,0:T(8,128)S(1)} %copy-done.10), channel_id=1, source_target_pairs={{0,2},{2,0},{4,6},{6,4},{8,10},{10,8},{12,14},{14,12},{1,3},{3,1},... | collective-permute-start | bytes 786440 | tf_op jit(solution)/shard_map/ppermute | solution.py:160
  59.3 2.9 %fusion.92 = f32[32,64,128]{2,1,0:T(8,128)S(1)} fusion(f32[40,64,128]{2,1,0:T(8,128)S(1)} %constant_dynamic-update-slice_fusion.2, f32[32,64,128]{2,1,0:T(8,128)S(1)} %bitcast.200, f32[32,64,128]{2,1,0:T(8,128)S(1)} %get-tuple-element.86, f32[32,64,128]{2,1,0:T(8,128)S(1)} %mul.340, f32[128]{0:T(128)S(1)} %copy-done.15, f32[32,64]{1,0:T(8,128)S(1)} %broadcast_add_fusion, ...), kind=kLoop, calls=%fused_computation.208 | loop fusion | flops 11272192 | bytes 16007680 | tf_op jit(solution)/shard_map/add | solution.py:241
  62.3 2.7 %collective-permute-done.12 = f32[4,4,32,128]{3,2,1,0:T(8,128)S(1)} collective-permute-done((f32[4,4,32,128]{3,2,1,0:T(8,128)S(1)}, f32[4,4,32,128]{3,2,1,0:T(8,128)S(1)}, u32[]{:S(2)}, u32[]{:S(2)}) %collective-permute-start.12) | collective-permute-done | bytes 262176 | tf_op jit(solution)/shard_map/ppermute | solution.py:160
  66.1 1.6 %collective-permute-start.17 = (f32[2,1,4,32,128]{4,3,2,0,1:T(8,128)S(1)}, f32[2,1,4,32,128]{4,3,2,0,1:T(8,128)S(1)}, u32[]{:S(2)}, u32[]{:S(2)}) collective-permute-start(f32[2,1,4,32,128]{4,3,2,0,1:T(8,128)S(1)} %dynamic-slice_bitcast_fusion.8), channel_id=1, source_target_pairs={{0,2},{2,0},{4,6},{6,4},{8,10},{10,8},{12,14},{14,12},{1,3},{3,1},... | collective-permute-start | bytes 393224 | tf_op jit(solution)/shard_map/ppermute | solution.py:186
  68.8 1.6 %collective-permute-start.15 = (f32[2,2,4,32,128]{4,3,2,1,0:T(8,128)S(1)}, f32[2,2,4,32,128]{4,3,2,1,0:T(8,128)S(1)}, u32[]{:S(2)}, u32[]{:S(2)}) collective-permute-start(f32[2,2,4,32,128]{4,3,2,1,0:T(8,128)S(1)} %dynamic-slice_bitcast_fusion), channel_id=1, source_target_pairs={{0,4},{2,6},{4,0},{6,2},{8,12},{10,14},{12,8},{14,10},{1,5},{3,7},... | collective-permute-start | bytes 786440 | tf_op jit(solution)/shard_map/ppermute | solution.py:186
  71.2 3.2 %fusion.117 = f32[32,64,128]{2,1,0:T(8,128)} fusion(f32[40,64,128]{2,1,0:T(8,128)S(1)} %constant_dynamic-update-slice_fusion.1, s32[32,64,128]{2,1,0:T(8,128)S(1)} %copy-done), kind=kLoop, calls=%fused_computation.233 | loop fusion | flops 9175040 | bytes 12845056 | tf_op jit(solution)/shard_map/mul | solution.py:233
  74.5 4.5 %collective-permute-done.15 = f32[2,2,4,32,128]{4,3,2,1,0:T(8,128)S(1)} collective-permute-done((f32[2,2,4,32,128]{4,3,2,1,0:T(8,128)S(1)}, f32[2,2,4,32,128]{4,3,2,1,0:T(8,128)S(1)}, u32[]{:S(2)}, u32[]{:S(2)}) %collective-permute-start.15) | collective-permute-done | bytes 262176 | tf_op jit(solution)/shard_map/ppermute | solution.py:186
  79.8 2.7 %collective-permute-start.21 = (f32[1,1,4,64,128]{4,3,2,1,0:T(8,128)S(1)}, f32[1,1,4,64,128]{4,3,2,1,0:T(8,128)S(1)}, u32[]{:S(2)}, u32[]{:S(2)}) collective-permute-start(f32[1,1,4,64,128]{4,3,2,1,0:T(8,128)S(1)} %dynamic-slice_bitcast_fusion.5), channel_id=1, source_target_pairs={{0,8},{2,10},{4,12},{6,14},{8,0},{10,2},{12,4},{14,6},{1,9},{3,11}... | collective-permute-start | bytes 393224 | tf_op jit(solution)/shard_map/ppermute | solution.py:186
  84.2 5.0 %collective-permute-done.19 = f32[2,1,4,32,128]{4,3,2,0,1:T(8,128)S(1)} collective-permute-done((f32[2,1,4,32,128]{4,3,2,0,1:T(8,128)S(1)}, f32[2,1,4,32,128]{4,3,2,0,1:T(8,128)S(1)}, u32[]{:S(2)}, u32[]{:S(2)}) %collective-permute-start.19) | collective-permute-done | bytes 131104 | tf_op jit(solution)/shard_map/ppermute | solution.py:186
  89.5 7.2 %collective-permute-done.22 = f32[1,1,4,64,128]{4,3,2,1,0:T(8,128)S(1)} collective-permute-done((f32[1,1,4,64,128]{4,3,2,1,0:T(8,128)S(1)}, f32[1,1,4,64,128]{4,3,2,1,0:T(8,128)S(1)}, u32[]{:S(2)}, u32[]{:S(2)}) %collective-permute-start.22) | collective-permute-done | bytes 131104 | tf_op jit(solution)/shard_map/ppermute | solution.py:186
  98.5 7.0 %collective-permute-done.23 = f32[1,4,64,128]{3,2,1,0:T(8,128)S(1)} collective-permute-done((f32[1,4,64,128]{3,2,1,0:T(8,128)S(1)}, f32[1,4,64,128]{3,2,1,0:T(8,128)S(1)}, u32[]{:S(2)}, u32[]{:S(2)}) %collective-permute-start.23) | collective-permute-done | bytes 131104 | tf_op jit(solution)/shard_map/ppermute | solution.py:120
  106.7 4.0 %collective-permute-done.25 = f32[2,4,32,128]{3,2,1,0:T(8,128)S(1)} collective-permute-done((f32[2,4,32,128]{3,2,1,0:T(8,128)S(1)}, f32[2,4,32,128]{3,2,1,0:T(8,128)S(1)}, u32[]{:S(2)}, u32[]{:S(2)}) %collective-permute-start.25) | collective-permute-done | bytes 131104 | tf_op jit(solution)/shard_map/ppermute | solution.py:120
  111.2 2.2 %collective-permute-start.26 = (f32[4,4,32,128]{3,2,1,0:T(8,128)S(1)}, f32[4,4,32,128]{3,2,1,0:T(8,128)S(1)}, u32[]{:S(2)}, u32[]{:S(2)}) collective-permute-start(f32[4,4,32,128]{3,2,1,0:T(8,128)S(1)} %bitcast.231), channel_id=1, source_target_pairs={{0,2},{2,0},{4,6},{6,4},{8,10},{10,8},{12,14},{14,12},{1,3},{3,1},... | collective-permute-start | bytes 786440 | tf_op jit(solution)/shard_map/ppermute | solution.py:120
  114.6 3.5 %collective-permute-done.26 = f32[4,4,32,128]{3,2,1,0:T(8,128)S(1)} collective-permute-done((f32[4,4,32,128]{3,2,1,0:T(8,128)S(1)}, f32[4,4,32,128]{3,2,1,0:T(8,128)S(1)}, u32[]{:S(2)}, u32[]{:S(2)}) %collective-permute-start.26) | collective-permute-done | bytes 262176 | tf_op jit(solution)/shard_map/ppermute | solution.py:120
  118.4 1.1 copy-done.3
  122.8 2.9 %fusion.145 = f32[32,64,128]{2,1,0:T(8,128)S(1)} fusion(f32[40,64,128]{2,1,0:T(8,128)S(1)} %constant_dynamic-update-slice_fusion, f32[32,64,128]{2,1,0:T(8,128)S(1)} %copy-done.7, f32[128]{0:T(128)S(1)} %copy-done.16, f32[32,64]{1,0:T(8,128)S(1)} %broadcast_add_fusion, f32[8,4,64,128]{3,2,1,0:T(8,128)S(1)} %pad_maximum_fusion.13, ...), kind=kLoop, calls=%fused_computation.261 | loop fusion | flops 11534336 | bytes 16007680 | tf_op jit(solution)/shard_map/add | solution.py:241
  (193 shorter events, 32.1 us)
Async XLA Ops:
  0.6 15.5 %copy-start.1 = (f32[1,32,64,128]{3,2,1,0:T(8,128)S(1)}, f32[1,32,64,128]{3,2,1,0:T(8,128)}, u32[]{:S(2)}) copy-start(f32[1,32,64,128]{3,2,1,0:T(8,128)} %param.12) | copy-start | bytes 3145732
  0.7 14.1 %copy-start.18 = (f32[1,4]{1,0:T(1,128)S(1)}, f32[1,4]{1,0:T(1,128)}, u32[]{:S(2)}) copy-start(f32[1,4]{1,0:T(1,128)} %param.16) | copy-start | bytes 52
  2.3 19.0 %collective-permute-start.2 = (f32[4,64,128]{2,1,0:T(8,128)}, f32[4,64,128]{2,1,0:T(8,128)}, u32[]{:S(2)}, u32[]{:S(2)}) collective-permute-start(f32[4,64,128]{2,1,0:T(8,128)} %dynamic-slice_bitcast_fusion.10), channel_id=1, source_target_pairs={{0,1},{1,0},{2,3},{3,2},{4,5},{5,4},{6,7},{7,6},{8,9},{9,8},{10,11... | collective-permute-start | bytes 393224 | tf_op jit(solution)/shard_map/ppermute | solution.py:52
  4.6 22.2 %collective-permute-start = (f32[1,16,2048]{2,1,0:T(8,128)}, f32[1,16,2048]{2,1,0:T(8,128)}, u32[]{:S(2)}, u32[]{:S(2)}) collective-permute-start(f32[1,16,2048]{2,1,0:T(8,128)} %concatenate.196), channel_id=1, source_target_pairs={{0,8},{2,10},{4,12},{6,14},{8,0},{10,2},{12,4},{14,6},{1,9},{3,11}... | collective-permute-start | bytes 393224 | tf_op jit(solution)/shard_map/ppermute | solution.py:120
  8.2 12.4 %collective-permute-start.1 = (f32[1,16,64]{2,1,0:T(8,128)}, f32[1,16,64]{2,1,0:T(8,128)}, u32[]{:S(2)}, u32[]{:S(2)}) collective-permute-start(f32[1,16,64]{2,1,0:T(8,128)} %bitcast.251), channel_id=1, source_target_pairs={{0,8},{2,10},{4,12},{6,14},{8,0},{10,2},{12,4},{14,6},{1,9},{3,11}... | collective-permute-start | bytes 12296 | tf_op jit(solution)/shard_map/ppermute | solution.py:120
  28.1 4.2 %collective-permute-start.5 = (f32[2,16,64]{2,1,0:T(8,128)S(1)}, f32[2,16,64]{2,1,0:T(8,128)S(1)}, u32[]{:S(2)}, u32[]{:S(2)}) collective-permute-start(f32[2,16,64]{2,1,0:T(8,128)S(1)} %maximum_select_fusion.12), channel_id=1, source_target_pairs={{0,4},{2,6},{4,0},{6,2},{8,12},{10,14},{12,8},{14,10},{1,5},{3,7},... | collective-permute-start | bytes 24584 | tf_op jit(solution)/shard_map/ppermute | solution.py:120
  30.1 5.1 %collective-permute-start.4 = (f32[2,8,2048]{2,1,0:T(8,128)S(1)}, f32[2,8,2048]{2,1,0:T(8,128)S(1)}, u32[]{:S(2)}, u32[]{:S(2)}) collective-permute-start(f32[2,8,2048]{2,1,0:T(8,128)S(1)} %get-tuple-element.154), channel_id=1, source_target_pairs={{0,2},{2,0},{4,6},{6,4},{8,10},{10,8},{12,14},{14,12},{1,3},{3,1},... | collective-permute-start | bytes 393224 | tf_op jit(solution)/shard_map/ppermute | solution.py:120
  31.7 6.0 %collective-permute-start.6 = (f32[4,64,128]{2,1,0:T(8,128)S(1)}, f32[4,64,128]{2,1,0:T(8,128)S(1)}, u32[]{:S(2)}, u32[]{:S(2)}) collective-permute-start(f32[4,64,128]{2,1,0:T(8,128)S(1)} %constant_dynamic-slice_fusion.7), channel_id=1, source_target_pairs={{0,1},{1,0},{2,3},{3,2},{4,5},{5,4},{6,7},{7,6},{8,9},{9,8},{10,11... | collective-permute-start | bytes 393224 | tf_op jit(solution)/shard_map/ppermute | solution.py:52
  31.8 5.9 %collective-permute-start.3 = (f32[2,8,2048]{2,1,0:T(8,128)S(1)}, f32[2,8,2048]{2,1,0:T(8,128)S(1)}, u32[]{:S(2)}, u32[]{:S(2)}) collective-permute-start(f32[2,8,2048]{2,1,0:T(8,128)S(1)} %get-tuple-element.155), channel_id=1, source_target_pairs={{0,4},{2,6},{4,0},{6,2},{8,12},{10,14},{12,8},{14,10},{1,5},{3,7},... | collective-permute-start | bytes 393224 | tf_op jit(solution)/shard_map/ppermute | solution.py:120
  41.5 5.0 %collective-permute-start.10 = (f32[4,64,128]{2,1,0:T(8,128)S(1)}, f32[4,64,128]{2,1,0:T(8,128)S(1)}, u32[]{:S(2)}, u32[]{:S(2)}) collective-permute-start(f32[4,64,128]{2,1,0:T(8,128)S(1)} %constant_dynamic-slice_fusion.6), channel_id=1, source_target_pairs={{0,1},{1,0},{2,3},{3,2},{4,5},{5,4},{6,7},{7,6},{8,9},{9,8},{10,11... | collective-permute-start | bytes 393224 | tf_op jit(solution)/shard_map/ppermute | solution.py:52
  41.5 4.3 %collective-permute-start.9 = (f32[4,16,64]{2,1,0:T(8,128)S(1)}, f32[4,16,64]{2,1,0:T(8,128)S(1)}, u32[]{:S(2)}, u32[]{:S(2)}) collective-permute-start(f32[4,16,64]{2,1,0:T(8,128)S(1)} %bitcast.244), channel_id=1, source_target_pairs={{0,2},{2,0},{4,6},{6,4},{8,10},{10,8},{12,14},{14,12},{1,3},{3,1},... | collective-permute-start | bytes 49160 | tf_op jit(solution)/shard_map/ppermute | solution.py:120
  42.1 8.4 %collective-permute-start.8 = (f32[4,8,2048]{2,1,0:T(8,128)S(1)}, f32[4,8,2048]{2,1,0:T(8,128)S(1)}, u32[]{:S(2)}, u32[]{:S(2)}) collective-permute-start(f32[4,8,2048]{2,1,0:T(8,128)S(1)} %bitcast.221), channel_id=1, source_target_pairs={{0,4},{2,6},{4,0},{6,2},{8,12},{10,14},{12,8},{14,10},{1,5},{3,7},... | collective-permute-start | bytes 786440 | tf_op jit(solution)/shard_map/ppermute | solution.py:120
  42.4 8.6 %collective-permute-start.7 = (f32[4,8,2048]{2,1,0:T(8,128)S(1)}, f32[4,8,2048]{2,1,0:T(8,128)S(1)}, u32[]{:S(2)}, u32[]{:S(2)}) collective-permute-start(f32[4,8,2048]{2,1,0:T(8,128)S(1)} %bitcast.223), channel_id=1, source_target_pairs={{0,2},{2,0},{4,6},{6,4},{8,10},{10,8},{12,14},{14,12},{1,3},{3,1},... | collective-permute-start | bytes 786440 | tf_op jit(solution)/shard_map/ppermute | solution.py:120
  56.1 3.1 %collective-permute-start.13 = (f32[4,64,128]{2,1,0:T(8,128)S(1)}, f32[4,64,128]{2,1,0:T(8,128)S(1)}, u32[]{:S(2)}, u32[]{:S(2)}) collective-permute-start(f32[4,64,128]{2,1,0:T(8,128)S(1)} %constant_dynamic-slice_fusion.3), channel_id=1, source_target_pairs={{0,1},{1,0},{2,3},{3,2},{4,5},{5,4},{6,7},{7,6},{8,9},{9,8},{10,11... | collective-permute-start | bytes 393224 | tf_op jit(solution)/shard_map/ppermute | solution.py:52
  56.2 8.7 %collective-permute-start.12 = (f32[4,4,32,128]{3,2,1,0:T(8,128)S(1)}, f32[4,4,32,128]{3,2,1,0:T(8,128)S(1)}, u32[]{:S(2)}, u32[]{:S(2)}) collective-permute-start(f32[4,4,32,128]{3,2,1,0:T(8,128)S(1)} %bitcast.233), channel_id=1, source_target_pairs={{0,4},{2,6},{4,0},{6,2},{8,12},{10,14},{12,8},{14,10},{1,5},{3,7},... | collective-permute-start | bytes 786440 | tf_op jit(solution)/shard_map/ppermute | solution.py:160
  57.5 8.4 %collective-permute-start.11 = (f32[4,4,32,128]{3,2,1,0:T(8,128)S(1)}, f32[4,4,32,128]{3,2,1,0:T(8,128)S(1)}, u32[]{:S(2)}, u32[]{:S(2)}) collective-permute-start(f32[4,4,32,128]{3,2,1,0:T(8,128)S(1)} %copy-done.10), channel_id=1, source_target_pairs={{0,2},{2,0},{4,6},{6,4},{8,10},{10,8},{12,14},{14,12},{1,3},{3,1},... | collective-permute-start | bytes 786440 | tf_op jit(solution)/shard_map/ppermute | solution.py:160
  66.0 5.1 %collective-permute-start.18 = (f32[4,64,128]{2,1,0:T(8,128)S(1)}, f32[4,64,128]{2,1,0:T(8,128)S(1)}, u32[]{:S(2)}, u32[]{:S(2)}) collective-permute-start(f32[4,64,128]{2,1,0:T(8,128)S(1)} %constant_dynamic-slice_fusion.2), channel_id=1, source_target_pairs={{0,1},{1,0},{2,3},{3,2},{4,5},{5,4},{6,7},{7,6},{8,9},{9,8},{10,11... | collective-permute-start | bytes 393224 | tf_op jit(solution)/shard_map/ppermute | solution.py:52
  66.1 8.3 %collective-permute-start.17 = (f32[2,1,4,32,128]{4,3,2,0,1:T(8,128)S(1)}, f32[2,1,4,32,128]{4,3,2,0,1:T(8,128)S(1)}, u32[]{:S(2)}, u32[]{:S(2)}) collective-permute-start(f32[2,1,4,32,128]{4,3,2,0,1:T(8,128)S(1)} %dynamic-slice_bitcast_fusion.8), channel_id=1, source_target_pairs={{0,2},{2,0},{4,6},{6,4},{8,10},{10,8},{12,14},{14,12},{1,3},{3,1},... | collective-permute-start | bytes 393224 | tf_op jit(solution)/shard_map/ppermute | solution.py:186
  67.7 6.7 %collective-permute-start.16 = (f32[2,1,4,32,128]{4,3,2,0,1:T(8,128)S(1)}, f32[2,1,4,32,128]{4,3,2,0,1:T(8,128)S(1)}, u32[]{:S(2)}, u32[]{:S(2)}) collective-permute-start(f32[2,1,4,32,128]{4,3,2,0,1:T(8,128)S(1)} %dynamic-slice_bitcast_fusion.9), channel_id=1, source_target_pairs={{0,4},{2,6},{4,0},{6,2},{8,12},{10,14},{12,8},{14,10},{1,5},{3,7},... | collective-permute-start | bytes 393224 | tf_op jit(solution)/shard_map/ppermute | solution.py:186
  68.8 10.2 %collective-permute-start.15 = (f32[2,2,4,32,128]{4,3,2,1,0:T(8,128)S(1)}, f32[2,2,4,32,128]{4,3,2,1,0:T(8,128)S(1)}, u32[]{:S(2)}, u32[]{:S(2)}) collective-permute-start(f32[2,2,4,32,128]{4,3,2,1,0:T(8,128)S(1)} %dynamic-slice_bitcast_fusion), channel_id=1, source_target_pairs={{0,4},{2,6},{4,0},{6,2},{8,12},{10,14},{12,8},{14,10},{1,5},{3,7},... | collective-permute-start | bytes 786440 | tf_op jit(solution)/shard_map/ppermute | solution.py:186
  70.4 8.6 %collective-permute-start.14 = (f32[4,1,4,32,128]{4,3,2,0,1:T(8,128)S(1)}, f32[4,1,4,32,128]{4,3,2,0,1:T(8,128)S(1)}, u32[]{:S(2)}, u32[]{:S(2)}) collective-permute-start(f32[4,1,4,32,128]{4,3,2,0,1:T(8,128)S(1)} %dynamic-slice_bitcast_fusion.1), channel_id=1, source_target_pairs={{0,2},{2,0},{4,6},{6,4},{8,10},{10,8},{12,14},{14,12},{1,3},{3,1},... | collective-permute-start | bytes 786440 | tf_op jit(solution)/shard_map/ppermute | solution.py:186
  79.1 5.0 %collective-permute-start.20 = (f32[2,1,4,32,128]{4,3,2,0,1:T(8,128)S(1)}, f32[2,1,4,32,128]{4,3,2,0,1:T(8,128)S(1)}, u32[]{:S(2)}, u32[]{:S(2)}) collective-permute-start(f32[2,1,4,32,128]{4,3,2,0,1:T(8,128)S(1)} %dynamic-slice_bitcast_fusion.6), channel_id=1, source_target_pairs={{0,2},{2,0},{4,6},{6,4},{8,10},{10,8},{12,14},{14,12},{1,3},{3,1},... | collective-permute-start | bytes 393224 | tf_op jit(solution)/shard_map/ppermute | solution.py:186
  79.8 9.5 %collective-permute-start.21 = (f32[1,1,4,64,128]{4,3,2,1,0:T(8,128)S(1)}, f32[1,1,4,64,128]{4,3,2,1,0:T(8,128)S(1)}, u32[]{:S(2)}, u32[]{:S(2)}) collective-permute-start(f32[1,1,4,64,128]{4,3,2,1,0:T(8,128)S(1)} %dynamic-slice_bitcast_fusion.5), channel_id=1, source_target_pairs={{0,8},{2,10},{4,12},{6,14},{8,0},{10,2},{12,4},{14,6},{1,9},{3,11}... | collective-permute-start | bytes 393224 | tf_op jit(solution)/shard_map/ppermute | solution.py:186
  82.4 6.8 %collective-permute-start.19 = (f32[2,1,4,32,128]{4,3,2,0,1:T(8,128)S(1)}, f32[2,1,4,32,128]{4,3,2,0,1:T(8,128)S(1)}, u32[]{:S(2)}, u32[]{:S(2)}) collective-permute-start(f32[2,1,4,32,128]{4,3,2,0,1:T(8,128)S(1)} %dynamic-slice_bitcast_fusion.7), channel_id=1, source_target_pairs={{0,4},{2,6},{4,0},{6,2},{8,12},{10,14},{12,8},{14,10},{1,5},{3,7},... | collective-permute-start | bytes 393224 | tf_op jit(solution)/shard_map/ppermute | solution.py:186
  89.4 7.3 %collective-permute-start.22 = (f32[1,1,4,64,128]{4,3,2,1,0:T(8,128)S(1)}, f32[1,1,4,64,128]{4,3,2,1,0:T(8,128)S(1)}, u32[]{:S(2)}, u32[]{:S(2)}) collective-permute-start(f32[1,1,4,64,128]{4,3,2,1,0:T(8,128)S(1)} %dynamic-slice_bitcast_fusion.4), channel_id=1, source_target_pairs={{0,8},{2,10},{4,12},{6,14},{8,0},{10,2},{12,4},{14,6},{1,9},{3,11}... | collective-permute-start | bytes 393224 | tf_op jit(solution)/shard_map/ppermute | solution.py:186
  98.4 7.2 %collective-permute-start.23 = (f32[1,4,64,128]{3,2,1,0:T(8,128)S(1)}, f32[1,4,64,128]{3,2,1,0:T(8,128)S(1)}, u32[]{:S(2)}, u32[]{:S(2)}) collective-permute-start(f32[1,4,64,128]{3,2,1,0:T(8,128)S(1)} %fusion.1), channel_id=1, source_target_pairs={{0,8},{2,10},{4,12},{6,14},{8,0},{10,2},{12,4},{14,6},{1,9},{3,11}... | collective-permute-start | bytes 393224 | tf_op jit(solution)/shard_map/ppermute | solution.py:120
  105.7 5.0 %collective-permute-start.25 = (f32[2,4,32,128]{3,2,1,0:T(8,128)S(1)}, f32[2,4,32,128]{3,2,1,0:T(8,128)S(1)}, u32[]{:S(2)}, u32[]{:S(2)}) collective-permute-start(f32[2,4,32,128]{3,2,1,0:T(8,128)S(1)} %get-tuple-element.150), channel_id=1, source_target_pairs={{0,2},{2,0},{4,6},{6,4},{8,10},{10,8},{12,14},{14,12},{1,3},{3,1},... | collective-permute-start | bytes 393224 | tf_op jit(solution)/shard_map/ppermute | solution.py:120
  106.1 5.0 %collective-permute-start.24 = (f32[2,4,32,128]{3,2,1,0:T(8,128)S(1)}, f32[2,4,32,128]{3,2,1,0:T(8,128)S(1)}, u32[]{:S(2)}, u32[]{:S(2)}) collective-permute-start(f32[2,4,32,128]{3,2,1,0:T(8,128)S(1)} %get-tuple-element.151), channel_id=1, source_target_pairs={{0,4},{2,6},{4,0},{6,2},{8,12},{10,14},{12,8},{14,10},{1,5},{3,7},... | collective-permute-start | bytes 393224 | tf_op jit(solution)/shard_map/ppermute | solution.py:120
  111.2 7.0 %collective-permute-start.27 = (f32[4,4,32,128]{3,2,1,0:T(8,128)S(1)}, f32[4,4,32,128]{3,2,1,0:T(8,128)S(1)}, u32[]{:S(2)}, u32[]{:S(2)}) collective-permute-start(f32[4,4,32,128]{3,2,1,0:T(8,128)S(1)} %bitcast.225), channel_id=1, source_target_pairs={{0,4},{2,6},{4,0},{6,2},{8,12},{10,14},{12,8},{14,10},{1,5},{3,7},... | collective-permute-start | bytes 786440 | tf_op jit(solution)/shard_map/ppermute | solution.py:120
  111.2 6.9 %collective-permute-start.26 = (f32[4,4,32,128]{3,2,1,0:T(8,128)S(1)}, f32[4,4,32,128]{3,2,1,0:T(8,128)S(1)}, u32[]{:S(2)}, u32[]{:S(2)}) collective-permute-start(f32[4,4,32,128]{3,2,1,0:T(8,128)S(1)} %bitcast.231), channel_id=1, source_target_pairs={{0,2},{2,0},{4,6},{6,4},{8,10},{10,8},{12,14},{14,12},{1,3},{3,1},... | collective-permute-start | bytes 786440 | tf_op jit(solution)/shard_map/ppermute | solution.py:120
  120.4 1.6 %collective-permute-start.28 = (f32[4,64,128]{2,1,0:T(8,128)}, f32[4,64,128]{2,1,0:T(8,128)S(1)}, u32[]{:S(2)}, u32[]{:S(2)}) collective-permute-start(f32[4,64,128]{2,1,0:T(8,128)} %constant_dynamic-slice_fusion), channel_id=1, source_target_pairs={{0,1},{1,0},{2,3},{3,2},{4,5},{5,4},{6,7},{7,6},{8,9},{9,8},{10,11... | collective-permute-start | bytes 393224 | tf_op jit(solution)/shard_map/ppermute | solution.py:52
  127.0 1.9 %collective-permute-start.29 = (f32[1,2,256]{2,1,0:T(2,128)S(1)}, f32[1,2,256]{2,1,0:T(2,128)S(1)}, u32[]{:S(2)}, u32[]{:S(2)}) collective-permute-start(f32[1,2,256]{2,1,0:T(2,128)S(1)} %maximum_bitcast_fusion), channel_id=1, source_target_pairs={{0,1},{1,0},{2,3},{3,2},{4,5},{5,4},{6,7},{7,6},{8,9},{9,8},{10,11... | collective-permute-start | bytes 6152 | tf_op jit(solution)/shard_map/ppermute | solution.py:379
  (22 other events, 101.6 us)

commit v22 on v15

--- a/solution.py
+++ b/solution.py
@@ -94,12 +94,12 @@
     angle = 2.0 * math.pi / count * phase.astype(jnp.float32)
     cosine = jnp.cos(angle)
     sine = jnp.sin(angle)
-    real_part = jnp.einsum("xyz,yk->xzk", field, cosine, precision=lax.Precision.HIGHEST)
-    imag_part = jnp.einsum("xyz,yk->xzk", field, sine, precision=lax.Precision.HIGHEST)
+    real_part = jnp.einsum("xyz,yk->xzk", field, cosine, precision=lax.Precision.HIGH)
+    imag_part = jnp.einsum("xyz,yk->xzk", field, sine, precision=lax.Precision.HIGH)
     weight = table[None, :, :]
-    back = jnp.einsum("xzk,yk->xyz", real_part * weight, cosine, precision=lax.Precision.HIGHEST)
+    back = jnp.einsum("xzk,yk->xyz", real_part * weight, cosine, precision=lax.Precision.HIGH)
     back = back + jnp.einsum(
-        "xzk,yk->xyz", imag_part * weight, sine, precision=lax.Precision.HIGHEST
+        "xzk,yk->xyz", imag_part * weight, sine, precision=lax.Precision.HIGH
     )
     return back / count
 

time: 130 us -> 130 us (level)
  no operation moved by 1% of the time
where the time goes in v22:
time: 130 us; the launch traced here: 129 us
  waiting for transfers between devices  41.9 us (32%)
  other arithmetic  34.8 us (27%)
  starting transfers between devices  25.6 us (20%)
  local copies, waits for them, and re-layouts  20.7 us (16%)
  between operations  4.71 us (4%)
  matrix products  1.41 us (1%)
    ppermute x13, waiting for transfers between devices, ag_step(): theirs = lax.ppermute(held, 'shot', [(i, i ^ k) for i in range(n)])  20.8 us
    ppermute x8, waiting for transfers between devices, rs_step(): got = lax.ppermute(send, 'shot', [(i, i ^ k) for i in range(n)])  17.6 us
    ppermute x13, starting transfers between devices, ag_step(): theirs = lax.ppermute(held, 'shot', [(i, i ^ k) for i in range(n)])  13 us
    ppermute x8, starting transfers between devices, rs_step(): got = lax.ppermute(send, 'shot', [(i, i ^ k) for i in range(n)])  8.48 us
    add x3, other arithmetic, inject(): return field + jnp.where(hit, source_gain[0] * wavelet[0, moment], 0.0)  8.05 us
    add x2, other arithmetic, born_second(): 2.0 * born + speed_term * laplace_x(with_halo(born)) - absorber * born  5.83 us
    unnamed x55, local copies, waits for them, and re-layouts  5.27 us
    another operation x1, other arithmetic, damping(): lower = jnp.stack([edges[0], edges[2], edges[4]])[:, None]  3.74 us
  transfers between devices with their start and end apart: 30, of which 15 were waited for; matrix products, arithmetic and copies ran while one was open for 28% of the time, Pallas kernels for 0%

profile of v22, /device:TPU:0, one launch (start us, length us, event | category | flops | bytes accessed | tf_op | source)
XLA Modules:
  0.0 129.1 jit_solution(12243257202657866856)
XLA Ops:
  0.7 1.7 %dynamic-slice_bitcast_fusion.10 = f32[4,64,128]{2,1,0:T(8,128)} fusion(f32[1,32,64,128]{3,2,1,0:T(8,128)} %param.12, s32[]{:T(128)S(6)} %select_n.404), kind=kLoop, calls=%fused_computation.441 | loop fusion | bytes 262148 | tf_op jit(solution)/shard_map/dynamic_slice | solution.py:51
  2.8 1.0 copy.38
  4.6 3.6 %collective-permute-start = (f32[1,16,2048]{2,1,0:T(8,128)}, f32[1,16,2048]{2,1,0:T(8,128)}, u32[]{:S(2)}, u32[]{:S(2)}) collective-permute-start(f32[1,16,2048]{2,1,0:T(8,128)} %concatenate.199), channel_id=1, source_target_pairs={{0,8},{2,10},{4,12},{6,14},{8,0},{10,2},{12,4},{14,6},{1,9},{3,11}... | collective-permute-start | bytes 393224 | tf_op jit(solution)/shard_map/ppermute | solution.py:120
  10.2 3.7 %pad_maximum_fusion.15 = (f32[3]{0:T(128)S(1)}, f32[3]{0:T(128)S(1)}) fusion(f32[1]{0:T(128)} %get-tuple-element.167, f32[1]{0:T(128)} %get-tuple-element.168, f32[1]{0:T(128)} %get-tuple-element.163, f32[1]{0:T(128)} %get-tuple-element.164, f32[1]{0:T(128)} %get-tuple-element.165, f32[1]{0:T(128)} %get-tuple-element.166), kind=kLoop, calls=%fused_computation.500 | loop fusion | flops 12 | bytes 48 | tf_op jit(solution)/shard_map/stack | solution.py:37
  16.3 2.6 %fusion.144 = f32[24,64,128]{2,1,0:T(8,128)} fusion(f32[32,64,128]{2,1,0:T(8,128)S(1)} %bitcast.205, f32[1,32,64,128]{3,2,1,0:T(8,128)S(1)} %copy-done), kind=kLoop, calls=%fused_computation.324 | loop fusion | flops 5701632 | bytes 8912896 | tf_op jit(solution)/shard_map/add | solution.py:86
  28.2 1.1 maximum_select_fusion.4
  29.5 1.9 %collective-permute-start.5 = (f32[2,16,64]{2,1,0:T(8,128)S(1)}, f32[2,16,64]{2,1,0:T(8,128)S(1)}, u32[]{:S(2)}, u32[]{:S(2)}) collective-permute-start(f32[2,16,64]{2,1,0:T(8,128)S(1)} %maximum_select_fusion.12), channel_id=1, source_target_pairs={{0,4},{2,6},{4,0},{6,2},{8,12},{10,14},{12,8},{14,10},{1,5},{3,7},... | collective-permute-start | bytes 24584 | tf_op jit(solution)/shard_map/ppermute | solution.py:120
  31.5 1.6 %collective-permute-start.4 = (f32[2,8,2048]{2,1,0:T(8,128)S(1)}, f32[2,8,2048]{2,1,0:T(8,128)S(1)}, u32[]{:S(2)}, u32[]{:S(2)}) collective-permute-start(f32[2,8,2048]{2,1,0:T(8,128)S(1)} %get-tuple-element.156), channel_id=1, source_target_pairs={{0,2},{2,0},{4,6},{6,4},{8,10},{10,8},{12,14},{14,12},{1,3},{3,1},... | collective-permute-start | bytes 393224 | tf_op jit(solution)/shard_map/ppermute | solution.py:120
  33.7 2.9 %collective-permute-done.4 = f32[2,8,2048]{2,1,0:T(8,128)S(1)} collective-permute-done((f32[2,8,2048]{2,1,0:T(8,128)S(1)}, f32[2,8,2048]{2,1,0:T(8,128)S(1)}, u32[]{:S(2)}, u32[]{:S(2)}) %collective-permute-start.4) | collective-permute-done | bytes 131104 | tf_op jit(solution)/shard_map/ppermute | solution.py:120
  36.6 2.4 %collective-permute-done.3 = f32[2,8,2048]{2,1,0:T(8,128)S(1)} collective-permute-done((f32[2,8,2048]{2,1,0:T(8,128)S(1)}, f32[2,8,2048]{2,1,0:T(8,128)S(1)}, u32[]{:S(2)}, u32[]{:S(2)}) %collective-permute-start.3) | collective-permute-done | bytes 131104 | tf_op jit(solution)/shard_map/ppermute | solution.py:120
  39.1 3.2 %fusion.3 = (f32[32,64,128]{2,1,0:T(8,128)S(1)}, f32[32,64,128]{2,1,0:T(8,128)S(1)}) fusion(f32[32,64,128]{2,1,0:T(8,128)S(1)} %get-tuple-element.73, f32[32,64,128]{2,1,0:T(8,128)S(1)} %bitcast.207, f32[]{:T(128)S(6)} %mul.394, f32[128]{0:T(128)S(1)} %copy-done.16, f32[32,64]{1,0:T(8,128)S(1)} %broadcast_add_fusion, pred[128]{0:T(512)(128)(4,1)S(1)} %copy-done.19, ...), kind=kLoop, calls=%fused_computation.151 | loop fusion | flops 12058624 | bytes 16012292 | tf_op jit(solution)/shard_map/add | solution.py:230
  44.5 1.7 %collective-permute-start.7 = (f32[4,8,2048]{2,1,0:T(8,128)S(1)}, f32[4,8,2048]{2,1,0:T(8,128)S(1)}, u32[]{:S(2)}, u32[]{:S(2)}) collective-permute-start(f32[4,8,2048]{2,1,0:T(8,128)S(1)} %bitcast.234), channel_id=1, source_target_pairs={{0,2},{2,0},{4,6},{6,4},{8,10},{10,8},{12,14},{14,12},{1,3},{3,1},... | collective-permute-start | bytes 786440 | tf_op jit(solution)/shard_map/ppermute | solution.py:120
  48.6 4.0 %fusion.4 = (f32[32,64,128]{2,1,0:T(8,128)}, f32[32,64,128]{2,1,0:T(8,128)}) fusion(f32[32,64,128]{2,1,0:T(8,128)S(1)} %get-tuple-element.71, f32[32,64,128]{2,1,0:T(8,128)S(1)} %get-tuple-element.73, f32[]{:T(128)S(6)} %mul.403, f32[128]{0:T(128)S(1)} %copy-done.16, f32[32,64]{1,0:T(8,128)S(1)} %broadcast_add_fusion, pred[128]{0:T(512)(128)(4,1)S(1)} %copy-done.19, ...), kind=kLoop, calls=%fused_computation.152 | loop fusion | flops 12058624 | bytes 16012292 | tf_op jit(solution)/shard_map/add | solution.py:230
  53.2 1.1 pad_maximum_fusion.12
  54.2 1.5 %copy.48 = f32[2048,128]{1,0:T(8,128)S(1)} copy(f32[2048,128]{0,1:T(8,128)} %bitcast.216) | data formatting | bytes 2097152 | tf_op jit(solution)/shard_map/transpose | solution.py:325
  56.7 1.3 collective-permute-start.12
  58.0 1.5 %collective-permute-start.11 = (f32[4,4,32,128]{3,2,1,0:T(8,128)S(1)}, f32[4,4,32,128]{3,2,1,0:T(8,128)S(1)}, u32[]{:S(2)}, u32[]{:S(2)}) collective-permute-start(f32[4,4,32,128]{3,2,1,0:T(8,128)S(1)} %copy-done.12), channel_id=1, source_target_pairs={{0,2},{2,0},{4,6},{6,4},{8,10},{10,8},{12,14},{14,12},{1,3},{3,1},... | collective-permute-start | bytes 786440 | tf_op jit(solution)/shard_map/ppermute | solution.py:160
  59.8 2.9 %fusion.67 = f32[32,64,128]{2,1,0:T(8,128)S(1)} fusion(f32[40,64,128]{2,1,0:T(8,128)S(1)} %constant_dynamic-update-slice_fusion.2, f32[32,64,128]{2,1,0:T(8,128)S(1)} %bitcast.211, f32[32,64,128]{2,1,0:T(8,128)S(1)} %copy-done.3, f32[32,64,128]{2,1,0:T(8,128)S(1)} %mul.404, f32[128]{0:T(128)S(1)} %copy-done.17, f32[32,64]{1,0:T(8,128)S(1)} %broadcast_add_fusion, ...), kind=kLoop, calls=%fused_computation.215 | loop fusion | flops 11272192 | bytes 16007680 | tf_op jit(solution)/shard_map/add | solution.py:251
  62.7 2.1 %collective-permute-done.12 = f32[4,4,32,128]{3,2,1,0:T(8,128)S(1)} collective-permute-done((f32[4,4,32,128]{3,2,1,0:T(8,128)S(1)}, f32[4,4,32,128]{3,2,1,0:T(8,128)S(1)}, u32[]{:S(2)}, u32[]{:S(2)}) %collective-permute-start.12) | collective-permute-done | bytes 262176 | tf_op jit(solution)/shard_map/ppermute | solution.py:160
  66.0 1.6 %collective-permute-start.17 = (f32[2,1,4,32,128]{4,3,2,0,1:T(8,128)S(1)}, f32[2,1,4,32,128]{4,3,2,0,1:T(8,128)S(1)}, u32[]{:S(2)}, u32[]{:S(2)}) collective-permute-start(f32[2,1,4,32,128]{4,3,2,0,1:T(8,128)S(1)} %dynamic-slice_bitcast_fusion.8), channel_id=1, source_target_pairs={{0,2},{2,0},{4,6},{6,4},{8,10},{10,8},{12,14},{14,12},{1,3},{3,1},... | collective-permute-start | bytes 393224 | tf_op jit(solution)/shard_map/ppermute | solution.py:186
  68.7 1.6 %collective-permute-start.15 = (f32[2,2,4,32,128]{4,3,2,1,0:T(8,128)S(1)}, f32[2,2,4,32,128]{4,3,2,1,0:T(8,128)S(1)}, u32[]{:S(2)}, u32[]{:S(2)}) collective-permute-start(f32[2,2,4,32,128]{4,3,2,1,0:T(8,128)S(1)} %dynamic-slice_bitcast_fusion), channel_id=1, source_target_pairs={{0,4},{2,6},{4,0},{6,2},{8,12},{10,14},{12,8},{14,10},{1,5},{3,7},... | collective-permute-start | bytes 786440 | tf_op jit(solution)/shard_map/ppermute | solution.py:186
  71.0 3.2 %fusion.92 = f32[32,64,128]{2,1,0:T(8,128)} fusion(f32[40,64,128]{2,1,0:T(8,128)S(1)} %constant_dynamic-update-slice_fusion.1, s32[32,64,128]{2,1,0:T(8,128)S(1)} %copy-done.1), kind=kLoop, calls=%fused_computation.240 | loop fusion | flops 9175040 | bytes 12845056 | tf_op jit(solution)/shard_map/mul | solution.py:243
  74.4 4.5 %collective-permute-done.15 = f32[2,2,4,32,128]{4,3,2,1,0:T(8,128)S(1)} collective-permute-done((f32[2,2,4,32,128]{4,3,2,1,0:T(8,128)S(1)}, f32[2,2,4,32,128]{4,3,2,1,0:T(8,128)S(1)}, u32[]{:S(2)}, u32[]{:S(2)}) %collective-permute-start.15) | collective-permute-done | bytes 262176 | tf_op jit(solution)/shard_map/ppermute | solution.py:186
  79.6 2.7 %collective-permute-start.21 = (f32[1,1,4,64,128]{4,3,2,1,0:T(8,128)S(1)}, f32[1,1,4,64,128]{4,3,2,1,0:T(8,128)S(1)}, u32[]{:S(2)}, u32[]{:S(2)}) collective-permute-start(f32[1,1,4,64,128]{4,3,2,1,0:T(8,128)S(1)} %dynamic-slice_bitcast_fusion.5), channel_id=1, source_target_pairs={{0,8},{2,10},{4,12},{6,14},{8,0},{10,2},{12,4},{14,6},{1,9},{3,11}... | collective-permute-start | bytes 393224 | tf_op jit(solution)/shard_map/ppermute | solution.py:186
  84.1 5.0 %collective-permute-done.19 = f32[2,1,4,32,128]{4,3,2,0,1:T(8,128)S(1)} collective-permute-done((f32[2,1,4,32,128]{4,3,2,0,1:T(8,128)S(1)}, f32[2,1,4,32,128]{4,3,2,0,1:T(8,128)S(1)}, u32[]{:S(2)}, u32[]{:S(2)}) %collective-permute-start.19) | collective-permute-done | bytes 131104 | tf_op jit(solution)/shard_map/ppermute | solution.py:186
  89.4 7.2 %collective-permute-done.22 = f32[1,1,4,64,128]{4,3,2,1,0:T(8,128)S(1)} collective-permute-done((f32[1,1,4,64,128]{4,3,2,1,0:T(8,128)S(1)}, f32[1,1,4,64,128]{4,3,2,1,0:T(8,128)S(1)}, u32[]{:S(2)}, u32[]{:S(2)}) %collective-permute-start.22) | collective-permute-done | bytes 131104 | tf_op jit(solution)/shard_map/ppermute | solution.py:186
  98.1 7.0 %collective-permute-done.23 = f32[1,4,64,128]{3,2,1,0:T(8,128)S(1)} collective-permute-done((f32[1,4,64,128]{3,2,1,0:T(8,128)S(1)}, f32[1,4,64,128]{3,2,1,0:T(8,128)S(1)}, u32[]{:S(2)}, u32[]{:S(2)}) %collective-permute-start.23) | collective-permute-done | bytes 131104 | tf_op jit(solution)/shard_map/ppermute | solution.py:120
  106.3 4.0 %collective-permute-done.25 = f32[2,4,32,128]{3,2,1,0:T(8,128)S(1)} collective-permute-done((f32[2,4,32,128]{3,2,1,0:T(8,128)S(1)}, f32[2,4,32,128]{3,2,1,0:T(8,128)S(1)}, u32[]{:S(2)}, u32[]{:S(2)}) %collective-permute-start.25) | collective-permute-done | bytes 131104 | tf_op jit(solution)/shard_map/ppermute | solution.py:120
  110.8 2.2 %collective-permute-start.26 = (f32[4,4,32,128]{3,2,1,0:T(8,128)S(1)}, f32[4,4,32,128]{3,2,1,0:T(8,128)S(1)}, u32[]{:S(2)}, u32[]{:S(2)}) collective-permute-start(f32[4,4,32,128]{3,2,1,0:T(8,128)S(1)} %bitcast.242), channel_id=1, source_target_pairs={{0,2},{2,0},{4,6},{6,4},{8,10},{10,8},{12,14},{14,12},{1,3},{3,1},... | collective-permute-start | bytes 786440 | tf_op jit(solution)/shard_map/ppermute | solution.py:120
  114.2 3.5 %collective-permute-done.26 = f32[4,4,32,128]{3,2,1,0:T(8,128)S(1)} collective-permute-done((f32[4,4,32,128]{3,2,1,0:T(8,128)S(1)}, f32[4,4,32,128]{3,2,1,0:T(8,128)S(1)}, u32[]{:S(2)}, u32[]{:S(2)}) %collective-permute-start.26) | collective-permute-done | bytes 262176 | tf_op jit(solution)/shard_map/ppermute | solution.py:120
  117.9 1.1 copy-done.4
  122.3 2.9 %fusion.120 = f32[32,64,128]{2,1,0:T(8,128)S(1)} fusion(f32[40,64,128]{2,1,0:T(8,128)S(1)} %constant_dynamic-update-slice_fusion, f32[32,64,128]{2,1,0:T(8,128)S(1)} %copy-done.7, f32[128]{0:T(128)S(1)} %copy-done.18, f32[32,64]{1,0:T(8,128)S(1)} %broadcast_add_fusion, f32[8,4,64,128]{3,2,1,0:T(8,128)S(1)} %pad_maximum_fusion.13, ...), kind=kLoop, calls=%fused_computation.268 | loop fusion | flops 11534336 | bytes 16007680 | tf_op jit(solution)/shard_map/add | solution.py:251
  (201 shorter events, 35.9 us)
Async XLA Ops:
  0.6 15.7 %copy-start = (f32[1,32,64,128]{3,2,1,0:T(8,128)S(1)}, f32[1,32,64,128]{3,2,1,0:T(8,128)}, u32[]{:S(2)}) copy-start(f32[1,32,64,128]{3,2,1,0:T(8,128)} %param.12) | copy-start | bytes 3145732
  0.7 15.1 %copy-start.20 = (f32[1,4]{1,0:T(1,128)S(1)}, f32[1,4]{1,0:T(1,128)}, u32[]{:S(2)}) copy-start(f32[1,4]{1,0:T(1,128)} %param.16) | copy-start | bytes 52
  2.3 22.5 %collective-permute-start.2 = (f32[4,64,128]{2,1,0:T(8,128)}, f32[4,64,128]{2,1,0:T(8,128)}, u32[]{:S(2)}, u32[]{:S(2)}) collective-permute-start(f32[4,64,128]{2,1,0:T(8,128)} %dynamic-slice_bitcast_fusion.10), channel_id=1, source_target_pairs={{0,1},{1,0},{2,3},{3,2},{4,5},{5,4},{6,7},{7,6},{8,9},{9,8},{10,11... | collective-permute-start | bytes 393224 | tf_op jit(solution)/shard_map/ppermute | solution.py:52
  4.6 23.6 %collective-permute-start = (f32[1,16,2048]{2,1,0:T(8,128)}, f32[1,16,2048]{2,1,0:T(8,128)}, u32[]{:S(2)}, u32[]{:S(2)}) collective-permute-start(f32[1,16,2048]{2,1,0:T(8,128)} %concatenate.199), channel_id=1, source_target_pairs={{0,8},{2,10},{4,12},{6,14},{8,0},{10,2},{12,4},{14,6},{1,9},{3,11}... | collective-permute-start | bytes 393224 | tf_op jit(solution)/shard_map/ppermute | solution.py:120
  8.2 15.8 %collective-permute-start.1 = (f32[1,16,64]{2,1,0:T(8,128)}, f32[1,16,64]{2,1,0:T(8,128)}, u32[]{:S(2)}, u32[]{:S(2)}) collective-permute-start(f32[1,16,64]{2,1,0:T(8,128)} %bitcast.262), channel_id=1, source_target_pairs={{0,8},{2,10},{4,12},{6,14},{8,0},{10,2},{12,4},{14,6},{1,9},{3,11}... | collective-permute-start | bytes 12296 | tf_op jit(solution)/shard_map/ppermute | solution.py:120
  29.5 4.2 %collective-permute-start.5 = (f32[2,16,64]{2,1,0:T(8,128)S(1)}, f32[2,16,64]{2,1,0:T(8,128)S(1)}, u32[]{:S(2)}, u32[]{:S(2)}) collective-permute-start(f32[2,16,64]{2,1,0:T(8,128)S(1)} %maximum_select_fusion.12), channel_id=1, source_target_pairs={{0,4},{2,6},{4,0},{6,2},{8,12},{10,14},{12,8},{14,10},{1,5},{3,7},... | collective-permute-start | bytes 24584 | tf_op jit(solution)/shard_map/ppermute | solution.py:120
  31.5 5.1 %collective-permute-start.4 = (f32[2,8,2048]{2,1,0:T(8,128)S(1)}, f32[2,8,2048]{2,1,0:T(8,128)S(1)}, u32[]{:S(2)}, u32[]{:S(2)}) collective-permute-start(f32[2,8,2048]{2,1,0:T(8,128)S(1)} %get-tuple-element.156), channel_id=1, source_target_pairs={{0,2},{2,0},{4,6},{6,4},{8,10},{10,8},{12,14},{14,12},{1,3},{3,1},... | collective-permute-start | bytes 393224 | tf_op jit(solution)/shard_map/ppermute | solution.py:120
  33.1 6.0 %collective-permute-start.6 = (f32[4,64,128]{2,1,0:T(8,128)S(1)}, f32[4,64,128]{2,1,0:T(8,128)S(1)}, u32[]{:S(2)}, u32[]{:S(2)}) collective-permute-start(f32[4,64,128]{2,1,0:T(8,128)S(1)} %constant_dynamic-slice_fusion.7), channel_id=1, source_target_pairs={{0,1},{1,0},{2,3},{3,2},{4,5},{5,4},{6,7},{7,6},{8,9},{9,8},{10,11... | collective-permute-start | bytes 393224 | tf_op jit(solution)/shard_map/ppermute | solution.py:52
  33.1 5.9 %collective-permute-start.3 = (f32[2,8,2048]{2,1,0:T(8,128)S(1)}, f32[2,8,2048]{2,1,0:T(8,128)S(1)}, u32[]{:S(2)}, u32[]{:S(2)}) collective-permute-start(f32[2,8,2048]{2,1,0:T(8,128)S(1)} %get-tuple-element.157), channel_id=1, source_target_pairs={{0,4},{2,6},{4,0},{6,2},{8,12},{10,14},{12,8},{14,10},{1,5},{3,7},... | collective-permute-start | bytes 393224 | tf_op jit(solution)/shard_map/ppermute | solution.py:120
  43.6 5.0 %collective-permute-start.10 = (f32[4,64,128]{2,1,0:T(8,128)S(1)}, f32[4,64,128]{2,1,0:T(8,128)S(1)}, u32[]{:S(2)}, u32[]{:S(2)}) collective-permute-start(f32[4,64,128]{2,1,0:T(8,128)S(1)} %constant_dynamic-slice_fusion.6), channel_id=1, source_target_pairs={{0,1},{1,0},{2,3},{3,2},{4,5},{5,4},{6,7},{7,6},{8,9},{9,8},{10,11... | collective-permute-start | bytes 393224 | tf_op jit(solution)/shard_map/ppermute | solution.py:52
  43.6 4.3 %collective-permute-start.9 = (f32[4,16,64]{2,1,0:T(8,128)S(1)}, f32[4,16,64]{2,1,0:T(8,128)S(1)}, u32[]{:S(2)}, u32[]{:S(2)}) collective-permute-start(f32[4,16,64]{2,1,0:T(8,128)S(1)} %bitcast.255), channel_id=1, source_target_pairs={{0,2},{2,0},{4,6},{6,4},{8,10},{10,8},{12,14},{14,12},{1,3},{3,1},... | collective-permute-start | bytes 49160 | tf_op jit(solution)/shard_map/ppermute | solution.py:120
  44.2 8.4 %collective-permute-start.8 = (f32[4,8,2048]{2,1,0:T(8,128)S(1)}, f32[4,8,2048]{2,1,0:T(8,128)S(1)}, u32[]{:S(2)}, u32[]{:S(2)}) collective-permute-start(f32[4,8,2048]{2,1,0:T(8,128)S(1)} %bitcast.232), channel_id=1, source_target_pairs={{0,4},{2,6},{4,0},{6,2},{8,12},{10,14},{12,8},{14,10},{1,5},{3,7},... | collective-permute-start | bytes 786440 | tf_op jit(solution)/shard_map/ppermute | solution.py:120
  44.5 8.6 %collective-permute-start.7 = (f32[4,8,2048]{2,1,0:T(8,128)S(1)}, f32[4,8,2048]{2,1,0:T(8,128)S(1)}, u32[]{:S(2)}, u32[]{:S(2)}) collective-permute-start(f32[4,8,2048]{2,1,0:T(8,128)S(1)} %bitcast.234), channel_id=1, source_target_pairs={{0,2},{2,0},{4,6},{6,4},{8,10},{10,8},{12,14},{14,12},{1,3},{3,1},... | collective-permute-start | bytes 786440 | tf_op jit(solution)/shard_map/ppermute | solution.py:120
  56.0 3.7 %collective-permute-start.13 = (f32[4,64,128]{2,1,0:T(8,128)S(1)}, f32[4,64,128]{2,1,0:T(8,128)S(1)}, u32[]{:S(2)}, u32[]{:S(2)}) collective-permute-start(f32[4,64,128]{2,1,0:T(8,128)S(1)} %constant_dynamic-slice_fusion.3), channel_id=1, source_target_pairs={{0,1},{1,0},{2,3},{3,2},{4,5},{5,4},{6,7},{7,6},{8,9},{9,8},{10,11... | collective-permute-start | bytes 393224 | tf_op jit(solution)/shard_map/ppermute | solution.py:52
  56.7 8.0 %collective-permute-start.12 = (f32[4,4,32,128]{3,2,1,0:T(8,128)S(1)}, f32[4,4,32,128]{3,2,1,0:T(8,128)S(1)}, u32[]{:S(2)}, u32[]{:S(2)}) collective-permute-start(f32[4,4,32,128]{3,2,1,0:T(8,128)S(1)} %bitcast.244), channel_id=1, source_target_pairs={{0,4},{2,6},{4,0},{6,2},{8,12},{10,14},{12,8},{14,10},{1,5},{3,7},... | collective-permute-start | bytes 786440 | tf_op jit(solution)/shard_map/ppermute | solution.py:160
  58.0 7.8 %collective-permute-start.11 = (f32[4,4,32,128]{3,2,1,0:T(8,128)S(1)}, f32[4,4,32,128]{3,2,1,0:T(8,128)S(1)}, u32[]{:S(2)}, u32[]{:S(2)}) collective-permute-start(f32[4,4,32,128]{3,2,1,0:T(8,128)S(1)} %copy-done.12), channel_id=1, source_target_pairs={{0,2},{2,0},{4,6},{6,4},{8,10},{10,8},{12,14},{14,12},{1,3},{3,1},... | collective-permute-start | bytes 786440 | tf_op jit(solution)/shard_map/ppermute | solution.py:160
  65.9 5.1 %collective-permute-start.18 = (f32[4,64,128]{2,1,0:T(8,128)S(1)}, f32[4,64,128]{2,1,0:T(8,128)S(1)}, u32[]{:S(2)}, u32[]{:S(2)}) collective-permute-start(f32[4,64,128]{2,1,0:T(8,128)S(1)} %constant_dynamic-slice_fusion.2), channel_id=1, source_target_pairs={{0,1},{1,0},{2,3},{3,2},{4,5},{5,4},{6,7},{7,6},{8,9},{9,8},{10,11... | collective-permute-start | bytes 393224 | tf_op jit(solution)/shard_map/ppermute | solution.py:52
  66.0 8.3 %collective-permute-start.17 = (f32[2,1,4,32,128]{4,3,2,0,1:T(8,128)S(1)}, f32[2,1,4,32,128]{4,3,2,0,1:T(8,128)S(1)}, u32[]{:S(2)}, u32[]{:S(2)}) collective-permute-start(f32[2,1,4,32,128]{4,3,2,0,1:T(8,128)S(1)} %dynamic-slice_bitcast_fusion.8), channel_id=1, source_target_pairs={{0,2},{2,0},{4,6},{6,4},{8,10},{10,8},{12,14},{14,12},{1,3},{3,1},... | collective-permute-start | bytes 393224 | tf_op jit(solution)/shard_map/ppermute | solution.py:186
  67.6 6.7 %collective-permute-start.16 = (f32[2,1,4,32,128]{4,3,2,0,1:T(8,128)S(1)}, f32[2,1,4,32,128]{4,3,2,0,1:T(8,128)S(1)}, u32[]{:S(2)}, u32[]{:S(2)}) collective-permute-start(f32[2,1,4,32,128]{4,3,2,0,1:T(8,128)S(1)} %dynamic-slice_bitcast_fusion.9), channel_id=1, source_target_pairs={{0,4},{2,6},{4,0},{6,2},{8,12},{10,14},{12,8},{14,10},{1,5},{3,7},... | collective-permute-start | bytes 393224 | tf_op jit(solution)/shard_map/ppermute | solution.py:186
  68.7 10.2 %collective-permute-start.15 = (f32[2,2,4,32,128]{4,3,2,1,0:T(8,128)S(1)}, f32[2,2,4,32,128]{4,3,2,1,0:T(8,128)S(1)}, u32[]{:S(2)}, u32[]{:S(2)}) collective-permute-start(f32[2,2,4,32,128]{4,3,2,1,0:T(8,128)S(1)} %dynamic-slice_bitcast_fusion), channel_id=1, source_target_pairs={{0,4},{2,6},{4,0},{6,2},{8,12},{10,14},{12,8},{14,10},{1,5},{3,7},... | collective-permute-start | bytes 786440 | tf_op jit(solution)/shard_map/ppermute | solution.py:186
  70.3 8.6 %collective-permute-start.14 = (f32[4,1,4,32,128]{4,3,2,0,1:T(8,128)S(1)}, f32[4,1,4,32,128]{4,3,2,0,1:T(8,128)S(1)}, u32[]{:S(2)}, u32[]{:S(2)}) collective-permute-start(f32[4,1,4,32,128]{4,3,2,0,1:T(8,128)S(1)} %dynamic-slice_bitcast_fusion.1), channel_id=1, source_target_pairs={{0,2},{2,0},{4,6},{6,4},{8,10},{10,8},{12,14},{14,12},{1,3},{3,1},... | collective-permute-start | bytes 786440 | tf_op jit(solution)/shard_map/ppermute | solution.py:186
  79.0 5.0 %collective-permute-start.20 = (f32[2,1,4,32,128]{4,3,2,0,1:T(8,128)S(1)}, f32[2,1,4,32,128]{4,3,2,0,1:T(8,128)S(1)}, u32[]{:S(2)}, u32[]{:S(2)}) collective-permute-start(f32[2,1,4,32,128]{4,3,2,0,1:T(8,128)S(1)} %dynamic-slice_bitcast_fusion.6), channel_id=1, source_target_pairs={{0,2},{2,0},{4,6},{6,4},{8,10},{10,8},{12,14},{14,12},{1,3},{3,1},... | collective-permute-start | bytes 393224 | tf_op jit(solution)/shard_map/ppermute | solution.py:186
  79.6 9.5 %collective-permute-start.21 = (f32[1,1,4,64,128]{4,3,2,1,0:T(8,128)S(1)}, f32[1,1,4,64,128]{4,3,2,1,0:T(8,128)S(1)}, u32[]{:S(2)}, u32[]{:S(2)}) collective-permute-start(f32[1,1,4,64,128]{4,3,2,1,0:T(8,128)S(1)} %dynamic-slice_bitcast_fusion.5), channel_id=1, source_target_pairs={{0,8},{2,10},{4,12},{6,14},{8,0},{10,2},{12,4},{14,6},{1,9},{3,11}... | collective-permute-start | bytes 393224 | tf_op jit(solution)/shard_map/ppermute | solution.py:186
  82.3 6.8 %collective-permute-start.19 = (f32[2,1,4,32,128]{4,3,2,0,1:T(8,128)S(1)}, f32[2,1,4,32,128]{4,3,2,0,1:T(8,128)S(1)}, u32[]{:S(2)}, u32[]{:S(2)}) collective-permute-start(f32[2,1,4,32,128]{4,3,2,0,1:T(8,128)S(1)} %dynamic-slice_bitcast_fusion.7), channel_id=1, source_target_pairs={{0,4},{2,6},{4,0},{6,2},{8,12},{10,14},{12,8},{14,10},{1,5},{3,7},... | collective-permute-start | bytes 393224 | tf_op jit(solution)/shard_map/ppermute | solution.py:186
  89.2 7.3 %collective-permute-start.22 = (f32[1,1,4,64,128]{4,3,2,1,0:T(8,128)S(1)}, f32[1,1,4,64,128]{4,3,2,1,0:T(8,128)S(1)}, u32[]{:S(2)}, u32[]{:S(2)}) collective-permute-start(f32[1,1,4,64,128]{4,3,2,1,0:T(8,128)S(1)} %dynamic-slice_bitcast_fusion.4), channel_id=1, source_target_pairs={{0,8},{2,10},{4,12},{6,14},{8,0},{10,2},{12,4},{14,6},{1,9},{3,11}... | collective-permute-start | bytes 393224 | tf_op jit(solution)/shard_map/ppermute | solution.py:186
  98.0 7.2 %collective-permute-start.23 = (f32[1,4,64,128]{3,2,1,0:T(8,128)S(1)}, f32[1,4,64,128]{3,2,1,0:T(8,128)S(1)}, u32[]{:S(2)}, u32[]{:S(2)}) collective-permute-start(f32[1,4,64,128]{3,2,1,0:T(8,128)S(1)} %fusion.1), channel_id=1, source_target_pairs={{0,8},{2,10},{4,12},{6,14},{8,0},{10,2},{12,4},{14,6},{1,9},{3,11}... | collective-permute-start | bytes 393224 | tf_op jit(solution)/shard_map/ppermute | solution.py:120
  105.2 5.0 %collective-permute-start.25 = (f32[2,4,32,128]{3,2,1,0:T(8,128)S(1)}, f32[2,4,32,128]{3,2,1,0:T(8,128)S(1)}, u32[]{:S(2)}, u32[]{:S(2)}) collective-permute-start(f32[2,4,32,128]{3,2,1,0:T(8,128)S(1)} %get-tuple-element.152), channel_id=1, source_target_pairs={{0,2},{2,0},{4,6},{6,4},{8,10},{10,8},{12,14},{14,12},{1,3},{3,1},... | collective-permute-start | bytes 393224 | tf_op jit(solution)/shard_map/ppermute | solution.py:120
  105.7 5.0 %collective-permute-start.24 = (f32[2,4,32,128]{3,2,1,0:T(8,128)S(1)}, f32[2,4,32,128]{3,2,1,0:T(8,128)S(1)}, u32[]{:S(2)}, u32[]{:S(2)}) collective-permute-start(f32[2,4,32,128]{3,2,1,0:T(8,128)S(1)} %get-tuple-element.153), channel_id=1, source_target_pairs={{0,4},{2,6},{4,0},{6,2},{8,12},{10,14},{12,8},{14,10},{1,5},{3,7},... | collective-permute-start | bytes 393224 | tf_op jit(solution)/shard_map/ppermute | solution.py:120
  110.7 7.1 %collective-permute-start.27 = (f32[4,4,32,128]{3,2,1,0:T(8,128)S(1)}, f32[4,4,32,128]{3,2,1,0:T(8,128)S(1)}, u32[]{:S(2)}, u32[]{:S(2)}) collective-permute-start(f32[4,4,32,128]{3,2,1,0:T(8,128)S(1)} %bitcast.236), channel_id=1, source_target_pairs={{0,4},{2,6},{4,0},{6,2},{8,12},{10,14},{12,8},{14,10},{1,5},{3,7},... | collective-permute-start | bytes 786440 | tf_op jit(solution)/shard_map/ppermute | solution.py:120
  110.8 6.9 %collective-permute-start.26 = (f32[4,4,32,128]{3,2,1,0:T(8,128)S(1)}, f32[4,4,32,128]{3,2,1,0:T(8,128)S(1)}, u32[]{:S(2)}, u32[]{:S(2)}) collective-permute-start(f32[4,4,32,128]{3,2,1,0:T(8,128)S(1)} %bitcast.242), channel_id=1, source_target_pairs={{0,2},{2,0},{4,6},{6,4},{8,10},{10,8},{12,14},{14,12},{1,3},{3,1},... | collective-permute-start | bytes 786440 | tf_op jit(solution)/shard_map/ppermute | solution.py:120
  119.9 1.6 %collective-permute-start.28 = (f32[4,64,128]{2,1,0:T(8,128)}, f32[4,64,128]{2,1,0:T(8,128)S(1)}, u32[]{:S(2)}, u32[]{:S(2)}) collective-permute-start(f32[4,64,128]{2,1,0:T(8,128)} %constant_dynamic-slice_fusion), channel_id=1, source_target_pairs={{0,1},{1,0},{2,3},{3,2},{4,5},{5,4},{6,7},{7,6},{8,9},{9,8},{10,11... | collective-permute-start | bytes 393224 | tf_op jit(solution)/shard_map/ppermute | solution.py:52
  126.6 1.9 %collective-permute-start.29 = (f32[1,2,256]{2,1,0:T(2,128)S(1)}, f32[1,2,256]{2,1,0:T(2,128)S(1)}, u32[]{:S(2)}, u32[]{:S(2)}) collective-permute-start(f32[1,2,256]{2,1,0:T(2,128)S(1)} %maximum_bitcast_fusion), channel_id=1, source_target_pairs={{0,1},{1,0},{2,3},{3,2},{4,5},{5,4},{6,7},{7,6},{8,9},{9,8},{10,11... | collective-permute-start | bytes 6152 | tf_op jit(solution)/shard_map/ppermute | solution.py:389
  (24 other events, 77.7 us)
